TPU v7x, 32 devices: a whole 2x2x4 slice. The times are simulated.
32 devices in a mesh: phi: 8 (over z, x), query: 2 (over core), event: 2 (over y).
Axes of the slice: x: 2, y: 2, z: 4, core: 2. Of those that a mesh axis runs over, the one named last changes fastest.
Arguments:
- hits: bfloat16 [8192, 256], P(('event', 'phi', 'query')), parts along dimension 0, may hold values from -6 to 6
- enc_qkv: bfloat16 [256, 768], replicated, may hold values from -15 to 15
- enc_out: bfloat16 [256, 256], replicated, may hold values from -0.375 to 0.375
- enc_up: bfloat16 [256, 1024], replicated, may hold values from -0.375 to 0.375
- enc_down: bfloat16 [1024, 256], replicated, may hold values from -0.1875 to 0.1875
- queries: bfloat16 [1024, 256], P('query'), may hold values from -240 to 240
- cross_q: bfloat16 [256, 256], replicated, may hold values from -0.375 to 0.375
- cross_kv: bfloat16 [256, 512], replicated, may hold values from -0.375 to 0.375
- cross_out: bfloat16 [256, 256], replicated, may hold values from -0.375 to 0.375
- mask_first: bfloat16 [256, 256], replicated, may hold values from -0.375 to 0.375
- mask_second: bfloat16 [256, 256], replicated, may hold values from -0.375 to 0.375
- truth: int32 [8192], P(('event', 'phi', 'query')), parts along dimension 0, may hold values from -1 to 511
- match: int32 [2048], P(('event', 'query')), parts along dimension 0, may hold values from 0 to 1023, each once
Outputs:
- encoded: bfloat16 [8192, 256], P(('event', 'phi', 'query')), parts along dimension 0
- mask_embed: bfloat16 [2048, 256], P(('event', 'query')), parts along dimension 0
- hit_grad: float32 [8192, 256], P(('event', 'phi', 'query')), parts along dimension 0
- mask_grad: float32 [2048, 256], P(('event', 'query')), parts along dimension 0
- mask_fill: float32 [2048], P(('event', 'query')), parts along dimension 0
There are 2 independent parts, one for each index of `event`. A program takes and returns all parts, laid end to end along the dimension named above; an argument that names none is the same for every part. Nothing has to cross between parts.
All inputs are finite; a program needn't handle non-finite values.
Results may differ from a plain program's by a relative error of at most 0.017.
Values may be sent and summed in bfloat16 or wider, within the bound.
No kernel may reach another device: no remote copies, remote signals or barrier semaphores. Data moves between devices by JAX's collectives and lax.ppermute only.
A program may use at most 64 MiB of HBM per device.

v0:
```python
import jax
import jax.numpy as jnp
from jax import lax
from jax.sharding import PartitionSpec as P

HEADS = 8
WIN = 512


def extended_2(block, sides, width):
    for axis, dim in sides:
        count = lax.axis_size(axis)
        forward = [(i, i + 1) for i in range(count - 1)]
        forward.append((count - 1, 0))
        backward = [(target, source) for source, target in forward]
        low = lax.ppermute(
            lax.slice_in_dim(block, block.shape[dim] - width, None, axis=dim), axis, forward
        )
        high = lax.ppermute(lax.slice_in_dim(block, 0, width, axis=dim), axis, backward)
        block = jnp.concatenate([low, block, high], axis=dim)
    return block


def norm_rows(entries):
    widened = entries.astype(jnp.float32)
    centred = widened - jnp.mean(widened, axis=-1, keepdims=True)
    spread = jnp.mean(centred * centred, axis=-1, keepdims=True)
    return centred * lax.rsqrt(spread + 1e-05)


def window_attend(query_rows, kv_ext):
    row_count, model_width = query_rows.shape
    head_size = model_width // HEADS
    key_count = kv_ext.shape[0]
    key_span = key_count - row_count
    query_heads = query_rows.reshape(row_count, HEADS, head_size)
    key_heads = kv_ext[:, :model_width].reshape(key_count, HEADS, head_size)
    value_heads = kv_ext[:, model_width:].reshape(key_count, HEADS, head_size)
    scores = jnp.einsum(
        "qhd,khd->hqk", query_heads, key_heads, preferred_element_type=jnp.float32
    ) * head_size ** (-0.5)
    offset = lax.broadcasted_iota(jnp.int32, (row_count, key_count), 1) - lax.broadcasted_iota(
        jnp.int32, (row_count, key_count), 0
    )
    inside = jnp.logical_and(offset >= 0, offset < key_span)
    scores = jnp.where(inside[None, :, :], scores, -1e30)
    raised = jnp.exp(scores - jnp.max(scores, axis=-1, keepdims=True))
    weights = (raised / jnp.sum(raised, axis=-1, keepdims=True)).astype(jnp.bfloat16)
    attended = jnp.einsum("hqk,khd->qhd", weights, value_heads, preferred_element_type=jnp.float32)
    return attended.reshape(row_count, model_width).astype(jnp.bfloat16)


def split_heads(matrix):
    row_count, model_width = matrix.shape
    return matrix.reshape(row_count, HEADS, model_width // HEADS).transpose(1, 0, 2)


def head_partial(operands):
    query_head, key_head, value_head = operands
    scores = lax.dot_general(
        query_head, key_head, (((1,), (1,)), ((), ())), preferred_element_type=jnp.float32
    ) * query_head.shape[1] ** (-0.5)
    local_max = jnp.max(scores, axis=1)
    raised = jnp.exp(scores - local_max[:, None]).astype(jnp.bfloat16)
    total = jnp.sum(raised.astype(jnp.float32), axis=1)
    mixed = jnp.dot(raised, value_head, preferred_element_type=jnp.float32)
    return (local_max, total, mixed)


def scale_heads(mixed, factor):
    query_count, model_width = mixed.shape
    head_count = factor.shape[0]
    shaped = mixed.reshape(query_count, head_count, model_width // head_count)
    return (shaped * factor.T[:, :, None]).reshape(query_count, model_width)


def loss_coefficients(
    sigma, target, matched, intersection, predicted, truth_count, hits_total, model_width
):
    denom = predicted + truth_count + 1.0
    slope = -2.0 / denom
    level = (2.0 * intersection + 1.0) / (denom * denom)
    dice_part = hits_total * (slope[:, None] * target + level[:, None]) * sigma * (1.0 - sigma)
    return (matched[:, None] * (sigma - target + dice_part) * model_width ** (-0.5)).astype(
        jnp.bfloat16
    )


def body(
    hits,
    enc_qkv,
    enc_out,
    enc_up,
    enc_down,
    queries,
    cross_q,
    cross_kv,
    cross_out,
    mask_first,
    mask_second,
    truth,
    match,
):
    model_width = hits.shape[1]
    local_hits = hits.shape[0]
    query_count = queries.shape[0]
    hits_total = float(local_hits * lax.axis_size("phi") * lax.axis_size("query"))
    track_count = query_count * lax.axis_size("query") // 2
    normed = norm_rows(hits).astype(jnp.bfloat16)
    projected = jnp.dot(normed, enc_qkv, preferred_element_type=jnp.float32).astype(jnp.bfloat16)
    extended = extended_2(projected[:, model_width:], ((("phi", "query"), 0),), WIN // 2)
    attended = window_attend(projected[:, :model_width], extended)
    residual = hits.astype(jnp.float32) + jnp.dot(
        attended, enc_out, preferred_element_type=jnp.float32
    )
    upper = jax.nn.gelu(
        jnp.dot(
            norm_rows(residual).astype(jnp.bfloat16), enc_up, preferred_element_type=jnp.float32
        ),
        approximate=True,
    ).astype(jnp.bfloat16)
    encoded = (residual + jnp.dot(upper, enc_down, preferred_element_type=jnp.float32)).astype(
        jnp.bfloat16
    )
    local_kv = jnp.dot(
        norm_rows(encoded).astype(jnp.bfloat16), cross_kv, preferred_element_type=jnp.float32
    ).astype(jnp.bfloat16)
    group_kv, group_hits, group_truth = (
        lax.all_gather(local_kv, "query", axis=0, tiled=True),
        lax.all_gather(encoded, "query", axis=0, tiled=True),
        lax.all_gather(truth, "query", axis=0, tiled=True),
    )
    query_proj = jnp.dot(queries, cross_q, preferred_element_type=jnp.float32).astype(jnp.bfloat16)
    local_max, local_total, head_mixed = lax.map(
        head_partial,
        (
            split_heads(query_proj),
            split_heads(group_kv[:, :model_width]),
            split_heads(group_kv[:, model_width:]),
        ),
    )
    local_mixed = head_mixed.transpose(1, 0, 2).reshape(query_count, model_width)
    top = lax.pmax(local_max, "phi")
    factor = jnp.exp(local_max - top)
    total, mixed = lax.psum((local_total * factor, scale_heads(local_mixed, factor)), "phi")
    context = scale_heads(mixed, 1.0 / total).astype(jnp.bfloat16)
    mixed_queries = queries.astype(jnp.float32) + jnp.dot(
        context, cross_out, preferred_element_type=jnp.float32
    )
    mask_hidden = jax.nn.relu(
        jnp.dot(
            norm_rows(mixed_queries).astype(jnp.bfloat16),
            mask_first,
            preferred_element_type=jnp.float32,
        )
    ).astype(jnp.bfloat16)
    mask_embed = jnp.dot(mask_hidden, mask_second, preferred_element_type=jnp.float32).astype(
        jnp.bfloat16
    )
    logits = lax.dot_general(
        mask_embed, group_hits, (((1,), (1,)), ((), ())), preferred_element_type=jnp.float32
    ) * model_width ** (-0.5)
    sigma = jax.nn.sigmoid(logits)
    matched_flag = match < track_count
    matched = matched_flag.astype(jnp.float32)
    target = jnp.logical_and(match[:, None] == group_truth[None, :], matched_flag[:, None]).astype(
        jnp.float32
    )
    intersection, predicted, truth_count = lax.psum(
        (jnp.sum(sigma * target, axis=1), jnp.sum(sigma, axis=1), jnp.sum(target, axis=1)), "phi"
    )
    mask_fill = predicted / hits_total
    coef = loss_coefficients(
        sigma, target, matched, intersection, predicted, truth_count, hits_total, model_width
    )
    mask_grad = lax.psum(jnp.dot(coef, group_hits, preferred_element_type=jnp.float32), "phi")
    hit_grad = lax.psum_scatter(
        lax.dot_general(
            coef, mask_embed, (((0,), (0,)), ((), ())), preferred_element_type=jnp.float32
        ),
        "query",
        scatter_dimension=0,
        tiled=True,
    )
    return (encoded, mask_embed, hit_grad, mask_grad, mask_fill)


def solution(mesh):
    return jax.shard_map(
        body,
        mesh=mesh,
        in_specs=(
            P(("event", "phi", "query"), None),
            P(),
            P(),
            P(),
            P(),
            P("query", None),
            P(),
            P(),
            P(),
            P(),
            P(),
            P(("event", "phi", "query")),
            P(("event", "query")),
        ),
        out_specs=(
            P(("event", "phi", "query"), None),
            P(("event", "query"), None),
            P(("event", "phi", "query"), None),
            P(("event", "query"), None),
            P(("event", "query")),
        ),
        check_vma=False,
    )
```

profile of v0, /device:TPU:0, one launch (start us, length us, event | category | flops | bytes accessed | tf_op | source)
XLA Modules:
  0.0 292.6 jit_solution(17762094528635554202)
XLA Ops:
  9.8 5.5 %collective-permute-start.1 = (bf16[256,512]{1,0:T(8,128)(2,1)S(1)}, bf16[256,512]{1,0:T(8,128)(2,1)S(1)}, u32[]{:S(2)}, u32[]{:S(2)}) collective-permute-start(bf16[256,512]{1,0:T(8,128)(2,1)S(1)} %slice.24), channel_id=1, source_target_pairs={{2,0},{4,2},{6,4},{8,6},{10,8},{12,10},{14,12},{16,14},{18,16},{20... | collective-permute-start | bytes 786440 | tf_op jit(solution)/shard_map/ppermute | solution.py:19
  19.1 4.6 %collective-permute-done = bf16[256,512]{1,0:T(8,128)(2,1)S(1)} collective-permute-done((bf16[256,512]{1,0:T(8,128)(2,1)S(1)}, bf16[256,512]{1,0:T(8,128)(2,1)S(1)}, u32[]{:S(2)}, u32[]{:S(2)}) %collective-permute-start) | collective-permute-done | bytes 262176 | tf_op jit(solution)/shard_map/ppermute | solution.py:16
  24.2 6.0 %fusion.83 = (f32[8,256]{1,0:T(8,128)S(1)}, f32[8,256,768]{2,1,0:T(8,128)}) fusion(pred[256,768]{1,0:T(8,128)(4,1)S(1)} %fusion.36, bf16[256,8,32]{0,2,1:T(8,128)(2,1)} %bitcast.93, bf16[768,8,32]{0,2,1:T(8,128)(2,1)S(1)} %bitcast.90), kind=kOutput, calls=%fused_computation.123 | convolution fusion | flops 106955520 | bytes 7020544 | tf_op jit(solution)/shard_map/sub | solution.py:47
  30.2 4.0 %fusion.21 = bf16[8,32,256]{2,1,0:T(8,128)(2,1)S(1)} fusion(bf16[768,8,32]{0,2,1:T(8,128)(2,1)S(1)} %bitcast.89, f32[8,256,768]{2,1,0:T(8,128)} %get-tuple-element.110, f32[8,256]{1,0:T(8,128)S(1)} %get-tuple-element.109), kind=kOutput, calls=%fused_computation.40 | convolution fusion | flops 103874560 | bytes 6823936 | tf_op jit(solution)/shard_map/hqk,khd->qhd/dot_general | solution.py:49
  35.7 2.2 all_gather.9
  38.3 33.1 %while.14 = (s32[]{:T(128)}, f32[8,512]{1,0:T(8,128)}, f32[8,512]{1,0:T(8,128)}, f32[8,512,32]{1,2,0:T(8,128)}, bf16[8,512,32]{2,1,0:T(8,128)(2,1)S(1)}, /*index...) while((s32[]{:T(128)}, f32[8,512]{1,0:T(8,128)}, ...), condition=%wide.region_11.12_spmd, body=%wide.region_8.11_spmd.sunk | while | flops 35650560 | bytes 3426413 | solution.py:134
  38.7 1.3 dynamic_update_slice.16
  40.2 1.3 dynamic_update_slice.17
  42.8 1.3 dynamic_update_slice.16
  44.3 1.3 dynamic_update_slice.17
  46.9 1.3 dynamic_update_slice.16
  48.5 1.3 dynamic_update_slice.17
  51.1 1.3 dynamic_update_slice.16
  52.6 1.3 dynamic_update_slice.17
  55.2 1.3 dynamic_update_slice.16
  56.8 1.3 dynamic_update_slice.17
  59.4 1.3 dynamic_update_slice.16
  60.9 1.3 dynamic_update_slice.17
  63.5 1.3 dynamic_update_slice.16
  65.0 1.3 dynamic_update_slice.17
  67.6 1.3 dynamic_update_slice.16
  71.4 33.6 %pmax.7 = f32[8,512]{1,0:T(8,128)S(1)} all-reduce(f32[8,512]{1,0:T(8,128)} %get-tuple-element.45), channel_id=1, replica_groups=mesh['phi'=8,'query'=2,'event'=2] {'phi'}, use_global_device_ids=true, to_apply=%region_12.13 | all-reduce | flops 4096 | bytes 32768 | tf_op jit(solution)/shard_map/pmax | solution.py:143
  105.7 1.9 bitcast_multiply_fusion.1
  107.9 1.8 all-gather
  109.7 33.1 %psum.43 = f32[8,512]{1,0:T(8,128)S(1)} all-reduce(f32[8,512]{1,0:T(8,128)S(1)} %get-tuple-element.104), channel_id=1, replica_groups=mesh['phi'=8,'query'=2,'event'=2] {'phi'}, use_global_device_ids=true, to_apply=%region_14.15 | all-reduce | flops 4096 | bytes 32768 | tf_op jit(solution)/shard_map/psum | solution.py:145
  142.8 2.0 all_gather.10
  144.8 32.7 %all-reduce.4.cloned.1.call-done = f32[512,256]{0,1:T(8,128)} async-done(((f32[512,256]{0,1:T(8,128)}), f32[512,256]{0,1:T(8,128)}) %all-reduce.4.cloned.1.call-update) | async-done | bytes 524304 | tf_op jit(solution)/shard_map/psum | solution.py:145
  179.9 1.4 convolution_convert_fusion.1
  182.0 20.0 %all-reduce = (f32[512]{0:T(512)S(1)}, f32[512]{0:T(512)S(1)}, f32[512]{0:T(512)S(1)}) all-reduce(f32[512]{0:T(512)S(1)} %get-tuple-element.77, f32[512]{0:T(512)S(1)} %get-tuple-element.76, f32[512]{0:T(512)S(1)} %get-tuple-element.78), channel_id=1, replica_groups=mesh['phi'=8,'query'=2,'event'=2] {'phi'}, use_global_device_ids=true, to_apply=%region_22.23 | all-reduce | flops 1536 | bytes 12288 | tf_op jit(solution)/shard_map/psum | solution.py:169
  206.3 67.8 %all-reduce.6.cloned.1.call-done = f32[512,256]{1,0:T(8,128)} async-done(((f32[512,256]{1,0:T(8,128)}), f32[512,256]{1,0:T(8,128)}) %all-reduce.6.cloned.1.call-update) | async-done | bytes 524304 | tf_op jit(solution)/shard_map/psum | solution.py:176
  274.1 10.1 %reduce-scatter.2.cloned.1.call-done = f32[256,256]{1,0:T(8,128)} async-done(((f32[512,256]{1,0:T(8,128)}), f32[256,256]{1,0:T(8,128)}) %reduce-scatter.2.cloned.1.call-update) | async-done | bytes 262160 | tf_op jit(solution)/shard_map/reduce_scatter | solution.py:177
  284.2 1.9 copy.68
  (95 shorter events, 29.9 us)
Async XLA Ops:
  7.2 27.4 %copy-start = (bf16[1024,256]{1,0:T(8,128)(2,1)S(1)}, bf16[1024,256]{1,0:T(8,128)(2,1)}, u32[]{:S(2)}) copy-start(bf16[1024,256]{1,0:T(8,128)(2,1)} %param.19) | copy-start | bytes 1572868
  7.2 170.3 %all-reduce.4.cloned.1.call-start = ((), (), s32[]{:S(2)}) async-start(), calls=%async_computation.1 | async-start | bytes 1048576 | tf_op jit(solution)/shard_map/psum | solution.py:145
  9.8 9.4 %collective-permute-start.1 = (bf16[256,512]{1,0:T(8,128)(2,1)S(1)}, bf16[256,512]{1,0:T(8,128)(2,1)S(1)}, u32[]{:S(2)}, u32[]{:S(2)}) collective-permute-start(bf16[256,512]{1,0:T(8,128)(2,1)S(1)} %slice.24), channel_id=1, source_target_pairs={{2,0},{4,2},{6,4},{8,6},{10,8},{12,10},{14,12},{16,14},{18,16},{20... | collective-permute-start | bytes 786440 | tf_op jit(solution)/shard_map/ppermute | solution.py:19
  15.2 8.5 %collective-permute-start = (bf16[256,512]{1,0:T(8,128)(2,1)S(1)}, bf16[256,512]{1,0:T(8,128)(2,1)S(1)}, u32[]{:S(2)}, u32[]{:S(2)}) collective-permute-start(bf16[256,512]{1,0:T(8,128)(2,1)S(1)} %slice.24), channel_id=1, source_target_pairs={{0,2},{2,4},{4,6},{6,8},{8,10},{10,12},{12,14},{14,16},{16,18},{18... | collective-permute-start | bytes 786440 | tf_op jit(solution)/shard_map/ppermute | solution.py:16
  30.2 4.0 %copy-start.4 = (bf16[256,256]{1,0:T(8,128)(2,1)S(1)}, bf16[256,256]{1,0:T(8,128)(2,1)}, u32[]{:S(2)}) copy-start(bf16[256,256]{1,0:T(8,128)(2,1)} %param.17) | copy-start | bytes 393220
  30.2 4.4 %copy-start.7 = (bf16[256,1024]{1,0:T(8,128)(2,1)S(1)}, bf16[256,1024]{1,0:T(8,128)(2,1)}, u32[]{:S(2)}) copy-start(bf16[256,1024]{1,0:T(8,128)(2,1)} %param.18) | copy-start | bytes 1572868
  30.2 5.3 %copy-start.3 = (bf16[256,512]{1,0:T(8,128)(2,1)S(1)}, bf16[256,512]{1,0:T(8,128)(2,1)}, u32[]{:S(2)}) copy-start(bf16[256,512]{1,0:T(8,128)(2,1)} %param.22) | copy-start | bytes 786436
  38.2 69.5 %copy-start.1 = (bf16[512,256]{1,0:T(8,128)(2,1)S(1)}, bf16[512,256]{1,0:T(8,128)(2,1)}, u32[]{:S(2)}) copy-start(bf16[512,256]{1,0:T(8,128)(2,1)} %param.20) | copy-start | bytes 786436
  38.3 69.6 %copy-start.6 = (s32[256]{0:T(256)S(1)}, s32[256]{0:T(256)}, u32[]{:S(2)}) copy-start(s32[256]{0:T(256)} %param.26) | copy-start | bytes 3076
  38.3 71.4 %copy-start.5 = (s32[512]{0:T(512)S(1)}, s32[512]{0:T(512)}, u32[]{:S(2)}) copy-start(s32[512]{0:T(512)} %param.27) | copy-start | bytes 6148
  107.7 166.4 %all-reduce.6.cloned.1.call-start = ((), (), s32[]{:S(2)}) async-start(), calls=%async_computation.3 | async-start | bytes 1048576 | tf_op jit(solution)/shard_map/psum | solution.py:176
  181.3 104.7 %copy-start.2 = (bf16[512,256]{1,0:T(8,128)(2,1)}, bf16[512,256]{1,0:T(8,128)(2,1)S(1)}, u32[]{:S(2)}) copy-start(bf16[512,256]{1,0:T(8,128)(2,1)S(1)} %convolution_convert_fusion.1) | copy-start | bytes 786436
  204.4 79.8 %reduce-scatter.2.cloned.1.call-start = ((), (), s32[]{:S(2)}) async-start(), calls=%async_computation.2 | async-start | bytes 786432 | tf_op jit(solution)/shard_map/reduce_scatter | solution.py:177
Sparse Core Ops, SparseCore 0:
  107.8 69.7 all-reduce.3
  204.5 69.5 all-reduce.5
  276.9 7.2 reduce-scatter.1
where the time goes:
time: 295 us; the launch traced here: 293 us
  waiting for transfers between devices  117 us (40%)
  blocking collectives  92.6 us (31%)
  matrix products  29.5 us (10%)
  local copies, waits for them, and re-layouts  27.3 us (9%)
  between operations  14 us (5%)
  other arithmetic  7 us (2%)
  starting transfers between devices  5.59 us (2%)
    psum x1, waiting for transfers between devices, body(): lax.psum(jnp.dot(coef, group_hits, preferred_element_type=jnp.float32), '...  67.8 us
    pmax x1, blocking collectives, body(): top = lax.pmax(local_max, 'phi')  33.6 us
    psum x1, blocking collectives, body(): lax.psum((local_total * factor, scale_heads(local_mixed, factor)), 'phi')  33.1 us
    psum x1, waiting for transfers between devices, body(): lax.psum((local_total * factor, scale_heads(local_mixed, factor)), 'phi')  32.7 us
    dynamic_update_slice x16, local copies, waits for them, and re-layouts, body(): lax.map(head_partial, (split_heads(query_proj), split_heads(group_kv[:, :...  21.4 us
    psum x1, blocking collectives, body(): lax.psum((jnp.sum(sigma * target, axis=1), jnp.sum(sigma, axis=1), jnp.su...  20 us
    reduce_scatter x1, waiting for transfers between devices, body(): lax.psum_scatter(lax.dot_general(coef, mask_embed, (((0,), (0,)), ((), ()...  10.1 us
    dot_general x8, matrix products, head_partial(): mixed = jnp.dot(raised, value_head, preferred_element_type=jnp.float32)  7.23 us
  transfers between devices with their start and end apart: 5, of which 5 were waited for; matrix products, arithmetic and copies ran while one was open for 2% of the time, Pallas kernels for 0%

commit v1 on v0

--- a/solution.py
+++ b/solution.py
@@ -18,6 +18,61 @@
         )
         high = lax.ppermute(lax.slice_in_dim(block, 0, width, axis=dim), axis, backward)
         block = jnp.concatenate([low, block, high], axis=dim)
+    return block
+
+
+def partner_pairs(count, distance):
+    return [(i, i ^ distance) for i in range(count)]
+
+
+def butterfly(tree, axis, combine, ordered=False):
+    count = lax.axis_size(axis)
+    assert count & (count - 1) == 0
+    index = lax.axis_index(axis)
+    distance = 1
+    while distance < count:
+        other = lax.ppermute(tree, axis, partner_pairs(count, distance))
+        if ordered:
+            upper = (index // distance) % 2 == 1
+            first = jax.tree.map(lambda a, b: jnp.where(upper, b, a), tree, other)
+            second = jax.tree.map(lambda a, b: jnp.where(upper, a, b), tree, other)
+            tree = combine(first, second)
+        else:
+            tree = combine(tree, other)
+        distance *= 2
+    return tree
+
+
+def add_trees(a, b):
+    return jax.tree.map(jnp.add, a, b)
+
+
+def softmax_combine(a, b):
+    max_a, total_a, mixed_a = a
+    max_b, total_b, mixed_b = b
+    top = jnp.maximum(max_a, max_b)
+    factor_a = jnp.exp(max_a - top)
+    factor_b = jnp.exp(max_b - top)
+    return (
+        top,
+        total_a * factor_a + total_b * factor_b,
+        scale_heads(mixed_a, factor_a) + scale_heads(mixed_b, factor_b),
+    )
+
+
+def reduce_scatter_rows(block, axis):
+    count = lax.axis_size(axis)
+    assert count & (count - 1) == 0
+    index = lax.axis_index(axis)
+    distance = count // 2
+    while distance >= 1:
+        half = block.shape[0] // 2
+        upper = (index // distance) % 2 == 1
+        low, high = block[:half], block[half:]
+        keep = jnp.where(upper, high, low)
+        send = jnp.where(upper, low, high)
+        block = keep + lax.ppermute(send, axis, partner_pairs(count, distance))
+        distance //= 2
     return block
 
 
@@ -131,18 +186,23 @@
         lax.all_gather(truth, "query", axis=0, tiled=True),
     )
     query_proj = jnp.dot(queries, cross_q, preferred_element_type=jnp.float32).astype(jnp.bfloat16)
-    local_max, local_total, head_mixed = lax.map(
-        head_partial,
-        (
-            split_heads(query_proj),
-            split_heads(group_kv[:, :model_width]),
-            split_heads(group_kv[:, model_width:]),
-        ),
-    )
-    local_mixed = head_mixed.transpose(1, 0, 2).reshape(query_count, model_width)
-    top = lax.pmax(local_max, "phi")
-    factor = jnp.exp(local_max - top)
-    total, mixed = lax.psum((local_total * factor, scale_heads(local_mixed, factor)), "phi")
+    head_size = model_width // HEADS
+    group_count = group_kv.shape[0]
+    query_heads = query_proj.reshape(query_count, HEADS, head_size)
+    key_heads = group_kv[:, :model_width].reshape(group_count, HEADS, head_size)
+    value_heads = group_kv[:, model_width:].reshape(group_count, HEADS, head_size)
+    scores = jnp.einsum(
+        "qhd,khd->hqk", query_heads, key_heads, preferred_element_type=jnp.float32
+    ) * head_size ** (-0.5)
+    local_max = jnp.max(scores, axis=-1)
+    raised = jnp.exp(scores - local_max[..., None]).astype(jnp.bfloat16)
+    local_total = jnp.sum(raised.astype(jnp.float32), axis=-1)
+    local_mixed = jnp.einsum(
+        "hqk,khd->qhd", raised, value_heads, preferred_element_type=jnp.float32
+    ).reshape(query_count, model_width)
+    _, total, mixed = butterfly(
+        (local_max, local_total, local_mixed), "phi", softmax_combine, ordered=True
+    )
     context = scale_heads(mixed, 1.0 / total).astype(jnp.bfloat16)
     mixed_queries = queries.astype(jnp.float32) + jnp.dot(
         context, cross_out, preferred_element_type=jnp.float32
@@ -166,21 +226,23 @@
     target = jnp.logical_and(match[:, None] == group_truth[None, :], matched_flag[:, None]).astype(
         jnp.float32
     )
-    intersection, predicted, truth_count = lax.psum(
-        (jnp.sum(sigma * target, axis=1), jnp.sum(sigma, axis=1), jnp.sum(target, axis=1)), "phi"
+    intersection, predicted, truth_count = butterfly(
+        (jnp.sum(sigma * target, axis=1), jnp.sum(sigma, axis=1), jnp.sum(target, axis=1)),
+        "phi",
+        add_trees,
     )
     mask_fill = predicted / hits_total
     coef = loss_coefficients(
         sigma, target, matched, intersection, predicted, truth_count, hits_total, model_width
     )
-    mask_grad = lax.psum(jnp.dot(coef, group_hits, preferred_element_type=jnp.float32), "phi")
-    hit_grad = lax.psum_scatter(
+    mask_grad = butterfly(
+        jnp.dot(coef, group_hits, preferred_element_type=jnp.float32), "phi", add_trees
+    )
+    hit_grad = reduce_scatter_rows(
         lax.dot_general(
             coef, mask_embed, (((0,), (0,)), ((), ())), preferred_element_type=jnp.float32
         ),
         "query",
-        scatter_dimension=0,
-        tiled=True,
     )
     return (encoded, mask_embed, hit_grad, mask_grad, mask_fill)
 

time: 295 us -> 150 us (0.51)
  blocking collectives: 92.6 us -> 7.84 us
  waiting for transfers between devices: 117 us -> 77.7 us
  starting transfers between devices: 5.59 us -> 30.5 us
  local copies, waits for them, and re-layouts: 27.3 us -> 5.92 us
  between operations: 14 us -> 1.04 us
  matrix products: 29.5 us -> 21.3 us
    psum x2 -> x0, waiting for transfers between devices: 101 us -> none  [the longest x1 67.8 us: body(): lax.psum(jnp.dot(coef, group_hits, preferred_element_type=jnp.float32), '...]
    ppermute x0 -> x22, waiting for transfers between devices: none -> 75.1 us  [the longest x21 74.3 us: butterfly(): other = lax.ppermute(tree, axis, partner_pairs(count, distance))]
    psum x2 -> x0, blocking collectives: 53.1 us -> none  [the longest x1 33.1 us: body(): lax.psum((local_total * factor, scale_heads(local_mixed, factor)), 'phi')]
    pmax x1 -> x0, blocking collectives: 33.6 us -> none  [body(): top = lax.pmax(local_max, 'phi')]
    ppermute x0 -> x22, starting transfers between devices: none -> 25 us  [the longest x21 24.9 us: butterfly(): other = lax.ppermute(tree, axis, partner_pairs(count, distance))]
    dynamic_update_slice x16 -> x0, local copies, waits for them, and re-layouts: 21.4 us -> none  [body(): lax.map(head_partial, (split_heads(query_proj), split_heads(group_kv[:, :...]
    reduce_scatter x1 -> x0, waiting for transfers between devices: 10.1 us -> none  [body(): lax.psum_scatter(lax.dot_general(coef, mask_embed, (((0,), (0,)), ((), ()...]
    dot_general x16 -> x2, matrix products: 10.1 us -> 6.28 us  [the longest x1 4.97 us: body(): jnp.einsum('hqk,khd->qhd', raised, value_heads, preferred_element_type=jn...]
  transfers between devices with their start and end apart: 5 -> 24, of which waited for: 5 -> 17; matrix products, arithmetic and copies ran while one was open for 2% -> 7% of each run, Pallas kernels for 0% -> 0%
where the time goes in v1:
time: 150 us
  waiting for transfers between devices  77.7 us (52%)
  starting transfers between devices  30.5 us (20%)
  matrix products  21.3 us (14%)
  blocking collectives  7.84 us (5%)
  local copies, waits for them, and re-layouts  5.92 us (4%)
  other arithmetic  5.36 us (4%)
    ppermute x21, waiting for transfers between devices, butterfly(): other = lax.ppermute(tree, axis, partner_pairs(count, distance))  74.3 us
    ppermute x21, starting transfers between devices, butterfly(): other = lax.ppermute(tree, axis, partner_pairs(count, distance))  24.9 us
    sub x1, matrix products, window_attend(): raised = jnp.exp(scores - jnp.max(scores, axis=-1, keepdims=True))  5.11 us
    unnamed x27, local copies, waits for them, and re-layouts  5.08 us
    ppermute x1, starting transfers between devices, extended_2(): lax.ppermute(lax.slice_in_dim(block, 0, width, axis=dim), axis, backward)  5.03 us
    dot_general x1, matrix products, body(): jnp.einsum('hqk,khd->qhd', raised, value_heads, preferred_element_type=jn...  4.97 us
    dot_general x1, matrix products, window_attend(): jnp.einsum('hqk,khd->qhd', weights, value_heads, preferred_element_type=j...  3.99 us
    all_gather x1, blocking collectives, body(): lax.all_gather(local_kv, 'query', axis=0, tiled=True)  3.88 us
  transfers between devices with their start and end apart: 24, of which 17 were waited for; matrix products, arithmetic and copies ran while one was open for 7% of the time, Pallas kernels for 0%

profile of v1, /device:TPU:0, one launch (start us, length us, event | category | flops | bytes accessed | tf_op | source)
XLA Modules:
  0.0 149.6 jit_solution(9986652336215298837)
XLA Ops:
  3.7 5.0 %collective-permute-start.1 = (bf16[256,512]{1,0:T(8,128)(2,1)S(1)}, bf16[256,512]{1,0:T(8,128)(2,1)S(1)}, u32[]{:S(2)}, u32[]{:S(2)}) collective-permute-start(bf16[256,512]{1,0:T(8,128)(2,1)S(1)} %slice.32), channel_id=1, source_target_pairs={{2,0},{4,2},{6,4},{8,6},{10,8},{12,10},{14,12},{16,14},{18,16},{20... | collective-permute-start | bytes 786440 | tf_op jit(solution)/shard_map/ppermute | solution.py:19
  10.2 2.6 %collective-permute-done = bf16[256,512]{1,0:T(8,128)(2,1)S(1)} collective-permute-done((bf16[256,512]{1,0:T(8,128)(2,1)S(1)}, bf16[256,512]{1,0:T(8,128)(2,1)S(1)}, u32[]{:S(2)}, u32[]{:S(2)}) %collective-permute-start) | collective-permute-done | bytes 262176 | tf_op jit(solution)/shard_map/ppermute | solution.py:16
  13.3 5.1 %fusion.87 = (f32[8,256]{1,0:T(8,128)S(1)}, f32[8,256,768]{2,1,0:T(8,128)}) fusion(pred[256,768]{1,0:T(8,128)(4,1)S(1)} %fusion.27, bf16[256,8,32]{0,2,1:T(8,128)(2,1)S(1)} %bitcast.92, bf16[768,8,32]{0,2,1:T(8,128)(2,1)S(1)} %bitcast.89), kind=kOutput, calls=%fused_computation.144 | convolution fusion | flops 106955520 | bytes 7020544 | tf_op jit(solution)/shard_map/sub | solution.py:102
  18.4 4.0 %fusion.12 = bf16[8,32,256]{2,1,0:T(8,128)(2,1)S(1)} fusion(bf16[768,8,32]{0,2,1:T(8,128)(2,1)S(1)} %bitcast.90, f32[8,256,768]{2,1,0:T(8,128)} %get-tuple-element.48, f32[8,256]{1,0:T(8,128)S(1)} %get-tuple-element.47), kind=kOutput, calls=%fused_computation.30 | convolution fusion | flops 103874560 | bytes 6823936 | tf_op jit(solution)/shard_map/hqk,khd->qhd/dot_general | solution.py:104
  24.0 3.9 %all_gather.9 = bf16[512,512]{1,0:T(8,128)(2,1)S(1)} all-gather(bf16[256,512]{1,0:T(8,128)(2,1)S(1)} %convolution_convert_fusion.3), channel_id=1, replica_groups=mesh['phi'=8,'query'=2,'event'=2] {'query'}, dimensions={0}, use_global_device_ids=true | all-gather | bytes 786432 | tf_op jit(solution)/shard_map/all_gather | solution.py:184
  28.0 1.3 multiply_reduce_fusion
  29.5 3.0 %copy-done.1 = f32[8,512,512]{1,2,0:T(8,128)} copy-done((f32[8,512,512]{1,2,0:T(8,128)}, f32[8,512,512]{1,2,0:T(8,128)S(1)}, u32[]{:S(2)}) %copy-start.1) | copy-done | bytes 8388632
  32.6 1.4 convert_reduce_fusion
  34.3 5.0 %fusion.30 = f32[8,32,512]{2,1,0:T(8,128)S(1)} fusion(bf16[512,8,32]{0,2,1:T(8,128)(2,1)S(1)} %bitcast.88, f32[8,512,512]{1,2,0:T(8,128)} %copy-done.1, f32[8,512]{1,0:T(8,128)S(1)} %get-tuple-element.53), kind=kOutput, calls=%fused_computation.51 | convolution fusion | flops 140509184 | bytes 9191424 | tf_op jit(solution)/shard_map/hqk,khd->qhd/dot_general | solution.py:200
  39.3 2.0 %collective-permute-start.2 = (f32[512,256]{0,1:T(8,128)S(1)}, f32[512,256]{0,1:T(8,128)S(1)}, u32[]{:S(2)}, u32[]{:S(2)}) collective-permute-start(f32[512,256]{0,1:T(8,128)S(1)} %bitcast.85), channel_id=1, source_target_pairs={{0,4},{4,0},{8,12},{12,8},{16,20},{20,16},{24,28},{28,24},{1,5},{5... | collective-permute-start | bytes 1572872 | tf_op jit(solution)/shard_map/ppermute | solution.py:34
  42.1 1.3 collective-permute-start.9
  43.4 1.7 %collective-permute-done.5 = f32[8,512]{1,0:T(8,128)S(1)} collective-permute-done((f32[8,512]{1,0:T(8,128)S(1)}, f32[8,512]{1,0:T(8,128)S(1)}, u32[]{:S(2)}, u32[]{:S(2)}) %collective-permute-start.5) | collective-permute-done | bytes 16416 | tf_op jit(solution)/shard_map/ppermute | solution.py:34
  45.8 2.7 %collective-permute-start.10 = (f32[8,512]{1,0:T(8,128)S(1)}, f32[8,512]{1,0:T(8,128)S(1)}, u32[]{:S(2)}, u32[]{:S(2)}) collective-permute-start(f32[8,512]{1,0:T(8,128)S(1)} %get-tuple-element.27), channel_id=1, source_target_pairs={{0,16},{4,20},{8,24},{12,28},{16,0},{20,4},{24,8},{28,12},{1,17},{... | collective-permute-start | bytes 49160 | tf_op jit(solution)/shard_map/ppermute | solution.py:34
  48.8 2.0 %collective-permute-done.10 = f32[8,512]{1,0:T(8,128)S(1)} collective-permute-done((f32[8,512]{1,0:T(8,128)S(1)}, f32[8,512]{1,0:T(8,128)S(1)}, u32[]{:S(2)}, u32[]{:S(2)}) %collective-permute-start.10) | collective-permute-done | bytes 16416 | tf_op jit(solution)/shard_map/ppermute | solution.py:34
  50.8 2.4 %collective-permute-done.7 = f32[8,512]{1,0:T(8,128)S(1)} collective-permute-done((f32[8,512]{1,0:T(8,128)S(1)}, f32[8,512]{1,0:T(8,128)S(1)}, u32[]{:S(2)}, u32[]{:S(2)}) %collective-permute-start.7) | collective-permute-done | bytes 16416 | tf_op jit(solution)/shard_map/ppermute | solution.py:34
  54.6 12.3 %collective-permute-done.4 = f32[512,256]{0,1:T(8,128)S(1)} collective-permute-done((f32[512,256]{0,1:T(8,128)S(1)}, f32[512,256]{0,1:T(8,128)S(1)}, u32[]{:S(2)}, u32[]{:S(2)}) %collective-permute-start.4) | collective-permute-done | bytes 524320 | tf_op jit(solution)/shard_map/ppermute | solution.py:34
  67.1 1.8 %collective-permute-start.6 = (f32[512,256]{0,1:T(8,128)S(1)}, f32[512,256]{0,1:T(8,128)S(1)}, u32[]{:S(2)}, u32[]{:S(2)}) collective-permute-start(f32[512,256]{0,1:T(8,128)S(1)} %fusion.34), channel_id=1, source_target_pairs={{0,16},{4,20},{8,24},{12,28},{16,0},{20,4},{24,8},{28,12},{1,17},{... | collective-permute-start | bytes 1572872 | tf_op jit(solution)/shard_map/ppermute | solution.py:34
  69.1 1.8 %all-gather = s32[2,1,256]{2,1,0:T(1,128)S(1)} all-gather(s32[1,1,256]{2,1,0:T(1,128)S(1)} %bitcast.95), channel_id=1, replica_groups=mesh['phi'=8,'query'=2,'event'=2] {'query'}, dimensions={0}, use_global_device_ids=true | all-gather | bytes 3072 | tf_op jit(solution)/shard_map/all_gather | solution.py:186
  70.9 2.2 %all_gather.10 = bf16[512,256]{0,1:T(8,128)(2,1)S(1)} all-gather(bf16[256,256]{0,1:T(8,128)(2,1)S(1)} %get-tuple-element.52), channel_id=1, replica_groups=mesh['phi'=8,'query'=2,'event'=2] {'query'}, dimensions={0}, use_global_device_ids=true | all-gather | bytes 393216 | tf_op jit(solution)/shard_map/all_gather | solution.py:185
  73.0 18.6 %collective-permute-done.6 = f32[512,256]{0,1:T(8,128)S(1)} collective-permute-done((f32[512,256]{0,1:T(8,128)S(1)}, f32[512,256]{0,1:T(8,128)S(1)}, u32[]{:S(2)}, u32[]{:S(2)}) %collective-permute-start.6) | collective-permute-done | bytes 524320 | tf_op jit(solution)/shard_map/ppermute | solution.py:34
  93.3 1.4 collective-permute-start.11
  95.4 1.3 collective-permute-start.17
  100.6 1.5 %collective-permute-start.13 = (f32[512]{0:T(512)S(1)}, f32[512]{0:T(512)S(1)}, u32[]{:S(2)}, u32[]{:S(2)}) collective-permute-start(f32[512]{0:T(512)S(1)} %add.173), channel_id=1, source_target_pairs={{0,16},{4,20},{8,24},{12,28},{16,0},{20,4},{24,8},{28,12},{1,17},{... | collective-permute-start | bytes 6152 | tf_op jit(solution)/shard_map/ppermute | solution.py:34
  102.1 1.5 %collective-permute-start.16 = (f32[512]{0:T(512)S(1)}, f32[512]{0:T(512)S(1)}, u32[]{:S(2)}, u32[]{:S(2)}) collective-permute-start(f32[512]{0:T(512)S(1)} %add.176), channel_id=1, source_target_pairs={{0,16},{4,20},{8,24},{12,28},{16,0},{20,4},{24,8},{28,12},{1,17},{... | collective-permute-start | bytes 6152 | tf_op jit(solution)/shard_map/ppermute | solution.py:34
  103.6 1.4 collective-permute-start.19
  105.1 1.5 %collective-permute-done.16 = f32[512]{0:T(512)S(1)} collective-permute-done((f32[512]{0:T(512)S(1)}, f32[512]{0:T(512)S(1)}, u32[]{:S(2)}, u32[]{:S(2)}) %collective-permute-start.16) | collective-permute-done | bytes 2080 | tf_op jit(solution)/shard_map/ppermute | solution.py:34
  109.1 1.5 %collective-permute-start.21 = (f32[512,256]{1,0:T(8,128)S(1)}, f32[512,256]{1,0:T(8,128)S(1)}, u32[]{:S(2)}, u32[]{:S(2)}) collective-permute-start(f32[512,256]{1,0:T(8,128)S(1)} %fusion.91), channel_id=1, source_target_pairs={{0,4},{4,0},{8,12},{12,8},{16,20},{20,16},{24,28},{28,24},{1,5},{5... | collective-permute-start | bytes 1572872 | tf_op jit(solution)/shard_map/ppermute | solution.py:34
  110.6 8.6 %collective-permute-done.21 = f32[512,256]{1,0:T(8,128)S(1)} collective-permute-done((f32[512,256]{1,0:T(8,128)S(1)}, f32[512,256]{1,0:T(8,128)S(1)}, u32[]{:S(2)}, u32[]{:S(2)}) %collective-permute-start.21) | collective-permute-done | bytes 524320 | tf_op jit(solution)/shard_map/ppermute | solution.py:34
  119.3 1.4 collective-permute-start.22
  121.0 10.5 %collective-permute-done.22 = f32[512,256]{1,0:T(8,128)S(1)} collective-permute-done((f32[512,256]{1,0:T(8,128)S(1)}, f32[512,256]{1,0:T(8,128)S(1)}, u32[]{:S(2)}, u32[]{:S(2)}) %collective-permute-start.22) | collective-permute-done | bytes 524320 | tf_op jit(solution)/shard_map/ppermute | solution.py:34
  131.5 1.8 %collective-permute-start.23 = (f32[512,256]{1,0:T(8,128)S(1)}, f32[512,256]{1,0:T(8,128)S(1)}, u32[]{:S(2)}, u32[]{:S(2)}) collective-permute-start(f32[512,256]{1,0:T(8,128)S(1)} %add.189), channel_id=1, source_target_pairs={{0,16},{4,20},{8,24},{12,28},{16,0},{20,4},{24,8},{28,12},{1,17},{... | collective-permute-start | bytes 1572872 | tf_op jit(solution)/shard_map/ppermute | solution.py:34
  135.7 13.1 %collective-permute-done.23 = f32[512,256]{1,0:T(8,128)S(1)} collective-permute-done((f32[512,256]{1,0:T(8,128)S(1)}, f32[512,256]{1,0:T(8,128)S(1)}, u32[]{:S(2)}, u32[]{:S(2)}) %collective-permute-start.23) | collective-permute-done | bytes 524320 | tf_op jit(solution)/shard_map/ppermute | solution.py:34
  (106 shorter events, 23.1 us)
Async XLA Ops:
  0.6 22.1 %copy-start = (bf16[1024,256]{1,0:T(8,128)(2,1)S(1)}, bf16[1024,256]{1,0:T(8,128)(2,1)}, u32[]{:S(2)}) copy-start(bf16[1024,256]{1,0:T(8,128)(2,1)} %param.17) | copy-start | bytes 1572868
  3.2 9.6 %collective-permute-start = (bf16[256,512]{1,0:T(8,128)(2,1)S(1)}, bf16[256,512]{1,0:T(8,128)(2,1)S(1)}, u32[]{:S(2)}, u32[]{:S(2)}) collective-permute-start(bf16[256,512]{1,0:T(8,128)(2,1)S(1)} %slice.32), channel_id=1, source_target_pairs={{0,2},{2,4},{4,6},{6,8},{8,10},{10,12},{12,14},{14,16},{16,18},{18... | collective-permute-start | bytes 786440 | tf_op jit(solution)/shard_map/ppermute | solution.py:16
  3.7 9.1 %collective-permute-start.1 = (bf16[256,512]{1,0:T(8,128)(2,1)S(1)}, bf16[256,512]{1,0:T(8,128)(2,1)S(1)}, u32[]{:S(2)}, u32[]{:S(2)}) collective-permute-start(bf16[256,512]{1,0:T(8,128)(2,1)S(1)} %slice.32), channel_id=1, source_target_pairs={{2,0},{4,2},{6,4},{8,6},{10,8},{12,10},{14,12},{16,14},{18,16},{20... | collective-permute-start | bytes 786440 | tf_op jit(solution)/shard_map/ppermute | solution.py:19
  29.3 11.9 %collective-permute-start.3 = (f32[8,512]{1,0:T(8,128)S(1)}, f32[8,512]{1,0:T(8,128)S(1)}, u32[]{:S(2)}, u32[]{:S(2)}) collective-permute-start(f32[8,512]{1,0:T(8,128)S(1)} %get-tuple-element.53), channel_id=1, source_target_pairs={{0,4},{4,0},{8,12},{12,8},{16,20},{20,16},{24,28},{28,24},{1,5},{5... | collective-permute-start | bytes 49160 | tf_op jit(solution)/shard_map/ppermute | solution.py:34
  33.9 7.3 %collective-permute-start.8 = (f32[8,512]{1,0:T(8,128)S(1)}, f32[8,512]{1,0:T(8,128)S(1)}, u32[]{:S(2)}, u32[]{:S(2)}) collective-permute-start(f32[8,512]{1,0:T(8,128)S(1)} %convert_reduce_fusion), channel_id=1, source_target_pairs={{0,4},{4,0},{8,12},{12,8},{16,20},{20,16},{24,28},{28,24},{1,5},{5... | collective-permute-start | bytes 49160 | tf_op jit(solution)/shard_map/ppermute | solution.py:34
  34.3 34.7 %copy-start.2 = (bf16[512,256]{1,0:T(8,128)(2,1)S(1)}, bf16[512,256]{1,0:T(8,128)(2,1)}, u32[]{:S(2)}) copy-start(bf16[512,256]{1,0:T(8,128)(2,1)} %param.18) | copy-start | bytes 786436
  34.3 34.8 %copy-start.8 = (s32[256]{0:T(256)S(1)}, s32[256]{0:T(256)}, u32[]{:S(2)}) copy-start(s32[256]{0:T(256)} %param.24) | copy-start | bytes 3076
  34.3 36.6 %copy-start.7 = (s32[512]{0:T(512)S(1)}, s32[512]{0:T(512)}, u32[]{:S(2)}) copy-start(s32[512]{0:T(512)} %param.25) | copy-start | bytes 6148
  34.3 57.5 %copy-start.6 = (bf16[256,256]{1,0:T(8,128)(2,1)S(1)}, bf16[256,256]{1,0:T(8,128)(2,1)}, u32[]{:S(2)}) copy-start(bf16[256,256]{1,0:T(8,128)(2,1)} %param.21) | copy-start | bytes 393220
  34.3 57.9 %copy-start.10 = (bf16[256,256]{1,0:T(8,128)(2,1)S(1)}, bf16[256,256]{1,0:T(8,128)(2,1)}, u32[]{:S(2)}) copy-start(bf16[256,256]{1,0:T(8,128)(2,1)} %param.23) | copy-start | bytes 393220
  34.3 57.9 %copy-start.11 = (bf16[256,256]{1,0:T(8,128)(2,1)S(1)}, bf16[256,256]{1,0:T(8,128)(2,1)}, u32[]{:S(2)}) copy-start(bf16[256,256]{1,0:T(8,128)(2,1)} %param.22) | copy-start | bytes 393220
  39.3 14.2 %collective-permute-start.2 = (f32[512,256]{0,1:T(8,128)S(1)}, f32[512,256]{0,1:T(8,128)S(1)}, u32[]{:S(2)}, u32[]{:S(2)}) collective-permute-start(f32[512,256]{0,1:T(8,128)S(1)} %bitcast.85), channel_id=1, source_target_pairs={{0,4},{4,0},{8,12},{12,8},{16,20},{20,16},{24,28},{28,24},{1,5},{5... | collective-permute-start | bytes 1572872 | tf_op jit(solution)/shard_map/ppermute | solution.py:34
  41.3 3.8 %collective-permute-start.5 = (f32[8,512]{1,0:T(8,128)S(1)}, f32[8,512]{1,0:T(8,128)S(1)}, u32[]{:S(2)}, u32[]{:S(2)}) collective-permute-start(f32[8,512]{1,0:T(8,128)S(1)} %get-tuple-element.30), channel_id=1, source_target_pairs={{0,8},{4,12},{8,0},{12,4},{16,24},{20,28},{24,16},{28,20},{1,9},{5... | collective-permute-start | bytes 49160 | tf_op jit(solution)/shard_map/ppermute | solution.py:34
  42.1 3.7 %collective-permute-start.9 = (f32[8,512]{1,0:T(8,128)S(1)}, f32[8,512]{1,0:T(8,128)S(1)}, u32[]{:S(2)}, u32[]{:S(2)}) collective-permute-start(f32[8,512]{1,0:T(8,128)S(1)} %get-tuple-element.29), channel_id=1, source_target_pairs={{0,8},{4,12},{8,0},{12,4},{16,24},{20,28},{24,16},{28,20},{1,9},{5... | collective-permute-start | bytes 49160 | tf_op jit(solution)/shard_map/ppermute | solution.py:34
  45.8 4.9 %collective-permute-start.10 = (f32[8,512]{1,0:T(8,128)S(1)}, f32[8,512]{1,0:T(8,128)S(1)}, u32[]{:S(2)}, u32[]{:S(2)}) collective-permute-start(f32[8,512]{1,0:T(8,128)S(1)} %get-tuple-element.27), channel_id=1, source_target_pairs={{0,16},{4,20},{8,24},{12,28},{16,0},{20,4},{24,8},{28,12},{1,17},{... | collective-permute-start | bytes 49160 | tf_op jit(solution)/shard_map/ppermute | solution.py:34
  48.5 4.7 %collective-permute-start.7 = (f32[8,512]{1,0:T(8,128)S(1)}, f32[8,512]{1,0:T(8,128)S(1)}, u32[]{:S(2)}, u32[]{:S(2)}) collective-permute-start(f32[8,512]{1,0:T(8,128)S(1)} %get-tuple-element.28), channel_id=1, source_target_pairs={{0,16},{4,20},{8,24},{12,28},{16,0},{20,4},{24,8},{28,12},{1,17},{... | collective-permute-start | bytes 49160 | tf_op jit(solution)/shard_map/ppermute | solution.py:34
  53.6 13.4 %collective-permute-start.4 = (f32[512,256]{0,1:T(8,128)S(1)}, f32[512,256]{0,1:T(8,128)S(1)}, u32[]{:S(2)}, u32[]{:S(2)}) collective-permute-start(f32[512,256]{0,1:T(8,128)S(1)} %fusion.35), channel_id=1, source_target_pairs={{0,8},{4,12},{8,0},{12,4},{16,24},{20,28},{24,16},{28,20},{1,9},{5... | collective-permute-start | bytes 1572872 | tf_op jit(solution)/shard_map/ppermute | solution.py:34
  67.1 24.5 %collective-permute-start.6 = (f32[512,256]{0,1:T(8,128)S(1)}, f32[512,256]{0,1:T(8,128)S(1)}, u32[]{:S(2)}, u32[]{:S(2)}) collective-permute-start(f32[512,256]{0,1:T(8,128)S(1)} %fusion.34), channel_id=1, source_target_pairs={{0,16},{4,20},{8,24},{12,28},{16,0},{20,4},{24,8},{28,12},{1,17},{... | collective-permute-start | bytes 1572872 | tf_op jit(solution)/shard_map/ppermute | solution.py:34
  92.6 28.3 %copy-start.3 = (bf16[512,256]{1,0:T(8,128)(2,1)}, bf16[512,256]{1,0:T(8,128)(2,1)S(1)}, u32[]{:S(2)}) copy-start(bf16[512,256]{1,0:T(8,128)(2,1)S(1)} %convolution_convert_fusion.1) | copy-start | bytes 786436
  93.3 3.7 %collective-permute-start.11 = (f32[512]{0:T(512)S(1)}, f32[512]{0:T(512)S(1)}, u32[]{:S(2)}, u32[]{:S(2)}) collective-permute-start(f32[512]{0:T(512)S(1)} %get-tuple-element.21), channel_id=1, source_target_pairs={{0,4},{4,0},{8,12},{12,8},{16,20},{20,16},{24,28},{28,24},{1,5},{5... | collective-permute-start | bytes 6152 | tf_op jit(solution)/shard_map/ppermute | solution.py:34
  94.7 3.6 %collective-permute-start.14 = (f32[512]{0:T(512)S(1)}, f32[512]{0:T(512)S(1)}, u32[]{:S(2)}, u32[]{:S(2)}) collective-permute-start(f32[512]{0:T(512)S(1)} %get-tuple-element.22), channel_id=1, source_target_pairs={{0,4},{4,0},{8,12},{12,8},{16,20},{20,16},{24,28},{28,24},{1,5},{5... | collective-permute-start | bytes 6152 | tf_op jit(solution)/shard_map/ppermute | solution.py:34
  95.4 3.6 %collective-permute-start.17 = (f32[512]{0:T(512)S(1)}, f32[512]{0:T(512)S(1)}, u32[]{:S(2)}, u32[]{:S(2)}) collective-permute-start(f32[512]{0:T(512)S(1)} %get-tuple-element.20), channel_id=1, source_target_pairs={{0,4},{4,0},{8,12},{12,8},{16,20},{20,16},{24,28},{28,24},{1,5},{5... | collective-permute-start | bytes 6152 | tf_op jit(solution)/shard_map/ppermute | solution.py:34
  97.0 3.6 %collective-permute-start.12 = (f32[512]{0:T(512)S(1)}, f32[512]{0:T(512)S(1)}, u32[]{:S(2)}, u32[]{:S(2)}) collective-permute-start(f32[512]{0:T(512)S(1)} %add.172), channel_id=1, source_target_pairs={{0,8},{4,12},{8,0},{12,4},{16,24},{20,28},{24,16},{28,20},{1,9},{5... | collective-permute-start | bytes 6152 | tf_op jit(solution)/shard_map/ppermute | solution.py:34
  98.3 3.8 %collective-permute-start.15 = (f32[512]{0:T(512)S(1)}, f32[512]{0:T(512)S(1)}, u32[]{:S(2)}, u32[]{:S(2)}) collective-permute-start(f32[512]{0:T(512)S(1)} %add.175), channel_id=1, source_target_pairs={{0,8},{4,12},{8,0},{12,4},{16,24},{20,28},{24,16},{28,20},{1,9},{5... | collective-permute-start | bytes 6152 | tf_op jit(solution)/shard_map/ppermute | solution.py:34
  99.0 4.6 %collective-permute-start.18 = (f32[512]{0:T(512)S(1)}, f32[512]{0:T(512)S(1)}, u32[]{:S(2)}, u32[]{:S(2)}) collective-permute-start(f32[512]{0:T(512)S(1)} %add.180), channel_id=1, source_target_pairs={{0,8},{4,12},{8,0},{12,4},{16,24},{20,28},{24,16},{28,20},{1,9},{5... | collective-permute-start | bytes 6152 | tf_op jit(solution)/shard_map/ppermute | solution.py:34
  100.6 4.5 %collective-permute-start.13 = (f32[512]{0:T(512)S(1)}, f32[512]{0:T(512)S(1)}, u32[]{:S(2)}, u32[]{:S(2)}) collective-permute-start(f32[512]{0:T(512)S(1)} %add.173), channel_id=1, source_target_pairs={{0,16},{4,20},{8,24},{12,28},{16,0},{20,4},{24,8},{28,12},{1,17},{... | collective-permute-start | bytes 6152 | tf_op jit(solution)/shard_map/ppermute | solution.py:34
  102.1 4.5 %collective-permute-start.16 = (f32[512]{0:T(512)S(1)}, f32[512]{0:T(512)S(1)}, u32[]{:S(2)}, u32[]{:S(2)}) collective-permute-start(f32[512]{0:T(512)S(1)} %add.176), channel_id=1, source_target_pairs={{0,16},{4,20},{8,24},{12,28},{16,0},{20,4},{24,8},{28,12},{1,17},{... | collective-permute-start | bytes 6152 | tf_op jit(solution)/shard_map/ppermute | solution.py:34
  103.6 4.5 %collective-permute-start.19 = (f32[512]{0:T(512)S(1)}, f32[512]{0:T(512)S(1)}, u32[]{:S(2)}, u32[]{:S(2)}) collective-permute-start(f32[512]{0:T(512)S(1)} %add.181), channel_id=1, source_target_pairs={{0,16},{4,20},{8,24},{12,28},{16,0},{20,4},{24,8},{28,12},{1,17},{... | collective-permute-start | bytes 6152 | tf_op jit(solution)/shard_map/ppermute | solution.py:34
  109.1 10.1 %collective-permute-start.21 = (f32[512,256]{1,0:T(8,128)S(1)}, f32[512,256]{1,0:T(8,128)S(1)}, u32[]{:S(2)}, u32[]{:S(2)}) collective-permute-start(f32[512,256]{1,0:T(8,128)S(1)} %fusion.91), channel_id=1, source_target_pairs={{0,4},{4,0},{8,12},{12,8},{16,20},{20,16},{24,28},{28,24},{1,5},{5... | collective-permute-start | bytes 1572872 | tf_op jit(solution)/shard_map/ppermute | solution.py:34
  119.3 12.2 %collective-permute-start.22 = (f32[512,256]{1,0:T(8,128)S(1)}, f32[512,256]{1,0:T(8,128)S(1)}, u32[]{:S(2)}, u32[]{:S(2)}) collective-permute-start(f32[512,256]{1,0:T(8,128)S(1)} %add.188), channel_id=1, source_target_pairs={{0,8},{4,12},{8,0},{12,4},{16,24},{20,28},{24,16},{28,20},{1,9},{5... | collective-permute-start | bytes 1572872 | tf_op jit(solution)/shard_map/ppermute | solution.py:34
  131.5 17.2 %collective-permute-start.23 = (f32[512,256]{1,0:T(8,128)S(1)}, f32[512,256]{1,0:T(8,128)S(1)}, u32[]{:S(2)}, u32[]{:S(2)}) collective-permute-start(f32[512,256]{1,0:T(8,128)S(1)} %add.189), channel_id=1, source_target_pairs={{0,16},{4,20},{8,24},{12,28},{16,0},{20,4},{24,8},{28,12},{1,17},{... | collective-permute-start | bytes 1572872 | tf_op jit(solution)/shard_map/ppermute | solution.py:34
  133.4 1.6 %collective-permute-start.20 = (f32[256,256]{1,0:T(8,128)S(1)}, f32[256,256]{1,0:T(8,128)S(1)}, u32[]{:S(2)}, u32[]{:S(2)}) collective-permute-start(f32[256,256]{1,0:T(8,128)S(1)} %slice_select_fusion), channel_id=1, source_target_pairs={{0,2},{2,0},{1,3},{3,1},{4,6},{6,4},{5,7},{7,5},{8,10},{10,8},{9,1... | collective-permute-start | bytes 786440 | tf_op jit(solution)/shard_map/ppermute | solution.py:74
  (4 other events, 16.9 us)

commit v2 on v1

--- a/solution.py
+++ b/solution.py
@@ -47,16 +47,29 @@
     return jax.tree.map(jnp.add, a, b)
 
 
+def narrow_butterfly(block, axis):
+    count = lax.axis_size(axis)
+    distance = 1
+    while distance < count:
+        sent = block.astype(jnp.bfloat16)
+        other = lax.ppermute(sent, axis, partner_pairs(count, distance))
+        block = sent.astype(jnp.float32) + other.astype(jnp.float32)
+        distance *= 2
+    return block
+
+
 def softmax_combine(a, b):
     max_a, total_a, mixed_a = a
     max_b, total_b, mixed_b = b
+    mixed_a = mixed_a.astype(jnp.float32)
+    mixed_b = mixed_b.astype(jnp.float32)
     top = jnp.maximum(max_a, max_b)
     factor_a = jnp.exp(max_a - top)
     factor_b = jnp.exp(max_b - top)
     return (
         top,
         total_a * factor_a + total_b * factor_b,
-        scale_heads(mixed_a, factor_a) + scale_heads(mixed_b, factor_b),
+        (scale_heads(mixed_a, factor_a) + scale_heads(mixed_b, factor_b)).astype(jnp.bfloat16),
     )
 
 
@@ -180,11 +193,16 @@
     local_kv = jnp.dot(
         norm_rows(encoded).astype(jnp.bfloat16), cross_kv, preferred_element_type=jnp.float32
     ).astype(jnp.bfloat16)
-    group_kv, group_hits, group_truth = (
-        lax.all_gather(local_kv, "query", axis=0, tiled=True),
-        lax.all_gather(encoded, "query", axis=0, tiled=True),
-        lax.all_gather(truth, "query", axis=0, tiled=True),
-    )
+    shifted = truth + 1
+    digits = jnp.stack([shifted // 256, shifted % 256], axis=1).astype(jnp.bfloat16)
+    digits = jnp.pad(digits, ((0, 0), (0, 126)))
+    gathered = lax.all_gather(
+        jnp.concatenate([local_kv, encoded, digits], axis=1), "query", axis=0, tiled=True
+    )
+    group_kv = gathered[:, : 2 * model_width]
+    group_hits = gathered[:, 2 * model_width : 3 * model_width]
+    group_digits = gathered[:, 3 * model_width :].astype(jnp.int32)
+    group_truth = group_digits[:, 0] * 256 + group_digits[:, 1] - 1
     query_proj = jnp.dot(queries, cross_q, preferred_element_type=jnp.float32).astype(jnp.bfloat16)
     head_size = model_width // HEADS
     group_count = group_kv.shape[0]
@@ -201,8 +219,12 @@
         "hqk,khd->qhd", raised, value_heads, preferred_element_type=jnp.float32
     ).reshape(query_count, model_width)
     _, total, mixed = butterfly(
-        (local_max, local_total, local_mixed), "phi", softmax_combine, ordered=True
-    )
+        (local_max, local_total, local_mixed.astype(jnp.bfloat16)),
+        "phi",
+        softmax_combine,
+        ordered=True,
+    )
+    mixed = mixed.astype(jnp.float32)
     context = scale_heads(mixed, 1.0 / total).astype(jnp.bfloat16)
     mixed_queries = queries.astype(jnp.float32) + jnp.dot(
         context, cross_out, preferred_element_type=jnp.float32
@@ -235,8 +257,8 @@
     coef = loss_coefficients(
         sigma, target, matched, intersection, predicted, truth_count, hits_total, model_width
     )
-    mask_grad = butterfly(
-        jnp.dot(coef, group_hits, preferred_element_type=jnp.float32), "phi", add_trees
+    mask_grad = narrow_butterfly(
+        jnp.dot(coef, group_hits, preferred_element_type=jnp.float32), "phi"
     )
     hit_grad = reduce_scatter_rows(
         lax.dot_general(

time: 150 us -> 107 us (0.71)
  waiting for transfers between devices: 77.7 us -> 44.8 us
  local copies, waits for them, and re-layouts: 5.92 us -> 2.38 us
  matrix products: 21.3 us -> 17.8 us
  blocking collectives: 7.84 us -> 4.35 us
    ppermute x21 -> x18, waiting for transfers between devices: 74.3 us -> 23.8 us  [butterfly(): other = lax.ppermute(tree, axis, partner_pairs(count, distance))]
    ppermute x0 -> x3, waiting for transfers between devices: none -> 19.2 us  [narrow_butterfly(): other = lax.ppermute(sent, axis, partner_pairs(count, distance))]
    ppermute x21 -> x18, starting transfers between devices: 24.9 us -> 21 us  [butterfly(): other = lax.ppermute(tree, axis, partner_pairs(count, distance))]
    ppermute x0 -> x3, starting transfers between devices: none -> 3.78 us  [narrow_butterfly(): other = lax.ppermute(sent, axis, partner_pairs(count, distance))]
    unnamed x27 -> x25, local copies, waits for them, and re-layouts: 5.08 us -> 1.38 us
    all_gather x3 -> x1, blocking collectives: 7.84 us -> 4.35 us  [body(): lax.all_gather(jnp.concatenate([local_kv, encoded, digits], axis=1), 'que...]
    dot_general x1, matrix products: 4.97 us -> 1.51 us  [body(): jnp.einsum('hqk,khd->qhd', raised, value_heads, preferred_element_type=jn...]
  transfers between devices with their start and end apart: 24 -> 24, of which waited for: 17 -> 14; matrix products, arithmetic and copies ran while one was open for 7% -> 7% of each run, Pallas kernels for 0% -> 0%
where the time goes in v2:
time: 107 us
  waiting for transfers between devices  44.8 us (42%)
  starting transfers between devices  30.4 us (28%)
  matrix products  17.8 us (17%)
  other arithmetic  6.39 us (6%)
  blocking collectives  4.35 us (4%)
  local copies, waits for them, and re-layouts  2.38 us (2%)
  between operations  1.11 us (1%)
    ppermute x18, waiting for transfers between devices, butterfly(): other = lax.ppermute(tree, axis, partner_pairs(count, distance))  23.8 us
    ppermute x18, starting transfers between devices, butterfly(): other = lax.ppermute(tree, axis, partner_pairs(count, distance))  21 us
    ppermute x3, waiting for transfers between devices, narrow_butterfly(): other = lax.ppermute(sent, axis, partner_pairs(count, distance))  19.2 us
    sub x1, matrix products, window_attend(): raised = jnp.exp(scores - jnp.max(scores, axis=-1, keepdims=True))  5.09 us
    ppermute x1, starting transfers between devices, extended_2(): lax.ppermute(lax.slice_in_dim(block, 0, width, axis=dim), axis, backward)  5.03 us
    all_gather x1, blocking collectives, body(): lax.all_gather(jnp.concatenate([local_kv, encoded, digits], axis=1), 'que...  4.35 us
    dot_general x1, matrix products, window_attend(): jnp.einsum('hqk,khd->qhd', weights, value_heads, preferred_element_type=j...  3.97 us
    ppermute x3, starting transfers between devices, narrow_butterfly(): other = lax.ppermute(sent, axis, partner_pairs(count, distance))  3.78 us
  transfers between devices with their start and end apart: 24, of which 14 were waited for; matrix products, arithmetic and copies ran while one was open for 7% of the time, Pallas kernels for 0%

profile of v2, /device:TPU:0, one launch (start us, length us, event | category | flops | bytes accessed | tf_op | source)
XLA Modules:
  0.0 107.3 jit_solution(1000669311964911300)
XLA Ops:
  1.9 1.3 %convolution_convert_fusion = bf16[256,768]{1,0:T(8,128)(2,1)S(1)} fusion(bf16[256,768]{1,0:T(8,128)(2,1)} %param.14, bf16[256,256]{0,1:T(8,128)(2,1)S(1)} %copy.40, f32[256]{0:T(256)S(1)} %add_rsqrt_fusion.3, f32[256]{0:T(256)S(1)} %broadcast_multiply_fusion.4), kind=kOutput, calls=%fused_computation.20 | convolution fusion | flops 101122048 | bytes 919552 | tf_op jit(solution)/shard_map/dot_general | solution.py:178
  3.7 5.0 %collective-permute-start.1 = (bf16[256,512]{1,0:T(8,128)(2,1)S(1)}, bf16[256,512]{1,0:T(8,128)(2,1)S(1)}, u32[]{:S(2)}, u32[]{:S(2)}) collective-permute-start(bf16[256,512]{1,0:T(8,128)(2,1)S(1)} %slice.51), channel_id=1, source_target_pairs={{2,0},{4,2},{6,4},{8,6},{10,8},{12,10},{14,12},{16,14},{18,16},{20... | collective-permute-start | bytes 786440 | tf_op jit(solution)/shard_map/ppermute | solution.py:19
  9.8 1.2 %convolution_convert_fusion.4 = bf16[512,256]{0,1:T(8,128)(2,1)S(1)} fusion(bf16[512,256]{1,0:T(8,128)(2,1)} %param.18, bf16[256,256]{1,0:T(8,128)(2,1)} %param.19), kind=kOutput, calls=%fused_computation.26 | convolution fusion | flops 67239936 | bytes 655360 | tf_op jit(solution)/shard_map/dot_general | solution.py:206
  11.1 1.7 %collective-permute-done = bf16[256,512]{1,0:T(8,128)(2,1)S(1)} collective-permute-done((bf16[256,512]{1,0:T(8,128)(2,1)S(1)}, bf16[256,512]{1,0:T(8,128)(2,1)S(1)}, u32[]{:S(2)}, u32[]{:S(2)}) %collective-permute-start) | collective-permute-done | bytes 262176 | tf_op jit(solution)/shard_map/ppermute | solution.py:16
  13.3 5.1 %fusion.97 = (f32[8,256]{1,0:T(8,128)S(1)}, f32[8,256,768]{2,1,0:T(8,128)}) fusion(pred[256,768]{1,0:T(8,128)(4,1)S(1)} %fusion.28, bf16[256,8,32]{0,2,1:T(8,128)(2,1)S(1)} %bitcast.96, bf16[768,8,32]{0,2,1:T(8,128)(2,1)S(1)} %bitcast.93), kind=kOutput, calls=%fused_computation.171 | convolution fusion | flops 106955520 | bytes 7020544 | tf_op jit(solution)/shard_map/sub | solution.py:115
  18.4 4.0 %fusion.12 = bf16[8,32,256]{2,1,0:T(8,128)(2,1)S(1)} fusion(bf16[768,8,32]{0,2,1:T(8,128)(2,1)S(1)} %bitcast.94, f32[8,256,768]{2,1,0:T(8,128)} %get-tuple-element.48, f32[8,256]{1,0:T(8,128)S(1)} %get-tuple-element.47), kind=kOutput, calls=%fused_computation.32 | convolution fusion | flops 103874560 | bytes 6823936 | tf_op jit(solution)/shard_map/hqk,khd->qhd/dot_general | solution.py:117
  24.1 4.3 %all_gather.3 = bf16[512,896]{1,0:T(8,128)(2,1)S(1)} all-gather(bf16[256,896]{1,0:T(8,128)(2,1)S(1)} %fusion.43), channel_id=1, replica_groups=mesh['phi'=8,'query'=2,'event'=2] {'query'}, dimensions={0}, use_global_device_ids=true | all-gather | bytes 1376256 | tf_op jit(solution)/shard_map/all_gather | solution.py:199
  28.8 1.3 %multiply_reduce_fusion = (f32[8,512]{1,0:T(8,128)S(1)}, f32[8,512,512]{1,2,0:T(8,128)S(1)}) fusion(bf16[512,8,32]{0,2,1:T(8,128)(2,1)S(1)} %bitcast.89, bf16[512,8,32]{0,2,1:T(8,128)(2,1)S(1)} %bitcast.91), kind=kOutput, calls=%fused_computation.3 | convolution fusion | flops 138407936 | bytes 8929280 | tf_op jit(solution)/shard_map/qhd,khd->hqk/dot_general | solution.py:212
  30.2 1.4 %convert_reduce_fusion = f32[8,512]{1,0:T(8,128)S(1)} fusion(f32[8,512]{1,0:T(8,128)S(1)} %get-tuple-element.53, f32[8,512,512]{1,2,0:T(8,128)S(1)} %get-tuple-element.54), kind=kLoop, calls=%fused_computation.1 | loop fusion | flops 10481664 | bytes 8421376 | tf_op jit(solution)/shard_map/reduce_sum | solution.py:217
  31.7 1.5 %convolution_convert_fusion.3 = bf16[8,32,512]{2,1,0:T(8,128)(2,1)S(1)} fusion(bf16[512,8,32]{0,2,1:T(8,128)(2,1)S(1)} %bitcast.90, f32[8,512,512]{1,2,0:T(8,128)S(1)} %get-tuple-element.54, f32[8,512]{1,0:T(8,128)S(1)} %get-tuple-element.53), kind=kOutput, calls=%fused_computation.25 | convolution fusion | flops 140640256 | bytes 8929280 | tf_op jit(solution)/shard_map/hqk,khd->qhd/dot_general | solution.py:218
  33.2 2.0 %collective-permute-start.2 = (bf16[512,256]{0,1:T(8,128)(2,1)S(1)}, bf16[512,256]{0,1:T(8,128)(2,1)S(1)}, u32[]{:S(2)}, u32[]{:S(2)}) collective-permute-start(bf16[512,256]{0,1:T(8,128)(2,1)S(1)} %bitcast.92), channel_id=1, source_target_pairs={{0,4},{4,0},{8,12},{12,8},{16,20},{20,16},{24,28},{28,24},{1,5},{5... | collective-permute-start | bytes 786440 | tf_op jit(solution)/shard_map/ppermute | solution.py:34
  35.3 1.3 %collective-permute-start.5 = (f32[8,512]{1,0:T(8,128)S(1)}, f32[8,512]{1,0:T(8,128)S(1)}, u32[]{:S(2)}, u32[]{:S(2)}) collective-permute-start(f32[8,512]{1,0:T(8,128)S(1)} %get-tuple-element.30), channel_id=1, source_target_pairs={{0,8},{4,12},{8,0},{12,4},{16,24},{20,28},{24,16},{28,20},{1,9},{5... | collective-permute-start | bytes 49160 | tf_op jit(solution)/shard_map/ppermute | solution.py:34
  36.7 5.4 %collective-permute-done.8 = f32[8,512]{1,0:T(8,128)S(1)} collective-permute-done((f32[8,512]{1,0:T(8,128)S(1)}, f32[8,512]{1,0:T(8,128)S(1)}, u32[]{:S(2)}, u32[]{:S(2)}) %collective-permute-start.8) | collective-permute-done | bytes 16416 | tf_op jit(solution)/shard_map/ppermute | solution.py:34
  43.3 1.1 %collective-permute-start.4 = (bf16[512,256]{0,1:T(8,128)(2,1)S(1)}, bf16[512,256]{0,1:T(8,128)(2,1)S(1)}, u32[]{:S(2)}, u32[]{:S(2)}) collective-permute-start(bf16[512,256]{0,1:T(8,128)(2,1)S(1)} %fusion.38), channel_id=1, source_target_pairs={{0,8},{4,12},{8,0},{12,4},{16,24},{20,28},{24,16},{28,20},{1,9},{5... | collective-permute-start | bytes 786440 | tf_op jit(solution)/shard_map/ppermute | solution.py:34
  44.5 2.1 %collective-permute-start.7 = (f32[8,512]{1,0:T(8,128)S(1)}, f32[8,512]{1,0:T(8,128)S(1)}, u32[]{:S(2)}, u32[]{:S(2)}) collective-permute-start(f32[8,512]{1,0:T(8,128)S(1)} %get-tuple-element.43), channel_id=1, source_target_pairs={{0,16},{4,20},{8,24},{12,28},{16,0},{20,4},{24,8},{28,12},{1,17},{... | collective-permute-start | bytes 49160 | tf_op jit(solution)/shard_map/ppermute | solution.py:34
  46.6 1.6 %collective-permute-start.10 = (f32[8,512]{1,0:T(8,128)S(1)}, f32[8,512]{1,0:T(8,128)S(1)}, u32[]{:S(2)}, u32[]{:S(2)}) collective-permute-start(f32[8,512]{1,0:T(8,128)S(1)} %get-tuple-element.38), channel_id=1, source_target_pairs={{0,16},{4,20},{8,24},{12,28},{16,0},{20,4},{24,8},{28,12},{1,17},{... | collective-permute-start | bytes 49160 | tf_op jit(solution)/shard_map/ppermute | solution.py:34
  48.2 3.3 %collective-permute-done.4 = bf16[512,256]{0,1:T(8,128)(2,1)S(1)} collective-permute-done((bf16[512,256]{0,1:T(8,128)(2,1)S(1)}, bf16[512,256]{0,1:T(8,128)(2,1)S(1)}, u32[]{:S(2)}, u32[]{:S(2)}) %collective-permute-start.4) | collective-permute-done | bytes 262176 | tf_op jit(solution)/shard_map/ppermute | solution.py:34
  51.6 2.3 %collective-permute-start.6 = (bf16[512,256]{0,1:T(8,128)(2,1)S(1)}, bf16[512,256]{0,1:T(8,128)(2,1)S(1)}, u32[]{:S(2)}, u32[]{:S(2)}) collective-permute-start(bf16[512,256]{0,1:T(8,128)(2,1)S(1)} %fusion.36), channel_id=1, source_target_pairs={{0,16},{4,20},{8,24},{12,28},{16,0},{20,4},{24,8},{28,12},{1,17},{... | collective-permute-start | bytes 786440 | tf_op jit(solution)/shard_map/ppermute | solution.py:34
  54.2 10.5 %collective-permute-done.6 = bf16[512,256]{0,1:T(8,128)(2,1)S(1)} collective-permute-done((bf16[512,256]{0,1:T(8,128)(2,1)S(1)}, bf16[512,256]{0,1:T(8,128)(2,1)S(1)}, u32[]{:S(2)}, u32[]{:S(2)}) %collective-permute-start.6) | collective-permute-done | bytes 262176 | tf_op jit(solution)/shard_map/ppermute | solution.py:34
  66.4 1.4 %collective-permute-start.11 = (f32[512]{0:T(512)S(1)}, f32[512]{0:T(512)S(1)}, u32[]{:S(2)}, u32[]{:S(2)}) collective-permute-start(f32[512]{0:T(512)S(1)} %get-tuple-element.21), channel_id=1, source_target_pairs={{0,4},{4,0},{8,12},{12,8},{16,20},{20,16},{24,28},{28,24},{1,5},{5... | collective-permute-start | bytes 6152 | tf_op jit(solution)/shard_map/ppermute | solution.py:34
  68.5 1.3 %collective-permute-start.17 = (f32[512]{0:T(512)S(1)}, f32[512]{0:T(512)S(1)}, u32[]{:S(2)}, u32[]{:S(2)}) collective-permute-start(f32[512]{0:T(512)S(1)} %get-tuple-element.20), channel_id=1, source_target_pairs={{0,4},{4,0},{8,12},{12,8},{16,20},{20,16},{24,28},{28,24},{1,5},{5... | collective-permute-start | bytes 6152 | tf_op jit(solution)/shard_map/ppermute | solution.py:34
  70.1 1.3 %collective-permute-done.14 = f32[512]{0:T(512)S(1)} collective-permute-done((f32[512]{0:T(512)S(1)}, f32[512]{0:T(512)S(1)}, u32[]{:S(2)}, u32[]{:S(2)}) %collective-permute-start.14) | collective-permute-done | bytes 2080 | tf_op jit(solution)/shard_map/ppermute | solution.py:34
  72.1 1.3 %collective-permute-start.18 = (f32[512]{0:T(512)S(1)}, f32[512]{0:T(512)S(1)}, u32[]{:S(2)}, u32[]{:S(2)}) collective-permute-start(f32[512]{0:T(512)S(1)} %add.213), channel_id=1, source_target_pairs={{0,8},{4,12},{8,0},{12,4},{16,24},{20,28},{24,16},{28,20},{1,9},{5... | collective-permute-start | bytes 6152 | tf_op jit(solution)/shard_map/ppermute | solution.py:34
  75.0 1.6 %collective-permute-start.16 = (f32[512]{0:T(512)S(1)}, f32[512]{0:T(512)S(1)}, u32[]{:S(2)}, u32[]{:S(2)}) collective-permute-start(f32[512]{0:T(512)S(1)} %add.209), channel_id=1, source_target_pairs={{0,16},{4,20},{8,24},{12,28},{16,0},{20,4},{24,8},{28,12},{1,17},{... | collective-permute-start | bytes 6152 | tf_op jit(solution)/shard_map/ppermute | solution.py:34
  76.6 1.3 %collective-permute-start.19 = (f32[512]{0:T(512)S(1)}, f32[512]{0:T(512)S(1)}, u32[]{:S(2)}, u32[]{:S(2)}) collective-permute-start(f32[512]{0:T(512)S(1)} %add.214), channel_id=1, source_target_pairs={{0,16},{4,20},{8,24},{12,28},{16,0},{20,4},{24,8},{28,12},{1,17},{... | collective-permute-start | bytes 6152 | tf_op jit(solution)/shard_map/ppermute | solution.py:34
  78.2 1.3 %collective-permute-done.16 = f32[512]{0:T(512)S(1)} collective-permute-done((f32[512]{0:T(512)S(1)}, f32[512]{0:T(512)S(1)}, u32[]{:S(2)}, u32[]{:S(2)}) %collective-permute-start.16) | collective-permute-done | bytes 2080 | tf_op jit(solution)/shard_map/ppermute | solution.py:34
  82.1 1.4 %collective-permute-start.21 = (bf16[512,256]{1,0:T(8,128)(2,1)S(1)}, bf16[512,256]{1,0:T(8,128)(2,1)S(1)}, u32[]{:S(2)}, u32[]{:S(2)}) collective-permute-start(bf16[512,256]{1,0:T(8,128)(2,1)S(1)} %convolution_convert_fusion.1), channel_id=1, source_target_pairs={{0,4},{4,0},{8,12},{12,8},{16,20},{20,16},{24,28},{28,24},{1,5},{5... | collective-permute-start | bytes 786440 | tf_op jit(solution)/shard_map/ppermute | solution.py:55
  83.5 5.0 %collective-permute-done.21 = bf16[512,256]{1,0:T(8,128)(2,1)S(1)} collective-permute-done((bf16[512,256]{1,0:T(8,128)(2,1)S(1)}, bf16[512,256]{1,0:T(8,128)(2,1)S(1)}, u32[]{:S(2)}, u32[]{:S(2)}) %collective-permute-start.21) | collective-permute-done | bytes 262176 | tf_op jit(solution)/shard_map/ppermute | solution.py:55
  88.6 1.1 %collective-permute-start.22 = (bf16[512,256]{1,0:T(8,128)(2,1)S(1)}, bf16[512,256]{1,0:T(8,128)(2,1)S(1)}, u32[]{:S(2)}, u32[]{:S(2)}) collective-permute-start(bf16[512,256]{1,0:T(8,128)(2,1)S(1)} %add_convert_fusion.1), channel_id=1, source_target_pairs={{0,8},{4,12},{8,0},{12,4},{16,24},{20,28},{24,16},{28,20},{1,9},{5... | collective-permute-start | bytes 786440 | tf_op jit(solution)/shard_map/ppermute | solution.py:55
  90.1 6.1 %collective-permute-done.22 = bf16[512,256]{1,0:T(8,128)(2,1)S(1)} collective-permute-done((bf16[512,256]{1,0:T(8,128)(2,1)S(1)}, bf16[512,256]{1,0:T(8,128)(2,1)S(1)}, u32[]{:S(2)}, u32[]{:S(2)}) %collective-permute-start.22) | collective-permute-done | bytes 262176 | tf_op jit(solution)/shard_map/ppermute | solution.py:55
  96.3 1.2 %collective-permute-start.23 = (bf16[512,256]{1,0:T(8,128)(2,1)S(1)}, bf16[512,256]{1,0:T(8,128)(2,1)S(1)}, u32[]{:S(2)}, u32[]{:S(2)}) collective-permute-start(bf16[512,256]{1,0:T(8,128)(2,1)S(1)} %add_convert_fusion), channel_id=1, source_target_pairs={{0,16},{4,20},{8,24},{12,28},{16,0},{20,4},{24,8},{28,12},{1,17},{... | collective-permute-start | bytes 786440 | tf_op jit(solution)/shard_map/ppermute | solution.py:55
  98.3 8.1 %collective-permute-done.23 = bf16[512,256]{1,0:T(8,128)(2,1)S(1)} collective-permute-done((bf16[512,256]{1,0:T(8,128)(2,1)S(1)}, bf16[512,256]{1,0:T(8,128)(2,1)S(1)}, u32[]{:S(2)}, u32[]{:S(2)}) %collective-permute-start.23) | collective-permute-done | bytes 262176 | tf_op jit(solution)/shard_map/ppermute | solution.py:55
  (111 shorter events, 17.0 us)
Async XLA Ops:
  0.6 22.1 %copy-start = (bf16[1024,256]{1,0:T(8,128)(2,1)S(1)}, bf16[1024,256]{1,0:T(8,128)(2,1)}, u32[]{:S(2)}) copy-start(bf16[1024,256]{1,0:T(8,128)(2,1)} %param.17) | copy-start | bytes 1572868
  3.2 9.6 %collective-permute-start = (bf16[256,512]{1,0:T(8,128)(2,1)S(1)}, bf16[256,512]{1,0:T(8,128)(2,1)S(1)}, u32[]{:S(2)}, u32[]{:S(2)}) collective-permute-start(bf16[256,512]{1,0:T(8,128)(2,1)S(1)} %slice.51), channel_id=1, source_target_pairs={{0,2},{2,4},{4,6},{6,8},{8,10},{10,12},{12,14},{14,16},{16,18},{18... | collective-permute-start | bytes 786440 | tf_op jit(solution)/shard_map/ppermute | solution.py:16
  3.7 9.1 %collective-permute-start.1 = (bf16[256,512]{1,0:T(8,128)(2,1)S(1)}, bf16[256,512]{1,0:T(8,128)(2,1)S(1)}, u32[]{:S(2)}, u32[]{:S(2)}) collective-permute-start(bf16[256,512]{1,0:T(8,128)(2,1)S(1)} %slice.51), channel_id=1, source_target_pairs={{2,0},{4,2},{6,4},{8,6},{10,8},{12,10},{14,12},{16,14},{18,16},{20... | collective-permute-start | bytes 786440 | tf_op jit(solution)/shard_map/ppermute | solution.py:19
  18.4 5.4 %copy-start.4 = (bf16[256,512]{1,0:T(8,128)(2,1)S(1)}, bf16[256,512]{1,0:T(8,128)(2,1)}, u32[]{:S(2)}) copy-start(bf16[256,512]{1,0:T(8,128)(2,1)} %param.20) | copy-start | bytes 786436
  23.7 6.4 %copy-start.2 = (bf16[256,256]{1,0:T(8,128)(2,1)}, bf16[256,256]{1,0:T(8,128)(2,1)S(1)}, u32[]{:S(2)}) copy-start(bf16[256,256]{1,0:T(8,128)(2,1)S(1)} %copy.50) | copy-start | bytes 393220
  30.1 5.2 %collective-permute-start.3 = (f32[8,512]{1,0:T(8,128)S(1)}, f32[8,512]{1,0:T(8,128)S(1)}, u32[]{:S(2)}, u32[]{:S(2)}) collective-permute-start(f32[8,512]{1,0:T(8,128)S(1)} %get-tuple-element.53), channel_id=1, source_target_pairs={{0,4},{4,0},{8,12},{12,8},{16,20},{20,16},{24,28},{28,24},{1,5},{5... | collective-permute-start | bytes 49160 | tf_op jit(solution)/shard_map/ppermute | solution.py:34
  31.6 4.9 %copy-start.7 = (s32[512]{0:T(512)S(1)}, s32[512]{0:T(512)}, u32[]{:S(2)}) copy-start(s32[512]{0:T(512)} %param.25) | copy-start | bytes 6148
  31.7 33.2 %copy-start.6 = (bf16[256,256]{1,0:T(8,128)(2,1)S(1)}, bf16[256,256]{1,0:T(8,128)(2,1)}, u32[]{:S(2)}) copy-start(bf16[256,256]{1,0:T(8,128)(2,1)} %param.21) | copy-start | bytes 393220
  31.7 33.6 %copy-start.9 = (bf16[256,256]{1,0:T(8,128)(2,1)S(1)}, bf16[256,256]{1,0:T(8,128)(2,1)}, u32[]{:S(2)}) copy-start(bf16[256,256]{1,0:T(8,128)(2,1)} %param.23) | copy-start | bytes 393220
  31.7 33.6 %copy-start.10 = (bf16[256,256]{1,0:T(8,128)(2,1)S(1)}, bf16[256,256]{1,0:T(8,128)(2,1)}, u32[]{:S(2)}) copy-start(bf16[256,256]{1,0:T(8,128)(2,1)} %param.22) | copy-start | bytes 393220
  33.2 10.0 %collective-permute-start.2 = (bf16[512,256]{0,1:T(8,128)(2,1)S(1)}, bf16[512,256]{0,1:T(8,128)(2,1)S(1)}, u32[]{:S(2)}, u32[]{:S(2)}) collective-permute-start(bf16[512,256]{0,1:T(8,128)(2,1)S(1)} %bitcast.92), channel_id=1, source_target_pairs={{0,4},{4,0},{8,12},{12,8},{16,20},{20,16},{24,28},{28,24},{1,5},{5... | collective-permute-start | bytes 786440 | tf_op jit(solution)/shard_map/ppermute | solution.py:34
  35.2 6.9 %collective-permute-start.8 = (f32[8,512]{1,0:T(8,128)S(1)}, f32[8,512]{1,0:T(8,128)S(1)}, u32[]{:S(2)}, u32[]{:S(2)}) collective-permute-start(f32[8,512]{1,0:T(8,128)S(1)} %convert_reduce_fusion), channel_id=1, source_target_pairs={{0,4},{4,0},{8,12},{12,8},{16,20},{20,16},{24,28},{28,24},{1,5},{5... | collective-permute-start | bytes 49160 | tf_op jit(solution)/shard_map/ppermute | solution.py:34
  35.3 6.8 %collective-permute-start.5 = (f32[8,512]{1,0:T(8,128)S(1)}, f32[8,512]{1,0:T(8,128)S(1)}, u32[]{:S(2)}, u32[]{:S(2)}) collective-permute-start(f32[8,512]{1,0:T(8,128)S(1)} %get-tuple-element.30), channel_id=1, source_target_pairs={{0,8},{4,12},{8,0},{12,4},{16,24},{20,28},{24,16},{28,20},{1,9},{5... | collective-permute-start | bytes 49160 | tf_op jit(solution)/shard_map/ppermute | solution.py:34
  42.1 4.4 %collective-permute-start.9 = (f32[8,512]{1,0:T(8,128)S(1)}, f32[8,512]{1,0:T(8,128)S(1)}, u32[]{:S(2)}, u32[]{:S(2)}) collective-permute-start(f32[8,512]{1,0:T(8,128)S(1)} %get-tuple-element.36), channel_id=1, source_target_pairs={{0,8},{4,12},{8,0},{12,4},{16,24},{20,28},{24,16},{28,20},{1,9},{5... | collective-permute-start | bytes 49160 | tf_op jit(solution)/shard_map/ppermute | solution.py:34
  43.3 8.1 %collective-permute-start.4 = (bf16[512,256]{0,1:T(8,128)(2,1)S(1)}, bf16[512,256]{0,1:T(8,128)(2,1)S(1)}, u32[]{:S(2)}, u32[]{:S(2)}) collective-permute-start(bf16[512,256]{0,1:T(8,128)(2,1)S(1)} %fusion.38), channel_id=1, source_target_pairs={{0,8},{4,12},{8,0},{12,4},{16,24},{20,28},{24,16},{28,20},{1,9},{5... | collective-permute-start | bytes 786440 | tf_op jit(solution)/shard_map/ppermute | solution.py:34
  44.5 9.6 %collective-permute-start.7 = (f32[8,512]{1,0:T(8,128)S(1)}, f32[8,512]{1,0:T(8,128)S(1)}, u32[]{:S(2)}, u32[]{:S(2)}) collective-permute-start(f32[8,512]{1,0:T(8,128)S(1)} %get-tuple-element.43), channel_id=1, source_target_pairs={{0,16},{4,20},{8,24},{12,28},{16,0},{20,4},{24,8},{28,12},{1,17},{... | collective-permute-start | bytes 49160 | tf_op jit(solution)/shard_map/ppermute | solution.py:34
  46.6 7.6 %collective-permute-start.10 = (f32[8,512]{1,0:T(8,128)S(1)}, f32[8,512]{1,0:T(8,128)S(1)}, u32[]{:S(2)}, u32[]{:S(2)}) collective-permute-start(f32[8,512]{1,0:T(8,128)S(1)} %get-tuple-element.38), channel_id=1, source_target_pairs={{0,16},{4,20},{8,24},{12,28},{16,0},{20,4},{24,8},{28,12},{1,17},{... | collective-permute-start | bytes 49160 | tf_op jit(solution)/shard_map/ppermute | solution.py:34
  51.6 13.1 %collective-permute-start.6 = (bf16[512,256]{0,1:T(8,128)(2,1)S(1)}, bf16[512,256]{0,1:T(8,128)(2,1)S(1)}, u32[]{:S(2)}, u32[]{:S(2)}) collective-permute-start(bf16[512,256]{0,1:T(8,128)(2,1)S(1)} %fusion.36), channel_id=1, source_target_pairs={{0,16},{4,20},{8,24},{12,28},{16,0},{20,4},{24,8},{28,12},{1,17},{... | collective-permute-start | bytes 786440 | tf_op jit(solution)/shard_map/ppermute | solution.py:34
  65.7 24.3 %copy-start.3 = (bf16[512,256]{1,0:T(8,128)(2,1)}, bf16[512,256]{1,0:T(8,128)(2,1)S(1)}, u32[]{:S(2)}) copy-start(bf16[512,256]{1,0:T(8,128)(2,1)S(1)} %convolution_convert_fusion.2) | copy-start | bytes 786436
  66.4 3.7 %collective-permute-start.11 = (f32[512]{0:T(512)S(1)}, f32[512]{0:T(512)S(1)}, u32[]{:S(2)}, u32[]{:S(2)}) collective-permute-start(f32[512]{0:T(512)S(1)} %get-tuple-element.21), channel_id=1, source_target_pairs={{0,4},{4,0},{8,12},{12,8},{16,20},{20,16},{24,28},{28,24},{1,5},{5... | collective-permute-start | bytes 6152 | tf_op jit(solution)/shard_map/ppermute | solution.py:34
  67.8 3.6 %collective-permute-start.14 = (f32[512]{0:T(512)S(1)}, f32[512]{0:T(512)S(1)}, u32[]{:S(2)}, u32[]{:S(2)}) collective-permute-start(f32[512]{0:T(512)S(1)} %get-tuple-element.22), channel_id=1, source_target_pairs={{0,4},{4,0},{8,12},{12,8},{16,20},{20,16},{24,28},{28,24},{1,5},{5... | collective-permute-start | bytes 6152 | tf_op jit(solution)/shard_map/ppermute | solution.py:34
  68.5 3.6 %collective-permute-start.17 = (f32[512]{0:T(512)S(1)}, f32[512]{0:T(512)S(1)}, u32[]{:S(2)}, u32[]{:S(2)}) collective-permute-start(f32[512]{0:T(512)S(1)} %get-tuple-element.20), channel_id=1, source_target_pairs={{0,4},{4,0},{8,12},{12,8},{16,20},{20,16},{24,28},{28,24},{1,5},{5... | collective-permute-start | bytes 6152 | tf_op jit(solution)/shard_map/ppermute | solution.py:34
  70.1 3.6 %collective-permute-start.12 = (f32[512]{0:T(512)S(1)}, f32[512]{0:T(512)S(1)}, u32[]{:S(2)}, u32[]{:S(2)}) collective-permute-start(f32[512]{0:T(512)S(1)} %add.205), channel_id=1, source_target_pairs={{0,8},{4,12},{8,0},{12,4},{16,24},{20,28},{24,16},{28,20},{1,9},{5... | collective-permute-start | bytes 6152 | tf_op jit(solution)/shard_map/ppermute | solution.py:34
  71.4 3.6 %collective-permute-start.15 = (f32[512]{0:T(512)S(1)}, f32[512]{0:T(512)S(1)}, u32[]{:S(2)}, u32[]{:S(2)}) collective-permute-start(f32[512]{0:T(512)S(1)} %add.208), channel_id=1, source_target_pairs={{0,8},{4,12},{8,0},{12,4},{16,24},{20,28},{24,16},{28,20},{1,9},{5... | collective-permute-start | bytes 6152 | tf_op jit(solution)/shard_map/ppermute | solution.py:34
  72.1 4.5 %collective-permute-start.18 = (f32[512]{0:T(512)S(1)}, f32[512]{0:T(512)S(1)}, u32[]{:S(2)}, u32[]{:S(2)}) collective-permute-start(f32[512]{0:T(512)S(1)} %add.213), channel_id=1, source_target_pairs={{0,8},{4,12},{8,0},{12,4},{16,24},{20,28},{24,16},{28,20},{1,9},{5... | collective-permute-start | bytes 6152 | tf_op jit(solution)/shard_map/ppermute | solution.py:34
  73.7 4.5 %collective-permute-start.13 = (f32[512]{0:T(512)S(1)}, f32[512]{0:T(512)S(1)}, u32[]{:S(2)}, u32[]{:S(2)}) collective-permute-start(f32[512]{0:T(512)S(1)} %add.206), channel_id=1, source_target_pairs={{0,16},{4,20},{8,24},{12,28},{16,0},{20,4},{24,8},{28,12},{1,17},{... | collective-permute-start | bytes 6152 | tf_op jit(solution)/shard_map/ppermute | solution.py:34
  75.0 4.5 %collective-permute-start.16 = (f32[512]{0:T(512)S(1)}, f32[512]{0:T(512)S(1)}, u32[]{:S(2)}, u32[]{:S(2)}) collective-permute-start(f32[512]{0:T(512)S(1)} %add.209), channel_id=1, source_target_pairs={{0,16},{4,20},{8,24},{12,28},{16,0},{20,4},{24,8},{28,12},{1,17},{... | collective-permute-start | bytes 6152 | tf_op jit(solution)/shard_map/ppermute | solution.py:34
  76.6 4.5 %collective-permute-start.19 = (f32[512]{0:T(512)S(1)}, f32[512]{0:T(512)S(1)}, u32[]{:S(2)}, u32[]{:S(2)}) collective-permute-start(f32[512]{0:T(512)S(1)} %add.214), channel_id=1, source_target_pairs={{0,16},{4,20},{8,24},{12,28},{16,0},{20,4},{24,8},{28,12},{1,17},{... | collective-permute-start | bytes 6152 | tf_op jit(solution)/shard_map/ppermute | solution.py:34
  82.1 6.4 %collective-permute-start.21 = (bf16[512,256]{1,0:T(8,128)(2,1)S(1)}, bf16[512,256]{1,0:T(8,128)(2,1)S(1)}, u32[]{:S(2)}, u32[]{:S(2)}) collective-permute-start(bf16[512,256]{1,0:T(8,128)(2,1)S(1)} %convolution_convert_fusion.1), channel_id=1, source_target_pairs={{0,4},{4,0},{8,12},{12,8},{16,20},{20,16},{24,28},{28,24},{1,5},{5... | collective-permute-start | bytes 786440 | tf_op jit(solution)/shard_map/ppermute | solution.py:55
  88.6 7.6 %collective-permute-start.22 = (bf16[512,256]{1,0:T(8,128)(2,1)S(1)}, bf16[512,256]{1,0:T(8,128)(2,1)S(1)}, u32[]{:S(2)}, u32[]{:S(2)}) collective-permute-start(bf16[512,256]{1,0:T(8,128)(2,1)S(1)} %add_convert_fusion.1), channel_id=1, source_target_pairs={{0,8},{4,12},{8,0},{12,4},{16,24},{20,28},{24,16},{28,20},{1,9},{5... | collective-permute-start | bytes 786440 | tf_op jit(solution)/shard_map/ppermute | solution.py:55
  90.1 7.5 %collective-permute-start.20 = (f32[256,256]{1,0:T(8,128)S(1)}, f32[256,256]{1,0:T(8,128)S(1)}, u32[]{:S(2)}, u32[]{:S(2)}) collective-permute-start(f32[256,256]{1,0:T(8,128)S(1)} %slice_select_fusion), channel_id=1, source_target_pairs={{0,2},{2,0},{1,3},{3,1},{4,6},{6,4},{5,7},{7,5},{8,10},{10,8},{9,1... | collective-permute-start | bytes 786440 | tf_op jit(solution)/shard_map/ppermute | solution.py:87
  96.3 10.1 %collective-permute-start.23 = (bf16[512,256]{1,0:T(8,128)(2,1)S(1)}, bf16[512,256]{1,0:T(8,128)(2,1)S(1)}, u32[]{:S(2)}, u32[]{:S(2)}) collective-permute-start(bf16[512,256]{1,0:T(8,128)(2,1)S(1)} %add_convert_fusion), channel_id=1, source_target_pairs={{0,16},{4,20},{8,24},{12,28},{16,0},{20,4},{24,8},{28,12},{1,17},{... | collective-permute-start | bytes 786440 | tf_op jit(solution)/shard_map/ppermute | solution.py:55
  (3 other events, 13.3 us)

commit v3 on v2

--- a/solution.py
+++ b/solution.py
@@ -59,16 +59,15 @@
 
 
 def softmax_combine(a, b):
-    max_a, total_a, mixed_a = a
-    max_b, total_b, mixed_b = b
+    (max_a, total_a), mixed_a = a
+    (max_b, total_b), mixed_b = b
     mixed_a = mixed_a.astype(jnp.float32)
     mixed_b = mixed_b.astype(jnp.float32)
     top = jnp.maximum(max_a, max_b)
     factor_a = jnp.exp(max_a - top)
     factor_b = jnp.exp(max_b - top)
     return (
-        top,
-        total_a * factor_a + total_b * factor_b,
+        jnp.stack([top, total_a * factor_a + total_b * factor_b]),
         (scale_heads(mixed_a, factor_a) + scale_heads(mixed_b, factor_b)).astype(jnp.bfloat16),
     )
 
@@ -87,6 +86,14 @@
         block = keep + lax.ppermute(send, axis, partner_pairs(count, distance))
         distance //= 2
     return block
+
+
+def gather_rows(block, axis):
+    if lax.axis_size(axis) != 2:
+        return lax.all_gather(block, axis, axis=0, tiled=True)
+    other = lax.ppermute(block, axis, [(0, 1), (1, 0)])
+    first = lax.axis_index(axis) == 0
+    return jnp.concatenate([jnp.where(first, block, other), jnp.where(first, other, block)])
 
 
 def norm_rows(entries):
@@ -196,9 +203,7 @@
     shifted = truth + 1
     digits = jnp.stack([shifted // 256, shifted % 256], axis=1).astype(jnp.bfloat16)
     digits = jnp.pad(digits, ((0, 0), (0, 126)))
-    gathered = lax.all_gather(
-        jnp.concatenate([local_kv, encoded, digits], axis=1), "query", axis=0, tiled=True
-    )
+    gathered = gather_rows(jnp.concatenate([local_kv, encoded, digits], axis=1), "query")
     group_kv = gathered[:, : 2 * model_width]
     group_hits = gathered[:, 2 * model_width : 3 * model_width]
     group_digits = gathered[:, 3 * model_width :].astype(jnp.int32)
@@ -218,8 +223,8 @@
     local_mixed = jnp.einsum(
         "hqk,khd->qhd", raised, value_heads, preferred_element_type=jnp.float32
     ).reshape(query_count, model_width)
-    _, total, mixed = butterfly(
-        (local_max, local_total, local_mixed.astype(jnp.bfloat16)),
+    (_, total), mixed = butterfly(
+        (jnp.stack([local_max, local_total]), local_mixed.astype(jnp.bfloat16)),
         "phi",
         softmax_combine,
         ordered=True,
@@ -249,7 +254,9 @@
         jnp.float32
     )
     intersection, predicted, truth_count = butterfly(
-        (jnp.sum(sigma * target, axis=1), jnp.sum(sigma, axis=1), jnp.sum(target, axis=1)),
+        jnp.stack(
+            [jnp.sum(sigma * target, axis=1), jnp.sum(sigma, axis=1), jnp.sum(target, axis=1)]
+        ),
         "phi",
         add_trees,
     )

time: 107 us -> 112 us (1.047)
  waiting for transfers between devices: 44.8 us -> 64.3 us
  starting transfers between devices: 30.4 us -> 12.1 us
  blocking collectives: 4.35 us -> 0 us
  local copies, waits for them, and re-layouts: 2.38 us -> 6.52 us
  matrix products: 17.8 us -> 20.4 us
    ppermute x18 -> x9, starting transfers between devices: 21 us -> 5.21 us  [butterfly(): other = lax.ppermute(tree, axis, partner_pairs(count, distance))]
    ppermute x18 -> x9, waiting for transfers between devices: 23.8 us -> 35.6 us  [butterfly(): other = lax.ppermute(tree, axis, partner_pairs(count, distance))]
    all_gather x1 -> x0, blocking collectives: 4.35 us -> none  [body(): lax.all_gather(jnp.concatenate([local_kv, encoded, digits], axis=1), 'que...]
    unnamed x25 -> x29, local copies, waits for them, and re-layouts: 1.38 us -> 5.55 us
    dot_general x1, matrix products: 1.51 us -> 4.93 us  [body(): jnp.einsum('hqk,khd->qhd', raised, value_heads, preferred_element_type=jn...]
    ppermute x1, waiting for transfers between devices: 1.74 us -> 4.6 us  [extended_2(): lax.ppermute(lax.slice_in_dim(block, block.shape[dim] - width, None, axis...]
    ppermute x3, starting transfers between devices: 3.78 us -> 1.3 us  [narrow_butterfly(): other = lax.ppermute(sent, axis, partner_pairs(count, distance))]
    ppermute x3, waiting for transfers between devices: 19.2 us -> 21 us  [narrow_butterfly(): other = lax.ppermute(sent, axis, partner_pairs(count, distance))]
  transfers between devices with their start and end apart: 24 -> 16, of which waited for: 14 -> 13; matrix products, arithmetic and copies ran while one was open for 7% -> 8% of each run, Pallas kernels for 0% -> 0%
where the time goes in v3:
time: 112 us; the launch traced here: 111 us
  waiting for transfers between devices  64.3 us (57%)
  matrix products  20.4 us (18%)
  starting transfers between devices  12.1 us (11%)
  other arithmetic  6.69 us (6%)
  local copies, waits for them, and re-layouts  6.52 us (6%)
  between operations  1.36 us (1%)
    ppermute x9, waiting for transfers between devices, butterfly(): other = lax.ppermute(tree, axis, partner_pairs(count, distance))  35.6 us
    ppermute x3, waiting for transfers between devices, narrow_butterfly(): other = lax.ppermute(sent, axis, partner_pairs(count, distance))  21 us
    unnamed x29, local copies, waits for them, and re-layouts  5.55 us
    ppermute x1, starting transfers between devices, extended_2(): lax.ppermute(lax.slice_in_dim(block, 0, width, axis=dim), axis, backward)  5.47 us
    ppermute x9, starting transfers between devices, butterfly(): other = lax.ppermute(tree, axis, partner_pairs(count, distance))  5.21 us
    sub x1, matrix products, window_attend(): raised = jnp.exp(scores - jnp.max(scores, axis=-1, keepdims=True))  5.1 us
    dot_general x1, matrix products, body(): jnp.einsum('hqk,khd->qhd', raised, value_heads, preferred_element_type=jn...  4.93 us
    ppermute x1, waiting for transfers between devices, extended_2(): lax.ppermute(lax.slice_in_dim(block, block.shape[dim] - width, None, axis...  4.6 us
  transfers between devices with their start and end apart: 16, of which 13 were waited for; matrix products, arithmetic and copies ran while one was open for 8% of the time, Pallas kernels for 0%

profile of v3, /device:TPU:0, one launch (start us, length us, event | category | flops | bytes accessed | tf_op | source)
XLA Modules:
  0.0 111.5 jit_solution(1507636295653575399)
XLA Ops:
  0.6 1.1 copy.40
  1.9 1.3 %convolution_convert_fusion = bf16[256,768]{1,0:T(8,128)(2,1)S(1)} fusion(bf16[256,768]{1,0:T(8,128)(2,1)} %param.14, bf16[256,256]{0,1:T(8,128)(2,1)S(1)} %copy.40, f32[256]{0:T(256)S(1)} %add_rsqrt_fusion.3, f32[256]{0:T(256)S(1)} %broadcast_multiply_fusion.3), kind=kOutput, calls=%fused_computation.20 | convolution fusion | flops 101122048 | bytes 919552 | tf_op jit(solution)/shard_map/dot_general | solution.py:185
  3.2 5.5 %collective-permute-start.1 = (bf16[256,512]{1,0:T(8,128)(2,1)S(1)}, bf16[256,512]{1,0:T(8,128)(2,1)S(1)}, u32[]{:S(2)}, u32[]{:S(2)}) collective-permute-start(bf16[256,512]{1,0:T(8,128)(2,1)S(1)} %slice.51), channel_id=1, source_target_pairs={{2,0},{4,2},{6,4},{8,6},{10,8},{12,10},{14,12},{16,14},{18,16},{20... | collective-permute-start | bytes 786440 | tf_op jit(solution)/shard_map/ppermute | solution.py:19
  8.7 0.7 fusion.97
  9.7 1.1 copy.44
  10.9 1.6 %collective-permute-done.1 = bf16[256,512]{1,0:T(8,128)(2,1)S(1)} collective-permute-done((bf16[256,512]{1,0:T(8,128)(2,1)S(1)}, bf16[256,512]{1,0:T(8,128)(2,1)S(1)}, u32[]{:S(2)}, u32[]{:S(2)}) %collective-permute-start.1) | collective-permute-done | bytes 262176 | tf_op jit(solution)/shard_map/ppermute | solution.py:19
  12.6 4.6 %collective-permute-done = bf16[256,512]{1,0:T(8,128)(2,1)S(1)} collective-permute-done((bf16[256,512]{1,0:T(8,128)(2,1)S(1)}, bf16[256,512]{1,0:T(8,128)(2,1)S(1)}, u32[]{:S(2)}, u32[]{:S(2)}) %collective-permute-start) | collective-permute-done | bytes 262176 | tf_op jit(solution)/shard_map/ppermute | solution.py:16
  17.6 5.1 %fusion.112 = (f32[8,256]{1,0:T(8,128)S(1)}, f32[8,256,768]{2,1,0:T(8,128)}) fusion(pred[256,768]{1,0:T(8,128)(4,1)S(1)} %fusion.28, bf16[256,8,32]{0,2,1:T(8,128)(2,1)S(1)} %bitcast.164, bf16[768,8,32]{0,2,1:T(8,128)(2,1)S(1)} %bitcast.160), kind=kOutput, calls=%fused_computation.204 | convolution fusion | flops 106955520 | bytes 7020544 | tf_op jit(solution)/shard_map/sub | solution.py:122
  22.7 4.0 %fusion.12 = bf16[8,32,256]{2,1,0:T(8,128)(2,1)S(1)} fusion(bf16[768,8,32]{0,2,1:T(8,128)(2,1)S(1)} %bitcast.159, f32[8,256,768]{2,1,0:T(8,128)} %get-tuple-element.55, f32[8,256]{1,0:T(8,128)S(1)} %get-tuple-element.54), kind=kOutput, calls=%fused_computation.38 | convolution fusion | flops 103874560 | bytes 6823936 | tf_op jit(solution)/shard_map/hqk,khd->qhd/dot_general | solution.py:124
  27.1 0.8 convert_reduce_fusion.3
  28.9 1.5 %collective-permute-done.2 = bf16[256,896]{1,0:T(8,128)(2,1)S(1)} collective-permute-done((bf16[256,896]{1,0:T(8,128)(2,1)S(1)}, bf16[256,896]{1,0:T(8,128)(2,1)S(1)}, u32[]{:S(2)}, u32[]{:S(2)}) %collective-permute-start.2) | collective-permute-done | bytes 458784 | tf_op jit(solution)/shard_map/ppermute | solution.py:94
  30.8 1.3 %multiply_reduce_fusion = (f32[8,512]{1,0:T(8,128)S(1)}, f32[8,512,512]{1,2,0:T(8,128)S(1)}) fusion(bf16[512,8,32]{0,2,1:T(8,128)(2,1)S(1)} %bitcast.153, bf16[512,8,32]{0,2,1:T(8,128)(2,1)S(1)} %bitcast.154), kind=kOutput, calls=%fused_computation.3 | convolution fusion | flops 138407936 | bytes 8929280 | tf_op jit(solution)/shard_map/qhd,khd->hqk/dot_general | solution.py:217
  32.1 3.2 %copy-done.1 = f32[8,512,512]{1,2,0:T(8,128)} copy-done((f32[8,512,512]{1,2,0:T(8,128)}, f32[8,512,512]{1,2,0:T(8,128)S(1)}, u32[]{:S(2)}) %copy-start.1) | copy-done | bytes 8388632
  35.3 1.4 %convert_reduce_fusion = f32[8,512]{1,0:T(8,128)S(1)} fusion(f32[8,512]{1,0:T(8,128)S(1)} %get-tuple-element.60, f32[8,512,512]{1,2,0:T(8,128)S(1)} %get-tuple-element.61), kind=kLoop, calls=%fused_computation.1 | loop fusion | flops 10481664 | bytes 8421376 | tf_op jit(solution)/shard_map/reduce_sum | solution.py:222
  37.0 4.9 %convolution_convert_fusion.3 = bf16[8,32,512]{2,1,0:T(8,128)(2,1)S(1)} fusion(bf16[512,8,32]{0,2,1:T(8,128)(2,1)S(1)} %bitcast.155, f32[8,512,512]{1,2,0:T(8,128)} %copy-done.1, f32[8,512]{1,0:T(8,128)S(1)} %get-tuple-element.60), kind=kOutput, calls=%fused_computation.25 | convolution fusion | flops 140640256 | bytes 8929280 | tf_op jit(solution)/shard_map/hqk,khd->qhd/dot_general | solution.py:223
  41.9 2.1 %collective-permute-start.3 = (bf16[512,256]{0,1:T(8,128)(2,1)S(1)}, bf16[512,256]{0,1:T(8,128)(2,1)S(1)}, u32[]{:S(2)}, u32[]{:S(2)}) collective-permute-start(bf16[512,256]{0,1:T(8,128)(2,1)S(1)} %bitcast.156), channel_id=1, source_target_pairs={{0,4},{4,0},{8,12},{12,8},{16,20},{20,16},{24,28},{28,24},{1,5},{5... | collective-permute-start | bytes 786440 | tf_op jit(solution)/shard_map/ppermute | solution.py:34
  44.4 3.9 %collective-permute-done.6 = f32[2,8,512]{2,1,0:T(8,128)S(1)} collective-permute-done((f32[2,8,512]{2,1,0:T(8,128)S(1)}, f32[2,8,512]{2,1,0:T(8,128)S(1)}, u32[]{:S(2)}, u32[]{:S(2)}) %collective-permute-start.6) | collective-permute-done | bytes 32800 | tf_op jit(solution)/shard_map/ppermute | solution.py:34
  48.3 2.0 %collective-permute-done.3 = bf16[512,256]{0,1:T(8,128)(2,1)S(1)} collective-permute-done((bf16[512,256]{0,1:T(8,128)(2,1)S(1)}, bf16[512,256]{0,1:T(8,128)(2,1)S(1)}, u32[]{:S(2)}, u32[]{:S(2)}) %collective-permute-start.3) | collective-permute-done | bytes 262176 | tf_op jit(solution)/shard_map/ppermute | solution.py:34
  50.6 1.6 %collective-permute-start.8 = (f32[2,8,512]{2,1,0:T(8,128)S(1)}, f32[2,8,512]{2,1,0:T(8,128)S(1)}, u32[]{:S(2)}, u32[]{:S(2)}) collective-permute-start(f32[2,8,512]{2,1,0:T(8,128)S(1)} %pad_maximum_fusion.4), channel_id=1, source_target_pairs={{0,16},{4,20},{8,24},{12,28},{16,0},{20,4},{24,8},{28,12},{1,17},{... | collective-permute-start | bytes 98312 | tf_op jit(solution)/shard_map/ppermute | solution.py:34
  52.1 6.6 %collective-permute-done.5 = bf16[512,256]{0,1:T(8,128)(2,1)S(1)} collective-permute-done((bf16[512,256]{0,1:T(8,128)(2,1)S(1)}, bf16[512,256]{0,1:T(8,128)(2,1)S(1)}, u32[]{:S(2)}, u32[]{:S(2)}) %collective-permute-start.5) | collective-permute-done | bytes 262176 | tf_op jit(solution)/shard_map/ppermute | solution.py:34
  59.0 12.4 %collective-permute-done.7 = bf16[512,256]{0,1:T(8,128)(2,1)S(1)} collective-permute-done((bf16[512,256]{0,1:T(8,128)(2,1)S(1)}, bf16[512,256]{0,1:T(8,128)(2,1)S(1)}, u32[]{:S(2)}, u32[]{:S(2)}) %collective-permute-start.7) | collective-permute-done | bytes 262176 | tf_op jit(solution)/shard_map/ppermute | solution.py:34
  72.6 0.7 select_reduce_fusion
  73.3 1.2 %collective-permute-start.9 = (f32[3,512]{1,0:T(4,128)S(1)}, f32[3,512]{1,0:T(4,128)S(1)}, u32[]{:S(2)}, u32[]{:S(2)}) collective-permute-start(f32[3,512]{1,0:T(4,128)S(1)} %pad_maximum_fusion.5), channel_id=1, source_target_pairs={{0,4},{4,0},{8,12},{12,8},{16,20},{20,16},{24,28},{28,24},{1,5},{5... | collective-permute-start | bytes 18440 | tf_op jit(solution)/shard_map/ppermute | solution.py:34
  74.5 2.6 %collective-permute-done.9 = f32[3,512]{1,0:T(4,128)S(1)} collective-permute-done((f32[3,512]{1,0:T(4,128)S(1)}, f32[3,512]{1,0:T(4,128)S(1)}, u32[]{:S(2)}, u32[]{:S(2)}) %collective-permute-start.9) | collective-permute-done | bytes 6176 | tf_op jit(solution)/shard_map/ppermute | solution.py:34
  77.1 3.6 %collective-permute-done.10 = f32[3,512]{1,0:T(4,128)S(1)} collective-permute-done((f32[3,512]{1,0:T(4,128)S(1)}, f32[3,512]{1,0:T(4,128)S(1)}, u32[]{:S(2)}, u32[]{:S(2)}) %collective-permute-start.10) | collective-permute-done | bytes 6176 | tf_op jit(solution)/shard_map/ppermute | solution.py:34
  80.9 4.5 %collective-permute-done.11 = f32[3,512]{1,0:T(4,128)S(1)} collective-permute-done((f32[3,512]{1,0:T(4,128)S(1)}, f32[3,512]{1,0:T(4,128)S(1)}, u32[]{:S(2)}, u32[]{:S(2)}) %collective-permute-start.11) | collective-permute-done | bytes 6176 | tf_op jit(solution)/shard_map/ppermute | solution.py:34
  87.0 1.2 %collective-permute-start.13 = (bf16[512,256]{1,0:T(8,128)(2,1)S(1)}, bf16[512,256]{1,0:T(8,128)(2,1)S(1)}, u32[]{:S(2)}, u32[]{:S(2)}) collective-permute-start(bf16[512,256]{1,0:T(8,128)(2,1)S(1)} %convolution_convert_fusion.1), channel_id=1, source_target_pairs={{0,4},{4,0},{8,12},{12,8},{16,20},{20,16},{24,28},{28,24},{1,5},{5... | collective-permute-start | bytes 786440 | tf_op jit(solution)/shard_map/ppermute | solution.py:55
  88.1 5.3 %collective-permute-done.13 = bf16[512,256]{1,0:T(8,128)(2,1)S(1)} collective-permute-done((bf16[512,256]{1,0:T(8,128)(2,1)S(1)}, bf16[512,256]{1,0:T(8,128)(2,1)S(1)}, u32[]{:S(2)}, u32[]{:S(2)}) %collective-permute-start.13) | collective-permute-done | bytes 262176 | tf_op jit(solution)/shard_map/ppermute | solution.py:55
  94.0 7.4 %collective-permute-done.14 = bf16[512,256]{1,0:T(8,128)(2,1)S(1)} collective-permute-done((bf16[512,256]{1,0:T(8,128)(2,1)S(1)}, bf16[512,256]{1,0:T(8,128)(2,1)S(1)}, u32[]{:S(2)}, u32[]{:S(2)}) %collective-permute-start.14) | collective-permute-done | bytes 262176 | tf_op jit(solution)/shard_map/ppermute | solution.py:55
  101.6 0.8 select_add_fusion
  102.3 8.3 %collective-permute-done.15 = bf16[512,256]{1,0:T(8,128)(2,1)S(1)} collective-permute-done((bf16[512,256]{1,0:T(8,128)(2,1)S(1)}, bf16[512,256]{1,0:T(8,128)(2,1)S(1)}, u32[]{:S(2)}, u32[]{:S(2)}) %collective-permute-start.15) | collective-permute-done | bytes 262176 | tf_op jit(solution)/shard_map/ppermute | solution.py:55
  110.6 0.8 convert_add_fusion
  (104 shorter events, 7.2 us)
Async XLA Ops:
  0.6 26.5 %copy-start = (bf16[1024,256]{1,0:T(8,128)(2,1)S(1)}, bf16[1024,256]{1,0:T(8,128)(2,1)}, u32[]{:S(2)}) copy-start(bf16[1024,256]{1,0:T(8,128)(2,1)} %param.17) | copy-start | bytes 1572868
  3.2 9.4 %collective-permute-start.1 = (bf16[256,512]{1,0:T(8,128)(2,1)S(1)}, bf16[256,512]{1,0:T(8,128)(2,1)S(1)}, u32[]{:S(2)}, u32[]{:S(2)}) collective-permute-start(bf16[256,512]{1,0:T(8,128)(2,1)S(1)} %slice.51), channel_id=1, source_target_pairs={{2,0},{4,2},{6,4},{8,6},{10,8},{12,10},{14,12},{16,14},{18,16},{20... | collective-permute-start | bytes 786440 | tf_op jit(solution)/shard_map/ppermute | solution.py:19
  8.7 8.5 %collective-permute-start = (bf16[256,512]{1,0:T(8,128)(2,1)S(1)}, bf16[256,512]{1,0:T(8,128)(2,1)S(1)}, u32[]{:S(2)}, u32[]{:S(2)}) collective-permute-start(bf16[256,512]{1,0:T(8,128)(2,1)S(1)} %slice.51), channel_id=1, source_target_pairs={{0,2},{2,4},{4,6},{6,8},{8,10},{10,12},{12,14},{14,16},{16,18},{18... | collective-permute-start | bytes 786440 | tf_op jit(solution)/shard_map/ppermute | solution.py:16
  22.7 4.0 %copy-start.6 = (bf16[256,256]{1,0:T(8,128)(2,1)S(1)}, bf16[256,256]{1,0:T(8,128)(2,1)}, u32[]{:S(2)}) copy-start(bf16[256,256]{1,0:T(8,128)(2,1)} %param.15) | copy-start | bytes 393220
  22.7 4.4 %copy-start.10 = (bf16[256,1024]{1,0:T(8,128)(2,1)S(1)}, bf16[256,1024]{1,0:T(8,128)(2,1)}, u32[]{:S(2)}) copy-start(bf16[256,1024]{1,0:T(8,128)(2,1)} %param.16) | copy-start | bytes 1572868
  22.7 5.4 %copy-start.5 = (bf16[256,512]{1,0:T(8,128)(2,1)S(1)}, bf16[256,512]{1,0:T(8,128)(2,1)}, u32[]{:S(2)}) copy-start(bf16[256,512]{1,0:T(8,128)(2,1)} %param.20) | copy-start | bytes 786436
  26.7 1.8 %copy-start.9 = (s32[512]{0:T(512)S(1)}, s32[512]{0:T(512)}, u32[]{:S(2)}) copy-start(s32[512]{0:T(512)} %param.25) | copy-start | bytes 6148
  26.7 1.8 %copy-start.3 = (bf16[512,256]{1,0:T(8,128)(2,1)S(1)}, bf16[512,256]{1,0:T(8,128)(2,1)}, u32[]{:S(2)}) copy-start(bf16[512,256]{1,0:T(8,128)(2,1)} %param.18) | copy-start | bytes 786436
  26.8 1.8 %copy-start.7 = (bf16[256,256]{1,0:T(8,128)(2,1)S(1)}, bf16[256,256]{1,0:T(8,128)(2,1)}, u32[]{:S(2)}) copy-start(bf16[256,256]{1,0:T(8,128)(2,1)} %param.19) | copy-start | bytes 393220
  28.1 4.0 %copy-start.2 = (bf16[256,256]{1,0:T(8,128)(2,1)}, bf16[256,256]{1,0:T(8,128)(2,1)S(1)}, u32[]{:S(2)}) copy-start(bf16[256,256]{1,0:T(8,128)(2,1)S(1)} %copy.50) | copy-start | bytes 393220
  28.5 1.9 %collective-permute-start.2 = (bf16[256,896]{1,0:T(8,128)(2,1)S(1)}, bf16[256,896]{1,0:T(8,128)(2,1)S(1)}, u32[]{:S(2)}, u32[]{:S(2)}) collective-permute-start(bf16[256,896]{1,0:T(8,128)(2,1)S(1)} %fusion.43), channel_id=1, source_target_pairs={{0,2},{2,0},{1,3},{3,1},{4,6},{6,4},{5,7},{7,5},{8,10},{10,8},{9,1... | collective-permute-start | bytes 1376264 | tf_op jit(solution)/shard_map/ppermute | solution.py:94
  32.1 3.2 %copy-start.1 = (f32[8,512,512]{1,2,0:T(8,128)}, f32[8,512,512]{1,2,0:T(8,128)S(1)}, u32[]{:S(2)}) copy-start(f32[8,512,512]{1,2,0:T(8,128)S(1)} %get-tuple-element.61) | copy-start | bytes 25165828
  36.7 7.5 %collective-permute-start.4 = (f32[2,8,512]{2,1,0:T(8,128)S(1)}, f32[2,8,512]{2,1,0:T(8,128)S(1)}, u32[]{:S(2)}, u32[]{:S(2)}) collective-permute-start(f32[2,8,512]{2,1,0:T(8,128)S(1)} %pad_maximum_fusion.2), channel_id=1, source_target_pairs={{0,4},{4,0},{8,12},{12,8},{16,20},{20,16},{24,28},{28,24},{1,5},{5... | collective-permute-start | bytes 98312 | tf_op jit(solution)/shard_map/ppermute | solution.py:34
  36.9 34.6 %copy-start.8 = (bf16[256,256]{1,0:T(8,128)(2,1)S(1)}, bf16[256,256]{1,0:T(8,128)(2,1)}, u32[]{:S(2)}) copy-start(bf16[256,256]{1,0:T(8,128)(2,1)} %param.21) | copy-start | bytes 393220
  36.9 35.0 %copy-start.11 = (bf16[256,256]{1,0:T(8,128)(2,1)S(1)}, bf16[256,256]{1,0:T(8,128)(2,1)}, u32[]{:S(2)}) copy-start(bf16[256,256]{1,0:T(8,128)(2,1)} %param.23) | copy-start | bytes 393220
  37.0 35.0 %copy-start.12 = (bf16[256,256]{1,0:T(8,128)(2,1)S(1)}, bf16[256,256]{1,0:T(8,128)(2,1)}, u32[]{:S(2)}) copy-start(bf16[256,256]{1,0:T(8,128)(2,1)} %param.22) | copy-start | bytes 393220
  41.9 8.4 %collective-permute-start.3 = (bf16[512,256]{0,1:T(8,128)(2,1)S(1)}, bf16[512,256]{0,1:T(8,128)(2,1)S(1)}, u32[]{:S(2)}, u32[]{:S(2)}) collective-permute-start(bf16[512,256]{0,1:T(8,128)(2,1)S(1)} %bitcast.156), channel_id=1, source_target_pairs={{0,4},{4,0},{8,12},{12,8},{16,20},{20,16},{24,28},{28,24},{1,5},{5... | collective-permute-start | bytes 786440 | tf_op jit(solution)/shard_map/ppermute | solution.py:34
  44.3 4.0 %collective-permute-start.6 = (f32[2,8,512]{2,1,0:T(8,128)S(1)}, f32[2,8,512]{2,1,0:T(8,128)S(1)}, u32[]{:S(2)}, u32[]{:S(2)}) collective-permute-start(f32[2,8,512]{2,1,0:T(8,128)S(1)} %pad_maximum_fusion.3), channel_id=1, source_target_pairs={{0,8},{4,12},{8,0},{12,4},{16,24},{20,28},{24,16},{28,20},{1,9},{5... | collective-permute-start | bytes 98312 | tf_op jit(solution)/shard_map/ppermute | solution.py:34
  50.5 8.3 %collective-permute-start.5 = (bf16[512,256]{0,1:T(8,128)(2,1)S(1)}, bf16[512,256]{0,1:T(8,128)(2,1)S(1)}, u32[]{:S(2)}, u32[]{:S(2)}) collective-permute-start(bf16[512,256]{0,1:T(8,128)(2,1)S(1)} %fusion.38), channel_id=1, source_target_pairs={{0,8},{4,12},{8,0},{12,4},{16,24},{20,28},{24,16},{28,20},{1,9},{5... | collective-permute-start | bytes 786440 | tf_op jit(solution)/shard_map/ppermute | solution.py:34
  50.6 8.4 %collective-permute-start.8 = (f32[2,8,512]{2,1,0:T(8,128)S(1)}, f32[2,8,512]{2,1,0:T(8,128)S(1)}, u32[]{:S(2)}, u32[]{:S(2)}) collective-permute-start(f32[2,8,512]{2,1,0:T(8,128)S(1)} %pad_maximum_fusion.4), channel_id=1, source_target_pairs={{0,16},{4,20},{8,24},{12,28},{16,0},{20,4},{24,8},{28,12},{1,17},{... | collective-permute-start | bytes 98312 | tf_op jit(solution)/shard_map/ppermute | solution.py:34
  58.9 12.5 %collective-permute-start.7 = (bf16[512,256]{0,1:T(8,128)(2,1)S(1)}, bf16[512,256]{0,1:T(8,128)(2,1)S(1)}, u32[]{:S(2)}, u32[]{:S(2)}) collective-permute-start(bf16[512,256]{0,1:T(8,128)(2,1)S(1)} %fusion.36), channel_id=1, source_target_pairs={{0,16},{4,20},{8,24},{12,28},{16,0},{20,4},{24,8},{28,12},{1,17},{... | collective-permute-start | bytes 786440 | tf_op jit(solution)/shard_map/ppermute | solution.py:34
  72.6 21.3 %copy-start.4 = (bf16[512,256]{1,0:T(8,128)(2,1)}, bf16[512,256]{1,0:T(8,128)(2,1)S(1)}, u32[]{:S(2)}) copy-start(bf16[512,256]{1,0:T(8,128)(2,1)S(1)} %convolution_convert_fusion.2) | copy-start | bytes 786436
  73.3 3.7 %collective-permute-start.9 = (f32[3,512]{1,0:T(4,128)S(1)}, f32[3,512]{1,0:T(4,128)S(1)}, u32[]{:S(2)}, u32[]{:S(2)}) collective-permute-start(f32[3,512]{1,0:T(4,128)S(1)} %pad_maximum_fusion.5), channel_id=1, source_target_pairs={{0,4},{4,0},{8,12},{12,8},{16,20},{20,16},{24,28},{28,24},{1,5},{5... | collective-permute-start | bytes 18440 | tf_op jit(solution)/shard_map/ppermute | solution.py:34
  77.0 3.7 %collective-permute-start.10 = (f32[3,512]{1,0:T(4,128)S(1)}, f32[3,512]{1,0:T(4,128)S(1)}, u32[]{:S(2)}, u32[]{:S(2)}) collective-permute-start(f32[3,512]{1,0:T(4,128)S(1)} %fusion.106), channel_id=1, source_target_pairs={{0,8},{4,12},{8,0},{12,4},{16,24},{20,28},{24,16},{28,20},{1,9},{5... | collective-permute-start | bytes 18440 | tf_op jit(solution)/shard_map/ppermute | solution.py:34
  80.8 4.6 %collective-permute-start.11 = (f32[3,512]{1,0:T(4,128)S(1)}, f32[3,512]{1,0:T(4,128)S(1)}, u32[]{:S(2)}, u32[]{:S(2)}) collective-permute-start(f32[3,512]{1,0:T(4,128)S(1)} %fusion.140), channel_id=1, source_target_pairs={{0,16},{4,20},{8,24},{12,28},{16,0},{20,4},{24,8},{28,12},{1,17},{... | collective-permute-start | bytes 18440 | tf_op jit(solution)/shard_map/ppermute | solution.py:34
  87.0 6.4 %collective-permute-start.13 = (bf16[512,256]{1,0:T(8,128)(2,1)S(1)}, bf16[512,256]{1,0:T(8,128)(2,1)S(1)}, u32[]{:S(2)}, u32[]{:S(2)}) collective-permute-start(bf16[512,256]{1,0:T(8,128)(2,1)S(1)} %convolution_convert_fusion.1), channel_id=1, source_target_pairs={{0,4},{4,0},{8,12},{12,8},{16,20},{20,16},{24,28},{28,24},{1,5},{5... | collective-permute-start | bytes 786440 | tf_op jit(solution)/shard_map/ppermute | solution.py:55
  93.5 7.9 %collective-permute-start.14 = (bf16[512,256]{1,0:T(8,128)(2,1)S(1)}, bf16[512,256]{1,0:T(8,128)(2,1)S(1)}, u32[]{:S(2)}, u32[]{:S(2)}) collective-permute-start(bf16[512,256]{1,0:T(8,128)(2,1)S(1)} %add_convert_fusion.1), channel_id=1, source_target_pairs={{0,8},{4,12},{8,0},{12,4},{16,24},{20,28},{24,16},{28,20},{1,9},{5... | collective-permute-start | bytes 786440 | tf_op jit(solution)/shard_map/ppermute | solution.py:55
  93.9 7.7 %collective-permute-start.12 = (f32[256,256]{1,0:T(8,128)S(1)}, f32[256,256]{1,0:T(8,128)S(1)}, u32[]{:S(2)}, u32[]{:S(2)}) collective-permute-start(f32[256,256]{1,0:T(8,128)S(1)} %slice_select_fusion), channel_id=1, source_target_pairs={{0,2},{2,0},{1,3},{3,1},{4,6},{6,4},{5,7},{7,5},{8,10},{10,8},{9,1... | collective-permute-start | bytes 786440 | tf_op jit(solution)/shard_map/ppermute | solution.py:86
  101.5 9.1 %collective-permute-start.15 = (bf16[512,256]{1,0:T(8,128)(2,1)S(1)}, bf16[512,256]{1,0:T(8,128)(2,1)S(1)}, u32[]{:S(2)}, u32[]{:S(2)}) collective-permute-start(bf16[512,256]{1,0:T(8,128)(2,1)S(1)} %add_convert_fusion), channel_id=1, source_target_pairs={{0,16},{4,20},{8,24},{12,28},{16,0},{20,4},{24,8},{28,12},{1,17},{... | collective-permute-start | bytes 786440 | tf_op jit(solution)/shard_map/ppermute | solution.py:55

commit v4 on v2

--- a/solution.py
+++ b/solution.py
@@ -87,6 +87,26 @@
         block = keep + lax.ppermute(send, axis, partner_pairs(count, distance))
         distance //= 2
     return block
+
+
+def shifted_exchange(piece_for, axis):
+    count = lax.axis_size(axis)
+    index = lax.axis_index(axis)
+    received = [piece_for(index)]
+    for shift in range(1, count):
+        pairs = [(i, (i + shift) % count) for i in range(count)]
+        received.append(lax.ppermute(piece_for((index + shift) % count), axis, pairs))
+    return received
+
+
+def by_source(received, axis):
+    index = lax.axis_index(axis)
+    order = (index - jnp.arange(len(received))) % len(received)
+    return jnp.take(jnp.stack(received), order, axis=0)
+
+
+def row_block(array, block_index, rows, axis=0):
+    return lax.dynamic_slice_in_dim(array, block_index * rows, rows, axis=axis)
 
 
 def norm_rows(entries):
@@ -218,15 +238,36 @@
     local_mixed = jnp.einsum(
         "hqk,khd->qhd", raised, value_heads, preferred_element_type=jnp.float32
     ).reshape(query_count, model_width)
-    _, total, mixed = butterfly(
-        (local_max, local_total, local_mixed.astype(jnp.bfloat16)),
-        "phi",
-        softmax_combine,
-        ordered=True,
-    )
-    mixed = mixed.astype(jnp.float32)
+    phi_count = lax.axis_size("phi")
+    direct = phi_count <= 8
+    if direct:
+        rows = query_count // phi_count
+        phi_index = lax.axis_index("phi")
+        stats = jnp.stack([local_max, local_total])
+        narrow = local_mixed.astype(jnp.bfloat16)
+        received = shifted_exchange(
+            lambda t: (row_block(stats, t, rows, axis=2), row_block(narrow, t, rows)), "phi"
+        )
+        maxima = jnp.stack([r[0][0] for r in received])
+        totals = jnp.stack([r[0][1] for r in received])
+        top = jnp.max(maxima, axis=0)
+        factor = jnp.exp(maxima - top[None])
+        total = jnp.sum(totals * factor, axis=0)
+        mixed = scale_heads(received[0][1].astype(jnp.float32), factor[0])
+        for k in range(1, phi_count):
+            mixed = mixed + scale_heads(received[k][1].astype(jnp.float32), factor[k])
+        own_queries = row_block(queries, phi_index, rows)
+    else:
+        _, total, mixed = butterfly(
+            (local_max, local_total, local_mixed.astype(jnp.bfloat16)),
+            "phi",
+            softmax_combine,
+            ordered=True,
+        )
+        mixed = mixed.astype(jnp.float32)
+        own_queries = queries
     context = scale_heads(mixed, 1.0 / total).astype(jnp.bfloat16)
-    mixed_queries = queries.astype(jnp.float32) + jnp.dot(
+    mixed_queries = own_queries.astype(jnp.float32) + jnp.dot(
         context, cross_out, preferred_element_type=jnp.float32
     )
     mask_hidden = jax.nn.relu(
@@ -239,6 +280,10 @@
     mask_embed = jnp.dot(mask_hidden, mask_second, preferred_element_type=jnp.float32).astype(
         jnp.bfloat16
     )
+    if direct:
+        mask_embed = by_source(shifted_exchange(lambda t: mask_embed, "phi"), "phi").reshape(
+            query_count, model_width
+        )
     logits = lax.dot_general(
         mask_embed, group_hits, (((1,), (1,)), ((), ())), preferred_element_type=jnp.float32
     ) * model_width ** (-0.5)
@@ -248,18 +293,32 @@
     target = jnp.logical_and(match[:, None] == group_truth[None, :], matched_flag[:, None]).astype(
         jnp.float32
     )
-    intersection, predicted, truth_count = butterfly(
-        (jnp.sum(sigma * target, axis=1), jnp.sum(sigma, axis=1), jnp.sum(target, axis=1)),
-        "phi",
-        add_trees,
-    )
+    partial_stats = jnp.stack(
+        [jnp.sum(sigma * target, axis=1), jnp.sum(sigma, axis=1), jnp.sum(target, axis=1)]
+    )
+    if direct:
+        intersection, predicted, truth_count = jnp.sum(
+            by_source(shifted_exchange(lambda t: partial_stats, "phi"), "phi"), axis=0
+        )
+    else:
+        intersection, predicted, truth_count = butterfly(partial_stats, "phi", add_trees)
     mask_fill = predicted / hits_total
     coef = loss_coefficients(
         sigma, target, matched, intersection, predicted, truth_count, hits_total, model_width
     )
-    mask_grad = narrow_butterfly(
-        jnp.dot(coef, group_hits, preferred_element_type=jnp.float32), "phi"
-    )
+    grad_partial = jnp.dot(coef, group_hits, preferred_element_type=jnp.float32)
+    if direct:
+        received = shifted_exchange(
+            lambda t: row_block(grad_partial, t, rows).astype(jnp.bfloat16), "phi"
+        )
+        grad_block = row_block(grad_partial, phi_index, rows)
+        for k in range(1, phi_count):
+            grad_block = grad_block + received[k].astype(jnp.float32)
+        mask_grad = by_source(shifted_exchange(lambda t: grad_block, "phi"), "phi").reshape(
+            query_count, model_width
+        )
+    else:
+        mask_grad = narrow_butterfly(grad_partial, "phi")
     hit_grad = reduce_scatter_rows(
         lax.dot_general(
             coef, mask_embed, (((0,), (0,)), ((), ())), preferred_element_type=jnp.float32

time: 107 us -> 136 us (1.27)
  starting transfers between devices: 30.4 us -> 72 us
  waiting for transfers between devices: 44.8 us -> 19.3 us
  local copies, waits for them, and re-layouts: 2.38 us -> 7.79 us
  matrix products: 17.8 us -> 22.8 us
  other arithmetic: 6.39 us -> 8.48 us
    ppermute x21 -> x42, starting transfers between devices: 24.8 us -> 66.4 us  [shifted_exchange(): lax.ppermute(piece_for((index + shift) % count), axis, pairs)]
    ppermute x21 -> x42, waiting for transfers between devices: 43.1 us -> 18.6 us  [shifted_exchange(): lax.ppermute(piece_for((index + shift) % count), axis, pairs)]
    dot_general x1, matrix products: 1.51 us -> 4.9 us  [body(): jnp.einsum('hqk,khd->qhd', raised, value_heads, preferred_element_type=jn...]
    unnamed x25 -> x48, local copies, waits for them, and re-layouts: 1.38 us -> 4.63 us
    gather x0 -> x3, local copies, waits for them, and re-layouts: none -> 1.73 us  [by_source(): return jnp.take(jnp.stack(received), order, axis=0)]
  transfers between devices with their start and end apart: 24 -> 45, of which waited for: 14 -> 17; matrix products, arithmetic and copies ran while one was open for 7% -> 8% of each run, Pallas kernels for 0% -> 0%
where the time goes in v4:
time: 136 us
  starting transfers between devices  72 us (53%)
  matrix products  22.8 us (17%)
  waiting for transfers between devices  19.3 us (14%)
  other arithmetic  8.48 us (6%)
  local copies, waits for them, and re-layouts  7.79 us (6%)
  blocking collectives  4.17 us (3%)
  between operations  1.42 us (1%)
    ppermute x42, starting transfers between devices, shifted_exchange(): lax.ppermute(piece_for((index + shift) % count), axis, pairs)  66.4 us
    ppermute x42, waiting for transfers between devices, shifted_exchange(): lax.ppermute(piece_for((index + shift) % count), axis, pairs)  18.6 us
    sub x1, matrix products, window_attend(): raised = jnp.exp(scores - jnp.max(scores, axis=-1, keepdims=True))  5.1 us
    ppermute x1, starting transfers between devices, extended_2(): lax.ppermute(lax.slice_in_dim(block, 0, width, axis=dim), axis, backward)  5.03 us
    dot_general x1, matrix products, body(): jnp.einsum('hqk,khd->qhd', raised, value_heads, preferred_element_type=jn...  4.9 us
    unnamed x48, local copies, waits for them, and re-layouts  4.63 us
    all_gather x1, blocking collectives, body(): lax.all_gather(jnp.concatenate([local_kv, encoded, digits], axis=1), 'que...  4.17 us
    dot_general x1, matrix products, window_attend(): jnp.einsum('hqk,khd->qhd', weights, value_heads, preferred_element_type=j...  3.99 us
  transfers between devices with their start and end apart: 45, of which 17 were waited for; matrix products, arithmetic and copies ran while one was open for 8% of the time, Pallas kernels for 0%

profile of v4, /device:TPU:0, one launch (start us, length us, event | category | flops | bytes accessed | tf_op | source)
XLA Modules:
  0.0 136.0 jit_solution(5486224725620361735)
XLA Ops:
  3.7 5.0 %collective-permute-start.1 = (bf16[256,512]{1,0:T(8,128)(2,1)S(1)}, bf16[256,512]{1,0:T(8,128)(2,1)S(1)}, u32[]{:S(2)}, u32[]{:S(2)}) collective-permute-start(bf16[256,512]{1,0:T(8,128)(2,1)S(1)} %slice.153), channel_id=1, source_target_pairs={{2,0},{4,2},{6,4},{8,6},{10,8},{12,10},{14,12},{16,14},{18,16},{20... | collective-permute-start | bytes 786440 | tf_op jit(solution)/shard_map/ppermute | solution.py:19
  13.3 5.1 %fusion.102 = (f32[8,256]{1,0:T(8,128)S(1)}, f32[8,256,768]{2,1,0:T(8,128)}) fusion(pred[256,768]{1,0:T(8,128)(4,1)S(1)} %fusion.28, bf16[256,8,32]{0,2,1:T(8,128)(2,1)S(1)} %bitcast.196, bf16[768,8,32]{0,2,1:T(8,128)(2,1)S(1)} %bitcast.191), kind=kOutput, calls=%fused_computation.260 | convolution fusion | flops 106955520 | bytes 7020544 | tf_op jit(solution)/shard_map/sub | solution.py:135
  18.4 4.0 %fusion.11 = bf16[8,32,256]{2,1,0:T(8,128)(2,1)S(1)} fusion(bf16[768,8,32]{0,2,1:T(8,128)(2,1)S(1)} %bitcast.192, f32[8,256,768]{2,1,0:T(8,128)} %get-tuple-element.96, f32[8,256]{1,0:T(8,128)S(1)} %get-tuple-element.95), kind=kOutput, calls=%fused_computation.30 | convolution fusion | flops 103874560 | bytes 6823936 | tf_op jit(solution)/shard_map/hqk,khd->qhd/dot_general | solution.py:137
  24.1 4.2 %all_gather.3 = bf16[512,896]{1,0:T(8,128)(2,1)S(1)} all-gather(bf16[256,896]{1,0:T(8,128)(2,1)S(1)} %fusion.36), channel_id=1, replica_groups=mesh['phi'=8,'query'=2,'event'=2] {'query'}, dimensions={0}, use_global_device_ids=true | all-gather | bytes 1376256 | tf_op jit(solution)/shard_map/all_gather | solution.py:219
  29.8 3.3 %copy-done.1 = f32[8,512,512]{1,2,0:T(8,128)} copy-done((f32[8,512,512]{1,2,0:T(8,128)}, f32[8,512,512]{1,2,0:T(8,128)S(1)}, u32[]{:S(2)}) %copy-start.1) | copy-done | bytes 8388632
  34.6 1.7 %collective-permute-start.6 = (f32[2,8,64]{2,1,0:T(8,128)S(1)}, f32[2,8,64]{2,1,0:T(8,128)S(1)}, u32[]{:S(2)}, u32[]{:S(2)}) collective-permute-start(f32[2,8,64]{2,1,0:T(8,128)S(1)} %get-tuple-element.74), channel_id=1, source_target_pairs={{0,20},{4,24},{8,28},{12,0},{16,4},{20,8},{24,12},{28,16},{1,21},{... | collective-permute-start | bytes 12296 | tf_op jit(solution)/shard_map/ppermute | solution.py:98
  37.8 1.6 %collective-permute-start.2 = (f32[2,8,64]{2,1,0:T(8,128)S(1)}, f32[2,8,64]{2,1,0:T(8,128)S(1)}, u32[]{:S(2)}, u32[]{:S(2)}) collective-permute-start(f32[2,8,64]{2,1,0:T(8,128)S(1)} %get-tuple-element.69), channel_id=1, source_target_pairs={{0,4},{4,8},{8,12},{12,16},{16,20},{20,24},{24,28},{28,0},{1,5},{5... | collective-permute-start | bytes 12296 | tf_op jit(solution)/shard_map/ppermute | solution.py:98
  39.4 1.6 %collective-permute-start.3 = (f32[2,8,64]{2,1,0:T(8,128)S(1)}, f32[2,8,64]{2,1,0:T(8,128)S(1)}, u32[]{:S(2)}, u32[]{:S(2)}) collective-permute-start(f32[2,8,64]{2,1,0:T(8,128)S(1)} %get-tuple-element.70), channel_id=1, source_target_pairs={{0,8},{4,12},{8,16},{12,20},{16,24},{20,28},{24,0},{28,4},{1,9},{5... | collective-permute-start | bytes 12296 | tf_op jit(solution)/shard_map/ppermute | solution.py:98
  41.2 4.9 %convolution_convert_fusion.1 = bf16[8,32,512]{2,1,0:T(8,128)(2,1)S(1)} fusion(bf16[512,8,32]{0,2,1:T(8,128)(2,1)S(1)} %bitcast.188, f32[8,512,512]{1,2,0:T(8,128)} %copy-done.1, f32[8,512]{1,0:T(8,128)S(1)} %get-tuple-element.101), kind=kOutput, calls=%fused_computation.24 | convolution fusion | flops 140640256 | bytes 8929280 | tf_op jit(solution)/shard_map/hqk,khd->qhd/dot_general | solution.py:238
  46.1 2.9 %collective-permute-start.5 = (f32[2,8,64]{2,1,0:T(8,128)S(1)}, f32[2,8,64]{2,1,0:T(8,128)S(1)}, u32[]{:S(2)}, u32[]{:S(2)}) collective-permute-start(f32[2,8,64]{2,1,0:T(8,128)S(1)} %get-tuple-element.72), channel_id=1, source_target_pairs={{0,16},{4,20},{8,24},{12,28},{16,0},{20,4},{24,8},{28,12},{1,17},{... | collective-permute-start | bytes 12296 | tf_op jit(solution)/shard_map/ppermute | solution.py:98
  49.0 3.2 %collective-permute-start.8 = (f32[2,8,64]{2,1,0:T(8,128)S(1)}, f32[2,8,64]{2,1,0:T(8,128)S(1)}, u32[]{:S(2)}, u32[]{:S(2)}) collective-permute-start(f32[2,8,64]{2,1,0:T(8,128)S(1)} %get-tuple-element.67), channel_id=1, source_target_pairs={{0,28},{4,0},{8,4},{12,8},{16,12},{20,16},{24,20},{28,24},{1,29},{... | collective-permute-start | bytes 12296 | tf_op jit(solution)/shard_map/ppermute | solution.py:98
  52.7 2.4 %collective-permute-start.12 = (bf16[64,256]{0,1:T(8,128)(2,1)S(1)}, bf16[64,256]{0,1:T(8,128)(2,1)S(1)}, u32[]{:S(2)}, u32[]{:S(2)}) collective-permute-start(bf16[64,256]{0,1:T(8,128)(2,1)S(1)} %get-tuple-element.56), channel_id=1, source_target_pairs={{0,16},{4,20},{8,24},{12,28},{16,0},{20,4},{24,8},{28,12},{1,17},{... | collective-permute-start | bytes 98312 | tf_op jit(solution)/shard_map/ppermute | solution.py:98
  56.6 3.6 %collective-permute-start.14 = (bf16[64,256]{0,1:T(8,128)(2,1)S(1)}, bf16[64,256]{0,1:T(8,128)(2,1)S(1)}, u32[]{:S(2)}, u32[]{:S(2)}) collective-permute-start(bf16[64,256]{0,1:T(8,128)(2,1)S(1)} %get-tuple-element.54), channel_id=1, source_target_pairs={{0,24},{4,28},{8,0},{12,4},{16,8},{20,12},{24,16},{28,20},{1,25},{... | collective-permute-start | bytes 98312 | tf_op jit(solution)/shard_map/ppermute | solution.py:98
  63.2 1.8 %collective-permute-done.15 = bf16[64,256]{0,1:T(8,128)(2,1)S(1)} collective-permute-done((bf16[64,256]{0,1:T(8,128)(2,1)S(1)}, bf16[64,256]{0,1:T(8,128)(2,1)S(1)}, u32[]{:S(2)}, u32[]{:S(2)}) %collective-permute-start.15) | collective-permute-done | bytes 32800 | tf_op jit(solution)/shard_map/ppermute | solution.py:98
  65.0 2.9 %collective-permute-done.9 = bf16[64,256]{0,1:T(8,128)(2,1)S(1)} collective-permute-done((bf16[64,256]{0,1:T(8,128)(2,1)S(1)}, bf16[64,256]{0,1:T(8,128)(2,1)S(1)}, u32[]{:S(2)}, u32[]{:S(2)}) %collective-permute-start.9) | collective-permute-done | bytes 32800 | tf_op jit(solution)/shard_map/ppermute | solution.py:98
  70.4 4.2 %collective-permute-start.18 = (bf16[64,256]{1,0:T(8,128)(2,1)S(1)}, bf16[64,256]{1,0:T(8,128)(2,1)S(1)}, u32[]{:S(2)}, u32[]{:S(2)}) collective-permute-start(bf16[64,256]{1,0:T(8,128)(2,1)S(1)} %get-tuple-element.106), channel_id=1, source_target_pairs={{0,12},{4,16},{8,20},{12,24},{16,28},{20,0},{24,4},{28,8},{1,13},{... | collective-permute-start | bytes 98312 | tf_op jit(solution)/shard_map/ppermute | solution.py:98
  75.3 1.6 %collective-permute-start.20 = (bf16[64,256]{1,0:T(8,128)(2,1)S(1)}, bf16[64,256]{1,0:T(8,128)(2,1)S(1)}, u32[]{:S(2)}, u32[]{:S(2)}) collective-permute-start(bf16[64,256]{1,0:T(8,128)(2,1)S(1)} %get-tuple-element.106), channel_id=1, source_target_pairs={{0,20},{4,24},{8,28},{12,0},{16,4},{20,8},{24,12},{28,16},{1,21},{... | collective-permute-start | bytes 98312 | tf_op jit(solution)/shard_map/ppermute | solution.py:98
  78.2 1.7 %collective-permute-start.22 = (bf16[64,256]{1,0:T(8,128)(2,1)S(1)}, bf16[64,256]{1,0:T(8,128)(2,1)S(1)}, u32[]{:S(2)}, u32[]{:S(2)}) collective-permute-start(bf16[64,256]{1,0:T(8,128)(2,1)S(1)} %get-tuple-element.106), channel_id=1, source_target_pairs={{0,28},{4,0},{8,4},{12,8},{16,12},{20,16},{24,20},{28,24},{1,29},{... | collective-permute-start | bytes 98312 | tf_op jit(solution)/shard_map/ppermute | solution.py:98
  83.1 1.6 %select_reduce_fusion = (f32[512]{0:T(512)S(1)}, f32[512]{0:T(512)S(1)}, f32[512]{0:T(512)S(1)}, f32[512,512]{0,1:T(8,128)}) fusion(s32[512]{0:T(512)S(1)} %copy-done.9, s32[512]{0:T(512)S(1)} %fusion.46, pred[512]{0:T(512)(128)(4,1)S(1)} %get-tuple-element.36, bf16[512,256]{1,0:T(8,128)(2,1)S(1)} %bitcast_select_fusion.1, bf16[512,896]{1,0:T(8,128)(2,1)S(1)} %all_gather.3), kind=kOutput, calls=%fused_computation.47 | convolution fusion | flops 137099776 | bytes 1583616 | tf_op jit(solution)/shard_map/dot_general | solution.py:287
  84.8 3.0 %collective-permute-start.23 = (f32[3,512]{1,0:T(4,128)S(1)}, f32[3,512]{1,0:T(4,128)S(1)}, u32[]{:S(2)}, u32[]{:S(2)}) collective-permute-start(f32[3,512]{1,0:T(4,128)S(1)} %pad_maximum_fusion.1), channel_id=1, source_target_pairs={{0,4},{4,8},{8,12},{12,16},{16,20},{20,24},{24,28},{28,0},{1,5},{5... | collective-permute-start | bytes 18440 | tf_op jit(solution)/shard_map/ppermute | solution.py:98
  89.4 2.2 %collective-permute-start.26 = (f32[3,512]{1,0:T(4,128)S(1)}, f32[3,512]{1,0:T(4,128)S(1)}, u32[]{:S(2)}, u32[]{:S(2)}) collective-permute-start(f32[3,512]{1,0:T(4,128)S(1)} %pad_maximum_fusion.1), channel_id=1, source_target_pairs={{0,16},{4,20},{8,24},{12,28},{16,0},{20,4},{24,8},{28,12},{1,17},{... | collective-permute-start | bytes 18440 | tf_op jit(solution)/shard_map/ppermute | solution.py:98
  91.6 2.4 %collective-permute-start.27 = (f32[3,512]{1,0:T(4,128)S(1)}, f32[3,512]{1,0:T(4,128)S(1)}, u32[]{:S(2)}, u32[]{:S(2)}) collective-permute-start(f32[3,512]{1,0:T(4,128)S(1)} %pad_maximum_fusion.1), channel_id=1, source_target_pairs={{0,20},{4,24},{8,28},{12,0},{16,4},{20,8},{24,12},{28,16},{1,21},{... | collective-permute-start | bytes 18440 | tf_op jit(solution)/shard_map/ppermute | solution.py:98
  100.4 1.8 %fusion.16 = bf16[512,512]{0,1:T(8,128)(2,1)S(1)} fusion(f32[512,512]{0,1:T(8,128)} %get-tuple-element.107, f32[512]{0:T(512)S(1)} %bitcast.198, f32[512]{0:T(512)S(1)} %bitcast.197, s32[512]{0:T(512)S(1)} %copy-done.9, f32[512]{0:T(512)S(1)} %get-tuple-element.35, s32[512]{0:T(512)S(1)} %fusion.46, pred[512]{0:T(512)(128)(4,1)S(1)} %get-tuple-element.36), kind=kLoop, calls=%fused_computation.38 | loop fusion | flops 3670016 | bytes 1583616 | tf_op jit(solution)/shard_map/convert_element_type | solution.py:172
  102.6 1.5 %collective-permute-start.31 = (bf16[64,256]{1,0:T(8,128)(2,1)S(1)}, bf16[64,256]{1,0:T(8,128)(2,1)S(1)}, u32[]{:S(2)}, u32[]{:S(2)}) collective-permute-start(bf16[64,256]{1,0:T(8,128)(2,1)S(1)} %get-tuple-element.45), channel_id=1, source_target_pairs={{0,4},{4,8},{8,12},{12,16},{16,20},{20,24},{24,28},{28,0},{1,5},{5... | collective-permute-start | bytes 98312 | tf_op jit(solution)/shard_map/ppermute | solution.py:98
  104.8 1.7 %collective-permute-start.33 = (bf16[64,256]{1,0:T(8,128)(2,1)S(1)}, bf16[64,256]{1,0:T(8,128)(2,1)S(1)}, u32[]{:S(2)}, u32[]{:S(2)}) collective-permute-start(bf16[64,256]{1,0:T(8,128)(2,1)S(1)} %get-tuple-element.50), channel_id=1, source_target_pairs={{0,12},{4,16},{8,20},{12,24},{16,28},{20,0},{24,4},{28,8},{1,13},{... | collective-permute-start | bytes 98312 | tf_op jit(solution)/shard_map/ppermute | solution.py:98
  106.5 2.1 %collective-permute-start.34 = (bf16[64,256]{1,0:T(8,128)(2,1)S(1)}, bf16[64,256]{1,0:T(8,128)(2,1)S(1)}, u32[]{:S(2)}, u32[]{:S(2)}) collective-permute-start(bf16[64,256]{1,0:T(8,128)(2,1)S(1)} %get-tuple-element.49), channel_id=1, source_target_pairs={{0,16},{4,20},{8,24},{12,28},{16,0},{20,4},{24,8},{28,12},{1,17},{... | collective-permute-start | bytes 98312 | tf_op jit(solution)/shard_map/ppermute | solution.py:98
  108.6 3.0 %collective-permute-start.35 = (bf16[64,256]{1,0:T(8,128)(2,1)S(1)}, bf16[64,256]{1,0:T(8,128)(2,1)S(1)}, u32[]{:S(2)}, u32[]{:S(2)}) collective-permute-start(bf16[64,256]{1,0:T(8,128)(2,1)S(1)} %get-tuple-element.48), channel_id=1, source_target_pairs={{0,20},{4,24},{8,28},{12,0},{16,4},{20,8},{24,12},{28,16},{1,21},{... | collective-permute-start | bytes 98312 | tf_op jit(solution)/shard_map/ppermute | solution.py:98
  111.8 2.6 %collective-permute-start.37 = (bf16[64,256]{1,0:T(8,128)(2,1)S(1)}, bf16[64,256]{1,0:T(8,128)(2,1)S(1)}, u32[]{:S(2)}, u32[]{:S(2)}) collective-permute-start(bf16[64,256]{1,0:T(8,128)(2,1)S(1)} %get-tuple-element.46), channel_id=1, source_target_pairs={{0,28},{4,0},{8,4},{12,8},{16,12},{20,16},{24,20},{28,24},{1,29},{... | collective-permute-start | bytes 98312 | tf_op jit(solution)/shard_map/ppermute | solution.py:98
  117.6 1.9 %collective-permute-start.39 = (f32[64,256]{1,0:T(8,128)S(1)}, f32[64,256]{1,0:T(8,128)S(1)}, u32[]{:S(2)}, u32[]{:S(2)}) collective-permute-start(f32[64,256]{1,0:T(8,128)S(1)} %get-tuple-element.34), channel_id=1, source_target_pairs={{0,8},{4,12},{8,16},{12,20},{16,24},{20,28},{24,0},{28,4},{1,9},{5... | collective-permute-start | bytes 196616 | tf_op jit(solution)/shard_map/ppermute | solution.py:98
  120.1 3.1 %collective-permute-start.41 = (f32[64,256]{1,0:T(8,128)S(1)}, f32[64,256]{1,0:T(8,128)S(1)}, u32[]{:S(2)}, u32[]{:S(2)}) collective-permute-start(f32[64,256]{1,0:T(8,128)S(1)} %get-tuple-element.34), channel_id=1, source_target_pairs={{0,16},{4,20},{8,24},{12,28},{16,0},{20,4},{24,8},{28,12},{1,17},{... | collective-permute-start | bytes 196616 | tf_op jit(solution)/shard_map/ppermute | solution.py:98
  123.4 2.9 %collective-permute-start.42 = (f32[64,256]{1,0:T(8,128)S(1)}, f32[64,256]{1,0:T(8,128)S(1)}, u32[]{:S(2)}, u32[]{:S(2)}) collective-permute-start(f32[64,256]{1,0:T(8,128)S(1)} %get-tuple-element.34), channel_id=1, source_target_pairs={{0,20},{4,24},{8,28},{12,0},{16,4},{20,8},{24,12},{28,16},{1,21},{... | collective-permute-start | bytes 196616 | tf_op jit(solution)/shard_map/ppermute | solution.py:98
  126.8 2.7 %collective-permute-done.40 = f32[64,256]{1,0:T(8,128)S(1)} collective-permute-done((f32[64,256]{1,0:T(8,128)S(1)}, f32[64,256]{1,0:T(8,128)S(1)}, u32[]{:S(2)}, u32[]{:S(2)}) %collective-permute-start.40) | collective-permute-done | bytes 65568 | tf_op jit(solution)/shard_map/ppermute | solution.py:98
  (187 shorter events, 46.2 us)
Async XLA Ops:
  3.2 9.6 %collective-permute-start = (bf16[256,512]{1,0:T(8,128)(2,1)S(1)}, bf16[256,512]{1,0:T(8,128)(2,1)S(1)}, u32[]{:S(2)}, u32[]{:S(2)}) collective-permute-start(bf16[256,512]{1,0:T(8,128)(2,1)S(1)} %slice.153), channel_id=1, source_target_pairs={{0,2},{2,4},{4,6},{6,8},{8,10},{10,12},{12,14},{14,16},{16,18},{18... | collective-permute-start | bytes 786440 | tf_op jit(solution)/shard_map/ppermute | solution.py:16
  3.7 9.1 %collective-permute-start.1 = (bf16[256,512]{1,0:T(8,128)(2,1)S(1)}, bf16[256,512]{1,0:T(8,128)(2,1)S(1)}, u32[]{:S(2)}, u32[]{:S(2)}) collective-permute-start(bf16[256,512]{1,0:T(8,128)(2,1)S(1)} %slice.153), channel_id=1, source_target_pairs={{2,0},{4,2},{6,4},{8,6},{10,8},{12,10},{14,12},{16,14},{18,16},{20... | collective-permute-start | bytes 786440 | tf_op jit(solution)/shard_map/ppermute | solution.py:19
  34.6 11.4 %collective-permute-start.6 = (f32[2,8,64]{2,1,0:T(8,128)S(1)}, f32[2,8,64]{2,1,0:T(8,128)S(1)}, u32[]{:S(2)}, u32[]{:S(2)}) collective-permute-start(f32[2,8,64]{2,1,0:T(8,128)S(1)} %get-tuple-element.74), channel_id=1, source_target_pairs={{0,20},{4,24},{8,28},{12,0},{16,4},{20,8},{24,12},{28,16},{1,21},{... | collective-permute-start | bytes 12296 | tf_op jit(solution)/shard_map/ppermute | solution.py:98
  36.4 12.6 %collective-permute-start.7 = (f32[2,8,64]{2,1,0:T(8,128)S(1)}, f32[2,8,64]{2,1,0:T(8,128)S(1)}, u32[]{:S(2)}, u32[]{:S(2)}) collective-permute-start(f32[2,8,64]{2,1,0:T(8,128)S(1)} %get-tuple-element.73), channel_id=1, source_target_pairs={{0,24},{4,28},{8,0},{12,4},{16,8},{20,12},{24,16},{28,20},{1,25},{... | collective-permute-start | bytes 12296 | tf_op jit(solution)/shard_map/ppermute | solution.py:98
  37.8 14.6 %collective-permute-start.2 = (f32[2,8,64]{2,1,0:T(8,128)S(1)}, f32[2,8,64]{2,1,0:T(8,128)S(1)}, u32[]{:S(2)}, u32[]{:S(2)}) collective-permute-start(f32[2,8,64]{2,1,0:T(8,128)S(1)} %get-tuple-element.69), channel_id=1, source_target_pairs={{0,4},{4,8},{8,12},{12,16},{16,20},{20,24},{24,28},{28,0},{1,5},{5... | collective-permute-start | bytes 12296 | tf_op jit(solution)/shard_map/ppermute | solution.py:98
  39.4 13.1 %collective-permute-start.3 = (f32[2,8,64]{2,1,0:T(8,128)S(1)}, f32[2,8,64]{2,1,0:T(8,128)S(1)}, u32[]{:S(2)}, u32[]{:S(2)}) collective-permute-start(f32[2,8,64]{2,1,0:T(8,128)S(1)} %get-tuple-element.70), channel_id=1, source_target_pairs={{0,8},{4,12},{8,16},{12,20},{16,24},{20,28},{24,0},{28,4},{1,9},{5... | collective-permute-start | bytes 12296 | tf_op jit(solution)/shard_map/ppermute | solution.py:98
  41.0 11.8 %collective-permute-start.4 = (f32[2,8,64]{2,1,0:T(8,128)S(1)}, f32[2,8,64]{2,1,0:T(8,128)S(1)}, u32[]{:S(2)}, u32[]{:S(2)}) collective-permute-start(f32[2,8,64]{2,1,0:T(8,128)S(1)} %get-tuple-element.71), channel_id=1, source_target_pairs={{0,12},{4,16},{8,20},{12,24},{16,28},{20,0},{24,4},{28,8},{1,13},{... | collective-permute-start | bytes 12296 | tf_op jit(solution)/shard_map/ppermute | solution.py:98
  46.1 9.0 %collective-permute-start.5 = (f32[2,8,64]{2,1,0:T(8,128)S(1)}, f32[2,8,64]{2,1,0:T(8,128)S(1)}, u32[]{:S(2)}, u32[]{:S(2)}) collective-permute-start(f32[2,8,64]{2,1,0:T(8,128)S(1)} %get-tuple-element.72), channel_id=1, source_target_pairs={{0,16},{4,20},{8,24},{12,28},{16,0},{20,4},{24,8},{28,12},{1,17},{... | collective-permute-start | bytes 12296 | tf_op jit(solution)/shard_map/ppermute | solution.py:98
  49.0 7.6 %collective-permute-start.8 = (f32[2,8,64]{2,1,0:T(8,128)S(1)}, f32[2,8,64]{2,1,0:T(8,128)S(1)}, u32[]{:S(2)}, u32[]{:S(2)}) collective-permute-start(f32[2,8,64]{2,1,0:T(8,128)S(1)} %get-tuple-element.67), channel_id=1, source_target_pairs={{0,28},{4,0},{8,4},{12,8},{16,12},{20,16},{24,20},{28,24},{1,29},{... | collective-permute-start | bytes 12296 | tf_op jit(solution)/shard_map/ppermute | solution.py:98
  52.4 7.9 %collective-permute-start.10 = (bf16[64,256]{0,1:T(8,128)(2,1)S(1)}, bf16[64,256]{0,1:T(8,128)(2,1)S(1)}, u32[]{:S(2)}, u32[]{:S(2)}) collective-permute-start(bf16[64,256]{0,1:T(8,128)(2,1)S(1)} %get-tuple-element.58), channel_id=1, source_target_pairs={{0,8},{4,12},{8,16},{12,20},{16,24},{20,28},{24,0},{28,4},{1,9},{5... | collective-permute-start | bytes 98312 | tf_op jit(solution)/shard_map/ppermute | solution.py:98
  52.5 8.5 %collective-permute-start.11 = (bf16[64,256]{0,1:T(8,128)(2,1)S(1)}, bf16[64,256]{0,1:T(8,128)(2,1)S(1)}, u32[]{:S(2)}, u32[]{:S(2)}) collective-permute-start(bf16[64,256]{0,1:T(8,128)(2,1)S(1)} %get-tuple-element.57), channel_id=1, source_target_pairs={{0,12},{4,16},{8,20},{12,24},{16,28},{20,0},{24,4},{28,8},{1,13},{... | collective-permute-start | bytes 98312 | tf_op jit(solution)/shard_map/ppermute | solution.py:98
  52.7 9.7 %collective-permute-start.12 = (bf16[64,256]{0,1:T(8,128)(2,1)S(1)}, bf16[64,256]{0,1:T(8,128)(2,1)S(1)}, u32[]{:S(2)}, u32[]{:S(2)}) collective-permute-start(bf16[64,256]{0,1:T(8,128)(2,1)S(1)} %get-tuple-element.56), channel_id=1, source_target_pairs={{0,16},{4,20},{8,24},{12,28},{16,0},{20,4},{24,8},{28,12},{1,17},{... | collective-permute-start | bytes 98312 | tf_op jit(solution)/shard_map/ppermute | solution.py:98
  55.1 7.3 %collective-permute-start.13 = (bf16[64,256]{0,1:T(8,128)(2,1)S(1)}, bf16[64,256]{0,1:T(8,128)(2,1)S(1)}, u32[]{:S(2)}, u32[]{:S(2)}) collective-permute-start(bf16[64,256]{0,1:T(8,128)(2,1)S(1)} %get-tuple-element.55), channel_id=1, source_target_pairs={{0,20},{4,24},{8,28},{12,0},{16,4},{20,8},{24,12},{28,16},{1,21},{... | collective-permute-start | bytes 98312 | tf_op jit(solution)/shard_map/ppermute | solution.py:98
  60.9 7.0 %collective-permute-start.9 = (bf16[64,256]{0,1:T(8,128)(2,1)S(1)}, bf16[64,256]{0,1:T(8,128)(2,1)S(1)}, u32[]{:S(2)}, u32[]{:S(2)}) collective-permute-start(bf16[64,256]{0,1:T(8,128)(2,1)S(1)} %get-tuple-element.52), channel_id=1, source_target_pairs={{0,4},{4,8},{8,12},{12,16},{16,20},{20,24},{24,28},{28,0},{1,5},{5... | collective-permute-start | bytes 98312 | tf_op jit(solution)/shard_map/ppermute | solution.py:98
  69.7 7.3 %collective-permute-start.16 = (bf16[64,256]{1,0:T(8,128)(2,1)S(1)}, bf16[64,256]{1,0:T(8,128)(2,1)S(1)}, u32[]{:S(2)}, u32[]{:S(2)}) collective-permute-start(bf16[64,256]{1,0:T(8,128)(2,1)S(1)} %get-tuple-element.106), channel_id=1, source_target_pairs={{0,4},{4,8},{8,12},{12,16},{16,20},{20,24},{24,28},{28,0},{1,5},{5... | collective-permute-start | bytes 98312 | tf_op jit(solution)/shard_map/ppermute | solution.py:98
  70.0 8.3 %collective-permute-start.17 = (bf16[64,256]{1,0:T(8,128)(2,1)S(1)}, bf16[64,256]{1,0:T(8,128)(2,1)S(1)}, u32[]{:S(2)}, u32[]{:S(2)}) collective-permute-start(bf16[64,256]{1,0:T(8,128)(2,1)S(1)} %get-tuple-element.106), channel_id=1, source_target_pairs={{0,8},{4,12},{8,16},{12,20},{16,24},{20,28},{24,0},{28,4},{1,9},{5... | collective-permute-start | bytes 98312 | tf_op jit(solution)/shard_map/ppermute | solution.py:98
  70.4 9.6 %collective-permute-start.18 = (bf16[64,256]{1,0:T(8,128)(2,1)S(1)}, bf16[64,256]{1,0:T(8,128)(2,1)S(1)}, u32[]{:S(2)}, u32[]{:S(2)}) collective-permute-start(bf16[64,256]{1,0:T(8,128)(2,1)S(1)} %get-tuple-element.106), channel_id=1, source_target_pairs={{0,12},{4,16},{8,20},{12,24},{16,28},{20,0},{24,4},{28,8},{1,13},{... | collective-permute-start | bytes 98312 | tf_op jit(solution)/shard_map/ppermute | solution.py:98
  84.8 9.3 %collective-permute-start.23 = (f32[3,512]{1,0:T(4,128)S(1)}, f32[3,512]{1,0:T(4,128)S(1)}, u32[]{:S(2)}, u32[]{:S(2)}) collective-permute-start(f32[3,512]{1,0:T(4,128)S(1)} %pad_maximum_fusion.1), channel_id=1, source_target_pairs={{0,4},{4,8},{8,12},{12,16},{16,20},{20,24},{24,28},{28,0},{1,5},{5... | collective-permute-start | bytes 18440 | tf_op jit(solution)/shard_map/ppermute | solution.py:98
  87.7 7.7 %collective-permute-start.24 = (f32[3,512]{1,0:T(4,128)S(1)}, f32[3,512]{1,0:T(4,128)S(1)}, u32[]{:S(2)}, u32[]{:S(2)}) collective-permute-start(f32[3,512]{1,0:T(4,128)S(1)} %pad_maximum_fusion.1), channel_id=1, source_target_pairs={{0,8},{4,12},{8,16},{12,20},{16,24},{20,28},{24,0},{28,4},{1,9},{5... | collective-permute-start | bytes 18440 | tf_op jit(solution)/shard_map/ppermute | solution.py:98
  89.0 7.7 %collective-permute-start.25 = (f32[3,512]{1,0:T(4,128)S(1)}, f32[3,512]{1,0:T(4,128)S(1)}, u32[]{:S(2)}, u32[]{:S(2)}) collective-permute-start(f32[3,512]{1,0:T(4,128)S(1)} %pad_maximum_fusion.1), channel_id=1, source_target_pairs={{0,12},{4,16},{8,20},{12,24},{16,28},{20,0},{24,4},{28,8},{1,13},{... | collective-permute-start | bytes 18440 | tf_op jit(solution)/shard_map/ppermute | solution.py:98
  89.4 7.3 %collective-permute-start.26 = (f32[3,512]{1,0:T(4,128)S(1)}, f32[3,512]{1,0:T(4,128)S(1)}, u32[]{:S(2)}, u32[]{:S(2)}) collective-permute-start(f32[3,512]{1,0:T(4,128)S(1)} %pad_maximum_fusion.1), channel_id=1, source_target_pairs={{0,16},{4,20},{8,24},{12,28},{16,0},{20,4},{24,8},{28,12},{1,17},{... | collective-permute-start | bytes 18440 | tf_op jit(solution)/shard_map/ppermute | solution.py:98
  102.6 9.0 %collective-permute-start.31 = (bf16[64,256]{1,0:T(8,128)(2,1)S(1)}, bf16[64,256]{1,0:T(8,128)(2,1)S(1)}, u32[]{:S(2)}, u32[]{:S(2)}) collective-permute-start(bf16[64,256]{1,0:T(8,128)(2,1)S(1)} %get-tuple-element.45), channel_id=1, source_target_pairs={{0,4},{4,8},{8,12},{12,16},{16,20},{20,24},{24,28},{28,0},{1,5},{5... | collective-permute-start | bytes 98312 | tf_op jit(solution)/shard_map/ppermute | solution.py:98
  104.2 7.7 %collective-permute-start.32 = (bf16[64,256]{1,0:T(8,128)(2,1)S(1)}, bf16[64,256]{1,0:T(8,128)(2,1)S(1)}, u32[]{:S(2)}, u32[]{:S(2)}) collective-permute-start(bf16[64,256]{1,0:T(8,128)(2,1)S(1)} %get-tuple-element.51), channel_id=1, source_target_pairs={{0,8},{4,12},{8,16},{12,20},{16,24},{20,28},{24,0},{28,4},{1,9},{5... | collective-permute-start | bytes 98312 | tf_op jit(solution)/shard_map/ppermute | solution.py:98
  104.8 9.9 %collective-permute-start.33 = (bf16[64,256]{1,0:T(8,128)(2,1)S(1)}, bf16[64,256]{1,0:T(8,128)(2,1)S(1)}, u32[]{:S(2)}, u32[]{:S(2)}) collective-permute-start(bf16[64,256]{1,0:T(8,128)(2,1)S(1)} %get-tuple-element.50), channel_id=1, source_target_pairs={{0,12},{4,16},{8,20},{12,24},{16,28},{20,0},{24,4},{28,8},{1,13},{... | collective-permute-start | bytes 98312 | tf_op jit(solution)/shard_map/ppermute | solution.py:98
  106.5 8.2 %collective-permute-start.34 = (bf16[64,256]{1,0:T(8,128)(2,1)S(1)}, bf16[64,256]{1,0:T(8,128)(2,1)S(1)}, u32[]{:S(2)}, u32[]{:S(2)}) collective-permute-start(bf16[64,256]{1,0:T(8,128)(2,1)S(1)} %get-tuple-element.49), channel_id=1, source_target_pairs={{0,16},{4,20},{8,24},{12,28},{16,0},{20,4},{24,8},{28,12},{1,17},{... | collective-permute-start | bytes 98312 | tf_op jit(solution)/shard_map/ppermute | solution.py:98
  116.0 7.3 %collective-permute-start.38 = (f32[64,256]{1,0:T(8,128)S(1)}, f32[64,256]{1,0:T(8,128)S(1)}, u32[]{:S(2)}, u32[]{:S(2)}) collective-permute-start(f32[64,256]{1,0:T(8,128)S(1)} %get-tuple-element.34), channel_id=1, source_target_pairs={{0,4},{4,8},{8,12},{12,16},{16,20},{20,24},{24,28},{28,0},{1,5},{5... | collective-permute-start | bytes 196616 | tf_op jit(solution)/shard_map/ppermute | solution.py:98
  117.6 17.7 %collective-permute-start.30 = (f32[256,256]{1,0:T(8,128)S(1)}, f32[256,256]{1,0:T(8,128)S(1)}, u32[]{:S(2)}, u32[]{:S(2)}) collective-permute-start(f32[256,256]{1,0:T(8,128)S(1)} %slice_select_fusion), channel_id=1, source_target_pairs={{0,2},{2,0},{1,3},{3,1},{4,6},{6,4},{5,7},{7,5},{8,10},{10,8},{9,1... | collective-permute-start | bytes 786440 | tf_op jit(solution)/shard_map/ppermute | solution.py:87
  117.6 8.6 %collective-permute-start.39 = (f32[64,256]{1,0:T(8,128)S(1)}, f32[64,256]{1,0:T(8,128)S(1)}, u32[]{:S(2)}, u32[]{:S(2)}) collective-permute-start(f32[64,256]{1,0:T(8,128)S(1)} %get-tuple-element.34), channel_id=1, source_target_pairs={{0,8},{4,12},{8,16},{12,20},{16,24},{20,28},{24,0},{28,4},{1,9},{5... | collective-permute-start | bytes 196616 | tf_op jit(solution)/shard_map/ppermute | solution.py:98
  119.5 9.9 %collective-permute-start.40 = (f32[64,256]{1,0:T(8,128)S(1)}, f32[64,256]{1,0:T(8,128)S(1)}, u32[]{:S(2)}, u32[]{:S(2)}) collective-permute-start(f32[64,256]{1,0:T(8,128)S(1)} %get-tuple-element.34), channel_id=1, source_target_pairs={{0,12},{4,16},{8,20},{12,24},{16,28},{20,0},{24,4},{28,8},{1,13},{... | collective-permute-start | bytes 196616 | tf_op jit(solution)/shard_map/ppermute | solution.py:98
  120.1 10.3 %collective-permute-start.41 = (f32[64,256]{1,0:T(8,128)S(1)}, f32[64,256]{1,0:T(8,128)S(1)}, u32[]{:S(2)}, u32[]{:S(2)}) collective-permute-start(f32[64,256]{1,0:T(8,128)S(1)} %get-tuple-element.34), channel_id=1, source_target_pairs={{0,16},{4,20},{8,24},{12,28},{16,0},{20,4},{24,8},{28,12},{1,17},{... | collective-permute-start | bytes 196616 | tf_op jit(solution)/shard_map/ppermute | solution.py:98
  123.4 8.2 %collective-permute-start.42 = (f32[64,256]{1,0:T(8,128)S(1)}, f32[64,256]{1,0:T(8,128)S(1)}, u32[]{:S(2)}, u32[]{:S(2)}) collective-permute-start(f32[64,256]{1,0:T(8,128)S(1)} %get-tuple-element.34), channel_id=1, source_target_pairs={{0,20},{4,24},{8,28},{12,0},{16,4},{20,8},{24,12},{28,16},{1,21},{... | collective-permute-start | bytes 196616 | tf_op jit(solution)/shard_map/ppermute | solution.py:98
  126.3 6.8 %collective-permute-start.43 = (f32[64,256]{1,0:T(8,128)S(1)}, f32[64,256]{1,0:T(8,128)S(1)}, u32[]{:S(2)}, u32[]{:S(2)}) collective-permute-start(f32[64,256]{1,0:T(8,128)S(1)} %get-tuple-element.34), channel_id=1, source_target_pairs={{0,24},{4,28},{8,0},{12,4},{16,8},{20,12},{24,16},{28,20},{1,25},{... | collective-permute-start | bytes 196616 | tf_op jit(solution)/shard_map/ppermute | solution.py:98
  (24 other events, 285.5 us)

commit v5 on v2

--- a/solution.py
+++ b/solution.py
@@ -85,6 +85,74 @@
         keep = jnp.where(upper, high, low)
         send = jnp.where(upper, low, high)
         block = keep + lax.ppermute(send, axis, partner_pairs(count, distance))
+        distance //= 2
+    return block
+
+
+def halves(array, upper, axis):
+    size = array.shape[axis] // 2
+    low = lax.slice_in_dim(array, 0, size, axis=axis)
+    high = lax.slice_in_dim(array, size, 2 * size, axis=axis)
+    return jnp.where(upper, high, low), jnp.where(upper, low, high)
+
+
+def owned_block(axis):
+    count = lax.axis_size(axis)
+    index = lax.axis_index(axis)
+    offset, size, distance = 0, count, 1
+    while distance < count:
+        size //= 2
+        offset = offset + ((index // distance) % 2) * size
+        distance *= 2
+    return offset
+
+
+def scatter_softmax(stats, mixed, axis):
+    count = lax.axis_size(axis)
+    assert count & (count - 1) == 0
+    index = lax.axis_index(axis)
+    distance = 1
+    while distance < count:
+        upper = (index // distance) % 2 == 1
+        keep_stats, send_stats = halves(stats, upper, 2)
+        keep_mixed, send_mixed = halves(mixed, upper, 0)
+        other_stats, other_mixed = lax.ppermute(
+            (send_stats, send_mixed.astype(jnp.bfloat16)), axis, partner_pairs(count, distance)
+        )
+        top = jnp.maximum(keep_stats[0], other_stats[0])
+        factor_keep = jnp.exp(keep_stats[0] - top)
+        factor_other = jnp.exp(other_stats[0] - top)
+        stats = jnp.stack([top, keep_stats[1] * factor_keep + other_stats[1] * factor_other])
+        mixed = scale_heads(keep_mixed.astype(jnp.float32), factor_keep) + scale_heads(
+            other_mixed.astype(jnp.float32), factor_other
+        )
+        distance *= 2
+    return stats, mixed
+
+
+def scatter_sum(block, axis):
+    count = lax.axis_size(axis)
+    index = lax.axis_index(axis)
+    distance = 1
+    while distance < count:
+        upper = (index // distance) % 2 == 1
+        keep, send = halves(block, upper, 0)
+        other = lax.ppermute(send.astype(jnp.bfloat16), axis, partner_pairs(count, distance))
+        block = keep + other.astype(jnp.float32)
+        distance *= 2
+    return block
+
+
+def gather_blocks(block, axis):
+    count = lax.axis_size(axis)
+    index = lax.axis_index(axis)
+    distance = count // 2
+    while distance >= 1:
+        upper = (index // distance) % 2 == 1
+        other = lax.ppermute(block, axis, partner_pairs(count, distance))
+        block = jnp.where(
+            upper, jnp.concatenate([other, block]), jnp.concatenate([block, other])
+        )
         distance //= 2
     return block
 
@@ -218,15 +286,14 @@
     local_mixed = jnp.einsum(
         "hqk,khd->qhd", raised, value_heads, preferred_element_type=jnp.float32
     ).reshape(query_count, model_width)
-    _, total, mixed = butterfly(
-        (local_max, local_total, local_mixed.astype(jnp.bfloat16)),
-        "phi",
-        softmax_combine,
-        ordered=True,
-    )
-    mixed = mixed.astype(jnp.float32)
+    phi_count = lax.axis_size("phi")
+    rows = query_count // phi_count
+    (_, total), mixed = scatter_softmax(
+        jnp.stack([local_max, local_total]), local_mixed, "phi"
+    )
+    own_queries = lax.dynamic_slice_in_dim(queries, owned_block("phi") * rows, rows, 0)
     context = scale_heads(mixed, 1.0 / total).astype(jnp.bfloat16)
-    mixed_queries = queries.astype(jnp.float32) + jnp.dot(
+    mixed_queries = own_queries.astype(jnp.float32) + jnp.dot(
         context, cross_out, preferred_element_type=jnp.float32
     )
     mask_hidden = jax.nn.relu(
@@ -236,8 +303,11 @@
             preferred_element_type=jnp.float32,
         )
     ).astype(jnp.bfloat16)
-    mask_embed = jnp.dot(mask_hidden, mask_second, preferred_element_type=jnp.float32).astype(
-        jnp.bfloat16
+    mask_embed = gather_blocks(
+        jnp.dot(mask_hidden, mask_second, preferred_element_type=jnp.float32).astype(
+            jnp.bfloat16
+        ),
+        "phi",
     )
     logits = lax.dot_general(
         mask_embed, group_hits, (((1,), (1,)), ((), ())), preferred_element_type=jnp.float32
@@ -249,7 +319,9 @@
         jnp.float32
     )
     intersection, predicted, truth_count = butterfly(
-        (jnp.sum(sigma * target, axis=1), jnp.sum(sigma, axis=1), jnp.sum(target, axis=1)),
+        jnp.stack(
+            [jnp.sum(sigma * target, axis=1), jnp.sum(sigma, axis=1), jnp.sum(target, axis=1)]
+        ),
         "phi",
         add_trees,
     )
@@ -257,9 +329,12 @@
     coef = loss_coefficients(
         sigma, target, matched, intersection, predicted, truth_count, hits_total, model_width
     )
-    mask_grad = narrow_butterfly(
-        jnp.dot(coef, group_hits, preferred_element_type=jnp.float32), "phi"
-    )
+    mask_grad = gather_blocks(
+        scatter_sum(jnp.dot(coef, group_hits, preferred_element_type=jnp.float32), "phi").astype(
+            jnp.bfloat16
+        ),
+        "phi",
+    ).astype(jnp.float32)
     hit_grad = reduce_scatter_rows(
         lax.dot_general(
             coef, mask_embed, (((0,), (0,)), ((), ())), preferred_element_type=jnp.float32

time: 107 us -> 113 us (1.056)
  waiting for transfers between devices: 44.8 us -> 55.4 us
  starting transfers between devices: 30.4 us -> 25.3 us
  blocking collectives: 4.35 us -> 2.64 us
    ppermute x3 -> x15, waiting for transfers between devices: 19.2 us -> 40.9 us  [the longest x6 20.1 us: gather_blocks(): other = lax.ppermute(block, axis, partner_pairs(count, distance))]
    ppermute x18 -> x3, starting transfers between devices: 21 us -> 3.58 us  [butterfly(): other = lax.ppermute(tree, axis, partner_pairs(count, distance))]
    ppermute x18 -> x3, waiting for transfers between devices: 23.8 us -> 8.47 us  [butterfly(): other = lax.ppermute(tree, axis, partner_pairs(count, distance))]
    ppermute x3 -> x15, starting transfers between devices: 3.78 us -> 16.2 us  [the longest x6 7.23 us: gather_blocks(): other = lax.ppermute(block, axis, partner_pairs(count, distance))]
    ppermute x1, waiting for transfers between devices: 1.74 us -> 4.6 us  [extended_2(): lax.ppermute(lax.slice_in_dim(block, block.shape[dim] - width, None, axis...]
    all_gather x1, blocking collectives: 4.35 us -> 2.64 us  [body(): lax.all_gather(jnp.concatenate([local_kv, encoded, digits], axis=1), 'que...]
    ppermute x1, waiting for transfers between devices: 0.01 us -> 1.45 us  [extended_2(): lax.ppermute(lax.slice_in_dim(block, 0, width, axis=dim), axis, backward)]
  transfers between devices with their start and end apart: 24 -> 21, of which waited for: 14 -> 18; matrix products, arithmetic and copies ran while one was open for 7% -> 4% of each run, Pallas kernels for 0% -> 0%
where the time goes in v5:
time: 113 us
  waiting for transfers between devices  55.4 us (49%)
  starting transfers between devices  25.3 us (22%)
  matrix products  18.4 us (16%)
  other arithmetic  6.56 us (6%)
  local copies, waits for them, and re-layouts  3.08 us (3%)
  blocking collectives  2.64 us (2%)
  between operations  1.39 us (1%)
    ppermute x6, waiting for transfers between devices, gather_blocks(): other = lax.ppermute(block, axis, partner_pairs(count, distance))  20.1 us
    ppermute x6, waiting for transfers between devices, scatter_softmax(): lax.ppermute((send_stats, send_mixed.astype(jnp.bfloat16)), axis, partner...  10.5 us
    ppermute x3, waiting for transfers between devices, scatter_sum(): lax.ppermute(send.astype(jnp.bfloat16), axis, partner_pairs(count, distan...  10.3 us
    ppermute x3, waiting for transfers between devices, butterfly(): other = lax.ppermute(tree, axis, partner_pairs(count, distance))  8.47 us
    ppermute x6, starting transfers between devices, gather_blocks(): other = lax.ppermute(block, axis, partner_pairs(count, distance))  7.23 us
    ppermute x1, starting transfers between devices, extended_2(): lax.ppermute(lax.slice_in_dim(block, 0, width, axis=dim), axis, backward)  5.47 us
    ppermute x6, starting transfers between devices, scatter_softmax(): lax.ppermute((send_stats, send_mixed.astype(jnp.bfloat16)), axis, partner...  5.28 us
    sub x1, matrix products, window_attend(): raised = jnp.exp(scores - jnp.max(scores, axis=-1, keepdims=True))  5.09 us
  transfers between devices with their start and end apart: 21, of which 18 were waited for; matrix products, arithmetic and copies ran while one was open for 4% of the time, Pallas kernels for 0%

profile of v5, /device:TPU:0, one launch (start us, length us, event | category | flops | bytes accessed | tf_op | source)
XLA Modules:
  0.0 112.8 jit_solution(2540605840841175515)
XLA Ops:
  1.9 1.3 %convolution_convert_fusion = bf16[256,768]{1,0:T(8,128)(2,1)S(1)} fusion(bf16[256,768]{1,0:T(8,128)(2,1)} %param.14, bf16[256,256]{0,1:T(8,128)(2,1)S(1)} %copy.54, f32[256]{0:T(256)S(1)} %add_rsqrt_fusion.2, f32[256]{0:T(256)S(1)} %broadcast_multiply_fusion.2), kind=kOutput, calls=%fused_computation.20 | convolution fusion | flops 101122048 | bytes 919552 | tf_op jit(solution)/shard_map/dot_general | solution.py:246
  3.2 5.5 %collective-permute-start.1 = (bf16[256,512]{1,0:T(8,128)(2,1)S(1)}, bf16[256,512]{1,0:T(8,128)(2,1)S(1)}, u32[]{:S(2)}, u32[]{:S(2)}) collective-permute-start(bf16[256,512]{1,0:T(8,128)(2,1)S(1)} %slice.179), channel_id=1, source_target_pairs={{2,0},{4,2},{6,4},{8,6},{10,8},{12,10},{14,12},{16,14},{18,16},{20... | collective-permute-start | bytes 786440 | tf_op jit(solution)/shard_map/ppermute | solution.py:19
  11.1 1.5 %collective-permute-done.1 = bf16[256,512]{1,0:T(8,128)(2,1)S(1)} collective-permute-done((bf16[256,512]{1,0:T(8,128)(2,1)S(1)}, bf16[256,512]{1,0:T(8,128)(2,1)S(1)}, u32[]{:S(2)}, u32[]{:S(2)}) %collective-permute-start.1) | collective-permute-done | bytes 262176 | tf_op jit(solution)/shard_map/ppermute | solution.py:19
  12.5 4.6 %collective-permute-done = bf16[256,512]{1,0:T(8,128)(2,1)S(1)} collective-permute-done((bf16[256,512]{1,0:T(8,128)(2,1)S(1)}, bf16[256,512]{1,0:T(8,128)(2,1)S(1)}, u32[]{:S(2)}, u32[]{:S(2)}) %collective-permute-start) | collective-permute-done | bytes 262176 | tf_op jit(solution)/shard_map/ppermute | solution.py:16
  17.6 5.1 %fusion.109 = (f32[8,256]{1,0:T(8,128)S(1)}, f32[8,256,768]{2,1,0:T(8,128)}) fusion(pred[256,768]{1,0:T(8,128)(4,1)S(1)} %fusion.28, bf16[256,8,32]{0,2,1:T(8,128)(2,1)S(1)} %bitcast.135, bf16[768,8,32]{0,2,1:T(8,128)(2,1)S(1)} %bitcast.131), kind=kOutput, calls=%fused_computation.206 | convolution fusion | flops 106955520 | bytes 7020544 | tf_op jit(solution)/shard_map/sub | solution.py:183
  22.7 4.0 %fusion.11 = bf16[8,32,256]{2,1,0:T(8,128)(2,1)S(1)} fusion(bf16[768,8,32]{0,2,1:T(8,128)(2,1)S(1)} %bitcast.132, f32[8,256,768]{2,1,0:T(8,128)} %get-tuple-element.53, f32[8,256]{1,0:T(8,128)S(1)} %get-tuple-element.52), kind=kOutput, calls=%fused_computation.27 | convolution fusion | flops 103874560 | bytes 6823936 | tf_op jit(solution)/shard_map/hqk,khd->qhd/dot_general | solution.py:185
  28.4 2.6 %all_gather.3 = bf16[512,896]{1,0:T(8,128)(2,1)S(1)} all-gather(bf16[256,896]{1,0:T(8,128)(2,1)S(1)} %fusion.36), channel_id=1, replica_groups=mesh['phi'=8,'query'=2,'event'=2] {'query'}, dimensions={0}, use_global_device_ids=true | all-gather | bytes 1376256 | tf_op jit(solution)/shard_map/all_gather | solution.py:267
  31.4 1.3 %multiply_reduce_fusion = (f32[8,512]{1,0:T(8,128)S(1)}, f32[8,512,512]{1,2,0:T(8,128)S(1)}) fusion(bf16[512,8,32]{0,2,1:T(8,128)(2,1)S(1)} %bitcast.120, bf16[512,8,32]{0,2,1:T(8,128)(2,1)S(1)} %bitcast.122), kind=kOutput, calls=%fused_computation.3 | convolution fusion | flops 138407936 | bytes 8929280 | tf_op jit(solution)/shard_map/qhd,khd->hqk/dot_general | solution.py:280
  32.7 1.4 %convert_reduce_fusion = f32[8,512]{1,0:T(8,128)S(1)} fusion(f32[8,512]{1,0:T(8,128)S(1)} %get-tuple-element.58, f32[8,512,512]{1,2,0:T(8,128)S(1)} %get-tuple-element.59), kind=kLoop, calls=%fused_computation.1 | loop fusion | flops 10481664 | bytes 8421376 | tf_op jit(solution)/shard_map/reduce_sum | solution.py:285
  34.2 1.5 %convolution_bitcast_fusion = f32[512,8,32]{0,2,1:T(8,128)S(1)} fusion(bf16[512,8,32]{0,2,1:T(8,128)(2,1)S(1)} %bitcast.121, f32[8,512,512]{1,2,0:T(8,128)S(1)} %get-tuple-element.59, f32[8,512]{1,0:T(8,128)S(1)} %get-tuple-element.58), kind=kOutput, calls=%fused_computation.21 | convolution fusion | flops 140509184 | bytes 9191424 | tf_op jit(solution)/shard_map/hqk,khd->qhd/dot_general | solution.py:286
  35.9 2.1 %collective-permute-start.3 = (bf16[256,256]{1,0:T(8,128)(2,1)S(1)}, bf16[256,256]{1,0:T(8,128)(2,1)S(1)}, u32[]{:S(2)}, u32[]{:S(2)}) collective-permute-start(bf16[256,256]{1,0:T(8,128)(2,1)S(1)} %copy.63), channel_id=1, source_target_pairs={{0,4},{4,0},{8,12},{12,8},{16,20},{20,16},{24,28},{28,24},{1,5},{5... | collective-permute-start | bytes 393224 | tf_op jit(solution)/shard_map/ppermute | solution.py:119
  38.0 1.6 %collective-permute-done.2 = f32[2,8,256]{2,1,0:T(8,128)S(1)} collective-permute-done((f32[2,8,256]{2,1,0:T(8,128)S(1)}, f32[2,8,256]{2,1,0:T(8,128)S(1)}, u32[]{:S(2)}, u32[]{:S(2)}) %collective-permute-start.2) | collective-permute-done | bytes 16416 | tf_op jit(solution)/shard_map/ppermute | solution.py:119
  40.1 3.3 %collective-permute-done.4 = f32[2,8,128]{2,1,0:T(8,128)S(1)} collective-permute-done((f32[2,8,128]{2,1,0:T(8,128)S(1)}, f32[2,8,128]{2,1,0:T(8,128)S(1)}, u32[]{:S(2)}, u32[]{:S(2)}) %collective-permute-start.4) | collective-permute-done | bytes 8224 | tf_op jit(solution)/shard_map/ppermute | solution.py:119
  43.9 4.0 %collective-permute-done.5 = bf16[128,256]{1,0:T(8,128)(2,1)S(1)} collective-permute-done((bf16[128,256]{1,0:T(8,128)(2,1)S(1)}, bf16[128,256]{1,0:T(8,128)(2,1)S(1)}, u32[]{:S(2)}, u32[]{:S(2)}) %collective-permute-start.5) | collective-permute-done | bytes 65568 | tf_op jit(solution)/shard_map/ppermute | solution.py:119
  48.0 3.0 %collective-permute-start.7 = (bf16[64,256]{1,0:T(8,128)(2,1)S(1)}, bf16[64,256]{1,0:T(8,128)(2,1)S(1)}, u32[]{:S(2)}, u32[]{:S(2)}) collective-permute-start(bf16[64,256]{1,0:T(8,128)(2,1)S(1)} %select_convert_fusion.5), channel_id=1, source_target_pairs={{0,16},{4,20},{8,24},{12,28},{16,0},{20,4},{24,8},{28,12},{1,17},{... | collective-permute-start | bytes 98312 | tf_op jit(solution)/shard_map/ppermute | solution.py:119
  51.3 1.6 %collective-permute-done.7 = bf16[64,256]{1,0:T(8,128)(2,1)S(1)} collective-permute-done((bf16[64,256]{1,0:T(8,128)(2,1)S(1)}, bf16[64,256]{1,0:T(8,128)(2,1)S(1)}, u32[]{:S(2)}, u32[]{:S(2)}) %collective-permute-start.7) | collective-permute-done | bytes 32800 | tf_op jit(solution)/shard_map/ppermute | solution.py:119
  54.4 3.0 %collective-permute-start.8 = (bf16[64,256]{1,0:T(8,128)(2,1)S(1)}, bf16[64,256]{1,0:T(8,128)(2,1)S(1)}, u32[]{:S(2)}, u32[]{:S(2)}) collective-permute-start(bf16[64,256]{1,0:T(8,128)(2,1)S(1)} %convolution_convert_fusion.3), channel_id=1, source_target_pairs={{0,16},{4,20},{8,24},{12,28},{16,0},{20,4},{24,8},{28,12},{1,17},{... | collective-permute-start | bytes 98312 | tf_op jit(solution)/shard_map/ppermute | solution.py:152
  57.4 1.9 %collective-permute-done.8 = bf16[64,256]{1,0:T(8,128)(2,1)S(1)} collective-permute-done((bf16[64,256]{1,0:T(8,128)(2,1)S(1)}, bf16[64,256]{1,0:T(8,128)(2,1)S(1)}, u32[]{:S(2)}, u32[]{:S(2)}) %collective-permute-start.8) | collective-permute-done | bytes 32800 | tf_op jit(solution)/shard_map/ppermute | solution.py:152
  59.5 4.1 %collective-permute-done.9 = bf16[128,256]{1,0:T(8,128)(2,1)S(1)} collective-permute-done((bf16[128,256]{1,0:T(8,128)(2,1)S(1)}, bf16[128,256]{1,0:T(8,128)(2,1)S(1)}, u32[]{:S(2)}, u32[]{:S(2)}) %collective-permute-start.9) | collective-permute-done | bytes 65568 | tf_op jit(solution)/shard_map/ppermute | solution.py:152
  64.3 4.4 %collective-permute-done.10 = bf16[256,256]{1,0:T(8,128)(2,1)S(1)} collective-permute-done((bf16[256,256]{1,0:T(8,128)(2,1)S(1)}, bf16[256,256]{1,0:T(8,128)(2,1)S(1)}, u32[]{:S(2)}, u32[]{:S(2)}) %collective-permute-start.10) | collective-permute-done | bytes 131104 | tf_op jit(solution)/shard_map/ppermute | solution.py:152
  69.9 3.3 %collective-permute-done.11 = f32[3,512]{1,0:T(4,128)S(1)} collective-permute-done((f32[3,512]{1,0:T(4,128)S(1)}, f32[3,512]{1,0:T(4,128)S(1)}, u32[]{:S(2)}, u32[]{:S(2)}) %collective-permute-start.11) | collective-permute-done | bytes 6176 | tf_op jit(solution)/shard_map/ppermute | solution.py:34
  73.5 3.5 %collective-permute-done.12 = f32[3,512]{1,0:T(4,128)S(1)} collective-permute-done((f32[3,512]{1,0:T(4,128)S(1)}, f32[3,512]{1,0:T(4,128)S(1)}, u32[]{:S(2)}, u32[]{:S(2)}) %collective-permute-start.12) | collective-permute-done | bytes 6176 | tf_op jit(solution)/shard_map/ppermute | solution.py:34
  77.0 3.0 %collective-permute-start.13 = (f32[3,512]{1,0:T(4,128)S(1)}, f32[3,512]{1,0:T(4,128)S(1)}, u32[]{:S(2)}, u32[]{:S(2)}) collective-permute-start(f32[3,512]{1,0:T(4,128)S(1)} %fusion.136), channel_id=1, source_target_pairs={{0,16},{4,20},{8,24},{12,28},{16,0},{20,4},{24,8},{28,12},{1,17},{... | collective-permute-start | bytes 18440 | tf_op jit(solution)/shard_map/ppermute | solution.py:34
  80.0 1.6 %collective-permute-done.13 = f32[3,512]{1,0:T(4,128)S(1)} collective-permute-done((f32[3,512]{1,0:T(4,128)S(1)}, f32[3,512]{1,0:T(4,128)S(1)}, u32[]{:S(2)}, u32[]{:S(2)}) %collective-permute-start.13) | collective-permute-done | bytes 6176 | tf_op jit(solution)/shard_map/ppermute | solution.py:34
  83.6 4.6 %collective-permute-done.15 = bf16[256,256]{1,0:T(8,128)(2,1)S(1)} collective-permute-done((bf16[256,256]{1,0:T(8,128)(2,1)S(1)}, bf16[256,256]{1,0:T(8,128)(2,1)S(1)}, u32[]{:S(2)}, u32[]{:S(2)}) %collective-permute-start.15) | collective-permute-done | bytes 131104 | tf_op jit(solution)/shard_map/ppermute | solution.py:140
  88.6 4.0 %collective-permute-done.16 = bf16[128,256]{1,0:T(8,128)(2,1)S(1)} collective-permute-done((bf16[128,256]{1,0:T(8,128)(2,1)S(1)}, bf16[128,256]{1,0:T(8,128)(2,1)S(1)}, u32[]{:S(2)}, u32[]{:S(2)}) %collective-permute-start.16) | collective-permute-done | bytes 65568 | tf_op jit(solution)/shard_map/ppermute | solution.py:140
  92.7 3.0 %collective-permute-start.17 = (bf16[64,256]{1,0:T(8,128)(2,1)S(1)}, bf16[64,256]{1,0:T(8,128)(2,1)S(1)}, u32[]{:S(2)}, u32[]{:S(2)}) collective-permute-start(bf16[64,256]{1,0:T(8,128)(2,1)S(1)} %select_convert_fusion.4), channel_id=1, source_target_pairs={{0,16},{4,20},{8,24},{12,28},{16,0},{20,4},{24,8},{28,12},{1,17},{... | collective-permute-start | bytes 98312 | tf_op jit(solution)/shard_map/ppermute | solution.py:140
  96.0 1.6 %collective-permute-done.17 = bf16[64,256]{1,0:T(8,128)(2,1)S(1)} collective-permute-done((bf16[64,256]{1,0:T(8,128)(2,1)S(1)}, bf16[64,256]{1,0:T(8,128)(2,1)S(1)}, u32[]{:S(2)}, u32[]{:S(2)}) %collective-permute-start.17) | collective-permute-done | bytes 32800 | tf_op jit(solution)/shard_map/ppermute | solution.py:140
  97.6 3.0 %collective-permute-start.18 = (bf16[64,256]{1,0:T(8,128)(2,1)S(1)}, bf16[64,256]{1,0:T(8,128)(2,1)S(1)}, u32[]{:S(2)}, u32[]{:S(2)}) collective-permute-start(bf16[64,256]{1,0:T(8,128)(2,1)S(1)} %add_convert_fusion), channel_id=1, source_target_pairs={{0,16},{4,20},{8,24},{12,28},{16,0},{20,4},{24,8},{28,12},{1,17},{... | collective-permute-start | bytes 98312 | tf_op jit(solution)/shard_map/ppermute | solution.py:152
  100.7 1.8 %collective-permute-done.18 = bf16[64,256]{1,0:T(8,128)(2,1)S(1)} collective-permute-done((bf16[64,256]{1,0:T(8,128)(2,1)S(1)}, bf16[64,256]{1,0:T(8,128)(2,1)S(1)}, u32[]{:S(2)}, u32[]{:S(2)}) %collective-permute-start.18) | collective-permute-done | bytes 32800 | tf_op jit(solution)/shard_map/ppermute | solution.py:152
  102.8 4.1 %collective-permute-done.19 = bf16[128,256]{1,0:T(8,128)(2,1)S(1)} collective-permute-done((bf16[128,256]{1,0:T(8,128)(2,1)S(1)}, bf16[128,256]{1,0:T(8,128)(2,1)S(1)}, u32[]{:S(2)}, u32[]{:S(2)}) %collective-permute-start.19) | collective-permute-done | bytes 65568 | tf_op jit(solution)/shard_map/ppermute | solution.py:152
  108.0 3.9 %collective-permute-done.20 = bf16[256,256]{1,0:T(8,128)(2,1)S(1)} collective-permute-done((bf16[256,256]{1,0:T(8,128)(2,1)S(1)}, bf16[256,256]{1,0:T(8,128)(2,1)S(1)}, u32[]{:S(2)}, u32[]{:S(2)}) %collective-permute-start.20) | collective-permute-done | bytes 131104 | tf_op jit(solution)/shard_map/ppermute | solution.py:152
  (130 shorter events, 16.3 us)
Async XLA Ops:
  0.6 26.5 %copy-start = (bf16[1024,256]{1,0:T(8,128)(2,1)S(1)}, bf16[1024,256]{1,0:T(8,128)(2,1)}, u32[]{:S(2)}) copy-start(bf16[1024,256]{1,0:T(8,128)(2,1)} %param.17) | copy-start | bytes 1572868
  3.2 9.4 %collective-permute-start.1 = (bf16[256,512]{1,0:T(8,128)(2,1)S(1)}, bf16[256,512]{1,0:T(8,128)(2,1)S(1)}, u32[]{:S(2)}, u32[]{:S(2)}) collective-permute-start(bf16[256,512]{1,0:T(8,128)(2,1)S(1)} %slice.179), channel_id=1, source_target_pairs={{2,0},{4,2},{6,4},{8,6},{10,8},{12,10},{14,12},{16,14},{18,16},{20... | collective-permute-start | bytes 786440 | tf_op jit(solution)/shard_map/ppermute | solution.py:19
  8.7 8.5 %collective-permute-start = (bf16[256,512]{1,0:T(8,128)(2,1)S(1)}, bf16[256,512]{1,0:T(8,128)(2,1)S(1)}, u32[]{:S(2)}, u32[]{:S(2)}) collective-permute-start(bf16[256,512]{1,0:T(8,128)(2,1)S(1)} %slice.179), channel_id=1, source_target_pairs={{0,2},{2,4},{4,6},{6,8},{8,10},{10,12},{12,14},{14,16},{16,18},{18... | collective-permute-start | bytes 786440 | tf_op jit(solution)/shard_map/ppermute | solution.py:16
  22.7 4.0 %copy-start.4 = (bf16[256,256]{1,0:T(8,128)(2,1)S(1)}, bf16[256,256]{1,0:T(8,128)(2,1)}, u32[]{:S(2)}) copy-start(bf16[256,256]{1,0:T(8,128)(2,1)} %param.15) | copy-start | bytes 393220
  22.7 4.4 %copy-start.9 = (bf16[256,1024]{1,0:T(8,128)(2,1)S(1)}, bf16[256,1024]{1,0:T(8,128)(2,1)}, u32[]{:S(2)}) copy-start(bf16[256,1024]{1,0:T(8,128)(2,1)} %param.16) | copy-start | bytes 1572868
  22.7 5.4 %copy-start.3 = (bf16[256,512]{1,0:T(8,128)(2,1)S(1)}, bf16[256,512]{1,0:T(8,128)(2,1)}, u32[]{:S(2)}) copy-start(bf16[256,512]{1,0:T(8,128)(2,1)} %param.20) | copy-start | bytes 786436
  28.0 4.7 %copy-start.2 = (bf16[256,256]{1,0:T(8,128)(2,1)}, bf16[256,256]{1,0:T(8,128)(2,1)S(1)}, u32[]{:S(2)}) copy-start(bf16[256,256]{1,0:T(8,128)(2,1)S(1)} %copy.71) | copy-start | bytes 393220
  34.1 18.7 %copy-start.5 = (bf16[256,256]{1,0:T(8,128)(2,1)S(1)}, bf16[256,256]{1,0:T(8,128)(2,1)}, u32[]{:S(2)}) copy-start(bf16[256,256]{1,0:T(8,128)(2,1)} %param.21) | copy-start | bytes 393220
  34.1 19.9 %copy-start.6 = (bf16[256,256]{1,0:T(8,128)(2,1)S(1)}, bf16[256,256]{1,0:T(8,128)(2,1)}, u32[]{:S(2)}) copy-start(bf16[256,256]{1,0:T(8,128)(2,1)} %param.23) | copy-start | bytes 393220
  34.1 19.9 %copy-start.7 = (bf16[256,256]{1,0:T(8,128)(2,1)S(1)}, bf16[256,256]{1,0:T(8,128)(2,1)}, u32[]{:S(2)}) copy-start(bf16[256,256]{1,0:T(8,128)(2,1)} %param.22) | copy-start | bytes 393220
  34.1 25.4 %copy-start.8 = (s32[512]{0:T(512)S(1)}, s32[512]{0:T(512)}, u32[]{:S(2)}) copy-start(s32[512]{0:T(512)} %param.25) | copy-start | bytes 6148
  35.7 3.9 %collective-permute-start.2 = (f32[2,8,256]{2,1,0:T(8,128)S(1)}, f32[2,8,256]{2,1,0:T(8,128)S(1)}, u32[]{:S(2)}, u32[]{:S(2)}) collective-permute-start(f32[2,8,256]{2,1,0:T(8,128)S(1)} %get-tuple-element.38), channel_id=1, source_target_pairs={{0,4},{4,0},{8,12},{12,8},{16,20},{20,16},{24,28},{28,24},{1,5},{5... | collective-permute-start | bytes 49160 | tf_op jit(solution)/shard_map/ppermute | solution.py:119
  35.9 7.6 %collective-permute-start.3 = (bf16[256,256]{1,0:T(8,128)(2,1)S(1)}, bf16[256,256]{1,0:T(8,128)(2,1)S(1)}, u32[]{:S(2)}, u32[]{:S(2)}) collective-permute-start(bf16[256,256]{1,0:T(8,128)(2,1)S(1)} %copy.63), channel_id=1, source_target_pairs={{0,4},{4,0},{8,12},{12,8},{16,20},{20,16},{24,28},{28,24},{1,5},{5... | collective-permute-start | bytes 393224 | tf_op jit(solution)/shard_map/ppermute | solution.py:119
  39.7 3.7 %collective-permute-start.4 = (f32[2,8,128]{2,1,0:T(8,128)S(1)}, f32[2,8,128]{2,1,0:T(8,128)S(1)}, u32[]{:S(2)}, u32[]{:S(2)}) collective-permute-start(f32[2,8,128]{2,1,0:T(8,128)S(1)} %get-tuple-element.45), channel_id=1, source_target_pairs={{0,8},{4,12},{8,0},{12,4},{16,24},{20,28},{24,16},{28,20},{1,9},{5... | collective-permute-start | bytes 24584 | tf_op jit(solution)/shard_map/ppermute | solution.py:119
  43.5 7.5 %collective-permute-start.6 = (f32[2,8,64]{2,1,0:T(8,128)S(1)}, f32[2,8,64]{2,1,0:T(8,128)S(1)}, u32[]{:S(2)}, u32[]{:S(2)}) collective-permute-start(f32[2,8,64]{2,1,0:T(8,128)S(1)} %get-tuple-element.49), channel_id=1, source_target_pairs={{0,16},{4,20},{8,24},{12,28},{16,0},{20,4},{24,8},{28,12},{1,17},{... | collective-permute-start | bytes 12296 | tf_op jit(solution)/shard_map/ppermute | solution.py:119
  43.6 4.3 %collective-permute-start.5 = (bf16[128,256]{1,0:T(8,128)(2,1)S(1)}, bf16[128,256]{1,0:T(8,128)(2,1)S(1)}, u32[]{:S(2)}, u32[]{:S(2)}) collective-permute-start(bf16[128,256]{1,0:T(8,128)(2,1)S(1)} %select_convert_fusion.3), channel_id=1, source_target_pairs={{0,8},{4,12},{8,0},{12,4},{16,24},{20,28},{24,16},{28,20},{1,9},{5... | collective-permute-start | bytes 196616 | tf_op jit(solution)/shard_map/ppermute | solution.py:119
  48.0 4.9 %collective-permute-start.7 = (bf16[64,256]{1,0:T(8,128)(2,1)S(1)}, bf16[64,256]{1,0:T(8,128)(2,1)S(1)}, u32[]{:S(2)}, u32[]{:S(2)}) collective-permute-start(bf16[64,256]{1,0:T(8,128)(2,1)S(1)} %select_convert_fusion.5), channel_id=1, source_target_pairs={{0,16},{4,20},{8,24},{12,28},{16,0},{20,4},{24,8},{28,12},{1,17},{... | collective-permute-start | bytes 98312 | tf_op jit(solution)/shard_map/ppermute | solution.py:119
  54.4 4.9 %collective-permute-start.8 = (bf16[64,256]{1,0:T(8,128)(2,1)S(1)}, bf16[64,256]{1,0:T(8,128)(2,1)S(1)}, u32[]{:S(2)}, u32[]{:S(2)}) collective-permute-start(bf16[64,256]{1,0:T(8,128)(2,1)S(1)} %convolution_convert_fusion.3), channel_id=1, source_target_pairs={{0,16},{4,20},{8,24},{12,28},{16,0},{20,4},{24,8},{28,12},{1,17},{... | collective-permute-start | bytes 98312 | tf_op jit(solution)/shard_map/ppermute | solution.py:152
  59.3 4.3 %collective-permute-start.9 = (bf16[128,256]{1,0:T(8,128)(2,1)S(1)}, bf16[128,256]{1,0:T(8,128)(2,1)S(1)}, u32[]{:S(2)}, u32[]{:S(2)}) collective-permute-start(bf16[128,256]{1,0:T(8,128)(2,1)S(1)} %maximum_select_fusion.4), channel_id=1, source_target_pairs={{0,8},{4,12},{8,0},{12,4},{16,24},{20,28},{24,16},{28,20},{1,9},{5... | collective-permute-start | bytes 196616 | tf_op jit(solution)/shard_map/ppermute | solution.py:152
  63.7 5.0 %collective-permute-start.10 = (bf16[256,256]{1,0:T(8,128)(2,1)S(1)}, bf16[256,256]{1,0:T(8,128)(2,1)S(1)}, u32[]{:S(2)}, u32[]{:S(2)}) collective-permute-start(bf16[256,256]{1,0:T(8,128)(2,1)S(1)} %maximum_select_fusion.2), channel_id=1, source_target_pairs={{0,4},{4,0},{8,12},{12,8},{16,20},{20,16},{24,28},{28,24},{1,5},{5... | collective-permute-start | bytes 393224 | tf_op jit(solution)/shard_map/ppermute | solution.py:152
  68.8 27.1 %copy-start.1 = (bf16[512,256]{1,0:T(8,128)(2,1)}, bf16[512,256]{1,0:T(8,128)(2,1)S(1)}, u32[]{:S(2)}) copy-start(bf16[512,256]{1,0:T(8,128)(2,1)S(1)} %maximum_select_fusion) | copy-start | bytes 786436
  69.5 3.7 %collective-permute-start.11 = (f32[3,512]{1,0:T(4,128)S(1)}, f32[3,512]{1,0:T(4,128)S(1)}, u32[]{:S(2)}, u32[]{:S(2)}) collective-permute-start(f32[3,512]{1,0:T(4,128)S(1)} %pad_maximum_fusion.4), channel_id=1, source_target_pairs={{0,4},{4,0},{8,12},{12,8},{16,20},{20,16},{24,28},{28,24},{1,5},{5... | collective-permute-start | bytes 18440 | tf_op jit(solution)/shard_map/ppermute | solution.py:34
  73.3 3.7 %collective-permute-start.12 = (f32[3,512]{1,0:T(4,128)S(1)}, f32[3,512]{1,0:T(4,128)S(1)}, u32[]{:S(2)}, u32[]{:S(2)}) collective-permute-start(f32[3,512]{1,0:T(4,128)S(1)} %fusion.104), channel_id=1, source_target_pairs={{0,8},{4,12},{8,0},{12,4},{16,24},{20,28},{24,16},{28,20},{1,9},{5... | collective-permute-start | bytes 18440 | tf_op jit(solution)/shard_map/ppermute | solution.py:34
  77.0 4.6 %collective-permute-start.13 = (f32[3,512]{1,0:T(4,128)S(1)}, f32[3,512]{1,0:T(4,128)S(1)}, u32[]{:S(2)}, u32[]{:S(2)}) collective-permute-start(f32[3,512]{1,0:T(4,128)S(1)} %fusion.136), channel_id=1, source_target_pairs={{0,16},{4,20},{8,24},{12,28},{16,0},{20,4},{24,8},{28,12},{1,17},{... | collective-permute-start | bytes 18440 | tf_op jit(solution)/shard_map/ppermute | solution.py:34
  83.2 5.0 %collective-permute-start.15 = (bf16[256,256]{1,0:T(8,128)(2,1)S(1)}, bf16[256,256]{1,0:T(8,128)(2,1)S(1)}, u32[]{:S(2)}, u32[]{:S(2)}) collective-permute-start(bf16[256,256]{1,0:T(8,128)(2,1)S(1)} %select_convert_fusion), channel_id=1, source_target_pairs={{0,4},{4,0},{8,12},{12,8},{16,20},{20,16},{24,28},{28,24},{1,5},{5... | collective-permute-start | bytes 393224 | tf_op jit(solution)/shard_map/ppermute | solution.py:140
  88.3 4.3 %collective-permute-start.16 = (bf16[128,256]{1,0:T(8,128)(2,1)S(1)}, bf16[128,256]{1,0:T(8,128)(2,1)S(1)}, u32[]{:S(2)}, u32[]{:S(2)}) collective-permute-start(bf16[128,256]{1,0:T(8,128)(2,1)S(1)} %select_convert_fusion.2), channel_id=1, source_target_pairs={{0,8},{4,12},{8,0},{12,4},{16,24},{20,28},{24,16},{28,20},{1,9},{5... | collective-permute-start | bytes 196616 | tf_op jit(solution)/shard_map/ppermute | solution.py:140
  92.7 4.9 %collective-permute-start.17 = (bf16[64,256]{1,0:T(8,128)(2,1)S(1)}, bf16[64,256]{1,0:T(8,128)(2,1)S(1)}, u32[]{:S(2)}, u32[]{:S(2)}) collective-permute-start(bf16[64,256]{1,0:T(8,128)(2,1)S(1)} %select_convert_fusion.4), channel_id=1, source_target_pairs={{0,16},{4,20},{8,24},{12,28},{16,0},{20,4},{24,8},{28,12},{1,17},{... | collective-permute-start | bytes 98312 | tf_op jit(solution)/shard_map/ppermute | solution.py:140
  97.6 4.9 %collective-permute-start.18 = (bf16[64,256]{1,0:T(8,128)(2,1)S(1)}, bf16[64,256]{1,0:T(8,128)(2,1)S(1)}, u32[]{:S(2)}, u32[]{:S(2)}) collective-permute-start(bf16[64,256]{1,0:T(8,128)(2,1)S(1)} %add_convert_fusion), channel_id=1, source_target_pairs={{0,16},{4,20},{8,24},{12,28},{16,0},{20,4},{24,8},{28,12},{1,17},{... | collective-permute-start | bytes 98312 | tf_op jit(solution)/shard_map/ppermute | solution.py:152
  100.6 6.6 %collective-permute-start.14 = (f32[256,256]{1,0:T(8,128)S(1)}, f32[256,256]{1,0:T(8,128)S(1)}, u32[]{:S(2)}, u32[]{:S(2)}) collective-permute-start(f32[256,256]{1,0:T(8,128)S(1)} %slice_select_fusion), channel_id=1, source_target_pairs={{0,2},{2,0},{1,3},{3,1},{4,6},{6,4},{5,7},{7,5},{8,10},{10,8},{9,1... | collective-permute-start | bytes 786440 | tf_op jit(solution)/shard_map/ppermute | solution.py:87
  102.5 4.3 %collective-permute-start.19 = (bf16[128,256]{1,0:T(8,128)(2,1)S(1)}, bf16[128,256]{1,0:T(8,128)(2,1)S(1)}, u32[]{:S(2)}, u32[]{:S(2)}) collective-permute-start(bf16[128,256]{1,0:T(8,128)(2,1)S(1)} %maximum_select_fusion.5), channel_id=1, source_target_pairs={{0,8},{4,12},{8,0},{12,4},{16,24},{20,28},{24,16},{28,20},{1,9},{5... | collective-permute-start | bytes 196616 | tf_op jit(solution)/shard_map/ppermute | solution.py:152
  106.9 5.0 %collective-permute-start.20 = (bf16[256,256]{1,0:T(8,128)(2,1)S(1)}, bf16[256,256]{1,0:T(8,128)(2,1)S(1)}, u32[]{:S(2)}, u32[]{:S(2)}) collective-permute-start(bf16[256,256]{1,0:T(8,128)(2,1)S(1)} %maximum_select_fusion.3), channel_id=1, source_target_pairs={{0,4},{4,0},{8,12},{12,8},{16,20},{20,16},{24,28},{28,24},{1,5},{5... | collective-permute-start | bytes 393224 | tf_op jit(solution)/shard_map/ppermute | solution.py:152

commit v6 on v2

--- a/solution.py
+++ b/solution.py
@@ -152,6 +152,82 @@
     return (matched[:, None] * (sigma - target + dice_part) * model_width ** (-0.5)).astype(
         jnp.bfloat16
     )
+
+
+def query_chain(
+    query_proj,
+    queries,
+    match,
+    group_kv,
+    group_hits,
+    group_truth,
+    cross_out,
+    mask_first,
+    mask_second,
+    track_count,
+    hits_total,
+):
+    query_count, model_width = queries.shape
+    head_size = model_width // HEADS
+    group_count = group_kv.shape[0]
+    query_heads = query_proj.reshape(query_count, HEADS, head_size)
+    key_heads = group_kv[:, :model_width].reshape(group_count, HEADS, head_size)
+    value_heads = group_kv[:, model_width:].reshape(group_count, HEADS, head_size)
+    scores = jnp.einsum(
+        "qhd,khd->hqk", query_heads, key_heads, preferred_element_type=jnp.float32
+    ) * head_size ** (-0.5)
+    local_max = jnp.max(scores, axis=-1)
+    raised = jnp.exp(scores - local_max[..., None]).astype(jnp.bfloat16)
+    local_total = jnp.sum(raised.astype(jnp.float32), axis=-1)
+    local_mixed = jnp.einsum(
+        "hqk,khd->qhd", raised, value_heads, preferred_element_type=jnp.float32
+    ).reshape(query_count, model_width)
+    _, total, mixed = butterfly(
+        (local_max, local_total, local_mixed.astype(jnp.bfloat16)),
+        "phi",
+        softmax_combine,
+        ordered=True,
+    )
+    mixed = mixed.astype(jnp.float32)
+    context = scale_heads(mixed, 1.0 / total).astype(jnp.bfloat16)
+    mixed_queries = queries.astype(jnp.float32) + jnp.dot(
+        context, cross_out, preferred_element_type=jnp.float32
+    )
+    mask_hidden = jax.nn.relu(
+        jnp.dot(
+            norm_rows(mixed_queries).astype(jnp.bfloat16),
+            mask_first,
+            preferred_element_type=jnp.float32,
+        )
+    ).astype(jnp.bfloat16)
+    mask_embed = jnp.dot(mask_hidden, mask_second, preferred_element_type=jnp.float32).astype(
+        jnp.bfloat16
+    )
+    logits = lax.dot_general(
+        mask_embed, group_hits, (((1,), (1,)), ((), ())), preferred_element_type=jnp.float32
+    ) * model_width ** (-0.5)
+    sigma = jax.nn.sigmoid(logits)
+    matched_flag = match < track_count
+    matched = matched_flag.astype(jnp.float32)
+    target = jnp.logical_and(match[:, None] == group_truth[None, :], matched_flag[:, None]).astype(
+        jnp.float32
+    )
+    intersection, predicted, truth_count = butterfly(
+        (jnp.sum(sigma * target, axis=1), jnp.sum(sigma, axis=1), jnp.sum(target, axis=1)),
+        "phi",
+        add_trees,
+    )
+    mask_fill = predicted / hits_total
+    coef = loss_coefficients(
+        sigma, target, matched, intersection, predicted, truth_count, hits_total, model_width
+    )
+    mask_grad = narrow_butterfly(
+        jnp.dot(coef, group_hits, preferred_element_type=jnp.float32), "phi"
+    )
+    hit_partial = lax.dot_general(
+        coef, mask_embed, (((0,), (0,)), ((), ())), preferred_element_type=jnp.float32
+    )
+    return mask_embed, mask_grad, mask_fill, hit_partial
 
 
 def body(
@@ -204,68 +280,31 @@
     group_digits = gathered[:, 3 * model_width :].astype(jnp.int32)
     group_truth = group_digits[:, 0] * 256 + group_digits[:, 1] - 1
     query_proj = jnp.dot(queries, cross_q, preferred_element_type=jnp.float32).astype(jnp.bfloat16)
-    head_size = model_width // HEADS
-    group_count = group_kv.shape[0]
-    query_heads = query_proj.reshape(query_count, HEADS, head_size)
-    key_heads = group_kv[:, :model_width].reshape(group_count, HEADS, head_size)
-    value_heads = group_kv[:, model_width:].reshape(group_count, HEADS, head_size)
-    scores = jnp.einsum(
-        "qhd,khd->hqk", query_heads, key_heads, preferred_element_type=jnp.float32
-    ) * head_size ** (-0.5)
-    local_max = jnp.max(scores, axis=-1)
-    raised = jnp.exp(scores - local_max[..., None]).astype(jnp.bfloat16)
-    local_total = jnp.sum(raised.astype(jnp.float32), axis=-1)
-    local_mixed = jnp.einsum(
-        "hqk,khd->qhd", raised, value_heads, preferred_element_type=jnp.float32
-    ).reshape(query_count, model_width)
-    _, total, mixed = butterfly(
-        (local_max, local_total, local_mixed.astype(jnp.bfloat16)),
-        "phi",
-        softmax_combine,
-        ordered=True,
-    )
-    mixed = mixed.astype(jnp.float32)
-    context = scale_heads(mixed, 1.0 / total).astype(jnp.bfloat16)
-    mixed_queries = queries.astype(jnp.float32) + jnp.dot(
-        context, cross_out, preferred_element_type=jnp.float32
-    )
-    mask_hidden = jax.nn.relu(
-        jnp.dot(
-            norm_rows(mixed_queries).astype(jnp.bfloat16),
+    chunks = 2
+    rows = query_count // chunks
+    outputs = [
+        query_chain(
+            query_proj[c * rows : (c + 1) * rows],
+            queries[c * rows : (c + 1) * rows],
+            match[c * rows : (c + 1) * rows],
+            group_kv,
+            group_hits,
+            group_truth,
+            cross_out,
             mask_first,
-            preferred_element_type=jnp.float32,
+            mask_second,
+            track_count,
+            hits_total,
         )
-    ).astype(jnp.bfloat16)
-    mask_embed = jnp.dot(mask_hidden, mask_second, preferred_element_type=jnp.float32).astype(
-        jnp.bfloat16
-    )
-    logits = lax.dot_general(
-        mask_embed, group_hits, (((1,), (1,)), ((), ())), preferred_element_type=jnp.float32
-    ) * model_width ** (-0.5)
-    sigma = jax.nn.sigmoid(logits)
-    matched_flag = match < track_count
-    matched = matched_flag.astype(jnp.float32)
-    target = jnp.logical_and(match[:, None] == group_truth[None, :], matched_flag[:, None]).astype(
-        jnp.float32
-    )
-    intersection, predicted, truth_count = butterfly(
-        (jnp.sum(sigma * target, axis=1), jnp.sum(sigma, axis=1), jnp.sum(target, axis=1)),
-        "phi",
-        add_trees,
-    )
-    mask_fill = predicted / hits_total
-    coef = loss_coefficients(
-        sigma, target, matched, intersection, predicted, truth_count, hits_total, model_width
-    )
-    mask_grad = narrow_butterfly(
-        jnp.dot(coef, group_hits, preferred_element_type=jnp.float32), "phi"
-    )
-    hit_grad = reduce_scatter_rows(
-        lax.dot_general(
-            coef, mask_embed, (((0,), (0,)), ((), ())), preferred_element_type=jnp.float32
-        ),
-        "query",
-    )
+        for c in range(chunks)
+    ]
+    mask_embed = jnp.concatenate([o[0] for o in outputs])
+    mask_grad = jnp.concatenate([o[1] for o in outputs])
+    mask_fill = jnp.concatenate([o[2] for o in outputs])
+    hit_partial = outputs[0][3]
+    for o in outputs[1:]:
+        hit_partial = hit_partial + o[3]
+    hit_grad = reduce_scatter_rows(hit_partial, "query")
     return (encoded, mask_embed, hit_grad, mask_grad, mask_fill)
 
 

time: 107 us -> 132 us (1.23)
  starting transfers between devices: 30.4 us -> 59.3 us
  waiting for transfers between devices: 44.8 us -> 30.6 us
  matrix products: 17.8 us -> 22 us
  local copies, waits for them, and re-layouts: 2.38 us -> 6.05 us
  other arithmetic: 6.39 us -> 9.37 us
  blocking collectives: 4.35 us -> 2.64 us
    ppermute x18 -> x36, starting transfers between devices: 21 us -> 42.3 us  [butterfly(): other = lax.ppermute(tree, axis, partner_pairs(count, distance))]
    ppermute x18 -> x36, waiting for transfers between devices: 23.8 us -> 15.2 us  [butterfly(): other = lax.ppermute(tree, axis, partner_pairs(count, distance))]
    ppermute x3 -> x6, starting transfers between devices: 3.78 us -> 11.5 us  [narrow_butterfly(): other = lax.ppermute(sent, axis, partner_pairs(count, distance))]
    ppermute x3 -> x6, waiting for transfers between devices: 19.2 us -> 12.1 us  [narrow_butterfly(): other = lax.ppermute(sent, axis, partner_pairs(count, distance))]
    dot_general x7 -> x14, matrix products: 4.84 us -> 8.99 us  [the longest x2 4.07 us: query_chain(): jnp.einsum('hqk,khd->qhd', raised, value_heads, preferred_element_type=jn...]
    concatenate x0 -> x3, other arithmetic: none -> 2.13 us  [the longest x1 0.83 us: body(): mask_grad = jnp.concatenate([o[1] for o in outputs])]
    unnamed x25 -> x22, local copies, waits for them, and re-layouts: 1.38 us -> 3.29 us
    slice x3 -> x6, local copies, waits for them, and re-layouts: 0.32 us -> 2.08 us  [the longest x1 0.98 us: body(): queries[c * rows:(c + 1) * rows]]
  transfers between devices with their start and end apart: 24 -> 45, of which waited for: 14 -> 16; matrix products, arithmetic and copies ran while one was open for 7% -> 12% of each run, Pallas kernels for 0% -> 0%
where the time goes in v6:
time: 132 us; the launch traced here: 131 us
  starting transfers between devices  59.3 us (45%)
  waiting for transfers between devices  30.6 us (23%)
  matrix products  22 us (17%)
  other arithmetic  9.37 us (7%)
  local copies, waits for them, and re-layouts  6.05 us (5%)
  blocking collectives  2.64 us (2%)
  between operations  1.32 us (1%)
    ppermute x36, starting transfers between devices, butterfly(): other = lax.ppermute(tree, axis, partner_pairs(count, distance))  42.3 us
    ppermute x36, waiting for transfers between devices, butterfly(): other = lax.ppermute(tree, axis, partner_pairs(count, distance))  15.2 us
    ppermute x6, waiting for transfers between devices, narrow_butterfly(): other = lax.ppermute(sent, axis, partner_pairs(count, distance))  12.1 us
    ppermute x6, starting transfers between devices, narrow_butterfly(): other = lax.ppermute(sent, axis, partner_pairs(count, distance))  11.5 us
    ppermute x1, starting transfers between devices, extended_2(): lax.ppermute(lax.slice_in_dim(block, 0, width, axis=dim), axis, backward)  5.47 us
    sub x1, matrix products, window_attend(): raised = jnp.exp(scores - jnp.max(scores, axis=-1, keepdims=True))  5.12 us
    dot_general x2, matrix products, query_chain(): jnp.einsum('hqk,khd->qhd', raised, value_heads, preferred_element_type=jn...  4.07 us
    dot_general x1, matrix products, window_attend(): jnp.einsum('hqk,khd->qhd', weights, value_heads, preferred_element_type=j...  3.97 us
  transfers between devices with their start and end apart: 45, of which 16 were waited for; matrix products, arithmetic and copies ran while one was open for 12% of the time, Pallas kernels for 0%

profile of v6, /device:TPU:0, one launch (start us, length us, event | category | flops | bytes accessed | tf_op | source)
XLA Modules:
  0.0 131.3 jit_solution(3633302719008537163)
XLA Ops:
  3.2 5.5 %collective-permute-start.1 = (bf16[256,512]{1,0:T(8,128)(2,1)S(1)}, bf16[256,512]{1,0:T(8,128)(2,1)S(1)}, u32[]{:S(2)}, u32[]{:S(2)}) collective-permute-start(bf16[256,512]{1,0:T(8,128)(2,1)S(1)} %slice.77), channel_id=1, source_target_pairs={{2,0},{4,2},{6,4},{8,6},{10,8},{12,10},{14,12},{16,14},{18,16},{20... | collective-permute-start | bytes 786440 | tf_op jit(solution)/shard_map/ppermute | solution.py:19
  13.9 3.3 %collective-permute-done = bf16[256,512]{1,0:T(8,128)(2,1)S(1)} collective-permute-done((bf16[256,512]{1,0:T(8,128)(2,1)S(1)}, bf16[256,512]{1,0:T(8,128)(2,1)S(1)}, u32[]{:S(2)}, u32[]{:S(2)}) %collective-permute-start) | collective-permute-done | bytes 262176 | tf_op jit(solution)/shard_map/ppermute | solution.py:16
  17.6 5.1 %fusion.138 = (f32[8,256]{1,0:T(8,128)S(1)}, f32[8,256,768]{2,1,0:T(8,128)}) fusion(pred[256,768]{1,0:T(8,128)(4,1)S(1)} %fusion.29, bf16[256,8,32]{0,2,1:T(8,128)(2,1)S(1)} %bitcast.168, bf16[768,8,32]{0,2,1:T(8,128)(2,1)S(1)} %bitcast.166), kind=kOutput, calls=%fused_computation.259 | convolution fusion | flops 106955520 | bytes 7020544 | tf_op jit(solution)/shard_map/sub | solution.py:115
  22.8 4.0 %fusion.17 = bf16[8,32,256]{2,1,0:T(8,128)(2,1)S(1)} fusion(bf16[768,8,32]{0,2,1:T(8,128)(2,1)S(1)} %bitcast.165, f32[8,256,768]{2,1,0:T(8,128)} %get-tuple-element.82, f32[8,256]{1,0:T(8,128)S(1)} %get-tuple-element.81), kind=kOutput, calls=%fused_computation.45 | convolution fusion | flops 103874560 | bytes 6823936 | tf_op jit(solution)/shard_map/hqk,khd->qhd/dot_general | solution.py:117
  28.5 2.6 %all_gather.3 = bf16[512,896]{1,0:T(8,128)(2,1)S(1)} all-gather(bf16[256,896]{1,0:T(8,128)(2,1)S(1)} %fusion.45), channel_id=1, replica_groups=mesh['phi'=8,'query'=2,'event'=2] {'query'}, dimensions={0}, use_global_device_ids=true | all-gather | bytes 1376256 | tf_op jit(solution)/shard_map/all_gather | solution.py:275
  32.2 1.9 %copy-done.1 = f32[8,256,512]{2,1,0:T(8,128)} copy-done((f32[8,256,512]{2,1,0:T(8,128)}, f32[8,256,512]{2,1,0:T(8,128)S(1)}, u32[]{:S(2)}) %copy-start.1) | copy-done | bytes 4194328
  35.5 3.1 %convolution_convert_fusion.5 = bf16[8,32,256]{2,1,0:T(8,128)(2,1)S(1)} fusion(bf16[512,8,32]{0,2,1:T(8,128)(2,1)S(1)} %bitcast.159, f32[8,256,512]{2,1,0:T(8,128)} %copy-done.1, f32[8,256]{1,0:T(8,128)S(1)} %get-tuple-element.87), kind=kOutput, calls=%fused_computation.40 | convolution fusion | flops 70320128 | bytes 4595712 | tf_op jit(solution)/shard_map/hqk,khd->qhd/dot_general | solution.py:182
  42.0 1.9 %collective-permute-start.17 = (f32[8,256]{1,0:T(8,128)S(1)}, f32[8,256]{1,0:T(8,128)S(1)}, u32[]{:S(2)}, u32[]{:S(2)}) collective-permute-start(f32[8,256]{1,0:T(8,128)S(1)} %convert_reduce_fusion), channel_id=1, source_target_pairs={{0,4},{4,0},{8,12},{12,8},{16,20},{20,16},{24,28},{28,24},{1,5},{5... | collective-permute-start | bytes 24584 | tf_op jit(solution)/shard_map/ppermute | solution.py:34
  44.1 1.9 %collective-permute-start.8 = (f32[8,256]{1,0:T(8,128)S(1)}, f32[8,256]{1,0:T(8,128)S(1)}, u32[]{:S(2)}, u32[]{:S(2)}) collective-permute-start(f32[8,256]{1,0:T(8,128)S(1)} %convert_reduce_fusion.1), channel_id=1, source_target_pairs={{0,4},{4,0},{8,12},{12,8},{16,20},{20,16},{24,28},{28,24},{1,5},{5... | collective-permute-start | bytes 24584 | tf_op jit(solution)/shard_map/ppermute | solution.py:34
  46.5 2.1 %collective-permute-start.5 = (f32[8,256]{1,0:T(8,128)S(1)}, f32[8,256]{1,0:T(8,128)S(1)}, u32[]{:S(2)}, u32[]{:S(2)}) collective-permute-start(f32[8,256]{1,0:T(8,128)S(1)} %get-tuple-element.40), channel_id=1, source_target_pairs={{0,8},{4,12},{8,0},{12,4},{16,24},{20,28},{24,16},{28,20},{1,9},{5... | collective-permute-start | bytes 24584 | tf_op jit(solution)/shard_map/ppermute | solution.py:34
  50.4 2.0 %collective-permute-start.18 = (f32[8,256]{1,0:T(8,128)S(1)}, f32[8,256]{1,0:T(8,128)S(1)}, u32[]{:S(2)}, u32[]{:S(2)}) collective-permute-start(f32[8,256]{1,0:T(8,128)S(1)} %get-tuple-element.58), channel_id=1, source_target_pairs={{0,8},{4,12},{8,0},{12,4},{16,24},{20,28},{24,16},{28,20},{1,9},{5... | collective-permute-start | bytes 24584 | tf_op jit(solution)/shard_map/ppermute | solution.py:34
  54.0 2.0 %collective-permute-start.9 = (f32[8,256]{1,0:T(8,128)S(1)}, f32[8,256]{1,0:T(8,128)S(1)}, u32[]{:S(2)}, u32[]{:S(2)}) collective-permute-start(f32[8,256]{1,0:T(8,128)S(1)} %get-tuple-element.54), channel_id=1, source_target_pairs={{0,8},{4,12},{8,0},{12,4},{16,24},{20,28},{24,16},{28,20},{1,9},{5... | collective-permute-start | bytes 24584 | tf_op jit(solution)/shard_map/ppermute | solution.py:34
  57.7 2.7 %collective-permute-start.19 = (f32[8,256]{1,0:T(8,128)S(1)}, f32[8,256]{1,0:T(8,128)S(1)}, u32[]{:S(2)}, u32[]{:S(2)}) collective-permute-start(f32[8,256]{1,0:T(8,128)S(1)} %get-tuple-element.60), channel_id=1, source_target_pairs={{0,16},{4,20},{8,24},{12,28},{16,0},{20,4},{24,8},{28,12},{1,17},{... | collective-permute-start | bytes 24584 | tf_op jit(solution)/shard_map/ppermute | solution.py:34
  60.9 2.0 %collective-permute-start.13 = (bf16[256,256]{0,1:T(8,128)(2,1)S(1)}, bf16[256,256]{0,1:T(8,128)(2,1)S(1)}, u32[]{:S(2)}, u32[]{:S(2)}) collective-permute-start(bf16[256,256]{0,1:T(8,128)(2,1)S(1)} %fusion.62), channel_id=1, source_target_pairs={{0,8},{4,12},{8,0},{12,4},{16,24},{20,28},{24,16},{28,20},{1,9},{5... | collective-permute-start | bytes 393224 | tf_op jit(solution)/shard_map/ppermute | solution.py:34
  64.4 2.4 %collective-permute-done.13 = bf16[256,256]{0,1:T(8,128)(2,1)S(1)} collective-permute-done((bf16[256,256]{0,1:T(8,128)(2,1)S(1)}, bf16[256,256]{0,1:T(8,128)(2,1)S(1)}, u32[]{:S(2)}, u32[]{:S(2)}) %collective-permute-start.13) | collective-permute-done | bytes 131104 | tf_op jit(solution)/shard_map/ppermute | solution.py:34
  66.9 2.8 %collective-permute-start.15 = (bf16[256,256]{0,1:T(8,128)(2,1)S(1)}, bf16[256,256]{0,1:T(8,128)(2,1)S(1)}, u32[]{:S(2)}, u32[]{:S(2)}) collective-permute-start(bf16[256,256]{0,1:T(8,128)(2,1)S(1)} %fusion.60), channel_id=1, source_target_pairs={{0,16},{4,20},{8,24},{12,28},{16,0},{20,4},{24,8},{28,12},{1,17},{... | collective-permute-start | bytes 393224 | tf_op jit(solution)/shard_map/ppermute | solution.py:34
  71.0 1.8 %collective-permute-done.15 = bf16[256,256]{0,1:T(8,128)(2,1)S(1)} collective-permute-done((bf16[256,256]{0,1:T(8,128)(2,1)S(1)}, bf16[256,256]{0,1:T(8,128)(2,1)S(1)}, u32[]{:S(2)}, u32[]{:S(2)}) %collective-permute-start.15) | collective-permute-done | bytes 131104 | tf_op jit(solution)/shard_map/ppermute | solution.py:34
  73.2 4.4 %collective-permute-done.6 = bf16[256,256]{0,1:T(8,128)(2,1)S(1)} collective-permute-done((bf16[256,256]{0,1:T(8,128)(2,1)S(1)}, bf16[256,256]{0,1:T(8,128)(2,1)S(1)}, u32[]{:S(2)}, u32[]{:S(2)}) %collective-permute-start.6) | collective-permute-done | bytes 131104 | tf_op jit(solution)/shard_map/ppermute | solution.py:34
  86.0 2.0 %collective-permute-start.30 = (f32[256]{0:T(256)S(1)}, f32[256]{0:T(256)S(1)}, u32[]{:S(2)}, u32[]{:S(2)}) collective-permute-start(f32[256]{0:T(256)S(1)} %add.319), channel_id=1, source_target_pairs={{0,8},{4,12},{8,0},{12,4},{16,24},{20,28},{24,16},{28,20},{1,9},{5... | collective-permute-start | bytes 3080 | tf_op jit(solution)/shard_map/ppermute | solution.py:34
  88.1 1.9 %collective-permute-start.24 = (f32[256]{0:T(256)S(1)}, f32[256]{0:T(256)S(1)}, u32[]{:S(2)}, u32[]{:S(2)}) collective-permute-start(f32[256]{0:T(256)S(1)} %add.306), channel_id=1, source_target_pairs={{0,8},{4,12},{8,0},{12,4},{16,24},{20,28},{24,16},{28,20},{1,9},{5... | collective-permute-start | bytes 3080 | tf_op jit(solution)/shard_map/ppermute | solution.py:34
  90.2 1.9 %collective-permute-start.27 = (f32[256]{0:T(256)S(1)}, f32[256]{0:T(256)S(1)}, u32[]{:S(2)}, u32[]{:S(2)}) collective-permute-start(f32[256]{0:T(256)S(1)} %add.311), channel_id=1, source_target_pairs={{0,8},{4,12},{8,0},{12,4},{16,24},{20,28},{24,16},{28,20},{1,9},{5... | collective-permute-start | bytes 3080 | tf_op jit(solution)/shard_map/ppermute | solution.py:34
  92.3 2.7 %collective-permute-start.31 = (f32[256]{0:T(256)S(1)}, f32[256]{0:T(256)S(1)}, u32[]{:S(2)}, u32[]{:S(2)}) collective-permute-start(f32[256]{0:T(256)S(1)} %add.320), channel_id=1, source_target_pairs={{0,16},{4,20},{8,24},{12,28},{16,0},{20,4},{24,8},{28,12},{1,17},{... | collective-permute-start | bytes 3080 | tf_op jit(solution)/shard_map/ppermute | solution.py:34
  96.0 2.7 %collective-permute-start.25 = (f32[256]{0:T(256)S(1)}, f32[256]{0:T(256)S(1)}, u32[]{:S(2)}, u32[]{:S(2)}) collective-permute-start(f32[256]{0:T(256)S(1)} %add.307), channel_id=1, source_target_pairs={{0,16},{4,20},{8,24},{12,28},{16,0},{20,4},{24,8},{28,12},{1,17},{... | collective-permute-start | bytes 3080 | tf_op jit(solution)/shard_map/ppermute | solution.py:34
  98.9 2.7 %collective-permute-start.28 = (f32[256]{0:T(256)S(1)}, f32[256]{0:T(256)S(1)}, u32[]{:S(2)}, u32[]{:S(2)}) collective-permute-start(f32[256]{0:T(256)S(1)} %add.312), channel_id=1, source_target_pairs={{0,16},{4,20},{8,24},{12,28},{16,0},{20,4},{24,8},{28,12},{1,17},{... | collective-permute-start | bytes 3080 | tf_op jit(solution)/shard_map/ppermute | solution.py:34
  105.2 1.8 %collective-permute-start.42 = (bf16[256,256]{1,0:T(8,128)(2,1)S(1)}, bf16[256,256]{1,0:T(8,128)(2,1)S(1)}, u32[]{:S(2)}, u32[]{:S(2)}) collective-permute-start(bf16[256,256]{1,0:T(8,128)(2,1)S(1)} %convolution_convert_fusion.3), channel_id=1, source_target_pairs={{0,4},{4,0},{8,12},{12,8},{16,20},{20,16},{24,28},{28,24},{1,5},{5... | collective-permute-start | bytes 393224 | tf_op jit(solution)/shard_map/ppermute | solution.py:55
  108.1 2.8 %collective-permute-done.42 = bf16[256,256]{1,0:T(8,128)(2,1)S(1)} collective-permute-done((bf16[256,256]{1,0:T(8,128)(2,1)S(1)}, bf16[256,256]{1,0:T(8,128)(2,1)S(1)}, u32[]{:S(2)}, u32[]{:S(2)}) %collective-permute-start.42) | collective-permute-done | bytes 131104 | tf_op jit(solution)/shard_map/ppermute | solution.py:55
  110.9 2.0 %collective-permute-start.43 = (bf16[256,256]{1,0:T(8,128)(2,1)S(1)}, bf16[256,256]{1,0:T(8,128)(2,1)S(1)}, u32[]{:S(2)}, u32[]{:S(2)}) collective-permute-start(bf16[256,256]{1,0:T(8,128)(2,1)S(1)} %add_convert_fusion.1), channel_id=1, source_target_pairs={{0,8},{4,12},{8,0},{12,4},{16,24},{20,28},{24,16},{28,20},{1,9},{5... | collective-permute-start | bytes 393224 | tf_op jit(solution)/shard_map/ppermute | solution.py:55
  113.1 2.0 %collective-permute-start.40 = (bf16[256,256]{1,0:T(8,128)(2,1)S(1)}, bf16[256,256]{1,0:T(8,128)(2,1)S(1)}, u32[]{:S(2)}, u32[]{:S(2)}) collective-permute-start(bf16[256,256]{1,0:T(8,128)(2,1)S(1)} %add_convert_fusion.3), channel_id=1, source_target_pairs={{0,8},{4,12},{8,0},{12,4},{16,24},{20,28},{24,16},{28,20},{1,9},{5... | collective-permute-start | bytes 393224 | tf_op jit(solution)/shard_map/ppermute | solution.py:55
  116.3 3.2 %collective-permute-start.44 = (bf16[256,256]{1,0:T(8,128)(2,1)S(1)}, bf16[256,256]{1,0:T(8,128)(2,1)S(1)}, u32[]{:S(2)}, u32[]{:S(2)}) collective-permute-start(bf16[256,256]{1,0:T(8,128)(2,1)S(1)} %add_convert_fusion), channel_id=1, source_target_pairs={{0,16},{4,20},{8,24},{12,28},{16,0},{20,4},{24,8},{28,12},{1,17},{... | collective-permute-start | bytes 393224 | tf_op jit(solution)/shard_map/ppermute | solution.py:55
  120.2 2.2 %collective-permute-start.41 = (bf16[256,256]{1,0:T(8,128)(2,1)S(1)}, bf16[256,256]{1,0:T(8,128)(2,1)S(1)}, u32[]{:S(2)}, u32[]{:S(2)}) collective-permute-start(bf16[256,256]{1,0:T(8,128)(2,1)S(1)} %add_convert_fusion.2), channel_id=1, source_target_pairs={{0,16},{4,20},{8,24},{12,28},{16,0},{20,4},{24,8},{28,12},{1,17},{... | collective-permute-start | bytes 393224 | tf_op jit(solution)/shard_map/ppermute | solution.py:55
  123.1 5.6 %collective-permute-done.44 = bf16[256,256]{1,0:T(8,128)(2,1)S(1)} collective-permute-done((bf16[256,256]{1,0:T(8,128)(2,1)S(1)}, bf16[256,256]{1,0:T(8,128)(2,1)S(1)}, u32[]{:S(2)}, u32[]{:S(2)}) %collective-permute-start.44) | collective-permute-done | bytes 131104 | tf_op jit(solution)/shard_map/ppermute | solution.py:55
  128.7 1.7 %collective-permute-done.41 = bf16[256,256]{1,0:T(8,128)(2,1)S(1)} collective-permute-done((bf16[256,256]{1,0:T(8,128)(2,1)S(1)}, bf16[256,256]{1,0:T(8,128)(2,1)S(1)}, u32[]{:S(2)}, u32[]{:S(2)}) %collective-permute-start.41) | collective-permute-done | bytes 131104 | tf_op jit(solution)/shard_map/ppermute | solution.py:55
  (185 shorter events, 43.3 us)
Async XLA Ops:
  3.2 10.7 %collective-permute-start.1 = (bf16[256,512]{1,0:T(8,128)(2,1)S(1)}, bf16[256,512]{1,0:T(8,128)(2,1)S(1)}, u32[]{:S(2)}, u32[]{:S(2)}) collective-permute-start(bf16[256,512]{1,0:T(8,128)(2,1)S(1)} %slice.77), channel_id=1, source_target_pairs={{2,0},{4,2},{6,4},{8,6},{10,8},{12,10},{14,12},{16,14},{18,16},{20... | collective-permute-start | bytes 786440 | tf_op jit(solution)/shard_map/ppermute | solution.py:19
  8.7 8.5 %collective-permute-start = (bf16[256,512]{1,0:T(8,128)(2,1)S(1)}, bf16[256,512]{1,0:T(8,128)(2,1)S(1)}, u32[]{:S(2)}, u32[]{:S(2)}) collective-permute-start(bf16[256,512]{1,0:T(8,128)(2,1)S(1)} %slice.77), channel_id=1, source_target_pairs={{0,2},{2,4},{4,6},{6,8},{8,10},{10,12},{12,14},{14,16},{16,18},{18... | collective-permute-start | bytes 786440 | tf_op jit(solution)/shard_map/ppermute | solution.py:16
  32.1 14.1 %collective-permute-start.12 = (f32[8,256]{1,0:T(8,128)S(1)}, f32[8,256]{1,0:T(8,128)S(1)}, u32[]{:S(2)}, u32[]{:S(2)}) collective-permute-start(f32[8,256]{1,0:T(8,128)S(1)} %get-tuple-element.87), channel_id=1, source_target_pairs={{0,4},{4,0},{8,12},{12,8},{16,20},{20,16},{24,28},{28,24},{1,5},{5... | collective-permute-start | bytes 24584 | tf_op jit(solution)/shard_map/ppermute | solution.py:34
  39.5 7.0 %collective-permute-start.3 = (f32[8,256]{1,0:T(8,128)S(1)}, f32[8,256]{1,0:T(8,128)S(1)}, u32[]{:S(2)}, u32[]{:S(2)}) collective-permute-start(f32[8,256]{1,0:T(8,128)S(1)} %get-tuple-element.91), channel_id=1, source_target_pairs={{0,4},{4,0},{8,12},{12,8},{16,20},{20,16},{24,28},{28,24},{1,5},{5... | collective-permute-start | bytes 24584 | tf_op jit(solution)/shard_map/ppermute | solution.py:34
  43.9 16.5 %collective-permute-start.11 = (bf16[256,256]{0,1:T(8,128)(2,1)S(1)}, bf16[256,256]{0,1:T(8,128)(2,1)S(1)}, u32[]{:S(2)}, u32[]{:S(2)}) collective-permute-start(bf16[256,256]{0,1:T(8,128)(2,1)S(1)} %bitcast.162), channel_id=1, source_target_pairs={{0,4},{4,0},{8,12},{12,8},{16,20},{20,16},{24,28},{28,24},{1,5},{5... | collective-permute-start | bytes 393224 | tf_op jit(solution)/shard_map/ppermute | solution.py:34
  44.1 6.3 %collective-permute-start.8 = (f32[8,256]{1,0:T(8,128)S(1)}, f32[8,256]{1,0:T(8,128)S(1)}, u32[]{:S(2)}, u32[]{:S(2)}) collective-permute-start(f32[8,256]{1,0:T(8,128)S(1)} %convert_reduce_fusion.1), channel_id=1, source_target_pairs={{0,4},{4,0},{8,12},{12,8},{16,20},{20,16},{24,28},{28,24},{1,5},{5... | collective-permute-start | bytes 24584 | tf_op jit(solution)/shard_map/ppermute | solution.py:34
  46.2 16.7 %collective-permute-start.2 = (bf16[256,256]{0,1:T(8,128)(2,1)S(1)}, bf16[256,256]{0,1:T(8,128)(2,1)S(1)}, u32[]{:S(2)}, u32[]{:S(2)}) collective-permute-start(bf16[256,256]{0,1:T(8,128)(2,1)S(1)} %bitcast.161), channel_id=1, source_target_pairs={{0,4},{4,0},{8,12},{12,8},{16,20},{20,16},{24,28},{28,24},{1,5},{5... | collective-permute-start | bytes 393224 | tf_op jit(solution)/shard_map/ppermute | solution.py:34
  46.5 5.9 %collective-permute-start.5 = (f32[8,256]{1,0:T(8,128)S(1)}, f32[8,256]{1,0:T(8,128)S(1)}, u32[]{:S(2)}, u32[]{:S(2)}) collective-permute-start(f32[8,256]{1,0:T(8,128)S(1)} %get-tuple-element.40), channel_id=1, source_target_pairs={{0,8},{4,12},{8,0},{12,4},{16,24},{20,28},{24,16},{28,20},{1,9},{5... | collective-permute-start | bytes 24584 | tf_op jit(solution)/shard_map/ppermute | solution.py:34
  50.2 10.7 %collective-permute-start.16 = (f32[8,256]{1,0:T(8,128)S(1)}, f32[8,256]{1,0:T(8,128)S(1)}, u32[]{:S(2)}, u32[]{:S(2)}) collective-permute-start(f32[8,256]{1,0:T(8,128)S(1)} %get-tuple-element.70), channel_id=1, source_target_pairs={{0,16},{4,20},{8,24},{12,28},{16,0},{20,4},{24,8},{28,12},{1,17},{... | collective-permute-start | bytes 24584 | tf_op jit(solution)/shard_map/ppermute | solution.py:34
  52.4 17.2 %collective-permute-start.7 = (f32[8,256]{1,0:T(8,128)S(1)}, f32[8,256]{1,0:T(8,128)S(1)}, u32[]{:S(2)}, u32[]{:S(2)}) collective-permute-start(f32[8,256]{1,0:T(8,128)S(1)} %get-tuple-element.68), channel_id=1, source_target_pairs={{0,16},{4,20},{8,24},{12,28},{16,0},{20,4},{24,8},{28,12},{1,17},{... | collective-permute-start | bytes 24584 | tf_op jit(solution)/shard_map/ppermute | solution.py:34
  57.7 5.1 %collective-permute-start.19 = (f32[8,256]{1,0:T(8,128)S(1)}, f32[8,256]{1,0:T(8,128)S(1)}, u32[]{:S(2)}, u32[]{:S(2)}) collective-permute-start(f32[8,256]{1,0:T(8,128)S(1)} %get-tuple-element.60), channel_id=1, source_target_pairs={{0,16},{4,20},{8,24},{12,28},{16,0},{20,4},{24,8},{28,12},{1,17},{... | collective-permute-start | bytes 24584 | tf_op jit(solution)/shard_map/ppermute | solution.py:34
  60.5 9.2 %collective-permute-start.10 = (f32[8,256]{1,0:T(8,128)S(1)}, f32[8,256]{1,0:T(8,128)S(1)}, u32[]{:S(2)}, u32[]{:S(2)}) collective-permute-start(f32[8,256]{1,0:T(8,128)S(1)} %get-tuple-element.56), channel_id=1, source_target_pairs={{0,16},{4,20},{8,24},{12,28},{16,0},{20,4},{24,8},{28,12},{1,17},{... | collective-permute-start | bytes 24584 | tf_op jit(solution)/shard_map/ppermute | solution.py:34
  60.9 5.9 %collective-permute-start.13 = (bf16[256,256]{0,1:T(8,128)(2,1)S(1)}, bf16[256,256]{0,1:T(8,128)(2,1)S(1)}, u32[]{:S(2)}, u32[]{:S(2)}) collective-permute-start(bf16[256,256]{0,1:T(8,128)(2,1)S(1)} %fusion.62), channel_id=1, source_target_pairs={{0,8},{4,12},{8,0},{12,4},{16,24},{20,28},{24,16},{28,20},{1,9},{5... | collective-permute-start | bytes 393224 | tf_op jit(solution)/shard_map/ppermute | solution.py:34
  63.0 7.5 %collective-permute-start.4 = (bf16[256,256]{0,1:T(8,128)(2,1)S(1)}, bf16[256,256]{0,1:T(8,128)(2,1)S(1)}, u32[]{:S(2)}, u32[]{:S(2)}) collective-permute-start(bf16[256,256]{0,1:T(8,128)(2,1)S(1)} %fusion.69), channel_id=1, source_target_pairs={{0,8},{4,12},{8,0},{12,4},{16,24},{20,28},{24,16},{28,20},{1,9},{5... | collective-permute-start | bytes 393224 | tf_op jit(solution)/shard_map/ppermute | solution.py:34
  66.9 5.9 %collective-permute-start.15 = (bf16[256,256]{0,1:T(8,128)(2,1)S(1)}, bf16[256,256]{0,1:T(8,128)(2,1)S(1)}, u32[]{:S(2)}, u32[]{:S(2)}) collective-permute-start(bf16[256,256]{0,1:T(8,128)(2,1)S(1)} %fusion.60), channel_id=1, source_target_pairs={{0,16},{4,20},{8,24},{12,28},{16,0},{20,4},{24,8},{28,12},{1,17},{... | collective-permute-start | bytes 393224 | tf_op jit(solution)/shard_map/ppermute | solution.py:34
  70.6 7.1 %collective-permute-start.6 = (bf16[256,256]{0,1:T(8,128)(2,1)S(1)}, bf16[256,256]{0,1:T(8,128)(2,1)S(1)}, u32[]{:S(2)}, u32[]{:S(2)}) collective-permute-start(bf16[256,256]{0,1:T(8,128)(2,1)S(1)} %fusion.67), channel_id=1, source_target_pairs={{0,16},{4,20},{8,24},{12,28},{16,0},{20,4},{24,8},{28,12},{1,17},{... | collective-permute-start | bytes 393224 | tf_op jit(solution)/shard_map/ppermute | solution.py:34
  79.8 5.3 %collective-permute-start.32 = (f32[256]{0:T(256)S(1)}, f32[256]{0:T(256)S(1)}, u32[]{:S(2)}, u32[]{:S(2)}) collective-permute-start(f32[256]{0:T(256)S(1)} %get-tuple-element.24), channel_id=1, source_target_pairs={{0,4},{4,0},{8,12},{12,8},{16,20},{20,16},{24,28},{28,24},{1,5},{5... | collective-permute-start | bytes 3080 | tf_op jit(solution)/shard_map/ppermute | solution.py:34
  86.0 6.1 %collective-permute-start.30 = (f32[256]{0:T(256)S(1)}, f32[256]{0:T(256)S(1)}, u32[]{:S(2)}, u32[]{:S(2)}) collective-permute-start(f32[256]{0:T(256)S(1)} %add.319), channel_id=1, source_target_pairs={{0,8},{4,12},{8,0},{12,4},{16,24},{20,28},{24,16},{28,20},{1,9},{5... | collective-permute-start | bytes 3080 | tf_op jit(solution)/shard_map/ppermute | solution.py:34
  88.1 7.6 %collective-permute-start.24 = (f32[256]{0:T(256)S(1)}, f32[256]{0:T(256)S(1)}, u32[]{:S(2)}, u32[]{:S(2)}) collective-permute-start(f32[256]{0:T(256)S(1)} %add.306), channel_id=1, source_target_pairs={{0,8},{4,12},{8,0},{12,4},{16,24},{20,28},{24,16},{28,20},{1,9},{5... | collective-permute-start | bytes 3080 | tf_op jit(solution)/shard_map/ppermute | solution.py:34
  90.1 5.9 %collective-permute-start.21 = (f32[256]{0:T(256)S(1)}, f32[256]{0:T(256)S(1)}, u32[]{:S(2)}, u32[]{:S(2)}) collective-permute-start(f32[256]{0:T(256)S(1)} %add.303), channel_id=1, source_target_pairs={{0,8},{4,12},{8,0},{12,4},{16,24},{20,28},{24,16},{28,20},{1,9},{5... | collective-permute-start | bytes 3080 | tf_op jit(solution)/shard_map/ppermute | solution.py:34
  90.2 8.5 %collective-permute-start.27 = (f32[256]{0:T(256)S(1)}, f32[256]{0:T(256)S(1)}, u32[]{:S(2)}, u32[]{:S(2)}) collective-permute-start(f32[256]{0:T(256)S(1)} %add.311), channel_id=1, source_target_pairs={{0,8},{4,12},{8,0},{12,4},{16,24},{20,28},{24,16},{28,20},{1,9},{5... | collective-permute-start | bytes 3080 | tf_op jit(solution)/shard_map/ppermute | solution.py:34
  92.1 6.8 %collective-permute-start.34 = (f32[256]{0:T(256)S(1)}, f32[256]{0:T(256)S(1)}, u32[]{:S(2)}, u32[]{:S(2)}) collective-permute-start(f32[256]{0:T(256)S(1)} %add.323), channel_id=1, source_target_pairs={{0,16},{4,20},{8,24},{12,28},{16,0},{20,4},{24,8},{28,12},{1,17},{... | collective-permute-start | bytes 3080 | tf_op jit(solution)/shard_map/ppermute | solution.py:34
  92.3 9.3 %collective-permute-start.31 = (f32[256]{0:T(256)S(1)}, f32[256]{0:T(256)S(1)}, u32[]{:S(2)}, u32[]{:S(2)}) collective-permute-start(f32[256]{0:T(256)S(1)} %add.320), channel_id=1, source_target_pairs={{0,16},{4,20},{8,24},{12,28},{16,0},{20,4},{24,8},{28,12},{1,17},{... | collective-permute-start | bytes 3080 | tf_op jit(solution)/shard_map/ppermute | solution.py:34
  95.8 7.4 %collective-permute-start.37 = (f32[256]{0:T(256)S(1)}, f32[256]{0:T(256)S(1)}, u32[]{:S(2)}, u32[]{:S(2)}) collective-permute-start(f32[256]{0:T(256)S(1)} %add.328), channel_id=1, source_target_pairs={{0,16},{4,20},{8,24},{12,28},{16,0},{20,4},{24,8},{28,12},{1,17},{... | collective-permute-start | bytes 3080 | tf_op jit(solution)/shard_map/ppermute | solution.py:34
  96.0 5.7 %collective-permute-start.25 = (f32[256]{0:T(256)S(1)}, f32[256]{0:T(256)S(1)}, u32[]{:S(2)}, u32[]{:S(2)}) collective-permute-start(f32[256]{0:T(256)S(1)} %add.307), channel_id=1, source_target_pairs={{0,16},{4,20},{8,24},{12,28},{16,0},{20,4},{24,8},{28,12},{1,17},{... | collective-permute-start | bytes 3080 | tf_op jit(solution)/shard_map/ppermute | solution.py:34
  105.2 5.7 %collective-permute-start.42 = (bf16[256,256]{1,0:T(8,128)(2,1)S(1)}, bf16[256,256]{1,0:T(8,128)(2,1)S(1)}, u32[]{:S(2)}, u32[]{:S(2)}) collective-permute-start(bf16[256,256]{1,0:T(8,128)(2,1)S(1)} %convolution_convert_fusion.3), channel_id=1, source_target_pairs={{0,4},{4,0},{8,12},{12,8},{16,20},{20,16},{24,28},{28,24},{1,5},{5... | collective-permute-start | bytes 393224 | tf_op jit(solution)/shard_map/ppermute | solution.py:55
  107.0 15.3 %collective-permute-start.38 = (f32[256,256]{1,0:T(8,128)S(1)}, f32[256,256]{1,0:T(8,128)S(1)}, u32[]{:S(2)}, u32[]{:S(2)}) collective-permute-start(f32[256,256]{1,0:T(8,128)S(1)} %slice_select_fusion), channel_id=1, source_target_pairs={{0,2},{2,0},{1,3},{3,1},{4,6},{6,4},{5,7},{7,5},{8,10},{10,8},{9,1... | collective-permute-start | bytes 786440 | tf_op jit(solution)/shard_map/ppermute | solution.py:87
  107.1 5.9 %collective-permute-start.39 = (bf16[256,256]{1,0:T(8,128)(2,1)S(1)}, bf16[256,256]{1,0:T(8,128)(2,1)S(1)}, u32[]{:S(2)}, u32[]{:S(2)}) collective-permute-start(bf16[256,256]{1,0:T(8,128)(2,1)S(1)} %convolution_convert_fusion.4), channel_id=1, source_target_pairs={{0,4},{4,0},{8,12},{12,8},{16,20},{20,16},{24,28},{28,24},{1,5},{5... | collective-permute-start | bytes 393224 | tf_op jit(solution)/shard_map/ppermute | solution.py:55
  110.9 5.4 %collective-permute-start.43 = (bf16[256,256]{1,0:T(8,128)(2,1)S(1)}, bf16[256,256]{1,0:T(8,128)(2,1)S(1)}, u32[]{:S(2)}, u32[]{:S(2)}) collective-permute-start(bf16[256,256]{1,0:T(8,128)(2,1)S(1)} %add_convert_fusion.1), channel_id=1, source_target_pairs={{0,8},{4,12},{8,0},{12,4},{16,24},{20,28},{24,16},{28,20},{1,9},{5... | collective-permute-start | bytes 393224 | tf_op jit(solution)/shard_map/ppermute | solution.py:55
  113.1 7.1 %collective-permute-start.40 = (bf16[256,256]{1,0:T(8,128)(2,1)S(1)}, bf16[256,256]{1,0:T(8,128)(2,1)S(1)}, u32[]{:S(2)}, u32[]{:S(2)}) collective-permute-start(bf16[256,256]{1,0:T(8,128)(2,1)S(1)} %add_convert_fusion.3), channel_id=1, source_target_pairs={{0,8},{4,12},{8,0},{12,4},{16,24},{20,28},{24,16},{28,20},{1,9},{5... | collective-permute-start | bytes 393224 | tf_op jit(solution)/shard_map/ppermute | solution.py:55
  116.3 12.4 %collective-permute-start.44 = (bf16[256,256]{1,0:T(8,128)(2,1)S(1)}, bf16[256,256]{1,0:T(8,128)(2,1)S(1)}, u32[]{:S(2)}, u32[]{:S(2)}) collective-permute-start(bf16[256,256]{1,0:T(8,128)(2,1)S(1)} %add_convert_fusion), channel_id=1, source_target_pairs={{0,16},{4,20},{8,24},{12,28},{16,0},{20,4},{24,8},{28,12},{1,17},{... | collective-permute-start | bytes 393224 | tf_op jit(solution)/shard_map/ppermute | solution.py:55
  120.2 10.2 %collective-permute-start.41 = (bf16[256,256]{1,0:T(8,128)(2,1)S(1)}, bf16[256,256]{1,0:T(8,128)(2,1)S(1)}, u32[]{:S(2)}, u32[]{:S(2)}) collective-permute-start(bf16[256,256]{1,0:T(8,128)(2,1)S(1)} %add_convert_fusion.2), channel_id=1, source_target_pairs={{0,16},{4,20},{8,24},{12,28},{16,0},{20,4},{24,8},{28,12},{1,17},{... | collective-permute-start | bytes 393224 | tf_op jit(solution)/shard_map/ppermute | solution.py:55
  (22 other events, 204.7 us)

commit v7 on v2

--- a/solution.py
+++ b/solution.py
@@ -249,7 +249,9 @@
         jnp.float32
     )
     intersection, predicted, truth_count = butterfly(
-        (jnp.sum(sigma * target, axis=1), jnp.sum(sigma, axis=1), jnp.sum(target, axis=1)),
+        jnp.stack(
+            [jnp.sum(sigma * target, axis=1), jnp.sum(sigma, axis=1), jnp.sum(target, axis=1)]
+        ),
         "phi",
         add_trees,
     )

time: 107 us -> 105 us (0.981)
  starting transfers between devices: 30.4 us -> 20.8 us
  waiting for transfers between devices: 44.8 us -> 52 us
    ppermute x18 -> x12, starting transfers between devices: 21 us -> 13.7 us  [butterfly(): other = lax.ppermute(tree, axis, partner_pairs(count, distance))]
    ppermute x18 -> x12, waiting for transfers between devices: 23.8 us -> 29.2 us  [butterfly(): other = lax.ppermute(tree, axis, partner_pairs(count, distance))]
    ppermute x3, starting transfers between devices: 3.78 us -> 1.52 us  [narrow_butterfly(): other = lax.ppermute(sent, axis, partner_pairs(count, distance))]
    ppermute x3, waiting for transfers between devices: 19.2 us -> 21.1 us  [narrow_butterfly(): other = lax.ppermute(sent, axis, partner_pairs(count, distance))]
  transfers between devices with their start and end apart: 24 -> 18, of which waited for: 14 -> 10; matrix products, arithmetic and copies ran while one was open for 7% -> 7% of each run, Pallas kernels for 0% -> 0%
where the time goes in v7:
time: 105 us
  waiting for transfers between devices  52 us (50%)
  starting transfers between devices  20.8 us (20%)
  matrix products  17.8 us (17%)
  other arithmetic  6.42 us (6%)
  blocking collectives  4.35 us (4%)
  local copies, waits for them, and re-layouts  2.38 us (2%)
  between operations  1.15 us (1%)
    ppermute x12, waiting for transfers between devices, butterfly(): other = lax.ppermute(tree, axis, partner_pairs(count, distance))  29.2 us
    ppermute x3, waiting for transfers between devices, narrow_butterfly(): other = lax.ppermute(sent, axis, partner_pairs(count, distance))  21.1 us
    ppermute x12, starting transfers between devices, butterfly(): other = lax.ppermute(tree, axis, partner_pairs(count, distance))  13.7 us
    sub x1, matrix products, window_attend(): raised = jnp.exp(scores - jnp.max(scores, axis=-1, keepdims=True))  5.11 us
    ppermute x1, starting transfers between devices, extended_2(): lax.ppermute(lax.slice_in_dim(block, 0, width, axis=dim), axis, backward)  5.03 us
    all_gather x1, blocking collectives, body(): lax.all_gather(jnp.concatenate([local_kv, encoded, digits], axis=1), 'que...  4.35 us
    dot_general x1, matrix products, window_attend(): jnp.einsum('hqk,khd->qhd', weights, value_heads, preferred_element_type=j...  3.97 us
  transfers between devices with their start and end apart: 18, of which 10 were waited for; matrix products, arithmetic and copies ran while one was open for 7% of the time, Pallas kernels for 0%

profile of v7, /device:TPU:0, one launch (start us, length us, event | category | flops | bytes accessed | tf_op | source)
XLA Modules:
  0.0 104.9 jit_solution(14582765735948454879)
XLA Ops:
  0.6 1.1 %copy.40 = bf16[256,256]{0,1:T(8,128)(2,1)S(1)} copy(bf16[256,256]{1,0:T(8,128)(2,1)} %param.13) | data formatting | bytes 262144 | tf_op args[0]
  1.9 1.3 %convolution_convert_fusion = bf16[256,768]{1,0:T(8,128)(2,1)S(1)} fusion(bf16[256,768]{1,0:T(8,128)(2,1)} %param.14, bf16[256,256]{0,1:T(8,128)(2,1)S(1)} %copy.40, f32[256]{0:T(256)S(1)} %add_rsqrt_fusion.3, f32[256]{0:T(256)S(1)} %broadcast_multiply_fusion.3), kind=kOutput, calls=%fused_computation.20 | convolution fusion | flops 101122048 | bytes 919552 | tf_op jit(solution)/shard_map/dot_general | solution.py:178
  3.7 5.0 %collective-permute-start.1 = (bf16[256,512]{1,0:T(8,128)(2,1)S(1)}, bf16[256,512]{1,0:T(8,128)(2,1)S(1)}, u32[]{:S(2)}, u32[]{:S(2)}) collective-permute-start(bf16[256,512]{1,0:T(8,128)(2,1)S(1)} %slice.51), channel_id=1, source_target_pairs={{2,0},{4,2},{6,4},{8,6},{10,8},{12,10},{14,12},{16,14},{18,16},{20... | collective-permute-start | bytes 786440 | tf_op jit(solution)/shard_map/ppermute | solution.py:19
  9.8 1.2 %convolution_convert_fusion.4 = bf16[512,256]{0,1:T(8,128)(2,1)S(1)} fusion(bf16[512,256]{1,0:T(8,128)(2,1)} %param.18, bf16[256,256]{1,0:T(8,128)(2,1)} %param.19), kind=kOutput, calls=%fused_computation.26 | convolution fusion | flops 67239936 | bytes 655360 | tf_op jit(solution)/shard_map/dot_general | solution.py:206
  11.1 1.7 %collective-permute-done = bf16[256,512]{1,0:T(8,128)(2,1)S(1)} collective-permute-done((bf16[256,512]{1,0:T(8,128)(2,1)S(1)}, bf16[256,512]{1,0:T(8,128)(2,1)S(1)}, u32[]{:S(2)}, u32[]{:S(2)}) %collective-permute-start) | collective-permute-done | bytes 262176 | tf_op jit(solution)/shard_map/ppermute | solution.py:16
  13.3 5.1 %fusion.102 = (f32[8,256]{1,0:T(8,128)S(1)}, f32[8,256,768]{2,1,0:T(8,128)}) fusion(pred[256,768]{1,0:T(8,128)(4,1)S(1)} %fusion.28, bf16[256,8,32]{0,2,1:T(8,128)(2,1)S(1)} %bitcast.102, bf16[768,8,32]{0,2,1:T(8,128)(2,1)S(1)} %bitcast.99), kind=kOutput, calls=%fused_computation.176 | convolution fusion | flops 106955520 | bytes 7020544 | tf_op jit(solution)/shard_map/sub | solution.py:115
  18.4 4.0 %fusion.12 = bf16[8,32,256]{2,1,0:T(8,128)(2,1)S(1)} fusion(bf16[768,8,32]{0,2,1:T(8,128)(2,1)S(1)} %bitcast.100, f32[8,256,768]{2,1,0:T(8,128)} %get-tuple-element.49, f32[8,256]{1,0:T(8,128)S(1)} %get-tuple-element.48), kind=kOutput, calls=%fused_computation.32 | convolution fusion | flops 103874560 | bytes 6823936 | tf_op jit(solution)/shard_map/hqk,khd->qhd/dot_general | solution.py:117
  22.8 0.8 convert_reduce_fusion.3
  24.1 4.3 %all_gather.3 = bf16[512,896]{1,0:T(8,128)(2,1)S(1)} all-gather(bf16[256,896]{1,0:T(8,128)(2,1)S(1)} %fusion.43), channel_id=1, replica_groups=mesh['phi'=8,'query'=2,'event'=2] {'query'}, dimensions={0}, use_global_device_ids=true | all-gather | bytes 1376256 | tf_op jit(solution)/shard_map/all_gather | solution.py:199
  28.8 1.3 %multiply_reduce_fusion = (f32[8,512]{1,0:T(8,128)S(1)}, f32[8,512,512]{1,2,0:T(8,128)S(1)}) fusion(bf16[512,8,32]{0,2,1:T(8,128)(2,1)S(1)} %bitcast.95, bf16[512,8,32]{0,2,1:T(8,128)(2,1)S(1)} %bitcast.97), kind=kOutput, calls=%fused_computation.3 | convolution fusion | flops 138407936 | bytes 8929280 | tf_op jit(solution)/shard_map/qhd,khd->hqk/dot_general | solution.py:212
  30.3 1.4 %convert_reduce_fusion = f32[8,512]{1,0:T(8,128)S(1)} fusion(f32[8,512]{1,0:T(8,128)S(1)} %get-tuple-element.54, f32[8,512,512]{1,2,0:T(8,128)S(1)} %get-tuple-element.55), kind=kLoop, calls=%fused_computation.1 | loop fusion | flops 10481664 | bytes 8421376 | tf_op jit(solution)/shard_map/reduce_sum | solution.py:217
  31.7 1.5 %convolution_convert_fusion.3 = bf16[8,32,512]{2,1,0:T(8,128)(2,1)S(1)} fusion(bf16[512,8,32]{0,2,1:T(8,128)(2,1)S(1)} %bitcast.96, f32[8,512,512]{1,2,0:T(8,128)S(1)} %get-tuple-element.55, f32[8,512]{1,0:T(8,128)S(1)} %get-tuple-element.54), kind=kOutput, calls=%fused_computation.25 | convolution fusion | flops 140640256 | bytes 8929280 | tf_op jit(solution)/shard_map/hqk,khd->qhd/dot_general | solution.py:218
  33.2 2.0 %collective-permute-start.2 = (bf16[512,256]{0,1:T(8,128)(2,1)S(1)}, bf16[512,256]{0,1:T(8,128)(2,1)S(1)}, u32[]{:S(2)}, u32[]{:S(2)}) collective-permute-start(bf16[512,256]{0,1:T(8,128)(2,1)S(1)} %bitcast.98), channel_id=1, source_target_pairs={{0,4},{4,0},{8,12},{12,8},{16,20},{20,16},{24,28},{28,24},{1,5},{5... | collective-permute-start | bytes 786440 | tf_op jit(solution)/shard_map/ppermute | solution.py:34
  35.3 1.3 %collective-permute-start.5 = (f32[8,512]{1,0:T(8,128)S(1)}, f32[8,512]{1,0:T(8,128)S(1)}, u32[]{:S(2)}, u32[]{:S(2)}) collective-permute-start(f32[8,512]{1,0:T(8,128)S(1)} %get-tuple-element.30), channel_id=1, source_target_pairs={{0,8},{4,12},{8,0},{12,4},{16,24},{20,28},{24,16},{28,20},{1,9},{5... | collective-permute-start | bytes 49160 | tf_op jit(solution)/shard_map/ppermute | solution.py:34
  36.8 5.4 %collective-permute-done.8 = f32[8,512]{1,0:T(8,128)S(1)} collective-permute-done((f32[8,512]{1,0:T(8,128)S(1)}, f32[8,512]{1,0:T(8,128)S(1)}, u32[]{:S(2)}, u32[]{:S(2)}) %collective-permute-start.8) | collective-permute-done | bytes 16416 | tf_op jit(solution)/shard_map/ppermute | solution.py:34
  42.2 1.0 collective-permute-start.9
  43.4 1.1 %collective-permute-start.4 = (bf16[512,256]{0,1:T(8,128)(2,1)S(1)}, bf16[512,256]{0,1:T(8,128)(2,1)S(1)}, u32[]{:S(2)}, u32[]{:S(2)}) collective-permute-start(bf16[512,256]{0,1:T(8,128)(2,1)S(1)} %fusion.38), channel_id=1, source_target_pairs={{0,8},{4,12},{8,0},{12,4},{16,24},{20,28},{24,16},{28,20},{1,9},{5... | collective-permute-start | bytes 786440 | tf_op jit(solution)/shard_map/ppermute | solution.py:34
  44.5 2.1 %collective-permute-start.7 = (f32[8,512]{1,0:T(8,128)S(1)}, f32[8,512]{1,0:T(8,128)S(1)}, u32[]{:S(2)}, u32[]{:S(2)}) collective-permute-start(f32[8,512]{1,0:T(8,128)S(1)} %get-tuple-element.43), channel_id=1, source_target_pairs={{0,16},{4,20},{8,24},{12,28},{16,0},{20,4},{24,8},{28,12},{1,17},{... | collective-permute-start | bytes 49160 | tf_op jit(solution)/shard_map/ppermute | solution.py:34
  46.6 1.6 %collective-permute-start.10 = (f32[8,512]{1,0:T(8,128)S(1)}, f32[8,512]{1,0:T(8,128)S(1)}, u32[]{:S(2)}, u32[]{:S(2)}) collective-permute-start(f32[8,512]{1,0:T(8,128)S(1)} %get-tuple-element.38), channel_id=1, source_target_pairs={{0,16},{4,20},{8,24},{12,28},{16,0},{20,4},{24,8},{28,12},{1,17},{... | collective-permute-start | bytes 49160 | tf_op jit(solution)/shard_map/ppermute | solution.py:34
  48.2 3.3 %collective-permute-done.4 = bf16[512,256]{0,1:T(8,128)(2,1)S(1)} collective-permute-done((bf16[512,256]{0,1:T(8,128)(2,1)S(1)}, bf16[512,256]{0,1:T(8,128)(2,1)S(1)}, u32[]{:S(2)}, u32[]{:S(2)}) %collective-permute-start.4) | collective-permute-done | bytes 262176 | tf_op jit(solution)/shard_map/ppermute | solution.py:34
  51.6 2.3 %collective-permute-start.6 = (bf16[512,256]{0,1:T(8,128)(2,1)S(1)}, bf16[512,256]{0,1:T(8,128)(2,1)S(1)}, u32[]{:S(2)}, u32[]{:S(2)}) collective-permute-start(bf16[512,256]{0,1:T(8,128)(2,1)S(1)} %fusion.36), channel_id=1, source_target_pairs={{0,16},{4,20},{8,24},{12,28},{16,0},{20,4},{24,8},{28,12},{1,17},{... | collective-permute-start | bytes 786440 | tf_op jit(solution)/shard_map/ppermute | solution.py:34
  54.2 10.5 %collective-permute-done.6 = bf16[512,256]{0,1:T(8,128)(2,1)S(1)} collective-permute-done((bf16[512,256]{0,1:T(8,128)(2,1)S(1)}, bf16[512,256]{0,1:T(8,128)(2,1)S(1)}, u32[]{:S(2)}, u32[]{:S(2)}) %collective-permute-start.6) | collective-permute-done | bytes 262176 | tf_op jit(solution)/shard_map/ppermute | solution.py:34
  66.5 1.4 %collective-permute-start.11 = (f32[3,512]{1,0:T(4,128)S(1)}, f32[3,512]{1,0:T(4,128)S(1)}, u32[]{:S(2)}, u32[]{:S(2)}) collective-permute-start(f32[3,512]{1,0:T(4,128)S(1)} %pad_maximum_fusion.1), channel_id=1, source_target_pairs={{0,4},{4,0},{8,12},{12,8},{16,20},{20,16},{24,28},{28,24},{1,5},{5... | collective-permute-start | bytes 18440 | tf_op jit(solution)/shard_map/ppermute | solution.py:34
  67.8 2.3 %collective-permute-done.11 = f32[3,512]{1,0:T(4,128)S(1)} collective-permute-done((f32[3,512]{1,0:T(4,128)S(1)}, f32[3,512]{1,0:T(4,128)S(1)}, u32[]{:S(2)}, u32[]{:S(2)}) %collective-permute-start.11) | collective-permute-done | bytes 6176 | tf_op jit(solution)/shard_map/ppermute | solution.py:34
  70.3 3.6 %collective-permute-done.12 = f32[3,512]{1,0:T(4,128)S(1)} collective-permute-done((f32[3,512]{1,0:T(4,128)S(1)}, f32[3,512]{1,0:T(4,128)S(1)}, u32[]{:S(2)}, u32[]{:S(2)}) %collective-permute-start.12) | collective-permute-done | bytes 6176 | tf_op jit(solution)/shard_map/ppermute | solution.py:34
  74.5 4.0 %collective-permute-done.13 = f32[3,512]{1,0:T(4,128)S(1)} collective-permute-done((f32[3,512]{1,0:T(4,128)S(1)}, f32[3,512]{1,0:T(4,128)S(1)}, u32[]{:S(2)}, u32[]{:S(2)}) %collective-permute-start.13) | collective-permute-done | bytes 6176 | tf_op jit(solution)/shard_map/ppermute | solution.py:34
  80.1 1.4 %collective-permute-start.15 = (bf16[512,256]{1,0:T(8,128)(2,1)S(1)}, bf16[512,256]{1,0:T(8,128)(2,1)S(1)}, u32[]{:S(2)}, u32[]{:S(2)}) collective-permute-start(bf16[512,256]{1,0:T(8,128)(2,1)S(1)} %convolution_convert_fusion.1), channel_id=1, source_target_pairs={{0,4},{4,0},{8,12},{12,8},{16,20},{20,16},{24,28},{28,24},{1,5},{5... | collective-permute-start | bytes 786440 | tf_op jit(solution)/shard_map/ppermute | solution.py:55
  81.5 5.1 %collective-permute-done.15 = bf16[512,256]{1,0:T(8,128)(2,1)S(1)} collective-permute-done((bf16[512,256]{1,0:T(8,128)(2,1)S(1)}, bf16[512,256]{1,0:T(8,128)(2,1)S(1)}, u32[]{:S(2)}, u32[]{:S(2)}) %collective-permute-start.15) | collective-permute-done | bytes 262176 | tf_op jit(solution)/shard_map/ppermute | solution.py:55
  87.1 7.8 %collective-permute-done.16 = bf16[512,256]{1,0:T(8,128)(2,1)S(1)} collective-permute-done((bf16[512,256]{1,0:T(8,128)(2,1)S(1)}, bf16[512,256]{1,0:T(8,128)(2,1)S(1)}, u32[]{:S(2)}, u32[]{:S(2)}) %collective-permute-start.16) | collective-permute-done | bytes 262176 | tf_op jit(solution)/shard_map/ppermute | solution.py:55
  95.0 0.8 select_add_fusion
  95.8 8.3 %collective-permute-done.17 = bf16[512,256]{1,0:T(8,128)(2,1)S(1)} collective-permute-done((bf16[512,256]{1,0:T(8,128)(2,1)S(1)}, bf16[512,256]{1,0:T(8,128)(2,1)S(1)}, u32[]{:S(2)}, u32[]{:S(2)}) %collective-permute-start.17) | collective-permute-done | bytes 262176 | tf_op jit(solution)/shard_map/ppermute | solution.py:55
  104.1 0.8 convert_add_fusion
  (97 shorter events, 9.0 us)
Async XLA Ops:
  0.6 22.1 %copy-start = (bf16[1024,256]{1,0:T(8,128)(2,1)S(1)}, bf16[1024,256]{1,0:T(8,128)(2,1)}, u32[]{:S(2)}) copy-start(bf16[1024,256]{1,0:T(8,128)(2,1)} %param.17) | copy-start | bytes 1572868
  3.2 9.6 %collective-permute-start = (bf16[256,512]{1,0:T(8,128)(2,1)S(1)}, bf16[256,512]{1,0:T(8,128)(2,1)S(1)}, u32[]{:S(2)}, u32[]{:S(2)}) collective-permute-start(bf16[256,512]{1,0:T(8,128)(2,1)S(1)} %slice.51), channel_id=1, source_target_pairs={{0,2},{2,4},{4,6},{6,8},{8,10},{10,12},{12,14},{14,16},{16,18},{18... | collective-permute-start | bytes 786440 | tf_op jit(solution)/shard_map/ppermute | solution.py:16
  3.7 9.1 %collective-permute-start.1 = (bf16[256,512]{1,0:T(8,128)(2,1)S(1)}, bf16[256,512]{1,0:T(8,128)(2,1)S(1)}, u32[]{:S(2)}, u32[]{:S(2)}) collective-permute-start(bf16[256,512]{1,0:T(8,128)(2,1)S(1)} %slice.51), channel_id=1, source_target_pairs={{2,0},{4,2},{6,4},{8,6},{10,8},{12,10},{14,12},{16,14},{18,16},{20... | collective-permute-start | bytes 786440 | tf_op jit(solution)/shard_map/ppermute | solution.py:19
  18.4 4.0 %copy-start.5 = (bf16[256,256]{1,0:T(8,128)(2,1)S(1)}, bf16[256,256]{1,0:T(8,128)(2,1)}, u32[]{:S(2)}) copy-start(bf16[256,256]{1,0:T(8,128)(2,1)} %param.15) | copy-start | bytes 393220
  18.4 4.4 %copy-start.8 = (bf16[256,1024]{1,0:T(8,128)(2,1)S(1)}, bf16[256,1024]{1,0:T(8,128)(2,1)}, u32[]{:S(2)}) copy-start(bf16[256,1024]{1,0:T(8,128)(2,1)} %param.16) | copy-start | bytes 1572868
  18.4 5.4 %copy-start.4 = (bf16[256,512]{1,0:T(8,128)(2,1)S(1)}, bf16[256,512]{1,0:T(8,128)(2,1)}, u32[]{:S(2)}) copy-start(bf16[256,512]{1,0:T(8,128)(2,1)} %param.20) | copy-start | bytes 786436
  23.7 6.4 %copy-start.2 = (bf16[256,256]{1,0:T(8,128)(2,1)}, bf16[256,256]{1,0:T(8,128)(2,1)S(1)}, u32[]{:S(2)}) copy-start(bf16[256,256]{1,0:T(8,128)(2,1)S(1)} %copy.50) | copy-start | bytes 393220
  30.1 5.2 %collective-permute-start.3 = (f32[8,512]{1,0:T(8,128)S(1)}, f32[8,512]{1,0:T(8,128)S(1)}, u32[]{:S(2)}, u32[]{:S(2)}) collective-permute-start(f32[8,512]{1,0:T(8,128)S(1)} %get-tuple-element.54), channel_id=1, source_target_pairs={{0,4},{4,0},{8,12},{12,8},{16,20},{20,16},{24,28},{28,24},{1,5},{5... | collective-permute-start | bytes 49160 | tf_op jit(solution)/shard_map/ppermute | solution.py:34
  31.6 4.9 %copy-start.7 = (s32[512]{0:T(512)S(1)}, s32[512]{0:T(512)}, u32[]{:S(2)}) copy-start(s32[512]{0:T(512)} %param.25) | copy-start | bytes 6148
  31.7 4.9 %copy-start.1 = (bf16[512,256]{1,0:T(8,128)(2,1)S(1)}, bf16[512,256]{1,0:T(8,128)(2,1)}, u32[]{:S(2)}) copy-start(bf16[512,256]{1,0:T(8,128)(2,1)} %param.18) | copy-start | bytes 786436
  31.7 33.2 %copy-start.6 = (bf16[256,256]{1,0:T(8,128)(2,1)S(1)}, bf16[256,256]{1,0:T(8,128)(2,1)}, u32[]{:S(2)}) copy-start(bf16[256,256]{1,0:T(8,128)(2,1)} %param.21) | copy-start | bytes 393220
  31.7 33.6 %copy-start.9 = (bf16[256,256]{1,0:T(8,128)(2,1)S(1)}, bf16[256,256]{1,0:T(8,128)(2,1)}, u32[]{:S(2)}) copy-start(bf16[256,256]{1,0:T(8,128)(2,1)} %param.23) | copy-start | bytes 393220
  31.7 33.6 %copy-start.10 = (bf16[256,256]{1,0:T(8,128)(2,1)S(1)}, bf16[256,256]{1,0:T(8,128)(2,1)}, u32[]{:S(2)}) copy-start(bf16[256,256]{1,0:T(8,128)(2,1)} %param.22) | copy-start | bytes 393220
  33.2 10.0 %collective-permute-start.2 = (bf16[512,256]{0,1:T(8,128)(2,1)S(1)}, bf16[512,256]{0,1:T(8,128)(2,1)S(1)}, u32[]{:S(2)}, u32[]{:S(2)}) collective-permute-start(bf16[512,256]{0,1:T(8,128)(2,1)S(1)} %bitcast.98), channel_id=1, source_target_pairs={{0,4},{4,0},{8,12},{12,8},{16,20},{20,16},{24,28},{28,24},{1,5},{5... | collective-permute-start | bytes 786440 | tf_op jit(solution)/shard_map/ppermute | solution.py:34
  35.2 6.9 %collective-permute-start.8 = (f32[8,512]{1,0:T(8,128)S(1)}, f32[8,512]{1,0:T(8,128)S(1)}, u32[]{:S(2)}, u32[]{:S(2)}) collective-permute-start(f32[8,512]{1,0:T(8,128)S(1)} %convert_reduce_fusion), channel_id=1, source_target_pairs={{0,4},{4,0},{8,12},{12,8},{16,20},{20,16},{24,28},{28,24},{1,5},{5... | collective-permute-start | bytes 49160 | tf_op jit(solution)/shard_map/ppermute | solution.py:34
  35.3 6.8 %collective-permute-start.5 = (f32[8,512]{1,0:T(8,128)S(1)}, f32[8,512]{1,0:T(8,128)S(1)}, u32[]{:S(2)}, u32[]{:S(2)}) collective-permute-start(f32[8,512]{1,0:T(8,128)S(1)} %get-tuple-element.30), channel_id=1, source_target_pairs={{0,8},{4,12},{8,0},{12,4},{16,24},{20,28},{24,16},{28,20},{1,9},{5... | collective-permute-start | bytes 49160 | tf_op jit(solution)/shard_map/ppermute | solution.py:34
  42.2 4.4 %collective-permute-start.9 = (f32[8,512]{1,0:T(8,128)S(1)}, f32[8,512]{1,0:T(8,128)S(1)}, u32[]{:S(2)}, u32[]{:S(2)}) collective-permute-start(f32[8,512]{1,0:T(8,128)S(1)} %get-tuple-element.36), channel_id=1, source_target_pairs={{0,8},{4,12},{8,0},{12,4},{16,24},{20,28},{24,16},{28,20},{1,9},{5... | collective-permute-start | bytes 49160 | tf_op jit(solution)/shard_map/ppermute | solution.py:34
  43.4 8.1 %collective-permute-start.4 = (bf16[512,256]{0,1:T(8,128)(2,1)S(1)}, bf16[512,256]{0,1:T(8,128)(2,1)S(1)}, u32[]{:S(2)}, u32[]{:S(2)}) collective-permute-start(bf16[512,256]{0,1:T(8,128)(2,1)S(1)} %fusion.38), channel_id=1, source_target_pairs={{0,8},{4,12},{8,0},{12,4},{16,24},{20,28},{24,16},{28,20},{1,9},{5... | collective-permute-start | bytes 786440 | tf_op jit(solution)/shard_map/ppermute | solution.py:34
  44.5 9.6 %collective-permute-start.7 = (f32[8,512]{1,0:T(8,128)S(1)}, f32[8,512]{1,0:T(8,128)S(1)}, u32[]{:S(2)}, u32[]{:S(2)}) collective-permute-start(f32[8,512]{1,0:T(8,128)S(1)} %get-tuple-element.43), channel_id=1, source_target_pairs={{0,16},{4,20},{8,24},{12,28},{16,0},{20,4},{24,8},{28,12},{1,17},{... | collective-permute-start | bytes 49160 | tf_op jit(solution)/shard_map/ppermute | solution.py:34
  46.6 7.6 %collective-permute-start.10 = (f32[8,512]{1,0:T(8,128)S(1)}, f32[8,512]{1,0:T(8,128)S(1)}, u32[]{:S(2)}, u32[]{:S(2)}) collective-permute-start(f32[8,512]{1,0:T(8,128)S(1)} %get-tuple-element.38), channel_id=1, source_target_pairs={{0,16},{4,20},{8,24},{12,28},{16,0},{20,4},{24,8},{28,12},{1,17},{... | collective-permute-start | bytes 49160 | tf_op jit(solution)/shard_map/ppermute | solution.py:34
  51.6 13.1 %collective-permute-start.6 = (bf16[512,256]{0,1:T(8,128)(2,1)S(1)}, bf16[512,256]{0,1:T(8,128)(2,1)S(1)}, u32[]{:S(2)}, u32[]{:S(2)}) collective-permute-start(bf16[512,256]{0,1:T(8,128)(2,1)S(1)} %fusion.36), channel_id=1, source_target_pairs={{0,16},{4,20},{8,24},{12,28},{16,0},{20,4},{24,8},{28,12},{1,17},{... | collective-permute-start | bytes 786440 | tf_op jit(solution)/shard_map/ppermute | solution.py:34
  65.8 21.3 %copy-start.3 = (bf16[512,256]{1,0:T(8,128)(2,1)}, bf16[512,256]{1,0:T(8,128)(2,1)S(1)}, u32[]{:S(2)}) copy-start(bf16[512,256]{1,0:T(8,128)(2,1)S(1)} %convolution_convert_fusion.2) | copy-start | bytes 786436
  66.5 3.7 %collective-permute-start.11 = (f32[3,512]{1,0:T(4,128)S(1)}, f32[3,512]{1,0:T(4,128)S(1)}, u32[]{:S(2)}, u32[]{:S(2)}) collective-permute-start(f32[3,512]{1,0:T(4,128)S(1)} %pad_maximum_fusion.1), channel_id=1, source_target_pairs={{0,4},{4,0},{8,12},{12,8},{16,20},{20,16},{24,28},{28,24},{1,5},{5... | collective-permute-start | bytes 18440 | tf_op jit(solution)/shard_map/ppermute | solution.py:34
  70.2 3.7 %collective-permute-start.12 = (f32[3,512]{1,0:T(4,128)S(1)}, f32[3,512]{1,0:T(4,128)S(1)}, u32[]{:S(2)}, u32[]{:S(2)}) collective-permute-start(f32[3,512]{1,0:T(4,128)S(1)} %fusion.95), channel_id=1, source_target_pairs={{0,8},{4,12},{8,0},{12,4},{16,24},{20,28},{24,16},{28,20},{1,9},{5... | collective-permute-start | bytes 18440 | tf_op jit(solution)/shard_map/ppermute | solution.py:34
  73.9 4.6 %collective-permute-start.13 = (f32[3,512]{1,0:T(4,128)S(1)}, f32[3,512]{1,0:T(4,128)S(1)}, u32[]{:S(2)}, u32[]{:S(2)}) collective-permute-start(f32[3,512]{1,0:T(4,128)S(1)} %fusion.130), channel_id=1, source_target_pairs={{0,16},{4,20},{8,24},{12,28},{16,0},{20,4},{24,8},{28,12},{1,17},{... | collective-permute-start | bytes 18440 | tf_op jit(solution)/shard_map/ppermute | solution.py:34
  80.1 6.4 %collective-permute-start.15 = (bf16[512,256]{1,0:T(8,128)(2,1)S(1)}, bf16[512,256]{1,0:T(8,128)(2,1)S(1)}, u32[]{:S(2)}, u32[]{:S(2)}) collective-permute-start(bf16[512,256]{1,0:T(8,128)(2,1)S(1)} %convolution_convert_fusion.1), channel_id=1, source_target_pairs={{0,4},{4,0},{8,12},{12,8},{16,20},{20,16},{24,28},{28,24},{1,5},{5... | collective-permute-start | bytes 786440 | tf_op jit(solution)/shard_map/ppermute | solution.py:55
  86.6 8.3 %collective-permute-start.16 = (bf16[512,256]{1,0:T(8,128)(2,1)S(1)}, bf16[512,256]{1,0:T(8,128)(2,1)S(1)}, u32[]{:S(2)}, u32[]{:S(2)}) collective-permute-start(bf16[512,256]{1,0:T(8,128)(2,1)S(1)} %add_convert_fusion.1), channel_id=1, source_target_pairs={{0,8},{4,12},{8,0},{12,4},{16,24},{20,28},{24,16},{28,20},{1,9},{5... | collective-permute-start | bytes 786440 | tf_op jit(solution)/shard_map/ppermute | solution.py:55
  87.0 8.0 %collective-permute-start.14 = (f32[256,256]{1,0:T(8,128)S(1)}, f32[256,256]{1,0:T(8,128)S(1)}, u32[]{:S(2)}, u32[]{:S(2)}) collective-permute-start(f32[256,256]{1,0:T(8,128)S(1)} %slice_select_fusion), channel_id=1, source_target_pairs={{0,2},{2,0},{1,3},{3,1},{4,6},{6,4},{5,7},{7,5},{8,10},{10,8},{9,1... | collective-permute-start | bytes 786440 | tf_op jit(solution)/shard_map/ppermute | solution.py:87
  94.9 9.1 %collective-permute-start.17 = (bf16[512,256]{1,0:T(8,128)(2,1)S(1)}, bf16[512,256]{1,0:T(8,128)(2,1)S(1)}, u32[]{:S(2)}, u32[]{:S(2)}) collective-permute-start(bf16[512,256]{1,0:T(8,128)(2,1)S(1)} %add_convert_fusion), channel_id=1, source_target_pairs={{0,16},{4,20},{8,24},{12,28},{16,0},{20,4},{24,8},{28,12},{1,17},{... | collective-permute-start | bytes 786440 | tf_op jit(solution)/shard_map/ppermute | solution.py:55

commit v8 on v7

--- a/solution.py
+++ b/solution.py
@@ -25,11 +25,10 @@
     return [(i, i ^ distance) for i in range(count)]
 
 
-def butterfly(tree, axis, combine, ordered=False):
+def butterfly(tree, axis, combine, ordered=False, distance=1):
     count = lax.axis_size(axis)
     assert count & (count - 1) == 0
     index = lax.axis_index(axis)
-    distance = 1
     while distance < count:
         other = lax.ppermute(tree, axis, partner_pairs(count, distance))
         if ordered:
@@ -47,9 +46,8 @@
     return jax.tree.map(jnp.add, a, b)
 
 
-def narrow_butterfly(block, axis):
+def narrow_butterfly(block, axis, distance=1):
     count = lax.axis_size(axis)
-    distance = 1
     while distance < count:
         sent = block.astype(jnp.bfloat16)
         other = lax.ppermute(sent, axis, partner_pairs(count, distance))
@@ -239,13 +237,26 @@
     mask_embed = jnp.dot(mask_hidden, mask_second, preferred_element_type=jnp.float32).astype(
         jnp.bfloat16
     )
+    pair_upper = lax.axis_index("phi") % 2 == 1
+    own_payload = gathered[:, 2 * model_width :]
+    other_payload = lax.ppermute(
+        own_payload, "phi", partner_pairs(lax.axis_size("phi"), 1)
+    )
+    pair_payload = jnp.where(
+        pair_upper,
+        jnp.concatenate([other_payload, own_payload]),
+        jnp.concatenate([own_payload, other_payload]),
+    )
+    pair_hits = pair_payload[:, :model_width]
+    pair_digits = pair_payload[:, model_width:].astype(jnp.int32)
+    pair_truth = pair_digits[:, 0] * 256 + pair_digits[:, 1] - 1
     logits = lax.dot_general(
-        mask_embed, group_hits, (((1,), (1,)), ((), ())), preferred_element_type=jnp.float32
+        mask_embed, pair_hits, (((1,), (1,)), ((), ())), preferred_element_type=jnp.float32
     ) * model_width ** (-0.5)
     sigma = jax.nn.sigmoid(logits)
     matched_flag = match < track_count
     matched = matched_flag.astype(jnp.float32)
-    target = jnp.logical_and(match[:, None] == group_truth[None, :], matched_flag[:, None]).astype(
+    target = jnp.logical_and(match[:, None] == pair_truth[None, :], matched_flag[:, None]).astype(
         jnp.float32
     )
     intersection, predicted, truth_count = butterfly(
@@ -254,17 +265,20 @@
         ),
         "phi",
         add_trees,
+        distance=2,
     )
     mask_fill = predicted / hits_total
     coef = loss_coefficients(
         sigma, target, matched, intersection, predicted, truth_count, hits_total, model_width
     )
     mask_grad = narrow_butterfly(
-        jnp.dot(coef, group_hits, preferred_element_type=jnp.float32), "phi"
-    )
+        jnp.dot(coef, pair_hits, preferred_element_type=jnp.float32), "phi", distance=2
+    )
+    group_count = group_hits.shape[0]
+    own_coef = jnp.where(pair_upper, coef[:, group_count:], coef[:, :group_count])
     hit_grad = reduce_scatter_rows(
         lax.dot_general(
-            coef, mask_embed, (((0,), (0,)), ((), ())), preferred_element_type=jnp.float32
+            own_coef, mask_embed, (((0,), (0,)), ((), ())), preferred_element_type=jnp.float32
         ),
         "query",
     )

time: 105 us -> 104 us (level)
  waiting for transfers between devices: 52 us -> 42.1 us
  matrix products: 17.8 us -> 22.6 us
  local copies, waits for them, and re-layouts: 2.38 us -> 4.1 us
  other arithmetic: 6.42 us -> 7.95 us
    ppermute x3 -> x2, waiting for transfers between devices: 21.1 us -> 13.7 us  [narrow_butterfly(): other = lax.ppermute(sent, axis, partner_pairs(count, distance))]
    ppermute x12 -> x11, waiting for transfers between devices: 29.2 us -> 25 us  [butterfly(): other = lax.ppermute(tree, axis, partner_pairs(count, distance))]
    dot_general x1, matrix products: 1.51 us -> 4.9 us  [body(): jnp.einsum('hqk,khd->qhd', raised, value_heads, preferred_element_type=jn...]
    dot_general x3, matrix products: 1.31 us -> 3.02 us  [the longest x1 2.21 us: body(): lax.dot_general(mask_embed, pair_hits, (((1,), (1,)), ((), ())), preferre...]
    unnamed x25 -> x31, local copies, waits for them, and re-layouts: 1.38 us -> 3.07 us
    ppermute x1, waiting for transfers between devices: 1.74 us -> 3.37 us  [extended_2(): lax.ppermute(lax.slice_in_dim(block, block.shape[dim] - width, None, axis...]
    ppermute x12 -> x11, starting transfers between devices: 13.7 us -> 12.1 us  [butterfly(): other = lax.ppermute(tree, axis, partner_pairs(count, distance))]
    ppermute x0 -> x1, starting transfers between devices: none -> 1.49 us  [body(): lax.ppermute(own_payload, 'phi', partner_pairs(lax.axis_size('phi'), 1))]
  transfers between devices with their start and end apart: 18 -> 17, of which waited for: 10 -> 11; matrix products, arithmetic and copies ran while one was open for 7% -> 10% of each run, Pallas kernels for 0% -> 0%
where the time goes in v8:
time: 104 us
  waiting for transfers between devices  42.1 us (40%)
  matrix products  22.6 us (22%)
  starting transfers between devices  21.3 us (20%)
  other arithmetic  7.95 us (8%)
  blocking collectives  4.35 us (4%)
  local copies, waits for them, and re-layouts  4.1 us (4%)
  between operations  1.16 us (1%)
    ppermute x11, waiting for transfers between devices, butterfly(): other = lax.ppermute(tree, axis, partner_pairs(count, distance))  25 us
    ppermute x2, waiting for transfers between devices, narrow_butterfly(): other = lax.ppermute(sent, axis, partner_pairs(count, distance))  13.7 us
    ppermute x11, starting transfers between devices, butterfly(): other = lax.ppermute(tree, axis, partner_pairs(count, distance))  12.1 us
    sub x1, matrix products, window_attend(): raised = jnp.exp(scores - jnp.max(scores, axis=-1, keepdims=True))  5.11 us
    ppermute x1, starting transfers between devices, extended_2(): lax.ppermute(lax.slice_in_dim(block, 0, width, axis=dim), axis, backward)  5.03 us
    dot_general x1, matrix products, body(): jnp.einsum('hqk,khd->qhd', raised, value_heads, preferred_element_type=jn...  4.9 us
    all_gather x1, blocking collectives, body(): lax.all_gather(jnp.concatenate([local_kv, encoded, digits], axis=1), 'que...  4.35 us
    dot_general x1, matrix products, window_attend(): jnp.einsum('hqk,khd->qhd', weights, value_heads, preferred_element_type=j...  3.96 us
  transfers between devices with their start and end apart: 17, of which 11 were waited for; matrix products, arithmetic and copies ran while one was open for 10% of the time, Pallas kernels for 0%

profile of v8, /device:TPU:0, one launch (start us, length us, event | category | flops | bytes accessed | tf_op | source)
XLA Modules:
  0.0 103.6 jit_solution(16827353307084197338)
XLA Ops:
  0.7 1.1 %copy.40 = bf16[256,256]{0,1:T(8,128)(2,1)S(1)} copy(bf16[256,256]{1,0:T(8,128)(2,1)} %param.13) | data formatting | bytes 262144 | tf_op args[0]
  1.9 1.3 %convolution_convert_fusion = bf16[256,768]{1,0:T(8,128)(2,1)S(1)} fusion(bf16[256,768]{1,0:T(8,128)(2,1)} %param.14, bf16[256,256]{0,1:T(8,128)(2,1)S(1)} %copy.40, f32[256]{0:T(256)S(1)} %add_rsqrt_fusion.3, f32[256]{0:T(256)S(1)} %broadcast_multiply_fusion.3), kind=kOutput, calls=%fused_computation.22 | convolution fusion | flops 101122048 | bytes 919552 | tf_op jit(solution)/shard_map/dot_general | solution.py:176
  3.7 5.0 %collective-permute-start.1 = (bf16[256,512]{1,0:T(8,128)(2,1)S(1)}, bf16[256,512]{1,0:T(8,128)(2,1)S(1)}, u32[]{:S(2)}, u32[]{:S(2)}) collective-permute-start(bf16[256,512]{1,0:T(8,128)(2,1)S(1)} %slice.63), channel_id=1, source_target_pairs={{2,0},{4,2},{6,4},{8,6},{10,8},{12,10},{14,12},{16,14},{18,16},{20... | collective-permute-start | bytes 786440 | tf_op jit(solution)/shard_map/ppermute | solution.py:19
  9.5 3.4 %collective-permute-done = bf16[256,512]{1,0:T(8,128)(2,1)S(1)} collective-permute-done((bf16[256,512]{1,0:T(8,128)(2,1)S(1)}, bf16[256,512]{1,0:T(8,128)(2,1)S(1)}, u32[]{:S(2)}, u32[]{:S(2)}) %collective-permute-start) | collective-permute-done | bytes 262176 | tf_op jit(solution)/shard_map/ppermute | solution.py:16
  13.3 5.1 %fusion.101 = (f32[8,256]{1,0:T(8,128)S(1)}, f32[8,256,768]{2,1,0:T(8,128)}) fusion(pred[256,768]{1,0:T(8,128)(4,1)S(1)} %fusion.24, bf16[256,8,32]{0,2,1:T(8,128)(2,1)S(1)} %bitcast.101, bf16[768,8,32]{0,2,1:T(8,128)(2,1)S(1)} %bitcast.98), kind=kOutput, calls=%fused_computation.176 | convolution fusion | flops 106955520 | bytes 7020544 | tf_op jit(solution)/shard_map/sub | solution.py:113
  18.5 4.0 %fusion.12 = bf16[8,32,256]{2,1,0:T(8,128)(2,1)S(1)} fusion(bf16[768,8,32]{0,2,1:T(8,128)(2,1)S(1)} %bitcast.99, f32[8,256,768]{2,1,0:T(8,128)} %get-tuple-element.49, f32[8,256]{1,0:T(8,128)S(1)} %get-tuple-element.48), kind=kOutput, calls=%fused_computation.34 | convolution fusion | flops 103874560 | bytes 6823936 | tf_op jit(solution)/shard_map/hqk,khd->qhd/dot_general | solution.py:115
  22.8 0.8 convert_reduce_fusion.3
  24.2 4.3 %all_gather.3 = bf16[512,896]{1,0:T(8,128)(2,1)S(1)} all-gather(bf16[256,896]{1,0:T(8,128)(2,1)S(1)} %fusion.46), channel_id=1, replica_groups=mesh['phi'=8,'query'=2,'event'=2] {'query'}, dimensions={0}, use_global_device_ids=true | all-gather | bytes 1376256 | tf_op jit(solution)/shard_map/all_gather | solution.py:197
  28.7 1.3 %multiply_reduce_fusion = (f32[8,512]{1,0:T(8,128)S(1)}, f32[8,512,512]{1,2,0:T(8,128)S(1)}) fusion(bf16[512,8,32]{0,2,1:T(8,128)(2,1)S(1)} %bitcast.94, bf16[512,8,32]{0,2,1:T(8,128)(2,1)S(1)} %bitcast.96), kind=kOutput, calls=%fused_computation.3 | convolution fusion | flops 138407936 | bytes 8929280 | tf_op jit(solution)/shard_map/qhd,khd->hqk/dot_general | solution.py:210
  30.2 1.4 %convert_reduce_fusion = f32[8,512]{1,0:T(8,128)S(1)} fusion(f32[8,512]{1,0:T(8,128)S(1)} %get-tuple-element.54, f32[8,512,512]{1,2,0:T(8,128)S(1)} %get-tuple-element.55), kind=kLoop, calls=%fused_computation.1 | loop fusion | flops 10481664 | bytes 8421376 | tf_op jit(solution)/shard_map/reduce_sum | solution.py:215
  31.6 1.7 %copy-done.1 = f32[8,512,512]{1,2,0:T(8,128)} copy-done((f32[8,512,512]{1,2,0:T(8,128)}, f32[8,512,512]{1,2,0:T(8,128)S(1)}, u32[]{:S(2)}) %copy-start.1) | copy-done | bytes 8388632
  33.8 0.8 collective-permute-start.5
  34.6 1.5 %collective-permute-start.11 = (bf16[512,384]{1,0:T(8,128)(2,1)S(1)}, bf16[512,384]{1,0:T(8,128)(2,1)}, u32[]{:S(2)}, u32[]{:S(2)}) collective-permute-start(bf16[512,384]{1,0:T(8,128)(2,1)S(1)} %slice.69), channel_id=1, source_target_pairs={{0,4},{4,0},{8,12},{12,8},{16,20},{20,16},{24,28},{28,24},{1,5},{5... | collective-permute-start | bytes 1179656 | tf_op jit(solution)/shard_map/ppermute | solution.py:242
  38.4 4.9 %convolution_convert_fusion.3 = bf16[8,32,512]{2,1,0:T(8,128)(2,1)S(1)} fusion(bf16[512,8,32]{0,2,1:T(8,128)(2,1)S(1)} %bitcast.95, f32[8,512,512]{1,2,0:T(8,128)} %copy-done.1, f32[8,512]{1,0:T(8,128)S(1)} %get-tuple-element.54), kind=kOutput, calls=%fused_computation.27 | convolution fusion | flops 140640256 | bytes 8929280 | tf_op jit(solution)/shard_map/hqk,khd->qhd/dot_general | solution.py:216
  43.3 1.5 %collective-permute-start.2 = (bf16[512,256]{0,1:T(8,128)(2,1)S(1)}, bf16[512,256]{0,1:T(8,128)(2,1)S(1)}, u32[]{:S(2)}, u32[]{:S(2)}) collective-permute-start(bf16[512,256]{0,1:T(8,128)(2,1)S(1)} %bitcast.97), channel_id=1, source_target_pairs={{0,4},{4,0},{8,12},{12,8},{16,20},{20,16},{24,28},{28,24},{1,5},{5... | collective-permute-start | bytes 786440 | tf_op jit(solution)/shard_map/ppermute | solution.py:33
  44.8 2.6 %collective-permute-start.7 = (f32[8,512]{1,0:T(8,128)S(1)}, f32[8,512]{1,0:T(8,128)S(1)}, u32[]{:S(2)}, u32[]{:S(2)}) collective-permute-start(f32[8,512]{1,0:T(8,128)S(1)} %get-tuple-element.43), channel_id=1, source_target_pairs={{0,16},{4,20},{8,24},{12,28},{16,0},{20,4},{24,8},{28,12},{1,17},{... | collective-permute-start | bytes 49160 | tf_op jit(solution)/shard_map/ppermute | solution.py:33
  48.0 3.1 %collective-permute-done.2 = bf16[512,256]{0,1:T(8,128)(2,1)S(1)} collective-permute-done((bf16[512,256]{0,1:T(8,128)(2,1)S(1)}, bf16[512,256]{0,1:T(8,128)(2,1)S(1)}, u32[]{:S(2)}, u32[]{:S(2)}) %collective-permute-start.2) | collective-permute-done | bytes 262176 | tf_op jit(solution)/shard_map/ppermute | solution.py:33
  51.3 1.1 %collective-permute-start.4 = (bf16[512,256]{0,1:T(8,128)(2,1)S(1)}, bf16[512,256]{0,1:T(8,128)(2,1)S(1)}, u32[]{:S(2)}, u32[]{:S(2)}) collective-permute-start(bf16[512,256]{0,1:T(8,128)(2,1)S(1)} %fusion.38), channel_id=1, source_target_pairs={{0,8},{4,12},{8,0},{12,4},{16,24},{20,28},{24,16},{28,20},{1,9},{5... | collective-permute-start | bytes 786440 | tf_op jit(solution)/shard_map/ppermute | solution.py:33
  52.4 1.4 %maximum_select_fusion = bf16[1024,384]{1,0:T(8,128)(2,1)S(1)} fusion(bf16[512,384]{1,0:T(8,128)(2,1)S(1)} %slice.69, bf16[512,384]{1,0:T(8,128)(2,1)} %collective-permute-done.11, pred[]{:T(512)S(6)} %eq.36), kind=kLoop, calls=%fused_computation.46 | loop fusion | flops 3538944 | bytes 1572865 | tf_op jit(solution)/shard_map/jit(_where)/select_n | solution.py:245
  53.8 4.4 %collective-permute-done.4 = bf16[512,256]{0,1:T(8,128)(2,1)S(1)} collective-permute-done((bf16[512,256]{0,1:T(8,128)(2,1)S(1)}, bf16[512,256]{0,1:T(8,128)(2,1)S(1)}, u32[]{:S(2)}, u32[]{:S(2)}) %collective-permute-start.4) | collective-permute-done | bytes 262176 | tf_op jit(solution)/shard_map/ppermute | solution.py:33
  58.4 3.0 %collective-permute-start.6 = (bf16[512,256]{0,1:T(8,128)(2,1)S(1)}, bf16[512,256]{0,1:T(8,128)(2,1)S(1)}, u32[]{:S(2)}, u32[]{:S(2)}) collective-permute-start(bf16[512,256]{0,1:T(8,128)(2,1)S(1)} %fusion.36), channel_id=1, source_target_pairs={{0,16},{4,20},{8,24},{12,28},{16,0},{20,4},{24,8},{28,12},{1,17},{... | collective-permute-start | bytes 786440 | tf_op jit(solution)/shard_map/ppermute | solution.py:33
  61.8 9.0 %collective-permute-done.6 = bf16[512,256]{0,1:T(8,128)(2,1)S(1)} collective-permute-done((bf16[512,256]{0,1:T(8,128)(2,1)S(1)}, bf16[512,256]{0,1:T(8,128)(2,1)S(1)}, u32[]{:S(2)}, u32[]{:S(2)}) %collective-permute-start.6) | collective-permute-done | bytes 262176 | tf_op jit(solution)/shard_map/ppermute | solution.py:33
  71.4 1.1 %convolution_convert_fusion.2 = bf16[512,256]{1,0:T(8,128)(2,1)} fusion(bf16[256,256]{1,0:T(8,128)(2,1)S(1)} %copy-done.11, bf16[256,256]{1,0:T(8,128)(2,1)S(1)} %copy-done.12, f32[512,256]{0,1:T(8,128)S(1)} %get-tuple-element.57, f32[512]{0:T(512)S(1)} %add_rsqrt_fusion, f32[512]{0:T(512)S(1)} %broadcast_multiply_fusion), kind=kOutput, calls=%fused_computation.26 | convolution fusion | flops 135004160 | bytes 1052672 | tf_op jit(solution)/shard_map/dot_general | solution.py:237
  72.6 2.2 %select_reduce_fusion = (f32[512]{0:T(512)S(1)}, f32[512]{0:T(512)S(1)}, f32[512]{0:T(512)S(1)}, f32[512,1024]{1,0:T(8,128)S(1)}) fusion(s32[1024]{0:T(1024)S(1)} %fusion.31, s32[512]{0:T(512)S(1)} %copy-done.8, pred[512]{0:T(512)(128)(4,1)S(1)} %get-tuple-element.24, bf16[512,256]{1,0:T(8,128)(2,1)} %convolution_convert_fusion.2, ...), kind=kOutput, calls=%fused_computation.18 | convolution fusion | flops 274201088 | bytes 2896384 | tf_op jit(solution)/shard_map/dot_general | solution.py:253
  74.9 3.6 %collective-permute-done.12 = f32[3,512]{1,0:T(4,128)S(1)} collective-permute-done((f32[3,512]{1,0:T(4,128)S(1)}, f32[3,512]{1,0:T(4,128)S(1)}, u32[]{:S(2)}, u32[]{:S(2)}) %collective-permute-start.12) | collective-permute-done | bytes 6176 | tf_op jit(solution)/shard_map/ppermute | solution.py:33
  78.5 1.4 %collective-permute-start.13 = (f32[3,512]{1,0:T(4,128)S(1)}, f32[3,512]{1,0:T(4,128)S(1)}, u32[]{:S(2)}, u32[]{:S(2)}) collective-permute-start(f32[3,512]{1,0:T(4,128)S(1)} %fusion.94), channel_id=1, source_target_pairs={{0,16},{4,20},{8,24},{12,28},{16,0},{20,4},{24,8},{28,12},{1,17},{... | collective-permute-start | bytes 18440 | tf_op jit(solution)/shard_map/ppermute | solution.py:33
  79.9 3.2 %collective-permute-done.13 = f32[3,512]{1,0:T(4,128)S(1)} collective-permute-done((f32[3,512]{1,0:T(4,128)S(1)}, f32[3,512]{1,0:T(4,128)S(1)}, u32[]{:S(2)}, u32[]{:S(2)}) %collective-permute-start.13) | collective-permute-done | bytes 6176 | tf_op jit(solution)/shard_map/ppermute | solution.py:33
  83.8 1.4 %fusion.9 = bf16[512,1024]{1,0:T(8,128)(2,1)S(1)} fusion(f32[512,1024]{1,0:T(8,128)S(1)} %get-tuple-element.58, f32[512]{0:T(512)S(1)} %bitcast.111, f32[512]{0:T(512)S(1)} %bitcast.112, s32[1024]{0:T(1024)S(1)} %fusion.31, f32[512]{0:T(512)S(1)} %get-tuple-element.23, s32[512]{0:T(512)S(1)} %copy-done.8, pred[512]{0:T(512)(128)(4,1)S(1)} %get-tuple-element.24), kind=kLoop, calls=%fused_computation.17 | loop fusion | flops 7340032 | bytes 3158528 | tf_op jit(solution)/shard_map/convert_element_type | solution.py:150
  86.6 6.2 %collective-permute-done.15 = bf16[512,256]{1,0:T(8,128)(2,1)S(1)} collective-permute-done((bf16[512,256]{1,0:T(8,128)(2,1)S(1)}, bf16[512,256]{1,0:T(8,128)(2,1)S(1)}, u32[]{:S(2)}, u32[]{:S(2)}) %collective-permute-start.15) | collective-permute-done | bytes 262176 | tf_op jit(solution)/shard_map/ppermute | solution.py:53
  92.8 1.6 %collective-permute-start.16 = (bf16[512,256]{1,0:T(8,128)(2,1)S(1)}, bf16[512,256]{1,0:T(8,128)(2,1)S(1)}, u32[]{:S(2)}, u32[]{:S(2)}) collective-permute-start(bf16[512,256]{1,0:T(8,128)(2,1)S(1)} %add_convert_fusion), channel_id=1, source_target_pairs={{0,16},{4,20},{8,24},{12,28},{16,0},{20,4},{24,8},{28,12},{1,17},{... | collective-permute-start | bytes 786440 | tf_op jit(solution)/shard_map/ppermute | solution.py:53
  95.2 7.6 %collective-permute-done.16 = bf16[512,256]{1,0:T(8,128)(2,1)S(1)} collective-permute-done((bf16[512,256]{1,0:T(8,128)(2,1)S(1)}, bf16[512,256]{1,0:T(8,128)(2,1)S(1)}, u32[]{:S(2)}, u32[]{:S(2)}) %collective-permute-start.16) | collective-permute-done | bytes 262176 | tf_op jit(solution)/shard_map/ppermute | solution.py:53
  102.8 0.8 convert_add_fusion
  (101 shorter events, 10.7 us)
Async XLA Ops:
  0.6 22.2 %copy-start = (bf16[1024,256]{1,0:T(8,128)(2,1)S(1)}, bf16[1024,256]{1,0:T(8,128)(2,1)}, u32[]{:S(2)}) copy-start(bf16[1024,256]{1,0:T(8,128)(2,1)} %param.17) | copy-start | bytes 1572868
  0.6 8.2 %copy-start.9 = (s32[256]{0:T(256)S(1)}, s32[256]{0:T(256)}, u32[]{:S(2)}) copy-start(s32[256]{0:T(256)} %param.24) | copy-start | bytes 3076
  0.7 8.6 %copy-start.2 = (bf16[512,256]{1,0:T(8,128)(2,1)S(1)}, bf16[512,256]{1,0:T(8,128)(2,1)}, u32[]{:S(2)}) copy-start(bf16[512,256]{1,0:T(8,128)(2,1)} %param.18) | copy-start | bytes 786436
  0.7 8.6 %copy-start.5 = (bf16[256,256]{1,0:T(8,128)(2,1)S(1)}, bf16[256,256]{1,0:T(8,128)(2,1)}, u32[]{:S(2)}) copy-start(bf16[256,256]{1,0:T(8,128)(2,1)} %param.19) | copy-start | bytes 393220
  3.2 9.6 %collective-permute-start = (bf16[256,512]{1,0:T(8,128)(2,1)S(1)}, bf16[256,512]{1,0:T(8,128)(2,1)S(1)}, u32[]{:S(2)}, u32[]{:S(2)}) collective-permute-start(bf16[256,512]{1,0:T(8,128)(2,1)S(1)} %slice.63), channel_id=1, source_target_pairs={{0,2},{2,4},{4,6},{6,8},{8,10},{10,12},{12,14},{14,16},{16,18},{18... | collective-permute-start | bytes 786440 | tf_op jit(solution)/shard_map/ppermute | solution.py:16
  3.7 9.1 %collective-permute-start.1 = (bf16[256,512]{1,0:T(8,128)(2,1)S(1)}, bf16[256,512]{1,0:T(8,128)(2,1)S(1)}, u32[]{:S(2)}, u32[]{:S(2)}) collective-permute-start(bf16[256,512]{1,0:T(8,128)(2,1)S(1)} %slice.63), channel_id=1, source_target_pairs={{2,0},{4,2},{6,4},{8,6},{10,8},{12,10},{14,12},{16,14},{18,16},{20... | collective-permute-start | bytes 786440 | tf_op jit(solution)/shard_map/ppermute | solution.py:19
  18.5 4.0 %copy-start.6 = (bf16[256,256]{1,0:T(8,128)(2,1)S(1)}, bf16[256,256]{1,0:T(8,128)(2,1)}, u32[]{:S(2)}) copy-start(bf16[256,256]{1,0:T(8,128)(2,1)} %param.15) | copy-start | bytes 393220
  18.5 4.3 %copy-start.10 = (bf16[256,1024]{1,0:T(8,128)(2,1)S(1)}, bf16[256,1024]{1,0:T(8,128)(2,1)}, u32[]{:S(2)}) copy-start(bf16[256,1024]{1,0:T(8,128)(2,1)} %param.16) | copy-start | bytes 1572868
  22.8 1.1 %copy-start.4 = (bf16[256,512]{1,0:T(8,128)(2,1)S(1)}, bf16[256,512]{1,0:T(8,128)(2,1)}, u32[]{:S(2)}) copy-start(bf16[256,512]{1,0:T(8,128)(2,1)} %param.20) | copy-start | bytes 786436
  23.8 4.9 %copy-start.3 = (bf16[256,256]{1,0:T(8,128)(2,1)}, bf16[256,256]{1,0:T(8,128)(2,1)S(1)}, u32[]{:S(2)}) copy-start(bf16[256,256]{1,0:T(8,128)(2,1)S(1)} %copy.50) | copy-start | bytes 393220
  30.0 3.2 %copy-start.1 = (f32[8,512,512]{1,2,0:T(8,128)}, f32[8,512,512]{1,2,0:T(8,128)S(1)}, u32[]{:S(2)}) copy-start(f32[8,512,512]{1,2,0:T(8,128)S(1)} %get-tuple-element.55) | copy-start | bytes 25165828
  30.0 3.8 %collective-permute-start.3 = (f32[8,512]{1,0:T(8,128)S(1)}, f32[8,512]{1,0:T(8,128)S(1)}, u32[]{:S(2)}, u32[]{:S(2)}) collective-permute-start(f32[8,512]{1,0:T(8,128)S(1)} %get-tuple-element.54), channel_id=1, source_target_pairs={{0,4},{4,0},{8,12},{12,8},{16,20},{20,16},{24,28},{28,24},{1,5},{5... | collective-permute-start | bytes 49160 | tf_op jit(solution)/shard_map/ppermute | solution.py:33
  33.2 3.8 %collective-permute-start.8 = (f32[8,512]{1,0:T(8,128)S(1)}, f32[8,512]{1,0:T(8,128)S(1)}, u32[]{:S(2)}, u32[]{:S(2)}) collective-permute-start(f32[8,512]{1,0:T(8,128)S(1)} %convert_reduce_fusion), channel_id=1, source_target_pairs={{0,4},{4,0},{8,12},{12,8},{16,20},{20,16},{24,28},{28,24},{1,5},{5... | collective-permute-start | bytes 49160 | tf_op jit(solution)/shard_map/ppermute | solution.py:33
  33.8 3.8 %collective-permute-start.5 = (f32[8,512]{1,0:T(8,128)S(1)}, f32[8,512]{1,0:T(8,128)S(1)}, u32[]{:S(2)}, u32[]{:S(2)}) collective-permute-start(f32[8,512]{1,0:T(8,128)S(1)} %get-tuple-element.30), channel_id=1, source_target_pairs={{0,8},{4,12},{8,0},{12,4},{16,24},{20,28},{24,16},{28,20},{1,9},{5... | collective-permute-start | bytes 49160 | tf_op jit(solution)/shard_map/ppermute | solution.py:33
  34.6 17.8 %collective-permute-start.11 = (bf16[512,384]{1,0:T(8,128)(2,1)S(1)}, bf16[512,384]{1,0:T(8,128)(2,1)}, u32[]{:S(2)}, u32[]{:S(2)}) collective-permute-start(bf16[512,384]{1,0:T(8,128)(2,1)S(1)} %slice.69), channel_id=1, source_target_pairs={{0,4},{4,0},{8,12},{12,8},{16,20},{20,16},{24,28},{28,24},{1,5},{5... | collective-permute-start | bytes 1179656 | tf_op jit(solution)/shard_map/ppermute | solution.py:242
  37.7 9.7 %collective-permute-start.9 = (f32[8,512]{1,0:T(8,128)S(1)}, f32[8,512]{1,0:T(8,128)S(1)}, u32[]{:S(2)}, u32[]{:S(2)}) collective-permute-start(f32[8,512]{1,0:T(8,128)S(1)} %get-tuple-element.36), channel_id=1, source_target_pairs={{0,8},{4,12},{8,0},{12,4},{16,24},{20,28},{24,16},{28,20},{1,9},{5... | collective-permute-start | bytes 49160 | tf_op jit(solution)/shard_map/ppermute | solution.py:33
  38.4 9.4 %copy-start.8 = (s32[512]{0:T(512)S(1)}, s32[512]{0:T(512)}, u32[]{:S(2)}) copy-start(s32[512]{0:T(512)} %param.25) | copy-start | bytes 6148
  43.3 7.8 %collective-permute-start.2 = (bf16[512,256]{0,1:T(8,128)(2,1)S(1)}, bf16[512,256]{0,1:T(8,128)(2,1)S(1)}, u32[]{:S(2)}, u32[]{:S(2)}) collective-permute-start(bf16[512,256]{0,1:T(8,128)(2,1)S(1)} %bitcast.97), channel_id=1, source_target_pairs={{0,4},{4,0},{8,12},{12,8},{16,20},{20,16},{24,28},{28,24},{1,5},{5... | collective-permute-start | bytes 786440 | tf_op jit(solution)/shard_map/ppermute | solution.py:33
  44.8 7.6 %collective-permute-start.7 = (f32[8,512]{1,0:T(8,128)S(1)}, f32[8,512]{1,0:T(8,128)S(1)}, u32[]{:S(2)}, u32[]{:S(2)}) collective-permute-start(f32[8,512]{1,0:T(8,128)S(1)} %get-tuple-element.43), channel_id=1, source_target_pairs={{0,16},{4,20},{8,24},{12,28},{16,0},{20,4},{24,8},{28,12},{1,17},{... | collective-permute-start | bytes 49160 | tf_op jit(solution)/shard_map/ppermute | solution.py:33
  47.4 5.0 %collective-permute-start.10 = (f32[8,512]{1,0:T(8,128)S(1)}, f32[8,512]{1,0:T(8,128)S(1)}, u32[]{:S(2)}, u32[]{:S(2)}) collective-permute-start(f32[8,512]{1,0:T(8,128)S(1)} %get-tuple-element.38), channel_id=1, source_target_pairs={{0,16},{4,20},{8,24},{12,28},{16,0},{20,4},{24,8},{28,12},{1,17},{... | collective-permute-start | bytes 49160 | tf_op jit(solution)/shard_map/ppermute | solution.py:33
  51.3 6.9 %collective-permute-start.4 = (bf16[512,256]{0,1:T(8,128)(2,1)S(1)}, bf16[512,256]{0,1:T(8,128)(2,1)S(1)}, u32[]{:S(2)}, u32[]{:S(2)}) collective-permute-start(bf16[512,256]{0,1:T(8,128)(2,1)S(1)} %fusion.38), channel_id=1, source_target_pairs={{0,8},{4,12},{8,0},{12,4},{16,24},{20,28},{24,16},{28,20},{1,9},{5... | collective-permute-start | bytes 786440 | tf_op jit(solution)/shard_map/ppermute | solution.py:33
  53.8 17.2 %copy-start.7 = (bf16[256,256]{1,0:T(8,128)(2,1)S(1)}, bf16[256,256]{1,0:T(8,128)(2,1)}, u32[]{:S(2)}) copy-start(bf16[256,256]{1,0:T(8,128)(2,1)} %param.21) | copy-start | bytes 393220
  58.3 13.1 %copy-start.11 = (bf16[256,256]{1,0:T(8,128)(2,1)S(1)}, bf16[256,256]{1,0:T(8,128)(2,1)}, u32[]{:S(2)}) copy-start(bf16[256,256]{1,0:T(8,128)(2,1)} %param.23) | copy-start | bytes 393220
  58.3 13.1 %copy-start.12 = (bf16[256,256]{1,0:T(8,128)(2,1)S(1)}, bf16[256,256]{1,0:T(8,128)(2,1)}, u32[]{:S(2)}) copy-start(bf16[256,256]{1,0:T(8,128)(2,1)} %param.22) | copy-start | bytes 393220
  58.4 12.5 %collective-permute-start.6 = (bf16[512,256]{0,1:T(8,128)(2,1)S(1)}, bf16[512,256]{0,1:T(8,128)(2,1)S(1)}, u32[]{:S(2)}, u32[]{:S(2)}) collective-permute-start(bf16[512,256]{0,1:T(8,128)(2,1)S(1)} %fusion.36), channel_id=1, source_target_pairs={{0,16},{4,20},{8,24},{12,28},{16,0},{20,4},{24,8},{28,12},{1,17},{... | collective-permute-start | bytes 786440 | tf_op jit(solution)/shard_map/ppermute | solution.py:33
  74.8 3.7 %collective-permute-start.12 = (f32[3,512]{1,0:T(4,128)S(1)}, f32[3,512]{1,0:T(4,128)S(1)}, u32[]{:S(2)}, u32[]{:S(2)}) collective-permute-start(f32[3,512]{1,0:T(4,128)S(1)} %pad_maximum_fusion.1), channel_id=1, source_target_pairs={{0,8},{4,12},{8,0},{12,4},{16,24},{20,28},{24,16},{28,20},{1,9},{5... | collective-permute-start | bytes 18440 | tf_op jit(solution)/shard_map/ppermute | solution.py:33
  78.5 4.6 %collective-permute-start.13 = (f32[3,512]{1,0:T(4,128)S(1)}, f32[3,512]{1,0:T(4,128)S(1)}, u32[]{:S(2)}, u32[]{:S(2)}) collective-permute-start(f32[3,512]{1,0:T(4,128)S(1)} %fusion.94), channel_id=1, source_target_pairs={{0,16},{4,20},{8,24},{12,28},{16,0},{20,4},{24,8},{28,12},{1,17},{... | collective-permute-start | bytes 18440 | tf_op jit(solution)/shard_map/ppermute | solution.py:33
  83.7 2.3 %copy-start.13 = (bf16[512,256]{1,0:T(8,128)(2,1)S(1)}, bf16[512,256]{1,0:T(8,128)(2,1)}, u32[]{:S(2)}) copy-start(bf16[512,256]{1,0:T(8,128)(2,1)} %convolution_convert_fusion.2) | copy-start | bytes 786436
  85.6 7.2 %collective-permute-start.15 = (bf16[512,256]{1,0:T(8,128)(2,1)S(1)}, bf16[512,256]{1,0:T(8,128)(2,1)S(1)}, u32[]{:S(2)}, u32[]{:S(2)}) collective-permute-start(bf16[512,256]{1,0:T(8,128)(2,1)S(1)} %convolution_convert_fusion.1), channel_id=1, source_target_pairs={{0,8},{4,12},{8,0},{12,4},{16,24},{20,28},{24,16},{28,20},{1,9},{5... | collective-permute-start | bytes 786440 | tf_op jit(solution)/shard_map/ppermute | solution.py:53
  86.5 7.9 %collective-permute-start.14 = (f32[256,256]{1,0:T(8,128)S(1)}, f32[256,256]{1,0:T(8,128)S(1)}, u32[]{:S(2)}, u32[]{:S(2)}) collective-permute-start(f32[256,256]{1,0:T(8,128)S(1)} %slice_select_fusion.2), channel_id=1, source_target_pairs={{0,2},{2,0},{1,3},{3,1},{4,6},{6,4},{5,7},{7,5},{8,10},{10,8},{9,1... | collective-permute-start | bytes 786440 | tf_op jit(solution)/shard_map/ppermute | solution.py:85
  92.8 10.0 %collective-permute-start.16 = (bf16[512,256]{1,0:T(8,128)(2,1)S(1)}, bf16[512,256]{1,0:T(8,128)(2,1)S(1)}, u32[]{:S(2)}, u32[]{:S(2)}) collective-permute-start(bf16[512,256]{1,0:T(8,128)(2,1)S(1)} %add_convert_fusion), channel_id=1, source_target_pairs={{0,16},{4,20},{8,24},{12,28},{16,0},{20,4},{24,8},{28,12},{1,17},{... | collective-permute-start | bytes 786440 | tf_op jit(solution)/shard_map/ppermute | solution.py:53

commit v9 on v8

--- a/solution.py
+++ b/solution.py
@@ -216,8 +216,11 @@
     local_mixed = jnp.einsum(
         "hqk,khd->qhd", raised, value_heads, preferred_element_type=jnp.float32
     ).reshape(query_count, model_width)
+    softmax_parts = lax.optimization_barrier(
+        (local_max, local_total, local_mixed.astype(jnp.bfloat16))
+    )
     _, total, mixed = butterfly(
-        (local_max, local_total, local_mixed.astype(jnp.bfloat16)),
+        softmax_parts,
         "phi",
         softmax_combine,
         ordered=True,

time: 104 us -> 108 us (1.038)
  waiting for transfers between devices: 42.1 us -> 51.3 us
  matrix products: 22.6 us -> 19.2 us
    ppermute x11, waiting for transfers between devices: 25 us -> 32.4 us  [butterfly(): other = lax.ppermute(tree, axis, partner_pairs(count, distance))]
    dot_general x1, matrix products: 4.9 us -> 1.52 us  [body(): jnp.einsum('hqk,khd->qhd', raised, value_heads, preferred_element_type=jn...]
    ppermute x11, starting transfers between devices: 12.1 us -> 14.1 us  [butterfly(): other = lax.ppermute(tree, axis, partner_pairs(count, distance))]
    ppermute x2, waiting for transfers between devices: 13.7 us -> 15.5 us  [narrow_butterfly(): other = lax.ppermute(sent, axis, partner_pairs(count, distance))]
  transfers between devices with their start and end apart: 17 -> 17, of which waited for: 11 -> 10; matrix products, arithmetic and copies ran while one was open for 10% -> 3% of each run, Pallas kernels for 0% -> 0%
where the time goes in v9:
time: 108 us; the launch traced here: 107 us
  waiting for transfers between devices  51.3 us (48%)
  starting transfers between devices  21.5 us (20%)
  matrix products  19.2 us (18%)
  other arithmetic  6.88 us (6%)
  blocking collectives  4.35 us (4%)
  local copies, waits for them, and re-layouts  3.15 us (3%)
  between operations  1.12 us (1%)
    ppermute x11, waiting for transfers between devices, butterfly(): other = lax.ppermute(tree, axis, partner_pairs(count, distance))  32.4 us
    ppermute x2, waiting for transfers between devices, narrow_butterfly(): other = lax.ppermute(sent, axis, partner_pairs(count, distance))  15.5 us
    ppermute x11, starting transfers between devices, butterfly(): other = lax.ppermute(tree, axis, partner_pairs(count, distance))  14.1 us
    sub x1, matrix products, window_attend(): raised = jnp.exp(scores - jnp.max(scores, axis=-1, keepdims=True))  5.11 us
    ppermute x1, starting transfers between devices, extended_2(): lax.ppermute(lax.slice_in_dim(block, 0, width, axis=dim), axis, backward)  5.03 us
    all_gather x1, blocking collectives, body(): lax.all_gather(jnp.concatenate([local_kv, encoded, digits], axis=1), 'que...  4.35 us
    dot_general x1, matrix products, window_attend(): jnp.einsum('hqk,khd->qhd', weights, value_heads, preferred_element_type=j...  3.96 us
    ppermute x1, waiting for transfers between devices, extended_2(): lax.ppermute(lax.slice_in_dim(block, block.shape[dim] - width, None, axis...  3.39 us
  transfers between devices with their start and end apart: 17, of which 10 were waited for; matrix products, arithmetic and copies ran while one was open for 3% of the time, Pallas kernels for 0%

profile of v9, /device:TPU:0, one launch (start us, length us, event | category | flops | bytes accessed | tf_op | source)
XLA Modules:
  0.0 107.5 jit_solution(7401193055858209011)
XLA Ops:
  0.7 1.1 %copy.40 = bf16[256,256]{0,1:T(8,128)(2,1)S(1)} copy(bf16[256,256]{1,0:T(8,128)(2,1)} %param.13) | data formatting | bytes 262144 | tf_op args[0]
  1.9 1.3 %convolution_convert_fusion = bf16[256,768]{1,0:T(8,128)(2,1)S(1)} fusion(bf16[256,768]{1,0:T(8,128)(2,1)} %param.14, bf16[256,256]{0,1:T(8,128)(2,1)S(1)} %copy.40, f32[256]{0:T(256)S(1)} %add_rsqrt_fusion.3, f32[256]{0:T(256)S(1)} %broadcast_multiply_fusion.3), kind=kOutput, calls=%fused_computation.22 | convolution fusion | flops 101122048 | bytes 919552 | tf_op jit(solution)/shard_map/dot_general | solution.py:176
  3.7 5.0 %collective-permute-start.1 = (bf16[256,512]{1,0:T(8,128)(2,1)S(1)}, bf16[256,512]{1,0:T(8,128)(2,1)S(1)}, u32[]{:S(2)}, u32[]{:S(2)}) collective-permute-start(bf16[256,512]{1,0:T(8,128)(2,1)S(1)} %slice.63), channel_id=1, source_target_pairs={{2,0},{4,2},{6,4},{8,6},{10,8},{12,10},{14,12},{16,14},{18,16},{20... | collective-permute-start | bytes 786440 | tf_op jit(solution)/shard_map/ppermute | solution.py:19
  9.5 3.4 %collective-permute-done = bf16[256,512]{1,0:T(8,128)(2,1)S(1)} collective-permute-done((bf16[256,512]{1,0:T(8,128)(2,1)S(1)}, bf16[256,512]{1,0:T(8,128)(2,1)S(1)}, u32[]{:S(2)}, u32[]{:S(2)}) %collective-permute-start) | collective-permute-done | bytes 262176 | tf_op jit(solution)/shard_map/ppermute | solution.py:16
  13.3 5.1 %fusion.101 = (f32[8,256]{1,0:T(8,128)S(1)}, f32[8,256,768]{2,1,0:T(8,128)}) fusion(pred[256,768]{1,0:T(8,128)(4,1)S(1)} %fusion.24, bf16[256,8,32]{0,2,1:T(8,128)(2,1)S(1)} %bitcast.101, bf16[768,8,32]{0,2,1:T(8,128)(2,1)S(1)} %bitcast.98), kind=kOutput, calls=%fused_computation.176 | convolution fusion | flops 106955520 | bytes 7020544 | tf_op jit(solution)/shard_map/sub | solution.py:113
  18.5 4.0 %fusion.12 = bf16[8,32,256]{2,1,0:T(8,128)(2,1)S(1)} fusion(bf16[768,8,32]{0,2,1:T(8,128)(2,1)S(1)} %bitcast.99, f32[8,256,768]{2,1,0:T(8,128)} %get-tuple-element.55, f32[8,256]{1,0:T(8,128)S(1)} %get-tuple-element.54), kind=kOutput, calls=%fused_computation.34 | convolution fusion | flops 103874560 | bytes 6823936 | tf_op jit(solution)/shard_map/hqk,khd->qhd/dot_general | solution.py:115
  22.8 0.8 convert_reduce_fusion.3
  24.2 4.3 %all_gather.3 = bf16[512,896]{1,0:T(8,128)(2,1)S(1)} all-gather(bf16[256,896]{1,0:T(8,128)(2,1)S(1)} %fusion.46), channel_id=1, replica_groups=mesh['phi'=8,'query'=2,'event'=2] {'query'}, dimensions={0}, use_global_device_ids=true | all-gather | bytes 1376256 | tf_op jit(solution)/shard_map/all_gather | solution.py:197
  28.8 1.3 %multiply_reduce_fusion = (f32[8,512]{1,0:T(8,128)S(1)}, f32[8,512,512]{1,2,0:T(8,128)S(1)}) fusion(bf16[512,8,32]{0,2,1:T(8,128)(2,1)S(1)} %bitcast.93, bf16[512,8,32]{0,2,1:T(8,128)(2,1)S(1)} %bitcast.95), kind=kOutput, calls=%fused_computation.3 | convolution fusion | flops 138407936 | bytes 8929280 | tf_op jit(solution)/shard_map/qhd,khd->hqk/dot_general | solution.py:210
  30.1 1.4 %convert_reduce_fusion = f32[8,512]{1,0:T(8,128)S(1)} fusion(f32[8,512]{1,0:T(8,128)S(1)} %get-tuple-element.9, f32[8,512,512]{1,2,0:T(8,128)S(1)} %get-tuple-element.61), kind=kLoop, calls=%fused_computation.1 | loop fusion | flops 10481664 | bytes 8421376 | tf_op jit(solution)/shard_map/reduce_sum | solution.py:215
  31.6 1.5 %convolution_convert_fusion.3 = bf16[8,32,512]{2,1,0:T(8,128)(2,1)S(1)} fusion(bf16[512,8,32]{0,2,1:T(8,128)(2,1)S(1)} %bitcast.94, f32[8,512,512]{1,2,0:T(8,128)S(1)} %get-tuple-element.61, f32[8,512]{1,0:T(8,128)S(1)} %get-tuple-element.9), kind=kOutput, calls=%fused_computation.27 | convolution fusion | flops 140640256 | bytes 8929280 | tf_op jit(solution)/shard_map/hqk,khd->qhd/dot_general | solution.py:216
  33.2 2.0 %collective-permute-start.8 = (f32[8,512]{1,0:T(8,128)S(1)}, f32[8,512]{1,0:T(8,128)S(1)}, u32[]{:S(2)}, u32[]{:S(2)}) collective-permute-start(f32[8,512]{1,0:T(8,128)S(1)} %convert_reduce_fusion), channel_id=1, source_target_pairs={{0,4},{4,0},{8,12},{12,8},{16,20},{20,16},{24,28},{28,24},{1,5},{5... | collective-permute-start | bytes 49160 | tf_op jit(solution)/shard_map/ppermute | solution.py:33
  35.2 1.7 %collective-permute-done.3 = f32[8,512]{1,0:T(8,128)S(1)} collective-permute-done((f32[8,512]{1,0:T(8,128)S(1)}, f32[8,512]{1,0:T(8,128)S(1)}, u32[]{:S(2)}, u32[]{:S(2)}) %collective-permute-start.3) | collective-permute-done | bytes 16416 | tf_op jit(solution)/shard_map/ppermute | solution.py:33
  37.6 3.1 %collective-permute-done.5 = f32[8,512]{1,0:T(8,128)S(1)} collective-permute-done((f32[8,512]{1,0:T(8,128)S(1)}, f32[8,512]{1,0:T(8,128)S(1)}, u32[]{:S(2)}, u32[]{:S(2)}) %collective-permute-start.5) | collective-permute-done | bytes 16416 | tf_op jit(solution)/shard_map/ppermute | solution.py:33
  42.2 1.4 %collective-permute-start.2 = (bf16[512,256]{0,1:T(8,128)(2,1)S(1)}, bf16[512,256]{0,1:T(8,128)(2,1)S(1)}, u32[]{:S(2)}, u32[]{:S(2)}) collective-permute-start(bf16[512,256]{0,1:T(8,128)(2,1)S(1)} %bitcast.96), channel_id=1, source_target_pairs={{0,4},{4,0},{8,12},{12,8},{16,20},{20,16},{24,28},{28,24},{1,5},{5... | collective-permute-start | bytes 786440 | tf_op jit(solution)/shard_map/ppermute | solution.py:33
  43.6 2.6 %collective-permute-start.7 = (f32[8,512]{1,0:T(8,128)S(1)}, f32[8,512]{1,0:T(8,128)S(1)}, u32[]{:S(2)}, u32[]{:S(2)}) collective-permute-start(f32[8,512]{1,0:T(8,128)S(1)} %get-tuple-element.49), channel_id=1, source_target_pairs={{0,16},{4,20},{8,24},{12,28},{16,0},{20,4},{24,8},{28,12},{1,17},{... | collective-permute-start | bytes 49160 | tf_op jit(solution)/shard_map/ppermute | solution.py:33
  46.6 0.8 copy.44
  47.5 8.5 %collective-permute-done.2 = bf16[512,256]{0,1:T(8,128)(2,1)S(1)} collective-permute-done((bf16[512,256]{0,1:T(8,128)(2,1)S(1)}, bf16[512,256]{0,1:T(8,128)(2,1)S(1)}, u32[]{:S(2)}, u32[]{:S(2)}) %collective-permute-start.2) | collective-permute-done | bytes 262176 | tf_op jit(solution)/shard_map/ppermute | solution.py:33
  56.1 1.4 %collective-permute-start.4 = (bf16[512,256]{0,1:T(8,128)(2,1)S(1)}, bf16[512,256]{0,1:T(8,128)(2,1)S(1)}, u32[]{:S(2)}, u32[]{:S(2)}) collective-permute-start(bf16[512,256]{0,1:T(8,128)(2,1)S(1)} %fusion.38), channel_id=1, source_target_pairs={{0,8},{4,12},{8,0},{12,4},{16,24},{20,28},{24,16},{28,20},{1,9},{5... | collective-permute-start | bytes 786440 | tf_op jit(solution)/shard_map/ppermute | solution.py:33
  57.9 6.0 %collective-permute-done.4 = bf16[512,256]{0,1:T(8,128)(2,1)S(1)} collective-permute-done((bf16[512,256]{0,1:T(8,128)(2,1)S(1)}, bf16[512,256]{0,1:T(8,128)(2,1)S(1)}, u32[]{:S(2)}, u32[]{:S(2)}) %collective-permute-start.4) | collective-permute-done | bytes 262176 | tf_op jit(solution)/shard_map/ppermute | solution.py:33
  64.1 3.1 %collective-permute-start.6 = (bf16[512,256]{0,1:T(8,128)(2,1)S(1)}, bf16[512,256]{0,1:T(8,128)(2,1)S(1)}, u32[]{:S(2)}, u32[]{:S(2)}) collective-permute-start(bf16[512,256]{0,1:T(8,128)(2,1)S(1)} %fusion.36), channel_id=1, source_target_pairs={{0,16},{4,20},{8,24},{12,28},{16,0},{20,4},{24,8},{28,12},{1,17},{... | collective-permute-start | bytes 786440 | tf_op jit(solution)/shard_map/ppermute | solution.py:33
  67.6 6.2 %collective-permute-done.6 = bf16[512,256]{0,1:T(8,128)(2,1)S(1)} collective-permute-done((bf16[512,256]{0,1:T(8,128)(2,1)S(1)}, bf16[512,256]{0,1:T(8,128)(2,1)S(1)}, u32[]{:S(2)}, u32[]{:S(2)}) %collective-permute-start.6) | collective-permute-done | bytes 262176 | tf_op jit(solution)/shard_map/ppermute | solution.py:33
  74.4 1.1 %convolution_convert_fusion.2 = bf16[512,256]{1,0:T(8,128)(2,1)} fusion(bf16[256,256]{1,0:T(8,128)(2,1)S(1)} %copy-done.11, bf16[256,256]{1,0:T(8,128)(2,1)S(1)} %copy-done.12, f32[512,256]{0,1:T(8,128)S(1)} %get-tuple-element.63, f32[512]{0:T(512)S(1)} %add_rsqrt_fusion, f32[512]{0:T(512)S(1)} %broadcast_multiply_fusion), kind=kOutput, calls=%fused_computation.26 | convolution fusion | flops 135004160 | bytes 1052672 | tf_op jit(solution)/shard_map/dot_general | solution.py:240
  75.5 2.2 %select_reduce_fusion = (f32[512]{0:T(512)S(1)}, f32[512]{0:T(512)S(1)}, f32[512]{0:T(512)S(1)}, f32[512,1024]{1,0:T(8,128)S(1)}) fusion(s32[1024]{0:T(1024)S(1)} %fusion.31, s32[512]{0:T(512)S(1)} %copy-done.8, pred[512]{0:T(512)(128)(4,1)S(1)} %get-tuple-element.30, bf16[512,256]{1,0:T(8,128)(2,1)} %convolution_convert_fusion.2, ...), kind=kOutput, calls=%fused_computation.18 | convolution fusion | flops 274201088 | bytes 2896384 | tf_op jit(solution)/shard_map/dot_general | solution.py:256
  77.9 3.6 %collective-permute-done.12 = f32[3,512]{1,0:T(4,128)S(1)} collective-permute-done((f32[3,512]{1,0:T(4,128)S(1)}, f32[3,512]{1,0:T(4,128)S(1)}, u32[]{:S(2)}, u32[]{:S(2)}) %collective-permute-start.12) | collective-permute-done | bytes 6176 | tf_op jit(solution)/shard_map/ppermute | solution.py:33
  81.5 1.4 %collective-permute-start.13 = (f32[3,512]{1,0:T(4,128)S(1)}, f32[3,512]{1,0:T(4,128)S(1)}, u32[]{:S(2)}, u32[]{:S(2)}) collective-permute-start(f32[3,512]{1,0:T(4,128)S(1)} %fusion.94), channel_id=1, source_target_pairs={{0,16},{4,20},{8,24},{12,28},{16,0},{20,4},{24,8},{28,12},{1,17},{... | collective-permute-start | bytes 18440 | tf_op jit(solution)/shard_map/ppermute | solution.py:33
  82.9 3.2 %collective-permute-done.13 = f32[3,512]{1,0:T(4,128)S(1)} collective-permute-done((f32[3,512]{1,0:T(4,128)S(1)}, f32[3,512]{1,0:T(4,128)S(1)}, u32[]{:S(2)}, u32[]{:S(2)}) %collective-permute-start.13) | collective-permute-done | bytes 6176 | tf_op jit(solution)/shard_map/ppermute | solution.py:33
  86.8 1.4 %fusion.9 = bf16[512,1024]{1,0:T(8,128)(2,1)S(1)} fusion(f32[512,1024]{1,0:T(8,128)S(1)} %get-tuple-element.64, f32[512]{0:T(512)S(1)} %bitcast.111, f32[512]{0:T(512)S(1)} %bitcast.112, s32[1024]{0:T(1024)S(1)} %fusion.31, f32[512]{0:T(512)S(1)} %get-tuple-element.29, s32[512]{0:T(512)S(1)} %copy-done.8, pred[512]{0:T(512)(128)(4,1)S(1)} %get-tuple-element.30), kind=kLoop, calls=%fused_computation.17 | loop fusion | flops 7340032 | bytes 3158528 | tf_op jit(solution)/shard_map/convert_element_type | solution.py:150
  89.8 7.2 %collective-permute-done.15 = bf16[512,256]{1,0:T(8,128)(2,1)S(1)} collective-permute-done((bf16[512,256]{1,0:T(8,128)(2,1)S(1)}, bf16[512,256]{1,0:T(8,128)(2,1)S(1)}, u32[]{:S(2)}, u32[]{:S(2)}) %collective-permute-start.15) | collective-permute-done | bytes 262176 | tf_op jit(solution)/shard_map/ppermute | solution.py:53
  97.6 0.8 select_add_fusion
  98.3 8.3 %collective-permute-done.16 = bf16[512,256]{1,0:T(8,128)(2,1)S(1)} collective-permute-done((bf16[512,256]{1,0:T(8,128)(2,1)S(1)}, bf16[512,256]{1,0:T(8,128)(2,1)S(1)}, u32[]{:S(2)}, u32[]{:S(2)}) %collective-permute-start.16) | collective-permute-done | bytes 262176 | tf_op jit(solution)/shard_map/ppermute | solution.py:53
  106.6 0.8 convert_add_fusion
  (101 shorter events, 10.1 us)
Async XLA Ops:
  0.6 22.2 %copy-start = (bf16[1024,256]{1,0:T(8,128)(2,1)S(1)}, bf16[1024,256]{1,0:T(8,128)(2,1)}, u32[]{:S(2)}) copy-start(bf16[1024,256]{1,0:T(8,128)(2,1)} %param.17) | copy-start | bytes 1572868
  0.6 8.2 %copy-start.9 = (s32[256]{0:T(256)S(1)}, s32[256]{0:T(256)}, u32[]{:S(2)}) copy-start(s32[256]{0:T(256)} %param.24) | copy-start | bytes 3076
  0.7 8.5 %copy-start.1 = (bf16[512,256]{1,0:T(8,128)(2,1)S(1)}, bf16[512,256]{1,0:T(8,128)(2,1)}, u32[]{:S(2)}) copy-start(bf16[512,256]{1,0:T(8,128)(2,1)} %param.18) | copy-start | bytes 786436
  0.7 8.5 %copy-start.5 = (bf16[256,256]{1,0:T(8,128)(2,1)S(1)}, bf16[256,256]{1,0:T(8,128)(2,1)}, u32[]{:S(2)}) copy-start(bf16[256,256]{1,0:T(8,128)(2,1)} %param.19) | copy-start | bytes 393220
  3.2 9.6 %collective-permute-start = (bf16[256,512]{1,0:T(8,128)(2,1)S(1)}, bf16[256,512]{1,0:T(8,128)(2,1)S(1)}, u32[]{:S(2)}, u32[]{:S(2)}) collective-permute-start(bf16[256,512]{1,0:T(8,128)(2,1)S(1)} %slice.63), channel_id=1, source_target_pairs={{0,2},{2,4},{4,6},{6,8},{8,10},{10,12},{12,14},{14,16},{16,18},{18... | collective-permute-start | bytes 786440 | tf_op jit(solution)/shard_map/ppermute | solution.py:16
  3.7 9.1 %collective-permute-start.1 = (bf16[256,512]{1,0:T(8,128)(2,1)S(1)}, bf16[256,512]{1,0:T(8,128)(2,1)S(1)}, u32[]{:S(2)}, u32[]{:S(2)}) collective-permute-start(bf16[256,512]{1,0:T(8,128)(2,1)S(1)} %slice.63), channel_id=1, source_target_pairs={{2,0},{4,2},{6,4},{8,6},{10,8},{12,10},{14,12},{16,14},{18,16},{20... | collective-permute-start | bytes 786440 | tf_op jit(solution)/shard_map/ppermute | solution.py:19
  18.5 4.0 %copy-start.6 = (bf16[256,256]{1,0:T(8,128)(2,1)S(1)}, bf16[256,256]{1,0:T(8,128)(2,1)}, u32[]{:S(2)}) copy-start(bf16[256,256]{1,0:T(8,128)(2,1)} %param.15) | copy-start | bytes 393220
  18.5 4.3 %copy-start.10 = (bf16[256,1024]{1,0:T(8,128)(2,1)S(1)}, bf16[256,1024]{1,0:T(8,128)(2,1)}, u32[]{:S(2)}) copy-start(bf16[256,1024]{1,0:T(8,128)(2,1)} %param.16) | copy-start | bytes 1572868
  22.8 1.1 copy-start.4
  23.8 4.9 %copy-start.3 = (bf16[256,256]{1,0:T(8,128)(2,1)}, bf16[256,256]{1,0:T(8,128)(2,1)S(1)}, u32[]{:S(2)}) copy-start(bf16[256,256]{1,0:T(8,128)(2,1)S(1)} %copy.50) | copy-start | bytes 393220
  31.5 15.1 %copy-start.8 = (s32[512]{0:T(512)S(1)}, s32[512]{0:T(512)}, u32[]{:S(2)}) copy-start(s32[512]{0:T(512)} %param.25) | copy-start | bytes 6148
  33.1 3.8 %collective-permute-start.3 = (f32[8,512]{1,0:T(8,128)S(1)}, f32[8,512]{1,0:T(8,128)S(1)}, u32[]{:S(2)}, u32[]{:S(2)}) collective-permute-start(f32[8,512]{1,0:T(8,128)S(1)} %get-tuple-element.9), channel_id=1, source_target_pairs={{0,4},{4,0},{8,12},{12,8},{16,20},{20,16},{24,28},{28,24},{1,5},{5... | collective-permute-start | bytes 49160 | tf_op jit(solution)/shard_map/ppermute | solution.py:33
  33.2 4.4 %collective-permute-start.8 = (f32[8,512]{1,0:T(8,128)S(1)}, f32[8,512]{1,0:T(8,128)S(1)}, u32[]{:S(2)}, u32[]{:S(2)}) collective-permute-start(f32[8,512]{1,0:T(8,128)S(1)} %convert_reduce_fusion), channel_id=1, source_target_pairs={{0,4},{4,0},{8,12},{12,8},{16,20},{20,16},{24,28},{28,24},{1,5},{5... | collective-permute-start | bytes 49160 | tf_op jit(solution)/shard_map/ppermute | solution.py:33
  36.9 3.8 %collective-permute-start.5 = (f32[8,512]{1,0:T(8,128)S(1)}, f32[8,512]{1,0:T(8,128)S(1)}, u32[]{:S(2)}, u32[]{:S(2)}) collective-permute-start(f32[8,512]{1,0:T(8,128)S(1)} %get-tuple-element.36), channel_id=1, source_target_pairs={{0,8},{4,12},{8,0},{12,4},{16,24},{20,28},{24,16},{28,20},{1,9},{5... | collective-permute-start | bytes 49160 | tf_op jit(solution)/shard_map/ppermute | solution.py:33
  40.7 5.5 %collective-permute-start.9 = (f32[8,512]{1,0:T(8,128)S(1)}, f32[8,512]{1,0:T(8,128)S(1)}, u32[]{:S(2)}, u32[]{:S(2)}) collective-permute-start(f32[8,512]{1,0:T(8,128)S(1)} %get-tuple-element.42), channel_id=1, source_target_pairs={{0,8},{4,12},{8,0},{12,4},{16,24},{20,28},{24,16},{28,20},{1,9},{5... | collective-permute-start | bytes 49160 | tf_op jit(solution)/shard_map/ppermute | solution.py:33
  41.5 16.1 %collective-permute-start.11 = (bf16[512,384]{1,0:T(8,128)(2,1)S(1)}, bf16[512,384]{1,0:T(8,128)(2,1)S(1)}, u32[]{:S(2)}, u32[]{:S(2)}) collective-permute-start(bf16[512,384]{1,0:T(8,128)(2,1)S(1)} %slice.69), channel_id=1, source_target_pairs={{0,4},{4,0},{8,12},{12,8},{16,20},{20,16},{24,28},{28,24},{1,5},{5... | collective-permute-start | bytes 1179656 | tf_op jit(solution)/shard_map/ppermute | solution.py:245
  42.2 13.8 %collective-permute-start.2 = (bf16[512,256]{0,1:T(8,128)(2,1)S(1)}, bf16[512,256]{0,1:T(8,128)(2,1)S(1)}, u32[]{:S(2)}, u32[]{:S(2)}) collective-permute-start(bf16[512,256]{0,1:T(8,128)(2,1)S(1)} %bitcast.96), channel_id=1, source_target_pairs={{0,4},{4,0},{8,12},{12,8},{16,20},{20,16},{24,28},{28,24},{1,5},{5... | collective-permute-start | bytes 786440 | tf_op jit(solution)/shard_map/ppermute | solution.py:33
  43.6 13.9 %collective-permute-start.7 = (f32[8,512]{1,0:T(8,128)S(1)}, f32[8,512]{1,0:T(8,128)S(1)}, u32[]{:S(2)}, u32[]{:S(2)}) collective-permute-start(f32[8,512]{1,0:T(8,128)S(1)} %get-tuple-element.49), channel_id=1, source_target_pairs={{0,16},{4,20},{8,24},{12,28},{16,0},{20,4},{24,8},{28,12},{1,17},{... | collective-permute-start | bytes 49160 | tf_op jit(solution)/shard_map/ppermute | solution.py:33
  46.2 11.3 %collective-permute-start.10 = (f32[8,512]{1,0:T(8,128)S(1)}, f32[8,512]{1,0:T(8,128)S(1)}, u32[]{:S(2)}, u32[]{:S(2)}) collective-permute-start(f32[8,512]{1,0:T(8,128)S(1)} %get-tuple-element.44), channel_id=1, source_target_pairs={{0,16},{4,20},{8,24},{12,28},{16,0},{20,4},{24,8},{28,12},{1,17},{... | collective-permute-start | bytes 49160 | tf_op jit(solution)/shard_map/ppermute | solution.py:33
  56.1 7.8 %collective-permute-start.4 = (bf16[512,256]{0,1:T(8,128)(2,1)S(1)}, bf16[512,256]{0,1:T(8,128)(2,1)S(1)}, u32[]{:S(2)}, u32[]{:S(2)}) collective-permute-start(bf16[512,256]{0,1:T(8,128)(2,1)S(1)} %fusion.38), channel_id=1, source_target_pairs={{0,8},{4,12},{8,0},{12,4},{16,24},{20,28},{24,16},{28,20},{1,9},{5... | collective-permute-start | bytes 786440 | tf_op jit(solution)/shard_map/ppermute | solution.py:33
  57.9 16.1 %copy-start.2 = (bf16[512,256]{0,1:T(8,128)(2,1)S(1)}, bf16[512,256]{0,1:T(8,128)(2,1)}, u32[]{:S(2)}) copy-start(bf16[512,256]{0,1:T(8,128)(2,1)} %copy.44) | copy-start | bytes 786436
  57.9 16.1 %copy-start.7 = (bf16[256,256]{1,0:T(8,128)(2,1)S(1)}, bf16[256,256]{1,0:T(8,128)(2,1)}, u32[]{:S(2)}) copy-start(bf16[256,256]{1,0:T(8,128)(2,1)} %param.21) | copy-start | bytes 393220
  64.0 10.3 %copy-start.11 = (bf16[256,256]{1,0:T(8,128)(2,1)S(1)}, bf16[256,256]{1,0:T(8,128)(2,1)}, u32[]{:S(2)}) copy-start(bf16[256,256]{1,0:T(8,128)(2,1)} %param.23) | copy-start | bytes 393220
  64.1 10.3 %copy-start.12 = (bf16[256,256]{1,0:T(8,128)(2,1)S(1)}, bf16[256,256]{1,0:T(8,128)(2,1)}, u32[]{:S(2)}) copy-start(bf16[256,256]{1,0:T(8,128)(2,1)} %param.22) | copy-start | bytes 393220
  64.1 9.7 %collective-permute-start.6 = (bf16[512,256]{0,1:T(8,128)(2,1)S(1)}, bf16[512,256]{0,1:T(8,128)(2,1)S(1)}, u32[]{:S(2)}, u32[]{:S(2)}) collective-permute-start(bf16[512,256]{0,1:T(8,128)(2,1)S(1)} %fusion.36), channel_id=1, source_target_pairs={{0,16},{4,20},{8,24},{12,28},{16,0},{20,4},{24,8},{28,12},{1,17},{... | collective-permute-start | bytes 786440 | tf_op jit(solution)/shard_map/ppermute | solution.py:33
  77.8 3.7 %collective-permute-start.12 = (f32[3,512]{1,0:T(4,128)S(1)}, f32[3,512]{1,0:T(4,128)S(1)}, u32[]{:S(2)}, u32[]{:S(2)}) collective-permute-start(f32[3,512]{1,0:T(4,128)S(1)} %pad_maximum_fusion.1), channel_id=1, source_target_pairs={{0,8},{4,12},{8,0},{12,4},{16,24},{20,28},{24,16},{28,20},{1,9},{5... | collective-permute-start | bytes 18440 | tf_op jit(solution)/shard_map/ppermute | solution.py:33
  81.5 4.7 %collective-permute-start.13 = (f32[3,512]{1,0:T(4,128)S(1)}, f32[3,512]{1,0:T(4,128)S(1)}, u32[]{:S(2)}, u32[]{:S(2)}) collective-permute-start(f32[3,512]{1,0:T(4,128)S(1)} %fusion.94), channel_id=1, source_target_pairs={{0,16},{4,20},{8,24},{12,28},{16,0},{20,4},{24,8},{28,12},{1,17},{... | collective-permute-start | bytes 18440 | tf_op jit(solution)/shard_map/ppermute | solution.py:33
  86.8 2.4 %copy-start.13 = (bf16[512,256]{1,0:T(8,128)(2,1)S(1)}, bf16[512,256]{1,0:T(8,128)(2,1)}, u32[]{:S(2)}) copy-start(bf16[512,256]{1,0:T(8,128)(2,1)} %convolution_convert_fusion.2) | copy-start | bytes 786436
  88.6 8.3 %collective-permute-start.15 = (bf16[512,256]{1,0:T(8,128)(2,1)S(1)}, bf16[512,256]{1,0:T(8,128)(2,1)S(1)}, u32[]{:S(2)}, u32[]{:S(2)}) collective-permute-start(bf16[512,256]{1,0:T(8,128)(2,1)S(1)} %convolution_convert_fusion.1), channel_id=1, source_target_pairs={{0,8},{4,12},{8,0},{12,4},{16,24},{20,28},{24,16},{28,20},{1,9},{5... | collective-permute-start | bytes 786440 | tf_op jit(solution)/shard_map/ppermute | solution.py:53
  89.7 7.9 %collective-permute-start.14 = (f32[256,256]{1,0:T(8,128)S(1)}, f32[256,256]{1,0:T(8,128)S(1)}, u32[]{:S(2)}, u32[]{:S(2)}) collective-permute-start(f32[256,256]{1,0:T(8,128)S(1)} %slice_select_fusion.2), channel_id=1, source_target_pairs={{0,2},{2,0},{1,3},{3,1},{4,6},{6,4},{5,7},{7,5},{8,10},{10,8},{9,1... | collective-permute-start | bytes 786440 | tf_op jit(solution)/shard_map/ppermute | solution.py:85
  97.0 9.6 %collective-permute-start.16 = (bf16[512,256]{1,0:T(8,128)(2,1)S(1)}, bf16[512,256]{1,0:T(8,128)(2,1)S(1)}, u32[]{:S(2)}, u32[]{:S(2)}) collective-permute-start(bf16[512,256]{1,0:T(8,128)(2,1)S(1)} %add_convert_fusion), channel_id=1, source_target_pairs={{0,16},{4,20},{8,24},{12,28},{16,0},{20,4},{24,8},{28,12},{1,17},{... | collective-permute-start | bytes 786440 | tf_op jit(solution)/shard_map/ppermute | solution.py:53

commit v10 on v8

--- a/solution.py
+++ b/solution.py
@@ -175,7 +175,17 @@
     normed = norm_rows(hits).astype(jnp.bfloat16)
     projected = jnp.dot(normed, enc_qkv, preferred_element_type=jnp.float32).astype(jnp.bfloat16)
     extended = extended_2(projected[:, model_width:], ((("phi", "query"), 0),), WIN // 2)
-    attended = window_attend(projected[:, :model_width], extended)
+    block_rows = local_hits // 2
+    span = extended.shape[0] - local_hits
+    attended = jnp.concatenate(
+        [
+            window_attend(
+                projected[b * block_rows : (b + 1) * block_rows, :model_width],
+                extended[b * block_rows : b * block_rows + block_rows + span],
+            )
+            for b in range(2)
+        ]
+    )
     residual = hits.astype(jnp.float32) + jnp.dot(
         attended, enc_out, preferred_element_type=jnp.float32
     )

time: 104 us -> 101 us (0.971)
  matrix products: 22.6 us -> 18.5 us
  waiting for transfers between devices: 42.1 us -> 45.3 us
  starting transfers between devices: 21.3 us -> 19.2 us
    ppermute x1, waiting for transfers between devices: 0.01 us -> 4.45 us  [body(): lax.ppermute(own_payload, 'phi', partner_pairs(lax.axis_size('phi'), 1))]
    sub x1 -> x2, matrix products: 5.11 us -> 2.28 us  [window_attend(): raised = jnp.exp(scores - jnp.max(scores, axis=-1, keepdims=True))]
    ppermute x11, waiting for transfers between devices: 25 us -> 23.2 us  [butterfly(): other = lax.ppermute(tree, axis, partner_pairs(count, distance))]
    ppermute x2, starting transfers between devices: 2.13 us -> 0.68 us  [narrow_butterfly(): other = lax.ppermute(sent, axis, partner_pairs(count, distance))]
    dot_general x1 -> x2, matrix products: 3.96 us -> 2.68 us  [window_attend(): jnp.einsum('hqk,khd->qhd', weights, value_heads, preferred_element_type=j...]
    ppermute x2, waiting for transfers between devices: 13.7 us -> 15 us  [narrow_butterfly(): other = lax.ppermute(sent, axis, partner_pairs(count, distance))]
    select_n x1, other arithmetic: 1.37 us -> 0.31 us  [body(): jnp.where(pair_upper, jnp.concatenate([other_payload, own_payload]), jnp....]
    unnamed x31 -> x29, local copies, waits for them, and re-layouts: 3.07 us -> 3.07 us
  transfers between devices with their start and end apart: 17 -> 17, of which waited for: 11 -> 12; matrix products, arithmetic and copies ran while one was open for 10% -> 10% of each run, Pallas kernels for 0% -> 0%
where the time goes in v10:
time: 101 us
  waiting for transfers between devices  45.3 us (45%)
  starting transfers between devices  19.2 us (19%)
  matrix products  18.5 us (18%)
  other arithmetic  7.53 us (7%)
  local copies, waits for them, and re-layouts  4.73 us (5%)
  blocking collectives  4.35 us (4%)
  between operations  1.17 us (1%)
    ppermute x11, waiting for transfers between devices, butterfly(): other = lax.ppermute(tree, axis, partner_pairs(count, distance))  23.2 us
    ppermute x2, waiting for transfers between devices, narrow_butterfly(): other = lax.ppermute(sent, axis, partner_pairs(count, distance))  15 us
    ppermute x11, starting transfers between devices, butterfly(): other = lax.ppermute(tree, axis, partner_pairs(count, distance))  12.3 us
    ppermute x1, starting transfers between devices, extended_2(): lax.ppermute(lax.slice_in_dim(block, 0, width, axis=dim), axis, backward)  5.03 us
    dot_general x1, matrix products, body(): jnp.einsum('hqk,khd->qhd', raised, value_heads, preferred_element_type=jn...  4.9 us
    ppermute x1, waiting for transfers between devices, body(): lax.ppermute(own_payload, 'phi', partner_pairs(lax.axis_size('phi'), 1))  4.45 us
    all_gather x1, blocking collectives, body(): lax.all_gather(jnp.concatenate([local_kv, encoded, digits], axis=1), 'que...  4.35 us
    unnamed x29, local copies, waits for them, and re-layouts  3.07 us
  transfers between devices with their start and end apart: 17, of which 12 were waited for; matrix products, arithmetic and copies ran while one was open for 10% of the time, Pallas kernels for 0%

profile of v10, /device:TPU:0, one launch (start us, length us, event | category | flops | bytes accessed | tf_op | source)
XLA Modules:
  0.0 100.7 jit_solution(3141518806335994655)
XLA Ops:
  0.7 1.1 %copy.46 = bf16[256,256]{0,1:T(8,128)(2,1)S(1)} copy(bf16[256,256]{1,0:T(8,128)(2,1)} %param.13) | data formatting | bytes 262144 | tf_op args[0]
  1.9 1.3 %convolution_convert_fusion = bf16[256,768]{1,0:T(8,128)(2,1)S(1)} fusion(bf16[256,768]{1,0:T(8,128)(2,1)} %param.14, bf16[256,256]{0,1:T(8,128)(2,1)S(1)} %copy.46, f32[256]{0:T(256)S(1)} %add_rsqrt_fusion.3, f32[256]{0:T(256)S(1)} %broadcast_multiply_fusion.3), kind=kOutput, calls=%fused_computation.31 | convolution fusion | flops 101122048 | bytes 919552 | tf_op jit(solution)/shard_map/dot_general | solution.py:176
  3.7 5.0 %collective-permute-start.1 = (bf16[256,512]{1,0:T(8,128)(2,1)S(1)}, bf16[256,512]{1,0:T(8,128)(2,1)S(1)}, u32[]{:S(2)}, u32[]{:S(2)}) collective-permute-start(bf16[256,512]{1,0:T(8,128)(2,1)S(1)} %slice.81), channel_id=1, source_target_pairs={{2,0},{4,2},{6,4},{8,6},{10,8},{12,10},{14,12},{16,14},{18,16},{20... | collective-permute-start | bytes 786440 | tf_op jit(solution)/shard_map/ppermute | solution.py:19
  10.3 2.6 %collective-permute-done = bf16[256,512]{1,0:T(8,128)(2,1)S(1)} collective-permute-done((bf16[256,512]{1,0:T(8,128)(2,1)S(1)}, bf16[256,512]{1,0:T(8,128)(2,1)S(1)}, u32[]{:S(2)}, u32[]{:S(2)}) %collective-permute-start) | collective-permute-done | bytes 262176 | tf_op jit(solution)/shard_map/ppermute | solution.py:16
  13.8 1.1 %fusion.128 = f32[8,128]{1,0:T(8,128)S(1)} fusion(pred[128,640]{1,0:T(8,128)(4,1)S(1)} %fusion.51, bf16[128,8,32]{0,2,1:T(8,128)(2,1)S(1)} %bitcast.118, bf16[640,8,32]{0,2,1:T(8,128)(2,1)S(1)} %bitcast.111), kind=kOutput, calls=%fused_computation.201 | convolution fusion | flops 44565120 | bytes 479232 | tf_op jit(solution)/shard_map/sub | solution.py:113
  15.0 1.3 %fusion.19 = bf16[8,32,128]{2,1,0:T(8,128)(2,1)S(1)} fusion(bf16[640,8,32]{0,2,1:T(8,128)(2,1)S(1)} %bitcast.113, f32[8,128]{1,0:T(8,128)S(1)} %fusion.128, pred[128,640]{1,0:T(8,128)(4,1)S(1)} %fusion.51, bf16[128,8,32]{0,2,1:T(8,128)(2,1)S(1)} %bitcast.119, bf16[640,8,32]{0,2,1:T(8,128)(2,1)S(1)} %bitcast.112), kind=kOutput, calls=%fused_computation.44 | convolution fusion | flops 87197312 | bytes 872448 | tf_op jit(solution)/shard_map/hqk,khd->qhd/dot_general | solution.py:115
  16.3 1.2 %fusion.127 = f32[8,128]{1,0:T(8,128)S(1)} fusion(pred[128,640]{1,0:T(8,128)(4,1)S(1)} %fusion.51, bf16[128,8,32]{0,2,1:T(8,128)(2,1)S(1)} %bitcast.116, bf16[640,8,32]{0,2,1:T(8,128)(2,1)S(1)} %bitcast.108), kind=kOutput, calls=%fused_computation.200 | convolution fusion | flops 44565120 | bytes 479232 | tf_op jit(solution)/shard_map/sub | solution.py:113
  17.5 1.3 %fusion.18 = bf16[8,32,128]{2,1,0:T(8,128)(2,1)S(1)} fusion(bf16[640,8,32]{0,2,1:T(8,128)(2,1)S(1)} %bitcast.110, f32[8,128]{1,0:T(8,128)S(1)} %fusion.127, pred[128,640]{1,0:T(8,128)(4,1)S(1)} %fusion.51, bf16[128,8,32]{0,2,1:T(8,128)(2,1)S(1)} %bitcast.117, bf16[640,8,32]{0,2,1:T(8,128)(2,1)S(1)} %bitcast.109), kind=kOutput, calls=%fused_computation.43 | convolution fusion | flops 87197312 | bytes 872448 | tf_op jit(solution)/shard_map/hqk,khd->qhd/dot_general | solution.py:115
  19.2 0.8 convert_reduce_fusion.3
  20.6 4.3 %all_gather.3 = bf16[512,896]{1,0:T(8,128)(2,1)S(1)} all-gather(bf16[256,896]{1,0:T(8,128)(2,1)S(1)} %fusion.48), channel_id=1, replica_groups=mesh['phi'=8,'query'=2,'event'=2] {'query'}, dimensions={0}, use_global_device_ids=true | all-gather | bytes 1376256 | tf_op jit(solution)/shard_map/all_gather | solution.py:207
  25.1 1.3 %multiply_reduce_fusion = (f32[8,512]{1,0:T(8,128)S(1)}, f32[8,512,512]{1,2,0:T(8,128)S(1)}) fusion(bf16[512,8,32]{0,2,1:T(8,128)(2,1)S(1)} %bitcast.104, bf16[512,8,32]{0,2,1:T(8,128)(2,1)S(1)} %bitcast.106), kind=kOutput, calls=%fused_computation.4 | convolution fusion | flops 138407936 | bytes 8929280 | tf_op jit(solution)/shard_map/qhd,khd->hqk/dot_general | solution.py:220
  26.6 1.4 %convert_reduce_fusion = f32[8,512]{1,0:T(8,128)S(1)} fusion(f32[8,512]{1,0:T(8,128)S(1)} %get-tuple-element.56, f32[8,512,512]{1,2,0:T(8,128)S(1)} %get-tuple-element.57), kind=kLoop, calls=%fused_computation.2 | loop fusion | flops 10481664 | bytes 8421376 | tf_op jit(solution)/shard_map/reduce_sum | solution.py:225
  28.0 1.7 %copy-done.1 = f32[8,512,512]{1,2,0:T(8,128)} copy-done((f32[8,512,512]{1,2,0:T(8,128)}, f32[8,512,512]{1,2,0:T(8,128)S(1)}, u32[]{:S(2)}) %copy-start.1) | copy-done | bytes 8388632
  30.3 0.8 collective-permute-start.5
  31.2 2.2 %collective-permute-done.8 = f32[8,512]{1,0:T(8,128)S(1)} collective-permute-done((f32[8,512]{1,0:T(8,128)S(1)}, f32[8,512]{1,0:T(8,128)S(1)}, u32[]{:S(2)}, u32[]{:S(2)}) %collective-permute-start.8) | collective-permute-done | bytes 16416 | tf_op jit(solution)/shard_map/ppermute | solution.py:33
  34.9 4.9 %convolution_convert_fusion.3 = bf16[8,32,512]{2,1,0:T(8,128)(2,1)S(1)} fusion(bf16[512,8,32]{0,2,1:T(8,128)(2,1)S(1)} %bitcast.105, f32[8,512,512]{1,2,0:T(8,128)} %copy-done.1, f32[8,512]{1,0:T(8,128)S(1)} %get-tuple-element.56), kind=kOutput, calls=%fused_computation.36 | convolution fusion | flops 140640256 | bytes 8929280 | tf_op jit(solution)/shard_map/hqk,khd->qhd/dot_general | solution.py:226
  39.8 1.5 %collective-permute-start.2 = (bf16[512,256]{0,1:T(8,128)(2,1)S(1)}, bf16[512,256]{0,1:T(8,128)(2,1)S(1)}, u32[]{:S(2)}, u32[]{:S(2)}) collective-permute-start(bf16[512,256]{0,1:T(8,128)(2,1)S(1)} %bitcast.107), channel_id=1, source_target_pairs={{0,4},{4,0},{8,12},{12,8},{16,20},{20,16},{24,28},{28,24},{1,5},{5... | collective-permute-start | bytes 786440 | tf_op jit(solution)/shard_map/ppermute | solution.py:33
  41.9 2.6 %collective-permute-start.7 = (f32[8,512]{1,0:T(8,128)S(1)}, f32[8,512]{1,0:T(8,128)S(1)}, u32[]{:S(2)}, u32[]{:S(2)}) collective-permute-start(f32[8,512]{1,0:T(8,128)S(1)} %get-tuple-element.47), channel_id=1, source_target_pairs={{0,16},{4,20},{8,24},{12,28},{16,0},{20,4},{24,8},{28,12},{1,17},{... | collective-permute-start | bytes 49160 | tf_op jit(solution)/shard_map/ppermute | solution.py:33
  45.1 4.0 %collective-permute-done.2 = bf16[512,256]{0,1:T(8,128)(2,1)S(1)} collective-permute-done((bf16[512,256]{0,1:T(8,128)(2,1)S(1)}, bf16[512,256]{0,1:T(8,128)(2,1)S(1)}, u32[]{:S(2)}, u32[]{:S(2)}) %collective-permute-start.2) | collective-permute-done | bytes 262176 | tf_op jit(solution)/shard_map/ppermute | solution.py:33
  49.3 1.4 %collective-permute-start.4 = (bf16[512,256]{0,1:T(8,128)(2,1)S(1)}, bf16[512,256]{0,1:T(8,128)(2,1)S(1)}, u32[]{:S(2)}, u32[]{:S(2)}) collective-permute-start(bf16[512,256]{0,1:T(8,128)(2,1)S(1)} %fusion.40), channel_id=1, source_target_pairs={{0,8},{4,12},{8,0},{12,4},{16,24},{20,28},{24,16},{28,20},{1,9},{5... | collective-permute-start | bytes 786440 | tf_op jit(solution)/shard_map/ppermute | solution.py:33
  50.7 4.4 %collective-permute-done.11 = bf16[512,384]{1,0:T(8,128)(2,1)S(1)} collective-permute-done((bf16[512,384]{1,0:T(8,128)(2,1)S(1)}, bf16[512,384]{1,0:T(8,128)(2,1)S(1)}, u32[]{:S(2)}, u32[]{:S(2)}) %collective-permute-start.11) | collective-permute-done | bytes 393248 | tf_op jit(solution)/shard_map/ppermute | solution.py:252
  55.9 3.2 %collective-permute-start.6 = (bf16[512,256]{0,1:T(8,128)(2,1)S(1)}, bf16[512,256]{0,1:T(8,128)(2,1)S(1)}, u32[]{:S(2)}, u32[]{:S(2)}) collective-permute-start(bf16[512,256]{0,1:T(8,128)(2,1)S(1)} %fusion.38), channel_id=1, source_target_pairs={{0,16},{4,20},{8,24},{12,28},{16,0},{20,4},{24,8},{28,12},{1,17},{... | collective-permute-start | bytes 786440 | tf_op jit(solution)/shard_map/ppermute | solution.py:33
  59.5 8.7 %collective-permute-done.6 = bf16[512,256]{0,1:T(8,128)(2,1)S(1)} collective-permute-done((bf16[512,256]{0,1:T(8,128)(2,1)S(1)}, bf16[512,256]{0,1:T(8,128)(2,1)S(1)}, u32[]{:S(2)}, u32[]{:S(2)}) %collective-permute-start.6) | collective-permute-done | bytes 262176 | tf_op jit(solution)/shard_map/ppermute | solution.py:33
  68.7 1.1 %convolution_convert_fusion.2 = bf16[512,256]{1,0:T(8,128)(2,1)} fusion(bf16[256,256]{1,0:T(8,128)(2,1)S(1)} %copy-done.10, bf16[256,256]{1,0:T(8,128)(2,1)S(1)} %copy-done.11, f32[512,256]{0,1:T(8,128)S(1)} %get-tuple-element.59, f32[512]{0:T(512)S(1)} %add_rsqrt_fusion, f32[512]{0:T(512)S(1)} %broadcast_multiply_fusion), kind=kOutput, calls=%fused_computation.35 | convolution fusion | flops 135004160 | bytes 1052672 | tf_op jit(solution)/shard_map/dot_general | solution.py:247
  69.9 2.2 %select_reduce_fusion = (f32[512]{0:T(512)S(1)}, f32[512]{0:T(512)S(1)}, f32[512]{0:T(512)S(1)}, f32[512,1024]{1,0:T(8,128)S(1)}) fusion(s32[1024]{0:T(1024)S(1)} %fusion.33, s32[512]{0:T(512)S(1)} %copy-done.8, pred[512]{0:T(512)(128)(4,1)S(1)} %get-tuple-element.24, bf16[512,256]{1,0:T(8,128)(2,1)} %convolution_convert_fusion.2, ...), kind=kOutput, calls=%fused_computation.17 | convolution fusion | flops 274201088 | bytes 2896384 | tf_op jit(solution)/shard_map/dot_general | solution.py:263
  72.2 3.6 %collective-permute-done.12 = f32[3,512]{1,0:T(4,128)S(1)} collective-permute-done((f32[3,512]{1,0:T(4,128)S(1)}, f32[3,512]{1,0:T(4,128)S(1)}, u32[]{:S(2)}, u32[]{:S(2)}) %collective-permute-start.12) | collective-permute-done | bytes 6176 | tf_op jit(solution)/shard_map/ppermute | solution.py:33
  75.9 1.1 %collective-permute-start.13 = (f32[3,512]{1,0:T(4,128)S(1)}, f32[3,512]{1,0:T(4,128)S(1)}, u32[]{:S(2)}, u32[]{:S(2)}) collective-permute-start(f32[3,512]{1,0:T(4,128)S(1)} %fusion.119), channel_id=1, source_target_pairs={{0,16},{4,20},{8,24},{12,28},{16,0},{20,4},{24,8},{28,12},{1,17},{... | collective-permute-start | bytes 18440 | tf_op jit(solution)/shard_map/ppermute | solution.py:33
  76.9 3.5 %collective-permute-done.13 = f32[3,512]{1,0:T(4,128)S(1)} collective-permute-done((f32[3,512]{1,0:T(4,128)S(1)}, f32[3,512]{1,0:T(4,128)S(1)}, u32[]{:S(2)}, u32[]{:S(2)}) %collective-permute-start.13) | collective-permute-done | bytes 6176 | tf_op jit(solution)/shard_map/ppermute | solution.py:33
  81.1 1.4 %fusion.5 = bf16[512,1024]{1,0:T(8,128)(2,1)S(1)} fusion(f32[512,1024]{1,0:T(8,128)S(1)} %get-tuple-element.60, f32[512]{0:T(512)S(1)} %bitcast.129, f32[512]{0:T(512)S(1)} %bitcast.130, s32[1024]{0:T(1024)S(1)} %fusion.33, f32[512]{0:T(512)S(1)} %get-tuple-element.23, s32[512]{0:T(512)S(1)} %copy-done.8, pred[512]{0:T(512)(128)(4,1)S(1)} %get-tuple-element.24), kind=kLoop, calls=%fused_computation.16 | loop fusion | flops 7340032 | bytes 3158528 | tf_op jit(solution)/shard_map/convert_element_type | solution.py:150
  83.6 7.0 %collective-permute-done.15 = bf16[512,256]{1,0:T(8,128)(2,1)S(1)} collective-permute-done((bf16[512,256]{1,0:T(8,128)(2,1)S(1)}, bf16[512,256]{1,0:T(8,128)(2,1)S(1)}, u32[]{:S(2)}, u32[]{:S(2)}) %collective-permute-start.15) | collective-permute-done | bytes 262176 | tf_op jit(solution)/shard_map/ppermute | solution.py:53
  91.9 8.0 %collective-permute-done.16 = bf16[512,256]{1,0:T(8,128)(2,1)S(1)} collective-permute-done((bf16[512,256]{1,0:T(8,128)(2,1)S(1)}, bf16[512,256]{1,0:T(8,128)(2,1)S(1)}, u32[]{:S(2)}, u32[]{:S(2)}) %collective-permute-start.16) | collective-permute-done | bytes 262176 | tf_op jit(solution)/shard_map/ppermute | solution.py:53
  99.9 0.8 convert_add_fusion
  (104 shorter events, 12.6 us)
Async XLA Ops:
  0.6 18.6 %copy-start = (bf16[1024,256]{1,0:T(8,128)(2,1)S(1)}, bf16[1024,256]{1,0:T(8,128)(2,1)}, u32[]{:S(2)}) copy-start(bf16[1024,256]{1,0:T(8,128)(2,1)} %param.17) | copy-start | bytes 1572868
  0.6 9.3 %copy-start.2 = (bf16[512,256]{1,0:T(8,128)(2,1)S(1)}, bf16[512,256]{1,0:T(8,128)(2,1)}, u32[]{:S(2)}) copy-start(bf16[512,256]{1,0:T(8,128)(2,1)} %param.18) | copy-start | bytes 786436
  0.7 9.3 %copy-start.5 = (bf16[256,256]{1,0:T(8,128)(2,1)S(1)}, bf16[256,256]{1,0:T(8,128)(2,1)}, u32[]{:S(2)}) copy-start(bf16[256,256]{1,0:T(8,128)(2,1)} %param.19) | copy-start | bytes 393220
  3.2 9.6 %collective-permute-start = (bf16[256,512]{1,0:T(8,128)(2,1)S(1)}, bf16[256,512]{1,0:T(8,128)(2,1)S(1)}, u32[]{:S(2)}, u32[]{:S(2)}) collective-permute-start(bf16[256,512]{1,0:T(8,128)(2,1)S(1)} %slice.81), channel_id=1, source_target_pairs={{0,2},{2,4},{4,6},{6,8},{8,10},{10,12},{12,14},{14,16},{16,18},{18... | collective-permute-start | bytes 786440 | tf_op jit(solution)/shard_map/ppermute | solution.py:16
  3.7 9.1 %collective-permute-start.1 = (bf16[256,512]{1,0:T(8,128)(2,1)S(1)}, bf16[256,512]{1,0:T(8,128)(2,1)S(1)}, u32[]{:S(2)}, u32[]{:S(2)}) collective-permute-start(bf16[256,512]{1,0:T(8,128)(2,1)S(1)} %slice.81), channel_id=1, source_target_pairs={{2,0},{4,2},{6,4},{8,6},{10,8},{12,10},{14,12},{16,14},{18,16},{20... | collective-permute-start | bytes 786440 | tf_op jit(solution)/shard_map/ppermute | solution.py:19
  17.5 1.4 %copy-start.6 = (bf16[256,256]{1,0:T(8,128)(2,1)S(1)}, bf16[256,256]{1,0:T(8,128)(2,1)}, u32[]{:S(2)}) copy-start(bf16[256,256]{1,0:T(8,128)(2,1)} %param.15) | copy-start | bytes 393220
  17.5 1.7 %copy-start.9 = (bf16[256,1024]{1,0:T(8,128)(2,1)S(1)}, bf16[256,1024]{1,0:T(8,128)(2,1)}, u32[]{:S(2)}) copy-start(bf16[256,1024]{1,0:T(8,128)(2,1)} %param.16) | copy-start | bytes 1572868
  18.8 1.4 %copy-start.4 = (bf16[256,512]{1,0:T(8,128)(2,1)S(1)}, bf16[256,512]{1,0:T(8,128)(2,1)}, u32[]{:S(2)}) copy-start(bf16[256,512]{1,0:T(8,128)(2,1)} %param.20) | copy-start | bytes 786436
  20.2 6.2 %copy-start.3 = (bf16[256,256]{1,0:T(8,128)(2,1)}, bf16[256,256]{1,0:T(8,128)(2,1)S(1)}, u32[]{:S(2)}) copy-start(bf16[256,256]{1,0:T(8,128)(2,1)S(1)} %copy.59) | copy-start | bytes 393220
  26.4 3.2 %copy-start.1 = (f32[8,512,512]{1,2,0:T(8,128)}, f32[8,512,512]{1,2,0:T(8,128)S(1)}, u32[]{:S(2)}) copy-start(f32[8,512,512]{1,2,0:T(8,128)S(1)} %get-tuple-element.57) | copy-start | bytes 25165828
  26.4 3.8 %collective-permute-start.3 = (f32[8,512]{1,0:T(8,128)S(1)}, f32[8,512]{1,0:T(8,128)S(1)}, u32[]{:S(2)}, u32[]{:S(2)}) collective-permute-start(f32[8,512]{1,0:T(8,128)S(1)} %get-tuple-element.56), channel_id=1, source_target_pairs={{0,4},{4,0},{8,12},{12,8},{16,20},{20,16},{24,28},{28,24},{1,5},{5... | collective-permute-start | bytes 49160 | tf_op jit(solution)/shard_map/ppermute | solution.py:33
  29.6 3.8 %collective-permute-start.8 = (f32[8,512]{1,0:T(8,128)S(1)}, f32[8,512]{1,0:T(8,128)S(1)}, u32[]{:S(2)}, u32[]{:S(2)}) collective-permute-start(f32[8,512]{1,0:T(8,128)S(1)} %convert_reduce_fusion), channel_id=1, source_target_pairs={{0,4},{4,0},{8,12},{12,8},{16,20},{20,16},{24,28},{28,24},{1,5},{5... | collective-permute-start | bytes 49160 | tf_op jit(solution)/shard_map/ppermute | solution.py:33
  30.3 3.8 %collective-permute-start.5 = (f32[8,512]{1,0:T(8,128)S(1)}, f32[8,512]{1,0:T(8,128)S(1)}, u32[]{:S(2)}, u32[]{:S(2)}) collective-permute-start(f32[8,512]{1,0:T(8,128)S(1)} %get-tuple-element.30), channel_id=1, source_target_pairs={{0,8},{4,12},{8,0},{12,4},{16,24},{20,28},{24,16},{28,20},{1,9},{5... | collective-permute-start | bytes 49160 | tf_op jit(solution)/shard_map/ppermute | solution.py:33
  34.1 10.4 %collective-permute-start.9 = (f32[8,512]{1,0:T(8,128)S(1)}, f32[8,512]{1,0:T(8,128)S(1)}, u32[]{:S(2)}, u32[]{:S(2)}) collective-permute-start(f32[8,512]{1,0:T(8,128)S(1)} %get-tuple-element.40), channel_id=1, source_target_pairs={{0,8},{4,12},{8,0},{12,4},{16,24},{20,28},{24,16},{28,20},{1,9},{5... | collective-permute-start | bytes 49160 | tf_op jit(solution)/shard_map/ppermute | solution.py:33
  34.9 10.1 %copy-start.8 = (s32[512]{0:T(512)S(1)}, s32[512]{0:T(512)}, u32[]{:S(2)}) copy-start(s32[512]{0:T(512)} %param.25) | copy-start | bytes 6148
  39.8 9.3 %collective-permute-start.2 = (bf16[512,256]{0,1:T(8,128)(2,1)S(1)}, bf16[512,256]{0,1:T(8,128)(2,1)S(1)}, u32[]{:S(2)}, u32[]{:S(2)}) collective-permute-start(bf16[512,256]{0,1:T(8,128)(2,1)S(1)} %bitcast.107), channel_id=1, source_target_pairs={{0,4},{4,0},{8,12},{12,8},{16,20},{20,16},{24,28},{28,24},{1,5},{5... | collective-permute-start | bytes 786440 | tf_op jit(solution)/shard_map/ppermute | solution.py:33
  41.3 13.9 %collective-permute-start.11 = (bf16[512,384]{1,0:T(8,128)(2,1)S(1)}, bf16[512,384]{1,0:T(8,128)(2,1)S(1)}, u32[]{:S(2)}, u32[]{:S(2)}) collective-permute-start(bf16[512,384]{1,0:T(8,128)(2,1)S(1)} %slice.90), channel_id=1, source_target_pairs={{0,4},{4,0},{8,12},{12,8},{16,20},{20,16},{24,28},{28,24},{1,5},{5... | collective-permute-start | bytes 1179656 | tf_op jit(solution)/shard_map/ppermute | solution.py:252
  41.9 8.8 %collective-permute-start.7 = (f32[8,512]{1,0:T(8,128)S(1)}, f32[8,512]{1,0:T(8,128)S(1)}, u32[]{:S(2)}, u32[]{:S(2)}) collective-permute-start(f32[8,512]{1,0:T(8,128)S(1)} %get-tuple-element.47), channel_id=1, source_target_pairs={{0,16},{4,20},{8,24},{12,28},{16,0},{20,4},{24,8},{28,12},{1,17},{... | collective-permute-start | bytes 49160 | tf_op jit(solution)/shard_map/ppermute | solution.py:33
  44.5 6.2 %collective-permute-start.10 = (f32[8,512]{1,0:T(8,128)S(1)}, f32[8,512]{1,0:T(8,128)S(1)}, u32[]{:S(2)}, u32[]{:S(2)}) collective-permute-start(f32[8,512]{1,0:T(8,128)S(1)} %get-tuple-element.42), channel_id=1, source_target_pairs={{0,16},{4,20},{8,24},{12,28},{16,0},{20,4},{24,8},{28,12},{1,17},{... | collective-permute-start | bytes 49160 | tf_op jit(solution)/shard_map/ppermute | solution.py:33
  49.3 19.1 %copy-start.7 = (bf16[256,256]{1,0:T(8,128)(2,1)S(1)}, bf16[256,256]{1,0:T(8,128)(2,1)}, u32[]{:S(2)}) copy-start(bf16[256,256]{1,0:T(8,128)(2,1)} %param.21) | copy-start | bytes 393220
  49.3 6.4 %collective-permute-start.4 = (bf16[512,256]{0,1:T(8,128)(2,1)S(1)}, bf16[512,256]{0,1:T(8,128)(2,1)S(1)}, u32[]{:S(2)}, u32[]{:S(2)}) collective-permute-start(bf16[512,256]{0,1:T(8,128)(2,1)S(1)} %fusion.40), channel_id=1, source_target_pairs={{0,8},{4,12},{8,0},{12,4},{16,24},{20,28},{24,16},{28,20},{1,9},{5... | collective-permute-start | bytes 786440 | tf_op jit(solution)/shard_map/ppermute | solution.py:33
  55.5 13.3 %copy-start.10 = (bf16[256,256]{1,0:T(8,128)(2,1)S(1)}, bf16[256,256]{1,0:T(8,128)(2,1)}, u32[]{:S(2)}) copy-start(bf16[256,256]{1,0:T(8,128)(2,1)} %param.23) | copy-start | bytes 393220
  55.5 13.3 %copy-start.11 = (bf16[256,256]{1,0:T(8,128)(2,1)S(1)}, bf16[256,256]{1,0:T(8,128)(2,1)}, u32[]{:S(2)}) copy-start(bf16[256,256]{1,0:T(8,128)(2,1)} %param.22) | copy-start | bytes 393220
  55.9 12.3 %collective-permute-start.6 = (bf16[512,256]{0,1:T(8,128)(2,1)S(1)}, bf16[512,256]{0,1:T(8,128)(2,1)S(1)}, u32[]{:S(2)}, u32[]{:S(2)}) collective-permute-start(bf16[512,256]{0,1:T(8,128)(2,1)S(1)} %fusion.38), channel_id=1, source_target_pairs={{0,16},{4,20},{8,24},{12,28},{16,0},{20,4},{24,8},{28,12},{1,17},{... | collective-permute-start | bytes 786440 | tf_op jit(solution)/shard_map/ppermute | solution.py:33
  72.1 3.7 %collective-permute-start.12 = (f32[3,512]{1,0:T(4,128)S(1)}, f32[3,512]{1,0:T(4,128)S(1)}, u32[]{:S(2)}, u32[]{:S(2)}) collective-permute-start(f32[3,512]{1,0:T(4,128)S(1)} %pad_maximum_fusion.1), channel_id=1, source_target_pairs={{0,8},{4,12},{8,0},{12,4},{16,24},{20,28},{24,16},{28,20},{1,9},{5... | collective-permute-start | bytes 18440 | tf_op jit(solution)/shard_map/ppermute | solution.py:33
  75.9 4.6 %collective-permute-start.13 = (f32[3,512]{1,0:T(4,128)S(1)}, f32[3,512]{1,0:T(4,128)S(1)}, u32[]{:S(2)}, u32[]{:S(2)}) collective-permute-start(f32[3,512]{1,0:T(4,128)S(1)} %fusion.119), channel_id=1, source_target_pairs={{0,16},{4,20},{8,24},{12,28},{16,0},{20,4},{24,8},{28,12},{1,17},{... | collective-permute-start | bytes 18440 | tf_op jit(solution)/shard_map/ppermute | solution.py:33
  81.1 2.0 %copy-start.12 = (bf16[512,256]{1,0:T(8,128)(2,1)S(1)}, bf16[512,256]{1,0:T(8,128)(2,1)}, u32[]{:S(2)}) copy-start(bf16[512,256]{1,0:T(8,128)(2,1)} %convolution_convert_fusion.2) | copy-start | bytes 786436
  82.9 7.7 %collective-permute-start.15 = (bf16[512,256]{1,0:T(8,128)(2,1)S(1)}, bf16[512,256]{1,0:T(8,128)(2,1)S(1)}, u32[]{:S(2)}, u32[]{:S(2)}) collective-permute-start(bf16[512,256]{1,0:T(8,128)(2,1)S(1)} %convolution_convert_fusion.1), channel_id=1, source_target_pairs={{0,8},{4,12},{8,0},{12,4},{16,24},{20,28},{24,16},{28,20},{1,9},{5... | collective-permute-start | bytes 786440 | tf_op jit(solution)/shard_map/ppermute | solution.py:53
  83.5 7.6 %collective-permute-start.14 = (f32[256,256]{1,0:T(8,128)S(1)}, f32[256,256]{1,0:T(8,128)S(1)}, u32[]{:S(2)}, u32[]{:S(2)}) collective-permute-start(f32[256,256]{1,0:T(8,128)S(1)} %slice_select_fusion.2), channel_id=1, source_target_pairs={{0,2},{2,0},{1,3},{3,1},{4,6},{6,4},{5,7},{7,5},{8,10},{10,8},{9,1... | collective-permute-start | bytes 786440 | tf_op jit(solution)/shard_map/ppermute | solution.py:85
  90.7 9.2 %collective-permute-start.16 = (bf16[512,256]{1,0:T(8,128)(2,1)S(1)}, bf16[512,256]{1,0:T(8,128)(2,1)S(1)}, u32[]{:S(2)}, u32[]{:S(2)}) collective-permute-start(bf16[512,256]{1,0:T(8,128)(2,1)S(1)} %add_convert_fusion), channel_id=1, source_target_pairs={{0,16},{4,20},{8,24},{12,28},{16,0},{20,4},{24,8},{28,12},{1,17},{... | collective-permute-start | bytes 786440 | tf_op jit(solution)/shard_map/ppermute | solution.py:53

commit v11 on v10

--- a/solution.py
+++ b/solution.py
@@ -175,7 +175,7 @@
     normed = norm_rows(hits).astype(jnp.bfloat16)
     projected = jnp.dot(normed, enc_qkv, preferred_element_type=jnp.float32).astype(jnp.bfloat16)
     extended = extended_2(projected[:, model_width:], ((("phi", "query"), 0),), WIN // 2)
-    block_rows = local_hits // 2
+    block_rows = local_hits // 4
     span = extended.shape[0] - local_hits
     attended = jnp.concatenate(
         [
@@ -183,7 +183,7 @@
                 projected[b * block_rows : (b + 1) * block_rows, :model_width],
                 extended[b * block_rows : b * block_rows + block_rows + span],
             )
-            for b in range(2)
+            for b in range(4)
         ]
     )
     residual = hits.astype(jnp.float32) + jnp.dot(

time: 101 us -> 115 us (1.14)
  local copies, waits for them, and re-layouts: 4.73 us -> 14.4 us
  matrix products: 18.5 us -> 26.3 us
  waiting for transfers between devices: 45.3 us -> 39.7 us
  starting transfers between devices: 19.2 us -> 21.4 us
    sub x2 -> x4, matrix products: 2.28 us -> 9.74 us  [window_attend(): raised = jnp.exp(scores - jnp.max(scores, axis=-1, keepdims=True))]
    ppermute x1, waiting for transfers between devices: 4.45 us -> 0.01 us  [body(): lax.ppermute(own_payload, 'phi', partner_pairs(lax.axis_size('phi'), 1))]
    ppermute x11, waiting for transfers between devices: 23.2 us -> 26 us  [butterfly(): other = lax.ppermute(tree, axis, partner_pairs(count, distance))]
    slice x3 -> x5, local copies, waits for them, and re-layouts: 0.24 us -> 2.93 us  [body(): projected[b * block_rows:(b + 1) * block_rows, :model_width]]
    unnamed x29 -> x51, local copies, waits for them, and re-layouts: 3.07 us -> 5.73 us
    slice x3 -> x5, local copies, waits for them, and re-layouts: 0.49 us -> 3.1 us  [window_attend(): key_heads = kv_ext[:, :model_width].reshape(key_count, HEADS, head_size)]
    ppermute x1, waiting for transfers between devices: 2.6 us -> 0.01 us  [extended_2(): lax.ppermute(lax.slice_in_dim(block, block.shape[dim] - width, None, axis...]
    ppermute x2, starting transfers between devices: 0.68 us -> 2.15 us  [narrow_butterfly(): other = lax.ppermute(sent, axis, partner_pairs(count, distance))]
  transfers between devices with their start and end apart: 17 -> 17, of which waited for: 12 -> 10; matrix products, arithmetic and copies ran while one was open for 10% -> 12% of each run, Pallas kernels for 0% -> 0%
where the time goes in v11:
time: 115 us; the launch traced here: 114 us
  waiting for transfers between devices  39.7 us (35%)
  matrix products  26.3 us (23%)
  starting transfers between devices  21.4 us (19%)
  local copies, waits for them, and re-layouts  14.4 us (13%)
  other arithmetic  7.45 us (6%)
  blocking collectives  3.77 us (3%)
  between operations  1.2 us (1%)
    ppermute x11, waiting for transfers between devices, butterfly(): other = lax.ppermute(tree, axis, partner_pairs(count, distance))  26 us
    ppermute x2, waiting for transfers between devices, narrow_butterfly(): other = lax.ppermute(sent, axis, partner_pairs(count, distance))  13.7 us
    ppermute x11, starting transfers between devices, butterfly(): other = lax.ppermute(tree, axis, partner_pairs(count, distance))  12.2 us
    sub x4, matrix products, window_attend(): raised = jnp.exp(scores - jnp.max(scores, axis=-1, keepdims=True))  9.74 us
    unnamed x51, local copies, waits for them, and re-layouts  5.73 us
    ppermute x1, starting transfers between devices, extended_2(): lax.ppermute(lax.slice_in_dim(block, 0, width, axis=dim), axis, backward)  5.03 us
    dot_general x1, matrix products, body(): jnp.einsum('hqk,khd->qhd', raised, value_heads, preferred_element_type=jn...  4.9 us
    all_gather x1, blocking collectives, body(): lax.all_gather(jnp.concatenate([local_kv, encoded, digits], axis=1), 'que...  3.77 us
  transfers between devices with their start and end apart: 17, of which 10 were waited for; matrix products, arithmetic and copies ran while one was open for 12% of the time, Pallas kernels for 0%

profile of v11, /device:TPU:0, one launch (start us, length us, event | category | flops | bytes accessed | tf_op | source)
XLA Modules:
  0.0 114.2 jit_solution(10683384494576929915)
XLA Ops:
  0.7 1.1 copy.58
  1.9 1.3 %convolution_convert_fusion = bf16[256,768]{1,0:T(8,128)(2,1)S(1)} fusion(bf16[256,768]{1,0:T(8,128)(2,1)} %param.14, bf16[256,256]{0,1:T(8,128)(2,1)S(1)} %copy.58, f32[256]{0:T(256)S(1)} %add_rsqrt_fusion.3, f32[256]{0:T(256)S(1)} %broadcast_multiply_fusion.3), kind=kOutput, calls=%fused_computation.37 | convolution fusion | flops 101122048 | bytes 919552 | tf_op jit(solution)/shard_map/dot_general | solution.py:176
  3.7 5.0 %collective-permute-start.1 = (bf16[256,512]{1,0:T(8,128)(2,1)S(1)}, bf16[256,512]{1,0:T(8,128)(2,1)S(1)}, u32[]{:S(2)}, u32[]{:S(2)}) collective-permute-start(bf16[256,512]{1,0:T(8,128)(2,1)S(1)} %slice.111), channel_id=1, source_target_pairs={{2,0},{4,2},{6,4},{8,6},{10,8},{12,10},{14,12},{16,14},{18,16},{20... | collective-permute-start | bytes 786440 | tf_op jit(solution)/shard_map/ppermute | solution.py:19
  13.7 0.9 copy.61
  18.2 2.7 %fusion.130 = (f32[8,64]{1,0:T(8,128)S(1)}, f32[8,64,576]{2,1,0:T(8,128)}) fusion(bf16[64,8,32]{0,2,1:T(8,128)(2,1)S(1)} %bitcast.133, bf16[576,8,32]{0,2,1:T(8,128)(2,1)} %bitcast.129, pred[64,576]{1,0:T(8,128)(4,1)} %fusion.66), kind=kOutput, calls=%fused_computation.215 | convolution fusion | flops 20054592 | bytes 1546240 | tf_op jit(solution)/shard_map/sub | solution.py:113
  20.9 2.7 %fusion.129 = (f32[8,64]{1,0:T(8,128)S(1)}, f32[8,64,576]{2,1,0:T(8,128)}) fusion(bf16[64,8,32]{0,2,1:T(8,128)(2,1)S(1)} %bitcast.132, bf16[576,8,32]{0,2,1:T(8,128)(2,1)} %bitcast.128, pred[64,576]{1,0:T(8,128)(4,1)S(1)} %copy-done.13), kind=kOutput, calls=%fused_computation.214 | convolution fusion | flops 20054592 | bytes 1546240 | tf_op jit(solution)/shard_map/sub | solution.py:113
  23.6 1.7 %fusion.128 = (f32[8,64]{1,0:T(8,128)S(1)}, f32[8,64,576]{2,1,0:T(8,128)}) fusion(bf16[64,8,32]{0,2,1:T(8,128)(2,1)S(1)} %bitcast.131, bf16[576,8,32]{0,2,1:T(8,128)(2,1)S(1)} %bitcast.127, pred[64,576]{1,0:T(8,128)(4,1)S(1)} %copy-done.13), kind=kOutput, calls=%fused_computation.213 | convolution fusion | flops 20054592 | bytes 1546240 | tf_op jit(solution)/shard_map/sub | solution.py:113
  25.2 2.7 %fusion.127 = (f32[8,64]{1,0:T(8,128)S(1)}, f32[8,64,576]{2,1,0:T(8,128)}) fusion(bf16[64,8,32]{0,2,1:T(8,128)(2,1)S(1)} %bitcast.130, bf16[576,8,32]{0,2,1:T(8,128)(2,1)} %bitcast.126, pred[64,576]{1,0:T(8,128)(4,1)S(1)} %copy-done.13), kind=kOutput, calls=%fused_computation.212 | convolution fusion | flops 20054592 | bytes 1546240 | tf_op jit(solution)/shard_map/sub | solution.py:113
  27.9 1.8 %convolution_convert_fusion.9 = bf16[8,32,64]{2,1,0:T(8,128)(2,1)S(1)} fusion(bf16[576,8,32]{0,2,1:T(8,128)(2,1)S(1)} %bitcast.125, f32[8,64,576]{2,1,0:T(8,128)} %get-tuple-element.65, f32[8,64]{1,0:T(8,128)S(1)} %get-tuple-element.64), kind=kOutput, calls=%fused_computation.52 | convolution fusion | flops 19480576 | bytes 1509376 | tf_op jit(solution)/shard_map/hqk,khd->qhd/dot_general | solution.py:115
  31.5 0.9 copy-done.23
  35.4 3.8 %all_gather.3 = bf16[512,896]{1,0:T(8,128)(2,1)S(1)} all-gather(bf16[256,896]{1,0:T(8,128)(2,1)S(1)} %fusion.50), channel_id=1, replica_groups=mesh['phi'=8,'query'=2,'event'=2] {'query'}, dimensions={0}, use_global_device_ids=true | all-gather | bytes 1376256 | tf_op jit(solution)/shard_map/all_gather | solution.py:207
  39.4 1.3 %multiply_reduce_fusion = (f32[8,512]{1,0:T(8,128)S(1)}, f32[8,512,512]{1,2,0:T(8,128)S(1)}) fusion(bf16[512,8,32]{0,2,1:T(8,128)(2,1)S(1)} %bitcast.118, bf16[512,8,32]{0,2,1:T(8,128)(2,1)S(1)} %bitcast.120), kind=kOutput, calls=%fused_computation.6 | convolution fusion | flops 138407936 | bytes 8929280 | tf_op jit(solution)/shard_map/qhd,khd->hqk/dot_general | solution.py:220
  40.8 1.4 %convert_reduce_fusion = f32[8,512]{1,0:T(8,128)S(1)} fusion(f32[8,512]{1,0:T(8,128)S(1)} %get-tuple-element.70, f32[8,512,512]{1,2,0:T(8,128)S(1)} %get-tuple-element.71), kind=kLoop, calls=%fused_computation.4 | loop fusion | flops 10481664 | bytes 8421376 | tf_op jit(solution)/shard_map/reduce_sum | solution.py:225
  42.2 1.7 %copy-done.1 = f32[8,512,512]{1,2,0:T(8,128)} copy-done((f32[8,512,512]{1,2,0:T(8,128)}, f32[8,512,512]{1,2,0:T(8,128)S(1)}, u32[]{:S(2)}) %copy-start.1) | copy-done | bytes 8388632
  45.3 1.5 %collective-permute-start.11 = (bf16[512,384]{1,0:T(8,128)(2,1)S(1)}, bf16[512,384]{1,0:T(8,128)(2,1)S(1)}, u32[]{:S(2)}, u32[]{:S(2)}) collective-permute-start(bf16[512,384]{1,0:T(8,128)(2,1)S(1)} %slice.126), channel_id=1, source_target_pairs={{0,4},{4,0},{8,12},{12,8},{16,20},{20,16},{24,28},{28,24},{1,5},{5... | collective-permute-start | bytes 1179656 | tf_op jit(solution)/shard_map/ppermute | solution.py:252
  49.1 4.9 %convolution_convert_fusion.3 = bf16[8,32,512]{2,1,0:T(8,128)(2,1)S(1)} fusion(bf16[512,8,32]{0,2,1:T(8,128)(2,1)S(1)} %bitcast.119, f32[8,512,512]{1,2,0:T(8,128)} %copy-done.1, f32[8,512]{1,0:T(8,128)S(1)} %get-tuple-element.70), kind=kOutput, calls=%fused_computation.42 | convolution fusion | flops 140640256 | bytes 8929280 | tf_op jit(solution)/shard_map/hqk,khd->qhd/dot_general | solution.py:226
  54.0 1.5 %collective-permute-start.2 = (bf16[512,256]{0,1:T(8,128)(2,1)S(1)}, bf16[512,256]{0,1:T(8,128)(2,1)S(1)}, u32[]{:S(2)}, u32[]{:S(2)}) collective-permute-start(bf16[512,256]{0,1:T(8,128)(2,1)S(1)} %bitcast.121), channel_id=1, source_target_pairs={{0,4},{4,0},{8,12},{12,8},{16,20},{20,16},{24,28},{28,24},{1,5},{5... | collective-permute-start | bytes 786440 | tf_op jit(solution)/shard_map/ppermute | solution.py:33
  55.5 2.6 %collective-permute-start.7 = (f32[8,512]{1,0:T(8,128)S(1)}, f32[8,512]{1,0:T(8,128)S(1)}, u32[]{:S(2)}, u32[]{:S(2)}) collective-permute-start(f32[8,512]{1,0:T(8,128)S(1)} %get-tuple-element.53), channel_id=1, source_target_pairs={{0,16},{4,20},{8,24},{12,28},{16,0},{20,4},{24,8},{28,12},{1,17},{... | collective-permute-start | bytes 49160 | tf_op jit(solution)/shard_map/ppermute | solution.py:33
  58.7 3.1 %collective-permute-done.2 = bf16[512,256]{0,1:T(8,128)(2,1)S(1)} collective-permute-done((bf16[512,256]{0,1:T(8,128)(2,1)S(1)}, bf16[512,256]{0,1:T(8,128)(2,1)S(1)}, u32[]{:S(2)}, u32[]{:S(2)}) %collective-permute-start.2) | collective-permute-done | bytes 262176 | tf_op jit(solution)/shard_map/ppermute | solution.py:33
  62.0 1.1 collective-permute-start.4
  63.4 5.4 %collective-permute-done.4 = bf16[512,256]{0,1:T(8,128)(2,1)S(1)} collective-permute-done((bf16[512,256]{0,1:T(8,128)(2,1)S(1)}, bf16[512,256]{0,1:T(8,128)(2,1)S(1)}, u32[]{:S(2)}, u32[]{:S(2)}) %collective-permute-start.4) | collective-permute-done | bytes 262176 | tf_op jit(solution)/shard_map/ppermute | solution.py:33
  69.0 3.1 %collective-permute-start.6 = (bf16[512,256]{0,1:T(8,128)(2,1)S(1)}, bf16[512,256]{0,1:T(8,128)(2,1)S(1)}, u32[]{:S(2)}, u32[]{:S(2)}) collective-permute-start(bf16[512,256]{0,1:T(8,128)(2,1)S(1)} %fusion.40), channel_id=1, source_target_pairs={{0,16},{4,20},{8,24},{12,28},{16,0},{20,4},{24,8},{28,12},{1,17},{... | collective-permute-start | bytes 786440 | tf_op jit(solution)/shard_map/ppermute | solution.py:33
  72.5 9.0 %collective-permute-done.6 = bf16[512,256]{0,1:T(8,128)(2,1)S(1)} collective-permute-done((bf16[512,256]{0,1:T(8,128)(2,1)S(1)}, bf16[512,256]{0,1:T(8,128)(2,1)S(1)}, u32[]{:S(2)}, u32[]{:S(2)}) %collective-permute-start.6) | collective-permute-done | bytes 262176 | tf_op jit(solution)/shard_map/ppermute | solution.py:33
  82.1 1.1 convolution_convert_fusion.2
  83.2 2.2 %select_reduce_fusion = (f32[512]{0:T(512)S(1)}, f32[512]{0:T(512)S(1)}, f32[512]{0:T(512)S(1)}, f32[512,1024]{1,0:T(8,128)S(1)}) fusion(s32[1024]{0:T(1024)S(1)} %fusion.35, s32[512]{0:T(512)S(1)} %copy-done.14, pred[512]{0:T(512)(128)(4,1)S(1)} %get-tuple-element.24, bf16[512,256]{1,0:T(8,128)(2,1)} %convolution_convert_fusion.2, ...), kind=kOutput, calls=%fused_computation.13 | convolution fusion | flops 274201088 | bytes 2896384 | tf_op jit(solution)/shard_map/dot_general | solution.py:263
  85.5 3.6 %collective-permute-done.12 = f32[3,512]{1,0:T(4,128)S(1)} collective-permute-done((f32[3,512]{1,0:T(4,128)S(1)}, f32[3,512]{1,0:T(4,128)S(1)}, u32[]{:S(2)}, u32[]{:S(2)}) %collective-permute-start.12) | collective-permute-done | bytes 6176 | tf_op jit(solution)/shard_map/ppermute | solution.py:33
  89.2 1.4 %collective-permute-start.13 = (f32[3,512]{1,0:T(4,128)S(1)}, f32[3,512]{1,0:T(4,128)S(1)}, u32[]{:S(2)}, u32[]{:S(2)}) collective-permute-start(f32[3,512]{1,0:T(4,128)S(1)} %fusion.119), channel_id=1, source_target_pairs={{0,16},{4,20},{8,24},{12,28},{16,0},{20,4},{24,8},{28,12},{1,17},{... | collective-permute-start | bytes 18440 | tf_op jit(solution)/shard_map/ppermute | solution.py:33
  90.6 3.2 %collective-permute-done.13 = f32[3,512]{1,0:T(4,128)S(1)} collective-permute-done((f32[3,512]{1,0:T(4,128)S(1)}, f32[3,512]{1,0:T(4,128)S(1)}, u32[]{:S(2)}, u32[]{:S(2)}) %collective-permute-start.13) | collective-permute-done | bytes 6176 | tf_op jit(solution)/shard_map/ppermute | solution.py:33
  94.4 1.4 %fusion.7 = bf16[512,1024]{1,0:T(8,128)(2,1)S(1)} fusion(f32[512,1024]{1,0:T(8,128)S(1)} %get-tuple-element.74, f32[512]{0:T(512)S(1)} %bitcast.143, f32[512]{0:T(512)S(1)} %bitcast.144, s32[1024]{0:T(1024)S(1)} %fusion.35, f32[512]{0:T(512)S(1)} %get-tuple-element.23, s32[512]{0:T(512)S(1)} %copy-done.14, pred[512]{0:T(512)(128)(4,1)S(1)} %get-tuple-element.24), kind=kLoop, calls=%fused_computation.12 | loop fusion | flops 7340032 | bytes 3158528 | tf_op jit(solution)/shard_map/convert_element_type | solution.py:150
  97.3 6.2 %collective-permute-done.15 = bf16[512,256]{1,0:T(8,128)(2,1)S(1)} collective-permute-done((bf16[512,256]{1,0:T(8,128)(2,1)S(1)}, bf16[512,256]{1,0:T(8,128)(2,1)S(1)}, u32[]{:S(2)}, u32[]{:S(2)}) %collective-permute-start.15) | collective-permute-done | bytes 262176 | tf_op jit(solution)/shard_map/ppermute | solution.py:53
  103.5 1.6 %collective-permute-start.16 = (bf16[512,256]{1,0:T(8,128)(2,1)S(1)}, bf16[512,256]{1,0:T(8,128)(2,1)S(1)}, u32[]{:S(2)}, u32[]{:S(2)}) collective-permute-start(bf16[512,256]{1,0:T(8,128)(2,1)S(1)} %add_convert_fusion), channel_id=1, source_target_pairs={{0,16},{4,20},{8,24},{12,28},{16,0},{20,4},{24,8},{28,12},{1,17},{... | collective-permute-start | bytes 786440 | tf_op jit(solution)/shard_map/ppermute | solution.py:53
  105.9 7.5 %collective-permute-done.16 = bf16[512,256]{1,0:T(8,128)(2,1)S(1)} collective-permute-done((bf16[512,256]{1,0:T(8,128)(2,1)S(1)}, bf16[512,256]{1,0:T(8,128)(2,1)S(1)}, u32[]{:S(2)}, u32[]{:S(2)}) %collective-permute-start.16) | collective-permute-done | bytes 262176 | tf_op jit(solution)/shard_map/ppermute | solution.py:53
  (136 shorter events, 23.7 us)
Async XLA Ops:
  0.6 33.1 %copy-start = (bf16[1024,256]{1,0:T(8,128)(2,1)S(1)}, bf16[1024,256]{1,0:T(8,128)(2,1)}, u32[]{:S(2)}) copy-start(bf16[1024,256]{1,0:T(8,128)(2,1)} %param.17) | copy-start | bytes 1572868
  0.6 8.8 %copy-start.15 = (s32[256]{0:T(256)S(1)}, s32[256]{0:T(256)}, u32[]{:S(2)}) copy-start(s32[256]{0:T(256)} %param.24) | copy-start | bytes 3076
  0.7 12.5 %copy-start.2 = (bf16[512,256]{1,0:T(8,128)(2,1)S(1)}, bf16[512,256]{1,0:T(8,128)(2,1)}, u32[]{:S(2)}) copy-start(bf16[512,256]{1,0:T(8,128)(2,1)} %param.18) | copy-start | bytes 786436
  0.7 12.5 %copy-start.7 = (bf16[256,256]{1,0:T(8,128)(2,1)S(1)}, bf16[256,256]{1,0:T(8,128)(2,1)}, u32[]{:S(2)}) copy-start(bf16[256,256]{1,0:T(8,128)(2,1)} %param.19) | copy-start | bytes 393220
  3.2 10.2 %collective-permute-start = (bf16[256,512]{1,0:T(8,128)(2,1)S(1)}, bf16[256,512]{1,0:T(8,128)(2,1)S(1)}, u32[]{:S(2)}, u32[]{:S(2)}) collective-permute-start(bf16[256,512]{1,0:T(8,128)(2,1)S(1)} %slice.111), channel_id=1, source_target_pairs={{0,2},{2,4},{4,6},{6,8},{8,10},{10,12},{12,14},{14,16},{16,18},{18... | collective-permute-start | bytes 786440 | tf_op jit(solution)/shard_map/ppermute | solution.py:16
  3.7 9.7 %collective-permute-start.1 = (bf16[256,512]{1,0:T(8,128)(2,1)S(1)}, bf16[256,512]{1,0:T(8,128)(2,1)S(1)}, u32[]{:S(2)}, u32[]{:S(2)}) collective-permute-start(bf16[256,512]{1,0:T(8,128)(2,1)S(1)} %slice.111), channel_id=1, source_target_pairs={{2,0},{4,2},{6,4},{8,6},{10,8},{12,10},{14,12},{16,14},{18,16},{20... | collective-permute-start | bytes 786440 | tf_op jit(solution)/shard_map/ppermute | solution.py:19
  17.0 3.8 %copy-start.11 = (bf16[64,256]{0,1:T(8,128)(2,1)S(1)}, bf16[64,256]{0,1:T(8,128)(2,1)}, u32[]{:S(2)}) copy-start(bf16[64,256]{0,1:T(8,128)(2,1)} %copy.63) | copy-start | bytes 98308
  17.0 3.8 %copy-start.13 = (pred[64,576]{1,0:T(8,128)(4,1)S(1)}, pred[64,576]{1,0:T(8,128)(4,1)}, u32[]{:S(2)}) copy-start(pred[64,576]{1,0:T(8,128)(4,1)} %fusion.66) | copy-start | bytes 110596
  18.2 5.4 %copy-start.10 = (bf16[64,256]{0,1:T(8,128)(2,1)S(1)}, bf16[64,256]{0,1:T(8,128)(2,1)}, u32[]{:S(2)}) copy-start(bf16[64,256]{0,1:T(8,128)(2,1)} %copy.66) | copy-start | bytes 98308
  20.9 4.4 %copy-start.9 = (bf16[64,256]{0,1:T(8,128)(2,1)S(1)}, bf16[64,256]{0,1:T(8,128)(2,1)}, u32[]{:S(2)}) copy-start(bf16[64,256]{0,1:T(8,128)(2,1)} %copy.69) | copy-start | bytes 98308
  25.2 2.7 %copy-start.4 = (bf16[576,256]{0,1:T(8,128)(2,1)S(1)}, bf16[576,256]{0,1:T(8,128)(2,1)}, u32[]{:S(2)}) copy-start(bf16[576,256]{0,1:T(8,128)(2,1)} %copy.59) | copy-start | bytes 884740
  27.9 1.8 %copy-start.21 = (f32[8,64,576]{2,1,0:T(8,128)S(1)}, f32[8,64,576]{2,1,0:T(8,128)}, u32[]{:S(2)}) copy-start(f32[8,64,576]{2,1,0:T(8,128)} %get-tuple-element.63) | copy-start | bytes 3538948
  40.7 3.2 %copy-start.1 = (f32[8,512,512]{1,2,0:T(8,128)}, f32[8,512,512]{1,2,0:T(8,128)S(1)}, u32[]{:S(2)}) copy-start(f32[8,512,512]{1,2,0:T(8,128)S(1)} %get-tuple-element.71) | copy-start | bytes 25165828
  40.7 3.8 %collective-permute-start.3 = (f32[8,512]{1,0:T(8,128)S(1)}, f32[8,512]{1,0:T(8,128)S(1)}, u32[]{:S(2)}, u32[]{:S(2)}) collective-permute-start(f32[8,512]{1,0:T(8,128)S(1)} %get-tuple-element.70), channel_id=1, source_target_pairs={{0,4},{4,0},{8,12},{12,8},{16,20},{20,16},{24,28},{28,24},{1,5},{5... | collective-permute-start | bytes 49160 | tf_op jit(solution)/shard_map/ppermute | solution.py:33
  43.9 3.8 %collective-permute-start.8 = (f32[8,512]{1,0:T(8,128)S(1)}, f32[8,512]{1,0:T(8,128)S(1)}, u32[]{:S(2)}, u32[]{:S(2)}) collective-permute-start(f32[8,512]{1,0:T(8,128)S(1)} %convert_reduce_fusion), channel_id=1, source_target_pairs={{0,4},{4,0},{8,12},{12,8},{16,20},{20,16},{24,28},{28,24},{1,5},{5... | collective-permute-start | bytes 49160 | tf_op jit(solution)/shard_map/ppermute | solution.py:33
  44.5 3.8 %collective-permute-start.5 = (f32[8,512]{1,0:T(8,128)S(1)}, f32[8,512]{1,0:T(8,128)S(1)}, u32[]{:S(2)}, u32[]{:S(2)}) collective-permute-start(f32[8,512]{1,0:T(8,128)S(1)} %get-tuple-element.30), channel_id=1, source_target_pairs={{0,8},{4,12},{8,0},{12,4},{16,24},{20,28},{24,16},{28,20},{1,9},{5... | collective-permute-start | bytes 49160 | tf_op jit(solution)/shard_map/ppermute | solution.py:33
  45.3 17.8 %collective-permute-start.11 = (bf16[512,384]{1,0:T(8,128)(2,1)S(1)}, bf16[512,384]{1,0:T(8,128)(2,1)S(1)}, u32[]{:S(2)}, u32[]{:S(2)}) collective-permute-start(bf16[512,384]{1,0:T(8,128)(2,1)S(1)} %slice.126), channel_id=1, source_target_pairs={{0,4},{4,0},{8,12},{12,8},{16,20},{20,16},{24,28},{28,24},{1,5},{5... | collective-permute-start | bytes 1179656 | tf_op jit(solution)/shard_map/ppermute | solution.py:252
  48.3 9.8 %collective-permute-start.9 = (f32[8,512]{1,0:T(8,128)S(1)}, f32[8,512]{1,0:T(8,128)S(1)}, u32[]{:S(2)}, u32[]{:S(2)}) collective-permute-start(f32[8,512]{1,0:T(8,128)S(1)} %get-tuple-element.46), channel_id=1, source_target_pairs={{0,8},{4,12},{8,0},{12,4},{16,24},{20,28},{24,16},{28,20},{1,9},{5... | collective-permute-start | bytes 49160 | tf_op jit(solution)/shard_map/ppermute | solution.py:33
  49.1 9.4 %copy-start.14 = (s32[512]{0:T(512)S(1)}, s32[512]{0:T(512)}, u32[]{:S(2)}) copy-start(s32[512]{0:T(512)} %param.25) | copy-start | bytes 6148
  54.0 7.8 %collective-permute-start.2 = (bf16[512,256]{0,1:T(8,128)(2,1)S(1)}, bf16[512,256]{0,1:T(8,128)(2,1)S(1)}, u32[]{:S(2)}, u32[]{:S(2)}) collective-permute-start(bf16[512,256]{0,1:T(8,128)(2,1)S(1)} %bitcast.121), channel_id=1, source_target_pairs={{0,4},{4,0},{8,12},{12,8},{16,20},{20,16},{24,28},{28,24},{1,5},{5... | collective-permute-start | bytes 786440 | tf_op jit(solution)/shard_map/ppermute | solution.py:33
  55.5 7.6 %collective-permute-start.7 = (f32[8,512]{1,0:T(8,128)S(1)}, f32[8,512]{1,0:T(8,128)S(1)}, u32[]{:S(2)}, u32[]{:S(2)}) collective-permute-start(f32[8,512]{1,0:T(8,128)S(1)} %get-tuple-element.53), channel_id=1, source_target_pairs={{0,16},{4,20},{8,24},{12,28},{16,0},{20,4},{24,8},{28,12},{1,17},{... | collective-permute-start | bytes 49160 | tf_op jit(solution)/shard_map/ppermute | solution.py:33
  58.1 5.0 %collective-permute-start.10 = (f32[8,512]{1,0:T(8,128)S(1)}, f32[8,512]{1,0:T(8,128)S(1)}, u32[]{:S(2)}, u32[]{:S(2)}) collective-permute-start(f32[8,512]{1,0:T(8,128)S(1)} %get-tuple-element.48), channel_id=1, source_target_pairs={{0,16},{4,20},{8,24},{12,28},{16,0},{20,4},{24,8},{28,12},{1,17},{... | collective-permute-start | bytes 49160 | tf_op jit(solution)/shard_map/ppermute | solution.py:33
  62.0 6.9 %collective-permute-start.4 = (bf16[512,256]{0,1:T(8,128)(2,1)S(1)}, bf16[512,256]{0,1:T(8,128)(2,1)S(1)}, u32[]{:S(2)}, u32[]{:S(2)}) collective-permute-start(bf16[512,256]{0,1:T(8,128)(2,1)S(1)} %fusion.42), channel_id=1, source_target_pairs={{0,8},{4,12},{8,0},{12,4},{16,24},{20,28},{24,16},{28,20},{1,9},{5... | collective-permute-start | bytes 786440 | tf_op jit(solution)/shard_map/ppermute | solution.py:33
  68.9 12.8 %copy-start.8 = (bf16[256,256]{1,0:T(8,128)(2,1)S(1)}, bf16[256,256]{1,0:T(8,128)(2,1)}, u32[]{:S(2)}) copy-start(bf16[256,256]{1,0:T(8,128)(2,1)} %param.21) | copy-start | bytes 393220
  69.0 12.5 %collective-permute-start.6 = (bf16[512,256]{0,1:T(8,128)(2,1)S(1)}, bf16[512,256]{0,1:T(8,128)(2,1)S(1)}, u32[]{:S(2)}, u32[]{:S(2)}) collective-permute-start(bf16[512,256]{0,1:T(8,128)(2,1)S(1)} %fusion.40), channel_id=1, source_target_pairs={{0,16},{4,20},{8,24},{12,28},{16,0},{20,4},{24,8},{28,12},{1,17},{... | collective-permute-start | bytes 786440 | tf_op jit(solution)/shard_map/ppermute | solution.py:33
  72.1 9.9 %copy-start.18 = (bf16[256,256]{1,0:T(8,128)(2,1)S(1)}, bf16[256,256]{1,0:T(8,128)(2,1)}, u32[]{:S(2)}) copy-start(bf16[256,256]{1,0:T(8,128)(2,1)} %param.23) | copy-start | bytes 393220
  72.1 9.9 %copy-start.19 = (bf16[256,256]{1,0:T(8,128)(2,1)S(1)}, bf16[256,256]{1,0:T(8,128)(2,1)}, u32[]{:S(2)}) copy-start(bf16[256,256]{1,0:T(8,128)(2,1)} %param.22) | copy-start | bytes 393220
  85.4 3.7 %collective-permute-start.12 = (f32[3,512]{1,0:T(4,128)S(1)}, f32[3,512]{1,0:T(4,128)S(1)}, u32[]{:S(2)}, u32[]{:S(2)}) collective-permute-start(f32[3,512]{1,0:T(4,128)S(1)} %pad_maximum_fusion.1), channel_id=1, source_target_pairs={{0,8},{4,12},{8,0},{12,4},{16,24},{20,28},{24,16},{28,20},{1,9},{5... | collective-permute-start | bytes 18440 | tf_op jit(solution)/shard_map/ppermute | solution.py:33
  89.2 4.6 %collective-permute-start.13 = (f32[3,512]{1,0:T(4,128)S(1)}, f32[3,512]{1,0:T(4,128)S(1)}, u32[]{:S(2)}, u32[]{:S(2)}) collective-permute-start(f32[3,512]{1,0:T(4,128)S(1)} %fusion.119), channel_id=1, source_target_pairs={{0,16},{4,20},{8,24},{12,28},{16,0},{20,4},{24,8},{28,12},{1,17},{... | collective-permute-start | bytes 18440 | tf_op jit(solution)/shard_map/ppermute | solution.py:33
  96.2 7.2 %collective-permute-start.15 = (bf16[512,256]{1,0:T(8,128)(2,1)S(1)}, bf16[512,256]{1,0:T(8,128)(2,1)S(1)}, u32[]{:S(2)}, u32[]{:S(2)}) collective-permute-start(bf16[512,256]{1,0:T(8,128)(2,1)S(1)} %convolution_convert_fusion.1), channel_id=1, source_target_pairs={{0,8},{4,12},{8,0},{12,4},{16,24},{20,28},{24,16},{28,20},{1,9},{5... | collective-permute-start | bytes 786440 | tf_op jit(solution)/shard_map/ppermute | solution.py:53
  97.2 8.0 %collective-permute-start.14 = (f32[256,256]{1,0:T(8,128)S(1)}, f32[256,256]{1,0:T(8,128)S(1)}, u32[]{:S(2)}, u32[]{:S(2)}) collective-permute-start(f32[256,256]{1,0:T(8,128)S(1)} %slice_select_fusion.2), channel_id=1, source_target_pairs={{0,2},{2,0},{1,3},{3,1},{4,6},{6,4},{5,7},{7,5},{8,10},{10,8},{9,1... | collective-permute-start | bytes 786440 | tf_op jit(solution)/shard_map/ppermute | solution.py:85
  103.5 9.8 %collective-permute-start.16 = (bf16[512,256]{1,0:T(8,128)(2,1)S(1)}, bf16[512,256]{1,0:T(8,128)(2,1)S(1)}, u32[]{:S(2)}, u32[]{:S(2)}) collective-permute-start(bf16[512,256]{1,0:T(8,128)(2,1)S(1)} %add_convert_fusion), channel_id=1, source_target_pairs={{0,16},{4,20},{8,24},{12,28},{16,0},{20,4},{24,8},{28,12},{1,17},{... | collective-permute-start | bytes 786440 | tf_op jit(solution)/shard_map/ppermute | solution.py:53
  (9 other events, 10.9 us)

commit v12 on v10

--- a/solution.py
+++ b/solution.py
@@ -248,10 +248,23 @@
         jnp.bfloat16
     )
     pair_upper = lax.axis_index("phi") % 2 == 1
-    own_payload = gathered[:, 2 * model_width :]
+    group_count = group_hits.shape[0]
+    digit_rows = gathered[:, 3 * model_width : 3 * model_width + 2].T.reshape(
+        2 * group_count // model_width, model_width
+    )
+    own_payload = jnp.concatenate(
+        [group_hits, jnp.pad(digit_rows, ((0, 16 - digit_rows.shape[0]), (0, 0)))]
+    )
     other_payload = lax.ppermute(
         own_payload, "phi", partner_pairs(lax.axis_size("phi"), 1)
     )
+    other_digits = other_payload[group_count : group_count + digit_rows.shape[0]].reshape(
+        2, group_count
+    )
+    other_payload = jnp.concatenate(
+        [other_payload[:group_count], other_digits.T], axis=1
+    )
+    own_payload = gathered[:, 2 * model_width : 3 * model_width + 2]
     pair_payload = jnp.where(
         pair_upper,
         jnp.concatenate([other_payload, own_payload]),
@@ -284,7 +297,6 @@
     mask_grad = narrow_butterfly(
         jnp.dot(coef, pair_hits, preferred_element_type=jnp.float32), "phi", distance=2
     )
-    group_count = group_hits.shape[0]
     own_coef = jnp.where(pair_upper, coef[:, group_count:], coef[:, :group_count])
     hit_grad = reduce_scatter_rows(
         lax.dot_general(

time: 101 us -> 98.6 us (0.976)
  waiting for transfers between devices: 45.3 us -> 40.2 us
  starting transfers between devices: 19.2 us -> 20.8 us
  local copies, waits for them, and re-layouts: 4.73 us -> 5.81 us
    ppermute x1, waiting for transfers between devices: 4.45 us -> 0.01 us  [body(): lax.ppermute(own_payload, 'phi', partner_pairs(lax.axis_size('phi'), 1))]
    ppermute x11, waiting for transfers between devices: 23.2 us -> 21.8 us  [butterfly(): other = lax.ppermute(tree, axis, partner_pairs(count, distance))]
    unnamed x29 -> x31, local copies, waits for them, and re-layouts: 3.07 us -> 3.78 us
  transfers between devices with their start and end apart: 17 -> 17, of which waited for: 12 -> 12; matrix products, arithmetic and copies ran while one was open for 10% -> 11% of each run, Pallas kernels for 0% -> 0%
where the time goes in v12:
time: 98.6 us; the launch traced here: 98.3 us
  waiting for transfers between devices  40.2 us (41%)
  starting transfers between devices  20.8 us (21%)
  matrix products  18.5 us (19%)
  other arithmetic  7.54 us (8%)
  local copies, waits for them, and re-layouts  5.81 us (6%)
  blocking collectives  4.35 us (4%)
  between operations  1.23 us (1%)
    ppermute x11, waiting for transfers between devices, butterfly(): other = lax.ppermute(tree, axis, partner_pairs(count, distance))  21.8 us
    ppermute x2, waiting for transfers between devices, narrow_butterfly(): other = lax.ppermute(sent, axis, partner_pairs(count, distance))  15.8 us
    ppermute x11, starting transfers between devices, butterfly(): other = lax.ppermute(tree, axis, partner_pairs(count, distance))  13.2 us
    ppermute x1, starting transfers between devices, extended_2(): lax.ppermute(lax.slice_in_dim(block, 0, width, axis=dim), axis, backward)  5.03 us
    dot_general x1, matrix products, body(): jnp.einsum('hqk,khd->qhd', raised, value_heads, preferred_element_type=jn...  4.9 us
    all_gather x1, blocking collectives, body(): lax.all_gather(jnp.concatenate([local_kv, encoded, digits], axis=1), 'que...  4.35 us
    unnamed x31, local copies, waits for them, and re-layouts  3.78 us
    dot_general x2, matrix products, window_attend(): jnp.einsum('hqk,khd->qhd', weights, value_heads, preferred_element_type=j...  2.68 us
  transfers between devices with their start and end apart: 17, of which 12 were waited for; matrix products, arithmetic and copies ran while one was open for 11% of the time, Pallas kernels for 0%

profile of v12, /device:TPU:0, one launch (start us, length us, event | category | flops | bytes accessed | tf_op | source)
XLA Modules:
  0.0 98.3 jit_solution(10606289253119493084)
XLA Ops:
  0.7 1.1 %copy.49 = bf16[256,256]{0,1:T(8,128)(2,1)S(1)} copy(bf16[256,256]{1,0:T(8,128)(2,1)} %param.13) | data formatting | bytes 262144 | tf_op args[0]
  1.9 1.3 %convolution_convert_fusion = bf16[256,768]{1,0:T(8,128)(2,1)S(1)} fusion(bf16[256,768]{1,0:T(8,128)(2,1)} %param.14, bf16[256,256]{0,1:T(8,128)(2,1)S(1)} %copy.49, f32[256]{0:T(256)S(1)} %add_rsqrt_fusion.3, f32[256]{0:T(256)S(1)} %broadcast_multiply_fusion.3), kind=kOutput, calls=%fused_computation.31 | convolution fusion | flops 101122048 | bytes 919552 | tf_op jit(solution)/shard_map/dot_general | solution.py:176
  3.7 5.0 %collective-permute-start.1 = (bf16[256,512]{1,0:T(8,128)(2,1)S(1)}, bf16[256,512]{1,0:T(8,128)(2,1)S(1)}, u32[]{:S(2)}, u32[]{:S(2)}) collective-permute-start(bf16[256,512]{1,0:T(8,128)(2,1)S(1)} %slice.97), channel_id=1, source_target_pairs={{2,0},{4,2},{6,4},{8,6},{10,8},{12,10},{14,12},{16,14},{18,16},{20... | collective-permute-start | bytes 786440 | tf_op jit(solution)/shard_map/ppermute | solution.py:19
  10.3 2.6 %collective-permute-done = bf16[256,512]{1,0:T(8,128)(2,1)S(1)} collective-permute-done((bf16[256,512]{1,0:T(8,128)(2,1)S(1)}, bf16[256,512]{1,0:T(8,128)(2,1)S(1)}, u32[]{:S(2)}, u32[]{:S(2)}) %collective-permute-start) | collective-permute-done | bytes 262176 | tf_op jit(solution)/shard_map/ppermute | solution.py:16
  13.8 1.1 %fusion.130 = f32[8,128]{1,0:T(8,128)S(1)} fusion(pred[128,640]{1,0:T(8,128)(4,1)S(1)} %fusion.52, bf16[128,8,32]{0,2,1:T(8,128)(2,1)S(1)} %bitcast.122, bf16[640,8,32]{0,2,1:T(8,128)(2,1)S(1)} %bitcast.115), kind=kOutput, calls=%fused_computation.205 | convolution fusion | flops 44565120 | bytes 479232 | tf_op jit(solution)/shard_map/sub | solution.py:113
  15.0 1.3 %fusion.19 = bf16[8,32,128]{2,1,0:T(8,128)(2,1)S(1)} fusion(bf16[640,8,32]{0,2,1:T(8,128)(2,1)S(1)} %bitcast.117, f32[8,128]{1,0:T(8,128)S(1)} %fusion.130, pred[128,640]{1,0:T(8,128)(4,1)S(1)} %fusion.52, bf16[128,8,32]{0,2,1:T(8,128)(2,1)S(1)} %bitcast.123, bf16[640,8,32]{0,2,1:T(8,128)(2,1)S(1)} %bitcast.116), kind=kOutput, calls=%fused_computation.44 | convolution fusion | flops 87197312 | bytes 872448 | tf_op jit(solution)/shard_map/hqk,khd->qhd/dot_general | solution.py:115
  16.3 1.2 %fusion.129 = f32[8,128]{1,0:T(8,128)S(1)} fusion(pred[128,640]{1,0:T(8,128)(4,1)S(1)} %fusion.52, bf16[128,8,32]{0,2,1:T(8,128)(2,1)S(1)} %bitcast.120, bf16[640,8,32]{0,2,1:T(8,128)(2,1)S(1)} %bitcast.112), kind=kOutput, calls=%fused_computation.204 | convolution fusion | flops 44565120 | bytes 479232 | tf_op jit(solution)/shard_map/sub | solution.py:113
  17.5 1.3 %fusion.18 = bf16[8,32,128]{2,1,0:T(8,128)(2,1)S(1)} fusion(bf16[640,8,32]{0,2,1:T(8,128)(2,1)S(1)} %bitcast.114, f32[8,128]{1,0:T(8,128)S(1)} %fusion.129, pred[128,640]{1,0:T(8,128)(4,1)S(1)} %fusion.52, bf16[128,8,32]{0,2,1:T(8,128)(2,1)S(1)} %bitcast.121, bf16[640,8,32]{0,2,1:T(8,128)(2,1)S(1)} %bitcast.113), kind=kOutput, calls=%fused_computation.43 | convolution fusion | flops 87197312 | bytes 872448 | tf_op jit(solution)/shard_map/hqk,khd->qhd/dot_general | solution.py:115
  20.6 4.3 %all_gather.3 = bf16[512,896]{1,0:T(8,128)(2,1)S(1)} all-gather(bf16[256,896]{1,0:T(8,128)(2,1)S(1)} %fusion.49), channel_id=1, replica_groups=mesh['phi'=8,'query'=2,'event'=2] {'query'}, dimensions={0}, use_global_device_ids=true | all-gather | bytes 1376256 | tf_op jit(solution)/shard_map/all_gather | solution.py:207
  25.1 1.3 %multiply_reduce_fusion = (f32[8,512]{1,0:T(8,128)S(1)}, f32[8,512,512]{1,2,0:T(8,128)S(1)}) fusion(bf16[512,8,32]{0,2,1:T(8,128)(2,1)S(1)} %bitcast.107, bf16[512,8,32]{0,2,1:T(8,128)(2,1)S(1)} %bitcast.109), kind=kOutput, calls=%fused_computation.4 | convolution fusion | flops 138407936 | bytes 8929280 | tf_op jit(solution)/shard_map/qhd,khd->hqk/dot_general | solution.py:220
  26.6 1.4 %convert_reduce_fusion = f32[8,512]{1,0:T(8,128)S(1)} fusion(f32[8,512]{1,0:T(8,128)S(1)} %get-tuple-element.57, f32[8,512,512]{1,2,0:T(8,128)S(1)} %get-tuple-element.58), kind=kLoop, calls=%fused_computation.2 | loop fusion | flops 10481664 | bytes 8421376 | tf_op jit(solution)/shard_map/reduce_sum | solution.py:225
  28.0 1.7 %copy-done.1 = f32[8,512,512]{1,2,0:T(8,128)} copy-done((f32[8,512,512]{1,2,0:T(8,128)}, f32[8,512,512]{1,2,0:T(8,128)S(1)}, u32[]{:S(2)}) %copy-start.1) | copy-done | bytes 8388632
  30.3 0.9 collective-permute-start.5
  31.3 1.5 %collective-permute-start.11 = (bf16[528,256]{1,0:T(8,128)(2,1)S(1)}, bf16[528,256]{1,0:T(8,128)(2,1)S(1)}, u32[]{:S(2)}, u32[]{:S(2)}) collective-permute-start(bf16[528,256]{1,0:T(8,128)(2,1)S(1)} %fusion.61), channel_id=1, source_target_pairs={{0,4},{4,0},{8,12},{12,8},{16,20},{20,16},{24,28},{28,24},{1,5},{5... | collective-permute-start | bytes 811016 | tf_op jit(solution)/shard_map/ppermute | solution.py:258
  34.1 0.9 collective-permute-start.9
  35.1 4.9 %convolution_convert_fusion.3 = bf16[8,32,512]{2,1,0:T(8,128)(2,1)S(1)} fusion(bf16[512,8,32]{0,2,1:T(8,128)(2,1)S(1)} %bitcast.108, f32[8,512,512]{1,2,0:T(8,128)} %copy-done.1, f32[8,512]{1,0:T(8,128)S(1)} %get-tuple-element.57), kind=kOutput, calls=%fused_computation.36 | convolution fusion | flops 140640256 | bytes 8929280 | tf_op jit(solution)/shard_map/hqk,khd->qhd/dot_general | solution.py:226
  40.0 1.5 %collective-permute-start.2 = (bf16[512,256]{0,1:T(8,128)(2,1)S(1)}, bf16[512,256]{0,1:T(8,128)(2,1)S(1)}, u32[]{:S(2)}, u32[]{:S(2)}) collective-permute-start(bf16[512,256]{0,1:T(8,128)(2,1)S(1)} %bitcast.110), channel_id=1, source_target_pairs={{0,4},{4,0},{8,12},{12,8},{16,20},{20,16},{24,28},{28,24},{1,5},{5... | collective-permute-start | bytes 786440 | tf_op jit(solution)/shard_map/ppermute | solution.py:33
  41.5 2.6 %collective-permute-start.7 = (f32[8,512]{1,0:T(8,128)S(1)}, f32[8,512]{1,0:T(8,128)S(1)}, u32[]{:S(2)}, u32[]{:S(2)}) collective-permute-start(f32[8,512]{1,0:T(8,128)S(1)} %get-tuple-element.48), channel_id=1, source_target_pairs={{0,16},{4,20},{8,24},{12,28},{16,0},{20,4},{24,8},{28,12},{1,17},{... | collective-permute-start | bytes 49160 | tf_op jit(solution)/shard_map/ppermute | solution.py:33
  45.4 1.5 %collective-permute-done.2 = bf16[512,256]{0,1:T(8,128)(2,1)S(1)} collective-permute-done((bf16[512,256]{0,1:T(8,128)(2,1)S(1)}, bf16[512,256]{0,1:T(8,128)(2,1)S(1)}, u32[]{:S(2)}, u32[]{:S(2)}) %collective-permute-start.2) | collective-permute-done | bytes 262176 | tf_op jit(solution)/shard_map/ppermute | solution.py:33
  47.0 1.1 %collective-permute-start.4 = (bf16[512,256]{0,1:T(8,128)(2,1)S(1)}, bf16[512,256]{0,1:T(8,128)(2,1)S(1)}, u32[]{:S(2)}, u32[]{:S(2)}) collective-permute-start(bf16[512,256]{0,1:T(8,128)(2,1)S(1)} %fusion.41), channel_id=1, source_target_pairs={{0,8},{4,12},{8,0},{12,4},{16,24},{20,28},{24,16},{28,20},{1,9},{5... | collective-permute-start | bytes 786440 | tf_op jit(solution)/shard_map/ppermute | solution.py:33
  49.6 3.9 %collective-permute-done.4 = bf16[512,256]{0,1:T(8,128)(2,1)S(1)} collective-permute-done((bf16[512,256]{0,1:T(8,128)(2,1)S(1)}, bf16[512,256]{0,1:T(8,128)(2,1)S(1)}, u32[]{:S(2)}, u32[]{:S(2)}) %collective-permute-start.4) | collective-permute-done | bytes 262176 | tf_op jit(solution)/shard_map/ppermute | solution.py:33
  53.6 4.0 %collective-permute-start.6 = (bf16[512,256]{0,1:T(8,128)(2,1)S(1)}, bf16[512,256]{0,1:T(8,128)(2,1)S(1)}, u32[]{:S(2)}, u32[]{:S(2)}) collective-permute-start(bf16[512,256]{0,1:T(8,128)(2,1)S(1)} %fusion.39), channel_id=1, source_target_pairs={{0,16},{4,20},{8,24},{12,28},{16,0},{20,4},{24,8},{28,12},{1,17},{... | collective-permute-start | bytes 786440 | tf_op jit(solution)/shard_map/ppermute | solution.py:33
  58.0 7.2 %collective-permute-done.6 = bf16[512,256]{0,1:T(8,128)(2,1)S(1)} collective-permute-done((bf16[512,256]{0,1:T(8,128)(2,1)S(1)}, bf16[512,256]{0,1:T(8,128)(2,1)S(1)}, u32[]{:S(2)}, u32[]{:S(2)}) %collective-permute-start.6) | collective-permute-done | bytes 262176 | tf_op jit(solution)/shard_map/ppermute | solution.py:33
  65.8 1.1 %convolution_convert_fusion.2 = bf16[512,256]{1,0:T(8,128)(2,1)} fusion(bf16[256,256]{1,0:T(8,128)(2,1)S(1)} %copy-done.11, bf16[256,256]{1,0:T(8,128)(2,1)S(1)} %copy-done.12, f32[512,256]{0,1:T(8,128)S(1)} %get-tuple-element.60, f32[512]{0:T(512)S(1)} %add_rsqrt_fusion, f32[512]{0:T(512)S(1)} %broadcast_multiply_fusion), kind=kOutput, calls=%fused_computation.35 | convolution fusion | flops 135004160 | bytes 1052672 | tf_op jit(solution)/shard_map/dot_general | solution.py:247
  66.9 2.2 %select_reduce_fusion = (f32[512]{0:T(512)S(1)}, f32[512]{0:T(512)S(1)}, f32[512]{0:T(512)S(1)}, f32[512,1024]{1,0:T(8,128)S(1)}) fusion(s32[1024]{0:T(1024)S(1)} %fusion.34, s32[512]{0:T(512)S(1)} %copy-done.9, pred[512]{0:T(512)(128)(4,1)S(1)} %get-tuple-element.24, bf16[512,256]{1,0:T(8,128)(2,1)} %convolution_convert_fusion.2, ...), kind=kOutput, calls=%fused_computation.17 | convolution fusion | flops 274201088 | bytes 2896384 | tf_op jit(solution)/shard_map/dot_general | solution.py:276
  69.2 3.6 %collective-permute-done.12 = f32[3,512]{1,0:T(4,128)S(1)} collective-permute-done((f32[3,512]{1,0:T(4,128)S(1)}, f32[3,512]{1,0:T(4,128)S(1)}, u32[]{:S(2)}, u32[]{:S(2)}) %collective-permute-start.12) | collective-permute-done | bytes 6176 | tf_op jit(solution)/shard_map/ppermute | solution.py:33
  72.9 1.2 %collective-permute-start.13 = (f32[3,512]{1,0:T(4,128)S(1)}, f32[3,512]{1,0:T(4,128)S(1)}, u32[]{:S(2)}, u32[]{:S(2)}) collective-permute-start(f32[3,512]{1,0:T(4,128)S(1)} %fusion.121), channel_id=1, source_target_pairs={{0,16},{4,20},{8,24},{12,28},{16,0},{20,4},{24,8},{28,12},{1,17},{... | collective-permute-start | bytes 18440 | tf_op jit(solution)/shard_map/ppermute | solution.py:33
  74.0 3.4 %collective-permute-done.13 = f32[3,512]{1,0:T(4,128)S(1)} collective-permute-done((f32[3,512]{1,0:T(4,128)S(1)}, f32[3,512]{1,0:T(4,128)S(1)}, u32[]{:S(2)}, u32[]{:S(2)}) %collective-permute-start.13) | collective-permute-done | bytes 6176 | tf_op jit(solution)/shard_map/ppermute | solution.py:33
  78.1 1.4 %fusion.5 = bf16[512,1024]{1,0:T(8,128)(2,1)S(1)} fusion(f32[512,1024]{1,0:T(8,128)S(1)} %get-tuple-element.61, f32[512]{0:T(512)S(1)} %bitcast.133, f32[512]{0:T(512)S(1)} %bitcast.134, s32[1024]{0:T(1024)S(1)} %fusion.34, f32[512]{0:T(512)S(1)} %get-tuple-element.23, s32[512]{0:T(512)S(1)} %copy-done.9, pred[512]{0:T(512)(128)(4,1)S(1)} %get-tuple-element.24), kind=kLoop, calls=%fused_computation.16 | loop fusion | flops 7340032 | bytes 3158528 | tf_op jit(solution)/shard_map/convert_element_type | solution.py:150
  80.7 7.5 %collective-permute-done.15 = bf16[512,256]{1,0:T(8,128)(2,1)S(1)} collective-permute-done((bf16[512,256]{1,0:T(8,128)(2,1)S(1)}, bf16[512,256]{1,0:T(8,128)(2,1)S(1)}, u32[]{:S(2)}, u32[]{:S(2)}) %collective-permute-start.15) | collective-permute-done | bytes 262176 | tf_op jit(solution)/shard_map/ppermute | solution.py:53
  89.2 8.3 %collective-permute-done.16 = bf16[512,256]{1,0:T(8,128)(2,1)S(1)} collective-permute-done((bf16[512,256]{1,0:T(8,128)(2,1)S(1)}, bf16[512,256]{1,0:T(8,128)(2,1)S(1)}, u32[]{:S(2)}, u32[]{:S(2)}) %collective-permute-start.16) | collective-permute-done | bytes 262176 | tf_op jit(solution)/shard_map/ppermute | solution.py:53
  97.5 0.8 convert_add_fusion
  (114 shorter events, 13.8 us)
Async XLA Ops:
  0.6 18.6 %copy-start = (bf16[1024,256]{1,0:T(8,128)(2,1)S(1)}, bf16[1024,256]{1,0:T(8,128)(2,1)}, u32[]{:S(2)}) copy-start(bf16[1024,256]{1,0:T(8,128)(2,1)} %param.17) | copy-start | bytes 1572868
  0.6 9.3 %copy-start.2 = (bf16[512,256]{1,0:T(8,128)(2,1)S(1)}, bf16[512,256]{1,0:T(8,128)(2,1)}, u32[]{:S(2)}) copy-start(bf16[512,256]{1,0:T(8,128)(2,1)} %param.18) | copy-start | bytes 786436
  0.7 9.3 %copy-start.6 = (bf16[256,256]{1,0:T(8,128)(2,1)S(1)}, bf16[256,256]{1,0:T(8,128)(2,1)}, u32[]{:S(2)}) copy-start(bf16[256,256]{1,0:T(8,128)(2,1)} %param.19) | copy-start | bytes 393220
  3.2 9.6 %collective-permute-start = (bf16[256,512]{1,0:T(8,128)(2,1)S(1)}, bf16[256,512]{1,0:T(8,128)(2,1)S(1)}, u32[]{:S(2)}, u32[]{:S(2)}) collective-permute-start(bf16[256,512]{1,0:T(8,128)(2,1)S(1)} %slice.97), channel_id=1, source_target_pairs={{0,2},{2,4},{4,6},{6,8},{8,10},{10,12},{12,14},{14,16},{16,18},{18... | collective-permute-start | bytes 786440 | tf_op jit(solution)/shard_map/ppermute | solution.py:16
  3.7 9.1 %collective-permute-start.1 = (bf16[256,512]{1,0:T(8,128)(2,1)S(1)}, bf16[256,512]{1,0:T(8,128)(2,1)S(1)}, u32[]{:S(2)}, u32[]{:S(2)}) collective-permute-start(bf16[256,512]{1,0:T(8,128)(2,1)S(1)} %slice.97), channel_id=1, source_target_pairs={{2,0},{4,2},{6,4},{8,6},{10,8},{12,10},{14,12},{16,14},{18,16},{20... | collective-permute-start | bytes 786440 | tf_op jit(solution)/shard_map/ppermute | solution.py:19
  17.5 1.4 %copy-start.7 = (bf16[256,256]{1,0:T(8,128)(2,1)S(1)}, bf16[256,256]{1,0:T(8,128)(2,1)}, u32[]{:S(2)}) copy-start(bf16[256,256]{1,0:T(8,128)(2,1)} %param.15) | copy-start | bytes 393220
  17.5 1.7 %copy-start.10 = (bf16[256,1024]{1,0:T(8,128)(2,1)S(1)}, bf16[256,1024]{1,0:T(8,128)(2,1)}, u32[]{:S(2)}) copy-start(bf16[256,1024]{1,0:T(8,128)(2,1)} %param.16) | copy-start | bytes 1572868
  18.8 1.4 %copy-start.5 = (bf16[256,512]{1,0:T(8,128)(2,1)S(1)}, bf16[256,512]{1,0:T(8,128)(2,1)}, u32[]{:S(2)}) copy-start(bf16[256,512]{1,0:T(8,128)(2,1)} %param.20) | copy-start | bytes 786436
  20.2 6.3 %copy-start.4 = (bf16[256,256]{1,0:T(8,128)(2,1)}, bf16[256,256]{1,0:T(8,128)(2,1)S(1)}, u32[]{:S(2)}) copy-start(bf16[256,256]{1,0:T(8,128)(2,1)S(1)} %copy.64) | copy-start | bytes 393220
  26.4 3.2 %copy-start.1 = (f32[8,512,512]{1,2,0:T(8,128)}, f32[8,512,512]{1,2,0:T(8,128)S(1)}, u32[]{:S(2)}) copy-start(f32[8,512,512]{1,2,0:T(8,128)S(1)} %get-tuple-element.58) | copy-start | bytes 25165828
  26.4 3.8 %collective-permute-start.3 = (f32[8,512]{1,0:T(8,128)S(1)}, f32[8,512]{1,0:T(8,128)S(1)}, u32[]{:S(2)}, u32[]{:S(2)}) collective-permute-start(f32[8,512]{1,0:T(8,128)S(1)} %get-tuple-element.57), channel_id=1, source_target_pairs={{0,4},{4,0},{8,12},{12,8},{16,20},{20,16},{24,28},{28,24},{1,5},{5... | collective-permute-start | bytes 49160 | tf_op jit(solution)/shard_map/ppermute | solution.py:33
  29.8 3.8 %collective-permute-start.8 = (f32[8,512]{1,0:T(8,128)S(1)}, f32[8,512]{1,0:T(8,128)S(1)}, u32[]{:S(2)}, u32[]{:S(2)}) collective-permute-start(f32[8,512]{1,0:T(8,128)S(1)} %convert_reduce_fusion), channel_id=1, source_target_pairs={{0,4},{4,0},{8,12},{12,8},{16,20},{20,16},{24,28},{28,24},{1,5},{5... | collective-permute-start | bytes 49160 | tf_op jit(solution)/shard_map/ppermute | solution.py:33
  30.3 3.8 %collective-permute-start.5 = (f32[8,512]{1,0:T(8,128)S(1)}, f32[8,512]{1,0:T(8,128)S(1)}, u32[]{:S(2)}, u32[]{:S(2)}) collective-permute-start(f32[8,512]{1,0:T(8,128)S(1)} %get-tuple-element.30), channel_id=1, source_target_pairs={{0,8},{4,12},{8,0},{12,4},{16,24},{20,28},{24,16},{28,20},{1,9},{5... | collective-permute-start | bytes 49160 | tf_op jit(solution)/shard_map/ppermute | solution.py:33
  31.3 17.7 %collective-permute-start.11 = (bf16[528,256]{1,0:T(8,128)(2,1)S(1)}, bf16[528,256]{1,0:T(8,128)(2,1)S(1)}, u32[]{:S(2)}, u32[]{:S(2)}) collective-permute-start(bf16[528,256]{1,0:T(8,128)(2,1)S(1)} %fusion.61), channel_id=1, source_target_pairs={{0,4},{4,0},{8,12},{12,8},{16,20},{20,16},{24,28},{28,24},{1,5},{5... | collective-permute-start | bytes 811016 | tf_op jit(solution)/shard_map/ppermute | solution.py:258
  34.1 9.9 %collective-permute-start.9 = (f32[8,512]{1,0:T(8,128)S(1)}, f32[8,512]{1,0:T(8,128)S(1)}, u32[]{:S(2)}, u32[]{:S(2)}) collective-permute-start(f32[8,512]{1,0:T(8,128)S(1)} %get-tuple-element.41), channel_id=1, source_target_pairs={{0,8},{4,12},{8,0},{12,4},{16,24},{20,28},{24,16},{28,20},{1,9},{5... | collective-permute-start | bytes 49160 | tf_op jit(solution)/shard_map/ppermute | solution.py:33
  35.1 9.4 %copy-start.9 = (s32[512]{0:T(512)S(1)}, s32[512]{0:T(512)}, u32[]{:S(2)}) copy-start(s32[512]{0:T(512)} %param.25) | copy-start | bytes 6148
  40.0 6.9 %collective-permute-start.2 = (bf16[512,256]{0,1:T(8,128)(2,1)S(1)}, bf16[512,256]{0,1:T(8,128)(2,1)S(1)}, u32[]{:S(2)}, u32[]{:S(2)}) collective-permute-start(bf16[512,256]{0,1:T(8,128)(2,1)S(1)} %bitcast.110), channel_id=1, source_target_pairs={{0,4},{4,0},{8,12},{12,8},{16,20},{20,16},{24,28},{28,24},{1,5},{5... | collective-permute-start | bytes 786440 | tf_op jit(solution)/shard_map/ppermute | solution.py:33
  41.5 6.7 %collective-permute-start.7 = (f32[8,512]{1,0:T(8,128)S(1)}, f32[8,512]{1,0:T(8,128)S(1)}, u32[]{:S(2)}, u32[]{:S(2)}) collective-permute-start(f32[8,512]{1,0:T(8,128)S(1)} %get-tuple-element.48), channel_id=1, source_target_pairs={{0,16},{4,20},{8,24},{12,28},{16,0},{20,4},{24,8},{28,12},{1,17},{... | collective-permute-start | bytes 49160 | tf_op jit(solution)/shard_map/ppermute | solution.py:33
  44.1 4.9 %collective-permute-start.10 = (f32[8,512]{1,0:T(8,128)S(1)}, f32[8,512]{1,0:T(8,128)S(1)}, u32[]{:S(2)}, u32[]{:S(2)}) collective-permute-start(f32[8,512]{1,0:T(8,128)S(1)} %get-tuple-element.43), channel_id=1, source_target_pairs={{0,16},{4,20},{8,24},{12,28},{16,0},{20,4},{24,8},{28,12},{1,17},{... | collective-permute-start | bytes 49160 | tf_op jit(solution)/shard_map/ppermute | solution.py:33
  47.0 6.4 %collective-permute-start.4 = (bf16[512,256]{0,1:T(8,128)(2,1)S(1)}, bf16[512,256]{0,1:T(8,128)(2,1)S(1)}, u32[]{:S(2)}, u32[]{:S(2)}) collective-permute-start(bf16[512,256]{0,1:T(8,128)(2,1)S(1)} %fusion.41), channel_id=1, source_target_pairs={{0,8},{4,12},{8,0},{12,4},{16,24},{20,28},{24,16},{28,20},{1,9},{5... | collective-permute-start | bytes 786440 | tf_op jit(solution)/shard_map/ppermute | solution.py:33
  49.2 16.1 %copy-start.3 = (bf16[512,256]{0,1:T(8,128)(2,1)S(1)}, bf16[512,256]{0,1:T(8,128)(2,1)}, u32[]{:S(2)}) copy-start(bf16[512,256]{0,1:T(8,128)(2,1)} %copy.56) | copy-start | bytes 786436
  49.2 16.1 %copy-start.8 = (bf16[256,256]{1,0:T(8,128)(2,1)S(1)}, bf16[256,256]{1,0:T(8,128)(2,1)}, u32[]{:S(2)}) copy-start(bf16[256,256]{1,0:T(8,128)(2,1)} %param.21) | copy-start | bytes 393220
  49.6 16.2 %copy-start.11 = (bf16[256,256]{1,0:T(8,128)(2,1)S(1)}, bf16[256,256]{1,0:T(8,128)(2,1)}, u32[]{:S(2)}) copy-start(bf16[256,256]{1,0:T(8,128)(2,1)} %param.23) | copy-start | bytes 393220
  49.6 16.2 %copy-start.12 = (bf16[256,256]{1,0:T(8,128)(2,1)S(1)}, bf16[256,256]{1,0:T(8,128)(2,1)}, u32[]{:S(2)}) copy-start(bf16[256,256]{1,0:T(8,128)(2,1)} %param.22) | copy-start | bytes 393220
  53.6 11.5 %collective-permute-start.6 = (bf16[512,256]{0,1:T(8,128)(2,1)S(1)}, bf16[512,256]{0,1:T(8,128)(2,1)S(1)}, u32[]{:S(2)}, u32[]{:S(2)}) collective-permute-start(bf16[512,256]{0,1:T(8,128)(2,1)S(1)} %fusion.39), channel_id=1, source_target_pairs={{0,16},{4,20},{8,24},{12,28},{16,0},{20,4},{24,8},{28,12},{1,17},{... | collective-permute-start | bytes 786440 | tf_op jit(solution)/shard_map/ppermute | solution.py:33
  69.1 3.7 %collective-permute-start.12 = (f32[3,512]{1,0:T(4,128)S(1)}, f32[3,512]{1,0:T(4,128)S(1)}, u32[]{:S(2)}, u32[]{:S(2)}) collective-permute-start(f32[3,512]{1,0:T(4,128)S(1)} %pad_maximum_fusion.1), channel_id=1, source_target_pairs={{0,8},{4,12},{8,0},{12,4},{16,24},{20,28},{24,16},{28,20},{1,9},{5... | collective-permute-start | bytes 18440 | tf_op jit(solution)/shard_map/ppermute | solution.py:33
  72.9 4.6 %collective-permute-start.13 = (f32[3,512]{1,0:T(4,128)S(1)}, f32[3,512]{1,0:T(4,128)S(1)}, u32[]{:S(2)}, u32[]{:S(2)}) collective-permute-start(f32[3,512]{1,0:T(4,128)S(1)} %fusion.121), channel_id=1, source_target_pairs={{0,16},{4,20},{8,24},{12,28},{16,0},{20,4},{24,8},{28,12},{1,17},{... | collective-permute-start | bytes 18440 | tf_op jit(solution)/shard_map/ppermute | solution.py:33
  78.1 2.1 %copy-start.13 = (bf16[512,256]{1,0:T(8,128)(2,1)S(1)}, bf16[512,256]{1,0:T(8,128)(2,1)}, u32[]{:S(2)}) copy-start(bf16[512,256]{1,0:T(8,128)(2,1)} %convolution_convert_fusion.2) | copy-start | bytes 786436
  79.9 8.3 %collective-permute-start.15 = (bf16[512,256]{1,0:T(8,128)(2,1)S(1)}, bf16[512,256]{1,0:T(8,128)(2,1)S(1)}, u32[]{:S(2)}, u32[]{:S(2)}) collective-permute-start(bf16[512,256]{1,0:T(8,128)(2,1)S(1)} %convolution_convert_fusion.1), channel_id=1, source_target_pairs={{0,8},{4,12},{8,0},{12,4},{16,24},{20,28},{24,16},{28,20},{1,9},{5... | collective-permute-start | bytes 786440 | tf_op jit(solution)/shard_map/ppermute | solution.py:53
  80.6 7.8 %collective-permute-start.14 = (f32[256,256]{1,0:T(8,128)S(1)}, f32[256,256]{1,0:T(8,128)S(1)}, u32[]{:S(2)}, u32[]{:S(2)}) collective-permute-start(f32[256,256]{1,0:T(8,128)S(1)} %slice_select_fusion.2), channel_id=1, source_target_pairs={{0,2},{2,0},{1,3},{3,1},{4,6},{6,4},{5,7},{7,5},{8,10},{10,8},{9,1... | collective-permute-start | bytes 786440 | tf_op jit(solution)/shard_map/ppermute | solution.py:85
  88.3 9.2 %collective-permute-start.16 = (bf16[512,256]{1,0:T(8,128)(2,1)S(1)}, bf16[512,256]{1,0:T(8,128)(2,1)S(1)}, u32[]{:S(2)}, u32[]{:S(2)}) collective-permute-start(bf16[512,256]{1,0:T(8,128)(2,1)S(1)} %add_convert_fusion), channel_id=1, source_target_pairs={{0,16},{4,20},{8,24},{12,28},{16,0},{20,4},{24,8},{28,12},{1,17},{... | collective-permute-start | bytes 786440 | tf_op jit(solution)/shard_map/ppermute | solution.py:53

commit v13 on v10

--- a/solution.py
+++ b/solution.py
@@ -85,6 +85,25 @@
         block = keep + lax.ppermute(send, axis, partner_pairs(count, distance))
         distance //= 2
     return block
+
+
+def partner_rows(hits, digits, distance):
+    count_rows, width = hits.shape
+    digit_rows = digits.T.reshape(2 * count_rows // width, width)
+    payload = jnp.concatenate(
+        [hits, jnp.pad(digit_rows, ((0, (-digit_rows.shape[0]) % 16), (0, 0)))]
+    )
+    other = lax.ppermute(payload, "phi", partner_pairs(lax.axis_size("phi"), distance))
+    other_hits = other[:count_rows]
+    other_digits = other[count_rows : count_rows + digit_rows.shape[0]].reshape(2, count_rows).T
+    upper = (lax.axis_index("phi") // distance) % 2 == 1
+    hits = jnp.where(
+        upper, jnp.concatenate([other_hits, hits]), jnp.concatenate([hits, other_hits])
+    )
+    digits = jnp.where(
+        upper, jnp.concatenate([other_digits, digits]), jnp.concatenate([digits, other_digits])
+    )
+    return hits, digits
 
 
 def norm_rows(entries):
@@ -247,18 +266,11 @@
     mask_embed = jnp.dot(mask_hidden, mask_second, preferred_element_type=jnp.float32).astype(
         jnp.bfloat16
     )
-    pair_upper = lax.axis_index("phi") % 2 == 1
-    own_payload = gathered[:, 2 * model_width :]
-    other_payload = lax.ppermute(
-        own_payload, "phi", partner_pairs(lax.axis_size("phi"), 1)
-    )
-    pair_payload = jnp.where(
-        pair_upper,
-        jnp.concatenate([other_payload, own_payload]),
-        jnp.concatenate([own_payload, other_payload]),
-    )
-    pair_hits = pair_payload[:, :model_width]
-    pair_digits = pair_payload[:, model_width:].astype(jnp.int32)
+    pair_hits = group_hits
+    pair_digits = gathered[:, 3 * model_width : 3 * model_width + 2]
+    for distance in (1, 2):
+        pair_hits, pair_digits = partner_rows(pair_hits, pair_digits, distance)
+    pair_digits = pair_digits.astype(jnp.int32)
     pair_truth = pair_digits[:, 0] * 256 + pair_digits[:, 1] - 1
     logits = lax.dot_general(
         mask_embed, pair_hits, (((1,), (1,)), ((), ())), preferred_element_type=jnp.float32
@@ -275,17 +287,19 @@
         ),
         "phi",
         add_trees,
-        distance=2,
+        distance=4,
     )
     mask_fill = predicted / hits_total
     coef = loss_coefficients(
         sigma, target, matched, intersection, predicted, truth_count, hits_total, model_width
     )
     mask_grad = narrow_butterfly(
-        jnp.dot(coef, pair_hits, preferred_element_type=jnp.float32), "phi", distance=2
+        jnp.dot(coef, pair_hits, preferred_element_type=jnp.float32), "phi", distance=4
     )
     group_count = group_hits.shape[0]
-    own_coef = jnp.where(pair_upper, coef[:, group_count:], coef[:, :group_count])
+    own_coef = lax.dynamic_slice_in_dim(
+        coef, (lax.axis_index("phi") % 4) * group_count, group_count, axis=1
+    )
     hit_grad = reduce_scatter_rows(
         lax.dot_general(
             own_coef, mask_embed, (((0,), (0,)), ((), ())), preferred_element_type=jnp.float32

time: 101 us -> 98 us (0.970)
  waiting for transfers between devices: 45.3 us -> 33.7 us
  starting transfers between devices: 19.2 us -> 22.6 us
  matrix products: 18.5 us -> 21.1 us
  other arithmetic: 7.53 us -> 9.89 us
    ppermute x2 -> x1, waiting for transfers between devices: 15 us -> 7.96 us  [narrow_butterfly(): other = lax.ppermute(sent, axis, partner_pairs(count, distance))]
    ppermute x11 -> x10, waiting for transfers between devices: 23.2 us -> 18.8 us  [butterfly(): other = lax.ppermute(tree, axis, partner_pairs(count, distance))]
    convert_element_type x1, other arithmetic: 1.37 us -> 4.16 us  [loss_coefficients(): (matched[:, None] * (sigma - target + dice_part) * model_width ** (-0.5))...]
    dot_general x1, matrix products: 2.22 us -> 4.23 us  [body(): lax.dot_general(mask_embed, pair_hits, (((1,), (1,)), ((), ())), preferre...]
    ppermute x11 -> x10, starting transfers between devices: 12.3 us -> 13.7 us  [butterfly(): other = lax.ppermute(tree, axis, partner_pairs(count, distance))]
    ppermute x2 -> x1, starting transfers between devices: 0.68 us -> 1.72 us  [narrow_butterfly(): other = lax.ppermute(sent, axis, partner_pairs(count, distance))]
    ppermute x1 -> x2, waiting for transfers between devices: 4.45 us -> 4.29 us  [partner_rows(): lax.ppermute(payload, 'phi', partner_pairs(lax.axis_size('phi'), distance))]
    unnamed x29 -> x25, local copies, waits for them, and re-layouts: 3.07 us -> 3.03 us
  transfers between devices with their start and end apart: 17 -> 16, of which waited for: 12 -> 11; matrix products, arithmetic and copies ran while one was open for 10% -> 12% of each run, Pallas kernels for 0% -> 0%
where the time goes in v13:
time: 98 us; the launch traced here: 97.8 us
  waiting for transfers between devices  33.7 us (34%)
  starting transfers between devices  22.6 us (23%)
  matrix products  21.1 us (22%)
  other arithmetic  9.89 us (10%)
  local copies, waits for them, and re-layouts  5.02 us (5%)
  blocking collectives  4.35 us (4%)
  between operations  1.21 us (1%)
    ppermute x10, waiting for transfers between devices, butterfly(): other = lax.ppermute(tree, axis, partner_pairs(count, distance))  18.8 us
    ppermute x10, starting transfers between devices, butterfly(): other = lax.ppermute(tree, axis, partner_pairs(count, distance))  13.7 us
    ppermute x1, waiting for transfers between devices, narrow_butterfly(): other = lax.ppermute(sent, axis, partner_pairs(count, distance))  7.96 us
    ppermute x1, starting transfers between devices, extended_2(): lax.ppermute(lax.slice_in_dim(block, 0, width, axis=dim), axis, backward)  5.03 us
    dot_general x1, matrix products, body(): jnp.einsum('hqk,khd->qhd', raised, value_heads, preferred_element_type=jn...  4.91 us
    all_gather x1, blocking collectives, body(): lax.all_gather(jnp.concatenate([local_kv, encoded, digits], axis=1), 'que...  4.35 us
    ppermute x2, waiting for transfers between devices, partner_rows(): lax.ppermute(payload, 'phi', partner_pairs(lax.axis_size('phi'), distance))  4.29 us
    dot_general x1, matrix products, body(): lax.dot_general(mask_embed, pair_hits, (((1,), (1,)), ((), ())), preferre...  4.23 us
  transfers between devices with their start and end apart: 16, of which 11 were waited for; matrix products, arithmetic and copies ran while one was open for 12% of the time, Pallas kernels for 0%

profile of v13, /device:TPU:0, one launch (start us, length us, event | category | flops | bytes accessed | tf_op | source)
XLA Modules:
  0.0 97.8 jit_solution(10952162778059828203)
XLA Ops:
  0.7 1.1 %copy.50 = bf16[256,256]{0,1:T(8,128)(2,1)S(1)} copy(bf16[256,256]{1,0:T(8,128)(2,1)} %param.13) | data formatting | bytes 262144 | tf_op args[0]
  1.9 1.3 %convolution_convert_fusion = bf16[256,768]{1,0:T(8,128)(2,1)S(1)} fusion(bf16[256,768]{1,0:T(8,128)(2,1)} %param.14, bf16[256,256]{0,1:T(8,128)(2,1)S(1)} %copy.50, f32[256]{0:T(256)S(1)} %add_rsqrt_fusion.3, f32[256]{0:T(256)S(1)} %broadcast_multiply_fusion.3), kind=kOutput, calls=%fused_computation.31 | convolution fusion | flops 101122048 | bytes 919552 | tf_op jit(solution)/shard_map/dot_general | solution.py:195
  3.7 5.0 %collective-permute-start.1 = (bf16[256,512]{1,0:T(8,128)(2,1)S(1)}, bf16[256,512]{1,0:T(8,128)(2,1)S(1)}, u32[]{:S(2)}, u32[]{:S(2)}) collective-permute-start(bf16[256,512]{1,0:T(8,128)(2,1)S(1)} %slice.85), channel_id=1, source_target_pairs={{2,0},{4,2},{6,4},{8,6},{10,8},{12,10},{14,12},{16,14},{18,16},{20... | collective-permute-start | bytes 786440 | tf_op jit(solution)/shard_map/ppermute | solution.py:19
  10.3 2.6 %collective-permute-done = bf16[256,512]{1,0:T(8,128)(2,1)S(1)} collective-permute-done((bf16[256,512]{1,0:T(8,128)(2,1)S(1)}, bf16[256,512]{1,0:T(8,128)(2,1)S(1)}, u32[]{:S(2)}, u32[]{:S(2)}) %collective-permute-start) | collective-permute-done | bytes 262176 | tf_op jit(solution)/shard_map/ppermute | solution.py:16
  13.8 1.1 %fusion.133 = f32[8,128]{1,0:T(8,128)S(1)} fusion(pred[128,640]{1,0:T(8,128)(4,1)S(1)} %fusion.49, bf16[128,8,32]{0,2,1:T(8,128)(2,1)S(1)} %bitcast.124, bf16[640,8,32]{0,2,1:T(8,128)(2,1)S(1)} %bitcast.117), kind=kOutput, calls=%fused_computation.209 | convolution fusion | flops 44565120 | bytes 479232 | tf_op jit(solution)/shard_map/sub | solution.py:132
  15.0 1.3 %fusion.19 = bf16[8,32,128]{2,1,0:T(8,128)(2,1)S(1)} fusion(bf16[640,8,32]{0,2,1:T(8,128)(2,1)S(1)} %bitcast.119, f32[8,128]{1,0:T(8,128)S(1)} %fusion.133, pred[128,640]{1,0:T(8,128)(4,1)S(1)} %fusion.49, bf16[128,8,32]{0,2,1:T(8,128)(2,1)S(1)} %bitcast.125, bf16[640,8,32]{0,2,1:T(8,128)(2,1)S(1)} %bitcast.118), kind=kOutput, calls=%fused_computation.44 | convolution fusion | flops 87197312 | bytes 872448 | tf_op jit(solution)/shard_map/hqk,khd->qhd/dot_general | solution.py:134
  16.3 1.2 %fusion.132 = f32[8,128]{1,0:T(8,128)S(1)} fusion(pred[128,640]{1,0:T(8,128)(4,1)S(1)} %fusion.49, bf16[128,8,32]{0,2,1:T(8,128)(2,1)S(1)} %bitcast.122, bf16[640,8,32]{0,2,1:T(8,128)(2,1)S(1)} %bitcast.114), kind=kOutput, calls=%fused_computation.208 | convolution fusion | flops 44565120 | bytes 479232 | tf_op jit(solution)/shard_map/sub | solution.py:132
  17.5 1.3 %fusion.18 = bf16[8,32,128]{2,1,0:T(8,128)(2,1)S(1)} fusion(bf16[640,8,32]{0,2,1:T(8,128)(2,1)S(1)} %bitcast.116, f32[8,128]{1,0:T(8,128)S(1)} %fusion.132, pred[128,640]{1,0:T(8,128)(4,1)S(1)} %fusion.49, bf16[128,8,32]{0,2,1:T(8,128)(2,1)S(1)} %bitcast.123, bf16[640,8,32]{0,2,1:T(8,128)(2,1)S(1)} %bitcast.115), kind=kOutput, calls=%fused_computation.43 | convolution fusion | flops 87197312 | bytes 872448 | tf_op jit(solution)/shard_map/hqk,khd->qhd/dot_general | solution.py:134
  20.6 4.3 %all_gather.3 = bf16[512,896]{1,0:T(8,128)(2,1)S(1)} all-gather(bf16[256,896]{1,0:T(8,128)(2,1)S(1)} %fusion.46), channel_id=1, replica_groups=mesh['phi'=8,'query'=2,'event'=2] {'query'}, dimensions={0}, use_global_device_ids=true | all-gather | bytes 1376256 | tf_op jit(solution)/shard_map/all_gather | solution.py:226
  25.1 1.3 %multiply_reduce_fusion = (f32[8,512]{1,0:T(8,128)S(1)}, f32[8,512,512]{1,2,0:T(8,128)S(1)}) fusion(bf16[512,8,32]{0,2,1:T(8,128)(2,1)S(1)} %bitcast.110, bf16[512,8,32]{0,2,1:T(8,128)(2,1)S(1)} %bitcast.112), kind=kOutput, calls=%fused_computation.4 | convolution fusion | flops 138407936 | bytes 8929280 | tf_op jit(solution)/shard_map/qhd,khd->hqk/dot_general | solution.py:239
  26.6 1.4 %convert_reduce_fusion = f32[8,512]{1,0:T(8,128)S(1)} fusion(f32[8,512]{1,0:T(8,128)S(1)} %get-tuple-element.59, f32[8,512,512]{1,2,0:T(8,128)S(1)} %get-tuple-element.60), kind=kLoop, calls=%fused_computation.2 | loop fusion | flops 10481664 | bytes 8421376 | tf_op jit(solution)/shard_map/reduce_sum | solution.py:244
  28.0 1.6 %copy-done.1 = f32[8,512,512]{1,2,0:T(8,128)} copy-done((f32[8,512,512]{1,2,0:T(8,128)}, f32[8,512,512]{1,2,0:T(8,128)S(1)}, u32[]{:S(2)}) %copy-start.1) | copy-done | bytes 8388632
  30.3 1.0 collective-permute-start.5
  31.3 1.5 %collective-permute-start.11 = (bf16[528,256]{1,0:T(8,128)(2,1)S(1)}, bf16[528,256]{1,0:T(8,128)(2,1)S(1)}, u32[]{:S(2)}, u32[]{:S(2)}) collective-permute-start(bf16[528,256]{1,0:T(8,128)(2,1)S(1)} %fusion.58), channel_id=1, source_target_pairs={{0,4},{4,0},{8,12},{12,8},{16,20},{20,16},{24,28},{28,24},{1,5},{5... | collective-permute-start | bytes 811016 | tf_op jit(solution)/shard_map/ppermute | solution.py:96
  34.1 1.0 collective-permute-start.9
  35.1 4.9 %convolution_convert_fusion.3 = bf16[8,32,512]{2,1,0:T(8,128)(2,1)S(1)} fusion(bf16[512,8,32]{0,2,1:T(8,128)(2,1)S(1)} %bitcast.111, f32[8,512,512]{1,2,0:T(8,128)} %copy-done.1, f32[8,512]{1,0:T(8,128)S(1)} %get-tuple-element.59), kind=kOutput, calls=%fused_computation.36 | convolution fusion | flops 140640256 | bytes 8929280 | tf_op jit(solution)/shard_map/hqk,khd->qhd/dot_general | solution.py:245
  40.0 1.5 %collective-permute-start.2 = (bf16[512,256]{0,1:T(8,128)(2,1)S(1)}, bf16[512,256]{0,1:T(8,128)(2,1)S(1)}, u32[]{:S(2)}, u32[]{:S(2)}) collective-permute-start(bf16[512,256]{0,1:T(8,128)(2,1)S(1)} %bitcast.113), channel_id=1, source_target_pairs={{0,4},{4,0},{8,12},{12,8},{16,20},{20,16},{24,28},{28,24},{1,5},{5... | collective-permute-start | bytes 786440 | tf_op jit(solution)/shard_map/ppermute | solution.py:33
  41.5 2.6 %collective-permute-start.7 = (f32[8,512]{1,0:T(8,128)S(1)}, f32[8,512]{1,0:T(8,128)S(1)}, u32[]{:S(2)}, u32[]{:S(2)}) collective-permute-start(f32[8,512]{1,0:T(8,128)S(1)} %get-tuple-element.50), channel_id=1, source_target_pairs={{0,16},{4,20},{8,24},{12,28},{16,0},{20,4},{24,8},{28,12},{1,17},{... | collective-permute-start | bytes 49160 | tf_op jit(solution)/shard_map/ppermute | solution.py:33
  44.8 2.1 %collective-permute-done.2 = bf16[512,256]{0,1:T(8,128)(2,1)S(1)} collective-permute-done((bf16[512,256]{0,1:T(8,128)(2,1)S(1)}, bf16[512,256]{0,1:T(8,128)(2,1)S(1)}, u32[]{:S(2)}, u32[]{:S(2)}) %collective-permute-start.2) | collective-permute-done | bytes 262176 | tf_op jit(solution)/shard_map/ppermute | solution.py:33
  47.1 1.1 %collective-permute-start.4 = (bf16[512,256]{0,1:T(8,128)(2,1)S(1)}, bf16[512,256]{0,1:T(8,128)(2,1)S(1)}, u32[]{:S(2)}, u32[]{:S(2)}) collective-permute-start(bf16[512,256]{0,1:T(8,128)(2,1)S(1)} %fusion.39), channel_id=1, source_target_pairs={{0,8},{4,12},{8,0},{12,4},{16,24},{20,28},{24,16},{28,20},{1,9},{5... | collective-permute-start | bytes 786440 | tf_op jit(solution)/shard_map/ppermute | solution.py:33
  49.3 4.2 %collective-permute-done.4 = bf16[512,256]{0,1:T(8,128)(2,1)S(1)} collective-permute-done((bf16[512,256]{0,1:T(8,128)(2,1)S(1)}, bf16[512,256]{0,1:T(8,128)(2,1)S(1)}, u32[]{:S(2)}, u32[]{:S(2)}) %collective-permute-start.4) | collective-permute-done | bytes 262176 | tf_op jit(solution)/shard_map/ppermute | solution.py:33
  53.7 3.9 %collective-permute-start.6 = (bf16[512,256]{0,1:T(8,128)(2,1)S(1)}, bf16[512,256]{0,1:T(8,128)(2,1)S(1)}, u32[]{:S(2)}, u32[]{:S(2)}) collective-permute-start(bf16[512,256]{0,1:T(8,128)(2,1)S(1)} %fusion.37), channel_id=1, source_target_pairs={{0,16},{4,20},{8,24},{12,28},{16,0},{20,4},{24,8},{28,12},{1,17},{... | collective-permute-start | bytes 786440 | tf_op jit(solution)/shard_map/ppermute | solution.py:33
  57.7 7.5 %collective-permute-done.6 = bf16[512,256]{0,1:T(8,128)(2,1)S(1)} collective-permute-done((bf16[512,256]{0,1:T(8,128)(2,1)S(1)}, bf16[512,256]{0,1:T(8,128)(2,1)S(1)}, u32[]{:S(2)}, u32[]{:S(2)}) %collective-permute-start.6) | collective-permute-done | bytes 262176 | tf_op jit(solution)/shard_map/ppermute | solution.py:33
  65.8 1.4 %convolution_convert_fusion.2 = bf16[512,256]{1,0:T(8,128)(2,1)S(1)} fusion(bf16[256,256]{1,0:T(8,128)(2,1)} %param.23, bf16[256,256]{1,0:T(8,128)(2,1)} %param.22, f32[512,256]{0,1:T(8,128)S(1)} %get-tuple-element.62, f32[512]{0:T(512)S(1)} %add_rsqrt_fusion, f32[512]{0:T(512)S(1)} %broadcast_multiply_fusion), kind=kOutput, calls=%fused_computation.35 | convolution fusion | flops 135004160 | bytes 1052672 | tf_op jit(solution)/shard_map/dot_general | solution.py:266
  67.2 4.3 %collective-permute-done.12 = bf16[1040,256]{1,0:T(8,128)(2,1)S(1)} collective-permute-done((bf16[1040,256]{1,0:T(8,128)(2,1)S(1)}, bf16[1040,256]{1,0:T(8,128)(2,1)S(1)}, u32[]{:S(2)}, u32[]{:S(2)}) %collective-permute-start.12) | collective-permute-done | bytes 532512 | tf_op jit(solution)/shard_map/ppermute | solution.py:96
  71.6 4.2 %select_reduce_fusion = (f32[512]{0:T(512)S(1)}, f32[512]{0:T(512)S(1)}, f32[512]{0:T(512)S(1)}, f32[512,2048]{1,0:T(8,128)}) fusion(s32[2048]{0:T(1024)S(1)} %bitcast.127, s32[512]{0:T(512)S(1)} %copy-done.9, pred[512]{0:T(512)(128)(4,1)S(1)} %get-tuple-element.24, bf16[512,256]{1,0:T(8,128)(2,1)S(1)} %convolution_convert_fusion.2, ...), kind=kOutput, calls=%fused_computation.11 | convolution fusion | flops 553122304 | bytes 5521921 | tf_op jit(solution)/shard_map/dot_general | solution.py:275
  75.9 1.7 %collective-permute-start.13 = (f32[3,512]{1,0:T(4,128)S(1)}, f32[3,512]{1,0:T(4,128)S(1)}, u32[]{:S(2)}, u32[]{:S(2)}) collective-permute-start(f32[3,512]{1,0:T(4,128)S(1)} %pad_maximum_fusion.1), channel_id=1, source_target_pairs={{0,16},{4,20},{8,24},{12,28},{16,0},{20,4},{24,8},{28,12},{1,17},{... | collective-permute-start | bytes 18440 | tf_op jit(solution)/shard_map/ppermute | solution.py:33
  77.6 2.9 %collective-permute-done.13 = f32[3,512]{1,0:T(4,128)S(1)} collective-permute-done((f32[3,512]{1,0:T(4,128)S(1)}, f32[3,512]{1,0:T(4,128)S(1)}, u32[]{:S(2)}, u32[]{:S(2)}) %collective-permute-start.13) | collective-permute-done | bytes 6176 | tf_op jit(solution)/shard_map/ppermute | solution.py:33
  81.1 4.2 %fusion.5 = bf16[512,2048]{1,0:T(8,128)(2,1)S(1)} fusion(f32[512,2048]{1,0:T(8,128)} %get-tuple-element.63, f32[512]{0:T(512)S(1)} %bitcast.130, f32[512]{0:T(512)S(1)} %bitcast.131, s32[2048]{0:T(1024)S(1)} %bitcast.128, f32[512]{0:T(512)S(1)} %get-tuple-element.23, s32[512]{0:T(512)S(1)} %copy-done.9, pred[512]{0:T(512)(128)(4,1)S(1)} %get-tuple-element.24), kind=kLoop, calls=%fused_computation.10 | loop fusion | flops 14680064 | bytes 6308352 | tf_op jit(solution)/shard_map/convert_element_type | solution.py:169
  86.0 1.7 %collective-permute-start.15 = (bf16[512,256]{1,0:T(8,128)(2,1)S(1)}, bf16[512,256]{1,0:T(8,128)(2,1)S(1)}, u32[]{:S(2)}, u32[]{:S(2)}) collective-permute-start(bf16[512,256]{1,0:T(8,128)(2,1)S(1)} %convolution_convert_fusion.1), channel_id=1, source_target_pairs={{0,16},{4,20},{8,24},{12,28},{16,0},{20,4},{24,8},{28,12},{1,17},{... | collective-permute-start | bytes 786440 | tf_op jit(solution)/shard_map/ppermute | solution.py:53
  88.2 8.0 %collective-permute-done.15 = bf16[512,256]{1,0:T(8,128)(2,1)S(1)} collective-permute-done((bf16[512,256]{1,0:T(8,128)(2,1)S(1)}, bf16[512,256]{1,0:T(8,128)(2,1)S(1)}, u32[]{:S(2)}, u32[]{:S(2)}) %collective-permute-start.15) | collective-permute-done | bytes 262176 | tf_op jit(solution)/shard_map/ppermute | solution.py:53
  96.2 0.9 convert_add_fusion
  (109 shorter events, 12.4 us)
Async XLA Ops:
  0.6 18.6 %copy-start = (bf16[1024,256]{1,0:T(8,128)(2,1)S(1)}, bf16[1024,256]{1,0:T(8,128)(2,1)}, u32[]{:S(2)}) copy-start(bf16[1024,256]{1,0:T(8,128)(2,1)} %param.17) | copy-start | bytes 1572868
  0.6 9.3 %copy-start.2 = (bf16[512,256]{1,0:T(8,128)(2,1)S(1)}, bf16[512,256]{1,0:T(8,128)(2,1)}, u32[]{:S(2)}) copy-start(bf16[512,256]{1,0:T(8,128)(2,1)} %param.18) | copy-start | bytes 786436
  0.7 9.3 %copy-start.6 = (bf16[256,256]{1,0:T(8,128)(2,1)S(1)}, bf16[256,256]{1,0:T(8,128)(2,1)}, u32[]{:S(2)}) copy-start(bf16[256,256]{1,0:T(8,128)(2,1)} %param.19) | copy-start | bytes 393220
  3.2 9.6 %collective-permute-start = (bf16[256,512]{1,0:T(8,128)(2,1)S(1)}, bf16[256,512]{1,0:T(8,128)(2,1)S(1)}, u32[]{:S(2)}, u32[]{:S(2)}) collective-permute-start(bf16[256,512]{1,0:T(8,128)(2,1)S(1)} %slice.85), channel_id=1, source_target_pairs={{0,2},{2,4},{4,6},{6,8},{8,10},{10,12},{12,14},{14,16},{16,18},{18... | collective-permute-start | bytes 786440 | tf_op jit(solution)/shard_map/ppermute | solution.py:16
  3.7 9.1 %collective-permute-start.1 = (bf16[256,512]{1,0:T(8,128)(2,1)S(1)}, bf16[256,512]{1,0:T(8,128)(2,1)S(1)}, u32[]{:S(2)}, u32[]{:S(2)}) collective-permute-start(bf16[256,512]{1,0:T(8,128)(2,1)S(1)} %slice.85), channel_id=1, source_target_pairs={{2,0},{4,2},{6,4},{8,6},{10,8},{12,10},{14,12},{16,14},{18,16},{20... | collective-permute-start | bytes 786440 | tf_op jit(solution)/shard_map/ppermute | solution.py:19
  17.5 1.4 %copy-start.7 = (bf16[256,256]{1,0:T(8,128)(2,1)S(1)}, bf16[256,256]{1,0:T(8,128)(2,1)}, u32[]{:S(2)}) copy-start(bf16[256,256]{1,0:T(8,128)(2,1)} %param.15) | copy-start | bytes 393220
  17.5 1.7 %copy-start.10 = (bf16[256,1024]{1,0:T(8,128)(2,1)S(1)}, bf16[256,1024]{1,0:T(8,128)(2,1)}, u32[]{:S(2)}) copy-start(bf16[256,1024]{1,0:T(8,128)(2,1)} %param.16) | copy-start | bytes 1572868
  18.8 1.4 %copy-start.5 = (bf16[256,512]{1,0:T(8,128)(2,1)S(1)}, bf16[256,512]{1,0:T(8,128)(2,1)}, u32[]{:S(2)}) copy-start(bf16[256,512]{1,0:T(8,128)(2,1)} %param.20) | copy-start | bytes 786436
  20.2 6.3 %copy-start.3 = (bf16[256,256]{1,0:T(8,128)(2,1)}, bf16[256,256]{1,0:T(8,128)(2,1)S(1)}, u32[]{:S(2)}) copy-start(bf16[256,256]{1,0:T(8,128)(2,1)S(1)} %copy.66) | copy-start | bytes 393220
  26.4 3.2 %copy-start.1 = (f32[8,512,512]{1,2,0:T(8,128)}, f32[8,512,512]{1,2,0:T(8,128)S(1)}, u32[]{:S(2)}) copy-start(f32[8,512,512]{1,2,0:T(8,128)S(1)} %get-tuple-element.60) | copy-start | bytes 25165828
  26.5 3.8 %collective-permute-start.3 = (f32[8,512]{1,0:T(8,128)S(1)}, f32[8,512]{1,0:T(8,128)S(1)}, u32[]{:S(2)}, u32[]{:S(2)}) collective-permute-start(f32[8,512]{1,0:T(8,128)S(1)} %get-tuple-element.59), channel_id=1, source_target_pairs={{0,4},{4,0},{8,12},{12,8},{16,20},{20,16},{24,28},{28,24},{1,5},{5... | collective-permute-start | bytes 49160 | tf_op jit(solution)/shard_map/ppermute | solution.py:33
  29.8 3.8 %collective-permute-start.8 = (f32[8,512]{1,0:T(8,128)S(1)}, f32[8,512]{1,0:T(8,128)S(1)}, u32[]{:S(2)}, u32[]{:S(2)}) collective-permute-start(f32[8,512]{1,0:T(8,128)S(1)} %convert_reduce_fusion), channel_id=1, source_target_pairs={{0,4},{4,0},{8,12},{12,8},{16,20},{20,16},{24,28},{28,24},{1,5},{5... | collective-permute-start | bytes 49160 | tf_op jit(solution)/shard_map/ppermute | solution.py:33
  30.3 3.8 %collective-permute-start.5 = (f32[8,512]{1,0:T(8,128)S(1)}, f32[8,512]{1,0:T(8,128)S(1)}, u32[]{:S(2)}, u32[]{:S(2)}) collective-permute-start(f32[8,512]{1,0:T(8,128)S(1)} %get-tuple-element.30), channel_id=1, source_target_pairs={{0,8},{4,12},{8,0},{12,4},{16,24},{20,28},{24,16},{28,20},{1,9},{5... | collective-permute-start | bytes 49160 | tf_op jit(solution)/shard_map/ppermute | solution.py:33
  31.3 17.7 %collective-permute-start.11 = (bf16[528,256]{1,0:T(8,128)(2,1)S(1)}, bf16[528,256]{1,0:T(8,128)(2,1)S(1)}, u32[]{:S(2)}, u32[]{:S(2)}) collective-permute-start(bf16[528,256]{1,0:T(8,128)(2,1)S(1)} %fusion.58), channel_id=1, source_target_pairs={{0,4},{4,0},{8,12},{12,8},{16,20},{20,16},{24,28},{28,24},{1,5},{5... | collective-permute-start | bytes 811016 | tf_op jit(solution)/shard_map/ppermute | solution.py:96
  34.1 10.0 %collective-permute-start.9 = (f32[8,512]{1,0:T(8,128)S(1)}, f32[8,512]{1,0:T(8,128)S(1)}, u32[]{:S(2)}, u32[]{:S(2)}) collective-permute-start(f32[8,512]{1,0:T(8,128)S(1)} %get-tuple-element.43), channel_id=1, source_target_pairs={{0,8},{4,12},{8,0},{12,4},{16,24},{20,28},{24,16},{28,20},{1,9},{5... | collective-permute-start | bytes 49160 | tf_op jit(solution)/shard_map/ppermute | solution.py:33
  35.1 9.4 %copy-start.9 = (s32[512]{0:T(512)S(1)}, s32[512]{0:T(512)}, u32[]{:S(2)}) copy-start(s32[512]{0:T(512)} %param.25) | copy-start | bytes 6148
  40.0 6.9 %collective-permute-start.2 = (bf16[512,256]{0,1:T(8,128)(2,1)S(1)}, bf16[512,256]{0,1:T(8,128)(2,1)S(1)}, u32[]{:S(2)}, u32[]{:S(2)}) collective-permute-start(bf16[512,256]{0,1:T(8,128)(2,1)S(1)} %bitcast.113), channel_id=1, source_target_pairs={{0,4},{4,0},{8,12},{12,8},{16,20},{20,16},{24,28},{28,24},{1,5},{5... | collective-permute-start | bytes 786440 | tf_op jit(solution)/shard_map/ppermute | solution.py:33
  41.5 6.7 %collective-permute-start.7 = (f32[8,512]{1,0:T(8,128)S(1)}, f32[8,512]{1,0:T(8,128)S(1)}, u32[]{:S(2)}, u32[]{:S(2)}) collective-permute-start(f32[8,512]{1,0:T(8,128)S(1)} %get-tuple-element.50), channel_id=1, source_target_pairs={{0,16},{4,20},{8,24},{12,28},{16,0},{20,4},{24,8},{28,12},{1,17},{... | collective-permute-start | bytes 49160 | tf_op jit(solution)/shard_map/ppermute | solution.py:33
  44.1 4.9 %collective-permute-start.10 = (f32[8,512]{1,0:T(8,128)S(1)}, f32[8,512]{1,0:T(8,128)S(1)}, u32[]{:S(2)}, u32[]{:S(2)}) collective-permute-start(f32[8,512]{1,0:T(8,128)S(1)} %get-tuple-element.45), channel_id=1, source_target_pairs={{0,16},{4,20},{8,24},{12,28},{16,0},{20,4},{24,8},{28,12},{1,17},{... | collective-permute-start | bytes 49160 | tf_op jit(solution)/shard_map/ppermute | solution.py:33
  46.9 18.5 %copy-start.8 = (bf16[256,256]{1,0:T(8,128)(2,1)S(1)}, bf16[256,256]{1,0:T(8,128)(2,1)}, u32[]{:S(2)}) copy-start(bf16[256,256]{1,0:T(8,128)(2,1)} %param.21) | copy-start | bytes 393220
  47.1 6.4 %collective-permute-start.4 = (bf16[512,256]{0,1:T(8,128)(2,1)S(1)}, bf16[512,256]{0,1:T(8,128)(2,1)S(1)}, u32[]{:S(2)}, u32[]{:S(2)}) collective-permute-start(bf16[512,256]{0,1:T(8,128)(2,1)S(1)} %fusion.39), channel_id=1, source_target_pairs={{0,8},{4,12},{8,0},{12,4},{16,24},{20,28},{24,16},{28,20},{1,9},{5... | collective-permute-start | bytes 786440 | tf_op jit(solution)/shard_map/ppermute | solution.py:33
  53.7 11.6 %collective-permute-start.6 = (bf16[512,256]{0,1:T(8,128)(2,1)S(1)}, bf16[512,256]{0,1:T(8,128)(2,1)S(1)}, u32[]{:S(2)}, u32[]{:S(2)}) collective-permute-start(bf16[512,256]{0,1:T(8,128)(2,1)S(1)} %fusion.37), channel_id=1, source_target_pairs={{0,16},{4,20},{8,24},{12,28},{16,0},{20,4},{24,8},{28,12},{1,17},{... | collective-permute-start | bytes 786440 | tf_op jit(solution)/shard_map/ppermute | solution.py:33
  57.7 13.9 %collective-permute-start.12 = (bf16[1040,256]{1,0:T(8,128)(2,1)S(1)}, bf16[1040,256]{1,0:T(8,128)(2,1)S(1)}, u32[]{:S(2)}, u32[]{:S(2)}) collective-permute-start(bf16[1040,256]{1,0:T(8,128)(2,1)S(1)} %fusion.31), channel_id=1, source_target_pairs={{0,8},{4,12},{8,0},{12,4},{16,24},{20,28},{24,16},{28,20},{1,9},{5... | collective-permute-start | bytes 1597448 | tf_op jit(solution)/shard_map/ppermute | solution.py:96
  67.2 20.5 %copy-start.4 = (bf16[512,256]{1,0:T(8,128)(2,1)}, bf16[512,256]{1,0:T(8,128)(2,1)S(1)}, u32[]{:S(2)}) copy-start(bf16[512,256]{1,0:T(8,128)(2,1)S(1)} %convolution_convert_fusion.2) | copy-start | bytes 786436
  75.9 4.6 %collective-permute-start.13 = (f32[3,512]{1,0:T(4,128)S(1)}, f32[3,512]{1,0:T(4,128)S(1)}, u32[]{:S(2)}, u32[]{:S(2)}) collective-permute-start(f32[3,512]{1,0:T(4,128)S(1)} %pad_maximum_fusion.1), channel_id=1, source_target_pairs={{0,16},{4,20},{8,24},{12,28},{16,0},{20,4},{24,8},{28,12},{1,17},{... | collective-permute-start | bytes 18440 | tf_op jit(solution)/shard_map/ppermute | solution.py:33
  86.0 10.1 %collective-permute-start.15 = (bf16[512,256]{1,0:T(8,128)(2,1)S(1)}, bf16[512,256]{1,0:T(8,128)(2,1)S(1)}, u32[]{:S(2)}, u32[]{:S(2)}) collective-permute-start(bf16[512,256]{1,0:T(8,128)(2,1)S(1)} %convolution_convert_fusion.1), channel_id=1, source_target_pairs={{0,16},{4,20},{8,24},{12,28},{16,0},{20,4},{24,8},{28,12},{1,17},{... | collective-permute-start | bytes 786440 | tf_op jit(solution)/shard_map/ppermute | solution.py:53
  88.1 8.9 %collective-permute-start.14 = (f32[256,256]{1,0:T(8,128)S(1)}, f32[256,256]{1,0:T(8,128)S(1)}, u32[]{:S(2)}, u32[]{:S(2)}) collective-permute-start(f32[256,256]{1,0:T(8,128)S(1)} %slice_select_fusion), channel_id=1, source_target_pairs={{0,2},{2,0},{1,3},{3,1},{4,6},{6,4},{5,7},{7,5},{8,10},{10,8},{9,1... | collective-permute-start | bytes 786440 | tf_op jit(solution)/shard_map/ppermute | solution.py:85

commit v14 on v13

--- a/solution.py
+++ b/solution.py
@@ -1,6 +1,7 @@
 import jax
 import jax.numpy as jnp
 from jax import lax
+from jax.experimental import pallas as pl
 from jax.sharding import PartitionSpec as P
 
 HEADS = 8
@@ -104,6 +105,43 @@
         upper, jnp.concatenate([other_digits, digits]), jnp.concatenate([digits, other_digits])
     )
     return hits, digits
+
+
+def cross_kernel(query_ref, key_ref, value_ref, max_ref, total_ref, mixed_ref):
+    query = query_ref[...]
+    scores = lax.dot_general(
+        query, key_ref[...], (((1,), (1,)), ((), ())), preferred_element_type=jnp.float32
+    ) * query.shape[1] ** (-0.5)
+    local_max = jnp.max(scores, axis=1, keepdims=True)
+    raised = jnp.exp(scores - local_max).astype(jnp.bfloat16)
+    max_ref[...] = local_max
+    total_ref[...] = jnp.sum(raised.astype(jnp.float32), axis=1, keepdims=True)
+    mixed_ref[...] = jnp.dot(raised, value_ref[...], preferred_element_type=jnp.float32)
+
+
+def cross_partials(query_heads, key_heads, value_heads):
+    head_count, query_count, head_size = query_heads.shape
+    key_count = key_heads.shape[1]
+    query_spec = pl.BlockSpec((None, query_count, head_size), lambda h: (h, 0, 0))
+    key_spec = pl.BlockSpec((None, key_count, head_size), lambda h: (h, 0, 0))
+    stat_spec = pl.BlockSpec((None, query_count, 1), lambda h: (h, 0, 0))
+    return pl.pallas_call(
+        cross_kernel,
+        grid=(head_count,),
+        in_specs=[query_spec, key_spec, key_spec],
+        out_specs=[stat_spec, stat_spec, query_spec],
+        out_shape=[
+            jax.ShapeDtypeStruct((head_count, query_count, 1), jnp.float32),
+            jax.ShapeDtypeStruct((head_count, query_count, 1), jnp.float32),
+            jax.ShapeDtypeStruct((head_count, query_count, head_size), jnp.float32),
+        ],
+        cost_estimate=pl.CostEstimate(
+            flops=4 * head_count * query_count * key_count * head_size,
+            transcendentals=head_count * query_count * key_count,
+            bytes_accessed=2 * head_count * (query_count + 2 * key_count) * head_size
+            + 4 * head_count * query_count * (head_size + 2),
+        ),
+    )(query_heads, key_heads, value_heads)
 
 
 def norm_rows(entries):
@@ -233,18 +271,15 @@
     query_proj = jnp.dot(queries, cross_q, preferred_element_type=jnp.float32).astype(jnp.bfloat16)
     head_size = model_width // HEADS
     group_count = group_kv.shape[0]
-    query_heads = query_proj.reshape(query_count, HEADS, head_size)
-    key_heads = group_kv[:, :model_width].reshape(group_count, HEADS, head_size)
-    value_heads = group_kv[:, model_width:].reshape(group_count, HEADS, head_size)
-    scores = jnp.einsum(
-        "qhd,khd->hqk", query_heads, key_heads, preferred_element_type=jnp.float32
-    ) * head_size ** (-0.5)
-    local_max = jnp.max(scores, axis=-1)
-    raised = jnp.exp(scores - local_max[..., None]).astype(jnp.bfloat16)
-    local_total = jnp.sum(raised.astype(jnp.float32), axis=-1)
-    local_mixed = jnp.einsum(
-        "hqk,khd->qhd", raised, value_heads, preferred_element_type=jnp.float32
-    ).reshape(query_count, model_width)
+    query_heads = query_proj.reshape(query_count, HEADS, head_size).transpose(1, 0, 2)
+    key_heads = group_kv[:, :model_width].reshape(group_count, HEADS, head_size).transpose(1, 0, 2)
+    value_heads = (
+        group_kv[:, model_width:].reshape(group_count, HEADS, head_size).transpose(1, 0, 2)
+    )
+    head_max, head_total, head_mixed = cross_partials(query_heads, key_heads, value_heads)
+    local_max = head_max[:, :, 0]
+    local_total = head_total[:, :, 0]
+    local_mixed = head_mixed.transpose(1, 0, 2).reshape(query_count, model_width)
     _, total, mixed = butterfly(
         (local_max, local_total, local_mixed.astype(jnp.bfloat16)),
         "phi",

time: 98 us -> 112 us (1.14)
  Pallas kernels: 0 us -> 9.5 us
  matrix products: 21.1 us -> 14.8 us
  waiting for transfers between devices: 33.7 us -> 39.5 us
  other arithmetic: 9.89 us -> 14.6 us
  starting transfers between devices: 22.6 us -> 19.8 us
  local copies, waits for them, and re-layouts: 5.02 us -> 7.79 us
    pallas_call x0 -> x1, Pallas kernels: none -> 9.5 us  [cross_partials(): pl.pallas_call(cross_kernel, grid=(head_count,), in_specs=[query_spec, ke...]
    dot_general x2 -> x0, matrix products: 6.22 us -> none  [the longest x1 4.91 us: body(): jnp.einsum('hqk,khd->qhd', raised, value_heads, preferred_element_type=jn...]
    ppermute x10, waiting for transfers between devices: 18.8 us -> 24.2 us  [butterfly(): other = lax.ppermute(tree, axis, partner_pairs(count, distance))]
    pallas_call x0 -> x2, other arithmetic: none -> 4.41 us  [cross_partials(): pl.pallas_call(cross_kernel, grid=(head_count,), in_specs=[query_spec, ke...]
    reshape x0 -> x3, local copies, waits for them, and re-layouts: none -> 4.09 us  [the longest x1 1.41 us: body(): group_kv[:, model_width:].reshape(group_count, HEADS, head_size)]
    convert_element_type x0 -> x1, other arithmetic: none -> 1.75 us  [body(): local_mixed.astype(jnp.bfloat16)]
    ppermute x1, waiting for transfers between devices: 7.96 us -> 9.61 us  [narrow_butterfly(): other = lax.ppermute(sent, axis, partner_pairs(count, distance))]
    unnamed x25 -> x23, local copies, waits for them, and re-layouts: 3.03 us -> 1.4 us
  transfers between devices with their start and end apart: 16 -> 16, of which waited for: 11 -> 9; matrix products, arithmetic and copies ran while one was open for 12% -> 10% of each run, Pallas kernels for 0% -> 0%
where the time goes in v14:
time: 112 us; the launch traced here: 111 us
  waiting for transfers between devices  39.5 us (35%)
  starting transfers between devices  19.8 us (18%)
  matrix products  14.8 us (13%)
  other arithmetic  14.6 us (13%)
  Pallas kernels  9.5 us (8%)
  local copies, waits for them, and re-layouts  7.79 us (7%)
  blocking collectives  4.35 us (4%)
  between operations  1.19 us (1%)
    ppermute x10, waiting for transfers between devices, butterfly(): other = lax.ppermute(tree, axis, partner_pairs(count, distance))  24.2 us
    ppermute x10, starting transfers between devices, butterfly(): other = lax.ppermute(tree, axis, partner_pairs(count, distance))  12.2 us
    ppermute x1, waiting for transfers between devices, narrow_butterfly(): other = lax.ppermute(sent, axis, partner_pairs(count, distance))  9.61 us
    pallas_call x1, Pallas kernels, cross_partials(): pl.pallas_call(cross_kernel, grid=(head_count,), in_specs=[query_spec, ke...  9.5 us
    ppermute x1, starting transfers between devices, extended_2(): lax.ppermute(lax.slice_in_dim(block, 0, width, axis=dim), axis, backward)  5.03 us
    ppermute x2, waiting for transfers between devices, partner_rows(): lax.ppermute(payload, 'phi', partner_pairs(lax.axis_size('phi'), distance))  4.42 us
    pallas_call x2, other arithmetic, cross_partials(): pl.pallas_call(cross_kernel, grid=(head_count,), in_specs=[query_spec, ke...  4.41 us
    all_gather x1, blocking collectives, body(): lax.all_gather(jnp.concatenate([local_kv, encoded, digits], axis=1), 'que...  4.35 us
  transfers between devices with their start and end apart: 16, of which 9 were waited for; matrix products, arithmetic and copies ran while one was open for 10% of the time, Pallas kernels for 0%

profile of v14, /device:TPU:0, one launch (start us, length us, event | category | flops | bytes accessed | tf_op | source)
XLA Modules:
  0.0 111.5 jit_solution(10457710581042995389)
XLA Ops:
  0.7 1.1 copy.57
  1.9 1.3 %convolution_convert_fusion = bf16[256,768]{1,0:T(8,128)(2,1)S(1)} fusion(bf16[256,768]{1,0:T(8,128)(2,1)} %param.14, bf16[256,256]{0,1:T(8,128)(2,1)S(1)} %copy.57, f32[256]{0:T(256)S(1)} %add_rsqrt_fusion.3, f32[256]{0:T(256)S(1)} %broadcast_multiply_fusion.3), kind=kOutput, calls=%fused_computation.28 | convolution fusion | flops 101122048 | bytes 919552 | tf_op jit(solution)/shard_map/dot_general | solution.py:233
  3.7 5.0 %collective-permute-start.1 = (bf16[256,512]{1,0:T(8,128)(2,1)S(1)}, bf16[256,512]{1,0:T(8,128)(2,1)S(1)}, u32[]{:S(2)}, u32[]{:S(2)}) collective-permute-start(bf16[256,512]{1,0:T(8,128)(2,1)S(1)} %slice.85), channel_id=1, source_target_pairs={{2,0},{4,2},{6,4},{8,6},{10,8},{12,10},{14,12},{16,14},{18,16},{20... | collective-permute-start | bytes 786440 | tf_op jit(solution)/shard_map/ppermute | solution.py:20
  10.2 1.4 %copy.65 = bf16[512,8,32]{2,0,1:T(8,128)(2,1)} copy(bf16[512,8,32]{0,2,1:T(8,128)(2,1)S(1)} %bitcast.115) | data formatting | bytes 524288 | tf_op jit(solution)/shard_map/reshape | solution.py:274
  11.6 1.2 %collective-permute-done = bf16[256,512]{1,0:T(8,128)(2,1)S(1)} collective-permute-done((bf16[256,512]{1,0:T(8,128)(2,1)S(1)}, bf16[256,512]{1,0:T(8,128)(2,1)S(1)}, u32[]{:S(2)}, u32[]{:S(2)}) %collective-permute-start) | collective-permute-done | bytes 262176 | tf_op jit(solution)/shard_map/ppermute | solution.py:17
  13.8 1.1 %fusion.132 = f32[8,128]{1,0:T(8,128)S(1)} fusion(pred[128,640]{1,0:T(8,128)(4,1)S(1)} %fusion.49, bf16[128,8,32]{0,2,1:T(8,128)(2,1)S(1)} %bitcast.127, bf16[640,8,32]{0,2,1:T(8,128)(2,1)S(1)} %bitcast.120), kind=kOutput, calls=%fused_computation.205 | convolution fusion | flops 44565120 | bytes 479232 | tf_op jit(solution)/shard_map/sub | solution.py:170
  15.0 1.3 %fusion.19 = bf16[8,32,128]{2,1,0:T(8,128)(2,1)S(1)} fusion(bf16[640,8,32]{0,2,1:T(8,128)(2,1)S(1)} %bitcast.122, f32[8,128]{1,0:T(8,128)S(1)} %fusion.132, pred[128,640]{1,0:T(8,128)(4,1)S(1)} %fusion.49, bf16[128,8,32]{0,2,1:T(8,128)(2,1)S(1)} %bitcast.128, bf16[640,8,32]{0,2,1:T(8,128)(2,1)S(1)} %bitcast.121), kind=kOutput, calls=%fused_computation.40 | convolution fusion | flops 87197312 | bytes 872448 | tf_op jit(solution)/shard_map/hqk,khd->qhd/dot_general | solution.py:172
  16.3 1.2 %fusion.131 = f32[8,128]{1,0:T(8,128)S(1)} fusion(pred[128,640]{1,0:T(8,128)(4,1)S(1)} %fusion.49, bf16[128,8,32]{0,2,1:T(8,128)(2,1)S(1)} %bitcast.125, bf16[640,8,32]{0,2,1:T(8,128)(2,1)S(1)} %bitcast.117), kind=kOutput, calls=%fused_computation.204 | convolution fusion | flops 44565120 | bytes 479232 | tf_op jit(solution)/shard_map/sub | solution.py:170
  17.5 1.3 %fusion.18 = bf16[8,32,128]{2,1,0:T(8,128)(2,1)S(1)} fusion(bf16[640,8,32]{0,2,1:T(8,128)(2,1)S(1)} %bitcast.119, f32[8,128]{1,0:T(8,128)S(1)} %fusion.131, pred[128,640]{1,0:T(8,128)(4,1)S(1)} %fusion.49, bf16[128,8,32]{0,2,1:T(8,128)(2,1)S(1)} %bitcast.126, bf16[640,8,32]{0,2,1:T(8,128)(2,1)S(1)} %bitcast.118), kind=kOutput, calls=%fused_computation.39 | convolution fusion | flops 87197312 | bytes 872448 | tf_op jit(solution)/shard_map/hqk,khd->qhd/dot_general | solution.py:172
  19.2 0.8 convert_reduce_fusion.2
  20.6 4.3 %all_gather.3 = bf16[512,896]{1,0:T(8,128)(2,1)S(1)} all-gather(bf16[256,896]{1,0:T(8,128)(2,1)S(1)} %fusion.46), channel_id=1, replica_groups=mesh['phi'=8,'query'=2,'event'=2] {'query'}, dimensions={0}, use_global_device_ids=true | all-gather | bytes 1376256 | tf_op jit(solution)/shard_map/all_gather | solution.py:264
  25.1 1.3 %copy.69 = bf16[512,8,32]{2,0,1:T(8,128)(2,1)} copy(bf16[512,8,32]{0,2,1:T(8,128)(2,1)S(1)} %bitcast.113) | data formatting | bytes 524288 | tf_op jit(solution)/shard_map/reshape | solution.py:275
  26.6 1.4 %copy.71 = bf16[512,8,32]{2,0,1:T(8,128)(2,1)} copy(bf16[512,8,32]{0,2,1:T(8,128)(2,1)S(1)} %bitcast.114) | data formatting | bytes 524288 | tf_op jit(solution)/shard_map/reshape | solution.py:277
  28.0 9.5 %shard_map.164 = (f32[8,512,1]{2,1,0:T(8,128)}, f32[8,512,1]{2,1,0:T(8,128)}, f32[8,512,32]{2,1,0:T(8,128)}) custom-call(bf16[8,512,32]{2,1,0:T(8,128)(2,1)} %bitcast.110, bf16[8,512,32]{2,1,0:T(8,128)(2,1)} %bitcast.111, bf16[8,512,32]{2,1,0:T(8,128)(2,1)} %bitcast.112), custom_call_target="tpu_custom_call" | custom-call | flops 268435456 | bytes 1343488 | tf_op jit(solution)/shard_map/pallas_call | solution.py:128
  37.5 2.2 %reduce = f32[8,512]{1,0:T(8,128)S(1)} reduce(f32[8,512,1]{2,1,0:T(8,128)} %get-tuple-element.9, f32[]{:T(128)} %constant.181), dimensions={2}, to_apply=%get-tuple-element.9.reduce_sub_computation | reduce | bytes 32772 | tf_op jit(solution)/shard_map/pallas_call | solution.py:128
  40.0 2.2 %reduce.1 = f32[8,512]{1,0:T(8,128)S(1)} reduce(f32[8,512,1]{2,1,0:T(8,128)} %get-tuple-element.10, f32[]{:T(128)} %constant.181), dimensions={2}, to_apply=%get-tuple-element.10.reduce_sub_computation | reduce | bytes 32772 | tf_op jit(solution)/shard_map/pallas_call | solution.py:128
  42.2 2.0 %collective-permute-start.8 = (f32[8,512]{1,0:T(8,128)S(1)}, f32[8,512]{1,0:T(8,128)S(1)}, u32[]{:S(2)}, u32[]{:S(2)}) collective-permute-start(f32[8,512]{1,0:T(8,128)S(1)} %reduce.1), channel_id=1, source_target_pairs={{0,4},{4,0},{8,12},{12,8},{16,20},{20,16},{24,28},{28,24},{1,5},{5... | collective-permute-start | bytes 49160 | tf_op jit(solution)/shard_map/ppermute | solution.py:34
  46.0 2.0 %collective-permute-done.5 = f32[8,512]{1,0:T(8,128)S(1)} collective-permute-done((f32[8,512]{1,0:T(8,128)S(1)}, f32[8,512]{1,0:T(8,128)S(1)}, u32[]{:S(2)}, u32[]{:S(2)}) %collective-permute-start.5) | collective-permute-done | bytes 16416 | tf_op jit(solution)/shard_map/ppermute | solution.py:34
  48.8 1.8 %convert_bitcast_fusion = bf16[512,8,32]{2,0,1:T(8,128)(2,1)S(1)} fusion(f32[8,512,32]{2,1,0:T(8,128)} %get-tuple-element.8), kind=kLoop, calls=%fused_computation.52 | loop fusion | flops 131072 | bytes 786432 | tf_op jit(solution)/shard_map/convert_element_type | solution.py:284
  51.6 2.6 %collective-permute-start.7 = (f32[8,512]{1,0:T(8,128)S(1)}, f32[8,512]{1,0:T(8,128)S(1)}, u32[]{:S(2)}, u32[]{:S(2)}) collective-permute-start(f32[8,512]{1,0:T(8,128)S(1)} %get-tuple-element.56), channel_id=1, source_target_pairs={{0,16},{4,20},{8,24},{12,28},{16,0},{20,4},{24,8},{28,12},{1,17},{... | collective-permute-start | bytes 49160 | tf_op jit(solution)/shard_map/ppermute | solution.py:34
  54.9 3.8 %collective-permute-done.2 = bf16[512,256]{0,1:T(8,128)(2,1)S(1)} collective-permute-done((bf16[512,256]{0,1:T(8,128)(2,1)S(1)}, bf16[512,256]{0,1:T(8,128)(2,1)S(1)}, u32[]{:S(2)}, u32[]{:S(2)}) %collective-permute-start.2) | collective-permute-done | bytes 262176 | tf_op jit(solution)/shard_map/ppermute | solution.py:34
  58.8 1.4 %collective-permute-start.4 = (bf16[512,256]{0,1:T(8,128)(2,1)S(1)}, bf16[512,256]{0,1:T(8,128)(2,1)S(1)}, u32[]{:S(2)}, u32[]{:S(2)}) collective-permute-start(bf16[512,256]{0,1:T(8,128)(2,1)S(1)} %fusion.39), channel_id=1, source_target_pairs={{0,8},{4,12},{8,0},{12,4},{16,24},{20,28},{24,16},{28,20},{1,9},{5... | collective-permute-start | bytes 786440 | tf_op jit(solution)/shard_map/ppermute | solution.py:34
  60.5 5.0 %collective-permute-done.4 = bf16[512,256]{0,1:T(8,128)(2,1)S(1)} collective-permute-done((bf16[512,256]{0,1:T(8,128)(2,1)S(1)}, bf16[512,256]{0,1:T(8,128)(2,1)S(1)}, u32[]{:S(2)}, u32[]{:S(2)}) %collective-permute-start.4) | collective-permute-done | bytes 262176 | tf_op jit(solution)/shard_map/ppermute | solution.py:34
  65.7 2.7 %collective-permute-start.6 = (bf16[512,256]{0,1:T(8,128)(2,1)S(1)}, bf16[512,256]{0,1:T(8,128)(2,1)S(1)}, u32[]{:S(2)}, u32[]{:S(2)}) collective-permute-start(bf16[512,256]{0,1:T(8,128)(2,1)S(1)} %fusion.37), channel_id=1, source_target_pairs={{0,16},{4,20},{8,24},{12,28},{16,0},{20,4},{24,8},{28,12},{1,17},{... | collective-permute-start | bytes 786440 | tf_op jit(solution)/shard_map/ppermute | solution.py:34
  68.9 9.2 %collective-permute-done.6 = bf16[512,256]{0,1:T(8,128)(2,1)S(1)} collective-permute-done((bf16[512,256]{0,1:T(8,128)(2,1)S(1)}, bf16[512,256]{0,1:T(8,128)(2,1)S(1)}, u32[]{:S(2)}, u32[]{:S(2)}) %collective-permute-start.6) | collective-permute-done | bytes 262176 | tf_op jit(solution)/shard_map/ppermute | solution.py:34
  78.7 1.4 %convolution_convert_fusion.2 = bf16[512,256]{1,0:T(8,128)(2,1)S(1)} fusion(bf16[256,256]{1,0:T(8,128)(2,1)} %param.23, bf16[256,256]{1,0:T(8,128)(2,1)} %param.22, f32[512,256]{0,1:T(8,128)S(1)} %get-tuple-element.66, f32[512]{0:T(512)S(1)} %add_rsqrt_fusion, f32[512]{0:T(512)S(1)} %broadcast_multiply_fusion), kind=kOutput, calls=%fused_computation.32 | convolution fusion | flops 135004160 | bytes 1052672 | tf_op jit(solution)/shard_map/dot_general | solution.py:301
  80.1 4.4 %collective-permute-done.12 = bf16[1040,256]{1,0:T(8,128)(2,1)S(1)} collective-permute-done((bf16[1040,256]{1,0:T(8,128)(2,1)S(1)}, bf16[1040,256]{1,0:T(8,128)(2,1)S(1)}, u32[]{:S(2)}, u32[]{:S(2)}) %collective-permute-start.12) | collective-permute-done | bytes 532512 | tf_op jit(solution)/shard_map/ppermute | solution.py:97
  84.6 4.2 %select_reduce_fusion = (f32[512]{0:T(512)S(1)}, f32[512]{0:T(512)S(1)}, f32[512]{0:T(512)S(1)}, f32[512,2048]{1,0:T(8,128)}) fusion(s32[2048]{0:T(1024)S(1)} %bitcast.130, s32[512]{0:T(512)S(1)} %copy-done.8, pred[512]{0:T(512)(128)(4,1)S(1)} %get-tuple-element.30, bf16[512,256]{1,0:T(8,128)(2,1)S(1)} %convolution_convert_fusion.2, ...), kind=kOutput, calls=%fused_computation.8 | convolution fusion | flops 553122304 | bytes 5521921 | tf_op jit(solution)/shard_map/dot_general | solution.py:310
  89.6 3.8 %collective-permute-done.13 = f32[3,512]{1,0:T(4,128)S(1)} collective-permute-done((f32[3,512]{1,0:T(4,128)S(1)}, f32[3,512]{1,0:T(4,128)S(1)}, u32[]{:S(2)}, u32[]{:S(2)}) %collective-permute-start.13) | collective-permute-done | bytes 6176 | tf_op jit(solution)/shard_map/ppermute | solution.py:34
  94.1 4.2 %fusion.5 = bf16[512,2048]{1,0:T(8,128)(2,1)S(1)} fusion(f32[512,2048]{1,0:T(8,128)} %get-tuple-element.67, f32[512]{0:T(512)S(1)} %bitcast.133, f32[512]{0:T(512)S(1)} %bitcast.134, s32[2048]{0:T(1024)S(1)} %bitcast.131, f32[512]{0:T(512)S(1)} %get-tuple-element.29, s32[512]{0:T(512)S(1)} %copy-done.8, pred[512]{0:T(512)(128)(4,1)S(1)} %get-tuple-element.30), kind=kLoop, calls=%fused_computation.7 | loop fusion | flops 14680064 | bytes 6308352 | tf_op jit(solution)/shard_map/convert_element_type | solution.py:207
  100.2 9.6 %collective-permute-done.15 = bf16[512,256]{1,0:T(8,128)(2,1)S(1)} collective-permute-done((bf16[512,256]{1,0:T(8,128)(2,1)S(1)}, bf16[512,256]{1,0:T(8,128)(2,1)S(1)}, u32[]{:S(2)}, u32[]{:S(2)}) %collective-permute-start.15) | collective-permute-done | bytes 262176 | tf_op jit(solution)/shard_map/ppermute | solution.py:54
  109.9 0.8 convert_add_fusion
  (112 shorter events, 14.6 us)
Async XLA Ops:
  0.6 18.6 %copy-start = (bf16[1024,256]{1,0:T(8,128)(2,1)S(1)}, bf16[1024,256]{1,0:T(8,128)(2,1)}, u32[]{:S(2)}) copy-start(bf16[1024,256]{1,0:T(8,128)(2,1)} %param.17) | copy-start | bytes 1572868
  0.6 9.3 %copy-start.1 = (bf16[512,256]{1,0:T(8,128)(2,1)S(1)}, bf16[512,256]{1,0:T(8,128)(2,1)}, u32[]{:S(2)}) copy-start(bf16[512,256]{1,0:T(8,128)(2,1)} %param.18) | copy-start | bytes 786436
  0.7 9.3 %copy-start.5 = (bf16[256,256]{1,0:T(8,128)(2,1)S(1)}, bf16[256,256]{1,0:T(8,128)(2,1)}, u32[]{:S(2)}) copy-start(bf16[256,256]{1,0:T(8,128)(2,1)} %param.19) | copy-start | bytes 393220
  3.2 9.6 %collective-permute-start = (bf16[256,512]{1,0:T(8,128)(2,1)S(1)}, bf16[256,512]{1,0:T(8,128)(2,1)S(1)}, u32[]{:S(2)}, u32[]{:S(2)}) collective-permute-start(bf16[256,512]{1,0:T(8,128)(2,1)S(1)} %slice.85), channel_id=1, source_target_pairs={{0,2},{2,4},{4,6},{6,8},{8,10},{10,12},{12,14},{14,16},{16,18},{18... | collective-permute-start | bytes 786440 | tf_op jit(solution)/shard_map/ppermute | solution.py:17
  3.7 9.1 %collective-permute-start.1 = (bf16[256,512]{1,0:T(8,128)(2,1)S(1)}, bf16[256,512]{1,0:T(8,128)(2,1)S(1)}, u32[]{:S(2)}, u32[]{:S(2)}) collective-permute-start(bf16[256,512]{1,0:T(8,128)(2,1)S(1)} %slice.85), channel_id=1, source_target_pairs={{2,0},{4,2},{6,4},{8,6},{10,8},{12,10},{14,12},{16,14},{18,16},{20... | collective-permute-start | bytes 786440 | tf_op jit(solution)/shard_map/ppermute | solution.py:20
  17.5 1.4 %copy-start.6 = (bf16[256,256]{1,0:T(8,128)(2,1)S(1)}, bf16[256,256]{1,0:T(8,128)(2,1)}, u32[]{:S(2)}) copy-start(bf16[256,256]{1,0:T(8,128)(2,1)} %param.15) | copy-start | bytes 393220
  17.5 1.7 %copy-start.9 = (bf16[256,1024]{1,0:T(8,128)(2,1)S(1)}, bf16[256,1024]{1,0:T(8,128)(2,1)}, u32[]{:S(2)}) copy-start(bf16[256,1024]{1,0:T(8,128)(2,1)} %param.16) | copy-start | bytes 1572868
  18.8 1.4 %copy-start.4 = (bf16[256,512]{1,0:T(8,128)(2,1)S(1)}, bf16[256,512]{1,0:T(8,128)(2,1)}, u32[]{:S(2)}) copy-start(bf16[256,512]{1,0:T(8,128)(2,1)} %param.20) | copy-start | bytes 786436
  20.2 6.3 %copy-start.2 = (bf16[256,256]{1,0:T(8,128)(2,1)}, bf16[256,256]{1,0:T(8,128)(2,1)S(1)}, u32[]{:S(2)}) copy-start(bf16[256,256]{1,0:T(8,128)(2,1)S(1)} %copy.76) | copy-start | bytes 393220
  39.7 4.5 %collective-permute-start.3 = (f32[8,512]{1,0:T(8,128)S(1)}, f32[8,512]{1,0:T(8,128)S(1)}, u32[]{:S(2)}, u32[]{:S(2)}) collective-permute-start(f32[8,512]{1,0:T(8,128)S(1)} %reduce), channel_id=1, source_target_pairs={{0,4},{4,0},{8,12},{12,8},{16,20},{20,16},{24,28},{28,24},{1,5},{5... | collective-permute-start | bytes 49160 | tf_op jit(solution)/shard_map/ppermute | solution.py:34
  42.2 3.8 %collective-permute-start.8 = (f32[8,512]{1,0:T(8,128)S(1)}, f32[8,512]{1,0:T(8,128)S(1)}, u32[]{:S(2)}, u32[]{:S(2)}) collective-permute-start(f32[8,512]{1,0:T(8,128)S(1)} %reduce.1), channel_id=1, source_target_pairs={{0,4},{4,0},{8,12},{12,8},{16,20},{20,16},{24,28},{28,24},{1,5},{5... | collective-permute-start | bytes 49160 | tf_op jit(solution)/shard_map/ppermute | solution.py:34
  44.3 3.8 %collective-permute-start.5 = (f32[8,512]{1,0:T(8,128)S(1)}, f32[8,512]{1,0:T(8,128)S(1)}, u32[]{:S(2)}, u32[]{:S(2)}) collective-permute-start(f32[8,512]{1,0:T(8,128)S(1)} %get-tuple-element.36), channel_id=1, source_target_pairs={{0,8},{4,12},{8,0},{12,4},{16,24},{20,28},{24,16},{28,20},{1,9},{5... | collective-permute-start | bytes 49160 | tf_op jit(solution)/shard_map/ppermute | solution.py:34
  45.0 9.6 %copy-start.8 = (s32[512]{0:T(512)S(1)}, s32[512]{0:T(512)}, u32[]{:S(2)}) copy-start(s32[512]{0:T(512)} %param.25) | copy-start | bytes 6148
  45.0 15.2 %collective-permute-start.11 = (bf16[528,256]{1,0:T(8,128)(2,1)S(1)}, bf16[528,256]{1,0:T(8,128)(2,1)S(1)}, u32[]{:S(2)}, u32[]{:S(2)}) collective-permute-start(bf16[528,256]{1,0:T(8,128)(2,1)S(1)} %fusion.58), channel_id=1, source_target_pairs={{0,4},{4,0},{8,12},{12,8},{16,20},{20,16},{24,28},{28,24},{1,5},{5... | collective-permute-start | bytes 811016 | tf_op jit(solution)/shard_map/ppermute | solution.py:97
  48.1 6.1 %collective-permute-start.9 = (f32[8,512]{1,0:T(8,128)S(1)}, f32[8,512]{1,0:T(8,128)S(1)}, u32[]{:S(2)}, u32[]{:S(2)}) collective-permute-start(f32[8,512]{1,0:T(8,128)S(1)} %get-tuple-element.49), channel_id=1, source_target_pairs={{0,8},{4,12},{8,0},{12,4},{16,24},{20,28},{24,16},{28,20},{1,9},{5... | collective-permute-start | bytes 49160 | tf_op jit(solution)/shard_map/ppermute | solution.py:34
  50.9 7.7 %collective-permute-start.2 = (bf16[512,256]{0,1:T(8,128)(2,1)S(1)}, bf16[512,256]{0,1:T(8,128)(2,1)S(1)}, u32[]{:S(2)}, u32[]{:S(2)}) collective-permute-start(bf16[512,256]{0,1:T(8,128)(2,1)S(1)} %bitcast.116), channel_id=1, source_target_pairs={{0,4},{4,0},{8,12},{12,8},{16,20},{20,16},{24,28},{28,24},{1,5},{5... | collective-permute-start | bytes 786440 | tf_op jit(solution)/shard_map/ppermute | solution.py:34
  51.6 8.6 %collective-permute-start.7 = (f32[8,512]{1,0:T(8,128)S(1)}, f32[8,512]{1,0:T(8,128)S(1)}, u32[]{:S(2)}, u32[]{:S(2)}) collective-permute-start(f32[8,512]{1,0:T(8,128)S(1)} %get-tuple-element.56), channel_id=1, source_target_pairs={{0,16},{4,20},{8,24},{12,28},{16,0},{20,4},{24,8},{28,12},{1,17},{... | collective-permute-start | bytes 49160 | tf_op jit(solution)/shard_map/ppermute | solution.py:34
  54.2 6.0 %collective-permute-start.10 = (f32[8,512]{1,0:T(8,128)S(1)}, f32[8,512]{1,0:T(8,128)S(1)}, u32[]{:S(2)}, u32[]{:S(2)}) collective-permute-start(f32[8,512]{1,0:T(8,128)S(1)} %get-tuple-element.51), channel_id=1, source_target_pairs={{0,16},{4,20},{8,24},{12,28},{16,0},{20,4},{24,8},{28,12},{1,17},{... | collective-permute-start | bytes 49160 | tf_op jit(solution)/shard_map/ppermute | solution.py:34
  58.6 19.7 %copy-start.7 = (bf16[256,256]{1,0:T(8,128)(2,1)S(1)}, bf16[256,256]{1,0:T(8,128)(2,1)}, u32[]{:S(2)}) copy-start(bf16[256,256]{1,0:T(8,128)(2,1)} %param.21) | copy-start | bytes 393220
  58.8 6.8 %collective-permute-start.4 = (bf16[512,256]{0,1:T(8,128)(2,1)S(1)}, bf16[512,256]{0,1:T(8,128)(2,1)S(1)}, u32[]{:S(2)}, u32[]{:S(2)}) collective-permute-start(bf16[512,256]{0,1:T(8,128)(2,1)S(1)} %fusion.39), channel_id=1, source_target_pairs={{0,8},{4,12},{8,0},{12,4},{16,24},{20,28},{24,16},{28,20},{1,9},{5... | collective-permute-start | bytes 786440 | tf_op jit(solution)/shard_map/ppermute | solution.py:34
  65.7 12.4 %collective-permute-start.6 = (bf16[512,256]{0,1:T(8,128)(2,1)S(1)}, bf16[512,256]{0,1:T(8,128)(2,1)S(1)}, u32[]{:S(2)}, u32[]{:S(2)}) collective-permute-start(bf16[512,256]{0,1:T(8,128)(2,1)S(1)} %fusion.37), channel_id=1, source_target_pairs={{0,16},{4,20},{8,24},{12,28},{16,0},{20,4},{24,8},{28,12},{1,17},{... | collective-permute-start | bytes 786440 | tf_op jit(solution)/shard_map/ppermute | solution.py:34
  68.4 16.1 %collective-permute-start.12 = (bf16[1040,256]{1,0:T(8,128)(2,1)S(1)}, bf16[1040,256]{1,0:T(8,128)(2,1)S(1)}, u32[]{:S(2)}, u32[]{:S(2)}) collective-permute-start(bf16[1040,256]{1,0:T(8,128)(2,1)S(1)} %fusion.31), channel_id=1, source_target_pairs={{0,8},{4,12},{8,0},{12,4},{16,24},{20,28},{24,16},{28,20},{1,9},{5... | collective-permute-start | bytes 1597448 | tf_op jit(solution)/shard_map/ppermute | solution.py:97
  80.1 19.7 %copy-start.3 = (bf16[512,256]{1,0:T(8,128)(2,1)}, bf16[512,256]{1,0:T(8,128)(2,1)S(1)}, u32[]{:S(2)}) copy-start(bf16[512,256]{1,0:T(8,128)(2,1)S(1)} %convolution_convert_fusion.2) | copy-start | bytes 786436
  88.8 4.6 %collective-permute-start.13 = (f32[3,512]{1,0:T(4,128)S(1)}, f32[3,512]{1,0:T(4,128)S(1)}, u32[]{:S(2)}, u32[]{:S(2)}) collective-permute-start(f32[3,512]{1,0:T(4,128)S(1)} %pad_maximum_fusion.1), channel_id=1, source_target_pairs={{0,16},{4,20},{8,24},{12,28},{16,0},{20,4},{24,8},{28,12},{1,17},{... | collective-permute-start | bytes 18440 | tf_op jit(solution)/shard_map/ppermute | solution.py:34
  99.0 10.9 %collective-permute-start.15 = (bf16[512,256]{1,0:T(8,128)(2,1)S(1)}, bf16[512,256]{1,0:T(8,128)(2,1)S(1)}, u32[]{:S(2)}, u32[]{:S(2)}) collective-permute-start(bf16[512,256]{1,0:T(8,128)(2,1)S(1)} %convolution_convert_fusion.1), channel_id=1, source_target_pairs={{0,16},{4,20},{8,24},{12,28},{16,0},{20,4},{24,8},{28,12},{1,17},{... | collective-permute-start | bytes 786440 | tf_op jit(solution)/shard_map/ppermute | solution.py:54
  100.2 10.5 %collective-permute-start.14 = (f32[256,256]{1,0:T(8,128)S(1)}, f32[256,256]{1,0:T(8,128)S(1)}, u32[]{:S(2)}, u32[]{:S(2)}) collective-permute-start(f32[256,256]{1,0:T(8,128)S(1)} %slice_select_fusion), channel_id=1, source_target_pairs={{0,2},{2,0},{1,3},{3,1},{4,6},{6,4},{5,7},{7,5},{8,10},{10,8},{9,1... | collective-permute-start | bytes 786440 | tf_op jit(solution)/shard_map/ppermute | solution.py:86

commit v15 on v13

--- a/solution.py
+++ b/solution.py
@@ -57,16 +57,15 @@
 
 
 def softmax_combine(a, b):
-    max_a, total_a, mixed_a = a
-    max_b, total_b, mixed_b = b
+    (max_a, total_a), mixed_a = a
+    (max_b, total_b), mixed_b = b
     mixed_a = mixed_a.astype(jnp.float32)
     mixed_b = mixed_b.astype(jnp.float32)
     top = jnp.maximum(max_a, max_b)
     factor_a = jnp.exp(max_a - top)
     factor_b = jnp.exp(max_b - top)
     return (
-        top,
-        total_a * factor_a + total_b * factor_b,
+        jnp.stack([top, total_a * factor_a + total_b * factor_b]),
         (scale_heads(mixed_a, factor_a) + scale_heads(mixed_b, factor_b)).astype(jnp.bfloat16),
     )
 
@@ -245,8 +244,8 @@
     local_mixed = jnp.einsum(
         "hqk,khd->qhd", raised, value_heads, preferred_element_type=jnp.float32
     ).reshape(query_count, model_width)
-    _, total, mixed = butterfly(
-        (local_max, local_total, local_mixed.astype(jnp.bfloat16)),
+    (_, total), mixed = butterfly(
+        (jnp.stack([local_max, local_total]), local_mixed.astype(jnp.bfloat16)),
         "phi",
         softmax_combine,
         ordered=True,

time: 98 us -> 94.9 us (0.968)
  waiting for transfers between devices: 33.7 us -> 40.5 us
  starting transfers between devices: 22.6 us -> 17.8 us
  matrix products: 21.1 us -> 16.8 us
  local copies, waits for them, and re-layouts: 5.02 us -> 3.42 us
    ppermute x10 -> x7, waiting for transfers between devices: 18.8 us -> 25.2 us  [butterfly(): other = lax.ppermute(tree, axis, partner_pairs(count, distance))]
    ppermute x10 -> x7, starting transfers between devices: 13.7 us -> 8.76 us  [butterfly(): other = lax.ppermute(tree, axis, partner_pairs(count, distance))]
    dot_general x1, matrix products: 4.91 us -> 1.52 us  [body(): jnp.einsum('hqk,khd->qhd', raised, value_heads, preferred_element_type=jn...]
    unnamed x25 -> x27, local copies, waits for them, and re-layouts: 3.03 us -> 1.42 us
  transfers between devices with their start and end apart: 16 -> 13, of which waited for: 11 -> 9; matrix products, arithmetic and copies ran while one was open for 12% -> 10% of each run, Pallas kernels for 0% -> 0%
where the time goes in v15:
time: 94.9 us; the launch traced here: 94.7 us
  waiting for transfers between devices  40.5 us (43%)
  starting transfers between devices  17.8 us (19%)
  matrix products  16.8 us (18%)
  other arithmetic  10.6 us (11%)
  blocking collectives  4.35 us (5%)
  local copies, waits for them, and re-layouts  3.42 us (4%)
  between operations  1.31 us (1%)
    ppermute x7, waiting for transfers between devices, butterfly(): other = lax.ppermute(tree, axis, partner_pairs(count, distance))  25.2 us
    ppermute x7, starting transfers between devices, butterfly(): other = lax.ppermute(tree, axis, partner_pairs(count, distance))  8.76 us
    ppermute x1, waiting for transfers between devices, narrow_butterfly(): other = lax.ppermute(sent, axis, partner_pairs(count, distance))  8.69 us
    ppermute x1, starting transfers between devices, extended_2(): lax.ppermute(lax.slice_in_dim(block, 0, width, axis=dim), axis, backward)  5.03 us
    ppermute x2, waiting for transfers between devices, partner_rows(): lax.ppermute(payload, 'phi', partner_pairs(lax.axis_size('phi'), distance))  4.87 us
    all_gather x1, blocking collectives, body(): lax.all_gather(jnp.concatenate([local_kv, encoded, digits], axis=1), 'que...  4.35 us
    dot_general x1, matrix products, body(): lax.dot_general(mask_embed, pair_hits, (((1,), (1,)), ((), ())), preferre...  4.24 us
    convert_element_type x1, other arithmetic, loss_coefficients(): (matched[:, None] * (sigma - target + dice_part) * model_width ** (-0.5))...  4.16 us
  transfers between devices with their start and end apart: 13, of which 9 were waited for; matrix products, arithmetic and copies ran while one was open for 10% of the time, Pallas kernels for 0%

profile of v15, /device:TPU:0, one launch (start us, length us, event | category | flops | bytes accessed | tf_op | source)
XLA Modules:
  0.0 94.7 jit_solution(7106013527384464986)
XLA Ops:
  0.7 1.1 %copy.50 = bf16[256,256]{0,1:T(8,128)(2,1)S(1)} copy(bf16[256,256]{1,0:T(8,128)(2,1)} %param.13) | data formatting | bytes 262144 | tf_op args[0]
  1.9 1.3 %convolution_convert_fusion = bf16[256,768]{1,0:T(8,128)(2,1)S(1)} fusion(bf16[256,768]{1,0:T(8,128)(2,1)} %param.14, bf16[256,256]{0,1:T(8,128)(2,1)S(1)} %copy.50, f32[256]{0:T(256)S(1)} %add_rsqrt_fusion.3, f32[256]{0:T(256)S(1)} %broadcast_multiply_fusion.3), kind=kOutput, calls=%fused_computation.31 | convolution fusion | flops 101122048 | bytes 919552 | tf_op jit(solution)/shard_map/dot_general | solution.py:194
  3.7 5.0 %collective-permute-start.1 = (bf16[256,512]{1,0:T(8,128)(2,1)S(1)}, bf16[256,512]{1,0:T(8,128)(2,1)S(1)}, u32[]{:S(2)}, u32[]{:S(2)}) collective-permute-start(bf16[256,512]{1,0:T(8,128)(2,1)S(1)} %slice.85), channel_id=1, source_target_pairs={{2,0},{4,2},{6,4},{8,6},{10,8},{12,10},{14,12},{16,14},{18,16},{20... | collective-permute-start | bytes 786440 | tf_op jit(solution)/shard_map/ppermute | solution.py:19
  11.2 1.7 %collective-permute-done = bf16[256,512]{1,0:T(8,128)(2,1)S(1)} collective-permute-done((bf16[256,512]{1,0:T(8,128)(2,1)S(1)}, bf16[256,512]{1,0:T(8,128)(2,1)S(1)}, u32[]{:S(2)}, u32[]{:S(2)}) %collective-permute-start) | collective-permute-done | bytes 262176 | tf_op jit(solution)/shard_map/ppermute | solution.py:16
  13.8 1.1 %fusion.140 = f32[8,128]{1,0:T(8,128)S(1)} fusion(pred[128,640]{1,0:T(8,128)(4,1)S(1)} %fusion.49, bf16[128,8,32]{0,2,1:T(8,128)(2,1)S(1)} %bitcast.186, bf16[640,8,32]{0,2,1:T(8,128)(2,1)S(1)} %bitcast.177), kind=kOutput, calls=%fused_computation.228 | convolution fusion | flops 44565120 | bytes 479232 | tf_op jit(solution)/shard_map/sub | solution.py:131
  15.0 1.4 %fusion.19 = bf16[8,32,128]{2,1,0:T(8,128)(2,1)S(1)} fusion(bf16[640,8,32]{0,2,1:T(8,128)(2,1)S(1)} %bitcast.179, f32[8,128]{1,0:T(8,128)S(1)} %fusion.140, pred[128,640]{1,0:T(8,128)(4,1)S(1)} %fusion.49, bf16[128,8,32]{0,2,1:T(8,128)(2,1)S(1)} %bitcast.187, bf16[640,8,32]{0,2,1:T(8,128)(2,1)S(1)} %bitcast.178), kind=kOutput, calls=%fused_computation.44 | convolution fusion | flops 87197312 | bytes 872448 | tf_op jit(solution)/shard_map/hqk,khd->qhd/dot_general | solution.py:133
  16.3 1.2 %fusion.139 = f32[8,128]{1,0:T(8,128)S(1)} fusion(pred[128,640]{1,0:T(8,128)(4,1)S(1)} %fusion.49, bf16[128,8,32]{0,2,1:T(8,128)(2,1)S(1)} %bitcast.184, bf16[640,8,32]{0,2,1:T(8,128)(2,1)S(1)} %bitcast.174), kind=kOutput, calls=%fused_computation.227 | convolution fusion | flops 44565120 | bytes 479232 | tf_op jit(solution)/shard_map/sub | solution.py:131
  17.5 1.3 %fusion.18 = bf16[8,32,128]{2,1,0:T(8,128)(2,1)S(1)} fusion(bf16[640,8,32]{0,2,1:T(8,128)(2,1)S(1)} %bitcast.176, f32[8,128]{1,0:T(8,128)S(1)} %fusion.139, pred[128,640]{1,0:T(8,128)(4,1)S(1)} %fusion.49, bf16[128,8,32]{0,2,1:T(8,128)(2,1)S(1)} %bitcast.185, bf16[640,8,32]{0,2,1:T(8,128)(2,1)S(1)} %bitcast.175), kind=kOutput, calls=%fused_computation.43 | convolution fusion | flops 87197312 | bytes 872448 | tf_op jit(solution)/shard_map/hqk,khd->qhd/dot_general | solution.py:133
  19.3 0.8 convert_reduce_fusion.3
  20.6 4.3 %all_gather.3 = bf16[512,896]{1,0:T(8,128)(2,1)S(1)} all-gather(bf16[256,896]{1,0:T(8,128)(2,1)S(1)} %fusion.46), channel_id=1, replica_groups=mesh['phi'=8,'query'=2,'event'=2] {'query'}, dimensions={0}, use_global_device_ids=true | all-gather | bytes 1376256 | tf_op jit(solution)/shard_map/all_gather | solution.py:225
  25.7 1.3 %multiply_reduce_fusion = (f32[8,512]{1,0:T(8,128)S(1)}, f32[8,512,512]{1,2,0:T(8,128)S(1)}) fusion(bf16[512,8,32]{0,2,1:T(8,128)(2,1)S(1)} %bitcast.168, bf16[512,8,32]{0,2,1:T(8,128)(2,1)S(1)} %bitcast.170), kind=kOutput, calls=%fused_computation.4 | convolution fusion | flops 138407936 | bytes 8929280 | tf_op jit(solution)/shard_map/qhd,khd->hqk/dot_general | solution.py:238
  27.0 1.4 %convert_reduce_fusion = f32[8,512]{1,0:T(8,128)S(1)} fusion(f32[8,512]{1,0:T(8,128)S(1)} %get-tuple-element.63, f32[8,512,512]{1,2,0:T(8,128)S(1)} %get-tuple-element.64), kind=kLoop, calls=%fused_computation.2 | loop fusion | flops 10481664 | bytes 8421376 | tf_op jit(solution)/shard_map/reduce_sum | solution.py:243
  28.4 2.0 %collective-permute-start.3 = (f32[2,8,512]{2,1,0:T(8,128)S(1)}, f32[2,8,512]{2,1,0:T(8,128)S(1)}, u32[]{:S(2)}, u32[]{:S(2)}) collective-permute-start(f32[2,8,512]{2,1,0:T(8,128)S(1)} %pad_maximum_fusion.1), channel_id=1, source_target_pairs={{0,4},{4,0},{8,12},{12,8},{16,20},{20,16},{24,28},{28,24},{1,5},{5... | collective-permute-start | bytes 98312 | tf_op jit(solution)/shard_map/ppermute | solution.py:33
  30.4 1.5 %convolution_convert_fusion.3 = bf16[8,32,512]{2,1,0:T(8,128)(2,1)S(1)} fusion(bf16[512,8,32]{0,2,1:T(8,128)(2,1)S(1)} %bitcast.169, f32[8,512,512]{1,2,0:T(8,128)S(1)} %get-tuple-element.64, f32[8,512]{1,0:T(8,128)S(1)} %get-tuple-element.63), kind=kOutput, calls=%fused_computation.36 | convolution fusion | flops 140640256 | bytes 8929280 | tf_op jit(solution)/shard_map/hqk,khd->qhd/dot_general | solution.py:244
  32.1 2.8 %collective-permute-done.3 = f32[2,8,512]{2,1,0:T(8,128)S(1)} collective-permute-done((f32[2,8,512]{2,1,0:T(8,128)S(1)}, f32[2,8,512]{2,1,0:T(8,128)S(1)}, u32[]{:S(2)}, u32[]{:S(2)}) %collective-permute-start.3) | collective-permute-done | bytes 32800 | tf_op jit(solution)/shard_map/ppermute | solution.py:33
  35.0 0.8 collective-permute-start.5
  35.8 3.2 %collective-permute-done.5 = f32[2,8,512]{2,1,0:T(8,128)S(1)} collective-permute-done((f32[2,8,512]{2,1,0:T(8,128)S(1)}, f32[2,8,512]{2,1,0:T(8,128)S(1)}, u32[]{:S(2)}, u32[]{:S(2)}) %collective-permute-start.5) | collective-permute-done | bytes 32800 | tf_op jit(solution)/shard_map/ppermute | solution.py:33
  39.0 1.8 %collective-permute-start.7 = (f32[2,8,512]{2,1,0:T(8,128)S(1)}, f32[2,8,512]{2,1,0:T(8,128)S(1)}, u32[]{:S(2)}, u32[]{:S(2)}) collective-permute-start(f32[2,8,512]{2,1,0:T(8,128)S(1)} %pad_maximum_fusion.3), channel_id=1, source_target_pairs={{0,16},{4,20},{8,24},{12,28},{16,0},{20,4},{24,8},{28,12},{1,17},{... | collective-permute-start | bytes 98312 | tf_op jit(solution)/shard_map/ppermute | solution.py:33
  40.8 3.4 %collective-permute-done.7 = f32[2,8,512]{2,1,0:T(8,128)S(1)} collective-permute-done((f32[2,8,512]{2,1,0:T(8,128)S(1)}, f32[2,8,512]{2,1,0:T(8,128)S(1)}, u32[]{:S(2)}, u32[]{:S(2)}) %collective-permute-start.7) | collective-permute-done | bytes 32800 | tf_op jit(solution)/shard_map/ppermute | solution.py:33
  45.3 5.7 %collective-permute-done.4 = bf16[512,256]{0,1:T(8,128)(2,1)S(1)} collective-permute-done((bf16[512,256]{0,1:T(8,128)(2,1)S(1)}, bf16[512,256]{0,1:T(8,128)(2,1)S(1)}, u32[]{:S(2)}, u32[]{:S(2)}) %collective-permute-start.4) | collective-permute-done | bytes 262176 | tf_op jit(solution)/shard_map/ppermute | solution.py:33
  51.2 2.2 %collective-permute-start.6 = (bf16[512,256]{0,1:T(8,128)(2,1)S(1)}, bf16[512,256]{0,1:T(8,128)(2,1)S(1)}, u32[]{:S(2)}, u32[]{:S(2)}) collective-permute-start(bf16[512,256]{0,1:T(8,128)(2,1)S(1)} %fusion.37), channel_id=1, source_target_pairs={{0,16},{4,20},{8,24},{12,28},{16,0},{20,4},{24,8},{28,12},{1,17},{... | collective-permute-start | bytes 786440 | tf_op jit(solution)/shard_map/ppermute | solution.py:33
  53.4 1.8 %collective-permute-start.9 = (bf16[1040,256]{1,0:T(8,128)(2,1)S(1)}, bf16[1040,256]{1,0:T(8,128)(2,1)S(1)}, u32[]{:S(2)}, u32[]{:S(2)}) collective-permute-start(bf16[1040,256]{1,0:T(8,128)(2,1)S(1)} %fusion.31), channel_id=1, source_target_pairs={{0,8},{4,12},{8,0},{12,4},{16,24},{20,28},{24,16},{28,20},{1,9},{5... | collective-permute-start | bytes 1597448 | tf_op jit(solution)/shard_map/ppermute | solution.py:95
  55.3 6.8 %collective-permute-done.6 = bf16[512,256]{0,1:T(8,128)(2,1)S(1)} collective-permute-done((bf16[512,256]{0,1:T(8,128)(2,1)S(1)}, bf16[512,256]{0,1:T(8,128)(2,1)S(1)}, u32[]{:S(2)}, u32[]{:S(2)}) %collective-permute-start.6) | collective-permute-done | bytes 262176 | tf_op jit(solution)/shard_map/ppermute | solution.py:33
  63.1 4.9 %collective-permute-done.9 = bf16[1040,256]{1,0:T(8,128)(2,1)S(1)} collective-permute-done((bf16[1040,256]{1,0:T(8,128)(2,1)S(1)}, bf16[1040,256]{1,0:T(8,128)(2,1)S(1)}, u32[]{:S(2)}, u32[]{:S(2)}) %collective-permute-start.9) | collective-permute-done | bytes 532512 | tf_op jit(solution)/shard_map/ppermute | solution.py:95
  68.1 4.2 %select_reduce_fusion = (f32[512]{0:T(512)S(1)}, f32[512]{0:T(512)S(1)}, f32[512]{0:T(512)S(1)}, f32[512,2048]{1,0:T(8,128)}) fusion(s32[2048]{0:T(1024)S(1)} %bitcast.189, s32[512]{0:T(512)S(1)} %copy-done.8, pred[512]{0:T(512)(128)(4,1)S(1)} %get-tuple-element.24, bf16[512,256]{1,0:T(8,128)(2,1)S(1)} %convolution_convert_fusion.2, ...), kind=kOutput, calls=%fused_computation.11 | convolution fusion | flops 553122304 | bytes 5521921 | tf_op jit(solution)/shard_map/dot_general | solution.py:274
  72.3 1.4 %collective-permute-start.10 = (f32[3,512]{1,0:T(4,128)S(1)}, f32[3,512]{1,0:T(4,128)S(1)}, u32[]{:S(2)}, u32[]{:S(2)}) collective-permute-start(f32[3,512]{1,0:T(4,128)S(1)} %pad_maximum_fusion.4), channel_id=1, source_target_pairs={{0,16},{4,20},{8,24},{12,28},{16,0},{20,4},{24,8},{28,12},{1,17},{... | collective-permute-start | bytes 18440 | tf_op jit(solution)/shard_map/ppermute | solution.py:33
  73.8 3.2 %collective-permute-done.10 = f32[3,512]{1,0:T(4,128)S(1)} collective-permute-done((f32[3,512]{1,0:T(4,128)S(1)}, f32[3,512]{1,0:T(4,128)S(1)}, u32[]{:S(2)}, u32[]{:S(2)}) %collective-permute-start.10) | collective-permute-done | bytes 6176 | tf_op jit(solution)/shard_map/ppermute | solution.py:33
  77.6 4.2 %fusion.5 = bf16[512,2048]{1,0:T(8,128)(2,1)S(1)} fusion(f32[512,2048]{1,0:T(8,128)} %get-tuple-element.67, f32[512]{0:T(512)S(1)} %bitcast.192, f32[512]{0:T(512)S(1)} %bitcast.193, s32[2048]{0:T(1024)S(1)} %bitcast.190, f32[512]{0:T(512)S(1)} %get-tuple-element.23, s32[512]{0:T(512)S(1)} %copy-done.8, pred[512]{0:T(512)(128)(4,1)S(1)} %get-tuple-element.24), kind=kLoop, calls=%fused_computation.10 | loop fusion | flops 14680064 | bytes 6308352 | tf_op jit(solution)/shard_map/convert_element_type | solution.py:168
  82.5 1.4 %collective-permute-start.12 = (bf16[512,256]{1,0:T(8,128)(2,1)S(1)}, bf16[512,256]{1,0:T(8,128)(2,1)S(1)}, u32[]{:S(2)}, u32[]{:S(2)}) collective-permute-start(bf16[512,256]{1,0:T(8,128)(2,1)S(1)} %convolution_convert_fusion.1), channel_id=1, source_target_pairs={{0,16},{4,20},{8,24},{12,28},{16,0},{20,4},{24,8},{28,12},{1,17},{... | collective-permute-start | bytes 786440 | tf_op jit(solution)/shard_map/ppermute | solution.py:53
  84.4 8.7 %collective-permute-done.12 = bf16[512,256]{1,0:T(8,128)(2,1)S(1)} collective-permute-done((bf16[512,256]{1,0:T(8,128)(2,1)S(1)}, bf16[512,256]{1,0:T(8,128)(2,1)S(1)}, u32[]{:S(2)}, u32[]{:S(2)}) %collective-permute-start.12) | collective-permute-done | bytes 262176 | tf_op jit(solution)/shard_map/ppermute | solution.py:53
  93.1 0.9 convert_add_fusion
  93.9 0.8 select_add_fusion
  (112 shorter events, 9.8 us)
Async XLA Ops:
  0.6 18.6 %copy-start = (bf16[1024,256]{1,0:T(8,128)(2,1)S(1)}, bf16[1024,256]{1,0:T(8,128)(2,1)}, u32[]{:S(2)}) copy-start(bf16[1024,256]{1,0:T(8,128)(2,1)} %param.17) | copy-start | bytes 1572868
  0.6 10.1 %copy-start.1 = (bf16[512,256]{1,0:T(8,128)(2,1)S(1)}, bf16[512,256]{1,0:T(8,128)(2,1)}, u32[]{:S(2)}) copy-start(bf16[512,256]{1,0:T(8,128)(2,1)} %param.18) | copy-start | bytes 786436
  0.7 10.2 %copy-start.5 = (bf16[256,256]{1,0:T(8,128)(2,1)S(1)}, bf16[256,256]{1,0:T(8,128)(2,1)}, u32[]{:S(2)}) copy-start(bf16[256,256]{1,0:T(8,128)(2,1)} %param.19) | copy-start | bytes 393220
  3.2 9.6 %collective-permute-start = (bf16[256,512]{1,0:T(8,128)(2,1)S(1)}, bf16[256,512]{1,0:T(8,128)(2,1)S(1)}, u32[]{:S(2)}, u32[]{:S(2)}) collective-permute-start(bf16[256,512]{1,0:T(8,128)(2,1)S(1)} %slice.85), channel_id=1, source_target_pairs={{0,2},{2,4},{4,6},{6,8},{8,10},{10,12},{12,14},{14,16},{16,18},{18... | collective-permute-start | bytes 786440 | tf_op jit(solution)/shard_map/ppermute | solution.py:16
  3.7 9.1 %collective-permute-start.1 = (bf16[256,512]{1,0:T(8,128)(2,1)S(1)}, bf16[256,512]{1,0:T(8,128)(2,1)S(1)}, u32[]{:S(2)}, u32[]{:S(2)}) collective-permute-start(bf16[256,512]{1,0:T(8,128)(2,1)S(1)} %slice.85), channel_id=1, source_target_pairs={{2,0},{4,2},{6,4},{8,6},{10,8},{12,10},{14,12},{16,14},{18,16},{20... | collective-permute-start | bytes 786440 | tf_op jit(solution)/shard_map/ppermute | solution.py:19
  17.5 1.4 %copy-start.6 = (bf16[256,256]{1,0:T(8,128)(2,1)S(1)}, bf16[256,256]{1,0:T(8,128)(2,1)}, u32[]{:S(2)}) copy-start(bf16[256,256]{1,0:T(8,128)(2,1)} %param.15) | copy-start | bytes 393220
  17.5 1.8 %copy-start.9 = (bf16[256,1024]{1,0:T(8,128)(2,1)S(1)}, bf16[256,1024]{1,0:T(8,128)(2,1)}, u32[]{:S(2)}) copy-start(bf16[256,1024]{1,0:T(8,128)(2,1)} %param.16) | copy-start | bytes 1572868
  18.9 1.4 %copy-start.4 = (bf16[256,512]{1,0:T(8,128)(2,1)S(1)}, bf16[256,512]{1,0:T(8,128)(2,1)}, u32[]{:S(2)}) copy-start(bf16[256,512]{1,0:T(8,128)(2,1)} %param.20) | copy-start | bytes 786436
  20.2 5.0 %copy-start.2 = (bf16[256,256]{1,0:T(8,128)(2,1)}, bf16[256,256]{1,0:T(8,128)(2,1)S(1)}, u32[]{:S(2)}) copy-start(bf16[256,256]{1,0:T(8,128)(2,1)S(1)} %copy.66) | copy-start | bytes 393220
  25.2 19.8 %collective-permute-start.8 = (bf16[528,256]{1,0:T(8,128)(2,1)S(1)}, bf16[528,256]{1,0:T(8,128)(2,1)S(1)}, u32[]{:S(2)}, u32[]{:S(2)}) collective-permute-start(bf16[528,256]{1,0:T(8,128)(2,1)S(1)} %fusion.58), channel_id=1, source_target_pairs={{0,4},{4,0},{8,12},{12,8},{16,20},{20,16},{24,28},{28,24},{1,5},{5... | collective-permute-start | bytes 811016 | tf_op jit(solution)/shard_map/ppermute | solution.py:95
  28.4 6.6 %collective-permute-start.3 = (f32[2,8,512]{2,1,0:T(8,128)S(1)}, f32[2,8,512]{2,1,0:T(8,128)S(1)}, u32[]{:S(2)}, u32[]{:S(2)}) collective-permute-start(f32[2,8,512]{2,1,0:T(8,128)S(1)} %pad_maximum_fusion.1), channel_id=1, source_target_pairs={{0,4},{4,0},{8,12},{12,8},{16,20},{20,16},{24,28},{28,24},{1,5},{5... | collective-permute-start | bytes 98312 | tf_op jit(solution)/shard_map/ppermute | solution.py:33
  32.0 12.3 %collective-permute-start.2 = (bf16[512,256]{0,1:T(8,128)(2,1)S(1)}, bf16[512,256]{0,1:T(8,128)(2,1)S(1)}, u32[]{:S(2)}, u32[]{:S(2)}) collective-permute-start(bf16[512,256]{0,1:T(8,128)(2,1)S(1)} %bitcast.171), channel_id=1, source_target_pairs={{0,4},{4,0},{8,12},{12,8},{16,20},{20,16},{24,28},{28,24},{1,5},{5... | collective-permute-start | bytes 786440 | tf_op jit(solution)/shard_map/ppermute | solution.py:33
  35.0 4.0 %collective-permute-start.5 = (f32[2,8,512]{2,1,0:T(8,128)S(1)}, f32[2,8,512]{2,1,0:T(8,128)S(1)}, u32[]{:S(2)}, u32[]{:S(2)}) collective-permute-start(f32[2,8,512]{2,1,0:T(8,128)S(1)} %pad_maximum_fusion.2), channel_id=1, source_target_pairs={{0,8},{4,12},{8,0},{12,4},{16,24},{20,28},{24,16},{28,20},{1,9},{5... | collective-permute-start | bytes 98312 | tf_op jit(solution)/shard_map/ppermute | solution.py:33
  39.0 5.2 %collective-permute-start.7 = (f32[2,8,512]{2,1,0:T(8,128)S(1)}, f32[2,8,512]{2,1,0:T(8,128)S(1)}, u32[]{:S(2)}, u32[]{:S(2)}) collective-permute-start(f32[2,8,512]{2,1,0:T(8,128)S(1)} %pad_maximum_fusion.3), channel_id=1, source_target_pairs={{0,16},{4,20},{8,24},{12,28},{16,0},{20,4},{24,8},{28,12},{1,17},{... | collective-permute-start | bytes 98312 | tf_op jit(solution)/shard_map/ppermute | solution.py:33
  44.3 18.0 %copy-start.7 = (bf16[256,256]{1,0:T(8,128)(2,1)S(1)}, bf16[256,256]{1,0:T(8,128)(2,1)}, u32[]{:S(2)}) copy-start(bf16[256,256]{1,0:T(8,128)(2,1)} %param.21) | copy-start | bytes 393220
  44.4 6.6 %collective-permute-start.4 = (bf16[512,256]{0,1:T(8,128)(2,1)S(1)}, bf16[512,256]{0,1:T(8,128)(2,1)S(1)}, u32[]{:S(2)}, u32[]{:S(2)}) collective-permute-start(bf16[512,256]{0,1:T(8,128)(2,1)S(1)} %fusion.39), channel_id=1, source_target_pairs={{0,8},{4,12},{8,0},{12,4},{16,24},{20,28},{24,16},{28,20},{1,9},{5... | collective-permute-start | bytes 786440 | tf_op jit(solution)/shard_map/ppermute | solution.py:33
  45.0 17.6 %copy-start.10 = (bf16[256,256]{1,0:T(8,128)(2,1)S(1)}, bf16[256,256]{1,0:T(8,128)(2,1)}, u32[]{:S(2)}) copy-start(bf16[256,256]{1,0:T(8,128)(2,1)} %param.23) | copy-start | bytes 393220
  45.1 17.6 %copy-start.11 = (bf16[256,256]{1,0:T(8,128)(2,1)S(1)}, bf16[256,256]{1,0:T(8,128)(2,1)}, u32[]{:S(2)}) copy-start(bf16[256,256]{1,0:T(8,128)(2,1)} %param.22) | copy-start | bytes 393220
  51.2 10.9 %collective-permute-start.6 = (bf16[512,256]{0,1:T(8,128)(2,1)S(1)}, bf16[512,256]{0,1:T(8,128)(2,1)S(1)}, u32[]{:S(2)}, u32[]{:S(2)}) collective-permute-start(bf16[512,256]{0,1:T(8,128)(2,1)S(1)} %fusion.37), channel_id=1, source_target_pairs={{0,16},{4,20},{8,24},{12,28},{16,0},{20,4},{24,8},{28,12},{1,17},{... | collective-permute-start | bytes 786440 | tf_op jit(solution)/shard_map/ppermute | solution.py:33
  53.4 14.7 %copy-start.8 = (s32[512]{0:T(512)S(1)}, s32[512]{0:T(512)}, u32[]{:S(2)}) copy-start(s32[512]{0:T(512)} %param.25) | copy-start | bytes 6148
  53.4 14.5 %collective-permute-start.9 = (bf16[1040,256]{1,0:T(8,128)(2,1)S(1)}, bf16[1040,256]{1,0:T(8,128)(2,1)S(1)}, u32[]{:S(2)}, u32[]{:S(2)}) collective-permute-start(bf16[1040,256]{1,0:T(8,128)(2,1)S(1)} %fusion.31), channel_id=1, source_target_pairs={{0,8},{4,12},{8,0},{12,4},{16,24},{20,28},{24,16},{28,20},{1,9},{5... | collective-permute-start | bytes 1597448 | tf_op jit(solution)/shard_map/ppermute | solution.py:95
  63.1 20.8 %copy-start.3 = (bf16[512,256]{1,0:T(8,128)(2,1)}, bf16[512,256]{1,0:T(8,128)(2,1)S(1)}, u32[]{:S(2)}) copy-start(bf16[512,256]{1,0:T(8,128)(2,1)S(1)} %convolution_convert_fusion.2) | copy-start | bytes 786436
  72.3 4.6 %collective-permute-start.10 = (f32[3,512]{1,0:T(4,128)S(1)}, f32[3,512]{1,0:T(4,128)S(1)}, u32[]{:S(2)}, u32[]{:S(2)}) collective-permute-start(f32[3,512]{1,0:T(4,128)S(1)} %pad_maximum_fusion.4), channel_id=1, source_target_pairs={{0,16},{4,20},{8,24},{12,28},{16,0},{20,4},{24,8},{28,12},{1,17},{... | collective-permute-start | bytes 18440 | tf_op jit(solution)/shard_map/ppermute | solution.py:33
  82.5 10.6 %collective-permute-start.12 = (bf16[512,256]{1,0:T(8,128)(2,1)S(1)}, bf16[512,256]{1,0:T(8,128)(2,1)S(1)}, u32[]{:S(2)}, u32[]{:S(2)}) collective-permute-start(bf16[512,256]{1,0:T(8,128)(2,1)S(1)} %convolution_convert_fusion.1), channel_id=1, source_target_pairs={{0,16},{4,20},{8,24},{12,28},{16,0},{20,4},{24,8},{28,12},{1,17},{... | collective-permute-start | bytes 786440 | tf_op jit(solution)/shard_map/ppermute | solution.py:53
  84.3 9.6 %collective-permute-start.11 = (f32[256,256]{1,0:T(8,128)S(1)}, f32[256,256]{1,0:T(8,128)S(1)}, u32[]{:S(2)}, u32[]{:S(2)}) collective-permute-start(f32[256,256]{1,0:T(8,128)S(1)} %slice_select_fusion), channel_id=1, source_target_pairs={{0,2},{2,0},{1,3},{3,1},{4,6},{6,4},{5,7},{7,5},{8,10},{10,8},{9,1... | collective-permute-start | bytes 786440 | tf_op jit(solution)/shard_map/ppermute | solution.py:84

commit v16 on v15

--- a/solution.py
+++ b/solution.py
@@ -67,6 +67,36 @@
     return (
         jnp.stack([top, total_a * factor_a + total_b * factor_b]),
         (scale_heads(mixed_a, factor_a) + scale_heads(mixed_b, factor_b)).astype(jnp.bfloat16),
+    )
+
+
+def pack_softmax(stats, mixed):
+    width = mixed.shape[1]
+    flat = stats.reshape(-1)
+    high = flat.astype(jnp.bfloat16)
+    rest = flat - high.astype(jnp.float32)
+    middle = rest.astype(jnp.bfloat16)
+    low = (rest - middle.astype(jnp.float32)).astype(jnp.bfloat16)
+    pieces = jnp.concatenate([high, middle, low]).reshape(-1, width)
+    return jnp.concatenate([mixed.astype(jnp.bfloat16), pieces])
+
+
+def unpack_softmax(packed, query_count):
+    pieces = packed[query_count:].reshape(3, -1).astype(jnp.float32)
+    stats = (pieces[0] + pieces[1] + pieces[2]).reshape(2, HEADS, query_count)
+    return stats, packed[:query_count].astype(jnp.float32)
+
+
+def packed_combine(a, b):
+    query_count = a.shape[0] * a.shape[1] // (a.shape[1] + 6 * HEADS)
+    (max_a, total_a), mixed_a = unpack_softmax(a, query_count)
+    (max_b, total_b), mixed_b = unpack_softmax(b, query_count)
+    top = jnp.maximum(max_a, max_b)
+    factor_a = jnp.exp(max_a - top)
+    factor_b = jnp.exp(max_b - top)
+    return pack_softmax(
+        jnp.stack([top, total_a * factor_a + total_b * factor_b]),
+        scale_heads(mixed_a, factor_a) + scale_heads(mixed_b, factor_b),
     )
 
 
@@ -244,13 +274,13 @@
     local_mixed = jnp.einsum(
         "hqk,khd->qhd", raised, value_heads, preferred_element_type=jnp.float32
     ).reshape(query_count, model_width)
-    (_, total), mixed = butterfly(
-        (jnp.stack([local_max, local_total]), local_mixed.astype(jnp.bfloat16)),
+    packed = butterfly(
+        pack_softmax(jnp.stack([local_max, local_total]), local_mixed),
         "phi",
-        softmax_combine,
+        packed_combine,
         ordered=True,
     )
-    mixed = mixed.astype(jnp.float32)
+    (_, total), mixed = unpack_softmax(packed, query_count)
     context = scale_heads(mixed, 1.0 / total).astype(jnp.bfloat16)
     mixed_queries = queries.astype(jnp.float32) + jnp.dot(
         context, cross_out, preferred_element_type=jnp.float32

time: 94.9 us -> 102 us (1.075)
  starting transfers between devices: 17.8 us -> 11.8 us
  other arithmetic: 10.6 us -> 16.2 us
  waiting for transfers between devices: 40.5 us -> 44.7 us
  local copies, waits for them, and re-layouts: 3.42 us -> 6.58 us
    ppermute x2, waiting for transfers between devices: 4.87 us -> 11.2 us  [partner_rows(): lax.ppermute(payload, 'phi', partner_pairs(lax.axis_size('phi'), distance))]
    ppermute x7 -> x4, starting transfers between devices: 8.76 us -> 4.6 us  [butterfly(): other = lax.ppermute(tree, axis, partner_pairs(count, distance))]
    ppermute x7 -> x4, waiting for transfers between devices: 25.2 us -> 21.5 us  [butterfly(): other = lax.ppermute(tree, axis, partner_pairs(count, distance))]
    select_n x3, other arithmetic: 0.02 us -> 2.47 us  [butterfly(): first = jax.tree.map(lambda a, b: jnp.where(upper, b, a), tree, other)]
    another operation x0 -> x30, local copies, waits for them, and re-layouts: none -> 1.45 us  [the longest x15 0.74 us: packed_combine(): (max_a, total_a), mixed_a = unpack_softmax(a, query_count)]
    ppermute x1, starting transfers between devices: 1.42 us -> 0.07 us  [narrow_butterfly(): other = lax.ppermute(sent, axis, partner_pairs(count, distance))]
    convert_element_type x0 -> x9, local copies, waits for them, and re-layouts: none -> 1.06 us  [the longest x3 0.36 us: pack_softmax(): high = flat.astype(jnp.bfloat16)]
  transfers between devices with their start and end apart: 13 -> 10, of which waited for: 9 -> 8; matrix products, arithmetic and copies ran while one was open for 10% -> 14% of each run, Pallas kernels for 0% -> 0%
where the time goes in v16:
time: 102 us
  waiting for transfers between devices  44.7 us (44%)
  matrix products  16.7 us (16%)
  other arithmetic  16.2 us (16%)
  starting transfers between devices  11.8 us (12%)
  local copies, waits for them, and re-layouts  6.58 us (6%)
  blocking collectives  4.35 us (4%)
  between operations  1.67 us (2%)
    ppermute x4, waiting for transfers between devices, butterfly(): other = lax.ppermute(tree, axis, partner_pairs(count, distance))  21.5 us
    ppermute x2, waiting for transfers between devices, partner_rows(): lax.ppermute(payload, 'phi', partner_pairs(lax.axis_size('phi'), distance))  11.2 us
    ppermute x1, waiting for transfers between devices, narrow_butterfly(): other = lax.ppermute(sent, axis, partner_pairs(count, distance))  9.61 us
    ppermute x1, starting transfers between devices, extended_2(): lax.ppermute(lax.slice_in_dim(block, 0, width, axis=dim), axis, backward)  5.03 us
    ppermute x4, starting transfers between devices, butterfly(): other = lax.ppermute(tree, axis, partner_pairs(count, distance))  4.6 us
    all_gather x1, blocking collectives, body(): lax.all_gather(jnp.concatenate([local_kv, encoded, digits], axis=1), 'que...  4.35 us
    dot_general x1, matrix products, body(): lax.dot_general(mask_embed, pair_hits, (((1,), (1,)), ((), ())), preferre...  4.18 us
    convert_element_type x1, other arithmetic, loss_coefficients(): (matched[:, None] * (sigma - target + dice_part) * model_width ** (-0.5))...  4.15 us
  transfers between devices with their start and end apart: 10, of which 8 were waited for; matrix products, arithmetic and copies ran while one was open for 14% of the time, Pallas kernels for 0%

profile of v16, /device:TPU:0, one launch (start us, length us, event | category | flops | bytes accessed | tf_op | source)
XLA Modules:
  0.0 102.0 jit_solution(5596494336352908954)
XLA Ops:
  0.7 1.1 %copy.168 = bf16[256,256]{0,1:T(8,128)(2,1)S(1)} copy(bf16[256,256]{1,0:T(8,128)(2,1)} %param.13) | data formatting | bytes 262144 | tf_op args[0]
  1.9 1.3 %convolution_convert_fusion = bf16[256,768]{1,0:T(8,128)(2,1)S(1)} fusion(bf16[256,768]{1,0:T(8,128)(2,1)} %param.14, bf16[256,256]{0,1:T(8,128)(2,1)S(1)} %copy.168, f32[256]{0:T(256)S(1)} %add_rsqrt_fusion.3, f32[256]{0:T(256)S(1)} %broadcast_multiply_fusion.3), kind=kOutput, calls=%fused_computation.31 | convolution fusion | flops 101122048 | bytes 919552 | tf_op jit(solution)/shard_map/dot_general | solution.py:224
  3.7 5.0 %collective-permute-start.1 = (bf16[256,512]{1,0:T(8,128)(2,1)S(1)}, bf16[256,512]{1,0:T(8,128)(2,1)S(1)}, u32[]{:S(2)}, u32[]{:S(2)}) collective-permute-start(bf16[256,512]{1,0:T(8,128)(2,1)S(1)} %slice.277), channel_id=1, source_target_pairs={{2,0},{4,2},{6,4},{8,6},{10,8},{12,10},{14,12},{16,14},{18,16},{20... | collective-permute-start | bytes 786440 | tf_op jit(solution)/shard_map/ppermute | solution.py:19
  10.5 2.4 %collective-permute-done = bf16[256,512]{1,0:T(8,128)(2,1)S(1)} collective-permute-done((bf16[256,512]{1,0:T(8,128)(2,1)S(1)}, bf16[256,512]{1,0:T(8,128)(2,1)S(1)}, u32[]{:S(2)}, u32[]{:S(2)}) %collective-permute-start) | collective-permute-done | bytes 262176 | tf_op jit(solution)/shard_map/ppermute | solution.py:16
  13.8 1.1 %fusion.142 = f32[8,128]{1,0:T(8,128)S(1)} fusion(pred[128,640]{1,0:T(8,128)(4,1)S(1)} %fusion.49, bf16[128,8,32]{0,2,1:T(8,128)(2,1)S(1)} %bitcast.145, bf16[640,8,32]{0,2,1:T(8,128)(2,1)S(1)} %bitcast.133), kind=kOutput, calls=%fused_computation.259 | convolution fusion | flops 44565120 | bytes 479232 | tf_op jit(solution)/shard_map/sub | solution.py:161
  15.0 1.3 %fusion.19 = bf16[8,32,128]{2,1,0:T(8,128)(2,1)S(1)} fusion(bf16[640,8,32]{0,2,1:T(8,128)(2,1)S(1)} %bitcast.135, f32[8,128]{1,0:T(8,128)S(1)} %fusion.142, pred[128,640]{1,0:T(8,128)(4,1)S(1)} %fusion.49, bf16[128,8,32]{0,2,1:T(8,128)(2,1)S(1)} %bitcast.146, bf16[640,8,32]{0,2,1:T(8,128)(2,1)S(1)} %bitcast.134), kind=kOutput, calls=%fused_computation.44 | convolution fusion | flops 87197312 | bytes 872448 | tf_op jit(solution)/shard_map/hqk,khd->qhd/dot_general | solution.py:163
  16.3 1.2 %fusion.141 = f32[8,128]{1,0:T(8,128)S(1)} fusion(pred[128,640]{1,0:T(8,128)(4,1)S(1)} %fusion.49, bf16[128,8,32]{0,2,1:T(8,128)(2,1)S(1)} %bitcast.143, bf16[640,8,32]{0,2,1:T(8,128)(2,1)S(1)} %bitcast.130), kind=kOutput, calls=%fused_computation.258 | convolution fusion | flops 44565120 | bytes 479232 | tf_op jit(solution)/shard_map/sub | solution.py:161
  17.5 1.3 %fusion.18 = bf16[8,32,128]{2,1,0:T(8,128)(2,1)S(1)} fusion(bf16[640,8,32]{0,2,1:T(8,128)(2,1)S(1)} %bitcast.132, f32[8,128]{1,0:T(8,128)S(1)} %fusion.141, pred[128,640]{1,0:T(8,128)(4,1)S(1)} %fusion.49, bf16[128,8,32]{0,2,1:T(8,128)(2,1)S(1)} %bitcast.144, bf16[640,8,32]{0,2,1:T(8,128)(2,1)S(1)} %bitcast.131), kind=kOutput, calls=%fused_computation.43 | convolution fusion | flops 87197312 | bytes 872448 | tf_op jit(solution)/shard_map/hqk,khd->qhd/dot_general | solution.py:163
  19.2 0.8 convert_reduce_fusion.3
  20.6 4.3 %all_gather.3 = bf16[512,896]{1,0:T(8,128)(2,1)S(1)} all-gather(bf16[256,896]{1,0:T(8,128)(2,1)S(1)} %fusion.46), channel_id=1, replica_groups=mesh['phi'=8,'query'=2,'event'=2] {'query'}, dimensions={0}, use_global_device_ids=true | all-gather | bytes 1376256 | tf_op jit(solution)/shard_map/all_gather | solution.py:255
  25.6 1.3 %multiply_reduce_fusion = (f32[8,512]{1,0:T(8,128)S(1)}, f32[8,512,512]{1,2,0:T(8,128)S(1)}) fusion(bf16[512,8,32]{0,2,1:T(8,128)(2,1)S(1)} %bitcast.127, bf16[512,8,32]{0,2,1:T(8,128)(2,1)S(1)} %bitcast.129), kind=kOutput, calls=%fused_computation.4 | convolution fusion | flops 138407936 | bytes 8929280 | tf_op jit(solution)/shard_map/qhd,khd->hqk/dot_general | solution.py:268
  26.9 1.4 %convert_reduce_fusion = f32[8,512]{1,0:T(8,128)S(1)} fusion(f32[8,512]{1,0:T(8,128)S(1)} %get-tuple-element.105, f32[8,512,512]{1,2,0:T(8,128)S(1)} %get-tuple-element.106), kind=kLoop, calls=%fused_computation.2 | loop fusion | flops 10481664 | bytes 8421376 | tf_op jit(solution)/shard_map/reduce_sum | solution.py:273
  28.3 1.5 %convolution_convert_fusion.3 = bf16[8,32,512]{2,1,0:T(8,128)(2,1)S(1)} fusion(bf16[512,8,32]{0,2,1:T(8,128)(2,1)S(1)} %bitcast.128, f32[8,512,512]{1,2,0:T(8,128)S(1)} %get-tuple-element.106, f32[8,512]{1,0:T(8,128)S(1)} %get-tuple-element.105), kind=kOutput, calls=%fused_computation.36 | convolution fusion | flops 140640256 | bytes 8929280 | tf_op jit(solution)/shard_map/hqk,khd->qhd/dot_general | solution.py:274
  30.4 2.0 %collective-permute-start.2 = (bf16[608,256]{0,1:T(8,128)(2,1)S(1)}, bf16[608,256]{0,1:T(8,128)(2,1)S(1)}, u32[]{:S(2)}, u32[]{:S(2)}) collective-permute-start(bf16[608,256]{0,1:T(8,128)(2,1)S(1)} %pad_maximum_fusion.1), channel_id=1, source_target_pairs={{0,4},{4,0},{8,12},{12,8},{16,20},{20,16},{24,28},{28,24},{1,5},{5... | collective-permute-start | bytes 933896 | tf_op jit(solution)/shard_map/ppermute | solution.py:33
  33.7 0.9 collective-permute-done.5
  34.8 6.2 %collective-permute-done.2 = bf16[608,256]{0,1:T(8,128)(2,1)S(1)} collective-permute-done((bf16[608,256]{0,1:T(8,128)(2,1)S(1)}, bf16[608,256]{0,1:T(8,128)(2,1)S(1)}, u32[]{:S(2)}, u32[]{:S(2)}) %collective-permute-start.2) | collective-permute-done | bytes 311328 | tf_op jit(solution)/shard_map/ppermute | solution.py:33
  42.7 0.8 collective-permute-start.3
  43.5 1.4 %collective-permute-start.6 = (bf16[1040,256]{1,0:T(8,128)(2,1)S(1)}, bf16[1040,256]{1,0:T(8,128)(2,1)S(1)}, u32[]{:S(2)}, u32[]{:S(2)}) collective-permute-start(bf16[1040,256]{1,0:T(8,128)(2,1)S(1)} %fusion.31), channel_id=1, source_target_pairs={{0,8},{4,12},{8,0},{12,4},{16,24},{20,28},{24,16},{28,20},{1,9},{5... | collective-permute-start | bytes 1597448 | tf_op jit(solution)/shard_map/ppermute | solution.py:125
  44.9 8.6 %collective-permute-done.3 = bf16[608,256]{0,1:T(8,128)(2,1)} collective-permute-done((bf16[608,256]{0,1:T(8,128)(2,1)S(1)}, bf16[608,256]{0,1:T(8,128)(2,1)}, u32[]{:S(2)}, u32[]{:S(2)}) %collective-permute-start.3) | collective-permute-done | bytes 311328 | tf_op jit(solution)/shard_map/ppermute | solution.py:33
  53.5 1.1 %broadcast_select_fusion.3 = (bf16[608,256]{0,1:T(8,128)(2,1)S(1)}, bf16[608,256]{0,1:T(8,128)(2,1)S(1)}) fusion(bf16[608,256]{0,1:T(8,128)(2,1)} %collective-permute-done.3, pred[]{:T(512)S(6)} %eq.38, bf16[32,256]{0,1:T(8,128)(2,1)S(1)} %copy.190, bf16[32,256]{0,1:T(8,128)(2,1)S(1)} %copy.189, bf16[32,256]{0,1:T(8,128)(2,1)S(1)} %copy.188, ...), kind=kLoop, calls=%fused_computation.101 | loop fusion | flops 1556480 | bytes 1245185 | tf_op jit(solution)/shard_map/jit(_where)/select_n | solution.py:36
  56.5 0.8 fusion.37
  57.5 1.8 %collective-permute-start.4 = (bf16[608,256]{0,1:T(8,128)(2,1)S(1)}, bf16[608,256]{0,1:T(8,128)(2,1)}, u32[]{:S(2)}, u32[]{:S(2)}) collective-permute-start(bf16[608,256]{0,1:T(8,128)(2,1)S(1)} %pad_maximum_fusion.3), channel_id=1, source_target_pairs={{0,16},{4,20},{8,24},{12,28},{16,0},{20,4},{24,8},{28,12},{1,17},{... | collective-permute-start | bytes 933896 | tf_op jit(solution)/shard_map/ppermute | solution.py:33
  59.2 10.3 %collective-permute-done.6 = bf16[1040,256]{1,0:T(8,128)(2,1)S(1)} collective-permute-done((bf16[1040,256]{1,0:T(8,128)(2,1)S(1)}, bf16[1040,256]{1,0:T(8,128)(2,1)S(1)}, u32[]{:S(2)}, u32[]{:S(2)}) %collective-permute-start.6) | collective-permute-done | bytes 532512 | tf_op jit(solution)/shard_map/ppermute | solution.py:125
  69.5 0.8 fusion.87
  70.4 2.3 %collective-permute-done.4 = bf16[608,256]{0,1:T(8,128)(2,1)} collective-permute-done((bf16[608,256]{0,1:T(8,128)(2,1)S(1)}, bf16[608,256]{0,1:T(8,128)(2,1)}, u32[]{:S(2)}, u32[]{:S(2)}) %collective-permute-start.4) | collective-permute-done | bytes 311328 | tf_op jit(solution)/shard_map/ppermute | solution.py:33
  72.6 1.1 %broadcast_select_fusion.5 = (bf16[608,256]{0,1:T(8,128)(2,1)S(1)}, bf16[608,256]{0,1:T(8,128)(2,1)S(1)}) fusion(bf16[608,256]{0,1:T(8,128)(2,1)} %collective-permute-done.4, pred[]{:T(512)S(6)} %eq.37, bf16[32,256]{0,1:T(8,128)(2,1)S(1)} %copy.197, bf16[32,256]{0,1:T(8,128)(2,1)S(1)} %copy.196, bf16[32,256]{0,1:T(8,128)(2,1)S(1)} %copy.195, ...), kind=kLoop, calls=%fused_computation.103 | loop fusion | flops 1556480 | bytes 1245185 | tf_op jit(solution)/shard_map/jit(_where)/select_n | solution.py:36
  75.8 4.2 %select_reduce_fusion = (f32[512]{0:T(512)S(1)}, f32[512]{0:T(512)S(1)}, f32[512]{0:T(512)S(1)}, f32[512,2048]{1,0:T(8,128)}) fusion(s32[2048]{0:T(1024)S(1)} %bitcast.148, s32[512]{0:T(512)S(1)} %copy-done.10, pred[512]{0:T(512)(128)(4,1)S(1)} %copy-done.13, bf16[512,256]{1,0:T(8,128)(2,1)S(1)} %convolution_convert_fusion.2, ...), kind=kOutput, calls=%fused_computation.11 | convolution fusion | flops 553122304 | bytes 5521921 | tf_op jit(solution)/shard_map/dot_general | solution.py:304
  80.1 4.5 %collective-permute-done.7 = f32[3,512]{1,0:T(4,128)S(1)} collective-permute-done((f32[3,512]{1,0:T(4,128)S(1)}, f32[3,512]{1,0:T(4,128)S(1)}, u32[]{:S(2)}, u32[]{:S(2)}) %collective-permute-start.7) | collective-permute-done | bytes 6176 | tf_op jit(solution)/shard_map/ppermute | solution.py:33
  85.3 4.2 %fusion.5 = bf16[512,2048]{1,0:T(8,128)(2,1)S(1)} fusion(f32[512,2048]{1,0:T(8,128)} %get-tuple-element.109, f32[512]{0:T(512)S(1)} %bitcast.151, f32[512]{0:T(512)S(1)} %bitcast.152, s32[2048]{0:T(1024)S(1)} %bitcast.149, f32[512]{0:T(512)S(1)} %copy-done.11, s32[512]{0:T(512)S(1)} %copy-done.10, pred[512]{0:T(512)(128)(4,1)S(1)} %copy-done.13), kind=kLoop, calls=%fused_computation.10 | loop fusion | flops 14680064 | bytes 6308352 | tf_op jit(solution)/shard_map/convert_element_type | solution.py:198
  90.7 9.6 %collective-permute-done.9 = bf16[512,256]{1,0:T(8,128)(2,1)S(1)} collective-permute-done((bf16[512,256]{1,0:T(8,128)(2,1)S(1)}, bf16[512,256]{1,0:T(8,128)(2,1)S(1)}, u32[]{:S(2)}, u32[]{:S(2)}) %collective-permute-start.9) | collective-permute-done | bytes 262176 | tf_op jit(solution)/shard_map/ppermute | solution.py:53
  100.4 0.9 convert_add_fusion
  101.2 0.8 select_add_fusion
  (181 shorter events, 14.1 us)
Async XLA Ops:
  0.6 18.6 %copy-start = (bf16[1024,256]{1,0:T(8,128)(2,1)S(1)}, bf16[1024,256]{1,0:T(8,128)(2,1)}, u32[]{:S(2)}) copy-start(bf16[1024,256]{1,0:T(8,128)(2,1)} %param.17) | copy-start | bytes 1572868
  0.6 9.4 %copy-start.1 = (bf16[512,256]{1,0:T(8,128)(2,1)S(1)}, bf16[512,256]{1,0:T(8,128)(2,1)}, u32[]{:S(2)}) copy-start(bf16[512,256]{1,0:T(8,128)(2,1)} %param.18) | copy-start | bytes 786436
  0.7 9.5 %copy-start.5 = (bf16[256,256]{1,0:T(8,128)(2,1)S(1)}, bf16[256,256]{1,0:T(8,128)(2,1)}, u32[]{:S(2)}) copy-start(bf16[256,256]{1,0:T(8,128)(2,1)} %param.19) | copy-start | bytes 393220
  3.2 9.6 %collective-permute-start = (bf16[256,512]{1,0:T(8,128)(2,1)S(1)}, bf16[256,512]{1,0:T(8,128)(2,1)S(1)}, u32[]{:S(2)}, u32[]{:S(2)}) collective-permute-start(bf16[256,512]{1,0:T(8,128)(2,1)S(1)} %slice.277), channel_id=1, source_target_pairs={{0,2},{2,4},{4,6},{6,8},{8,10},{10,12},{12,14},{14,16},{16,18},{18... | collective-permute-start | bytes 786440 | tf_op jit(solution)/shard_map/ppermute | solution.py:16
  3.7 9.1 %collective-permute-start.1 = (bf16[256,512]{1,0:T(8,128)(2,1)S(1)}, bf16[256,512]{1,0:T(8,128)(2,1)S(1)}, u32[]{:S(2)}, u32[]{:S(2)}) collective-permute-start(bf16[256,512]{1,0:T(8,128)(2,1)S(1)} %slice.277), channel_id=1, source_target_pairs={{2,0},{4,2},{6,4},{8,6},{10,8},{12,10},{14,12},{16,14},{18,16},{20... | collective-permute-start | bytes 786440 | tf_op jit(solution)/shard_map/ppermute | solution.py:19
  17.5 1.4 %copy-start.6 = (bf16[256,256]{1,0:T(8,128)(2,1)S(1)}, bf16[256,256]{1,0:T(8,128)(2,1)}, u32[]{:S(2)}) copy-start(bf16[256,256]{1,0:T(8,128)(2,1)} %param.15) | copy-start | bytes 393220
  17.5 1.7 %copy-start.14 = (bf16[256,1024]{1,0:T(8,128)(2,1)S(1)}, bf16[256,1024]{1,0:T(8,128)(2,1)}, u32[]{:S(2)}) copy-start(bf16[256,1024]{1,0:T(8,128)(2,1)} %param.16) | copy-start | bytes 1572868
  18.8 1.4 %copy-start.4 = (bf16[256,512]{1,0:T(8,128)(2,1)S(1)}, bf16[256,512]{1,0:T(8,128)(2,1)}, u32[]{:S(2)}) copy-start(bf16[256,512]{1,0:T(8,128)(2,1)} %param.20) | copy-start | bytes 786436
  20.2 5.0 %copy-start.2 = (bf16[256,256]{1,0:T(8,128)(2,1)}, bf16[256,256]{1,0:T(8,128)(2,1)S(1)}, u32[]{:S(2)}) copy-start(bf16[256,256]{1,0:T(8,128)(2,1)S(1)} %copy.205) | copy-start | bytes 393220
  25.2 9.4 %collective-permute-start.5 = (bf16[528,256]{1,0:T(8,128)(2,1)S(1)}, bf16[528,256]{1,0:T(8,128)(2,1)S(1)}, u32[]{:S(2)}, u32[]{:S(2)}) collective-permute-start(bf16[528,256]{1,0:T(8,128)(2,1)S(1)} %fusion.58), channel_id=1, source_target_pairs={{0,4},{4,0},{8,12},{12,8},{16,20},{20,16},{24,28},{28,24},{1,5},{5... | collective-permute-start | bytes 811016 | tf_op jit(solution)/shard_map/ppermute | solution.py:125
  28.3 4.1 %copy-start.9 = (s32[512]{0:T(512)S(1)}, s32[512]{0:T(512)}, u32[]{:S(2)}) copy-start(s32[512]{0:T(512)} %param.25) | copy-start | bytes 6148
  30.4 10.6 %collective-permute-start.2 = (bf16[608,256]{0,1:T(8,128)(2,1)S(1)}, bf16[608,256]{0,1:T(8,128)(2,1)S(1)}, u32[]{:S(2)}, u32[]{:S(2)}) collective-permute-start(bf16[608,256]{0,1:T(8,128)(2,1)S(1)} %pad_maximum_fusion.1), channel_id=1, source_target_pairs={{0,4},{4,0},{8,12},{12,8},{16,20},{20,16},{24,28},{28,24},{1,5},{5... | collective-permute-start | bytes 933896 | tf_op jit(solution)/shard_map/ppermute | solution.py:33
  41.2 2.3 %copy-start.12 = (bf16[512,2]{0,1:T(2,128)(2,1)S(1)}, bf16[512,2]{0,1:T(2,128)(2,1)}, u32[]{:S(2)}) copy-start(bf16[512,2]{0,1:T(2,128)(2,1)} %copy.203) | copy-start | bytes 6148
  42.7 10.8 %collective-permute-start.3 = (bf16[608,256]{0,1:T(8,128)(2,1)S(1)}, bf16[608,256]{0,1:T(8,128)(2,1)}, u32[]{:S(2)}, u32[]{:S(2)}) collective-permute-start(bf16[608,256]{0,1:T(8,128)(2,1)S(1)} %pad_maximum_fusion.2), channel_id=1, source_target_pairs={{0,8},{4,12},{8,0},{12,4},{16,24},{20,28},{24,16},{28,20},{1,9},{5... | collective-permute-start | bytes 933896 | tf_op jit(solution)/shard_map/ppermute | solution.py:33
  43.5 11.9 %copy-start.8 = (bf16[1024,2]{0,1:T(2,128)(2,1)}, bf16[1024,2]{0,1:T(2,128)(2,1)S(1)}, u32[]{:S(2)}) copy-start(bf16[1024,2]{0,1:T(2,128)(2,1)S(1)} %broadcast_select_fusion.7) | copy-start | bytes 12292
  43.5 26.0 %collective-permute-start.6 = (bf16[1040,256]{1,0:T(8,128)(2,1)S(1)}, bf16[1040,256]{1,0:T(8,128)(2,1)S(1)}, u32[]{:S(2)}, u32[]{:S(2)}) collective-permute-start(bf16[1040,256]{1,0:T(8,128)(2,1)S(1)} %fusion.31), channel_id=1, source_target_pairs={{0,8},{4,12},{8,0},{12,4},{16,24},{20,28},{24,16},{28,20},{1,9},{5... | collective-permute-start | bytes 1597448 | tf_op jit(solution)/shard_map/ppermute | solution.py:125
  57.5 15.2 %collective-permute-start.4 = (bf16[608,256]{0,1:T(8,128)(2,1)S(1)}, bf16[608,256]{0,1:T(8,128)(2,1)}, u32[]{:S(2)}, u32[]{:S(2)}) collective-permute-start(bf16[608,256]{0,1:T(8,128)(2,1)S(1)} %pad_maximum_fusion.3), channel_id=1, source_target_pairs={{0,16},{4,20},{8,24},{12,28},{16,0},{20,4},{24,8},{28,12},{1,17},{... | collective-permute-start | bytes 933896 | tf_op jit(solution)/shard_map/ppermute | solution.py:33
  73.8 1.2 %copy-start.7 = (bf16[256,256]{1,0:T(8,128)(2,1)S(1)}, bf16[256,256]{1,0:T(8,128)(2,1)}, u32[]{:S(2)}) copy-start(bf16[256,256]{1,0:T(8,128)(2,1)} %param.21) | copy-start | bytes 393220
  74.1 1.2 %copy-start.15 = (bf16[256,256]{1,0:T(8,128)(2,1)S(1)}, bf16[256,256]{1,0:T(8,128)(2,1)}, u32[]{:S(2)}) copy-start(bf16[256,256]{1,0:T(8,128)(2,1)} %param.23) | copy-start | bytes 393220
  74.1 1.2 %copy-start.16 = (bf16[256,256]{1,0:T(8,128)(2,1)S(1)}, bf16[256,256]{1,0:T(8,128)(2,1)}, u32[]{:S(2)}) copy-start(bf16[256,256]{1,0:T(8,128)(2,1)} %param.22) | copy-start | bytes 393220
  74.4 1.4 %copy-start.10 = (s32[512]{0:T(512)S(1)}, s32[512]{0:T(512)}, u32[]{:S(2)}) copy-start(s32[512]{0:T(512)} %param.25) | copy-start | bytes 6148
  74.4 1.4 %copy-start.13 = (pred[512]{0:T(512)(128)(4,1)S(1)}, pred[512]{0:T(512)(128)(4,1)}, u32[]{:S(2)}) copy-start(pred[512]{0:T(512)(128)(4,1)} %get-tuple-element.39) | copy-start | bytes 1540
  75.8 14.5 %copy-start.3 = (bf16[512,256]{1,0:T(8,128)(2,1)}, bf16[512,256]{1,0:T(8,128)(2,1)S(1)}, u32[]{:S(2)}) copy-start(bf16[512,256]{1,0:T(8,128)(2,1)S(1)} %convolution_convert_fusion.2) | copy-start | bytes 786436
  75.8 9.4 %copy-start.11 = (f32[512]{0:T(512)S(1)}, f32[512]{0:T(512)}, u32[]{:S(2)}) copy-start(f32[512]{0:T(512)} %get-tuple-element.38) | copy-start | bytes 6148
  80.0 4.6 %collective-permute-start.7 = (f32[3,512]{1,0:T(4,128)S(1)}, f32[3,512]{1,0:T(4,128)S(1)}, u32[]{:S(2)}, u32[]{:S(2)}) collective-permute-start(f32[3,512]{1,0:T(4,128)S(1)} %pad_maximum_fusion.7), channel_id=1, source_target_pairs={{0,16},{4,20},{8,24},{12,28},{16,0},{20,4},{24,8},{28,12},{1,17},{... | collective-permute-start | bytes 18440 | tf_op jit(solution)/shard_map/ppermute | solution.py:33
  90.2 10.2 %collective-permute-start.9 = (bf16[512,256]{1,0:T(8,128)(2,1)S(1)}, bf16[512,256]{1,0:T(8,128)(2,1)S(1)}, u32[]{:S(2)}, u32[]{:S(2)}) collective-permute-start(bf16[512,256]{1,0:T(8,128)(2,1)S(1)} %convolution_convert_fusion.1), channel_id=1, source_target_pairs={{0,16},{4,20},{8,24},{12,28},{16,0},{20,4},{24,8},{28,12},{1,17},{... | collective-permute-start | bytes 786440 | tf_op jit(solution)/shard_map/ppermute | solution.py:53
  90.7 10.6 %collective-permute-start.8 = (f32[256,256]{1,0:T(8,128)S(1)}, f32[256,256]{1,0:T(8,128)S(1)}, u32[]{:S(2)}, u32[]{:S(2)}) collective-permute-start(f32[256,256]{1,0:T(8,128)S(1)} %slice_select_fusion), channel_id=1, source_target_pairs={{0,2},{2,0},{1,3},{3,1},{4,6},{6,4},{5,7},{7,5},{8,10},{10,8},{9,1... | collective-permute-start | bytes 786440 | tf_op jit(solution)/shard_map/ppermute | solution.py:114

commit v17 on v15

--- a/solution.py
+++ b/solution.py
@@ -162,12 +162,11 @@
     sigma, target, matched, intersection, predicted, truth_count, hits_total, model_width
 ):
     denom = predicted + truth_count + 1.0
-    slope = -2.0 / denom
-    level = (2.0 * intersection + 1.0) / (denom * denom)
-    dice_part = hits_total * (slope[:, None] * target + level[:, None]) * sigma * (1.0 - sigma)
-    return (matched[:, None] * (sigma - target + dice_part) * model_width ** (-0.5)).astype(
-        jnp.bfloat16
-    )
+    weight = matched * model_width ** (-0.5)
+    slope = weight * hits_total * (-2.0 / denom)
+    level = weight * hits_total * ((2.0 * intersection + 1.0) / (denom * denom))
+    dice_part = (slope[:, None] * target + level[:, None]) * (sigma * (1.0 - sigma))
+    return (weight[:, None] * (sigma - target) + dice_part).astype(jnp.bfloat16)
 
 
 def body(

time: 94.9 us -> 94.7 us (level)
    convert_element_type x2 -> x1, other arithmetic: 4.85 us -> 3.89 us  [loss_coefficients(): return (weight[:, None] * (sigma - target) + dice_part).astype(jnp.bfloat16)]
where the time goes in v17:
time: 94.7 us; the launch traced here: 94.4 us
  waiting for transfers between devices  40.5 us (43%)
  starting transfers between devices  17.8 us (19%)
  matrix products  16.8 us (18%)
  other arithmetic  10.3 us (11%)
  blocking collectives  4.35 us (5%)
  local copies, waits for them, and re-layouts  3.42 us (4%)
  between operations  1.31 us (1%)
    ppermute x7, waiting for transfers between devices, butterfly(): other = lax.ppermute(tree, axis, partner_pairs(count, distance))  25.2 us
    ppermute x7, starting transfers between devices, butterfly(): other = lax.ppermute(tree, axis, partner_pairs(count, distance))  8.76 us
    ppermute x1, waiting for transfers between devices, narrow_butterfly(): other = lax.ppermute(sent, axis, partner_pairs(count, distance))  8.69 us
    ppermute x1, starting transfers between devices, extended_2(): lax.ppermute(lax.slice_in_dim(block, 0, width, axis=dim), axis, backward)  5.03 us
    ppermute x2, waiting for transfers between devices, partner_rows(): lax.ppermute(payload, 'phi', partner_pairs(lax.axis_size('phi'), distance))  4.87 us
    all_gather x1, blocking collectives, body(): lax.all_gather(jnp.concatenate([local_kv, encoded, digits], axis=1), 'que...  4.35 us
    dot_general x1, matrix products, body(): lax.dot_general(mask_embed, pair_hits, (((1,), (1,)), ((), ())), preferre...  4.24 us
    convert_element_type x1, other arithmetic, loss_coefficients(): return (weight[:, None] * (sigma - target) + dice_part).astype(jnp.bfloat16)  3.89 us
  transfers between devices with their start and end apart: 13, of which 9 were waited for; matrix products, arithmetic and copies ran while one was open for 10% of the time, Pallas kernels for 0%

profile of v17, /device:TPU:0, one launch (start us, length us, event | category | flops | bytes accessed | tf_op | source)
XLA Modules:
  0.0 94.4 jit_solution(7946173476953522747)
XLA Ops:
  0.7 1.1 %copy.50 = bf16[256,256]{0,1:T(8,128)(2,1)S(1)} copy(bf16[256,256]{1,0:T(8,128)(2,1)} %param.13) | data formatting | bytes 262144 | tf_op args[0]
  1.9 1.3 %convolution_convert_fusion = bf16[256,768]{1,0:T(8,128)(2,1)S(1)} fusion(bf16[256,768]{1,0:T(8,128)(2,1)} %param.14, bf16[256,256]{0,1:T(8,128)(2,1)S(1)} %copy.50, f32[256]{0:T(256)S(1)} %add_rsqrt_fusion.3, f32[256]{0:T(256)S(1)} %broadcast_multiply_fusion.3), kind=kOutput, calls=%fused_computation.32 | convolution fusion | flops 101122048 | bytes 919552 | tf_op jit(solution)/shard_map/dot_general | solution.py:193
  3.7 5.0 %collective-permute-start.1 = (bf16[256,512]{1,0:T(8,128)(2,1)S(1)}, bf16[256,512]{1,0:T(8,128)(2,1)S(1)}, u32[]{:S(2)}, u32[]{:S(2)}) collective-permute-start(bf16[256,512]{1,0:T(8,128)(2,1)S(1)} %slice.85), channel_id=1, source_target_pairs={{2,0},{4,2},{6,4},{8,6},{10,8},{12,10},{14,12},{16,14},{18,16},{20... | collective-permute-start | bytes 786440 | tf_op jit(solution)/shard_map/ppermute | solution.py:19
  11.2 1.7 %collective-permute-done = bf16[256,512]{1,0:T(8,128)(2,1)S(1)} collective-permute-done((bf16[256,512]{1,0:T(8,128)(2,1)S(1)}, bf16[256,512]{1,0:T(8,128)(2,1)S(1)}, u32[]{:S(2)}, u32[]{:S(2)}) %collective-permute-start) | collective-permute-done | bytes 262176 | tf_op jit(solution)/shard_map/ppermute | solution.py:16
  13.8 1.1 %fusion.139 = f32[8,128]{1,0:T(8,128)S(1)} fusion(pred[128,640]{1,0:T(8,128)(4,1)S(1)} %fusion.49, bf16[128,8,32]{0,2,1:T(8,128)(2,1)S(1)} %bitcast.186, bf16[640,8,32]{0,2,1:T(8,128)(2,1)S(1)} %bitcast.177), kind=kOutput, calls=%fused_computation.231 | convolution fusion | flops 44565120 | bytes 479232 | tf_op jit(solution)/shard_map/sub | solution.py:131
  15.0 1.4 %fusion.19 = bf16[8,32,128]{2,1,0:T(8,128)(2,1)S(1)} fusion(bf16[640,8,32]{0,2,1:T(8,128)(2,1)S(1)} %bitcast.179, f32[8,128]{1,0:T(8,128)S(1)} %fusion.139, pred[128,640]{1,0:T(8,128)(4,1)S(1)} %fusion.49, bf16[128,8,32]{0,2,1:T(8,128)(2,1)S(1)} %bitcast.187, bf16[640,8,32]{0,2,1:T(8,128)(2,1)S(1)} %bitcast.178), kind=kOutput, calls=%fused_computation.45 | convolution fusion | flops 87197312 | bytes 872448 | tf_op jit(solution)/shard_map/hqk,khd->qhd/dot_general | solution.py:133
  16.3 1.2 %fusion.138 = f32[8,128]{1,0:T(8,128)S(1)} fusion(pred[128,640]{1,0:T(8,128)(4,1)S(1)} %fusion.49, bf16[128,8,32]{0,2,1:T(8,128)(2,1)S(1)} %bitcast.184, bf16[640,8,32]{0,2,1:T(8,128)(2,1)S(1)} %bitcast.174), kind=kOutput, calls=%fused_computation.230 | convolution fusion | flops 44565120 | bytes 479232 | tf_op jit(solution)/shard_map/sub | solution.py:131
  17.5 1.3 %fusion.18 = bf16[8,32,128]{2,1,0:T(8,128)(2,1)S(1)} fusion(bf16[640,8,32]{0,2,1:T(8,128)(2,1)S(1)} %bitcast.176, f32[8,128]{1,0:T(8,128)S(1)} %fusion.138, pred[128,640]{1,0:T(8,128)(4,1)S(1)} %fusion.49, bf16[128,8,32]{0,2,1:T(8,128)(2,1)S(1)} %bitcast.185, bf16[640,8,32]{0,2,1:T(8,128)(2,1)S(1)} %bitcast.175), kind=kOutput, calls=%fused_computation.44 | convolution fusion | flops 87197312 | bytes 872448 | tf_op jit(solution)/shard_map/hqk,khd->qhd/dot_general | solution.py:133
  19.3 0.8 convert_reduce_fusion.3
  20.6 4.3 %all_gather.3 = bf16[512,896]{1,0:T(8,128)(2,1)S(1)} all-gather(bf16[256,896]{1,0:T(8,128)(2,1)S(1)} %fusion.46), channel_id=1, replica_groups=mesh['phi'=8,'query'=2,'event'=2] {'query'}, dimensions={0}, use_global_device_ids=true | all-gather | bytes 1376256 | tf_op jit(solution)/shard_map/all_gather | solution.py:224
  25.7 1.3 %multiply_reduce_fusion = (f32[8,512]{1,0:T(8,128)S(1)}, f32[8,512,512]{1,2,0:T(8,128)S(1)}) fusion(bf16[512,8,32]{0,2,1:T(8,128)(2,1)S(1)} %bitcast.168, bf16[512,8,32]{0,2,1:T(8,128)(2,1)S(1)} %bitcast.170), kind=kOutput, calls=%fused_computation.4 | convolution fusion | flops 138407936 | bytes 8929280 | tf_op jit(solution)/shard_map/qhd,khd->hqk/dot_general | solution.py:237
  27.0 1.4 %convert_reduce_fusion = f32[8,512]{1,0:T(8,128)S(1)} fusion(f32[8,512]{1,0:T(8,128)S(1)} %get-tuple-element.65, f32[8,512,512]{1,2,0:T(8,128)S(1)} %get-tuple-element.66), kind=kLoop, calls=%fused_computation.2 | loop fusion | flops 10481664 | bytes 8421376 | tf_op jit(solution)/shard_map/reduce_sum | solution.py:242
  28.4 2.0 %collective-permute-start.3 = (f32[2,8,512]{2,1,0:T(8,128)S(1)}, f32[2,8,512]{2,1,0:T(8,128)S(1)}, u32[]{:S(2)}, u32[]{:S(2)}) collective-permute-start(f32[2,8,512]{2,1,0:T(8,128)S(1)} %pad_maximum_fusion.1), channel_id=1, source_target_pairs={{0,4},{4,0},{8,12},{12,8},{16,20},{20,16},{24,28},{28,24},{1,5},{5... | collective-permute-start | bytes 98312 | tf_op jit(solution)/shard_map/ppermute | solution.py:33
  30.4 1.5 %convolution_convert_fusion.3 = bf16[8,32,512]{2,1,0:T(8,128)(2,1)S(1)} fusion(bf16[512,8,32]{0,2,1:T(8,128)(2,1)S(1)} %bitcast.169, f32[8,512,512]{1,2,0:T(8,128)S(1)} %get-tuple-element.66, f32[8,512]{1,0:T(8,128)S(1)} %get-tuple-element.65), kind=kOutput, calls=%fused_computation.37 | convolution fusion | flops 140640256 | bytes 8929280 | tf_op jit(solution)/shard_map/hqk,khd->qhd/dot_general | solution.py:243
  32.1 2.8 %collective-permute-done.3 = f32[2,8,512]{2,1,0:T(8,128)S(1)} collective-permute-done((f32[2,8,512]{2,1,0:T(8,128)S(1)}, f32[2,8,512]{2,1,0:T(8,128)S(1)}, u32[]{:S(2)}, u32[]{:S(2)}) %collective-permute-start.3) | collective-permute-done | bytes 32800 | tf_op jit(solution)/shard_map/ppermute | solution.py:33
  35.0 0.8 collective-permute-start.5
  35.8 3.2 %collective-permute-done.5 = f32[2,8,512]{2,1,0:T(8,128)S(1)} collective-permute-done((f32[2,8,512]{2,1,0:T(8,128)S(1)}, f32[2,8,512]{2,1,0:T(8,128)S(1)}, u32[]{:S(2)}, u32[]{:S(2)}) %collective-permute-start.5) | collective-permute-done | bytes 32800 | tf_op jit(solution)/shard_map/ppermute | solution.py:33
  39.0 1.8 %collective-permute-start.7 = (f32[2,8,512]{2,1,0:T(8,128)S(1)}, f32[2,8,512]{2,1,0:T(8,128)S(1)}, u32[]{:S(2)}, u32[]{:S(2)}) collective-permute-start(f32[2,8,512]{2,1,0:T(8,128)S(1)} %pad_maximum_fusion.3), channel_id=1, source_target_pairs={{0,16},{4,20},{8,24},{12,28},{16,0},{20,4},{24,8},{28,12},{1,17},{... | collective-permute-start | bytes 98312 | tf_op jit(solution)/shard_map/ppermute | solution.py:33
  40.8 3.4 %collective-permute-done.7 = f32[2,8,512]{2,1,0:T(8,128)S(1)} collective-permute-done((f32[2,8,512]{2,1,0:T(8,128)S(1)}, f32[2,8,512]{2,1,0:T(8,128)S(1)}, u32[]{:S(2)}, u32[]{:S(2)}) %collective-permute-start.7) | collective-permute-done | bytes 32800 | tf_op jit(solution)/shard_map/ppermute | solution.py:33
  45.3 5.7 %collective-permute-done.4 = bf16[512,256]{0,1:T(8,128)(2,1)S(1)} collective-permute-done((bf16[512,256]{0,1:T(8,128)(2,1)S(1)}, bf16[512,256]{0,1:T(8,128)(2,1)S(1)}, u32[]{:S(2)}, u32[]{:S(2)}) %collective-permute-start.4) | collective-permute-done | bytes 262176 | tf_op jit(solution)/shard_map/ppermute | solution.py:33
  51.2 2.2 %collective-permute-start.6 = (bf16[512,256]{0,1:T(8,128)(2,1)S(1)}, bf16[512,256]{0,1:T(8,128)(2,1)S(1)}, u32[]{:S(2)}, u32[]{:S(2)}) collective-permute-start(bf16[512,256]{0,1:T(8,128)(2,1)S(1)} %fusion.37), channel_id=1, source_target_pairs={{0,16},{4,20},{8,24},{12,28},{16,0},{20,4},{24,8},{28,12},{1,17},{... | collective-permute-start | bytes 786440 | tf_op jit(solution)/shard_map/ppermute | solution.py:33
  53.4 1.8 %collective-permute-start.9 = (bf16[1040,256]{1,0:T(8,128)(2,1)S(1)}, bf16[1040,256]{1,0:T(8,128)(2,1)S(1)}, u32[]{:S(2)}, u32[]{:S(2)}) collective-permute-start(bf16[1040,256]{1,0:T(8,128)(2,1)S(1)} %fusion.31), channel_id=1, source_target_pairs={{0,8},{4,12},{8,0},{12,4},{16,24},{20,28},{24,16},{28,20},{1,9},{5... | collective-permute-start | bytes 1597448 | tf_op jit(solution)/shard_map/ppermute | solution.py:95
  55.3 6.8 %collective-permute-done.6 = bf16[512,256]{0,1:T(8,128)(2,1)S(1)} collective-permute-done((bf16[512,256]{0,1:T(8,128)(2,1)S(1)}, bf16[512,256]{0,1:T(8,128)(2,1)S(1)}, u32[]{:S(2)}, u32[]{:S(2)}) %collective-permute-start.6) | collective-permute-done | bytes 262176 | tf_op jit(solution)/shard_map/ppermute | solution.py:33
  63.1 4.9 %collective-permute-done.9 = bf16[1040,256]{1,0:T(8,128)(2,1)S(1)} collective-permute-done((bf16[1040,256]{1,0:T(8,128)(2,1)S(1)}, bf16[1040,256]{1,0:T(8,128)(2,1)S(1)}, u32[]{:S(2)}, u32[]{:S(2)}) %collective-permute-start.9) | collective-permute-done | bytes 532512 | tf_op jit(solution)/shard_map/ppermute | solution.py:95
  68.1 4.2 %select_reduce_fusion = (f32[512]{0:T(512)S(1)}, f32[512]{0:T(512)S(1)}, f32[512]{0:T(512)S(1)}, f32[512,2048]{1,0:T(8,128)}) fusion(s32[2048]{0:T(1024)S(1)} %bitcast.189, s32[512]{0:T(512)S(1)} %copy-done.8, pred[512]{0:T(512)(128)(4,1)S(1)} %get-tuple-element.24, bf16[512,256]{1,0:T(8,128)(2,1)S(1)} %convolution_convert_fusion.2, ...), kind=kOutput, calls=%fused_computation.12 | convolution fusion | flops 553122304 | bytes 5521921 | tf_op jit(solution)/shard_map/dot_general | solution.py:273
  72.3 1.4 %collective-permute-start.10 = (f32[3,512]{1,0:T(4,128)S(1)}, f32[3,512]{1,0:T(4,128)S(1)}, u32[]{:S(2)}, u32[]{:S(2)}) collective-permute-start(f32[3,512]{1,0:T(4,128)S(1)} %pad_maximum_fusion.4), channel_id=1, source_target_pairs={{0,16},{4,20},{8,24},{12,28},{16,0},{20,4},{24,8},{28,12},{1,17},{... | collective-permute-start | bytes 18440 | tf_op jit(solution)/shard_map/ppermute | solution.py:33
  73.8 3.2 %collective-permute-done.10 = f32[3,512]{1,0:T(4,128)S(1)} collective-permute-done((f32[3,512]{1,0:T(4,128)S(1)}, f32[3,512]{1,0:T(4,128)S(1)}, u32[]{:S(2)}, u32[]{:S(2)}) %collective-permute-start.10) | collective-permute-done | bytes 6176 | tf_op jit(solution)/shard_map/ppermute | solution.py:33
  77.6 3.9 %fusion.4 = bf16[512,2048]{1,0:T(8,128)(2,1)S(1)} fusion(f32[512,2048]{1,0:T(8,128)} %get-tuple-element.69, f32[512]{0:T(512)S(1)} %get-tuple-element.60, f32[512]{0:T(512)S(1)} %get-tuple-element.59, s32[2048]{0:T(1024)S(1)} %bitcast.190, f32[512]{0:T(512)S(1)} %get-tuple-element.23, s32[512]{0:T(512)S(1)} %copy-done.8, pred[512]{0:T(512)(128)(4,1)S(1)} %get-tuple-element.24), kind=kLoop, calls=%fused_computation.10 | loop fusion | flops 12582912 | bytes 6308352 | tf_op jit(solution)/shard_map/convert_element_type | solution.py:169
  82.2 1.4 %collective-permute-start.12 = (bf16[512,256]{1,0:T(8,128)(2,1)S(1)}, bf16[512,256]{1,0:T(8,128)(2,1)S(1)}, u32[]{:S(2)}, u32[]{:S(2)}) collective-permute-start(bf16[512,256]{1,0:T(8,128)(2,1)S(1)} %convolution_convert_fusion.1), channel_id=1, source_target_pairs={{0,16},{4,20},{8,24},{12,28},{16,0},{20,4},{24,8},{28,12},{1,17},{... | collective-permute-start | bytes 786440 | tf_op jit(solution)/shard_map/ppermute | solution.py:53
  84.1 8.7 %collective-permute-done.12 = bf16[512,256]{1,0:T(8,128)(2,1)S(1)} collective-permute-done((bf16[512,256]{1,0:T(8,128)(2,1)S(1)}, bf16[512,256]{1,0:T(8,128)(2,1)S(1)}, u32[]{:S(2)}, u32[]{:S(2)}) %collective-permute-start.12) | collective-permute-done | bytes 262176 | tf_op jit(solution)/shard_map/ppermute | solution.py:53
  92.8 0.9 convert_add_fusion
  93.7 0.8 select_add_fusion
  (113 shorter events, 9.8 us)
Async XLA Ops:
  0.6 18.6 %copy-start = (bf16[1024,256]{1,0:T(8,128)(2,1)S(1)}, bf16[1024,256]{1,0:T(8,128)(2,1)}, u32[]{:S(2)}) copy-start(bf16[1024,256]{1,0:T(8,128)(2,1)} %param.17) | copy-start | bytes 1572868
  0.6 10.1 %copy-start.1 = (bf16[512,256]{1,0:T(8,128)(2,1)S(1)}, bf16[512,256]{1,0:T(8,128)(2,1)}, u32[]{:S(2)}) copy-start(bf16[512,256]{1,0:T(8,128)(2,1)} %param.18) | copy-start | bytes 786436
  0.7 10.2 %copy-start.5 = (bf16[256,256]{1,0:T(8,128)(2,1)S(1)}, bf16[256,256]{1,0:T(8,128)(2,1)}, u32[]{:S(2)}) copy-start(bf16[256,256]{1,0:T(8,128)(2,1)} %param.19) | copy-start | bytes 393220
  3.2 9.6 %collective-permute-start = (bf16[256,512]{1,0:T(8,128)(2,1)S(1)}, bf16[256,512]{1,0:T(8,128)(2,1)S(1)}, u32[]{:S(2)}, u32[]{:S(2)}) collective-permute-start(bf16[256,512]{1,0:T(8,128)(2,1)S(1)} %slice.85), channel_id=1, source_target_pairs={{0,2},{2,4},{4,6},{6,8},{8,10},{10,12},{12,14},{14,16},{16,18},{18... | collective-permute-start | bytes 786440 | tf_op jit(solution)/shard_map/ppermute | solution.py:16
  3.7 9.1 %collective-permute-start.1 = (bf16[256,512]{1,0:T(8,128)(2,1)S(1)}, bf16[256,512]{1,0:T(8,128)(2,1)S(1)}, u32[]{:S(2)}, u32[]{:S(2)}) collective-permute-start(bf16[256,512]{1,0:T(8,128)(2,1)S(1)} %slice.85), channel_id=1, source_target_pairs={{2,0},{4,2},{6,4},{8,6},{10,8},{12,10},{14,12},{16,14},{18,16},{20... | collective-permute-start | bytes 786440 | tf_op jit(solution)/shard_map/ppermute | solution.py:19
  17.5 1.4 %copy-start.6 = (bf16[256,256]{1,0:T(8,128)(2,1)S(1)}, bf16[256,256]{1,0:T(8,128)(2,1)}, u32[]{:S(2)}) copy-start(bf16[256,256]{1,0:T(8,128)(2,1)} %param.15) | copy-start | bytes 393220
  17.5 1.8 %copy-start.9 = (bf16[256,1024]{1,0:T(8,128)(2,1)S(1)}, bf16[256,1024]{1,0:T(8,128)(2,1)}, u32[]{:S(2)}) copy-start(bf16[256,1024]{1,0:T(8,128)(2,1)} %param.16) | copy-start | bytes 1572868
  18.9 1.4 %copy-start.4 = (bf16[256,512]{1,0:T(8,128)(2,1)S(1)}, bf16[256,512]{1,0:T(8,128)(2,1)}, u32[]{:S(2)}) copy-start(bf16[256,512]{1,0:T(8,128)(2,1)} %param.20) | copy-start | bytes 786436
  20.2 5.0 %copy-start.2 = (bf16[256,256]{1,0:T(8,128)(2,1)}, bf16[256,256]{1,0:T(8,128)(2,1)S(1)}, u32[]{:S(2)}) copy-start(bf16[256,256]{1,0:T(8,128)(2,1)S(1)} %copy.66) | copy-start | bytes 393220
  25.2 19.8 %collective-permute-start.8 = (bf16[528,256]{1,0:T(8,128)(2,1)S(1)}, bf16[528,256]{1,0:T(8,128)(2,1)S(1)}, u32[]{:S(2)}, u32[]{:S(2)}) collective-permute-start(bf16[528,256]{1,0:T(8,128)(2,1)S(1)} %fusion.58), channel_id=1, source_target_pairs={{0,4},{4,0},{8,12},{12,8},{16,20},{20,16},{24,28},{28,24},{1,5},{5... | collective-permute-start | bytes 811016 | tf_op jit(solution)/shard_map/ppermute | solution.py:95
  28.4 6.6 %collective-permute-start.3 = (f32[2,8,512]{2,1,0:T(8,128)S(1)}, f32[2,8,512]{2,1,0:T(8,128)S(1)}, u32[]{:S(2)}, u32[]{:S(2)}) collective-permute-start(f32[2,8,512]{2,1,0:T(8,128)S(1)} %pad_maximum_fusion.1), channel_id=1, source_target_pairs={{0,4},{4,0},{8,12},{12,8},{16,20},{20,16},{24,28},{28,24},{1,5},{5... | collective-permute-start | bytes 98312 | tf_op jit(solution)/shard_map/ppermute | solution.py:33
  32.0 12.3 %collective-permute-start.2 = (bf16[512,256]{0,1:T(8,128)(2,1)S(1)}, bf16[512,256]{0,1:T(8,128)(2,1)S(1)}, u32[]{:S(2)}, u32[]{:S(2)}) collective-permute-start(bf16[512,256]{0,1:T(8,128)(2,1)S(1)} %bitcast.171), channel_id=1, source_target_pairs={{0,4},{4,0},{8,12},{12,8},{16,20},{20,16},{24,28},{28,24},{1,5},{5... | collective-permute-start | bytes 786440 | tf_op jit(solution)/shard_map/ppermute | solution.py:33
  35.0 4.0 %collective-permute-start.5 = (f32[2,8,512]{2,1,0:T(8,128)S(1)}, f32[2,8,512]{2,1,0:T(8,128)S(1)}, u32[]{:S(2)}, u32[]{:S(2)}) collective-permute-start(f32[2,8,512]{2,1,0:T(8,128)S(1)} %pad_maximum_fusion.2), channel_id=1, source_target_pairs={{0,8},{4,12},{8,0},{12,4},{16,24},{20,28},{24,16},{28,20},{1,9},{5... | collective-permute-start | bytes 98312 | tf_op jit(solution)/shard_map/ppermute | solution.py:33
  39.0 5.2 %collective-permute-start.7 = (f32[2,8,512]{2,1,0:T(8,128)S(1)}, f32[2,8,512]{2,1,0:T(8,128)S(1)}, u32[]{:S(2)}, u32[]{:S(2)}) collective-permute-start(f32[2,8,512]{2,1,0:T(8,128)S(1)} %pad_maximum_fusion.3), channel_id=1, source_target_pairs={{0,16},{4,20},{8,24},{12,28},{16,0},{20,4},{24,8},{28,12},{1,17},{... | collective-permute-start | bytes 98312 | tf_op jit(solution)/shard_map/ppermute | solution.py:33
  44.3 18.0 %copy-start.7 = (bf16[256,256]{1,0:T(8,128)(2,1)S(1)}, bf16[256,256]{1,0:T(8,128)(2,1)}, u32[]{:S(2)}) copy-start(bf16[256,256]{1,0:T(8,128)(2,1)} %param.21) | copy-start | bytes 393220
  44.4 6.6 %collective-permute-start.4 = (bf16[512,256]{0,1:T(8,128)(2,1)S(1)}, bf16[512,256]{0,1:T(8,128)(2,1)S(1)}, u32[]{:S(2)}, u32[]{:S(2)}) collective-permute-start(bf16[512,256]{0,1:T(8,128)(2,1)S(1)} %fusion.39), channel_id=1, source_target_pairs={{0,8},{4,12},{8,0},{12,4},{16,24},{20,28},{24,16},{28,20},{1,9},{5... | collective-permute-start | bytes 786440 | tf_op jit(solution)/shard_map/ppermute | solution.py:33
  45.0 17.6 %copy-start.10 = (bf16[256,256]{1,0:T(8,128)(2,1)S(1)}, bf16[256,256]{1,0:T(8,128)(2,1)}, u32[]{:S(2)}) copy-start(bf16[256,256]{1,0:T(8,128)(2,1)} %param.23) | copy-start | bytes 393220
  45.1 17.6 %copy-start.11 = (bf16[256,256]{1,0:T(8,128)(2,1)S(1)}, bf16[256,256]{1,0:T(8,128)(2,1)}, u32[]{:S(2)}) copy-start(bf16[256,256]{1,0:T(8,128)(2,1)} %param.22) | copy-start | bytes 393220
  51.2 10.9 %collective-permute-start.6 = (bf16[512,256]{0,1:T(8,128)(2,1)S(1)}, bf16[512,256]{0,1:T(8,128)(2,1)S(1)}, u32[]{:S(2)}, u32[]{:S(2)}) collective-permute-start(bf16[512,256]{0,1:T(8,128)(2,1)S(1)} %fusion.37), channel_id=1, source_target_pairs={{0,16},{4,20},{8,24},{12,28},{16,0},{20,4},{24,8},{28,12},{1,17},{... | collective-permute-start | bytes 786440 | tf_op jit(solution)/shard_map/ppermute | solution.py:33
  53.4 14.7 %copy-start.8 = (s32[512]{0:T(512)S(1)}, s32[512]{0:T(512)}, u32[]{:S(2)}) copy-start(s32[512]{0:T(512)} %param.25) | copy-start | bytes 6148
  53.4 14.5 %collective-permute-start.9 = (bf16[1040,256]{1,0:T(8,128)(2,1)S(1)}, bf16[1040,256]{1,0:T(8,128)(2,1)S(1)}, u32[]{:S(2)}, u32[]{:S(2)}) collective-permute-start(bf16[1040,256]{1,0:T(8,128)(2,1)S(1)} %fusion.31), channel_id=1, source_target_pairs={{0,8},{4,12},{8,0},{12,4},{16,24},{20,28},{24,16},{28,20},{1,9},{5... | collective-permute-start | bytes 1597448 | tf_op jit(solution)/shard_map/ppermute | solution.py:95
  63.1 20.6 %copy-start.3 = (bf16[512,256]{1,0:T(8,128)(2,1)}, bf16[512,256]{1,0:T(8,128)(2,1)S(1)}, u32[]{:S(2)}) copy-start(bf16[512,256]{1,0:T(8,128)(2,1)S(1)} %convolution_convert_fusion.2) | copy-start | bytes 786436
  72.3 4.6 %collective-permute-start.10 = (f32[3,512]{1,0:T(4,128)S(1)}, f32[3,512]{1,0:T(4,128)S(1)}, u32[]{:S(2)}, u32[]{:S(2)}) collective-permute-start(f32[3,512]{1,0:T(4,128)S(1)} %pad_maximum_fusion.4), channel_id=1, source_target_pairs={{0,16},{4,20},{8,24},{12,28},{16,0},{20,4},{24,8},{28,12},{1,17},{... | collective-permute-start | bytes 18440 | tf_op jit(solution)/shard_map/ppermute | solution.py:33
  82.2 10.6 %collective-permute-start.12 = (bf16[512,256]{1,0:T(8,128)(2,1)S(1)}, bf16[512,256]{1,0:T(8,128)(2,1)S(1)}, u32[]{:S(2)}, u32[]{:S(2)}) collective-permute-start(bf16[512,256]{1,0:T(8,128)(2,1)S(1)} %convolution_convert_fusion.1), channel_id=1, source_target_pairs={{0,16},{4,20},{8,24},{12,28},{16,0},{20,4},{24,8},{28,12},{1,17},{... | collective-permute-start | bytes 786440 | tf_op jit(solution)/shard_map/ppermute | solution.py:53
  84.1 9.6 %collective-permute-start.11 = (f32[256,256]{1,0:T(8,128)S(1)}, f32[256,256]{1,0:T(8,128)S(1)}, u32[]{:S(2)}, u32[]{:S(2)}) collective-permute-start(f32[256,256]{1,0:T(8,128)S(1)} %slice_select_fusion), channel_id=1, source_target_pairs={{0,2},{2,0},{1,3},{3,1},{4,6},{6,4},{5,7},{7,5},{8,10},{10,8},{9,1... | collective-permute-start | bytes 786440 | tf_op jit(solution)/shard_map/ppermute | solution.py:84

commit v18 on v15

--- a/solution.py
+++ b/solution.py
@@ -25,11 +25,17 @@
     return [(i, i ^ distance) for i in range(count)]
 
 
-def butterfly(tree, axis, combine, ordered=False, distance=1):
+def butterfly(tree, axis, combine, ordered=False, distance=1, order=None):
     count = lax.axis_size(axis)
     assert count & (count - 1) == 0
     index = lax.axis_index(axis)
+    distances = []
     while distance < count:
+        distances.append(distance)
+        distance *= 2
+    if order is not None and len(distances) >= 2:
+        distances[0], distances[1] = distances[1], distances[0]
+    for distance in distances:
         other = lax.ppermute(tree, axis, partner_pairs(count, distance))
         if ordered:
             upper = (index // distance) % 2 == 1
@@ -38,7 +44,6 @@
             tree = combine(first, second)
         else:
             tree = combine(tree, other)
-        distance *= 2
     return tree
 
 
@@ -249,6 +254,7 @@
         "phi",
         softmax_combine,
         ordered=True,
+        order="near_first",
     )
     mixed = mixed.astype(jnp.float32)
     context = scale_heads(mixed, 1.0 / total).astype(jnp.bfloat16)

time: 94.9 us -> 93.2 us (0.982)
  waiting for transfers between devices: 40.5 us -> 32.1 us
  starting transfers between devices: 17.8 us -> 24.5 us
    ppermute x7, waiting for transfers between devices: 25.2 us -> 17.3 us  [butterfly(): other = lax.ppermute(tree, axis, partner_pairs(count, distance))]
    ppermute x7, starting transfers between devices: 8.76 us -> 13.9 us  [butterfly(): other = lax.ppermute(tree, axis, partner_pairs(count, distance))]
    ppermute x1, starting transfers between devices: 1.42 us -> 2.98 us  [narrow_butterfly(): other = lax.ppermute(sent, axis, partner_pairs(count, distance))]
where the time goes in v18:
time: 93.2 us; the launch traced here: 93 us
  waiting for transfers between devices  32.1 us (34%)
  starting transfers between devices  24.5 us (26%)
  matrix products  16.8 us (18%)
  other arithmetic  10.6 us (11%)
  blocking collectives  4.35 us (5%)
  local copies, waits for them, and re-layouts  3.42 us (4%)
  between operations  1.31 us (1%)
    ppermute x7, waiting for transfers between devices, butterfly(): other = lax.ppermute(tree, axis, partner_pairs(count, distance))  17.3 us
    ppermute x7, starting transfers between devices, butterfly(): other = lax.ppermute(tree, axis, partner_pairs(count, distance))  13.9 us
    ppermute x1, waiting for transfers between devices, narrow_butterfly(): other = lax.ppermute(sent, axis, partner_pairs(count, distance))  8.16 us
    ppermute x1, starting transfers between devices, extended_2(): lax.ppermute(lax.slice_in_dim(block, 0, width, axis=dim), axis, backward)  5.03 us
    ppermute x2, waiting for transfers between devices, partner_rows(): lax.ppermute(payload, 'phi', partner_pairs(lax.axis_size('phi'), distance))  4.91 us
    all_gather x1, blocking collectives, body(): lax.all_gather(jnp.concatenate([local_kv, encoded, digits], axis=1), 'que...  4.35 us
    dot_general x1, matrix products, body(): lax.dot_general(mask_embed, pair_hits, (((1,), (1,)), ((), ())), preferre...  4.24 us
    convert_element_type x1, other arithmetic, loss_coefficients(): (matched[:, None] * (sigma - target + dice_part) * model_width ** (-0.5))...  4.16 us
  transfers between devices with their start and end apart: 13, of which 9 were waited for; matrix products, arithmetic and copies ran while one was open for 10% of the time, Pallas kernels for 0%

profile of v18, /device:TPU:0, one launch (start us, length us, event | category | flops | bytes accessed | tf_op | source)
XLA Modules:
  0.0 93.0 jit_solution(18098288704197503214)
XLA Ops:
  0.7 1.1 %copy.50 = bf16[256,256]{0,1:T(8,128)(2,1)S(1)} copy(bf16[256,256]{1,0:T(8,128)(2,1)} %param.13) | data formatting | bytes 262144 | tf_op args[0]
  1.9 1.3 %convolution_convert_fusion = bf16[256,768]{1,0:T(8,128)(2,1)S(1)} fusion(bf16[256,768]{1,0:T(8,128)(2,1)} %param.14, bf16[256,256]{0,1:T(8,128)(2,1)S(1)} %copy.50, f32[256]{0:T(256)S(1)} %add_rsqrt_fusion.3, f32[256]{0:T(256)S(1)} %broadcast_multiply_fusion.3), kind=kOutput, calls=%fused_computation.31 | convolution fusion | flops 101122048 | bytes 919552 | tf_op jit(solution)/shard_map/dot_general | solution.py:199
  3.7 5.0 %collective-permute-start.1 = (bf16[256,512]{1,0:T(8,128)(2,1)S(1)}, bf16[256,512]{1,0:T(8,128)(2,1)S(1)}, u32[]{:S(2)}, u32[]{:S(2)}) collective-permute-start(bf16[256,512]{1,0:T(8,128)(2,1)S(1)} %slice.85), channel_id=1, source_target_pairs={{2,0},{4,2},{6,4},{8,6},{10,8},{12,10},{14,12},{16,14},{18,16},{20... | collective-permute-start | bytes 786440 | tf_op jit(solution)/shard_map/ppermute | solution.py:19
  11.2 1.7 %collective-permute-done = bf16[256,512]{1,0:T(8,128)(2,1)S(1)} collective-permute-done((bf16[256,512]{1,0:T(8,128)(2,1)S(1)}, bf16[256,512]{1,0:T(8,128)(2,1)S(1)}, u32[]{:S(2)}, u32[]{:S(2)}) %collective-permute-start) | collective-permute-done | bytes 262176 | tf_op jit(solution)/shard_map/ppermute | solution.py:16
  13.8 1.1 %fusion.140 = f32[8,128]{1,0:T(8,128)S(1)} fusion(pred[128,640]{1,0:T(8,128)(4,1)S(1)} %fusion.49, bf16[128,8,32]{0,2,1:T(8,128)(2,1)S(1)} %bitcast.186, bf16[640,8,32]{0,2,1:T(8,128)(2,1)S(1)} %bitcast.177), kind=kOutput, calls=%fused_computation.228 | convolution fusion | flops 44565120 | bytes 479232 | tf_op jit(solution)/shard_map/sub | solution.py:136
  15.0 1.4 %fusion.19 = bf16[8,32,128]{2,1,0:T(8,128)(2,1)S(1)} fusion(bf16[640,8,32]{0,2,1:T(8,128)(2,1)S(1)} %bitcast.179, f32[8,128]{1,0:T(8,128)S(1)} %fusion.140, pred[128,640]{1,0:T(8,128)(4,1)S(1)} %fusion.49, bf16[128,8,32]{0,2,1:T(8,128)(2,1)S(1)} %bitcast.187, bf16[640,8,32]{0,2,1:T(8,128)(2,1)S(1)} %bitcast.178), kind=kOutput, calls=%fused_computation.44 | convolution fusion | flops 87197312 | bytes 872448 | tf_op jit(solution)/shard_map/hqk,khd->qhd/dot_general | solution.py:138
  16.3 1.2 %fusion.139 = f32[8,128]{1,0:T(8,128)S(1)} fusion(pred[128,640]{1,0:T(8,128)(4,1)S(1)} %fusion.49, bf16[128,8,32]{0,2,1:T(8,128)(2,1)S(1)} %bitcast.184, bf16[640,8,32]{0,2,1:T(8,128)(2,1)S(1)} %bitcast.174), kind=kOutput, calls=%fused_computation.227 | convolution fusion | flops 44565120 | bytes 479232 | tf_op jit(solution)/shard_map/sub | solution.py:136
  17.5 1.3 %fusion.18 = bf16[8,32,128]{2,1,0:T(8,128)(2,1)S(1)} fusion(bf16[640,8,32]{0,2,1:T(8,128)(2,1)S(1)} %bitcast.176, f32[8,128]{1,0:T(8,128)S(1)} %fusion.139, pred[128,640]{1,0:T(8,128)(4,1)S(1)} %fusion.49, bf16[128,8,32]{0,2,1:T(8,128)(2,1)S(1)} %bitcast.185, bf16[640,8,32]{0,2,1:T(8,128)(2,1)S(1)} %bitcast.175), kind=kOutput, calls=%fused_computation.43 | convolution fusion | flops 87197312 | bytes 872448 | tf_op jit(solution)/shard_map/hqk,khd->qhd/dot_general | solution.py:138
  19.3 0.8 convert_reduce_fusion.3
  20.6 4.3 %all_gather.3 = bf16[512,896]{1,0:T(8,128)(2,1)S(1)} all-gather(bf16[256,896]{1,0:T(8,128)(2,1)S(1)} %fusion.46), channel_id=1, replica_groups=mesh['phi'=8,'query'=2,'event'=2] {'query'}, dimensions={0}, use_global_device_ids=true | all-gather | bytes 1376256 | tf_op jit(solution)/shard_map/all_gather | solution.py:230
  25.7 1.3 %multiply_reduce_fusion = (f32[8,512]{1,0:T(8,128)S(1)}, f32[8,512,512]{1,2,0:T(8,128)S(1)}) fusion(bf16[512,8,32]{0,2,1:T(8,128)(2,1)S(1)} %bitcast.168, bf16[512,8,32]{0,2,1:T(8,128)(2,1)S(1)} %bitcast.170), kind=kOutput, calls=%fused_computation.4 | convolution fusion | flops 138407936 | bytes 8929280 | tf_op jit(solution)/shard_map/qhd,khd->hqk/dot_general | solution.py:243
  27.0 1.4 %convert_reduce_fusion = f32[8,512]{1,0:T(8,128)S(1)} fusion(f32[8,512]{1,0:T(8,128)S(1)} %get-tuple-element.63, f32[8,512,512]{1,2,0:T(8,128)S(1)} %get-tuple-element.64), kind=kLoop, calls=%fused_computation.2 | loop fusion | flops 10481664 | bytes 8421376 | tf_op jit(solution)/shard_map/reduce_sum | solution.py:248
  28.4 1.3 %collective-permute-start.3 = (f32[2,8,512]{2,1,0:T(8,128)S(1)}, f32[2,8,512]{2,1,0:T(8,128)S(1)}, u32[]{:S(2)}, u32[]{:S(2)}) collective-permute-start(f32[2,8,512]{2,1,0:T(8,128)S(1)} %pad_maximum_fusion.1), channel_id=1, source_target_pairs={{0,8},{4,12},{8,0},{12,4},{16,24},{20,28},{24,16},{28,20},{1,9},{5... | collective-permute-start | bytes 98312 | tf_op jit(solution)/shard_map/ppermute | solution.py:39
  29.6 1.5 %convolution_convert_fusion.3 = bf16[8,32,512]{2,1,0:T(8,128)(2,1)S(1)} fusion(bf16[512,8,32]{0,2,1:T(8,128)(2,1)S(1)} %bitcast.169, f32[8,512,512]{1,2,0:T(8,128)S(1)} %get-tuple-element.64, f32[8,512]{1,0:T(8,128)S(1)} %get-tuple-element.63), kind=kOutput, calls=%fused_computation.36 | convolution fusion | flops 140640256 | bytes 8929280 | tf_op jit(solution)/shard_map/hqk,khd->qhd/dot_general | solution.py:249
  31.3 0.9 collective-permute-start.2
  32.4 2.0 %collective-permute-start.5 = (f32[2,8,512]{2,1,0:T(8,128)S(1)}, f32[2,8,512]{2,1,0:T(8,128)S(1)}, u32[]{:S(2)}, u32[]{:S(2)}) collective-permute-start(f32[2,8,512]{2,1,0:T(8,128)S(1)} %pad_maximum_fusion.2), channel_id=1, source_target_pairs={{0,4},{4,0},{8,12},{12,8},{16,20},{20,16},{24,28},{28,24},{1,5},{5... | collective-permute-start | bytes 98312 | tf_op jit(solution)/shard_map/ppermute | solution.py:39
  34.4 2.0 %collective-permute-done.5 = f32[2,8,512]{2,1,0:T(8,128)S(1)} collective-permute-done((f32[2,8,512]{2,1,0:T(8,128)S(1)}, f32[2,8,512]{2,1,0:T(8,128)S(1)}, u32[]{:S(2)}, u32[]{:S(2)}) %collective-permute-start.5) | collective-permute-done | bytes 32800 | tf_op jit(solution)/shard_map/ppermute | solution.py:39
  36.4 2.3 %collective-permute-start.7 = (f32[2,8,512]{2,1,0:T(8,128)S(1)}, f32[2,8,512]{2,1,0:T(8,128)S(1)}, u32[]{:S(2)}, u32[]{:S(2)}) collective-permute-start(f32[2,8,512]{2,1,0:T(8,128)S(1)} %pad_maximum_fusion.3), channel_id=1, source_target_pairs={{0,16},{4,20},{8,24},{12,28},{16,0},{20,4},{24,8},{28,12},{1,17},{... | collective-permute-start | bytes 98312 | tf_op jit(solution)/shard_map/ppermute | solution.py:39
  38.7 2.6 %collective-permute-done.7 = f32[2,8,512]{2,1,0:T(8,128)S(1)} collective-permute-done((f32[2,8,512]{2,1,0:T(8,128)S(1)}, f32[2,8,512]{2,1,0:T(8,128)S(1)}, u32[]{:S(2)}, u32[]{:S(2)}) %collective-permute-start.7) | collective-permute-done | bytes 32800 | tf_op jit(solution)/shard_map/ppermute | solution.py:39
  41.5 2.4 %collective-permute-start.4 = (bf16[512,256]{0,1:T(8,128)(2,1)S(1)}, bf16[512,256]{0,1:T(8,128)(2,1)S(1)}, u32[]{:S(2)}, u32[]{:S(2)}) collective-permute-start(bf16[512,256]{0,1:T(8,128)(2,1)S(1)} %fusion.39), channel_id=1, source_target_pairs={{0,4},{4,0},{8,12},{12,8},{16,20},{20,16},{24,28},{28,24},{1,5},{5... | collective-permute-start | bytes 786440 | tf_op jit(solution)/shard_map/ppermute | solution.py:39
  44.2 4.0 %collective-permute-done.4 = bf16[512,256]{0,1:T(8,128)(2,1)S(1)} collective-permute-done((bf16[512,256]{0,1:T(8,128)(2,1)S(1)}, bf16[512,256]{0,1:T(8,128)(2,1)S(1)}, u32[]{:S(2)}, u32[]{:S(2)}) %collective-permute-start.4) | collective-permute-done | bytes 262176 | tf_op jit(solution)/shard_map/ppermute | solution.py:39
  48.3 2.0 %collective-permute-start.6 = (bf16[512,256]{0,1:T(8,128)(2,1)S(1)}, bf16[512,256]{0,1:T(8,128)(2,1)S(1)}, u32[]{:S(2)}, u32[]{:S(2)}) collective-permute-start(bf16[512,256]{0,1:T(8,128)(2,1)S(1)} %fusion.37), channel_id=1, source_target_pairs={{0,16},{4,20},{8,24},{12,28},{16,0},{20,4},{24,8},{28,12},{1,17},{... | collective-permute-start | bytes 786440 | tf_op jit(solution)/shard_map/ppermute | solution.py:39
  50.5 1.9 %collective-permute-start.9 = (bf16[1040,256]{1,0:T(8,128)(2,1)S(1)}, bf16[1040,256]{1,0:T(8,128)(2,1)S(1)}, u32[]{:S(2)}, u32[]{:S(2)}) collective-permute-start(bf16[1040,256]{1,0:T(8,128)(2,1)S(1)} %fusion.31), channel_id=1, source_target_pairs={{0,8},{4,12},{8,0},{12,4},{16,24},{20,28},{24,16},{28,20},{1,9},{5... | collective-permute-start | bytes 1597448 | tf_op jit(solution)/shard_map/ppermute | solution.py:100
  52.3 6.9 %collective-permute-done.6 = bf16[512,256]{0,1:T(8,128)(2,1)S(1)} collective-permute-done((bf16[512,256]{0,1:T(8,128)(2,1)S(1)}, bf16[512,256]{0,1:T(8,128)(2,1)S(1)}, u32[]{:S(2)}, u32[]{:S(2)}) %collective-permute-start.6) | collective-permute-done | bytes 262176 | tf_op jit(solution)/shard_map/ppermute | solution.py:39
  60.2 4.9 %collective-permute-done.9 = bf16[1040,256]{1,0:T(8,128)(2,1)S(1)} collective-permute-done((bf16[1040,256]{1,0:T(8,128)(2,1)S(1)}, bf16[1040,256]{1,0:T(8,128)(2,1)S(1)}, u32[]{:S(2)}, u32[]{:S(2)}) %collective-permute-start.9) | collective-permute-done | bytes 532512 | tf_op jit(solution)/shard_map/ppermute | solution.py:100
  65.3 4.2 %select_reduce_fusion = (f32[512]{0:T(512)S(1)}, f32[512]{0:T(512)S(1)}, f32[512]{0:T(512)S(1)}, f32[512,2048]{1,0:T(8,128)}) fusion(s32[2048]{0:T(1024)S(1)} %bitcast.189, s32[512]{0:T(512)S(1)} %copy-done.8, pred[512]{0:T(512)(128)(4,1)S(1)} %get-tuple-element.24, bf16[512,256]{1,0:T(8,128)(2,1)S(1)} %convolution_convert_fusion.2, ...), kind=kOutput, calls=%fused_computation.11 | convolution fusion | flops 553122304 | bytes 5521921 | tf_op jit(solution)/shard_map/dot_general | solution.py:280
  69.5 3.1 %collective-permute-start.10 = (f32[3,512]{1,0:T(4,128)S(1)}, f32[3,512]{1,0:T(4,128)S(1)}, u32[]{:S(2)}, u32[]{:S(2)}) collective-permute-start(f32[3,512]{1,0:T(4,128)S(1)} %pad_maximum_fusion.4), channel_id=1, source_target_pairs={{0,16},{4,20},{8,24},{12,28},{16,0},{20,4},{24,8},{28,12},{1,17},{... | collective-permute-start | bytes 18440 | tf_op jit(solution)/shard_map/ppermute | solution.py:39
  72.6 1.6 %collective-permute-done.10 = f32[3,512]{1,0:T(4,128)S(1)} collective-permute-done((f32[3,512]{1,0:T(4,128)S(1)}, f32[3,512]{1,0:T(4,128)S(1)}, u32[]{:S(2)}, u32[]{:S(2)}) %collective-permute-start.10) | collective-permute-done | bytes 6176 | tf_op jit(solution)/shard_map/ppermute | solution.py:39
  74.9 4.2 %fusion.5 = bf16[512,2048]{1,0:T(8,128)(2,1)S(1)} fusion(f32[512,2048]{1,0:T(8,128)} %get-tuple-element.67, f32[512]{0:T(512)S(1)} %bitcast.192, f32[512]{0:T(512)S(1)} %bitcast.193, s32[2048]{0:T(1024)S(1)} %bitcast.190, f32[512]{0:T(512)S(1)} %get-tuple-element.23, s32[512]{0:T(512)S(1)} %copy-done.8, pred[512]{0:T(512)(128)(4,1)S(1)} %get-tuple-element.24), kind=kLoop, calls=%fused_computation.10 | loop fusion | flops 14680064 | bytes 6308352 | tf_op jit(solution)/shard_map/convert_element_type | solution.py:173
  79.8 3.0 %collective-permute-start.12 = (bf16[512,256]{1,0:T(8,128)(2,1)S(1)}, bf16[512,256]{1,0:T(8,128)(2,1)S(1)}, u32[]{:S(2)}, u32[]{:S(2)}) collective-permute-start(bf16[512,256]{1,0:T(8,128)(2,1)S(1)} %convolution_convert_fusion.1), channel_id=1, source_target_pairs={{0,16},{4,20},{8,24},{12,28},{16,0},{20,4},{24,8},{28,12},{1,17},{... | collective-permute-start | bytes 786440 | tf_op jit(solution)/shard_map/ppermute | solution.py:58
  83.2 8.2 %collective-permute-done.12 = bf16[512,256]{1,0:T(8,128)(2,1)S(1)} collective-permute-done((bf16[512,256]{1,0:T(8,128)(2,1)S(1)}, bf16[512,256]{1,0:T(8,128)(2,1)S(1)}, u32[]{:S(2)}, u32[]{:S(2)}) %collective-permute-start.12) | collective-permute-done | bytes 262176 | tf_op jit(solution)/shard_map/ppermute | solution.py:58
  91.4 0.9 convert_add_fusion
  (112 shorter events, 10.1 us)
Async XLA Ops:
  0.6 18.6 %copy-start = (bf16[1024,256]{1,0:T(8,128)(2,1)S(1)}, bf16[1024,256]{1,0:T(8,128)(2,1)}, u32[]{:S(2)}) copy-start(bf16[1024,256]{1,0:T(8,128)(2,1)} %param.17) | copy-start | bytes 1572868
  0.6 10.1 %copy-start.1 = (bf16[512,256]{1,0:T(8,128)(2,1)S(1)}, bf16[512,256]{1,0:T(8,128)(2,1)}, u32[]{:S(2)}) copy-start(bf16[512,256]{1,0:T(8,128)(2,1)} %param.18) | copy-start | bytes 786436
  0.7 10.2 %copy-start.5 = (bf16[256,256]{1,0:T(8,128)(2,1)S(1)}, bf16[256,256]{1,0:T(8,128)(2,1)}, u32[]{:S(2)}) copy-start(bf16[256,256]{1,0:T(8,128)(2,1)} %param.19) | copy-start | bytes 393220
  3.2 9.6 %collective-permute-start = (bf16[256,512]{1,0:T(8,128)(2,1)S(1)}, bf16[256,512]{1,0:T(8,128)(2,1)S(1)}, u32[]{:S(2)}, u32[]{:S(2)}) collective-permute-start(bf16[256,512]{1,0:T(8,128)(2,1)S(1)} %slice.85), channel_id=1, source_target_pairs={{0,2},{2,4},{4,6},{6,8},{8,10},{10,12},{12,14},{14,16},{16,18},{18... | collective-permute-start | bytes 786440 | tf_op jit(solution)/shard_map/ppermute | solution.py:16
  3.7 9.1 %collective-permute-start.1 = (bf16[256,512]{1,0:T(8,128)(2,1)S(1)}, bf16[256,512]{1,0:T(8,128)(2,1)S(1)}, u32[]{:S(2)}, u32[]{:S(2)}) collective-permute-start(bf16[256,512]{1,0:T(8,128)(2,1)S(1)} %slice.85), channel_id=1, source_target_pairs={{2,0},{4,2},{6,4},{8,6},{10,8},{12,10},{14,12},{16,14},{18,16},{20... | collective-permute-start | bytes 786440 | tf_op jit(solution)/shard_map/ppermute | solution.py:19
  17.5 1.4 %copy-start.6 = (bf16[256,256]{1,0:T(8,128)(2,1)S(1)}, bf16[256,256]{1,0:T(8,128)(2,1)}, u32[]{:S(2)}) copy-start(bf16[256,256]{1,0:T(8,128)(2,1)} %param.15) | copy-start | bytes 393220
  17.5 1.8 %copy-start.9 = (bf16[256,1024]{1,0:T(8,128)(2,1)S(1)}, bf16[256,1024]{1,0:T(8,128)(2,1)}, u32[]{:S(2)}) copy-start(bf16[256,1024]{1,0:T(8,128)(2,1)} %param.16) | copy-start | bytes 1572868
  18.9 1.4 %copy-start.4 = (bf16[256,512]{1,0:T(8,128)(2,1)S(1)}, bf16[256,512]{1,0:T(8,128)(2,1)}, u32[]{:S(2)}) copy-start(bf16[256,512]{1,0:T(8,128)(2,1)} %param.20) | copy-start | bytes 786436
  20.2 5.0 %copy-start.2 = (bf16[256,256]{1,0:T(8,128)(2,1)}, bf16[256,256]{1,0:T(8,128)(2,1)S(1)}, u32[]{:S(2)}) copy-start(bf16[256,256]{1,0:T(8,128)(2,1)S(1)} %copy.66) | copy-start | bytes 393220
  25.2 18.7 %collective-permute-start.8 = (bf16[528,256]{1,0:T(8,128)(2,1)S(1)}, bf16[528,256]{1,0:T(8,128)(2,1)S(1)}, u32[]{:S(2)}, u32[]{:S(2)}) collective-permute-start(bf16[528,256]{1,0:T(8,128)(2,1)S(1)} %fusion.58), channel_id=1, source_target_pairs={{0,4},{4,0},{8,12},{12,8},{16,20},{20,16},{24,28},{28,24},{1,5},{5... | collective-permute-start | bytes 811016 | tf_op jit(solution)/shard_map/ppermute | solution.py:100
  28.4 4.0 %collective-permute-start.3 = (f32[2,8,512]{2,1,0:T(8,128)S(1)}, f32[2,8,512]{2,1,0:T(8,128)S(1)}, u32[]{:S(2)}, u32[]{:S(2)}) collective-permute-start(f32[2,8,512]{2,1,0:T(8,128)S(1)} %pad_maximum_fusion.1), channel_id=1, source_target_pairs={{0,8},{4,12},{8,0},{12,4},{16,24},{20,28},{24,16},{28,20},{1,9},{5... | collective-permute-start | bytes 98312 | tf_op jit(solution)/shard_map/ppermute | solution.py:39
  31.3 10.0 %collective-permute-start.2 = (bf16[512,256]{0,1:T(8,128)(2,1)S(1)}, bf16[512,256]{0,1:T(8,128)(2,1)S(1)}, u32[]{:S(2)}, u32[]{:S(2)}) collective-permute-start(bf16[512,256]{0,1:T(8,128)(2,1)S(1)} %bitcast.171), channel_id=1, source_target_pairs={{0,8},{4,12},{8,0},{12,4},{16,24},{20,28},{24,16},{28,20},{1,9},{5... | collective-permute-start | bytes 786440 | tf_op jit(solution)/shard_map/ppermute | solution.py:39
  32.4 4.0 %collective-permute-start.5 = (f32[2,8,512]{2,1,0:T(8,128)S(1)}, f32[2,8,512]{2,1,0:T(8,128)S(1)}, u32[]{:S(2)}, u32[]{:S(2)}) collective-permute-start(f32[2,8,512]{2,1,0:T(8,128)S(1)} %pad_maximum_fusion.2), channel_id=1, source_target_pairs={{0,4},{4,0},{8,12},{12,8},{16,20},{20,16},{24,28},{28,24},{1,5},{5... | collective-permute-start | bytes 98312 | tf_op jit(solution)/shard_map/ppermute | solution.py:39
  36.4 4.9 %collective-permute-start.7 = (f32[2,8,512]{2,1,0:T(8,128)S(1)}, f32[2,8,512]{2,1,0:T(8,128)S(1)}, u32[]{:S(2)}, u32[]{:S(2)}) collective-permute-start(f32[2,8,512]{2,1,0:T(8,128)S(1)} %pad_maximum_fusion.3), channel_id=1, source_target_pairs={{0,16},{4,20},{8,24},{12,28},{16,0},{20,4},{24,8},{28,12},{1,17},{... | collective-permute-start | bytes 98312 | tf_op jit(solution)/shard_map/ppermute | solution.py:39
  41.3 18.0 %copy-start.7 = (bf16[256,256]{1,0:T(8,128)(2,1)S(1)}, bf16[256,256]{1,0:T(8,128)(2,1)}, u32[]{:S(2)}) copy-start(bf16[256,256]{1,0:T(8,128)(2,1)} %param.21) | copy-start | bytes 393220
  41.5 6.7 %collective-permute-start.4 = (bf16[512,256]{0,1:T(8,128)(2,1)S(1)}, bf16[512,256]{0,1:T(8,128)(2,1)S(1)}, u32[]{:S(2)}, u32[]{:S(2)}) collective-permute-start(bf16[512,256]{0,1:T(8,128)(2,1)S(1)} %fusion.39), channel_id=1, source_target_pairs={{0,4},{4,0},{8,12},{12,8},{16,20},{20,16},{24,28},{28,24},{1,5},{5... | collective-permute-start | bytes 786440 | tf_op jit(solution)/shard_map/ppermute | solution.py:39
  43.9 15.8 %copy-start.10 = (bf16[256,256]{1,0:T(8,128)(2,1)S(1)}, bf16[256,256]{1,0:T(8,128)(2,1)}, u32[]{:S(2)}) copy-start(bf16[256,256]{1,0:T(8,128)(2,1)} %param.23) | copy-start | bytes 393220
  44.0 15.8 %copy-start.11 = (bf16[256,256]{1,0:T(8,128)(2,1)S(1)}, bf16[256,256]{1,0:T(8,128)(2,1)}, u32[]{:S(2)}) copy-start(bf16[256,256]{1,0:T(8,128)(2,1)} %param.22) | copy-start | bytes 393220
  48.3 10.8 %collective-permute-start.6 = (bf16[512,256]{0,1:T(8,128)(2,1)S(1)}, bf16[512,256]{0,1:T(8,128)(2,1)S(1)}, u32[]{:S(2)}, u32[]{:S(2)}) collective-permute-start(bf16[512,256]{0,1:T(8,128)(2,1)S(1)} %fusion.37), channel_id=1, source_target_pairs={{0,16},{4,20},{8,24},{12,28},{16,0},{20,4},{24,8},{28,12},{1,17},{... | collective-permute-start | bytes 786440 | tf_op jit(solution)/shard_map/ppermute | solution.py:39
  50.4 14.8 %copy-start.8 = (s32[512]{0:T(512)S(1)}, s32[512]{0:T(512)}, u32[]{:S(2)}) copy-start(s32[512]{0:T(512)} %param.25) | copy-start | bytes 6148
  50.5 14.7 %collective-permute-start.9 = (bf16[1040,256]{1,0:T(8,128)(2,1)S(1)}, bf16[1040,256]{1,0:T(8,128)(2,1)S(1)}, u32[]{:S(2)}, u32[]{:S(2)}) collective-permute-start(bf16[1040,256]{1,0:T(8,128)(2,1)S(1)} %fusion.31), channel_id=1, source_target_pairs={{0,8},{4,12},{8,0},{12,4},{16,24},{20,28},{24,16},{28,20},{1,9},{5... | collective-permute-start | bytes 1597448 | tf_op jit(solution)/shard_map/ppermute | solution.py:100
  60.2 22.6 %copy-start.3 = (bf16[512,256]{1,0:T(8,128)(2,1)}, bf16[512,256]{1,0:T(8,128)(2,1)S(1)}, u32[]{:S(2)}) copy-start(bf16[512,256]{1,0:T(8,128)(2,1)S(1)} %convolution_convert_fusion.2) | copy-start | bytes 786436
  69.5 4.7 %collective-permute-start.10 = (f32[3,512]{1,0:T(4,128)S(1)}, f32[3,512]{1,0:T(4,128)S(1)}, u32[]{:S(2)}, u32[]{:S(2)}) collective-permute-start(f32[3,512]{1,0:T(4,128)S(1)} %pad_maximum_fusion.4), channel_id=1, source_target_pairs={{0,16},{4,20},{8,24},{12,28},{16,0},{20,4},{24,8},{28,12},{1,17},{... | collective-permute-start | bytes 18440 | tf_op jit(solution)/shard_map/ppermute | solution.py:39
  79.8 11.6 %collective-permute-start.12 = (bf16[512,256]{1,0:T(8,128)(2,1)S(1)}, bf16[512,256]{1,0:T(8,128)(2,1)S(1)}, u32[]{:S(2)}, u32[]{:S(2)}) collective-permute-start(bf16[512,256]{1,0:T(8,128)(2,1)S(1)} %convolution_convert_fusion.1), channel_id=1, source_target_pairs={{0,16},{4,20},{8,24},{12,28},{16,0},{20,4},{24,8},{28,12},{1,17},{... | collective-permute-start | bytes 786440 | tf_op jit(solution)/shard_map/ppermute | solution.py:58
  83.2 9.1 %collective-permute-start.11 = (f32[256,256]{1,0:T(8,128)S(1)}, f32[256,256]{1,0:T(8,128)S(1)}, u32[]{:S(2)}, u32[]{:S(2)}) collective-permute-start(f32[256,256]{1,0:T(8,128)S(1)} %slice_select_fusion), channel_id=1, source_target_pairs={{0,2},{2,0},{1,3},{3,1},{4,6},{6,4},{5,7},{7,5},{8,10},{10,8},{9,1... | collective-permute-start | bytes 786440 | tf_op jit(solution)/shard_map/ppermute | solution.py:89

commit v19 on v18

--- a/solution.py
+++ b/solution.py
@@ -34,7 +34,7 @@
         distances.append(distance)
         distance *= 2
     if order is not None and len(distances) >= 2:
-        distances[0], distances[1] = distances[1], distances[0]
+        distances = distances[1:] + distances[:1]
     for distance in distances:
         other = lax.ppermute(tree, axis, partner_pairs(count, distance))
         if ordered:

time: 93.2 us -> 97.9 us (1.050)
  waiting for transfers between devices: 32.1 us -> 37.8 us
  starting transfers between devices: 24.5 us -> 23.5 us
    ppermute x7, waiting for transfers between devices: 17.3 us -> 22.1 us  [butterfly(): other = lax.ppermute(tree, axis, partner_pairs(count, distance))]
    ppermute x2, starting transfers between devices: 2.02 us -> 0.23 us  [partner_rows(): lax.ppermute(payload, 'phi', partner_pairs(lax.axis_size('phi'), distance))]
where the time goes in v19:
time: 97.9 us; the launch traced here: 97.7 us
  waiting for transfers between devices  37.8 us (39%)
  starting transfers between devices  23.5 us (24%)
  matrix products  16.8 us (17%)
  other arithmetic  10.6 us (11%)
  blocking collectives  4.35 us (4%)
  local copies, waits for them, and re-layouts  3.42 us (3%)
  between operations  1.31 us (1%)
    ppermute x7, waiting for transfers between devices, butterfly(): other = lax.ppermute(tree, axis, partner_pairs(count, distance))  22.1 us
    ppermute x7, starting transfers between devices, butterfly(): other = lax.ppermute(tree, axis, partner_pairs(count, distance))  14.7 us
    ppermute x1, waiting for transfers between devices, narrow_butterfly(): other = lax.ppermute(sent, axis, partner_pairs(count, distance))  8.75 us
    ppermute x2, waiting for transfers between devices, partner_rows(): lax.ppermute(payload, 'phi', partner_pairs(lax.axis_size('phi'), distance))  5.24 us
    ppermute x1, starting transfers between devices, extended_2(): lax.ppermute(lax.slice_in_dim(block, 0, width, axis=dim), axis, backward)  5.03 us
    all_gather x1, blocking collectives, body(): lax.all_gather(jnp.concatenate([local_kv, encoded, digits], axis=1), 'que...  4.35 us
    dot_general x1, matrix products, body(): lax.dot_general(mask_embed, pair_hits, (((1,), (1,)), ((), ())), preferre...  4.24 us
    convert_element_type x1, other arithmetic, loss_coefficients(): (matched[:, None] * (sigma - target + dice_part) * model_width ** (-0.5))...  4.16 us
  transfers between devices with their start and end apart: 13, of which 9 were waited for; matrix products, arithmetic and copies ran while one was open for 10% of the time, Pallas kernels for 0%

profile of v19, /device:TPU:0, one launch (start us, length us, event | category | flops | bytes accessed | tf_op | source)
XLA Modules:
  0.0 97.7 jit_solution(5416865665083762499)
XLA Ops:
  0.7 1.1 %copy.50 = bf16[256,256]{0,1:T(8,128)(2,1)S(1)} copy(bf16[256,256]{1,0:T(8,128)(2,1)} %param.13) | data formatting | bytes 262144 | tf_op args[0]
  1.9 1.3 %convolution_convert_fusion = bf16[256,768]{1,0:T(8,128)(2,1)S(1)} fusion(bf16[256,768]{1,0:T(8,128)(2,1)} %param.14, bf16[256,256]{0,1:T(8,128)(2,1)S(1)} %copy.50, f32[256]{0:T(256)S(1)} %add_rsqrt_fusion.3, f32[256]{0:T(256)S(1)} %broadcast_multiply_fusion.3), kind=kOutput, calls=%fused_computation.31 | convolution fusion | flops 101122048 | bytes 919552 | tf_op jit(solution)/shard_map/dot_general | solution.py:199
  3.7 5.0 %collective-permute-start.1 = (bf16[256,512]{1,0:T(8,128)(2,1)S(1)}, bf16[256,512]{1,0:T(8,128)(2,1)S(1)}, u32[]{:S(2)}, u32[]{:S(2)}) collective-permute-start(bf16[256,512]{1,0:T(8,128)(2,1)S(1)} %slice.85), channel_id=1, source_target_pairs={{2,0},{4,2},{6,4},{8,6},{10,8},{12,10},{14,12},{16,14},{18,16},{20... | collective-permute-start | bytes 786440 | tf_op jit(solution)/shard_map/ppermute | solution.py:19
  11.2 1.7 %collective-permute-done = bf16[256,512]{1,0:T(8,128)(2,1)S(1)} collective-permute-done((bf16[256,512]{1,0:T(8,128)(2,1)S(1)}, bf16[256,512]{1,0:T(8,128)(2,1)S(1)}, u32[]{:S(2)}, u32[]{:S(2)}) %collective-permute-start) | collective-permute-done | bytes 262176 | tf_op jit(solution)/shard_map/ppermute | solution.py:16
  13.8 1.1 %fusion.140 = f32[8,128]{1,0:T(8,128)S(1)} fusion(pred[128,640]{1,0:T(8,128)(4,1)S(1)} %fusion.49, bf16[128,8,32]{0,2,1:T(8,128)(2,1)S(1)} %bitcast.186, bf16[640,8,32]{0,2,1:T(8,128)(2,1)S(1)} %bitcast.177), kind=kOutput, calls=%fused_computation.228 | convolution fusion | flops 44565120 | bytes 479232 | tf_op jit(solution)/shard_map/sub | solution.py:136
  15.0 1.4 %fusion.19 = bf16[8,32,128]{2,1,0:T(8,128)(2,1)S(1)} fusion(bf16[640,8,32]{0,2,1:T(8,128)(2,1)S(1)} %bitcast.179, f32[8,128]{1,0:T(8,128)S(1)} %fusion.140, pred[128,640]{1,0:T(8,128)(4,1)S(1)} %fusion.49, bf16[128,8,32]{0,2,1:T(8,128)(2,1)S(1)} %bitcast.187, bf16[640,8,32]{0,2,1:T(8,128)(2,1)S(1)} %bitcast.178), kind=kOutput, calls=%fused_computation.44 | convolution fusion | flops 87197312 | bytes 872448 | tf_op jit(solution)/shard_map/hqk,khd->qhd/dot_general | solution.py:138
  16.3 1.2 %fusion.139 = f32[8,128]{1,0:T(8,128)S(1)} fusion(pred[128,640]{1,0:T(8,128)(4,1)S(1)} %fusion.49, bf16[128,8,32]{0,2,1:T(8,128)(2,1)S(1)} %bitcast.184, bf16[640,8,32]{0,2,1:T(8,128)(2,1)S(1)} %bitcast.174), kind=kOutput, calls=%fused_computation.227 | convolution fusion | flops 44565120 | bytes 479232 | tf_op jit(solution)/shard_map/sub | solution.py:136
  17.5 1.3 %fusion.18 = bf16[8,32,128]{2,1,0:T(8,128)(2,1)S(1)} fusion(bf16[640,8,32]{0,2,1:T(8,128)(2,1)S(1)} %bitcast.176, f32[8,128]{1,0:T(8,128)S(1)} %fusion.139, pred[128,640]{1,0:T(8,128)(4,1)S(1)} %fusion.49, bf16[128,8,32]{0,2,1:T(8,128)(2,1)S(1)} %bitcast.185, bf16[640,8,32]{0,2,1:T(8,128)(2,1)S(1)} %bitcast.175), kind=kOutput, calls=%fused_computation.43 | convolution fusion | flops 87197312 | bytes 872448 | tf_op jit(solution)/shard_map/hqk,khd->qhd/dot_general | solution.py:138
  19.3 0.8 convert_reduce_fusion.3
  20.6 4.3 %all_gather.3 = bf16[512,896]{1,0:T(8,128)(2,1)S(1)} all-gather(bf16[256,896]{1,0:T(8,128)(2,1)S(1)} %fusion.46), channel_id=1, replica_groups=mesh['phi'=8,'query'=2,'event'=2] {'query'}, dimensions={0}, use_global_device_ids=true | all-gather | bytes 1376256 | tf_op jit(solution)/shard_map/all_gather | solution.py:230
  25.7 1.3 %multiply_reduce_fusion = (f32[8,512]{1,0:T(8,128)S(1)}, f32[8,512,512]{1,2,0:T(8,128)S(1)}) fusion(bf16[512,8,32]{0,2,1:T(8,128)(2,1)S(1)} %bitcast.168, bf16[512,8,32]{0,2,1:T(8,128)(2,1)S(1)} %bitcast.170), kind=kOutput, calls=%fused_computation.4 | convolution fusion | flops 138407936 | bytes 8929280 | tf_op jit(solution)/shard_map/qhd,khd->hqk/dot_general | solution.py:243
  27.0 1.4 %convert_reduce_fusion = f32[8,512]{1,0:T(8,128)S(1)} fusion(f32[8,512]{1,0:T(8,128)S(1)} %get-tuple-element.63, f32[8,512,512]{1,2,0:T(8,128)S(1)} %get-tuple-element.64), kind=kLoop, calls=%fused_computation.2 | loop fusion | flops 10481664 | bytes 8421376 | tf_op jit(solution)/shard_map/reduce_sum | solution.py:248
  28.4 1.3 %collective-permute-start.3 = (f32[2,8,512]{2,1,0:T(8,128)S(1)}, f32[2,8,512]{2,1,0:T(8,128)S(1)}, u32[]{:S(2)}, u32[]{:S(2)}) collective-permute-start(f32[2,8,512]{2,1,0:T(8,128)S(1)} %pad_maximum_fusion.1), channel_id=1, source_target_pairs={{0,8},{4,12},{8,0},{12,4},{16,24},{20,28},{24,16},{28,20},{1,9},{5... | collective-permute-start | bytes 98312 | tf_op jit(solution)/shard_map/ppermute | solution.py:39
  29.6 1.5 %convolution_convert_fusion.3 = bf16[8,32,512]{2,1,0:T(8,128)(2,1)S(1)} fusion(bf16[512,8,32]{0,2,1:T(8,128)(2,1)S(1)} %bitcast.169, f32[8,512,512]{1,2,0:T(8,128)S(1)} %get-tuple-element.64, f32[8,512]{1,0:T(8,128)S(1)} %get-tuple-element.63), kind=kOutput, calls=%fused_computation.36 | convolution fusion | flops 140640256 | bytes 8929280 | tf_op jit(solution)/shard_map/hqk,khd->qhd/dot_general | solution.py:249
  31.3 0.9 collective-permute-start.2
  32.4 2.3 %collective-permute-start.5 = (f32[2,8,512]{2,1,0:T(8,128)S(1)}, f32[2,8,512]{2,1,0:T(8,128)S(1)}, u32[]{:S(2)}, u32[]{:S(2)}) collective-permute-start(f32[2,8,512]{2,1,0:T(8,128)S(1)} %pad_maximum_fusion.2), channel_id=1, source_target_pairs={{0,16},{4,20},{8,24},{12,28},{16,0},{20,4},{24,8},{28,12},{1,17},{... | collective-permute-start | bytes 98312 | tf_op jit(solution)/shard_map/ppermute | solution.py:39
  34.7 3.9 %collective-permute-done.5 = f32[2,8,512]{2,1,0:T(8,128)S(1)} collective-permute-done((f32[2,8,512]{2,1,0:T(8,128)S(1)}, f32[2,8,512]{2,1,0:T(8,128)S(1)}, u32[]{:S(2)}, u32[]{:S(2)}) %collective-permute-start.5) | collective-permute-done | bytes 32800 | tf_op jit(solution)/shard_map/ppermute | solution.py:39
  38.6 1.8 %collective-permute-start.7 = (f32[2,8,512]{2,1,0:T(8,128)S(1)}, f32[2,8,512]{2,1,0:T(8,128)S(1)}, u32[]{:S(2)}, u32[]{:S(2)}) collective-permute-start(f32[2,8,512]{2,1,0:T(8,128)S(1)} %pad_maximum_fusion.3), channel_id=1, source_target_pairs={{0,4},{4,0},{8,12},{12,8},{16,20},{20,16},{24,28},{28,24},{1,5},{5... | collective-permute-start | bytes 98312 | tf_op jit(solution)/shard_map/ppermute | solution.py:39
  40.4 2.2 %collective-permute-done.7 = f32[2,8,512]{2,1,0:T(8,128)S(1)} collective-permute-done((f32[2,8,512]{2,1,0:T(8,128)S(1)}, f32[2,8,512]{2,1,0:T(8,128)S(1)}, u32[]{:S(2)}, u32[]{:S(2)}) %collective-permute-start.7) | collective-permute-done | bytes 32800 | tf_op jit(solution)/shard_map/ppermute | solution.py:39
  42.8 3.5 %collective-permute-start.4 = (bf16[512,256]{0,1:T(8,128)(2,1)S(1)}, bf16[512,256]{0,1:T(8,128)(2,1)S(1)}, u32[]{:S(2)}, u32[]{:S(2)}) collective-permute-start(bf16[512,256]{0,1:T(8,128)(2,1)S(1)} %fusion.39), channel_id=1, source_target_pairs={{0,16},{4,20},{8,24},{12,28},{16,0},{20,4},{24,8},{28,12},{1,17},{... | collective-permute-start | bytes 786440 | tf_op jit(solution)/shard_map/ppermute | solution.py:39
  46.6 9.5 %collective-permute-done.4 = bf16[512,256]{0,1:T(8,128)(2,1)S(1)} collective-permute-done((bf16[512,256]{0,1:T(8,128)(2,1)S(1)}, bf16[512,256]{0,1:T(8,128)(2,1)S(1)}, u32[]{:S(2)}, u32[]{:S(2)}) %collective-permute-start.4) | collective-permute-done | bytes 262176 | tf_op jit(solution)/shard_map/ppermute | solution.py:39
  56.2 1.6 %collective-permute-start.6 = (bf16[512,256]{0,1:T(8,128)(2,1)S(1)}, bf16[512,256]{0,1:T(8,128)(2,1)S(1)}, u32[]{:S(2)}, u32[]{:S(2)}) collective-permute-start(bf16[512,256]{0,1:T(8,128)(2,1)S(1)} %fusion.37), channel_id=1, source_target_pairs={{0,4},{4,0},{8,12},{12,8},{16,20},{20,16},{24,28},{28,24},{1,5},{5... | collective-permute-start | bytes 786440 | tf_op jit(solution)/shard_map/ppermute | solution.py:39
  57.9 4.7 %collective-permute-done.6 = bf16[512,256]{0,1:T(8,128)(2,1)S(1)} collective-permute-done((bf16[512,256]{0,1:T(8,128)(2,1)S(1)}, bf16[512,256]{0,1:T(8,128)(2,1)S(1)}, u32[]{:S(2)}, u32[]{:S(2)}) %collective-permute-start.6) | collective-permute-done | bytes 262176 | tf_op jit(solution)/shard_map/ppermute | solution.py:39
  63.7 5.2 %collective-permute-done.9 = bf16[1040,256]{1,0:T(8,128)(2,1)S(1)} collective-permute-done((bf16[1040,256]{1,0:T(8,128)(2,1)S(1)}, bf16[1040,256]{1,0:T(8,128)(2,1)S(1)}, u32[]{:S(2)}, u32[]{:S(2)}) %collective-permute-start.9) | collective-permute-done | bytes 532512 | tf_op jit(solution)/shard_map/ppermute | solution.py:100
  69.0 4.2 %select_reduce_fusion = (f32[512]{0:T(512)S(1)}, f32[512]{0:T(512)S(1)}, f32[512]{0:T(512)S(1)}, f32[512,2048]{1,0:T(8,128)}) fusion(s32[2048]{0:T(1024)S(1)} %bitcast.189, s32[512]{0:T(512)S(1)} %copy-done.8, pred[512]{0:T(512)(128)(4,1)S(1)} %get-tuple-element.24, bf16[512,256]{1,0:T(8,128)(2,1)S(1)} %convolution_convert_fusion.2, ...), kind=kOutput, calls=%fused_computation.11 | convolution fusion | flops 553122304 | bytes 5521921 | tf_op jit(solution)/shard_map/dot_general | solution.py:280
  73.3 3.4 %collective-permute-start.10 = (f32[3,512]{1,0:T(4,128)S(1)}, f32[3,512]{1,0:T(4,128)S(1)}, u32[]{:S(2)}, u32[]{:S(2)}) collective-permute-start(f32[3,512]{1,0:T(4,128)S(1)} %pad_maximum_fusion.4), channel_id=1, source_target_pairs={{0,16},{4,20},{8,24},{12,28},{16,0},{20,4},{24,8},{28,12},{1,17},{... | collective-permute-start | bytes 18440 | tf_op jit(solution)/shard_map/ppermute | solution.py:39
  76.7 1.6 %collective-permute-done.10 = f32[3,512]{1,0:T(4,128)S(1)} collective-permute-done((f32[3,512]{1,0:T(4,128)S(1)}, f32[3,512]{1,0:T(4,128)S(1)}, u32[]{:S(2)}, u32[]{:S(2)}) %collective-permute-start.10) | collective-permute-done | bytes 6176 | tf_op jit(solution)/shard_map/ppermute | solution.py:39
  79.0 4.2 %fusion.5 = bf16[512,2048]{1,0:T(8,128)(2,1)S(1)} fusion(f32[512,2048]{1,0:T(8,128)} %get-tuple-element.67, f32[512]{0:T(512)S(1)} %bitcast.192, f32[512]{0:T(512)S(1)} %bitcast.193, s32[2048]{0:T(1024)S(1)} %bitcast.190, f32[512]{0:T(512)S(1)} %get-tuple-element.23, s32[512]{0:T(512)S(1)} %copy-done.8, pred[512]{0:T(512)(128)(4,1)S(1)} %get-tuple-element.24), kind=kLoop, calls=%fused_computation.10 | loop fusion | flops 14680064 | bytes 6308352 | tf_op jit(solution)/shard_map/convert_element_type | solution.py:173
  83.9 3.0 %collective-permute-start.12 = (bf16[512,256]{1,0:T(8,128)(2,1)S(1)}, bf16[512,256]{1,0:T(8,128)(2,1)S(1)}, u32[]{:S(2)}, u32[]{:S(2)}) collective-permute-start(bf16[512,256]{1,0:T(8,128)(2,1)S(1)} %convolution_convert_fusion.1), channel_id=1, source_target_pairs={{0,16},{4,20},{8,24},{12,28},{16,0},{20,4},{24,8},{28,12},{1,17},{... | collective-permute-start | bytes 786440 | tf_op jit(solution)/shard_map/ppermute | solution.py:58
  87.3 8.8 %collective-permute-done.12 = bf16[512,256]{1,0:T(8,128)(2,1)S(1)} collective-permute-done((bf16[512,256]{1,0:T(8,128)(2,1)S(1)}, bf16[512,256]{1,0:T(8,128)(2,1)S(1)}, u32[]{:S(2)}, u32[]{:S(2)}) %collective-permute-start.12) | collective-permute-done | bytes 262176 | tf_op jit(solution)/shard_map/ppermute | solution.py:58
  96.1 0.9 convert_add_fusion
  97.0 0.8 select_add_fusion
  (112 shorter events, 9.4 us)
Async XLA Ops:
  0.6 18.6 %copy-start = (bf16[1024,256]{1,0:T(8,128)(2,1)S(1)}, bf16[1024,256]{1,0:T(8,128)(2,1)}, u32[]{:S(2)}) copy-start(bf16[1024,256]{1,0:T(8,128)(2,1)} %param.17) | copy-start | bytes 1572868
  0.6 10.1 %copy-start.1 = (bf16[512,256]{1,0:T(8,128)(2,1)S(1)}, bf16[512,256]{1,0:T(8,128)(2,1)}, u32[]{:S(2)}) copy-start(bf16[512,256]{1,0:T(8,128)(2,1)} %param.18) | copy-start | bytes 786436
  0.7 10.2 %copy-start.5 = (bf16[256,256]{1,0:T(8,128)(2,1)S(1)}, bf16[256,256]{1,0:T(8,128)(2,1)}, u32[]{:S(2)}) copy-start(bf16[256,256]{1,0:T(8,128)(2,1)} %param.19) | copy-start | bytes 393220
  3.2 9.6 %collective-permute-start = (bf16[256,512]{1,0:T(8,128)(2,1)S(1)}, bf16[256,512]{1,0:T(8,128)(2,1)S(1)}, u32[]{:S(2)}, u32[]{:S(2)}) collective-permute-start(bf16[256,512]{1,0:T(8,128)(2,1)S(1)} %slice.85), channel_id=1, source_target_pairs={{0,2},{2,4},{4,6},{6,8},{8,10},{10,12},{12,14},{14,16},{16,18},{18... | collective-permute-start | bytes 786440 | tf_op jit(solution)/shard_map/ppermute | solution.py:16
  3.7 9.1 %collective-permute-start.1 = (bf16[256,512]{1,0:T(8,128)(2,1)S(1)}, bf16[256,512]{1,0:T(8,128)(2,1)S(1)}, u32[]{:S(2)}, u32[]{:S(2)}) collective-permute-start(bf16[256,512]{1,0:T(8,128)(2,1)S(1)} %slice.85), channel_id=1, source_target_pairs={{2,0},{4,2},{6,4},{8,6},{10,8},{12,10},{14,12},{16,14},{18,16},{20... | collective-permute-start | bytes 786440 | tf_op jit(solution)/shard_map/ppermute | solution.py:19
  17.5 1.4 %copy-start.6 = (bf16[256,256]{1,0:T(8,128)(2,1)S(1)}, bf16[256,256]{1,0:T(8,128)(2,1)}, u32[]{:S(2)}) copy-start(bf16[256,256]{1,0:T(8,128)(2,1)} %param.15) | copy-start | bytes 393220
  17.5 1.8 %copy-start.9 = (bf16[256,1024]{1,0:T(8,128)(2,1)S(1)}, bf16[256,1024]{1,0:T(8,128)(2,1)}, u32[]{:S(2)}) copy-start(bf16[256,1024]{1,0:T(8,128)(2,1)} %param.16) | copy-start | bytes 1572868
  18.9 1.4 %copy-start.4 = (bf16[256,512]{1,0:T(8,128)(2,1)S(1)}, bf16[256,512]{1,0:T(8,128)(2,1)}, u32[]{:S(2)}) copy-start(bf16[256,512]{1,0:T(8,128)(2,1)} %param.20) | copy-start | bytes 786436
  20.2 5.0 %copy-start.2 = (bf16[256,256]{1,0:T(8,128)(2,1)}, bf16[256,256]{1,0:T(8,128)(2,1)S(1)}, u32[]{:S(2)}) copy-start(bf16[256,256]{1,0:T(8,128)(2,1)S(1)} %copy.66) | copy-start | bytes 393220
  25.2 21.1 %collective-permute-start.8 = (bf16[528,256]{1,0:T(8,128)(2,1)S(1)}, bf16[528,256]{1,0:T(8,128)(2,1)S(1)}, u32[]{:S(2)}, u32[]{:S(2)}) collective-permute-start(bf16[528,256]{1,0:T(8,128)(2,1)S(1)} %fusion.58), channel_id=1, source_target_pairs={{0,4},{4,0},{8,12},{12,8},{16,20},{20,16},{24,28},{28,24},{1,5},{5... | collective-permute-start | bytes 811016 | tf_op jit(solution)/shard_map/ppermute | solution.py:100
  28.4 4.0 %collective-permute-start.3 = (f32[2,8,512]{2,1,0:T(8,128)S(1)}, f32[2,8,512]{2,1,0:T(8,128)S(1)}, u32[]{:S(2)}, u32[]{:S(2)}) collective-permute-start(f32[2,8,512]{2,1,0:T(8,128)S(1)} %pad_maximum_fusion.1), channel_id=1, source_target_pairs={{0,8},{4,12},{8,0},{12,4},{16,24},{20,28},{24,16},{28,20},{1,9},{5... | collective-permute-start | bytes 98312 | tf_op jit(solution)/shard_map/ppermute | solution.py:39
  31.3 11.3 %collective-permute-start.2 = (bf16[512,256]{0,1:T(8,128)(2,1)S(1)}, bf16[512,256]{0,1:T(8,128)(2,1)S(1)}, u32[]{:S(2)}, u32[]{:S(2)}) collective-permute-start(bf16[512,256]{0,1:T(8,128)(2,1)S(1)} %bitcast.171), channel_id=1, source_target_pairs={{0,8},{4,12},{8,0},{12,4},{16,24},{20,28},{24,16},{28,20},{1,9},{5... | collective-permute-start | bytes 786440 | tf_op jit(solution)/shard_map/ppermute | solution.py:39
  32.4 6.2 %collective-permute-start.5 = (f32[2,8,512]{2,1,0:T(8,128)S(1)}, f32[2,8,512]{2,1,0:T(8,128)S(1)}, u32[]{:S(2)}, u32[]{:S(2)}) collective-permute-start(f32[2,8,512]{2,1,0:T(8,128)S(1)} %pad_maximum_fusion.2), channel_id=1, source_target_pairs={{0,16},{4,20},{8,24},{12,28},{16,0},{20,4},{24,8},{28,12},{1,17},{... | collective-permute-start | bytes 98312 | tf_op jit(solution)/shard_map/ppermute | solution.py:39
  38.6 4.0 %collective-permute-start.7 = (f32[2,8,512]{2,1,0:T(8,128)S(1)}, f32[2,8,512]{2,1,0:T(8,128)S(1)}, u32[]{:S(2)}, u32[]{:S(2)}) collective-permute-start(f32[2,8,512]{2,1,0:T(8,128)S(1)} %pad_maximum_fusion.3), channel_id=1, source_target_pairs={{0,4},{4,0},{8,12},{12,8},{16,20},{20,16},{24,28},{28,24},{1,5},{5... | collective-permute-start | bytes 98312 | tf_op jit(solution)/shard_map/ppermute | solution.py:39
  42.6 20.2 %copy-start.7 = (bf16[256,256]{1,0:T(8,128)(2,1)S(1)}, bf16[256,256]{1,0:T(8,128)(2,1)}, u32[]{:S(2)}) copy-start(bf16[256,256]{1,0:T(8,128)(2,1)} %param.21) | copy-start | bytes 393220
  42.8 13.3 %collective-permute-start.4 = (bf16[512,256]{0,1:T(8,128)(2,1)S(1)}, bf16[512,256]{0,1:T(8,128)(2,1)S(1)}, u32[]{:S(2)}, u32[]{:S(2)}) collective-permute-start(bf16[512,256]{0,1:T(8,128)(2,1)S(1)} %fusion.39), channel_id=1, source_target_pairs={{0,16},{4,20},{8,24},{12,28},{16,0},{20,4},{24,8},{28,12},{1,17},{... | collective-permute-start | bytes 786440 | tf_op jit(solution)/shard_map/ppermute | solution.py:39
  46.3 16.9 %copy-start.10 = (bf16[256,256]{1,0:T(8,128)(2,1)S(1)}, bf16[256,256]{1,0:T(8,128)(2,1)}, u32[]{:S(2)}) copy-start(bf16[256,256]{1,0:T(8,128)(2,1)} %param.23) | copy-start | bytes 393220
  46.3 16.9 %copy-start.11 = (bf16[256,256]{1,0:T(8,128)(2,1)S(1)}, bf16[256,256]{1,0:T(8,128)(2,1)}, u32[]{:S(2)}) copy-start(bf16[256,256]{1,0:T(8,128)(2,1)} %param.22) | copy-start | bytes 393220
  56.2 6.4 %collective-permute-start.6 = (bf16[512,256]{0,1:T(8,128)(2,1)S(1)}, bf16[512,256]{0,1:T(8,128)(2,1)S(1)}, u32[]{:S(2)}, u32[]{:S(2)}) collective-permute-start(bf16[512,256]{0,1:T(8,128)(2,1)S(1)} %fusion.37), channel_id=1, source_target_pairs={{0,4},{4,0},{8,12},{12,8},{16,20},{20,16},{24,28},{28,24},{1,5},{5... | collective-permute-start | bytes 786440 | tf_op jit(solution)/shard_map/ppermute | solution.py:39
  57.8 11.2 %copy-start.8 = (s32[512]{0:T(512)S(1)}, s32[512]{0:T(512)}, u32[]{:S(2)}) copy-start(s32[512]{0:T(512)} %param.25) | copy-start | bytes 6148
  57.8 11.1 %collective-permute-start.9 = (bf16[1040,256]{1,0:T(8,128)(2,1)S(1)}, bf16[1040,256]{1,0:T(8,128)(2,1)S(1)}, u32[]{:S(2)}, u32[]{:S(2)}) collective-permute-start(bf16[1040,256]{1,0:T(8,128)(2,1)S(1)} %fusion.31), channel_id=1, source_target_pairs={{0,8},{4,12},{8,0},{12,4},{16,24},{20,28},{24,16},{28,20},{1,9},{5... | collective-permute-start | bytes 1597448 | tf_op jit(solution)/shard_map/ppermute | solution.py:100
  63.7 23.2 %copy-start.3 = (bf16[512,256]{1,0:T(8,128)(2,1)}, bf16[512,256]{1,0:T(8,128)(2,1)S(1)}, u32[]{:S(2)}) copy-start(bf16[512,256]{1,0:T(8,128)(2,1)S(1)} %convolution_convert_fusion.2) | copy-start | bytes 786436
  73.3 5.1 %collective-permute-start.10 = (f32[3,512]{1,0:T(4,128)S(1)}, f32[3,512]{1,0:T(4,128)S(1)}, u32[]{:S(2)}, u32[]{:S(2)}) collective-permute-start(f32[3,512]{1,0:T(4,128)S(1)} %pad_maximum_fusion.4), channel_id=1, source_target_pairs={{0,16},{4,20},{8,24},{12,28},{16,0},{20,4},{24,8},{28,12},{1,17},{... | collective-permute-start | bytes 18440 | tf_op jit(solution)/shard_map/ppermute | solution.py:39
  83.9 12.2 %collective-permute-start.12 = (bf16[512,256]{1,0:T(8,128)(2,1)S(1)}, bf16[512,256]{1,0:T(8,128)(2,1)S(1)}, u32[]{:S(2)}, u32[]{:S(2)}) collective-permute-start(bf16[512,256]{1,0:T(8,128)(2,1)S(1)} %convolution_convert_fusion.1), channel_id=1, source_target_pairs={{0,16},{4,20},{8,24},{12,28},{16,0},{20,4},{24,8},{28,12},{1,17},{... | collective-permute-start | bytes 786440 | tf_op jit(solution)/shard_map/ppermute | solution.py:58
  87.3 9.7 %collective-permute-start.11 = (f32[256,256]{1,0:T(8,128)S(1)}, f32[256,256]{1,0:T(8,128)S(1)}, u32[]{:S(2)}, u32[]{:S(2)}) collective-permute-start(f32[256,256]{1,0:T(8,128)S(1)} %slice_select_fusion), channel_id=1, source_target_pairs={{0,2},{2,0},{1,3},{3,1},{4,6},{6,4},{5,7},{7,5},{8,10},{10,8},{9,1... | collective-permute-start | bytes 786440 | tf_op jit(solution)/shard_map/ppermute | solution.py:89

commit v20 on v18

--- a/solution.py
+++ b/solution.py
@@ -108,6 +108,18 @@
         upper, jnp.concatenate([other_digits, digits]), jnp.concatenate([digits, other_digits])
     )
     return hits, digits
+
+
+def fetch_rows(hits, digits, mask):
+    count_rows, width = hits.shape
+    digit_rows = digits.T.reshape(2 * count_rows // width, width)
+    payload = jnp.concatenate(
+        [hits, jnp.pad(digit_rows, ((0, (-digit_rows.shape[0]) % 16), (0, 0)))]
+    )
+    count = lax.axis_size("phi")
+    other = lax.ppermute(payload, "phi", [(i, i ^ mask) for i in range(count)])
+    other_digits = other[count_rows : count_rows + digit_rows.shape[0]].reshape(2, count_rows).T
+    return other[:count_rows], other_digits
 
 
 def norm_rows(entries):
@@ -271,11 +283,15 @@
     mask_embed = jnp.dot(mask_hidden, mask_second, preferred_element_type=jnp.float32).astype(
         jnp.bfloat16
     )
-    pair_hits = group_hits
-    pair_digits = gathered[:, 3 * model_width : 3 * model_width + 2]
-    for distance in (1, 2):
-        pair_hits, pair_digits = partner_rows(pair_hits, pair_digits, distance)
-    pair_digits = pair_digits.astype(jnp.int32)
+    own_digits = gathered[:, 3 * model_width : 3 * model_width + 2]
+    pieces = [(group_hits, own_digits)] + [
+        fetch_rows(group_hits, own_digits, mask) for mask in (1, 2, 3)
+    ]
+    position = jnp.bitwise_xor(jnp.arange(4), lax.axis_index("phi") % 4)
+    pair_hits = jnp.take(jnp.stack([p[0] for p in pieces]), position, axis=0)
+    pair_digits = jnp.take(jnp.stack([p[1] for p in pieces]), position, axis=0)
+    pair_hits = pair_hits.reshape(-1, model_width)
+    pair_digits = pair_digits.reshape(-1, 2).astype(jnp.int32)
     pair_truth = pair_digits[:, 0] * 256 + pair_digits[:, 1] - 1
     logits = lax.dot_general(
         mask_embed, pair_hits, (((1,), (1,)), ((), ())), preferred_element_type=jnp.float32

time: 93.2 us -> 106 us (1.14)
  local copies, waits for them, and re-layouts: 3.42 us -> 12 us
  other arithmetic: 10.6 us -> 16.3 us
  starting transfers between devices: 24.5 us -> 19.3 us
  waiting for transfers between devices: 32.1 us -> 34.8 us
  matrix products: 16.8 us -> 18.6 us
  blocking collectives: 4.35 us -> 2.64 us
    ppermute x7, waiting for transfers between devices: 17.3 us -> 23.3 us  [butterfly(): other = lax.ppermute(tree, axis, partner_pairs(count, distance))]
    ppermute x2 -> x3, waiting for transfers between devices: 4.91 us -> 0.01 us  [fetch_rows(): other = lax.ppermute(payload, 'phi', [(i, i ^ mask) for i in range(count)])]
    ppermute x7, starting transfers between devices: 13.9 us -> 10 us  [butterfly(): other = lax.ppermute(tree, axis, partner_pairs(count, distance))]
    ppermute x1, waiting for transfers between devices: 8.16 us -> 11.5 us  [narrow_butterfly(): other = lax.ppermute(sent, axis, partner_pairs(count, distance))]
    another operation x0 -> x6, local copies, waits for them, and re-layouts: none -> 3.24 us  [the longest x4 2.98 us: body(): pair_hits = jnp.take(jnp.stack([p[0] for p in pieces]), position, axis=0)]
    ppermute x1, starting transfers between devices: 2.98 us -> 0.07 us  [narrow_butterfly(): other = lax.ppermute(sent, axis, partner_pairs(count, distance))]
    slice x7 -> x3, local copies, waits for them, and re-layouts: 0.25 us -> 2.03 us  [fetch_rows(): other[count_rows:count_rows + digit_rows.shape[0]].reshape(2, count_rows)]
    ppermute x1, waiting for transfers between devices: 1.72 us -> 0.01 us  [extended_2(): lax.ppermute(lax.slice_in_dim(block, block.shape[dim] - width, None, axis...]
  transfers between devices with their start and end apart: 13 -> 14, of which waited for: 9 -> 6; matrix products, arithmetic and copies ran while one was open for 10% -> 22% of each run, Pallas kernels for 0% -> 0%
where the time goes in v20:
time: 106 us; the launch traced here: 105 us
  waiting for transfers between devices  34.8 us (33%)
  starting transfers between devices  19.3 us (18%)
  matrix products  18.6 us (18%)
  other arithmetic  16.3 us (15%)
  local copies, waits for them, and re-layouts  12 us (11%)
  blocking collectives  2.64 us (2%)
  between operations  1.34 us (1%)
    ppermute x7, waiting for transfers between devices, butterfly(): other = lax.ppermute(tree, axis, partner_pairs(count, distance))  23.3 us
    ppermute x1, waiting for transfers between devices, narrow_butterfly(): other = lax.ppermute(sent, axis, partner_pairs(count, distance))  11.5 us
    ppermute x7, starting transfers between devices, butterfly(): other = lax.ppermute(tree, axis, partner_pairs(count, distance))  10 us
    ppermute x1, starting transfers between devices, extended_2(): lax.ppermute(lax.slice_in_dim(block, 0, width, axis=dim), axis, backward)  5.03 us
    dot_general x1, matrix products, body(): lax.dot_general(mask_embed, pair_hits, (((1,), (1,)), ((), ())), preferre...  4.2 us
    convert_element_type x1, other arithmetic, loss_coefficients(): (matched[:, None] * (sigma - target + dice_part) * model_width ** (-0.5))...  4.17 us
    ppermute x3, starting transfers between devices, fetch_rows(): other = lax.ppermute(payload, 'phi', [(i, i ^ mask) for i in range(count)])  3.55 us
    unnamed x25, local copies, waits for them, and re-layouts  2.99 us
  transfers between devices with their start and end apart: 14, of which 6 were waited for; matrix products, arithmetic and copies ran while one was open for 22% of the time, Pallas kernels for 0%

profile of v20, /device:TPU:0, one launch (start us, length us, event | category | flops | bytes accessed | tf_op | source)
XLA Modules:
  0.0 105.0 jit_solution(1390571753768402640)
XLA Ops:
  0.6 1.1 %copy.90 = bf16[256,256]{0,1:T(8,128)(2,1)S(1)} copy(bf16[256,256]{1,0:T(8,128)(2,1)} %param.13) | data formatting | bytes 262144 | tf_op args[0]
  1.9 1.3 %convolution_convert_fusion = bf16[256,768]{1,0:T(8,128)(2,1)S(1)} fusion(bf16[256,768]{1,0:T(8,128)(2,1)} %param.14, bf16[256,256]{0,1:T(8,128)(2,1)S(1)} %copy.90, f32[256]{0:T(256)S(1)} %add_rsqrt_fusion.3, f32[256]{0:T(256)S(1)} %broadcast_multiply_fusion.3), kind=kOutput, calls=%fused_computation.33 | convolution fusion | flops 101122048 | bytes 919552 | tf_op jit(solution)/shard_map/dot_general | solution.py:211
  3.7 5.0 %collective-permute-start.1 = (bf16[256,512]{1,0:T(8,128)(2,1)S(1)}, bf16[256,512]{1,0:T(8,128)(2,1)S(1)}, u32[]{:S(2)}, u32[]{:S(2)}) collective-permute-start(bf16[256,512]{1,0:T(8,128)(2,1)S(1)} %slice.97), channel_id=1, source_target_pairs={{2,0},{4,2},{6,4},{8,6},{10,8},{12,10},{14,12},{16,14},{18,16},{20... | collective-permute-start | bytes 786440 | tf_op jit(solution)/shard_map/ppermute | solution.py:19
  10.2 1.3 %fusion.130 = (f32[512]{0:T(512)}, pred[512]{0:T(512)(128)(4,1)}) fusion(s32[512]{0:T(512)} %param.25), kind=kLoop, calls=%fused_computation.230 | loop fusion | flops 1024 | bytes 4608 | tf_op jit(solution)/shard_map/convert_element_type | solution.py:301
  12.5 1.1 %copy.97 = bf16[512,256]{0,1:T(8,128)(2,1)S(1)} copy(bf16[512,256]{1,0:T(8,128)(2,1)} %param.18) | data formatting | bytes 524288 | tf_op args[5]
  13.6 1.2 %convolution_convert_fusion.4 = bf16[512,256]{0,1:T(8,128)(2,1)S(1)} fusion(bf16[512,256]{1,0:T(8,128)(2,1)} %param.18, bf16[256,256]{1,0:T(8,128)(2,1)} %param.19), kind=kOutput, calls=%fused_computation.39 | convolution fusion | flops 67239936 | bytes 655360 | tf_op jit(solution)/shard_map/dot_general | solution.py:249
  15.9 1.1 %fusion.135 = f32[8,128]{1,0:T(8,128)S(1)} fusion(pred[128,640]{1,0:T(8,128)(4,1)S(1)} %fusion.47, bf16[128,8,32]{0,2,1:T(8,128)(2,1)S(1)} %bitcast.216, bf16[640,8,32]{0,2,1:T(8,128)(2,1)S(1)} %bitcast.207), kind=kOutput, calls=%fused_computation.234 | convolution fusion | flops 44565120 | bytes 479232 | tf_op jit(solution)/shard_map/sub | solution.py:148
  17.0 1.3 %fusion.19 = bf16[8,32,128]{2,1,0:T(8,128)(2,1)S(1)} fusion(bf16[640,8,32]{0,2,1:T(8,128)(2,1)S(1)} %bitcast.209, f32[8,128]{1,0:T(8,128)S(1)} %fusion.135, pred[128,640]{1,0:T(8,128)(4,1)S(1)} %fusion.47, bf16[128,8,32]{0,2,1:T(8,128)(2,1)S(1)} %bitcast.217, bf16[640,8,32]{0,2,1:T(8,128)(2,1)S(1)} %bitcast.208), kind=kOutput, calls=%fused_computation.46 | convolution fusion | flops 87197312 | bytes 872448 | tf_op jit(solution)/shard_map/hqk,khd->qhd/dot_general | solution.py:150
  18.3 1.2 %fusion.134 = f32[8,128]{1,0:T(8,128)S(1)} fusion(pred[128,640]{1,0:T(8,128)(4,1)S(1)} %fusion.47, bf16[128,8,32]{0,2,1:T(8,128)(2,1)S(1)} %bitcast.214, bf16[640,8,32]{0,2,1:T(8,128)(2,1)S(1)} %bitcast.204), kind=kOutput, calls=%fused_computation.233 | convolution fusion | flops 44565120 | bytes 479232 | tf_op jit(solution)/shard_map/sub | solution.py:148
  19.5 1.3 %fusion.18 = bf16[8,32,128]{2,1,0:T(8,128)(2,1)S(1)} fusion(bf16[640,8,32]{0,2,1:T(8,128)(2,1)S(1)} %bitcast.206, f32[8,128]{1,0:T(8,128)S(1)} %fusion.134, pred[128,640]{1,0:T(8,128)(4,1)S(1)} %fusion.47, bf16[128,8,32]{0,2,1:T(8,128)(2,1)S(1)} %bitcast.215, bf16[640,8,32]{0,2,1:T(8,128)(2,1)S(1)} %bitcast.205), kind=kOutput, calls=%fused_computation.45 | convolution fusion | flops 87197312 | bytes 872448 | tf_op jit(solution)/shard_map/hqk,khd->qhd/dot_general | solution.py:150
  22.6 2.6 %all_gather.3 = bf16[512,896]{1,0:T(8,128)(2,1)S(1)} all-gather(bf16[256,896]{1,0:T(8,128)(2,1)S(1)} %fusion.44), channel_id=1, replica_groups=mesh['phi'=8,'query'=2,'event'=2] {'query'}, dimensions={0}, use_global_device_ids=true | all-gather | bytes 1376256 | tf_op jit(solution)/shard_map/all_gather | solution.py:242
  26.8 2.3 %collective-permute-start.8 = (bf16[528,256]{1,0:T(8,128)(2,1)S(1)}, bf16[528,256]{1,0:T(8,128)(2,1)}, u32[]{:S(2)}, u32[]{:S(2)}) collective-permute-start(bf16[528,256]{1,0:T(8,128)(2,1)S(1)} %fusion.56), channel_id=1, source_target_pairs={{0,4},{4,0},{8,12},{12,8},{16,20},{20,16},{24,28},{28,24},{1,5},{5... | collective-permute-start | bytes 811016 | tf_op jit(solution)/shard_map/ppermute | solution.py:120
  29.4 1.3 %multiply_reduce_fusion = (f32[8,512]{1,0:T(8,128)S(1)}, f32[8,512,512]{1,2,0:T(8,128)S(1)}) fusion(bf16[512,8,32]{0,2,1:T(8,128)(2,1)S(1)} %bitcast.195, bf16[512,8,32]{0,2,1:T(8,128)(2,1)S(1)} %bitcast.197), kind=kOutput, calls=%fused_computation.6 | convolution fusion | flops 138407936 | bytes 8929280 | tf_op jit(solution)/shard_map/qhd,khd->hqk/dot_general | solution.py:255
  30.7 1.4 %convert_reduce_fusion = f32[8,512]{1,0:T(8,128)S(1)} fusion(f32[8,512]{1,0:T(8,128)S(1)} %get-tuple-element.74, f32[8,512,512]{1,2,0:T(8,128)S(1)} %get-tuple-element.75), kind=kLoop, calls=%fused_computation.4 | loop fusion | flops 10481664 | bytes 8421376 | tf_op jit(solution)/shard_map/reduce_sum | solution.py:260
  32.5 1.5 %convolution_convert_fusion.3 = bf16[8,32,512]{2,1,0:T(8,128)(2,1)S(1)} fusion(bf16[512,8,32]{0,2,1:T(8,128)(2,1)S(1)} %bitcast.196, f32[8,512,512]{1,2,0:T(8,128)S(1)} %get-tuple-element.75, f32[8,512]{1,0:T(8,128)S(1)} %get-tuple-element.74), kind=kOutput, calls=%fused_computation.38 | convolution fusion | flops 140640256 | bytes 8929280 | tf_op jit(solution)/shard_map/hqk,khd->qhd/dot_general | solution.py:261
  34.0 1.7 %collective-permute-start.2 = (bf16[512,256]{0,1:T(8,128)(2,1)S(1)}, bf16[512,256]{0,1:T(8,128)(2,1)S(1)}, u32[]{:S(2)}, u32[]{:S(2)}) collective-permute-start(bf16[512,256]{0,1:T(8,128)(2,1)S(1)} %bitcast.198), channel_id=1, source_target_pairs={{0,8},{4,12},{8,0},{12,4},{16,24},{20,28},{24,16},{28,20},{1,9},{5... | collective-permute-start | bytes 786440 | tf_op jit(solution)/shard_map/ppermute | solution.py:39
  35.7 4.9 %collective-permute-done.3 = f32[2,8,512]{2,1,0:T(8,128)S(1)} collective-permute-done((f32[2,8,512]{2,1,0:T(8,128)S(1)}, f32[2,8,512]{2,1,0:T(8,128)S(1)}, u32[]{:S(2)}, u32[]{:S(2)}) %collective-permute-start.3) | collective-permute-done | bytes 32800 | tf_op jit(solution)/shard_map/ppermute | solution.py:39
  40.7 2.4 %collective-permute-start.5 = (f32[2,8,512]{2,1,0:T(8,128)S(1)}, f32[2,8,512]{2,1,0:T(8,128)S(1)}, u32[]{:S(2)}, u32[]{:S(2)}) collective-permute-start(f32[2,8,512]{2,1,0:T(8,128)S(1)} %pad_maximum_fusion.4), channel_id=1, source_target_pairs={{0,4},{4,0},{8,12},{12,8},{16,20},{20,16},{24,28},{28,24},{1,5},{5... | collective-permute-start | bytes 98312 | tf_op jit(solution)/shard_map/ppermute | solution.py:39
  43.0 1.9 %collective-permute-done.5 = f32[2,8,512]{2,1,0:T(8,128)S(1)} collective-permute-done((f32[2,8,512]{2,1,0:T(8,128)S(1)}, f32[2,8,512]{2,1,0:T(8,128)S(1)}, u32[]{:S(2)}, u32[]{:S(2)}) %collective-permute-start.5) | collective-permute-done | bytes 32800 | tf_op jit(solution)/shard_map/ppermute | solution.py:39
  45.0 2.0 %collective-permute-start.7 = (f32[2,8,512]{2,1,0:T(8,128)S(1)}, f32[2,8,512]{2,1,0:T(8,128)S(1)}, u32[]{:S(2)}, u32[]{:S(2)}) collective-permute-start(f32[2,8,512]{2,1,0:T(8,128)S(1)} %pad_maximum_fusion.5), channel_id=1, source_target_pairs={{0,16},{4,20},{8,24},{12,28},{16,0},{20,4},{24,8},{28,12},{1,17},{... | collective-permute-start | bytes 98312 | tf_op jit(solution)/shard_map/ppermute | solution.py:39
  47.6 2.3 %collective-permute-done.7 = f32[2,8,512]{2,1,0:T(8,128)S(1)} collective-permute-done((f32[2,8,512]{2,1,0:T(8,128)S(1)}, f32[2,8,512]{2,1,0:T(8,128)S(1)}, u32[]{:S(2)}, u32[]{:S(2)}) %collective-permute-start.7) | collective-permute-done | bytes 32800 | tf_op jit(solution)/shard_map/ppermute | solution.py:39
  50.6 2.2 %collective-permute-start.4 = (bf16[512,256]{0,1:T(8,128)(2,1)S(1)}, bf16[512,256]{0,1:T(8,128)(2,1)S(1)}, u32[]{:S(2)}, u32[]{:S(2)}) collective-permute-start(bf16[512,256]{0,1:T(8,128)(2,1)S(1)} %fusion.37), channel_id=1, source_target_pairs={{0,4},{4,0},{8,12},{12,8},{16,20},{20,16},{24,28},{28,24},{1,5},{5... | collective-permute-start | bytes 786440 | tf_op jit(solution)/shard_map/ppermute | solution.py:39
  55.9 1.0 slice_bitcast_fusion
  56.9 1.0 slice_bitcast_fusion.1
  60.4 1.1 %bitcast_select_fusion = bf16[2048,256]{1,0:T(8,128)(2,1)S(1)} fusion(bf16[4,512,256]{2,1,0:T(8,128)(2,1)S(1)} %gather_fusion, pred[2048]{0:T(1024)(128)(4,1)} %bitcast.220), kind=kLoop, calls=%fused_computation.56 | loop fusion | flops 524288 | bytes 2099200 | tf_op jit(solution)/shard_map/jit(_take)/select_n | solution.py:291
  63.1 1.3 %collective-permute-start.6 = (bf16[512,256]{0,1:T(8,128)(2,1)S(1)}, bf16[512,256]{0,1:T(8,128)(2,1)S(1)}, u32[]{:S(2)}, u32[]{:S(2)}) collective-permute-start(bf16[512,256]{0,1:T(8,128)(2,1)S(1)} %fusion.35), channel_id=1, source_target_pairs={{0,16},{4,20},{8,24},{12,28},{16,0},{20,4},{24,8},{28,12},{1,17},{... | collective-permute-start | bytes 786440 | tf_op jit(solution)/shard_map/ppermute | solution.py:39
  64.5 9.7 %collective-permute-done.6 = bf16[512,256]{0,1:T(8,128)(2,1)S(1)} collective-permute-done((bf16[512,256]{0,1:T(8,128)(2,1)S(1)}, bf16[512,256]{0,1:T(8,128)(2,1)S(1)}, u32[]{:S(2)}, u32[]{:S(2)}) %collective-permute-start.6) | collective-permute-done | bytes 262176 | tf_op jit(solution)/shard_map/ppermute | solution.py:39
  75.5 1.4 %convolution_convert_fusion.2 = bf16[512,256]{1,0:T(8,128)(2,1)S(1)} fusion(bf16[256,256]{1,0:T(8,128)(2,1)} %param.23, bf16[256,256]{1,0:T(8,128)(2,1)} %param.22, f32[512,256]{0,1:T(8,128)S(1)} %get-tuple-element.77, f32[512]{0:T(512)S(1)} %add_rsqrt_fusion, f32[512]{0:T(512)S(1)} %broadcast_multiply_fusion), kind=kOutput, calls=%fused_computation.37 | convolution fusion | flops 135004160 | bytes 1052672 | tf_op jit(solution)/shard_map/dot_general | solution.py:283
  77.0 4.2 %select_reduce_fusion = (f32[512]{0:T(512)S(1)}, f32[512]{0:T(512)S(1)}, f32[512]{0:T(512)S(1)}, f32[512,2048]{1,0:T(8,128)}) fusion(s32[2048]{0:T(1024)S(1)} %bitcast.218, s32[512]{0:T(512)} %param.25, pred[512]{0:T(512)(128)(4,1)} %get-tuple-element.34, bf16[512,256]{1,0:T(8,128)(2,1)S(1)} %convolution_convert_fusion.2, ...), kind=kOutput, calls=%fused_computation.13 | convolution fusion | flops 548403712 | bytes 5521920 | tf_op jit(solution)/shard_map/dot_general | solution.py:296
  81.3 4.5 %collective-permute-done.11 = f32[3,512]{1,0:T(4,128)S(1)} collective-permute-done((f32[3,512]{1,0:T(4,128)S(1)}, f32[3,512]{1,0:T(4,128)S(1)}, u32[]{:S(2)}, u32[]{:S(2)}) %collective-permute-start.11) | collective-permute-done | bytes 6176 | tf_op jit(solution)/shard_map/ppermute | solution.py:39
  86.4 4.2 %fusion.5 = bf16[512,2048]{1,0:T(8,128)(2,1)S(1)} fusion(f32[512,2048]{1,0:T(8,128)} %get-tuple-element.78, f32[512]{0:T(512)S(1)} %bitcast.222, f32[512]{0:T(512)S(1)} %bitcast.223, s32[2048]{0:T(1024)S(1)} %bitcast.219, f32[512]{0:T(512)S(1)} %copy-done.7, s32[512]{0:T(512)S(1)} %copy-done.6, pred[512]{0:T(512)(128)(4,1)S(1)} %copy-done.8), kind=kLoop, calls=%fused_computation.12 | loop fusion | flops 14680064 | bytes 6308352 | tf_op jit(solution)/shard_map/convert_element_type | solution.py:185
  91.9 11.5 %collective-permute-done.13 = bf16[512,256]{1,0:T(8,128)(2,1)S(1)} collective-permute-done((bf16[512,256]{1,0:T(8,128)(2,1)S(1)}, bf16[512,256]{1,0:T(8,128)(2,1)S(1)}, u32[]{:S(2)}, u32[]{:S(2)}) %collective-permute-start.13) | collective-permute-done | bytes 262176 | tf_op jit(solution)/shard_map/ppermute | solution.py:58
  (122 shorter events, 21.4 us)
Async XLA Ops:
  0.6 20.6 %copy-start = (bf16[1024,256]{1,0:T(8,128)(2,1)S(1)}, bf16[1024,256]{1,0:T(8,128)(2,1)}, u32[]{:S(2)}) copy-start(bf16[1024,256]{1,0:T(8,128)(2,1)} %param.17) | copy-start | bytes 1572868
  3.2 11.7 %collective-permute-start = (bf16[256,512]{1,0:T(8,128)(2,1)S(1)}, bf16[256,512]{1,0:T(8,128)(2,1)S(1)}, u32[]{:S(2)}, u32[]{:S(2)}) collective-permute-start(bf16[256,512]{1,0:T(8,128)(2,1)S(1)} %slice.97), channel_id=1, source_target_pairs={{0,2},{2,4},{4,6},{6,8},{8,10},{10,12},{12,14},{14,16},{16,18},{18... | collective-permute-start | bytes 786440 | tf_op jit(solution)/shard_map/ppermute | solution.py:16
  3.7 11.2 %collective-permute-start.1 = (bf16[256,512]{1,0:T(8,128)(2,1)S(1)}, bf16[256,512]{1,0:T(8,128)(2,1)S(1)}, u32[]{:S(2)}, u32[]{:S(2)}) collective-permute-start(bf16[256,512]{1,0:T(8,128)(2,1)S(1)} %slice.97), channel_id=1, source_target_pairs={{2,0},{4,2},{6,4},{8,6},{10,8},{12,10},{14,12},{16,14},{18,16},{20... | collective-permute-start | bytes 786440 | tf_op jit(solution)/shard_map/ppermute | solution.py:19
  19.5 1.4 %copy-start.4 = (bf16[256,256]{1,0:T(8,128)(2,1)S(1)}, bf16[256,256]{1,0:T(8,128)(2,1)}, u32[]{:S(2)}) copy-start(bf16[256,256]{1,0:T(8,128)(2,1)} %param.15) | copy-start | bytes 393220
  19.5 1.7 %copy-start.9 = (bf16[256,1024]{1,0:T(8,128)(2,1)S(1)}, bf16[256,1024]{1,0:T(8,128)(2,1)}, u32[]{:S(2)}) copy-start(bf16[256,1024]{1,0:T(8,128)(2,1)} %param.16) | copy-start | bytes 1572868
  20.9 1.4 %copy-start.3 = (bf16[256,512]{1,0:T(8,128)(2,1)S(1)}, bf16[256,512]{1,0:T(8,128)(2,1)}, u32[]{:S(2)}) copy-start(bf16[256,512]{1,0:T(8,128)(2,1)} %param.20) | copy-start | bytes 786436
  22.2 8.5 %copy-start.1 = (bf16[256,256]{1,0:T(8,128)(2,1)}, bf16[256,256]{1,0:T(8,128)(2,1)S(1)}, u32[]{:S(2)}) copy-start(bf16[256,256]{1,0:T(8,128)(2,1)S(1)} %copy.108) | copy-start | bytes 393220
  25.5 29.1 %collective-permute-start.10 = (bf16[528,256]{1,0:T(8,128)(2,1)S(1)}, bf16[528,256]{1,0:T(8,128)(2,1)}, u32[]{:S(2)}, u32[]{:S(2)}) collective-permute-start(bf16[528,256]{1,0:T(8,128)(2,1)S(1)} %fusion.56), channel_id=1, source_target_pairs={{0,12},{4,8},{8,4},{12,0},{16,28},{20,24},{24,20},{28,16},{1,13},{... | collective-permute-start | bytes 811016 | tf_op jit(solution)/shard_map/ppermute | solution.py:120
  25.9 27.8 %collective-permute-start.9 = (bf16[528,256]{1,0:T(8,128)(2,1)S(1)}, bf16[528,256]{1,0:T(8,128)(2,1)}, u32[]{:S(2)}, u32[]{:S(2)}) collective-permute-start(bf16[528,256]{1,0:T(8,128)(2,1)S(1)} %fusion.56), channel_id=1, source_target_pairs={{0,8},{4,12},{8,0},{12,4},{16,24},{20,28},{24,16},{28,20},{1,9},{5... | collective-permute-start | bytes 811016 | tf_op jit(solution)/shard_map/ppermute | solution.py:120
  26.8 26.0 %collective-permute-start.8 = (bf16[528,256]{1,0:T(8,128)(2,1)S(1)}, bf16[528,256]{1,0:T(8,128)(2,1)}, u32[]{:S(2)}, u32[]{:S(2)}) collective-permute-start(bf16[528,256]{1,0:T(8,128)(2,1)S(1)} %fusion.56), channel_id=1, source_target_pairs={{0,4},{4,0},{8,12},{12,8},{16,20},{20,16},{24,28},{28,24},{1,5},{5... | collective-permute-start | bytes 811016 | tf_op jit(solution)/shard_map/ppermute | solution.py:120
  32.1 8.5 %collective-permute-start.3 = (f32[2,8,512]{2,1,0:T(8,128)S(1)}, f32[2,8,512]{2,1,0:T(8,128)S(1)}, u32[]{:S(2)}, u32[]{:S(2)}) collective-permute-start(f32[2,8,512]{2,1,0:T(8,128)S(1)} %pad_maximum_fusion.3), channel_id=1, source_target_pairs={{0,8},{4,12},{8,0},{12,4},{16,24},{20,28},{24,16},{28,20},{1,9},{5... | collective-permute-start | bytes 98312 | tf_op jit(solution)/shard_map/ppermute | solution.py:39
  34.0 16.5 %collective-permute-start.2 = (bf16[512,256]{0,1:T(8,128)(2,1)S(1)}, bf16[512,256]{0,1:T(8,128)(2,1)S(1)}, u32[]{:S(2)}, u32[]{:S(2)}) collective-permute-start(bf16[512,256]{0,1:T(8,128)(2,1)S(1)} %bitcast.198), channel_id=1, source_target_pairs={{0,8},{4,12},{8,0},{12,4},{16,24},{20,28},{24,16},{28,20},{1,9},{5... | collective-permute-start | bytes 786440 | tf_op jit(solution)/shard_map/ppermute | solution.py:39
  40.7 4.2 %collective-permute-start.5 = (f32[2,8,512]{2,1,0:T(8,128)S(1)}, f32[2,8,512]{2,1,0:T(8,128)S(1)}, u32[]{:S(2)}, u32[]{:S(2)}) collective-permute-start(f32[2,8,512]{2,1,0:T(8,128)S(1)} %pad_maximum_fusion.4), channel_id=1, source_target_pairs={{0,4},{4,0},{8,12},{12,8},{16,20},{20,16},{24,28},{28,24},{1,5},{5... | collective-permute-start | bytes 98312 | tf_op jit(solution)/shard_map/ppermute | solution.py:39
  45.0 4.9 %collective-permute-start.7 = (f32[2,8,512]{2,1,0:T(8,128)S(1)}, f32[2,8,512]{2,1,0:T(8,128)S(1)}, u32[]{:S(2)}, u32[]{:S(2)}) collective-permute-start(f32[2,8,512]{2,1,0:T(8,128)S(1)} %pad_maximum_fusion.5), channel_id=1, source_target_pairs={{0,16},{4,20},{8,24},{12,28},{16,0},{20,4},{24,8},{28,12},{1,17},{... | collective-permute-start | bytes 98312 | tf_op jit(solution)/shard_map/ppermute | solution.py:39
  50.6 11.6 %collective-permute-start.4 = (bf16[512,256]{0,1:T(8,128)(2,1)S(1)}, bf16[512,256]{0,1:T(8,128)(2,1)S(1)}, u32[]{:S(2)}, u32[]{:S(2)}) collective-permute-start(bf16[512,256]{0,1:T(8,128)(2,1)S(1)} %fusion.37), channel_id=1, source_target_pairs={{0,4},{4,0},{8,12},{12,8},{16,20},{20,16},{24,28},{28,24},{1,5},{5... | collective-permute-start | bytes 786440 | tf_op jit(solution)/shard_map/ppermute | solution.py:39
  58.8 16.3 %copy-start.5 = (bf16[256,256]{1,0:T(8,128)(2,1)S(1)}, bf16[256,256]{1,0:T(8,128)(2,1)}, u32[]{:S(2)}) copy-start(bf16[256,256]{1,0:T(8,128)(2,1)} %param.21) | copy-start | bytes 393220
  63.1 11.1 %collective-permute-start.6 = (bf16[512,256]{0,1:T(8,128)(2,1)S(1)}, bf16[512,256]{0,1:T(8,128)(2,1)S(1)}, u32[]{:S(2)}, u32[]{:S(2)}) collective-permute-start(bf16[512,256]{0,1:T(8,128)(2,1)S(1)} %fusion.35), channel_id=1, source_target_pairs={{0,16},{4,20},{8,24},{12,28},{16,0},{20,4},{24,8},{28,12},{1,17},{... | collective-permute-start | bytes 786440 | tf_op jit(solution)/shard_map/ppermute | solution.py:39
  76.9 14.5 %copy-start.2 = (bf16[512,256]{1,0:T(8,128)(2,1)}, bf16[512,256]{1,0:T(8,128)(2,1)S(1)}, u32[]{:S(2)}) copy-start(bf16[512,256]{1,0:T(8,128)(2,1)S(1)} %convolution_convert_fusion.2) | copy-start | bytes 786436
  76.9 9.5 %copy-start.6 = (s32[512]{0:T(512)S(1)}, s32[512]{0:T(512)}, u32[]{:S(2)}) copy-start(s32[512]{0:T(512)} %param.25) | copy-start | bytes 6148
  76.9 9.5 %copy-start.7 = (f32[512]{0:T(512)S(1)}, f32[512]{0:T(512)}, u32[]{:S(2)}) copy-start(f32[512]{0:T(512)} %get-tuple-element.33) | copy-start | bytes 6148
  76.9 9.5 %copy-start.8 = (pred[512]{0:T(512)(128)(4,1)S(1)}, pred[512]{0:T(512)(128)(4,1)}, u32[]{:S(2)}) copy-start(pred[512]{0:T(512)(128)(4,1)} %get-tuple-element.34) | copy-start | bytes 1540
  81.2 4.6 %collective-permute-start.11 = (f32[3,512]{1,0:T(4,128)S(1)}, f32[3,512]{1,0:T(4,128)S(1)}, u32[]{:S(2)}, u32[]{:S(2)}) collective-permute-start(f32[3,512]{1,0:T(4,128)S(1)} %pad_maximum_fusion.6), channel_id=1, source_target_pairs={{0,16},{4,20},{8,24},{12,28},{16,0},{20,4},{24,8},{28,12},{1,17},{... | collective-permute-start | bytes 18440 | tf_op jit(solution)/shard_map/ppermute | solution.py:39
  91.3 12.0 %collective-permute-start.13 = (bf16[512,256]{1,0:T(8,128)(2,1)S(1)}, bf16[512,256]{1,0:T(8,128)(2,1)S(1)}, u32[]{:S(2)}, u32[]{:S(2)}) collective-permute-start(bf16[512,256]{1,0:T(8,128)(2,1)S(1)} %convolution_convert_fusion.1), channel_id=1, source_target_pairs={{0,16},{4,20},{8,24},{12,28},{16,0},{20,4},{24,8},{28,12},{1,17},{... | collective-permute-start | bytes 786440 | tf_op jit(solution)/shard_map/ppermute | solution.py:58
  91.8 12.4 %collective-permute-start.12 = (f32[256,256]{1,0:T(8,128)S(1)}, f32[256,256]{1,0:T(8,128)S(1)}, u32[]{:S(2)}, u32[]{:S(2)}) collective-permute-start(f32[256,256]{1,0:T(8,128)S(1)} %slice_select_fusion), channel_id=1, source_target_pairs={{0,2},{2,0},{1,3},{3,1},{4,6},{6,4},{5,7},{7,5},{8,10},{10,8},{9,1... | collective-permute-start | bytes 786440 | tf_op jit(solution)/shard_map/ppermute | solution.py:89

commit v21 on v18

--- a/solution.py
+++ b/solution.py
@@ -253,7 +253,6 @@
         (jnp.stack([local_max, local_total]), local_mixed.astype(jnp.bfloat16)),
         "phi",
         softmax_combine,
-        ordered=True,
         order="near_first",
     )
     mixed = mixed.astype(jnp.float32)

time: 93.2 us -> 106 us (1.14)
  waiting for transfers between devices: 32.1 us -> 49.8 us
  starting transfers between devices: 24.5 us -> 12.8 us
  matrix products: 16.8 us -> 21.1 us
  local copies, waits for them, and re-layouts: 3.42 us -> 6.94 us
    ppermute x7, waiting for transfers between devices: 17.3 us -> 37.2 us  [butterfly(): other = lax.ppermute(tree, axis, partner_pairs(count, distance))]
    ppermute x7, starting transfers between devices: 13.9 us -> 4.85 us  [butterfly(): other = lax.ppermute(tree, axis, partner_pairs(count, distance))]
    dot_general x1, matrix products: 1.52 us -> 4.93 us  [body(): jnp.einsum('hqk,khd->qhd', raised, value_heads, preferred_element_type=jn...]
    ppermute x1, starting transfers between devices: 2.98 us -> 0.07 us  [narrow_butterfly(): other = lax.ppermute(sent, axis, partner_pairs(count, distance))]
    ppermute x2, waiting for transfers between devices: 4.91 us -> 3.03 us  [partner_rows(): lax.ppermute(payload, 'phi', partner_pairs(lax.axis_size('phi'), distance))]
    unnamed x27, local copies, waits for them, and re-layouts: 1.42 us -> 3.22 us
    ppermute x1, waiting for transfers between devices: 8.16 us -> 6.92 us  [narrow_butterfly(): other = lax.ppermute(sent, axis, partner_pairs(count, distance))]
  transfers between devices with their start and end apart: 13 -> 13, of which waited for: 9 -> 10; matrix products, arithmetic and copies ran while one was open for 10% -> 10% of each run, Pallas kernels for 0% -> 0%
where the time goes in v21:
time: 106 us
  waiting for transfers between devices  49.8 us (47%)
  matrix products  21.1 us (20%)
  starting transfers between devices  12.8 us (12%)
  other arithmetic  9.77 us (9%)
  local copies, waits for them, and re-layouts  6.94 us (7%)
  blocking collectives  4.35 us (4%)
  between operations  1.23 us (1%)
    ppermute x7, waiting for transfers between devices, butterfly(): other = lax.ppermute(tree, axis, partner_pairs(count, distance))  37.2 us
    ppermute x1, waiting for transfers between devices, narrow_butterfly(): other = lax.ppermute(sent, axis, partner_pairs(count, distance))  6.92 us
    ppermute x1, starting transfers between devices, extended_2(): lax.ppermute(lax.slice_in_dim(block, 0, width, axis=dim), axis, backward)  5.03 us
    dot_general x1, matrix products, body(): jnp.einsum('hqk,khd->qhd', raised, value_heads, preferred_element_type=jn...  4.93 us
    ppermute x7, starting transfers between devices, butterfly(): other = lax.ppermute(tree, axis, partner_pairs(count, distance))  4.85 us
    all_gather x1, blocking collectives, body(): lax.all_gather(jnp.concatenate([local_kv, encoded, digits], axis=1), 'que...  4.35 us
    dot_general x1, matrix products, body(): lax.dot_general(mask_embed, pair_hits, (((1,), (1,)), ((), ())), preferre...  4.24 us
    convert_element_type x1, other arithmetic, loss_coefficients(): (matched[:, None] * (sigma - target + dice_part) * model_width ** (-0.5))...  4.17 us
  transfers between devices with their start and end apart: 13, of which 10 were waited for; matrix products, arithmetic and copies ran while one was open for 10% of the time, Pallas kernels for 0%

profile of v21, /device:TPU:0, one launch (start us, length us, event | category | flops | bytes accessed | tf_op | source)
XLA Modules:
  0.0 105.9 jit_solution(10723738054903249320)
XLA Ops:
  0.7 1.1 %copy.50 = bf16[256,256]{0,1:T(8,128)(2,1)S(1)} copy(bf16[256,256]{1,0:T(8,128)(2,1)} %param.13) | data formatting | bytes 262144 | tf_op args[0]
  1.9 1.3 %convolution_convert_fusion = bf16[256,768]{1,0:T(8,128)(2,1)S(1)} fusion(bf16[256,768]{1,0:T(8,128)(2,1)} %param.14, bf16[256,256]{0,1:T(8,128)(2,1)S(1)} %copy.50, f32[256]{0:T(256)S(1)} %add_rsqrt_fusion.3, f32[256]{0:T(256)S(1)} %broadcast_multiply_fusion.3), kind=kOutput, calls=%fused_computation.31 | convolution fusion | flops 101122048 | bytes 919552 | tf_op jit(solution)/shard_map/dot_general | solution.py:199
  3.7 5.0 %collective-permute-start.1 = (bf16[256,512]{1,0:T(8,128)(2,1)S(1)}, bf16[256,512]{1,0:T(8,128)(2,1)S(1)}, u32[]{:S(2)}, u32[]{:S(2)}) collective-permute-start(bf16[256,512]{1,0:T(8,128)(2,1)S(1)} %slice.85), channel_id=1, source_target_pairs={{2,0},{4,2},{6,4},{8,6},{10,8},{12,10},{14,12},{16,14},{18,16},{20... | collective-permute-start | bytes 786440 | tf_op jit(solution)/shard_map/ppermute | solution.py:19
  10.2 2.6 %collective-permute-done = bf16[256,512]{1,0:T(8,128)(2,1)S(1)} collective-permute-done((bf16[256,512]{1,0:T(8,128)(2,1)S(1)}, bf16[256,512]{1,0:T(8,128)(2,1)S(1)}, u32[]{:S(2)}, u32[]{:S(2)}) %collective-permute-start) | collective-permute-done | bytes 262176 | tf_op jit(solution)/shard_map/ppermute | solution.py:16
  13.8 1.1 %fusion.139 = f32[8,128]{1,0:T(8,128)S(1)} fusion(pred[128,640]{1,0:T(8,128)(4,1)S(1)} %fusion.49, bf16[128,8,32]{0,2,1:T(8,128)(2,1)S(1)} %bitcast.199, bf16[640,8,32]{0,2,1:T(8,128)(2,1)S(1)} %bitcast.190), kind=kOutput, calls=%fused_computation.221 | convolution fusion | flops 44565120 | bytes 479232 | tf_op jit(solution)/shard_map/sub | solution.py:136
  15.0 1.3 %fusion.19 = bf16[8,32,128]{2,1,0:T(8,128)(2,1)S(1)} fusion(bf16[640,8,32]{0,2,1:T(8,128)(2,1)S(1)} %bitcast.192, f32[8,128]{1,0:T(8,128)S(1)} %fusion.139, pred[128,640]{1,0:T(8,128)(4,1)S(1)} %fusion.49, bf16[128,8,32]{0,2,1:T(8,128)(2,1)S(1)} %bitcast.200, bf16[640,8,32]{0,2,1:T(8,128)(2,1)S(1)} %bitcast.191), kind=kOutput, calls=%fused_computation.44 | convolution fusion | flops 87197312 | bytes 872448 | tf_op jit(solution)/shard_map/hqk,khd->qhd/dot_general | solution.py:138
  16.3 1.2 %fusion.138 = f32[8,128]{1,0:T(8,128)S(1)} fusion(pred[128,640]{1,0:T(8,128)(4,1)S(1)} %fusion.49, bf16[128,8,32]{0,2,1:T(8,128)(2,1)S(1)} %bitcast.197, bf16[640,8,32]{0,2,1:T(8,128)(2,1)S(1)} %bitcast.187), kind=kOutput, calls=%fused_computation.220 | convolution fusion | flops 44565120 | bytes 479232 | tf_op jit(solution)/shard_map/sub | solution.py:136
  17.5 1.3 %fusion.18 = bf16[8,32,128]{2,1,0:T(8,128)(2,1)S(1)} fusion(bf16[640,8,32]{0,2,1:T(8,128)(2,1)S(1)} %bitcast.189, f32[8,128]{1,0:T(8,128)S(1)} %fusion.138, pred[128,640]{1,0:T(8,128)(4,1)S(1)} %fusion.49, bf16[128,8,32]{0,2,1:T(8,128)(2,1)S(1)} %bitcast.198, bf16[640,8,32]{0,2,1:T(8,128)(2,1)S(1)} %bitcast.188), kind=kOutput, calls=%fused_computation.43 | convolution fusion | flops 87197312 | bytes 872448 | tf_op jit(solution)/shard_map/hqk,khd->qhd/dot_general | solution.py:138
  19.2 0.8 convert_reduce_fusion.3
  20.6 4.3 %all_gather.3 = bf16[512,896]{1,0:T(8,128)(2,1)S(1)} all-gather(bf16[256,896]{1,0:T(8,128)(2,1)S(1)} %fusion.46), channel_id=1, replica_groups=mesh['phi'=8,'query'=2,'event'=2] {'query'}, dimensions={0}, use_global_device_ids=true | all-gather | bytes 1376256 | tf_op jit(solution)/shard_map/all_gather | solution.py:230
  25.1 1.3 %multiply_reduce_fusion = (f32[8,512]{1,0:T(8,128)S(1)}, f32[8,512,512]{1,2,0:T(8,128)S(1)}) fusion(bf16[512,8,32]{0,2,1:T(8,128)(2,1)S(1)} %bitcast.183, bf16[512,8,32]{0,2,1:T(8,128)(2,1)S(1)} %bitcast.185), kind=kOutput, calls=%fused_computation.4 | convolution fusion | flops 138407936 | bytes 8929280 | tf_op jit(solution)/shard_map/qhd,khd->hqk/dot_general | solution.py:243
  26.5 1.4 %convert_reduce_fusion = f32[8,512]{1,0:T(8,128)S(1)} fusion(f32[8,512]{1,0:T(8,128)S(1)} %get-tuple-element.58, f32[8,512,512]{1,2,0:T(8,128)S(1)} %get-tuple-element.59), kind=kLoop, calls=%fused_computation.2 | loop fusion | flops 10481664 | bytes 8421376 | tf_op jit(solution)/shard_map/reduce_sum | solution.py:248
  27.9 1.8 %copy-done.1 = f32[8,512,512]{1,2,0:T(8,128)} copy-done((f32[8,512,512]{1,2,0:T(8,128)}, f32[8,512,512]{1,2,0:T(8,128)S(1)}, u32[]{:S(2)}) %copy-start.1) | copy-done | bytes 8388632
  30.4 3.2 %collective-permute-done.2 = f32[2,8,512]{2,1,0:T(8,128)S(1)} collective-permute-done((f32[2,8,512]{2,1,0:T(8,128)S(1)}, f32[2,8,512]{2,1,0:T(8,128)S(1)}, u32[]{:S(2)}, u32[]{:S(2)}) %collective-permute-start.2) | collective-permute-done | bytes 32800 | tf_op jit(solution)/shard_map/ppermute | solution.py:39
  33.9 3.7 %collective-permute-done.4 = f32[2,8,512]{2,1,0:T(8,128)S(1)} collective-permute-done((f32[2,8,512]{2,1,0:T(8,128)S(1)}, f32[2,8,512]{2,1,0:T(8,128)S(1)}, u32[]{:S(2)}, u32[]{:S(2)}) %collective-permute-start.4) | collective-permute-done | bytes 32800 | tf_op jit(solution)/shard_map/ppermute | solution.py:39
  37.6 1.8 %collective-permute-start.6 = (f32[2,8,512]{2,1,0:T(8,128)S(1)}, f32[2,8,512]{2,1,0:T(8,128)S(1)}, u32[]{:S(2)}, u32[]{:S(2)}) collective-permute-start(f32[2,8,512]{2,1,0:T(8,128)S(1)} %pad_maximum_fusion.3), channel_id=1, source_target_pairs={{0,16},{4,20},{8,24},{12,28},{16,0},{20,4},{24,8},{28,12},{1,17},{... | collective-permute-start | bytes 98312 | tf_op jit(solution)/shard_map/ppermute | solution.py:39
  40.4 2.5 %collective-permute-done.6 = f32[2,8,512]{2,1,0:T(8,128)S(1)} collective-permute-done((f32[2,8,512]{2,1,0:T(8,128)S(1)}, f32[2,8,512]{2,1,0:T(8,128)S(1)}, u32[]{:S(2)}, u32[]{:S(2)}) %collective-permute-start.6) | collective-permute-done | bytes 32800 | tf_op jit(solution)/shard_map/ppermute | solution.py:39
  42.9 3.0 %collective-permute-done.8 = bf16[528,256]{1,0:T(8,128)(2,1)S(1)} collective-permute-done((bf16[528,256]{1,0:T(8,128)(2,1)S(1)}, bf16[528,256]{1,0:T(8,128)(2,1)S(1)}, u32[]{:S(2)}, u32[]{:S(2)}) %collective-permute-start.8) | collective-permute-done | bytes 270368 | tf_op jit(solution)/shard_map/ppermute | solution.py:100
  46.3 1.6 %collective-permute-start.9 = (bf16[1040,256]{1,0:T(8,128)(2,1)S(1)}, bf16[1040,256]{1,0:T(8,128)(2,1)}, u32[]{:S(2)}, u32[]{:S(2)}) collective-permute-start(bf16[1040,256]{1,0:T(8,128)(2,1)S(1)} %fusion.31), channel_id=1, source_target_pairs={{0,8},{4,12},{8,0},{12,4},{16,24},{20,28},{24,16},{28,20},{1,9},{5... | collective-permute-start | bytes 1597448 | tf_op jit(solution)/shard_map/ppermute | solution.py:100
  48.0 4.9 %convert_multiply_fusion = (f32[512,8,32]{0,2,1:T(8,128)S(1)}, bf16[8,32,512]{2,1,0:T(8,128)(2,1)S(1)}) fusion(f32[512,8]{0,1:T(8,128)S(1)} %get-tuple-element.49, bf16[512,8,32]{0,2,1:T(8,128)(2,1)S(1)} %bitcast.184, f32[8,512,512]{1,2,0:T(8,128)} %copy-done.1, f32[8,512]{1,0:T(8,128)S(1)} %get-tuple-element.58), kind=kOutput, calls=%fused_computation.81 | convolution fusion | flops 140902400 | bytes 9469952 | tf_op jit(solution)/shard_map/hqk,khd->qhd/dot_general | solution.py:249
  53.4 9.5 %collective-permute-done.3 = bf16[512,256]{0,1:T(8,128)(2,1)S(1)} collective-permute-done((bf16[512,256]{0,1:T(8,128)(2,1)S(1)}, bf16[512,256]{0,1:T(8,128)(2,1)S(1)}, u32[]{:S(2)}, u32[]{:S(2)}) %collective-permute-start.3) | collective-permute-done | bytes 262176 | tf_op jit(solution)/shard_map/ppermute | solution.py:39
  63.6 5.9 %collective-permute-done.5 = bf16[512,256]{0,1:T(8,128)(2,1)S(1)} collective-permute-done((bf16[512,256]{0,1:T(8,128)(2,1)S(1)}, bf16[512,256]{0,1:T(8,128)(2,1)S(1)}, u32[]{:S(2)}, u32[]{:S(2)}) %collective-permute-start.5) | collective-permute-done | bytes 262176 | tf_op jit(solution)/shard_map/ppermute | solution.py:39
  69.6 1.3 %collective-permute-start.7 = (bf16[512,256]{0,1:T(8,128)(2,1)S(1)}, bf16[512,256]{0,1:T(8,128)(2,1)S(1)}, u32[]{:S(2)}, u32[]{:S(2)}) collective-permute-start(bf16[512,256]{0,1:T(8,128)(2,1)S(1)} %fusion.37), channel_id=1, source_target_pairs={{0,16},{4,20},{8,24},{12,28},{16,0},{20,4},{24,8},{28,12},{1,17},{... | collective-permute-start | bytes 786440 | tf_op jit(solution)/shard_map/ppermute | solution.py:39
  71.6 1.1 %slice.98 = bf16[1024,256]{1,0:T(8,128)(2,1)S(1)} slice(bf16[1040,256]{1,0:T(8,128)(2,1)} %collective-permute-done.9), slice={[0:1024], [0:256]} | slice | bytes 1048576 | tf_op jit(solution)/shard_map/slice | solution.py:101
  72.7 7.0 %collective-permute-done.7 = bf16[512,256]{0,1:T(8,128)(2,1)S(1)} collective-permute-done((bf16[512,256]{0,1:T(8,128)(2,1)S(1)}, bf16[512,256]{0,1:T(8,128)(2,1)S(1)}, u32[]{:S(2)}, u32[]{:S(2)}) %collective-permute-start.7) | collective-permute-done | bytes 262176 | tf_op jit(solution)/shard_map/ppermute | solution.py:39
  80.2 1.3 %convolution_convert_fusion.2 = bf16[512,256]{1,0:T(8,128)(2,1)S(1)} fusion(bf16[256,256]{1,0:T(8,128)(2,1)S(1)} %copy-done.11, bf16[256,256]{1,0:T(8,128)(2,1)} %param.22, f32[512,256]{0,1:T(8,128)S(1)} %get-tuple-element.63, f32[512]{0:T(512)S(1)} %add_rsqrt_fusion, f32[512]{0:T(512)S(1)} %broadcast_multiply_fusion), kind=kOutput, calls=%fused_computation.35 | convolution fusion | flops 135004160 | bytes 1052672 | tf_op jit(solution)/shard_map/dot_general | solution.py:270
  81.6 4.2 %select_reduce_fusion = (f32[512]{0:T(512)S(1)}, f32[512]{0:T(512)S(1)}, f32[512]{0:T(512)S(1)}, f32[512,2048]{1,0:T(8,128)}) fusion(s32[2048]{0:T(1024)S(1)} %bitcast.202, s32[512]{0:T(512)S(1)} %copy-done.9, pred[512]{0:T(512)(128)(4,1)S(1)} %get-tuple-element.24, bf16[512,256]{1,0:T(8,128)(2,1)S(1)} %convolution_convert_fusion.2, ...), kind=kOutput, calls=%fused_computation.11 | convolution fusion | flops 553122304 | bytes 5521921 | tf_op jit(solution)/shard_map/dot_general | solution.py:279
  86.0 5.3 %collective-permute-done.10 = f32[3,512]{1,0:T(4,128)S(1)} collective-permute-done((f32[3,512]{1,0:T(4,128)S(1)}, f32[3,512]{1,0:T(4,128)S(1)}, u32[]{:S(2)}, u32[]{:S(2)}) %collective-permute-start.10) | collective-permute-done | bytes 6176 | tf_op jit(solution)/shard_map/ppermute | solution.py:39
  91.9 4.2 %fusion.5 = bf16[512,2048]{1,0:T(8,128)(2,1)S(1)} fusion(f32[512,2048]{1,0:T(8,128)} %get-tuple-element.64, f32[512]{0:T(512)S(1)} %bitcast.205, f32[512]{0:T(512)S(1)} %bitcast.206, s32[2048]{0:T(1024)S(1)} %bitcast.203, f32[512]{0:T(512)S(1)} %get-tuple-element.23, s32[512]{0:T(512)S(1)} %copy-done.9, pred[512]{0:T(512)(128)(4,1)S(1)} %get-tuple-element.24), kind=kLoop, calls=%fused_computation.10 | loop fusion | flops 14680064 | bytes 6308352 | tf_op jit(solution)/shard_map/convert_element_type | solution.py:173
  96.1 0.8 convolution_convert_fusion.1
  97.4 6.9 %collective-permute-done.12 = bf16[512,256]{1,0:T(8,128)(2,1)S(1)} collective-permute-done((bf16[512,256]{1,0:T(8,128)(2,1)S(1)}, bf16[512,256]{1,0:T(8,128)(2,1)S(1)}, u32[]{:S(2)}, u32[]{:S(2)}) %collective-permute-start.12) | collective-permute-done | bytes 262176 | tf_op jit(solution)/shard_map/ppermute | solution.py:58
  104.3 0.9 convert_add_fusion
  (108 shorter events, 10.8 us)
Async XLA Ops:
  0.6 18.6 %copy-start = (bf16[1024,256]{1,0:T(8,128)(2,1)S(1)}, bf16[1024,256]{1,0:T(8,128)(2,1)}, u32[]{:S(2)}) copy-start(bf16[1024,256]{1,0:T(8,128)(2,1)} %param.17) | copy-start | bytes 1572868
  0.6 9.3 %copy-start.2 = (bf16[512,256]{1,0:T(8,128)(2,1)S(1)}, bf16[512,256]{1,0:T(8,128)(2,1)}, u32[]{:S(2)}) copy-start(bf16[512,256]{1,0:T(8,128)(2,1)} %param.18) | copy-start | bytes 786436
  0.7 9.3 %copy-start.6 = (bf16[256,256]{1,0:T(8,128)(2,1)S(1)}, bf16[256,256]{1,0:T(8,128)(2,1)}, u32[]{:S(2)}) copy-start(bf16[256,256]{1,0:T(8,128)(2,1)} %param.19) | copy-start | bytes 393220
  3.2 9.6 %collective-permute-start = (bf16[256,512]{1,0:T(8,128)(2,1)S(1)}, bf16[256,512]{1,0:T(8,128)(2,1)S(1)}, u32[]{:S(2)}, u32[]{:S(2)}) collective-permute-start(bf16[256,512]{1,0:T(8,128)(2,1)S(1)} %slice.85), channel_id=1, source_target_pairs={{0,2},{2,4},{4,6},{6,8},{8,10},{10,12},{12,14},{14,16},{16,18},{18... | collective-permute-start | bytes 786440 | tf_op jit(solution)/shard_map/ppermute | solution.py:16
  3.7 9.1 %collective-permute-start.1 = (bf16[256,512]{1,0:T(8,128)(2,1)S(1)}, bf16[256,512]{1,0:T(8,128)(2,1)S(1)}, u32[]{:S(2)}, u32[]{:S(2)}) collective-permute-start(bf16[256,512]{1,0:T(8,128)(2,1)S(1)} %slice.85), channel_id=1, source_target_pairs={{2,0},{4,2},{6,4},{8,6},{10,8},{12,10},{14,12},{16,14},{18,16},{20... | collective-permute-start | bytes 786440 | tf_op jit(solution)/shard_map/ppermute | solution.py:19
  17.5 1.4 %copy-start.7 = (bf16[256,256]{1,0:T(8,128)(2,1)S(1)}, bf16[256,256]{1,0:T(8,128)(2,1)}, u32[]{:S(2)}) copy-start(bf16[256,256]{1,0:T(8,128)(2,1)} %param.15) | copy-start | bytes 393220
  17.5 1.7 %copy-start.10 = (bf16[256,1024]{1,0:T(8,128)(2,1)S(1)}, bf16[256,1024]{1,0:T(8,128)(2,1)}, u32[]{:S(2)}) copy-start(bf16[256,1024]{1,0:T(8,128)(2,1)} %param.16) | copy-start | bytes 1572868
  18.8 1.4 %copy-start.5 = (bf16[256,512]{1,0:T(8,128)(2,1)S(1)}, bf16[256,512]{1,0:T(8,128)(2,1)}, u32[]{:S(2)}) copy-start(bf16[256,512]{1,0:T(8,128)(2,1)} %param.20) | copy-start | bytes 786436
  20.2 6.3 %copy-start.3 = (bf16[256,256]{1,0:T(8,128)(2,1)}, bf16[256,256]{1,0:T(8,128)(2,1)S(1)}, u32[]{:S(2)}) copy-start(bf16[256,256]{1,0:T(8,128)(2,1)S(1)} %copy.66) | copy-start | bytes 393220
  26.5 3.2 %copy-start.1 = (f32[8,512,512]{1,2,0:T(8,128)}, f32[8,512,512]{1,2,0:T(8,128)S(1)}, u32[]{:S(2)}) copy-start(f32[8,512,512]{1,2,0:T(8,128)S(1)} %get-tuple-element.59) | copy-start | bytes 25165828
  29.7 3.9 %collective-permute-start.2 = (f32[2,8,512]{2,1,0:T(8,128)S(1)}, f32[2,8,512]{2,1,0:T(8,128)S(1)}, u32[]{:S(2)}, u32[]{:S(2)}) collective-permute-start(f32[2,8,512]{2,1,0:T(8,128)S(1)} %pad_maximum_fusion.1), channel_id=1, source_target_pairs={{0,8},{4,12},{8,0},{12,4},{16,24},{20,28},{24,16},{28,20},{1,9},{5... | collective-permute-start | bytes 98312 | tf_op jit(solution)/shard_map/ppermute | solution.py:39
  33.6 4.0 %collective-permute-start.4 = (f32[2,8,512]{2,1,0:T(8,128)S(1)}, f32[2,8,512]{2,1,0:T(8,128)S(1)}, u32[]{:S(2)}, u32[]{:S(2)}) collective-permute-start(f32[2,8,512]{2,1,0:T(8,128)S(1)} %pad_maximum_fusion.2), channel_id=1, source_target_pairs={{0,4},{4,0},{8,12},{12,8},{16,20},{20,16},{24,28},{28,24},{1,5},{5... | collective-permute-start | bytes 98312 | tf_op jit(solution)/shard_map/ppermute | solution.py:39
  37.6 5.2 %collective-permute-start.6 = (f32[2,8,512]{2,1,0:T(8,128)S(1)}, f32[2,8,512]{2,1,0:T(8,128)S(1)}, u32[]{:S(2)}, u32[]{:S(2)}) collective-permute-start(f32[2,8,512]{2,1,0:T(8,128)S(1)} %pad_maximum_fusion.3), channel_id=1, source_target_pairs={{0,16},{4,20},{8,24},{12,28},{16,0},{20,4},{24,8},{28,12},{1,17},{... | collective-permute-start | bytes 98312 | tf_op jit(solution)/shard_map/ppermute | solution.py:39
  39.4 6.5 %collective-permute-start.8 = (bf16[528,256]{1,0:T(8,128)(2,1)S(1)}, bf16[528,256]{1,0:T(8,128)(2,1)S(1)}, u32[]{:S(2)}, u32[]{:S(2)}) collective-permute-start(bf16[528,256]{1,0:T(8,128)(2,1)S(1)} %fusion.58), channel_id=1, source_target_pairs={{0,4},{4,0},{8,12},{12,8},{16,20},{20,16},{24,28},{28,24},{1,5},{5... | collective-permute-start | bytes 811016 | tf_op jit(solution)/shard_map/ppermute | solution.py:100
  46.3 24.5 %collective-permute-start.9 = (bf16[1040,256]{1,0:T(8,128)(2,1)S(1)}, bf16[1040,256]{1,0:T(8,128)(2,1)}, u32[]{:S(2)}, u32[]{:S(2)}) collective-permute-start(bf16[1040,256]{1,0:T(8,128)(2,1)S(1)} %fusion.31), channel_id=1, source_target_pairs={{0,8},{4,12},{8,0},{12,4},{16,24},{20,28},{24,16},{28,20},{1,9},{5... | collective-permute-start | bytes 1597448 | tf_op jit(solution)/shard_map/ppermute | solution.py:100
  48.0 15.6 %copy-start.9 = (s32[512]{0:T(512)S(1)}, s32[512]{0:T(512)}, u32[]{:S(2)}) copy-start(s32[512]{0:T(512)} %param.25) | copy-start | bytes 6148
  52.9 26.9 %copy-start.8 = (bf16[256,256]{1,0:T(8,128)(2,1)S(1)}, bf16[256,256]{1,0:T(8,128)(2,1)}, u32[]{:S(2)}) copy-start(bf16[256,256]{1,0:T(8,128)(2,1)} %param.21) | copy-start | bytes 393220
  52.9 10.0 %collective-permute-start.3 = (bf16[512,256]{0,1:T(8,128)(2,1)S(1)}, bf16[512,256]{0,1:T(8,128)(2,1)S(1)}, u32[]{:S(2)}, u32[]{:S(2)}) collective-permute-start(bf16[512,256]{0,1:T(8,128)(2,1)S(1)} %bitcast.194), channel_id=1, source_target_pairs={{0,8},{4,12},{8,0},{12,4},{16,24},{20,28},{24,16},{28,20},{1,9},{5... | collective-permute-start | bytes 786440 | tf_op jit(solution)/shard_map/ppermute | solution.py:39
  63.0 17.2 %copy-start.11 = (bf16[256,256]{1,0:T(8,128)(2,1)S(1)}, bf16[256,256]{1,0:T(8,128)(2,1)}, u32[]{:S(2)}) copy-start(bf16[256,256]{1,0:T(8,128)(2,1)} %param.23) | copy-start | bytes 393220
  63.0 6.4 %collective-permute-start.5 = (bf16[512,256]{0,1:T(8,128)(2,1)S(1)}, bf16[512,256]{0,1:T(8,128)(2,1)S(1)}, u32[]{:S(2)}, u32[]{:S(2)}) collective-permute-start(bf16[512,256]{0,1:T(8,128)(2,1)S(1)} %fusion.39), channel_id=1, source_target_pairs={{0,4},{4,0},{8,12},{12,8},{16,20},{20,16},{24,28},{28,24},{1,5},{5... | collective-permute-start | bytes 786440 | tf_op jit(solution)/shard_map/ppermute | solution.py:39
  69.6 10.1 %collective-permute-start.7 = (bf16[512,256]{0,1:T(8,128)(2,1)S(1)}, bf16[512,256]{0,1:T(8,128)(2,1)S(1)}, u32[]{:S(2)}, u32[]{:S(2)}) collective-permute-start(bf16[512,256]{0,1:T(8,128)(2,1)S(1)} %fusion.37), channel_id=1, source_target_pairs={{0,16},{4,20},{8,24},{12,28},{16,0},{20,4},{24,8},{28,12},{1,17},{... | collective-permute-start | bytes 786440 | tf_op jit(solution)/shard_map/ppermute | solution.py:39
  81.6 15.3 %copy-start.4 = (bf16[512,256]{1,0:T(8,128)(2,1)}, bf16[512,256]{1,0:T(8,128)(2,1)S(1)}, u32[]{:S(2)}) copy-start(bf16[512,256]{1,0:T(8,128)(2,1)S(1)} %convolution_convert_fusion.2) | copy-start | bytes 786436
  85.9 5.4 %collective-permute-start.10 = (f32[3,512]{1,0:T(4,128)S(1)}, f32[3,512]{1,0:T(4,128)S(1)}, u32[]{:S(2)}, u32[]{:S(2)}) collective-permute-start(f32[3,512]{1,0:T(4,128)S(1)} %pad_maximum_fusion.4), channel_id=1, source_target_pairs={{0,16},{4,20},{8,24},{12,28},{16,0},{20,4},{24,8},{28,12},{1,17},{... | collective-permute-start | bytes 18440 | tf_op jit(solution)/shard_map/ppermute | solution.py:39
  96.8 7.5 %collective-permute-start.12 = (bf16[512,256]{1,0:T(8,128)(2,1)S(1)}, bf16[512,256]{1,0:T(8,128)(2,1)S(1)}, u32[]{:S(2)}, u32[]{:S(2)}) collective-permute-start(bf16[512,256]{1,0:T(8,128)(2,1)S(1)} %convolution_convert_fusion.1), channel_id=1, source_target_pairs={{0,16},{4,20},{8,24},{12,28},{16,0},{20,4},{24,8},{28,12},{1,17},{... | collective-permute-start | bytes 786440 | tf_op jit(solution)/shard_map/ppermute | solution.py:58
  97.3 7.9 %collective-permute-start.11 = (f32[256,256]{1,0:T(8,128)S(1)}, f32[256,256]{1,0:T(8,128)S(1)}, u32[]{:S(2)}, u32[]{:S(2)}) collective-permute-start(f32[256,256]{1,0:T(8,128)S(1)} %slice_select_fusion), channel_id=1, source_target_pairs={{0,2},{2,0},{1,3},{3,1},{4,6},{6,4},{5,7},{7,5},{8,10},{10,8},{9,1... | collective-permute-start | bytes 786440 | tf_op jit(solution)/shard_map/ppermute | solution.py:89

commit v22 on v18

--- a/solution.py
+++ b/solution.py
@@ -273,7 +273,7 @@
     )
     pair_hits = group_hits
     pair_digits = gathered[:, 3 * model_width : 3 * model_width + 2]
-    for distance in (1, 2):
+    for distance in (2, 1):
         pair_hits, pair_digits = partner_rows(pair_hits, pair_digits, distance)
     pair_digits = pair_digits.astype(jnp.int32)
     pair_truth = pair_digits[:, 0] * 256 + pair_digits[:, 1] - 1
@@ -303,7 +303,10 @@
     )
     group_count = group_hits.shape[0]
     own_coef = lax.dynamic_slice_in_dim(
-        coef, (lax.axis_index("phi") % 4) * group_count, group_count, axis=1
+        coef,
+        ((lax.axis_index("phi") % 2) * 2 + (lax.axis_index("phi") // 2) % 2) * group_count,
+        group_count,
+        axis=1,
     )
     hit_grad = reduce_scatter_rows(
         lax.dot_general(

time: 93.2 us -> 90.7 us (0.973)
  starting transfers between devices: 24.5 us -> 14.7 us
  waiting for transfers between devices: 32.1 us -> 39.3 us
    ppermute x7, waiting for transfers between devices: 17.3 us -> 27.6 us  [butterfly(): other = lax.ppermute(tree, axis, partner_pairs(count, distance))]
    ppermute x7, starting transfers between devices: 13.9 us -> 6.55 us  [butterfly(): other = lax.ppermute(tree, axis, partner_pairs(count, distance))]
    ppermute x2, waiting for transfers between devices: 4.91 us -> 0.01 us  [partner_rows(): lax.ppermute(payload, 'phi', partner_pairs(lax.axis_size('phi'), distance))]
    ppermute x1, starting transfers between devices: 2.98 us -> 1.08 us  [narrow_butterfly(): other = lax.ppermute(sent, axis, partner_pairs(count, distance))]
    ppermute x1, waiting for transfers between devices: 8.16 us -> 9.9 us  [narrow_butterfly(): other = lax.ppermute(sent, axis, partner_pairs(count, distance))]
  transfers between devices with their start and end apart: 13 -> 13, of which waited for: 9 -> 8; matrix products, arithmetic and copies ran while one was open for 10% -> 11% of each run, Pallas kernels for 0% -> 0%
where the time goes in v22:
time: 90.7 us; the launch traced here: 90.4 us
  waiting for transfers between devices  39.3 us (43%)
  matrix products  16.8 us (19%)
  starting transfers between devices  14.7 us (16%)
  other arithmetic  10.6 us (12%)
  blocking collectives  4.35 us (5%)
  local copies, waits for them, and re-layouts  3.41 us (4%)
  between operations  1.36 us (1%)
    ppermute x7, waiting for transfers between devices, butterfly(): other = lax.ppermute(tree, axis, partner_pairs(count, distance))  27.6 us
    ppermute x1, waiting for transfers between devices, narrow_butterfly(): other = lax.ppermute(sent, axis, partner_pairs(count, distance))  9.9 us
    ppermute x7, starting transfers between devices, butterfly(): other = lax.ppermute(tree, axis, partner_pairs(count, distance))  6.55 us
    ppermute x1, starting transfers between devices, extended_2(): lax.ppermute(lax.slice_in_dim(block, 0, width, axis=dim), axis, backward)  5.03 us
    all_gather x1, blocking collectives, body(): lax.all_gather(jnp.concatenate([local_kv, encoded, digits], axis=1), 'que...  4.35 us
    dot_general x1, matrix products, body(): lax.dot_general(mask_embed, pair_hits, (((1,), (1,)), ((), ())), preferre...  4.24 us
    convert_element_type x1, other arithmetic, loss_coefficients(): (matched[:, None] * (sigma - target + dice_part) * model_width ** (-0.5))...  4.16 us
    dot_general x2, matrix products, window_attend(): jnp.einsum('hqk,khd->qhd', weights, value_heads, preferred_element_type=j...  2.7 us
  transfers between devices with their start and end apart: 13, of which 8 were waited for; matrix products, arithmetic and copies ran while one was open for 11% of the time, Pallas kernels for 0%

profile of v22, /device:TPU:0, one launch (start us, length us, event | category | flops | bytes accessed | tf_op | source)
XLA Modules:
  0.0 90.4 jit_solution(10216723183249025188)
XLA Ops:
  0.7 1.1 %copy.50 = bf16[256,256]{0,1:T(8,128)(2,1)S(1)} copy(bf16[256,256]{1,0:T(8,128)(2,1)} %param.13) | data formatting | bytes 262144 | tf_op args[0]
  1.9 1.3 %convolution_convert_fusion = bf16[256,768]{1,0:T(8,128)(2,1)S(1)} fusion(bf16[256,768]{1,0:T(8,128)(2,1)} %param.14, bf16[256,256]{0,1:T(8,128)(2,1)S(1)} %copy.50, f32[256]{0:T(256)S(1)} %add_rsqrt_fusion.3, f32[256]{0:T(256)S(1)} %broadcast_multiply_fusion.3), kind=kOutput, calls=%fused_computation.31 | convolution fusion | flops 101122048 | bytes 919552 | tf_op jit(solution)/shard_map/dot_general | solution.py:199
  3.7 5.0 %collective-permute-start.1 = (bf16[256,512]{1,0:T(8,128)(2,1)S(1)}, bf16[256,512]{1,0:T(8,128)(2,1)S(1)}, u32[]{:S(2)}, u32[]{:S(2)}) collective-permute-start(bf16[256,512]{1,0:T(8,128)(2,1)S(1)} %slice.85), channel_id=1, source_target_pairs={{2,0},{4,2},{6,4},{8,6},{10,8},{12,10},{14,12},{16,14},{18,16},{20... | collective-permute-start | bytes 786440 | tf_op jit(solution)/shard_map/ppermute | solution.py:19
  11.2 1.7 %collective-permute-done = bf16[256,512]{1,0:T(8,128)(2,1)S(1)} collective-permute-done((bf16[256,512]{1,0:T(8,128)(2,1)S(1)}, bf16[256,512]{1,0:T(8,128)(2,1)S(1)}, u32[]{:S(2)}, u32[]{:S(2)}) %collective-permute-start) | collective-permute-done | bytes 262176 | tf_op jit(solution)/shard_map/ppermute | solution.py:16
  13.8 1.1 %fusion.140 = f32[8,128]{1,0:T(8,128)S(1)} fusion(pred[128,640]{1,0:T(8,128)(4,1)S(1)} %fusion.49, bf16[128,8,32]{0,2,1:T(8,128)(2,1)S(1)} %bitcast.186, bf16[640,8,32]{0,2,1:T(8,128)(2,1)S(1)} %bitcast.177), kind=kOutput, calls=%fused_computation.228 | convolution fusion | flops 44565120 | bytes 479232 | tf_op jit(solution)/shard_map/sub | solution.py:136
  15.0 1.4 %fusion.19 = bf16[8,32,128]{2,1,0:T(8,128)(2,1)S(1)} fusion(bf16[640,8,32]{0,2,1:T(8,128)(2,1)S(1)} %bitcast.179, f32[8,128]{1,0:T(8,128)S(1)} %fusion.140, pred[128,640]{1,0:T(8,128)(4,1)S(1)} %fusion.49, bf16[128,8,32]{0,2,1:T(8,128)(2,1)S(1)} %bitcast.187, bf16[640,8,32]{0,2,1:T(8,128)(2,1)S(1)} %bitcast.178), kind=kOutput, calls=%fused_computation.44 | convolution fusion | flops 87197312 | bytes 872448 | tf_op jit(solution)/shard_map/hqk,khd->qhd/dot_general | solution.py:138
  16.3 1.2 %fusion.139 = f32[8,128]{1,0:T(8,128)S(1)} fusion(pred[128,640]{1,0:T(8,128)(4,1)S(1)} %fusion.49, bf16[128,8,32]{0,2,1:T(8,128)(2,1)S(1)} %bitcast.184, bf16[640,8,32]{0,2,1:T(8,128)(2,1)S(1)} %bitcast.174), kind=kOutput, calls=%fused_computation.227 | convolution fusion | flops 44565120 | bytes 479232 | tf_op jit(solution)/shard_map/sub | solution.py:136
  17.5 1.3 %fusion.18 = bf16[8,32,128]{2,1,0:T(8,128)(2,1)S(1)} fusion(bf16[640,8,32]{0,2,1:T(8,128)(2,1)S(1)} %bitcast.176, f32[8,128]{1,0:T(8,128)S(1)} %fusion.139, pred[128,640]{1,0:T(8,128)(4,1)S(1)} %fusion.49, bf16[128,8,32]{0,2,1:T(8,128)(2,1)S(1)} %bitcast.185, bf16[640,8,32]{0,2,1:T(8,128)(2,1)S(1)} %bitcast.175), kind=kOutput, calls=%fused_computation.43 | convolution fusion | flops 87197312 | bytes 872448 | tf_op jit(solution)/shard_map/hqk,khd->qhd/dot_general | solution.py:138
  19.3 0.8 convert_reduce_fusion.3
  20.6 4.3 %all_gather.3 = bf16[512,896]{1,0:T(8,128)(2,1)S(1)} all-gather(bf16[256,896]{1,0:T(8,128)(2,1)S(1)} %fusion.46), channel_id=1, replica_groups=mesh['phi'=8,'query'=2,'event'=2] {'query'}, dimensions={0}, use_global_device_ids=true | all-gather | bytes 1376256 | tf_op jit(solution)/shard_map/all_gather | solution.py:230
  25.2 0.8 collective-permute-start.8
  26.3 1.3 %multiply_reduce_fusion = (f32[8,512]{1,0:T(8,128)S(1)}, f32[8,512,512]{1,2,0:T(8,128)S(1)}) fusion(bf16[512,8,32]{0,2,1:T(8,128)(2,1)S(1)} %bitcast.168, bf16[512,8,32]{0,2,1:T(8,128)(2,1)S(1)} %bitcast.170), kind=kOutput, calls=%fused_computation.4 | convolution fusion | flops 138407936 | bytes 8929280 | tf_op jit(solution)/shard_map/qhd,khd->hqk/dot_general | solution.py:243
  27.6 1.4 %convert_reduce_fusion = f32[8,512]{1,0:T(8,128)S(1)} fusion(f32[8,512]{1,0:T(8,128)S(1)} %get-tuple-element.63, f32[8,512,512]{1,2,0:T(8,128)S(1)} %get-tuple-element.64), kind=kLoop, calls=%fused_computation.2 | loop fusion | flops 10481664 | bytes 8421376 | tf_op jit(solution)/shard_map/reduce_sum | solution.py:248
  29.0 1.4 %collective-permute-start.3 = (f32[2,8,512]{2,1,0:T(8,128)S(1)}, f32[2,8,512]{2,1,0:T(8,128)S(1)}, u32[]{:S(2)}, u32[]{:S(2)}) collective-permute-start(f32[2,8,512]{2,1,0:T(8,128)S(1)} %pad_maximum_fusion.1), channel_id=1, source_target_pairs={{0,8},{4,12},{8,0},{12,4},{16,24},{20,28},{24,16},{28,20},{1,9},{5... | collective-permute-start | bytes 98312 | tf_op jit(solution)/shard_map/ppermute | solution.py:39
  30.4 1.5 %convolution_convert_fusion.3 = bf16[8,32,512]{2,1,0:T(8,128)(2,1)S(1)} fusion(bf16[512,8,32]{0,2,1:T(8,128)(2,1)S(1)} %bitcast.169, f32[8,512,512]{1,2,0:T(8,128)S(1)} %get-tuple-element.64, f32[8,512]{1,0:T(8,128)S(1)} %get-tuple-element.63), kind=kOutput, calls=%fused_computation.36 | convolution fusion | flops 140640256 | bytes 8929280 | tf_op jit(solution)/shard_map/hqk,khd->qhd/dot_general | solution.py:249
  32.0 0.7 collective-permute-start.2
  32.7 2.2 %collective-permute-done.3 = f32[2,8,512]{2,1,0:T(8,128)S(1)} collective-permute-done((f32[2,8,512]{2,1,0:T(8,128)S(1)}, f32[2,8,512]{2,1,0:T(8,128)S(1)}, u32[]{:S(2)}, u32[]{:S(2)}) %collective-permute-start.3) | collective-permute-done | bytes 32800 | tf_op jit(solution)/shard_map/ppermute | solution.py:39
  35.1 3.9 %collective-permute-done.5 = f32[2,8,512]{2,1,0:T(8,128)S(1)} collective-permute-done((f32[2,8,512]{2,1,0:T(8,128)S(1)}, f32[2,8,512]{2,1,0:T(8,128)S(1)}, u32[]{:S(2)}, u32[]{:S(2)}) %collective-permute-start.5) | collective-permute-done | bytes 32800 | tf_op jit(solution)/shard_map/ppermute | solution.py:39
  39.0 1.8 %collective-permute-start.7 = (f32[2,8,512]{2,1,0:T(8,128)S(1)}, f32[2,8,512]{2,1,0:T(8,128)S(1)}, u32[]{:S(2)}, u32[]{:S(2)}) collective-permute-start(f32[2,8,512]{2,1,0:T(8,128)S(1)} %pad_maximum_fusion.3), channel_id=1, source_target_pairs={{0,16},{4,20},{8,24},{12,28},{16,0},{20,4},{24,8},{28,12},{1,17},{... | collective-permute-start | bytes 98312 | tf_op jit(solution)/shard_map/ppermute | solution.py:39
  40.8 3.4 %collective-permute-done.7 = f32[2,8,512]{2,1,0:T(8,128)S(1)} collective-permute-done((f32[2,8,512]{2,1,0:T(8,128)S(1)}, f32[2,8,512]{2,1,0:T(8,128)S(1)}, u32[]{:S(2)}, u32[]{:S(2)}) %collective-permute-start.7) | collective-permute-done | bytes 32800 | tf_op jit(solution)/shard_map/ppermute | solution.py:39
  44.9 6.0 %collective-permute-done.4 = bf16[512,256]{0,1:T(8,128)(2,1)S(1)} collective-permute-done((bf16[512,256]{0,1:T(8,128)(2,1)S(1)}, bf16[512,256]{0,1:T(8,128)(2,1)S(1)}, u32[]{:S(2)}, u32[]{:S(2)}) %collective-permute-start.4) | collective-permute-done | bytes 262176 | tf_op jit(solution)/shard_map/ppermute | solution.py:39
  51.0 1.4 %collective-permute-start.6 = (bf16[512,256]{0,1:T(8,128)(2,1)S(1)}, bf16[512,256]{0,1:T(8,128)(2,1)S(1)}, u32[]{:S(2)}, u32[]{:S(2)}) collective-permute-start(bf16[512,256]{0,1:T(8,128)(2,1)S(1)} %fusion.37), channel_id=1, source_target_pairs={{0,16},{4,20},{8,24},{12,28},{16,0},{20,4},{24,8},{28,12},{1,17},{... | collective-permute-start | bytes 786440 | tf_op jit(solution)/shard_map/ppermute | solution.py:39
  53.2 8.6 %collective-permute-done.6 = bf16[512,256]{0,1:T(8,128)(2,1)S(1)} collective-permute-done((bf16[512,256]{0,1:T(8,128)(2,1)S(1)}, bf16[512,256]{0,1:T(8,128)(2,1)S(1)}, u32[]{:S(2)}, u32[]{:S(2)}) %collective-permute-start.6) | collective-permute-done | bytes 262176 | tf_op jit(solution)/shard_map/ppermute | solution.py:39
  63.0 4.2 %select_reduce_fusion = (f32[512]{0:T(512)S(1)}, f32[512]{0:T(512)S(1)}, f32[512]{0:T(512)S(1)}, f32[512,2048]{1,0:T(8,128)}) fusion(s32[2048]{0:T(1024)S(1)} %bitcast.189, s32[512]{0:T(512)S(1)} %copy-done.8, pred[512]{0:T(512)(128)(4,1)S(1)} %get-tuple-element.24, bf16[512,256]{1,0:T(8,128)(2,1)S(1)} %convolution_convert_fusion.2, ...), kind=kOutput, calls=%fused_computation.11 | convolution fusion | flops 553122304 | bytes 5521921 | tf_op jit(solution)/shard_map/dot_general | solution.py:280
  67.2 1.1 %collective-permute-start.10 = (f32[3,512]{1,0:T(4,128)S(1)}, f32[3,512]{1,0:T(4,128)S(1)}, u32[]{:S(2)}, u32[]{:S(2)}) collective-permute-start(f32[3,512]{1,0:T(4,128)S(1)} %pad_maximum_fusion.4), channel_id=1, source_target_pairs={{0,16},{4,20},{8,24},{12,28},{16,0},{20,4},{24,8},{28,12},{1,17},{... | collective-permute-start | bytes 18440 | tf_op jit(solution)/shard_map/ppermute | solution.py:39
  68.3 3.5 %collective-permute-done.10 = f32[3,512]{1,0:T(4,128)S(1)} collective-permute-done((f32[3,512]{1,0:T(4,128)S(1)}, f32[3,512]{1,0:T(4,128)S(1)}, u32[]{:S(2)}, u32[]{:S(2)}) %collective-permute-start.10) | collective-permute-done | bytes 6176 | tf_op jit(solution)/shard_map/ppermute | solution.py:39
  72.5 4.2 %fusion.5 = bf16[512,2048]{1,0:T(8,128)(2,1)S(1)} fusion(f32[512,2048]{1,0:T(8,128)} %get-tuple-element.67, f32[512]{0:T(512)S(1)} %bitcast.192, f32[512]{0:T(512)S(1)} %bitcast.193, s32[2048]{0:T(1024)S(1)} %bitcast.190, f32[512]{0:T(512)S(1)} %get-tuple-element.23, s32[512]{0:T(512)S(1)} %copy-done.8, pred[512]{0:T(512)(128)(4,1)S(1)} %get-tuple-element.24), kind=kLoop, calls=%fused_computation.10 | loop fusion | flops 14680064 | bytes 6308352 | tf_op jit(solution)/shard_map/convert_element_type | solution.py:173
  76.6 0.7 convolution_convert_fusion.1
  77.4 1.1 %collective-permute-start.12 = (bf16[512,256]{1,0:T(8,128)(2,1)S(1)}, bf16[512,256]{1,0:T(8,128)(2,1)S(1)}, u32[]{:S(2)}, u32[]{:S(2)}) collective-permute-start(bf16[512,256]{1,0:T(8,128)(2,1)S(1)} %convolution_convert_fusion.1), channel_id=1, source_target_pairs={{0,16},{4,20},{8,24},{12,28},{16,0},{20,4},{24,8},{28,12},{1,17},{... | collective-permute-start | bytes 786440 | tf_op jit(solution)/shard_map/ppermute | solution.py:58
  78.9 9.9 %collective-permute-done.12 = bf16[512,256]{1,0:T(8,128)(2,1)S(1)} collective-permute-done((bf16[512,256]{1,0:T(8,128)(2,1)S(1)}, bf16[512,256]{1,0:T(8,128)(2,1)S(1)}, u32[]{:S(2)}, u32[]{:S(2)}) %collective-permute-start.12) | collective-permute-done | bytes 262176 | tf_op jit(solution)/shard_map/ppermute | solution.py:58
  88.8 0.9 convert_add_fusion
  89.7 0.8 select_add_fusion
  (112 shorter events, 9.1 us)
Async XLA Ops:
  0.6 18.6 %copy-start = (bf16[1024,256]{1,0:T(8,128)(2,1)S(1)}, bf16[1024,256]{1,0:T(8,128)(2,1)}, u32[]{:S(2)}) copy-start(bf16[1024,256]{1,0:T(8,128)(2,1)} %param.17) | copy-start | bytes 1572868
  0.6 10.1 %copy-start.1 = (bf16[512,256]{1,0:T(8,128)(2,1)S(1)}, bf16[512,256]{1,0:T(8,128)(2,1)}, u32[]{:S(2)}) copy-start(bf16[512,256]{1,0:T(8,128)(2,1)} %param.18) | copy-start | bytes 786436
  0.7 10.2 %copy-start.5 = (bf16[256,256]{1,0:T(8,128)(2,1)S(1)}, bf16[256,256]{1,0:T(8,128)(2,1)}, u32[]{:S(2)}) copy-start(bf16[256,256]{1,0:T(8,128)(2,1)} %param.19) | copy-start | bytes 393220
  3.2 9.6 %collective-permute-start = (bf16[256,512]{1,0:T(8,128)(2,1)S(1)}, bf16[256,512]{1,0:T(8,128)(2,1)S(1)}, u32[]{:S(2)}, u32[]{:S(2)}) collective-permute-start(bf16[256,512]{1,0:T(8,128)(2,1)S(1)} %slice.85), channel_id=1, source_target_pairs={{0,2},{2,4},{4,6},{6,8},{8,10},{10,12},{12,14},{14,16},{16,18},{18... | collective-permute-start | bytes 786440 | tf_op jit(solution)/shard_map/ppermute | solution.py:16
  3.7 9.1 %collective-permute-start.1 = (bf16[256,512]{1,0:T(8,128)(2,1)S(1)}, bf16[256,512]{1,0:T(8,128)(2,1)S(1)}, u32[]{:S(2)}, u32[]{:S(2)}) collective-permute-start(bf16[256,512]{1,0:T(8,128)(2,1)S(1)} %slice.85), channel_id=1, source_target_pairs={{2,0},{4,2},{6,4},{8,6},{10,8},{12,10},{14,12},{16,14},{18,16},{20... | collective-permute-start | bytes 786440 | tf_op jit(solution)/shard_map/ppermute | solution.py:19
  17.5 1.4 %copy-start.6 = (bf16[256,256]{1,0:T(8,128)(2,1)S(1)}, bf16[256,256]{1,0:T(8,128)(2,1)}, u32[]{:S(2)}) copy-start(bf16[256,256]{1,0:T(8,128)(2,1)} %param.15) | copy-start | bytes 393220
  17.5 1.8 %copy-start.9 = (bf16[256,1024]{1,0:T(8,128)(2,1)S(1)}, bf16[256,1024]{1,0:T(8,128)(2,1)}, u32[]{:S(2)}) copy-start(bf16[256,1024]{1,0:T(8,128)(2,1)} %param.16) | copy-start | bytes 1572868
  18.9 1.4 %copy-start.4 = (bf16[256,512]{1,0:T(8,128)(2,1)S(1)}, bf16[256,512]{1,0:T(8,128)(2,1)}, u32[]{:S(2)}) copy-start(bf16[256,512]{1,0:T(8,128)(2,1)} %param.20) | copy-start | bytes 786436
  20.2 5.0 %copy-start.2 = (bf16[256,256]{1,0:T(8,128)(2,1)}, bf16[256,256]{1,0:T(8,128)(2,1)S(1)}, u32[]{:S(2)}) copy-start(bf16[256,256]{1,0:T(8,128)(2,1)S(1)} %copy.66) | copy-start | bytes 393220
  25.2 19.4 %collective-permute-start.8 = (bf16[528,256]{1,0:T(8,128)(2,1)S(1)}, bf16[528,256]{1,0:T(8,128)(2,1)S(1)}, u32[]{:S(2)}, u32[]{:S(2)}) collective-permute-start(bf16[528,256]{1,0:T(8,128)(2,1)S(1)} %fusion.58), channel_id=1, source_target_pairs={{0,8},{4,12},{8,0},{12,4},{16,24},{20,28},{24,16},{28,20},{1,9},{5... | collective-permute-start | bytes 811016 | tf_op jit(solution)/shard_map/ppermute | solution.py:100
  29.0 6.0 %collective-permute-start.3 = (f32[2,8,512]{2,1,0:T(8,128)S(1)}, f32[2,8,512]{2,1,0:T(8,128)S(1)}, u32[]{:S(2)}, u32[]{:S(2)}) collective-permute-start(f32[2,8,512]{2,1,0:T(8,128)S(1)} %pad_maximum_fusion.1), channel_id=1, source_target_pairs={{0,8},{4,12},{8,0},{12,4},{16,24},{20,28},{24,16},{28,20},{1,9},{5... | collective-permute-start | bytes 98312 | tf_op jit(solution)/shard_map/ppermute | solution.py:39
  32.0 12.2 %collective-permute-start.2 = (bf16[512,256]{0,1:T(8,128)(2,1)S(1)}, bf16[512,256]{0,1:T(8,128)(2,1)S(1)}, u32[]{:S(2)}, u32[]{:S(2)}) collective-permute-start(bf16[512,256]{0,1:T(8,128)(2,1)S(1)} %bitcast.171), channel_id=1, source_target_pairs={{0,8},{4,12},{8,0},{12,4},{16,24},{20,28},{24,16},{28,20},{1,9},{5... | collective-permute-start | bytes 786440 | tf_op jit(solution)/shard_map/ppermute | solution.py:39
  35.0 4.0 %collective-permute-start.5 = (f32[2,8,512]{2,1,0:T(8,128)S(1)}, f32[2,8,512]{2,1,0:T(8,128)S(1)}, u32[]{:S(2)}, u32[]{:S(2)}) collective-permute-start(f32[2,8,512]{2,1,0:T(8,128)S(1)} %pad_maximum_fusion.2), channel_id=1, source_target_pairs={{0,4},{4,0},{8,12},{12,8},{16,20},{20,16},{24,28},{28,24},{1,5},{5... | collective-permute-start | bytes 98312 | tf_op jit(solution)/shard_map/ppermute | solution.py:39
  39.0 5.2 %collective-permute-start.7 = (f32[2,8,512]{2,1,0:T(8,128)S(1)}, f32[2,8,512]{2,1,0:T(8,128)S(1)}, u32[]{:S(2)}, u32[]{:S(2)}) collective-permute-start(f32[2,8,512]{2,1,0:T(8,128)S(1)} %pad_maximum_fusion.3), channel_id=1, source_target_pairs={{0,16},{4,20},{8,24},{12,28},{16,0},{20,4},{24,8},{28,12},{1,17},{... | collective-permute-start | bytes 98312 | tf_op jit(solution)/shard_map/ppermute | solution.py:39
  44.3 17.7 %copy-start.7 = (bf16[256,256]{1,0:T(8,128)(2,1)S(1)}, bf16[256,256]{1,0:T(8,128)(2,1)}, u32[]{:S(2)}) copy-start(bf16[256,256]{1,0:T(8,128)(2,1)} %param.21) | copy-start | bytes 393220
  44.4 6.4 %collective-permute-start.4 = (bf16[512,256]{0,1:T(8,128)(2,1)S(1)}, bf16[512,256]{0,1:T(8,128)(2,1)S(1)}, u32[]{:S(2)}, u32[]{:S(2)}) collective-permute-start(bf16[512,256]{0,1:T(8,128)(2,1)S(1)} %fusion.39), channel_id=1, source_target_pairs={{0,4},{4,0},{8,12},{12,8},{16,20},{20,16},{24,28},{28,24},{1,5},{5... | collective-permute-start | bytes 786440 | tf_op jit(solution)/shard_map/ppermute | solution.py:39
  44.6 17.7 %copy-start.10 = (bf16[256,256]{1,0:T(8,128)(2,1)S(1)}, bf16[256,256]{1,0:T(8,128)(2,1)}, u32[]{:S(2)}) copy-start(bf16[256,256]{1,0:T(8,128)(2,1)} %param.23) | copy-start | bytes 393220
  44.6 17.7 %copy-start.11 = (bf16[256,256]{1,0:T(8,128)(2,1)S(1)}, bf16[256,256]{1,0:T(8,128)(2,1)}, u32[]{:S(2)}) copy-start(bf16[256,256]{1,0:T(8,128)(2,1)} %param.22) | copy-start | bytes 393220
  51.0 10.8 %collective-permute-start.6 = (bf16[512,256]{0,1:T(8,128)(2,1)S(1)}, bf16[512,256]{0,1:T(8,128)(2,1)S(1)}, u32[]{:S(2)}, u32[]{:S(2)}) collective-permute-start(bf16[512,256]{0,1:T(8,128)(2,1)S(1)} %fusion.37), channel_id=1, source_target_pairs={{0,16},{4,20},{8,24},{12,28},{16,0},{20,4},{24,8},{28,12},{1,17},{... | collective-permute-start | bytes 786440 | tf_op jit(solution)/shard_map/ppermute | solution.py:39
  52.5 10.4 %copy-start.8 = (s32[512]{0:T(512)S(1)}, s32[512]{0:T(512)}, u32[]{:S(2)}) copy-start(s32[512]{0:T(512)} %param.25) | copy-start | bytes 6148
  52.5 10.3 %collective-permute-start.9 = (bf16[1040,256]{1,0:T(8,128)(2,1)S(1)}, bf16[1040,256]{1,0:T(8,128)(2,1)S(1)}, u32[]{:S(2)}, u32[]{:S(2)}) collective-permute-start(bf16[1040,256]{1,0:T(8,128)(2,1)S(1)} %fusion.31), channel_id=1, source_target_pairs={{0,4},{4,0},{8,12},{12,8},{16,20},{20,16},{24,28},{28,24},{1,5},{5... | collective-permute-start | bytes 1597448 | tf_op jit(solution)/shard_map/ppermute | solution.py:100
  62.8 15.6 %copy-start.3 = (bf16[512,256]{1,0:T(8,128)(2,1)}, bf16[512,256]{1,0:T(8,128)(2,1)S(1)}, u32[]{:S(2)}) copy-start(bf16[512,256]{1,0:T(8,128)(2,1)S(1)} %convolution_convert_fusion.2) | copy-start | bytes 786436
  67.2 4.6 %collective-permute-start.10 = (f32[3,512]{1,0:T(4,128)S(1)}, f32[3,512]{1,0:T(4,128)S(1)}, u32[]{:S(2)}, u32[]{:S(2)}) collective-permute-start(f32[3,512]{1,0:T(4,128)S(1)} %pad_maximum_fusion.4), channel_id=1, source_target_pairs={{0,16},{4,20},{8,24},{12,28},{16,0},{20,4},{24,8},{28,12},{1,17},{... | collective-permute-start | bytes 18440 | tf_op jit(solution)/shard_map/ppermute | solution.py:39
  77.4 11.4 %collective-permute-start.12 = (bf16[512,256]{1,0:T(8,128)(2,1)S(1)}, bf16[512,256]{1,0:T(8,128)(2,1)S(1)}, u32[]{:S(2)}, u32[]{:S(2)}) collective-permute-start(bf16[512,256]{1,0:T(8,128)(2,1)S(1)} %convolution_convert_fusion.1), channel_id=1, source_target_pairs={{0,16},{4,20},{8,24},{12,28},{16,0},{20,4},{24,8},{28,12},{1,17},{... | collective-permute-start | bytes 786440 | tf_op jit(solution)/shard_map/ppermute | solution.py:58
  78.8 10.8 %collective-permute-start.11 = (f32[256,256]{1,0:T(8,128)S(1)}, f32[256,256]{1,0:T(8,128)S(1)}, u32[]{:S(2)}, u32[]{:S(2)}) collective-permute-start(f32[256,256]{1,0:T(8,128)S(1)} %slice_select_fusion), channel_id=1, source_target_pairs={{0,2},{2,0},{1,3},{3,1},{4,6},{6,4},{5,7},{7,5},{8,10},{10,8},{9,1... | collective-permute-start | bytes 786440 | tf_op jit(solution)/shard_map/ppermute | solution.py:89

commit v23 on v22

--- a/solution.py
+++ b/solution.py
@@ -254,7 +254,6 @@
         "phi",
         softmax_combine,
         ordered=True,
-        order="near_first",
     )
     mixed = mixed.astype(jnp.float32)
     context = scale_heads(mixed, 1.0 / total).astype(jnp.bfloat16)

time: 90.7 us -> 88.2 us (0.972)
  waiting for transfers between devices: 39.3 us -> 33.3 us
  starting transfers between devices: 14.7 us -> 18.2 us
    ppermute x7, waiting for transfers between devices: 27.6 us -> 21 us  [butterfly(): other = lax.ppermute(tree, axis, partner_pairs(count, distance))]
    ppermute x7, starting transfers between devices: 6.55 us -> 10.7 us  [butterfly(): other = lax.ppermute(tree, axis, partner_pairs(count, distance))]
    ppermute x2, waiting for transfers between devices: 0.01 us -> 1.57 us  [partner_rows(): lax.ppermute(payload, 'phi', partner_pairs(lax.axis_size('phi'), distance))]
    ppermute x1, starting transfers between devices: 1.08 us -> 0.08 us  [narrow_butterfly(): other = lax.ppermute(sent, axis, partner_pairs(count, distance))]
  transfers between devices with their start and end apart: 13 -> 13, of which waited for: 8 -> 9; matrix products, arithmetic and copies ran while one was open for 11% -> 11% of each run, Pallas kernels for 0% -> 0%
where the time goes in v23:
time: 88.2 us; the launch traced here: 88 us
  waiting for transfers between devices  33.3 us (38%)
  starting transfers between devices  18.2 us (21%)
  matrix products  16.8 us (19%)
  other arithmetic  10.6 us (12%)
  blocking collectives  4.35 us (5%)
  local copies, waits for them, and re-layouts  3.42 us (4%)
  between operations  1.35 us (2%)
    ppermute x7, waiting for transfers between devices, butterfly(): other = lax.ppermute(tree, axis, partner_pairs(count, distance))  21 us
    ppermute x7, starting transfers between devices, butterfly(): other = lax.ppermute(tree, axis, partner_pairs(count, distance))  10.7 us
    ppermute x1, waiting for transfers between devices, narrow_butterfly(): other = lax.ppermute(sent, axis, partner_pairs(count, distance))  9.01 us
    ppermute x1, starting transfers between devices, extended_2(): lax.ppermute(lax.slice_in_dim(block, 0, width, axis=dim), axis, backward)  5.03 us
    all_gather x1, blocking collectives, body(): lax.all_gather(jnp.concatenate([local_kv, encoded, digits], axis=1), 'que...  4.35 us
    dot_general x1, matrix products, body(): lax.dot_general(mask_embed, pair_hits, (((1,), (1,)), ((), ())), preferre...  4.24 us
    convert_element_type x1, other arithmetic, loss_coefficients(): (matched[:, None] * (sigma - target + dice_part) * model_width ** (-0.5))...  4.16 us
    dot_general x2, matrix products, window_attend(): jnp.einsum('hqk,khd->qhd', weights, value_heads, preferred_element_type=j...  2.7 us
  transfers between devices with their start and end apart: 13, of which 9 were waited for; matrix products, arithmetic and copies ran while one was open for 11% of the time, Pallas kernels for 0%

profile of v23, /device:TPU:0, one launch (start us, length us, event | category | flops | bytes accessed | tf_op | source)
XLA Modules:
  0.0 88.0 jit_solution(6504817055071459798)
XLA Ops:
  0.7 1.1 %copy.50 = bf16[256,256]{0,1:T(8,128)(2,1)S(1)} copy(bf16[256,256]{1,0:T(8,128)(2,1)} %param.13) | data formatting | bytes 262144 | tf_op args[0]
  1.9 1.3 %convolution_convert_fusion = bf16[256,768]{1,0:T(8,128)(2,1)S(1)} fusion(bf16[256,768]{1,0:T(8,128)(2,1)} %param.14, bf16[256,256]{0,1:T(8,128)(2,1)S(1)} %copy.50, f32[256]{0:T(256)S(1)} %add_rsqrt_fusion.3, f32[256]{0:T(256)S(1)} %broadcast_multiply_fusion.3), kind=kOutput, calls=%fused_computation.31 | convolution fusion | flops 101122048 | bytes 919552 | tf_op jit(solution)/shard_map/dot_general | solution.py:199
  3.7 5.0 %collective-permute-start.1 = (bf16[256,512]{1,0:T(8,128)(2,1)S(1)}, bf16[256,512]{1,0:T(8,128)(2,1)S(1)}, u32[]{:S(2)}, u32[]{:S(2)}) collective-permute-start(bf16[256,512]{1,0:T(8,128)(2,1)S(1)} %slice.85), channel_id=1, source_target_pairs={{2,0},{4,2},{6,4},{8,6},{10,8},{12,10},{14,12},{16,14},{18,16},{20... | collective-permute-start | bytes 786440 | tf_op jit(solution)/shard_map/ppermute | solution.py:19
  11.2 1.7 %collective-permute-done = bf16[256,512]{1,0:T(8,128)(2,1)S(1)} collective-permute-done((bf16[256,512]{1,0:T(8,128)(2,1)S(1)}, bf16[256,512]{1,0:T(8,128)(2,1)S(1)}, u32[]{:S(2)}, u32[]{:S(2)}) %collective-permute-start) | collective-permute-done | bytes 262176 | tf_op jit(solution)/shard_map/ppermute | solution.py:16
  13.8 1.1 %fusion.140 = f32[8,128]{1,0:T(8,128)S(1)} fusion(pred[128,640]{1,0:T(8,128)(4,1)S(1)} %fusion.49, bf16[128,8,32]{0,2,1:T(8,128)(2,1)S(1)} %bitcast.186, bf16[640,8,32]{0,2,1:T(8,128)(2,1)S(1)} %bitcast.177), kind=kOutput, calls=%fused_computation.228 | convolution fusion | flops 44565120 | bytes 479232 | tf_op jit(solution)/shard_map/sub | solution.py:136
  15.0 1.4 %fusion.19 = bf16[8,32,128]{2,1,0:T(8,128)(2,1)S(1)} fusion(bf16[640,8,32]{0,2,1:T(8,128)(2,1)S(1)} %bitcast.179, f32[8,128]{1,0:T(8,128)S(1)} %fusion.140, pred[128,640]{1,0:T(8,128)(4,1)S(1)} %fusion.49, bf16[128,8,32]{0,2,1:T(8,128)(2,1)S(1)} %bitcast.187, bf16[640,8,32]{0,2,1:T(8,128)(2,1)S(1)} %bitcast.178), kind=kOutput, calls=%fused_computation.44 | convolution fusion | flops 87197312 | bytes 872448 | tf_op jit(solution)/shard_map/hqk,khd->qhd/dot_general | solution.py:138
  16.3 1.2 %fusion.139 = f32[8,128]{1,0:T(8,128)S(1)} fusion(pred[128,640]{1,0:T(8,128)(4,1)S(1)} %fusion.49, bf16[128,8,32]{0,2,1:T(8,128)(2,1)S(1)} %bitcast.184, bf16[640,8,32]{0,2,1:T(8,128)(2,1)S(1)} %bitcast.174), kind=kOutput, calls=%fused_computation.227 | convolution fusion | flops 44565120 | bytes 479232 | tf_op jit(solution)/shard_map/sub | solution.py:136
  17.5 1.3 %fusion.18 = bf16[8,32,128]{2,1,0:T(8,128)(2,1)S(1)} fusion(bf16[640,8,32]{0,2,1:T(8,128)(2,1)S(1)} %bitcast.176, f32[8,128]{1,0:T(8,128)S(1)} %fusion.139, pred[128,640]{1,0:T(8,128)(4,1)S(1)} %fusion.49, bf16[128,8,32]{0,2,1:T(8,128)(2,1)S(1)} %bitcast.185, bf16[640,8,32]{0,2,1:T(8,128)(2,1)S(1)} %bitcast.175), kind=kOutput, calls=%fused_computation.43 | convolution fusion | flops 87197312 | bytes 872448 | tf_op jit(solution)/shard_map/hqk,khd->qhd/dot_general | solution.py:138
  19.3 0.8 convert_reduce_fusion.3
  20.6 4.3 %all_gather.3 = bf16[512,896]{1,0:T(8,128)(2,1)S(1)} all-gather(bf16[256,896]{1,0:T(8,128)(2,1)S(1)} %fusion.46), channel_id=1, replica_groups=mesh['phi'=8,'query'=2,'event'=2] {'query'}, dimensions={0}, use_global_device_ids=true | all-gather | bytes 1376256 | tf_op jit(solution)/shard_map/all_gather | solution.py:230
  25.2 0.8 collective-permute-start.8
  26.3 1.3 %multiply_reduce_fusion = (f32[8,512]{1,0:T(8,128)S(1)}, f32[8,512,512]{1,2,0:T(8,128)S(1)}) fusion(bf16[512,8,32]{0,2,1:T(8,128)(2,1)S(1)} %bitcast.168, bf16[512,8,32]{0,2,1:T(8,128)(2,1)S(1)} %bitcast.170), kind=kOutput, calls=%fused_computation.4 | convolution fusion | flops 138407936 | bytes 8929280 | tf_op jit(solution)/shard_map/qhd,khd->hqk/dot_general | solution.py:243
  27.6 1.4 %convert_reduce_fusion = f32[8,512]{1,0:T(8,128)S(1)} fusion(f32[8,512]{1,0:T(8,128)S(1)} %get-tuple-element.63, f32[8,512,512]{1,2,0:T(8,128)S(1)} %get-tuple-element.64), kind=kLoop, calls=%fused_computation.2 | loop fusion | flops 10481664 | bytes 8421376 | tf_op jit(solution)/shard_map/reduce_sum | solution.py:248
  29.6 1.5 %convolution_convert_fusion.3 = bf16[8,32,512]{2,1,0:T(8,128)(2,1)S(1)} fusion(bf16[512,8,32]{0,2,1:T(8,128)(2,1)S(1)} %bitcast.169, f32[8,512,512]{1,2,0:T(8,128)S(1)} %get-tuple-element.64, f32[8,512]{1,0:T(8,128)S(1)} %get-tuple-element.63), kind=kOutput, calls=%fused_computation.36 | convolution fusion | flops 140640256 | bytes 8929280 | tf_op jit(solution)/shard_map/hqk,khd->qhd/dot_general | solution.py:249
  31.3 1.5 %collective-permute-start.2 = (bf16[512,256]{0,1:T(8,128)(2,1)S(1)}, bf16[512,256]{0,1:T(8,128)(2,1)S(1)}, u32[]{:S(2)}, u32[]{:S(2)}) collective-permute-start(bf16[512,256]{0,1:T(8,128)(2,1)S(1)} %bitcast.171), channel_id=1, source_target_pairs={{0,4},{4,0},{8,12},{12,8},{16,20},{20,16},{24,28},{28,24},{1,5},{5... | collective-permute-start | bytes 786440 | tf_op jit(solution)/shard_map/ppermute | solution.py:39
  33.0 1.4 %collective-permute-start.5 = (f32[2,8,512]{2,1,0:T(8,128)S(1)}, f32[2,8,512]{2,1,0:T(8,128)S(1)}, u32[]{:S(2)}, u32[]{:S(2)}) collective-permute-start(f32[2,8,512]{2,1,0:T(8,128)S(1)} %pad_maximum_fusion.2), channel_id=1, source_target_pairs={{0,8},{4,12},{8,0},{12,4},{16,24},{20,28},{24,16},{28,20},{1,9},{5... | collective-permute-start | bytes 98312 | tf_op jit(solution)/shard_map/ppermute | solution.py:39
  34.4 2.6 %collective-permute-done.5 = f32[2,8,512]{2,1,0:T(8,128)S(1)} collective-permute-done((f32[2,8,512]{2,1,0:T(8,128)S(1)}, f32[2,8,512]{2,1,0:T(8,128)S(1)}, u32[]{:S(2)}, u32[]{:S(2)}) %collective-permute-start.5) | collective-permute-done | bytes 32800 | tf_op jit(solution)/shard_map/ppermute | solution.py:39
  37.0 2.6 %collective-permute-start.7 = (f32[2,8,512]{2,1,0:T(8,128)S(1)}, f32[2,8,512]{2,1,0:T(8,128)S(1)}, u32[]{:S(2)}, u32[]{:S(2)}) collective-permute-start(f32[2,8,512]{2,1,0:T(8,128)S(1)} %pad_maximum_fusion.3), channel_id=1, source_target_pairs={{0,16},{4,20},{8,24},{12,28},{16,0},{20,4},{24,8},{28,12},{1,17},{... | collective-permute-start | bytes 98312 | tf_op jit(solution)/shard_map/ppermute | solution.py:39
  39.7 2.2 %collective-permute-done.7 = f32[2,8,512]{2,1,0:T(8,128)S(1)} collective-permute-done((f32[2,8,512]{2,1,0:T(8,128)S(1)}, f32[2,8,512]{2,1,0:T(8,128)S(1)}, u32[]{:S(2)}, u32[]{:S(2)}) %collective-permute-start.7) | collective-permute-done | bytes 32800 | tf_op jit(solution)/shard_map/ppermute | solution.py:39
  42.1 1.4 %collective-permute-start.4 = (bf16[512,256]{0,1:T(8,128)(2,1)S(1)}, bf16[512,256]{0,1:T(8,128)(2,1)S(1)}, u32[]{:S(2)}, u32[]{:S(2)}) collective-permute-start(bf16[512,256]{0,1:T(8,128)(2,1)S(1)} %fusion.39), channel_id=1, source_target_pairs={{0,8},{4,12},{8,0},{12,4},{16,24},{20,28},{24,16},{28,20},{1,9},{5... | collective-permute-start | bytes 786440 | tf_op jit(solution)/shard_map/ppermute | solution.py:39
  43.9 5.8 %collective-permute-done.4 = bf16[512,256]{0,1:T(8,128)(2,1)S(1)} collective-permute-done((bf16[512,256]{0,1:T(8,128)(2,1)S(1)}, bf16[512,256]{0,1:T(8,128)(2,1)S(1)}, u32[]{:S(2)}, u32[]{:S(2)}) %collective-permute-start.4) | collective-permute-done | bytes 262176 | tf_op jit(solution)/shard_map/ppermute | solution.py:39
  49.8 3.1 %collective-permute-start.6 = (bf16[512,256]{0,1:T(8,128)(2,1)S(1)}, bf16[512,256]{0,1:T(8,128)(2,1)S(1)}, u32[]{:S(2)}, u32[]{:S(2)}) collective-permute-start(bf16[512,256]{0,1:T(8,128)(2,1)S(1)} %fusion.37), channel_id=1, source_target_pairs={{0,16},{4,20},{8,24},{12,28},{16,0},{20,4},{24,8},{28,12},{1,17},{... | collective-permute-start | bytes 786440 | tf_op jit(solution)/shard_map/ppermute | solution.py:39
  52.9 1.0 %collective-permute-start.9 = (bf16[1040,256]{1,0:T(8,128)(2,1)S(1)}, bf16[1040,256]{1,0:T(8,128)(2,1)S(1)}, u32[]{:S(2)}, u32[]{:S(2)}) collective-permute-start(bf16[1040,256]{1,0:T(8,128)(2,1)S(1)} %fusion.31), channel_id=1, source_target_pairs={{0,4},{4,0},{8,12},{12,8},{16,20},{20,16},{24,28},{28,24},{1,5},{5... | collective-permute-start | bytes 1597448 | tf_op jit(solution)/shard_map/ppermute | solution.py:100
  53.9 5.7 %collective-permute-done.6 = bf16[512,256]{0,1:T(8,128)(2,1)S(1)} collective-permute-done((bf16[512,256]{0,1:T(8,128)(2,1)S(1)}, bf16[512,256]{0,1:T(8,128)(2,1)S(1)}, u32[]{:S(2)}, u32[]{:S(2)}) %collective-permute-start.6) | collective-permute-done | bytes 262176 | tf_op jit(solution)/shard_map/ppermute | solution.py:39
  60.7 1.6 %collective-permute-done.9 = bf16[1040,256]{1,0:T(8,128)(2,1)S(1)} collective-permute-done((bf16[1040,256]{1,0:T(8,128)(2,1)S(1)}, bf16[1040,256]{1,0:T(8,128)(2,1)S(1)}, u32[]{:S(2)}, u32[]{:S(2)}) %collective-permute-start.9) | collective-permute-done | bytes 532512 | tf_op jit(solution)/shard_map/ppermute | solution.py:100
  62.4 4.2 %select_reduce_fusion = (f32[512]{0:T(512)S(1)}, f32[512]{0:T(512)S(1)}, f32[512]{0:T(512)S(1)}, f32[512,2048]{1,0:T(8,128)}) fusion(s32[2048]{0:T(1024)S(1)} %bitcast.189, s32[512]{0:T(512)S(1)} %copy-done.8, pred[512]{0:T(512)(128)(4,1)S(1)} %get-tuple-element.24, bf16[512,256]{1,0:T(8,128)(2,1)S(1)} %convolution_convert_fusion.2, ...), kind=kOutput, calls=%fused_computation.11 | convolution fusion | flops 553122304 | bytes 5521921 | tf_op jit(solution)/shard_map/dot_general | solution.py:279
  66.8 4.5 %collective-permute-done.10 = f32[3,512]{1,0:T(4,128)S(1)} collective-permute-done((f32[3,512]{1,0:T(4,128)S(1)}, f32[3,512]{1,0:T(4,128)S(1)}, u32[]{:S(2)}, u32[]{:S(2)}) %collective-permute-start.10) | collective-permute-done | bytes 6176 | tf_op jit(solution)/shard_map/ppermute | solution.py:39
  71.9 4.2 %fusion.5 = bf16[512,2048]{1,0:T(8,128)(2,1)S(1)} fusion(f32[512,2048]{1,0:T(8,128)} %get-tuple-element.67, f32[512]{0:T(512)S(1)} %bitcast.192, f32[512]{0:T(512)S(1)} %bitcast.193, s32[2048]{0:T(1024)S(1)} %bitcast.190, f32[512]{0:T(512)S(1)} %get-tuple-element.23, s32[512]{0:T(512)S(1)} %copy-done.8, pred[512]{0:T(512)(128)(4,1)S(1)} %get-tuple-element.24), kind=kLoop, calls=%fused_computation.10 | loop fusion | flops 14680064 | bytes 6308352 | tf_op jit(solution)/shard_map/convert_element_type | solution.py:173
  76.1 0.7 convolution_convert_fusion.1
  77.4 9.0 %collective-permute-done.12 = bf16[512,256]{1,0:T(8,128)(2,1)S(1)} collective-permute-done((bf16[512,256]{1,0:T(8,128)(2,1)S(1)}, bf16[512,256]{1,0:T(8,128)(2,1)S(1)}, u32[]{:S(2)}, u32[]{:S(2)}) %collective-permute-start.12) | collective-permute-done | bytes 262176 | tf_op jit(solution)/shard_map/ppermute | solution.py:58
  86.4 0.9 convert_add_fusion
  87.2 0.8 select_add_fusion
  (112 shorter events, 9.2 us)
Async XLA Ops:
  0.6 18.6 %copy-start = (bf16[1024,256]{1,0:T(8,128)(2,1)S(1)}, bf16[1024,256]{1,0:T(8,128)(2,1)}, u32[]{:S(2)}) copy-start(bf16[1024,256]{1,0:T(8,128)(2,1)} %param.17) | copy-start | bytes 1572868
  0.6 10.1 %copy-start.1 = (bf16[512,256]{1,0:T(8,128)(2,1)S(1)}, bf16[512,256]{1,0:T(8,128)(2,1)}, u32[]{:S(2)}) copy-start(bf16[512,256]{1,0:T(8,128)(2,1)} %param.18) | copy-start | bytes 786436
  0.7 10.2 %copy-start.5 = (bf16[256,256]{1,0:T(8,128)(2,1)S(1)}, bf16[256,256]{1,0:T(8,128)(2,1)}, u32[]{:S(2)}) copy-start(bf16[256,256]{1,0:T(8,128)(2,1)} %param.19) | copy-start | bytes 393220
  3.2 9.6 %collective-permute-start = (bf16[256,512]{1,0:T(8,128)(2,1)S(1)}, bf16[256,512]{1,0:T(8,128)(2,1)S(1)}, u32[]{:S(2)}, u32[]{:S(2)}) collective-permute-start(bf16[256,512]{1,0:T(8,128)(2,1)S(1)} %slice.85), channel_id=1, source_target_pairs={{0,2},{2,4},{4,6},{6,8},{8,10},{10,12},{12,14},{14,16},{16,18},{18... | collective-permute-start | bytes 786440 | tf_op jit(solution)/shard_map/ppermute | solution.py:16
  3.7 9.1 %collective-permute-start.1 = (bf16[256,512]{1,0:T(8,128)(2,1)S(1)}, bf16[256,512]{1,0:T(8,128)(2,1)S(1)}, u32[]{:S(2)}, u32[]{:S(2)}) collective-permute-start(bf16[256,512]{1,0:T(8,128)(2,1)S(1)} %slice.85), channel_id=1, source_target_pairs={{2,0},{4,2},{6,4},{8,6},{10,8},{12,10},{14,12},{16,14},{18,16},{20... | collective-permute-start | bytes 786440 | tf_op jit(solution)/shard_map/ppermute | solution.py:19
  17.5 1.4 %copy-start.6 = (bf16[256,256]{1,0:T(8,128)(2,1)S(1)}, bf16[256,256]{1,0:T(8,128)(2,1)}, u32[]{:S(2)}) copy-start(bf16[256,256]{1,0:T(8,128)(2,1)} %param.15) | copy-start | bytes 393220
  17.5 1.8 %copy-start.9 = (bf16[256,1024]{1,0:T(8,128)(2,1)S(1)}, bf16[256,1024]{1,0:T(8,128)(2,1)}, u32[]{:S(2)}) copy-start(bf16[256,1024]{1,0:T(8,128)(2,1)} %param.16) | copy-start | bytes 1572868
  18.9 1.4 %copy-start.4 = (bf16[256,512]{1,0:T(8,128)(2,1)S(1)}, bf16[256,512]{1,0:T(8,128)(2,1)}, u32[]{:S(2)}) copy-start(bf16[256,512]{1,0:T(8,128)(2,1)} %param.20) | copy-start | bytes 786436
  20.2 5.0 %copy-start.2 = (bf16[256,256]{1,0:T(8,128)(2,1)}, bf16[256,256]{1,0:T(8,128)(2,1)S(1)}, u32[]{:S(2)}) copy-start(bf16[256,256]{1,0:T(8,128)(2,1)S(1)} %copy.66) | copy-start | bytes 393220
  25.2 18.3 %collective-permute-start.8 = (bf16[528,256]{1,0:T(8,128)(2,1)S(1)}, bf16[528,256]{1,0:T(8,128)(2,1)S(1)}, u32[]{:S(2)}, u32[]{:S(2)}) collective-permute-start(bf16[528,256]{1,0:T(8,128)(2,1)S(1)} %fusion.58), channel_id=1, source_target_pairs={{0,8},{4,12},{8,0},{12,4},{16,24},{20,28},{24,16},{28,20},{1,9},{5... | collective-permute-start | bytes 811016 | tf_op jit(solution)/shard_map/ppermute | solution.py:100
  29.0 4.0 %collective-permute-start.3 = (f32[2,8,512]{2,1,0:T(8,128)S(1)}, f32[2,8,512]{2,1,0:T(8,128)S(1)}, u32[]{:S(2)}, u32[]{:S(2)}) collective-permute-start(f32[2,8,512]{2,1,0:T(8,128)S(1)} %pad_maximum_fusion.1), channel_id=1, source_target_pairs={{0,4},{4,0},{8,12},{12,8},{16,20},{20,16},{24,28},{28,24},{1,5},{5... | collective-permute-start | bytes 98312 | tf_op jit(solution)/shard_map/ppermute | solution.py:39
  31.3 10.7 %collective-permute-start.2 = (bf16[512,256]{0,1:T(8,128)(2,1)S(1)}, bf16[512,256]{0,1:T(8,128)(2,1)S(1)}, u32[]{:S(2)}, u32[]{:S(2)}) collective-permute-start(bf16[512,256]{0,1:T(8,128)(2,1)S(1)} %bitcast.171), channel_id=1, source_target_pairs={{0,4},{4,0},{8,12},{12,8},{16,20},{20,16},{24,28},{28,24},{1,5},{5... | collective-permute-start | bytes 786440 | tf_op jit(solution)/shard_map/ppermute | solution.py:39
  33.0 4.0 %collective-permute-start.5 = (f32[2,8,512]{2,1,0:T(8,128)S(1)}, f32[2,8,512]{2,1,0:T(8,128)S(1)}, u32[]{:S(2)}, u32[]{:S(2)}) collective-permute-start(f32[2,8,512]{2,1,0:T(8,128)S(1)} %pad_maximum_fusion.2), channel_id=1, source_target_pairs={{0,8},{4,12},{8,0},{12,4},{16,24},{20,28},{24,16},{28,20},{1,9},{5... | collective-permute-start | bytes 98312 | tf_op jit(solution)/shard_map/ppermute | solution.py:39
  37.0 4.9 %collective-permute-start.7 = (f32[2,8,512]{2,1,0:T(8,128)S(1)}, f32[2,8,512]{2,1,0:T(8,128)S(1)}, u32[]{:S(2)}, u32[]{:S(2)}) collective-permute-start(f32[2,8,512]{2,1,0:T(8,128)S(1)} %pad_maximum_fusion.3), channel_id=1, source_target_pairs={{0,16},{4,20},{8,24},{12,28},{16,0},{20,4},{24,8},{28,12},{1,17},{... | collective-permute-start | bytes 98312 | tf_op jit(solution)/shard_map/ppermute | solution.py:39
  41.9 17.9 %copy-start.7 = (bf16[256,256]{1,0:T(8,128)(2,1)S(1)}, bf16[256,256]{1,0:T(8,128)(2,1)}, u32[]{:S(2)}) copy-start(bf16[256,256]{1,0:T(8,128)(2,1)} %param.21) | copy-start | bytes 393220
  42.1 7.5 %collective-permute-start.4 = (bf16[512,256]{0,1:T(8,128)(2,1)S(1)}, bf16[512,256]{0,1:T(8,128)(2,1)S(1)}, u32[]{:S(2)}, u32[]{:S(2)}) collective-permute-start(bf16[512,256]{0,1:T(8,128)(2,1)S(1)} %fusion.39), channel_id=1, source_target_pairs={{0,8},{4,12},{8,0},{12,4},{16,24},{20,28},{24,16},{28,20},{1,9},{5... | collective-permute-start | bytes 786440 | tf_op jit(solution)/shard_map/ppermute | solution.py:39
  43.6 16.6 %copy-start.10 = (bf16[256,256]{1,0:T(8,128)(2,1)S(1)}, bf16[256,256]{1,0:T(8,128)(2,1)}, u32[]{:S(2)}) copy-start(bf16[256,256]{1,0:T(8,128)(2,1)} %param.23) | copy-start | bytes 393220
  43.6 16.6 %copy-start.11 = (bf16[256,256]{1,0:T(8,128)(2,1)S(1)}, bf16[256,256]{1,0:T(8,128)(2,1)}, u32[]{:S(2)}) copy-start(bf16[256,256]{1,0:T(8,128)(2,1)} %param.22) | copy-start | bytes 393220
  49.8 9.9 %collective-permute-start.6 = (bf16[512,256]{0,1:T(8,128)(2,1)S(1)}, bf16[512,256]{0,1:T(8,128)(2,1)S(1)}, u32[]{:S(2)}, u32[]{:S(2)}) collective-permute-start(bf16[512,256]{0,1:T(8,128)(2,1)S(1)} %fusion.37), channel_id=1, source_target_pairs={{0,16},{4,20},{8,24},{12,28},{16,0},{20,4},{24,8},{28,12},{1,17},{... | collective-permute-start | bytes 786440 | tf_op jit(solution)/shard_map/ppermute | solution.py:39
  52.9 9.5 %copy-start.8 = (s32[512]{0:T(512)S(1)}, s32[512]{0:T(512)}, u32[]{:S(2)}) copy-start(s32[512]{0:T(512)} %param.25) | copy-start | bytes 6148
  52.9 9.3 %collective-permute-start.9 = (bf16[1040,256]{1,0:T(8,128)(2,1)S(1)}, bf16[1040,256]{1,0:T(8,128)(2,1)S(1)}, u32[]{:S(2)}, u32[]{:S(2)}) collective-permute-start(bf16[1040,256]{1,0:T(8,128)(2,1)S(1)} %fusion.31), channel_id=1, source_target_pairs={{0,4},{4,0},{8,12},{12,8},{16,20},{20,16},{24,28},{28,24},{1,5},{5... | collective-permute-start | bytes 1597448 | tf_op jit(solution)/shard_map/ppermute | solution.py:100
  60.7 16.2 %copy-start.3 = (bf16[512,256]{1,0:T(8,128)(2,1)}, bf16[512,256]{1,0:T(8,128)(2,1)S(1)}, u32[]{:S(2)}) copy-start(bf16[512,256]{1,0:T(8,128)(2,1)S(1)} %convolution_convert_fusion.2) | copy-start | bytes 786436
  66.7 4.6 %collective-permute-start.10 = (f32[3,512]{1,0:T(4,128)S(1)}, f32[3,512]{1,0:T(4,128)S(1)}, u32[]{:S(2)}, u32[]{:S(2)}) collective-permute-start(f32[3,512]{1,0:T(4,128)S(1)} %pad_maximum_fusion.4), channel_id=1, source_target_pairs={{0,16},{4,20},{8,24},{12,28},{16,0},{20,4},{24,8},{28,12},{1,17},{... | collective-permute-start | bytes 18440 | tf_op jit(solution)/shard_map/ppermute | solution.py:39
  76.8 9.6 %collective-permute-start.12 = (bf16[512,256]{1,0:T(8,128)(2,1)S(1)}, bf16[512,256]{1,0:T(8,128)(2,1)S(1)}, u32[]{:S(2)}, u32[]{:S(2)}) collective-permute-start(bf16[512,256]{1,0:T(8,128)(2,1)S(1)} %convolution_convert_fusion.1), channel_id=1, source_target_pairs={{0,16},{4,20},{8,24},{12,28},{16,0},{20,4},{24,8},{28,12},{1,17},{... | collective-permute-start | bytes 786440 | tf_op jit(solution)/shard_map/ppermute | solution.py:58
  77.3 10.0 %collective-permute-start.11 = (f32[256,256]{1,0:T(8,128)S(1)}, f32[256,256]{1,0:T(8,128)S(1)}, u32[]{:S(2)}, u32[]{:S(2)}) collective-permute-start(f32[256,256]{1,0:T(8,128)S(1)} %slice_select_fusion), channel_id=1, source_target_pairs={{0,2},{2,0},{1,3},{3,1},{4,6},{6,4},{5,7},{7,5},{8,10},{10,8},{9,1... | collective-permute-start | bytes 786440 | tf_op jit(solution)/shard_map/ppermute | solution.py:89
